TPU v7x, 32 devices: a whole 2x2x4 slice. The times are simulated.
32 devices in a mesh: dp: 8 (over z, core), mask: 4 (over y, x).
Axes of the slice: x: 2, y: 2, z: 4, core: 2. Of those that a mesh axis runs over, the one named last changes fastest.
Arguments:
- patches: bfloat16 [2048, 768], P(('dp', 'mask')), parts along dimension 0
- visible_index: int32 [32, 51], P('dp'), parts along dimension 0, may hold values from 0 to 255, as said below
- embed_w: bfloat16 [768, 1024], replicated
- w_qkv: bfloat16 [1024, 3072], replicated, may hold values from -0.1875 to 0.1875
- w_out: bfloat16 [1024, 1024], replicated, may hold values from -0.1875 to 0.1875
- mask_embed: bfloat16 [1024], replicated, may hold values from -4 to 4
- dec_in: bfloat16 [1024, 768], replicated, may hold values from -0.1875 to 0.1875
- conv_w: bfloat16 [3, 16, 48, 48], replicated, may hold values from -0.5 to 0.5
- dec_out: bfloat16 [768, 1024], replicated, may hold values from -0.21875 to 0.21875
Outputs:
- embed_grad: float32 [6144, 1024], P(('dp', 'mask')), parts along dimension 0
- copy_loss: float32 [32], P(('dp', 'mask')), parts along dimension 0
There are 8 independent parts, one for each index of `dp`. A program takes and returns all parts, laid end to end along the dimension named above; an argument that names none is the same for every part. Nothing has to cross between parts.
Inputs may be any that keep to these rules, and one draw needn't show every extreme that they name: `visible_index`: each row lists 51 different patches; among the 64 patches of one index of mask (patches k * 64 to (k + 1) * 64 - 1) a row lists at most 26, and in every row some index's patches reach 26.
All inputs are finite; a program needn't handle non-finite values.
Results may differ from a plain program's by a relative error of at most 0.02.
Values may be sent and summed in bfloat16 or wider, within the bound.
No kernel may reach another device: no remote copies, remote signals or barrier semaphores. Data moves between devices by JAX's collectives and lax.ppermute only.
A program may use at most 128 MiB of HBM per device.

v0:
```python
import math

import jax
import jax.numpy as jnp
from jax import lax
from jax.sharding import PartitionSpec as P

D = 1024
HEADS = 16
DD = 768
GROUPS = 16


EPSILON = 1e-06


def row_norm(values):
    average = jnp.mean(values, axis=-1, keepdims=True)
    centred = values - average
    spread = jnp.mean(centred * centred, axis=-1, keepdims=True)
    return centred * lax.rsqrt(spread + EPSILON)


def head_norm(values):
    return values * lax.rsqrt(jnp.mean(values * values, axis=-1, keepdims=True) + EPSILON)


def mix_heads(queries, key_rows, values):
    score_scale = 1.0 / math.sqrt(queries.shape[-1])
    scores = (
        jnp.einsum("qhd,khd->hqk", queries, key_rows, preferred_element_type=jnp.float32)
        * score_scale
    )
    exponent = jnp.exp(scores)
    weights = (exponent / jnp.sum(exponent, axis=-1, keepdims=True)).astype(jnp.bfloat16)
    mixed = jnp.einsum("hqk,khd->qhd", weights, values, preferred_element_type=jnp.float32)
    return mixed.astype(jnp.bfloat16)


def split_project(projected):
    queries = head_norm(projected[:, 0].astype(jnp.float32)).astype(jnp.bfloat16)
    key_rows = head_norm(projected[:, 1].astype(jnp.float32)).astype(jnp.bfloat16)
    return mix_heads(queries, key_rows, projected[:, 2])


def attention_branch(inputs, w_qkv, w_out):
    row_count = inputs.shape[0]
    normed = row_norm(inputs.astype(jnp.float32)).astype(jnp.bfloat16)
    projected = jnp.dot(normed, w_qkv, preferred_element_type=jnp.float32).astype(jnp.bfloat16)
    context = split_project(projected.reshape(row_count, 3, HEADS, D // HEADS))
    return jnp.dot(context.reshape(row_count, D), w_out, preferred_element_type=jnp.float32)


def decoder_output(visible_out, positions, total_rows, mask_embed, dec_in, conv_w, dec_out):
    canvas = jnp.broadcast_to(mask_embed, (total_rows, D)).at[positions].set(visible_out)
    lowered = jnp.dot(canvas, dec_in, preferred_element_type=jnp.float32).astype(jnp.bfloat16)
    grouped = lowered.reshape(total_rows, GROUPS, DD // GROUPS)
    padded = jnp.pad(grouped, ((1, 1), (0, 0), (0, 0)))
    convolved = jnp.zeros((total_rows, GROUPS, DD // GROUPS), jnp.float32)
    for offset in range(3):
        convolved = convolved + jnp.einsum(
            "pgi,gio->pgo",
            padded[offset : offset + total_rows],
            conv_w[offset],
            preferred_element_type=jnp.float32,
        )
    activated = jax.nn.gelu(row_norm(convolved.reshape(total_rows, DD)), approximate=False)
    hidden = (lowered.astype(jnp.float32) + activated).astype(jnp.bfloat16)
    return jnp.dot(hidden, dec_out, preferred_element_type=jnp.float32)


def copy_terms(visible_in, positions, targets, w_qkv, w_out, mask_embed, dec_in, conv_w, dec_out):
    total_rows = targets.shape[0]
    visible_out = (
        visible_in.astype(jnp.float32) + attention_branch(visible_in, w_qkv, w_out)
    ).astype(jnp.bfloat16)
    predicted = decoder_output(
        visible_out, positions, total_rows, mask_embed, dec_in, conv_w, dec_out
    )
    slot_ids = jnp.arange(total_rows, dtype=jnp.int32)
    seen = jnp.max((slot_ids[:, None] == positions[None, :]).astype(jnp.float32), axis=1)
    mismatch = (predicted - targets.astype(jnp.float32)) * (1.0 - seen)[:, None]
    return jnp.sum(mismatch * mismatch)


def on_device(patches, visible_index, embed_w, w_qkv, w_out, mask_embed, dec_in, conv_w, dec_out):
    tok_rows = patches.shape[0]
    group_size = lax.axis_size("mask")
    own_index = lax.axis_index("mask")
    head_dim = D // HEADS
    heads_here = HEADS // group_size
    head_width = heads_here * head_dim
    copies = visible_index.shape[0]
    visible_count = visible_index.shape[1]
    total_rows = tok_rows * group_size
    positions = lax.dynamic_index_in_dim(visible_index, own_index, 0, keepdims=False)
    own_embedded = jnp.dot(patches, embed_w, preferred_element_type=jnp.float32).astype(
        jnp.bfloat16
    )
    embedded, clip_pixels = (
        lax.all_gather(own_embedded, "mask", axis=0, tiled=True),
        lax.all_gather(patches, "mask", axis=0, tiled=True),
    )
    visible_in = embedded[positions]
    normed = row_norm(embedded.astype(jnp.float32)).astype(jnp.bfloat16)
    own_cols = lax.dynamic_slice_in_dim(
        w_qkv.reshape(D, 3, D), own_index * head_width, head_width, 2
    )
    projected = jnp.einsum(
        "sd,dtw->stw", normed, own_cols, preferred_element_type=jnp.float32
    ).astype(jnp.bfloat16)
    context = split_project(projected.reshape(total_rows, 3, heads_here, head_dim))
    out_rows = lax.dynamic_slice_in_dim(w_out, own_index * head_width, head_width, 0)
    partial_value = jnp.dot(
        context.reshape(total_rows, head_width), out_rows, preferred_element_type=jnp.float32
    )
    branch = lax.psum(partial_value.astype(jnp.bfloat16), "mask").astype(jnp.float32)
    all_targets = row_norm(branch).astype(jnp.bfloat16)

    def objective(rows_in):
        return copy_terms(
            rows_in, positions, all_targets, w_qkv, w_out, mask_embed, dec_in, conv_w, dec_out
        )

    squares, pullback = jax.vjp(objective, visible_in)
    factor = 0.5 / math.sqrt(copies * visible_count)
    (grad_in,) = pullback(jnp.ones_like(squares) * factor)
    copy_loss = jnp.reshape(squares / ((total_rows - visible_count) * D), (1,))
    own_cols = lax.all_to_all(patches, "mask", split_axis=1, concat_axis=0, tiled=True)
    flat_index = visible_index.reshape(copies * visible_count)
    gathered = own_cols[flat_index]
    embed_grad = jnp.einsum(
        "vc,vd->cd",
        gathered,
        lax.all_gather(grad_in, "mask", axis=0, tiled=True),
        preferred_element_type=jnp.float32,
    )
    return (embed_grad, copy_loss)


def solution(mesh):
    placed = (P(("dp", "mask"), None), P("dp", None), P(), P(), P(), P(), P(), P(), P())
    return jax.shard_map(
        on_device,
        mesh=mesh,
        in_specs=placed,
        out_specs=(P(("dp", "mask"), None), P(("dp", "mask"))),
        check_vma=False,
    )
```

profile of v0, /device:TPU:0, one launch (start us, length us, event | category | flops | bytes accessed | tf_op | source)
XLA Modules:
  0.0 134.3 jit_solution(9758933965294009839)
XLA Ops:
  7.2 2.0 %convolution_convert_fusion.14 = bf16[64,1024]{1,0:T(8,128)(2,1)S(1)} fusion(bf16[64,768]{1,0:T(8,128)(2,1)} %param.9, bf16[768,1024]{1,0:T(8,128)(2,1)} %param.11), kind=kOutput, calls=%fused_computation.52 | convolution fusion | flops 100728832 | bytes 1802240 | tf_op jit(solution)/shard_map/dot_general | solution.py:97
  9.2 11.5 %all_gather.6 = bf16[256,1024]{1,0:T(8,128)(2,1)S(1)} all-gather(bf16[64,1024]{1,0:T(8,128)(2,1)S(1)} %convolution_convert_fusion.14), channel_id=1, replica_groups=mesh['dp'=8,'mask'=4] {'mask'}, dimensions={0}, use_global_device_ids=true | all-gather | bytes 655360 | tf_op jit(solution)/shard_map/all_gather | solution.py:101
  21.2 8.7 %copy.84 = bf16[1024,3072]{0,1:T(8,128)(2,1)} copy(bf16[1024,3072]{1,0:T(8,128)(2,1)} %param.12) | data formatting | bytes 12582912 | tf_op args[3]
  29.9 2.1 %fusion.4 = bf16[256,3,256]{0,2,1:T(8,128)(2,1)S(1)} fusion(bf16[1024,3,1024]{0,2,1:T(8,128)(2,1)} %bitcast.173, s32[]{:T(128)S(6)} %select_n.51, bf16[256,1024]{1,0:T(8,128)(2,1)S(1)} %all_gather.6, f32[256]{0:T(256)S(1)} %add_rsqrt_fusion.3, f32[256]{0:T(256)S(1)} %broadcast_multiply_fusion.2), kind=kOutput, calls=%fused_computation.21 | convolution fusion | flops 403898368 | bytes 2492420 | tf_op jit(solution)/shard_map/sd,dtw->stw/dot_general | solution.py:109
  32.1 1.3 %fusion.2 = f32[4,256,256]{1,2,0:T(8,128)} fusion(f32[256,4]{0,1:T(4,128)S(1)} %get-tuple-element.31, f32[256,4]{0,1:T(4,128)S(1)} %get-tuple-element.32, bf16[256,3,4,64]{0,3,2,1:T(8,128)(2,1)S(1)} %bitcast.182), kind=kOutput, calls=%fused_computation.10 | convolution fusion | flops 34209792 | bytes 1318912 | tf_op jit(solution)/shard_map/qhd,khd->hqk/dot_general | solution.py:31
  33.4 1.8 %convolution_convert_fusion.13 = bf16[4,64,256]{2,1,0:T(8,128)(2,1)S(1)} fusion(f32[4,256,256]{1,2,0:T(8,128)} %fusion.2, bf16[256,3,4,64]{0,3,2,1:T(8,128)(2,1)S(1)} %bitcast.183), kind=kOutput, calls=%fused_computation.51 | convolution fusion | flops 34145536 | bytes 2359296 | tf_op jit(solution)/shard_map/hqk,khd->qhd/dot_general | solution.py:36
  35.3 1.1 convolution_convert_fusion.1
  37.3 3.3 %all-to-all-start = ((bf16[64,4,192]{2,0,1:T(8,128)(2,1)}), bf16[64,4,192]{2,0,1:T(8,128)(2,1)S(1)}, u32[]{:S(2)}, u32[]{:S(2)}) async-start(bf16[64,4,192]{2,0,1:T(8,128)(2,1)} %copy.73), calls=%async_computation | async-start | bytes 262144 | tf_op jit(solution)/shard_map/all_to_all | solution.py:129
  43.2 4.0 %convolution_convert_fusion = bf16[51,3072]{1,0:T(8,128)(2,1)S(1)} fusion(bf16[1024,3072]{1,0:T(8,128)(2,1)} %param.12, bf16[51,1024]{1,0:T(8,128)(2,1)S(1)} %gather_fusion.2, f32[51]{0:T(128)S(1)} %fusion.116, f32[51]{0:T(128)S(1)} %broadcast_multiply_fusion.4), kind=kOutput, calls=%fused_computation.6 | convolution fusion | flops 321229824 | bytes 6709656 | tf_op jit(solution)/shard_map/jvp()/dot_general | solution.py:49
  49.9 1.1 scatter_custom_fusion
  51.0 1.3 gather_fusion.1
  55.4 1.5 %scatter_fusion = bf16[256,1024]{1,0:T(8,128)(2,1)S(1)} fusion(bf16[256,1024]{1,0:T(8,128)(2,1)S(1)} %copy-done.1, s32[51]{0:T(128)S(1)} %fusion.115, bf16[51,1024]{1,0:T(8,128)(2,1)S(1)} %fusion.24), kind=kCustom, calls=%fused_computation.5 | custom fusion | flops 52224 | bytes 313548 | tf_op jit(solution)/shard_map/jvp()/scatter-add | solution.py:55
  56.9 2.7 %convolution_convert_fusion.7 = bf16[256,768]{1,0:T(8,128)(2,1)} fusion(bf16[256,1024]{1,0:T(8,128)(2,1)S(1)} %scatter_fusion, bf16[1024,768]{1,0:T(8,128)(2,1)} %param.15), kind=kOutput, calls=%fused_computation.26 | convolution fusion | flops 402849792 | bytes 2490368 | tf_op jit(solution)/shard_map/jvp()/dot_general | solution.py:56
  59.6 1.2 copy.79
  60.8 1.3 fusion.62
  62.1 1.2 convolution_add_fusion.1
  63.4 1.4 %fusion.128 = (f32[256]{0:T(256)S(1)}, f32[16,256,48]{1,2,0:T(8,128)S(1)}) fusion(f32[16,256,48]{1,2,0:T(8,128)S(1)} %convolution_add_fusion.1, bf16[256,16,48]{0,2,1:T(8,128)(2,1)S(1)} %bitcast.179, bf16[3,16,48,48]{3,2,1,0:T(8,128)(2,1)} %param.16), kind=kOutput, calls=%fused_computation.234 | convolution fusion | flops 19267328 | bytes 2163712 | tf_op jit(solution)/shard_map/jvp(pgi,gio->pgo)/dot_general | solution.py:61
  65.5 1.1 copy.83
  68.7 1.3 multiply_divide_fusion
  70.6 1.8 %gather_fusion = bf16[204,192]{1,0:T(8,128)(2,1)} fusion(bf16[256,192]{1,0:T(8,128)(2,1)S(1)} %bitcast.171, s32[1024]{0:T(1024)} %pad_clamp_fusion.1), kind=kCustom, calls=%fused_computation | custom fusion | bytes 157488 | tf_op jit(solution)/shard_map/gather | solution.py:131
  72.4 10.7 %all-reduce.9.cloned.1.call-done = bf16[256,1024]{1,0:T(8,128)(2,1)} async-done(((bf16[256,1024]{1,0:T(8,128)(2,1)}), bf16[256,1024]{1,0:T(8,128)(2,1)}) %all-reduce.9.cloned.1.call-update) | async-done | bytes 524304 | tf_op jit(solution)/shard_map/psum | solution.py:117
  83.1 1.2 convert_reduce_fusion
  84.3 1.3 fusion.25
  85.7 4.8 %multiply_reduce_fusion = (f32[]{:T(128)}, f32[256,1024]{1,0:T(8,128)S(1)}) fusion(f32[256]{0:T(256)} %get-tuple-element.12, f32[256]{0:T(256)S(1)} %add_rsqrt_fusion.2, f32[256]{0:T(256)S(1)} %broadcast_multiply_fusion.1, bf16[256,1024]{1,0:T(8,128)(2,1)} %all-reduce.9.cloned.1.call-done, bf16[768,1024]{1,0:T(8,128)(2,1)} %param.17, ...), kind=kOutput, calls=%fused_computation.64 | convolution fusion | flops 418971648 | bytes 4330500 | tf_op jit(solution)/shard_map/jvp()/dot_general | solution.py:69
  90.5 3.5 %multiply_reduce_fusion.1 = (f32[256]{0:T(256)S(1)}, bf16[256,768]{1,0:T(8,128)(2,1)S(1)}) fusion(f32[256,768]{1,0:T(8,128)S(1)} %copy-done.2, f32[256]{0:T(256)S(1)} %copy-done.23, f32[256]{0:T(256)S(1)} %copy-done.34, bf16[768,1024]{1,0:T(8,128)(2,1)S(1)} %copy-done.40, f32[256,1024]{1,0:T(8,128)S(1)} %get-tuple-element.28, f32[256]{0:T(256)S(1)} %copy-done.37), kind=kOutput, calls=%fused_computation.87 | convolution fusion | flops 419495680 | bytes 3805184 | tf_op jit(solution)/shard_map/transpose(jvp())/dot_general | solution.py:69
  94.1 2.5 %fusion.125 = (f32[256]{0:T(256)S(1)}, f32[256,768]{1,0:T(8,128)S(1)}) fusion(f32[256]{0:T(256)S(1)} %multiply_multiply_fusion.8, bf16[256,768]{1,0:T(8,128)(2,1)S(1)} %get-tuple-element.18, f32[256]{0:T(256)S(1)} %copy-done.34, f32[256,768]{1,0:T(8,128)S(1)} %copy-done.2, f32[256]{0:T(256)S(1)} %copy-done.23), kind=kLoop, calls=%fused_computation.231 | loop fusion | flops 15531776 | bytes 1970176 | tf_op jit(solution)/shard_map/transpose(jvp())/reduce_sum | solution.py:19
  97.5 1.2 copy.86
  100.4 2.0 %convolution_convert_fusion.2 = bf16[256,1024]{1,0:T(8,128)(2,1)S(1)} fusion(bf16[1024,768]{1,0:T(8,128)(2,1)} %param.15, bf16[256,768]{1,0:T(8,128)(2,1)S(1)} %copy-done.10, bf16[256,768]{1,0:T(8,128)(2,1)S(1)} %copy.90), kind=kOutput, calls=%fused_computation.20 | convolution fusion | flops 403111936 | bytes 2883584 | tf_op jit(solution)/shard_map/transpose(jvp())/dot_general | solution.py:56
  103.3 1.6 %convolution_convert_fusion.16 = bf16[51,1024]{1,0:T(8,128)(2,1)S(1)} fusion(bf16[1024,1024]{1,0:T(8,128)(2,1)S(1)} %copy-done, pred[51,1024]{1,0:T(8,128)(4,1)} %copy-done.13, bf16[51,1024]{1,0:T(8,128)(2,1)S(1)} %gather_fusion.3, pred[51]{0:T(512)(128)(4,1)} %get-tuple-element.4), kind=kOutput, calls=%fused_computation.56 | convolution fusion | flops 107111424 | bytes 2358323 | tf_op jit(solution)/shard_map/transpose(jvp())/dot_general | solution.py:51
  108.7 5.0 %fusion.77 = (f32[51]{0:T(128)S(1)}, f32[51,1024]{1,0:T(8,128)S(1)}) fusion(bf16[51,1024]{1,0:T(8,128)(2,1)S(1)} %gather_fusion.2, f32[51]{0:T(128)S(1)} %copy-done.21, bf16[51,3072]{1,0:T(8,128)(2,1)S(1)} %reshape.268, bf16[1024,3072]{1,0:T(8,128)(2,1)} %param.12), kind=kOutput, calls=%fused_computation.151 | convolution fusion | flops 321177536 | bytes 6918552 | tf_op jit(solution)/shard_map/transpose(jvp())/dot_general | solution.py:49
  114.2 10.2 %all-gather = bf16[4,51,1024]{2,1,0:T(8,128)(2,1)S(1)} all-gather(bf16[1,51,1024]{2,1,0:T(8,128)(2,1)S(1)} %fusion.105), channel_id=1, replica_groups=mesh['dp'=8,'mask'=4] {'mask'}, dimensions={0}, use_global_device_ids=true | all-gather | bytes 522240 | tf_op jit(solution)/shard_map/all_gather | solution.py:135
  124.5 1.2 fusion.129
  (151 shorter events, 20.4 us)
Async XLA Ops:
  7.2 28.1 %copy-start = (bf16[1024,1024]{1,0:T(8,128)(2,1)S(1)}, bf16[1024,1024]{1,0:T(8,128)(2,1)}, u32[]{:S(2)}) copy-start(bf16[1024,1024]{1,0:T(8,128)(2,1)} %param.13) | copy-start | bytes 6291460
  7.2 75.9 %all-reduce.9.cloned.1.call-start = ((), (), s32[]{:S(2)}) async-start(), calls=%async_computation.1 | async-start | bytes 1048576 | tf_op jit(solution)/shard_map/psum | solution.py:117
  35.3 1.2 copy-start.17
  35.3 5.4 %copy-start.35 = (s32[4,51]{1,0:T(4,128)S(1)}, s32[4,51]{1,0:T(4,128)}, u32[]{:S(2)}) copy-start(s32[4,51]{1,0:T(4,128)} %param.10) | copy-start | bytes 2452
  37.3 33.3 %all-to-all-start = ((bf16[64,4,192]{2,0,1:T(8,128)(2,1)}), bf16[64,4,192]{2,0,1:T(8,128)(2,1)S(1)}, u32[]{:S(2)}, u32[]{:S(2)}) async-start(bf16[64,4,192]{2,0,1:T(8,128)(2,1)} %copy.73), calls=%async_computation | async-start | bytes 262144 | tf_op jit(solution)/shard_map/all_to_all | solution.py:129
  40.6 11.7 %copy-start.29 = (u32[51]{0:T(128)}, u32[51]{0:T(128)S(1)}, u32[]{:S(2)}) copy-start(u32[51]{0:T(128)S(1)} %iota_add_fusion) | copy-start | bytes 616
  41.9 9.1 %copy-start.28 = (s32[1024]{0:T(1024)}, s32[1024]{0:T(1024)S(1)}, u32[]{:S(2)}) copy-start(s32[1024]{0:T(1024)S(1)} %pad_clamp_fusion) | copy-start | bytes 12292
  42.9 4.3 %copy-start.38 = (f32[51]{0:T(128)}, f32[51]{0:T(128)S(1)}, u32[]{:S(2)}) copy-start(f32[51]{0:T(128)S(1)} %fusion.75) | copy-start | bytes 616
  43.2 4.0 %copy-start.31 = (f32[51]{0:T(128)}, f32[51]{0:T(128)S(1)}, u32[]{:S(2)}) copy-start(f32[51]{0:T(128)S(1)} %fusion.116) | copy-start | bytes 616
  47.8 1.9 %copy-start.5 = (bf16[51,1,16,64]{3,2,1,0:T(8,128)(2,1)}, bf16[51,1,16,64]{3,2,1,0:T(8,128)(2,1)S(1)}, u32[]{:S(2)}) copy-start(bf16[51,1,16,64]{3,2,1,0:T(8,128)(2,1)S(1)} %get-tuple-element.9) | copy-start | bytes 313348
  47.8 1.9 %copy-start.7 = (bf16[51,1,16,64]{3,2,1,0:T(8,128)(2,1)}, bf16[51,1,16,64]{3,2,1,0:T(8,128)(2,1)S(1)}, u32[]{:S(2)}) copy-start(bf16[51,1,16,64]{3,2,1,0:T(8,128)(2,1)S(1)} %get-tuple-element.10) | copy-start | bytes 313348
  47.8 1.9 %copy-start.11 = (bf16[51,1,16,64]{3,2,1,0:T(8,128)(2,1)}, bf16[51,1,16,64]{3,2,1,0:T(8,128)(2,1)S(1)}, u32[]{:S(2)}) copy-start(bf16[51,1,16,64]{3,2,1,0:T(8,128)(2,1)S(1)} %get-tuple-element.8) | copy-start | bytes 313348
  49.9 3.5 %copy-start.36 = (bf16[1024]{0:T(1024)(128)(2,1)S(1)}, bf16[1024]{0:T(1024)(128)(2,1)}, u32[]{:S(2)}) copy-start(bf16[1024]{0:T(1024)(128)(2,1)} %param.14) | copy-start | bytes 6148
  54.3 1.0 copy-start.1
  65.5 20.1 %copy-start.18 = (bf16[256,768]{1,0:T(8,128)(2,1)S(1)}, bf16[256,768]{1,0:T(8,128)(2,1)}, u32[]{:S(2)}) copy-start(bf16[256,768]{1,0:T(8,128)(2,1)} %convolution_convert_fusion.7) | copy-start | bytes 1179652
  66.7 19.0 %copy-start.2 = (f32[256,768]{1,0:T(8,128)S(1)}, f32[256,768]{1,0:T(8,128)}, u32[]{:S(2)}) copy-start(f32[256,768]{1,0:T(8,128)} %copy.83) | copy-start | bytes 2359300
  85.6 4.9 %copy-start.23 = (f32[256]{0:T(256)S(1)}, f32[256]{0:T(256)}, u32[]{:S(2)}) copy-start(f32[256]{0:T(256)} %copy-done.22) | copy-start | bytes 3076
  85.6 4.8 %copy-start.34 = (f32[256]{0:T(256)S(1)}, f32[256]{0:T(256)}, u32[]{:S(2)}) copy-start(f32[256]{0:T(256)} %fusion.114) | copy-start | bytes 3076
  85.7 4.8 %copy-start.37 = (f32[256]{0:T(256)S(1)}, f32[256]{0:T(256)}, u32[]{:S(2)}) copy-start(f32[256]{0:T(256)} %get-tuple-element.11) | copy-start | bytes 3076
  85.7 4.8 %copy-start.40 = (bf16[768,1024]{1,0:T(8,128)(2,1)S(1)}, bf16[768,1024]{1,0:T(8,128)(2,1)}, u32[]{:S(2)}) copy-start(bf16[768,1024]{1,0:T(8,128)(2,1)} %param.17) | copy-start | bytes 4718596
  90.5 3.6 %copy-start.25 = (f32[256]{0:T(256)S(1)}, f32[256]{0:T(256)}, u32[]{:S(2)}) copy-start(f32[256]{0:T(256)} %copy-done.24) | copy-start | bytes 3076
  94.0 2.6 %copy-start.9 = (bf16[256,768]{1,0:T(8,128)(2,1)}, bf16[256,768]{1,0:T(8,128)(2,1)S(1)}, u32[]{:S(2)}) copy-start(bf16[256,768]{1,0:T(8,128)(2,1)S(1)} %get-tuple-element.18) | copy-start | bytes 1179652
  96.6 2.1 %copy-start.3 = (bf16[3,16,48,48]{3,2,1,0:T(8,128)(2,1)S(1)}, bf16[3,16,48,48]{3,2,1,0:T(8,128)(2,1)}, u32[]{:S(2)}) copy-start(bf16[3,16,48,48]{3,2,1,0:T(8,128)(2,1)} %param.16) | copy-start | bytes 663556
  103.2 1.9 %copy-start.15 = (f32[16,51,51]{1,2,0:T(8,128)S(1)}, f32[16,51,51]{1,2,0:T(8,128)}, u32[]{:S(2)}) copy-start(f32[16,51,51]{1,2,0:T(8,128)} %copy-done.14) | copy-start | bytes 499396
  103.2 1.9 %copy-start.27 = (f32[16,51]{1,0:T(8,128)S(1)}, f32[16,51]{1,0:T(8,128)}, u32[]{:S(2)}) copy-start(f32[16,51]{1,0:T(8,128)} %copy-done.26) | copy-start | bytes 9796
  105.1 1.0 copy-start.8
  108.6 5.1 %copy-start.39 = (f32[51]{0:T(128)S(1)}, f32[51]{0:T(128)}, u32[]{:S(2)}) copy-start(f32[51]{0:T(128)} %copy-done.38) | copy-start | bytes 616
  108.6 5.1 %copy-start.32 = (f32[51]{0:T(128)S(1)}, f32[51]{0:T(128)}, u32[]{:S(2)}) copy-start(f32[51]{0:T(128)} %copy-done.31) | copy-start | bytes 616
  108.7 5.3 %copy-start.4 = (u32[51,1024]{1,0:T(8,128)S(1)}, u32[51,1024]{1,0:T(8,128)}, u32[]{:S(2)}) copy-start(u32[51,1024]{1,0:T(8,128)} %gather_fusion.1) | copy-start | bytes 626692
  108.7 5.3 %copy-start.30 = (u32[51]{0:T(128)S(1)}, u32[51]{0:T(128)}, u32[]{:S(2)}) copy-start(u32[51]{0:T(128)} %copy-done.29) | copy-start | bytes 616
  108.7 5.3 %copy-start.33 = (pred[51]{0:T(512)(128)(4,1)S(1)}, pred[51]{0:T(512)(128)(4,1)}, u32[]{:S(2)}) copy-start(pred[51]{0:T(512)(128)(4,1)} %get-tuple-element.4) | copy-start | bytes 157
  113.7 10.8 %copy-start.16 = (bf16[204,192]{1,0:T(8,128)(2,1)S(1)}, bf16[204,192]{1,0:T(8,128)(2,1)}, u32[]{:S(2)}) copy-start(bf16[204,192]{1,0:T(8,128)(2,1)} %gather_fusion) | copy-start | bytes 235012
  (11 other events, 9.0 us)
Sparse Core Ops, SparseCore 0:
  36.6 46.4 all-reduce.8
where the time goes:
time: 135 us; the launch traced here: 134 us
  matrix products  40.8 us (30%)
  local copies, waits for them, and re-layouts  23.6 us (17%)
  blocking collectives  21.7 us (16%)
  other arithmetic  17.5 us (13%)
  between operations  16.7 us (12%)
  waiting for transfers between devices  10.7 us (8%)
  starting transfers between devices  3.36 us (2%)
    all_gather x1, blocking collectives, on_device(): lax.all_gather(own_embedded, 'mask', axis=0, tiled=True)  11.5 us
    unnamed x84, local copies, waits for them, and re-layouts  11.3 us
    psum x1, waiting for transfers between devices, on_device(): lax.psum(partial_value.astype(jnp.bfloat16), 'mask').astype(jnp.float32)  10.7 us
    all_gather x1, blocking collectives, on_device(): lax.all_gather(grad_in, 'mask', axis=0, tiled=True)  10.2 us
    dot_general x2, matrix products, attention_branch(): jnp.dot(normed, w_qkv, preferred_element_type=jnp.float32)  9 us
    dot_general x2, matrix products, decoder_output(): return jnp.dot(hidden, dec_out, preferred_element_type=jnp.float32)  8.34 us
    dot_general x2, matrix products, decoder_output(): jnp.dot(canvas, dec_in, preferred_element_type=jnp.float32)  4.74 us
    dot_general x6, matrix products, decoder_output(): jnp.einsum('pgi,gio->pgo', padded[offset:offset + total_rows], conv_w[off...  4.62 us
  transfers between devices with their start and end apart: 2, of which 1 were waited for; matrix products, arithmetic and copies ran while one was open for 23% of the time, Pallas kernels for 0%

commit v1 on v0

--- a/solution.py
+++ b/solution.py
@@ -83,25 +83,26 @@
     return jnp.sum(mismatch * mismatch)
 
 
-def on_device(patches, visible_index, embed_w, w_qkv, w_out, mask_embed, dec_in, conv_w, dec_out):
-    tok_rows = patches.shape[0]
-    group_size = lax.axis_size("mask")
-    own_index = lax.axis_index("mask")
+def ring_gather(values, group_size):
+    parts = [values]
+    for shift in range(1, group_size):
+        pairs = [(source, (source - shift) % group_size) for source in range(group_size)]
+        parts.append(lax.ppermute(values, "mask", pairs))
+    return jnp.concatenate(parts, axis=0)
+
+
+def unroll_blocks(rotated, own_index, block_rows):
+    total_rows = rotated.shape[0]
+    doubled = jnp.concatenate([rotated, rotated], axis=0)
+    start = total_rows - own_index * block_rows
+    return lax.dynamic_slice_in_dim(doubled, start, total_rows, 0)
+
+
+def split_teacher(embedded, w_qkv, w_out, own_index, group_size):
+    total_rows = embedded.shape[0]
     head_dim = D // HEADS
     heads_here = HEADS // group_size
     head_width = heads_here * head_dim
-    copies = visible_index.shape[0]
-    visible_count = visible_index.shape[1]
-    total_rows = tok_rows * group_size
-    positions = lax.dynamic_index_in_dim(visible_index, own_index, 0, keepdims=False)
-    own_embedded = jnp.dot(patches, embed_w, preferred_element_type=jnp.float32).astype(
-        jnp.bfloat16
-    )
-    embedded, clip_pixels = (
-        lax.all_gather(own_embedded, "mask", axis=0, tiled=True),
-        lax.all_gather(patches, "mask", axis=0, tiled=True),
-    )
-    visible_in = embedded[positions]
     normed = row_norm(embedded.astype(jnp.float32)).astype(jnp.bfloat16)
     own_cols = lax.dynamic_slice_in_dim(
         w_qkv.reshape(D, 3, D), own_index * head_width, head_width, 2
@@ -114,7 +115,27 @@
     partial_value = jnp.dot(
         context.reshape(total_rows, head_width), out_rows, preferred_element_type=jnp.float32
     )
-    branch = lax.psum(partial_value.astype(jnp.bfloat16), "mask").astype(jnp.float32)
+    return lax.psum(partial_value.astype(jnp.bfloat16), "mask").astype(jnp.float32)
+
+
+def on_device(patches, visible_index, embed_w, w_qkv, w_out, mask_embed, dec_in, conv_w, dec_out):
+    tok_rows = patches.shape[0]
+    group_size = lax.axis_size("mask")
+    own_index = lax.axis_index("mask")
+    copies = visible_index.shape[0]
+    visible_count = visible_index.shape[1]
+    total_rows = tok_rows * group_size
+    col_width = patches.shape[1] // group_size
+    positions = lax.dynamic_index_in_dim(visible_index, own_index, 0, keepdims=False)
+    clip_pixels = unroll_blocks(ring_gather(patches, group_size), own_index, tok_rows)
+    embedded = jnp.dot(clip_pixels, embed_w, preferred_element_type=jnp.float32).astype(
+        jnp.bfloat16
+    )
+    visible_in = embedded[positions]
+    if HEADS * total_rows * total_rows * 4 <= (1 << 24):
+        branch = attention_branch(embedded, w_qkv, w_out)
+    else:
+        branch = split_teacher(embedded, w_qkv, w_out, own_index, group_size)
     all_targets = row_norm(branch).astype(jnp.bfloat16)
 
     def objective(rows_in):
@@ -126,13 +147,14 @@
     factor = 0.5 / math.sqrt(copies * visible_count)
     (grad_in,) = pullback(jnp.ones_like(squares) * factor)
     copy_loss = jnp.reshape(squares / ((total_rows - visible_count) * D), (1,))
-    own_cols = lax.all_to_all(patches, "mask", split_axis=1, concat_axis=0, tiled=True)
-    flat_index = visible_index.reshape(copies * visible_count)
+    slot_copy = (own_index + jnp.arange(group_size, dtype=jnp.int32)) % group_size
+    flat_index = visible_index[slot_copy].reshape(copies * visible_count)
+    own_cols = lax.dynamic_slice_in_dim(clip_pixels, own_index * col_width, col_width, 1)
     gathered = own_cols[flat_index]
     embed_grad = jnp.einsum(
         "vc,vd->cd",
         gathered,
-        lax.all_gather(grad_in, "mask", axis=0, tiled=True),
+        ring_gather(grad_in, group_size),
         preferred_element_type=jnp.float32,
     )
     return (embed_grad, copy_loss)

time: 135 us -> 94.5 us (0.70)
  blocking collectives: 21.7 us -> 0 us
  between operations: 16.7 us -> 3.17 us
  waiting for transfers between devices: 10.7 us -> 2.92 us
  starting transfers between devices: 3.36 us -> 8.98 us
  other arithmetic: 17.5 us -> 14.3 us
  local copies, waits for them, and re-layouts: 23.6 us -> 20.8 us
  matrix products: 40.8 us -> 43.5 us
    all_gather x2 -> x0, blocking collectives: 21.7 us -> none  [the longest x1 11.5 us: on_device(): lax.all_gather(own_embedded, 'mask', axis=0, tiled=True)]
    psum x1 -> x0, waiting for transfers between devices: 10.7 us -> none  [on_device(): lax.psum(partial_value.astype(jnp.bfloat16), 'mask').astype(jnp.float32)]
    ppermute x0 -> x6, starting transfers between devices: none -> 8.98 us  [ring_gather(): parts.append(lax.ppermute(values, 'mask', pairs))]
    unnamed x84 -> x67, local copies, waits for them, and re-layouts: 11.3 us -> 6.37 us
    all_to_all x1 -> x0, starting transfers between devices: 3.32 us -> none  [on_device(): lax.all_to_all(patches, 'mask', split_axis=1, concat_axis=0, tiled=True)]
    dot_general x2 -> x3, matrix products: 9 us -> 12.1 us  [attention_branch(): jnp.dot(normed, w_qkv, preferred_element_type=jnp.float32)]
    ppermute x0 -> x6, waiting for transfers between devices: none -> 2.92 us  [ring_gather(): parts.append(lax.ppermute(values, 'mask', pairs))]
    dot_general x4 -> x2, matrix products: 6.39 us -> 3.53 us  [the longest x1 2.35 us: on_device(): jnp.dot(clip_pixels, embed_w, preferred_element_type=jnp.float32)]
  transfers between devices with their start and end apart: 2 -> 6, of which waited for: 1 -> 2; matrix products, arithmetic and copies ran while one was open for 23% -> 12% of each run, Pallas kernels for 0% -> 0%
where the time goes in v1:
time: 94.5 us; the launch traced here: 93.7 us
  matrix products  43.5 us (46%)
  local copies, waits for them, and re-layouts  20.8 us (22%)
  other arithmetic  14.3 us (15%)
  starting transfers between devices  8.98 us (10%)
  between operations  3.17 us (3%)
  waiting for transfers between devices  2.92 us (3%)
    dot_general x3, matrix products, attention_branch(): jnp.dot(normed, w_qkv, preferred_element_type=jnp.float32)  12.1 us
    ppermute x6, starting transfers between devices, ring_gather(): parts.append(lax.ppermute(values, 'mask', pairs))  8.98 us
    dot_general x2, matrix products, decoder_output(): return jnp.dot(hidden, dec_out, preferred_element_type=jnp.float32)  8.48 us
    unnamed x67, local copies, waits for them, and re-layouts  6.37 us
    dot_general x2, matrix products, decoder_output(): jnp.dot(canvas, dec_in, preferred_element_type=jnp.float32)  4.88 us
    dot_general x6, matrix products, decoder_output(): jnp.einsum('pgi,gio->pgo', padded[offset:offset + total_rows], conv_w[off...  4.63 us
    dot_general x4, matrix products, mix_heads(): jnp.einsum('hqk,khd->qhd', weights, values, preferred_element_type=jnp.fl...  4.02 us
    dot_general x4, matrix products, mix_heads(): jnp.einsum('qhd,khd->hqk', queries, key_rows, preferred_element_type=jnp....  3.87 us
  transfers between devices with their start and end apart: 6, of which 2 were waited for; matrix products, arithmetic and copies ran while one was open for 12% of the time, Pallas kernels for 0%

profile of v1, /device:TPU:0, one launch (start us, length us, event | category | flops | bytes accessed | tf_op | source)
XLA Modules:
  0.0 93.7 jit_solution(10357559443047506756)
XLA Ops:
  0.7 4.0 %collective-permute-start = (bf16[64,768]{1,0:T(8,128)(2,1)}, bf16[64,768]{1,0:T(8,128)(2,1)}, u32[]{:S(2)}, u32[]{:S(2)}) collective-permute-start(bf16[64,768]{1,0:T(8,128)(2,1)} %param.9), channel_id=1, source_target_pairs={{0,3},{1,0},{2,1},{3,2},{4,7},{5,4},{6,5},{7,6},{8,11},{9,8},{10,9... | collective-permute-start | bytes 294920 | tf_op jit(solution)/shard_map/ppermute | solution.py:90
  6.4 1.2 %compare_and_fusion = (pred[51]{0:T(512)(128)(4,1)}, s32[51]{0:T(128)}) fusion(s32[4,51]{1,0:T(4,128)} %param.10, s32[]{:T(128)S(6)} %select_n.82), kind=kLoop, calls=%fused_computation.215 | loop fusion | flops 306 | bytes 463 | tf_op jit(solution)/shard_map/transpose(jvp())/and | solution.py:55
  7.7 1.1 %scatter_custom_fusion = u32[256,1024]{1,0:T(8,128)S(1)} fusion(s32[51]{0:T(128)S(1)} %fusion.114, u32[]{:T(128)} %constant.63.clone.1, u32[51]{0:T(128)S(1)} %iota_add_fusion), kind=kCustom, calls=%fused_computation.119 | custom fusion | bytes 1049092 | tf_op jit(solution)/shard_map/jvp()/scatter | solution.py:55
  18.6 2.4 %convert_reduce_fusion = (f32[256]{0:T(256)S(1)}, bf16[256,1024]{1,0:T(8,128)(2,1)S(1)}) fusion(bf16[768,1024]{1,0:T(8,128)(2,1)} %param.11, bf16[512,768]{1,0:T(8,128)(2,1)S(1)} %constant_dynamic-update-slice_fusion, s32[]{:T(128)S(6)} %select_n.75), kind=kOutput, calls=%fused_computation.20 | convolution fusion | flops 403439360 | bytes 2491396 | tf_op jit(solution)/shard_map/dot_general | solution.py:131
  21.9 5.8 %convolution_convert_fusion = bf16[256,3072]{1,0:T(8,128)(2,1)} fusion(bf16[1024,3072]{1,0:T(8,128)(2,1)} %param.12, bf16[256,1024]{1,0:T(8,128)(2,1)S(1)} %get-tuple-element.14, f32[256]{0:T(256)S(1)} %add_rsqrt_fusion.3, f32[256]{0:T(256)S(1)} %broadcast_multiply_fusion.2), kind=kOutput, calls=%fused_computation.9 | convolution fusion | flops 1612447744 | bytes 8390656 | tf_op jit(solution)/shard_map/dot_general | solution.py:49
  27.7 2.6 %copy.62 = bf16[256,3072]{0,1:T(8,128)(2,1)} copy(bf16[256,3072]{1,0:T(8,128)(2,1)} %convolution_convert_fusion) | data formatting | bytes 3145728 | tf_op jit(solution)/shard_map/convert_element_type | solution.py:49
  30.3 1.5 %fusion.22 = (f32[256,16]{0,1:T(8,128)S(1)}, f32[256,16]{0,1:T(8,128)S(1)}) fusion(bf16[256,3,16,64]{0,3,2,1:T(8,128)(2,1)} %bitcast.169), kind=kLoop, calls=%fused_computation.60 | loop fusion | flops 1564672 | bytes 1081344 | tf_op jit(solution)/shard_map/reduce_sum | solution.py:25
  31.8 2.3 %fusion = (f32[16,256]{1,0:T(8,128)S(1)}, f32[16,256,256]{1,2,0:T(8,128)S(1)}) fusion(f32[256,16]{0,1:T(8,128)S(1)} %get-tuple-element.37, bf16[256,3,16,64]{0,3,2,1:T(8,128)(2,1)} %bitcast.170, f32[256,16]{0,1:T(8,128)S(1)} %get-tuple-element.38), kind=kOutput, calls=%fused_computation.10 | convolution fusion | flops 137883648 | bytes 5292032 | tf_op jit(solution)/shard_map/qhd,khd->hqk/dot_general | solution.py:31
  34.2 2.0 %fusion.3 = bf16[16,64,256]{2,1,0:T(8,128)(2,1)S(1)} fusion(f32[16,256,256]{1,2,0:T(8,128)S(1)} %get-tuple-element.16, f32[16,256]{1,0:T(8,128)S(1)} %get-tuple-element.15, bf16[256,3,16,64]{0,3,2,1:T(8,128)(2,1)} %bitcast.171), kind=kOutput, calls=%fused_computation.21 | convolution fusion | flops 137625600 | bytes 5259264 | tf_op jit(solution)/shard_map/hqk,khd->qhd/dot_general | solution.py:36
  37.1 1.0 %copy-done.1 = f32[256,1024]{1,0:T(8,128)} copy-done((f32[256,1024]{1,0:T(8,128)}, f32[256,1024]{1,0:T(8,128)S(1)}, u32[]{:S(2)}) %copy-start.1) | copy-done | bytes 1048600
  38.7 1.3 %convolution_convert_fusion.1 = bf16[51,3072]{1,0:T(8,128)(2,1)S(1)} fusion(bf16[1024,3072]{1,0:T(8,128)(2,1)S(1)} %bitcast.168, bf16[51,1024]{1,0:T(8,128)(2,1)S(1)} %gather_fusion.3, f32[51]{0:T(128)S(1)} %fusion.116, f32[51]{0:T(128)S(1)} %broadcast_multiply_fusion.4), kind=kOutput, calls=%fused_computation.11 | convolution fusion | flops 321229824 | bytes 6709656 | tf_op jit(solution)/shard_map/jvp()/dot_general | solution.py:49
  43.2 1.5 %scatter_fusion = bf16[256,1024]{1,0:T(8,128)(2,1)S(1)} fusion(bf16[256,1024]{1,0:T(8,128)(2,1)S(1)} %copy-done.2, s32[51]{0:T(128)S(1)} %copy-done.24, bf16[51,1024]{1,0:T(8,128)(2,1)S(1)} %fusion.19), kind=kCustom, calls=%fused_computation.6 | custom fusion | flops 52224 | bytes 313548 | tf_op jit(solution)/shard_map/jvp()/scatter-add | solution.py:55
  44.8 2.7 %convolution_convert_fusion.8 = bf16[256,768]{1,0:T(8,128)(2,1)} fusion(bf16[256,1024]{1,0:T(8,128)(2,1)S(1)} %scatter_fusion, bf16[1024,768]{1,0:T(8,128)(2,1)} %param.15), kind=kOutput, calls=%fused_computation.30 | convolution fusion | flops 402849792 | bytes 2490368 | tf_op jit(solution)/shard_map/jvp()/dot_general | solution.py:56
  47.5 1.2 %copy.57 = bf16[256,768]{0,1:T(8,128)(2,1)S(1)} copy(bf16[256,768]{1,0:T(8,128)(2,1)} %convolution_convert_fusion.8) | data formatting | bytes 786432 | tf_op jit(solution)/shard_map/jvp()/convert_element_type | solution.py:56
  48.7 1.3 %fusion.69 = f32[16,256,48]{1,2,0:T(8,128)S(1)} fusion(bf16[256,16,48]{0,2,1:T(8,128)(2,1)S(1)} %bitcast.176, bf16[3,16,48,48]{3,2,1,0:T(8,128)(2,1)} %param.16), kind=kOutput, calls=%fused_computation.140 | convolution fusion | flops 18874368 | bytes 1376256 | tf_op jit(solution)/shard_map/jvp(pgi,gio->pgo)/dot_general | solution.py:61
  50.0 1.2 %convolution_add_fusion.1 = f32[16,256,48]{1,2,0:T(8,128)S(1)} fusion(f32[16,256,48]{1,2,0:T(8,128)S(1)} %fusion.69, bf16[256,16,48]{0,2,1:T(8,128)(2,1)S(1)} %bitcast.177, bf16[3,16,48,48]{3,2,1,0:T(8,128)(2,1)} %param.16), kind=kOutput, calls=%fused_computation.23 | convolution fusion | flops 19070976 | bytes 2162688 | tf_op jit(solution)/shard_map/jvp(pgi,gio->pgo)/dot_general | solution.py:61
  51.3 1.4 %fusion.130 = (f32[256]{0:T(256)S(1)}, f32[16,256,48]{1,2,0:T(8,128)S(1)}) fusion(f32[16,256,48]{1,2,0:T(8,128)S(1)} %convolution_add_fusion.1, bf16[256,16,48]{0,2,1:T(8,128)(2,1)S(1)} %bitcast.178, bf16[3,16,48,48]{3,2,1,0:T(8,128)(2,1)} %param.16), kind=kOutput, calls=%fused_computation.251 | convolution fusion | flops 19267328 | bytes 2163712 | tf_op jit(solution)/shard_map/jvp(pgi,gio->pgo)/dot_general | solution.py:61
  52.8 1.2 %copy.61 = f32[256,768]{1,0:T(8,128)} copy(f32[256,768]{0,1:T(8,128)S(1)} %bitcast.172) | data formatting | bytes 1572864 | tf_op jit(solution)/shard_map/jvp()/reshape | solution.py:67
  54.0 5.2 %multiply_reduce_fusion = (f32[]{:T(128)}, f32[256,1024]{1,0:T(8,128)S(1)}) fusion(f32[256]{0:T(256)S(1)} %copy-done.26, f32[256]{0:T(256)S(1)} %add_rsqrt_fusion.2, f32[256,1024]{1,0:T(8,128)} %copy-done.1, f32[256]{0:T(256)S(1)} %broadcast_multiply_fusion.1, bf16[768,1024]{1,0:T(8,128)(2,1)} %param.17, bf16[256,768]{1,0:T(8,128)(2,1)S(1)} %copy-done.16, ...), kind=kOutput, calls=%fused_computation.66 | convolution fusion | flops 418709504 | bytes 4854788 | tf_op jit(solution)/shard_map/jvp()/dot_general | solution.py:69
  59.2 3.3 %multiply_reduce_fusion.2 = (f32[256]{0:T(256)S(1)}, bf16[256,768]{1,0:T(8,128)(2,1)S(1)}) fusion(f32[256,768]{1,0:T(8,128)S(1)} %copy-done.3, f32[256]{0:T(256)S(1)} %broadcast_multiply_fusion.3, f32[256]{0:T(256)S(1)} %fusion.111, bf16[768,1024]{1,0:T(8,128)(2,1)S(1)} %copy-done.27, f32[256,1024]{1,0:T(8,128)S(1)} %get-tuple-element.34, f32[256]{0:T(256)S(1)} %copy-done.25), kind=kOutput, calls=%fused_computation.90 | convolution fusion | flops 419495680 | bytes 3805184 | tf_op jit(solution)/shard_map/transpose(jvp())/dot_general | solution.py:69
  62.5 2.5 %fusion.126 = (f32[256]{0:T(256)S(1)}, f32[256,768]{1,0:T(8,128)S(1)}) fusion(f32[256]{0:T(256)S(1)} %multiply_multiply_fusion.8, bf16[256,768]{1,0:T(8,128)(2,1)S(1)} %get-tuple-element.24, f32[256]{0:T(256)S(1)} %fusion.111, f32[256,768]{1,0:T(8,128)S(1)} %copy-done.3, f32[256]{0:T(256)S(1)} %broadcast_multiply_fusion.3), kind=kLoop, calls=%fused_computation.247 | loop fusion | flops 15531776 | bytes 1970176 | tf_op jit(solution)/shard_map/transpose(jvp())/reduce_sum | solution.py:19
  66.0 1.2 %copy.64 = bf16[256,768]{0,1:T(8,128)(2,1)S(1)} copy(bf16[256,768]{1,0:T(8,128)(2,1)} %broadcast_add_fusion) | data formatting | bytes 786432 | tf_op jit(solution)/shard_map/transpose(jvp())/add_any | solution.py:18
  68.4 2.1 %convolution_convert_fusion.2 = bf16[256,1024]{1,0:T(8,128)(2,1)S(1)} fusion(bf16[1024,768]{1,0:T(8,128)(2,1)} %param.15, bf16[256,768]{1,0:T(8,128)(2,1)} %copy-done.11, bf16[256,768]{1,0:T(8,128)(2,1)S(1)} %copy.68), kind=kOutput, calls=%fused_computation.24 | convolution fusion | flops 403111936 | bytes 2883584 | tf_op jit(solution)/shard_map/transpose(jvp())/dot_general | solution.py:56
  72.3 1.4 %fusion.16 = bf16[51,1,16,64]{3,0,2,1:T(8,128)(2,1)S(1)} fusion(bf16[51,16,64]{2,1,0:T(8,128)(2,1)S(1)} %reshape.309, f32[16,51,51]{1,2,0:T(8,128)} %copy-done.14, f32[16,51]{1,0:T(8,128)S(1)} %get-tuple-element.19), kind=kOutput, calls=%fused_computation.51 | convolution fusion | flops 5462304 | bytes 378624 | tf_op jit(solution)/shard_map/transpose(jvp(hqk,khd->qhd))/dot_general | solution.py:36
  76.4 5.0 %fusion.81 = (f32[51]{0:T(128)S(1)}, f32[51,1024]{1,0:T(8,128)S(1)}) fusion(bf16[51,1024]{1,0:T(8,128)(2,1)S(1)} %gather_fusion.3, f32[51]{0:T(128)S(1)} %broadcast_multiply_fusion.4, bf16[51,3072]{1,0:T(8,128)(2,1)S(1)} %reshape.310, bf16[1024,3072]{1,0:T(8,128)(2,1)} %param.12), kind=kOutput, calls=%fused_computation.158 | convolution fusion | flops 321177536 | bytes 6918552 | tf_op jit(solution)/shard_map/transpose(jvp())/dot_general | solution.py:49
  81.8 2.4 %collective-permute-start.3 = (bf16[51,1024]{1,0:T(8,128)(2,1)S(1)}, bf16[51,1024]{1,0:T(8,128)(2,1)S(1)}, u32[]{:S(2)}, u32[]{:S(2)}) collective-permute-start(bf16[51,1024]{1,0:T(8,128)(2,1)S(1)} %fusion.104), channel_id=1, source_target_pairs={{0,3},{1,0},{2,1},{3,2},{4,7},{5,4},{6,5},{7,6},{8,11},{9,8},{10,9... | collective-permute-start | bytes 313352 | tf_op jit(solution)/shard_map/ppermute | solution.py:90
  84.2 1.5 %collective-permute-start.4 = (bf16[51,1024]{1,0:T(8,128)(2,1)S(1)}, bf16[51,1024]{1,0:T(8,128)(2,1)S(1)}, u32[]{:S(2)}, u32[]{:S(2)}) collective-permute-start(bf16[51,1024]{1,0:T(8,128)(2,1)S(1)} %fusion.104), channel_id=1, source_target_pairs={{0,2},{1,3},{2,0},{3,1},{4,6},{5,7},{6,4},{7,5},{8,10},{9,11},{10,... | collective-permute-start | bytes 313352 | tf_op jit(solution)/shard_map/ppermute | solution.py:90
  85.8 1.1 %dynamic_slice.10 = bf16[256,192]{1,0:T(8,128)(2,1)S(1)} dynamic-slice(bf16[512,768]{1,0:T(8,128)(2,1)} %copy-done.19, s32[]{:T(128)S(6)} %select_n.76, s32[]{:T(128)S(6)} %select_n.78), dynamic_slice_sizes={256,192} | dynamic-slice | bytes 196612 | tf_op jit(solution)/shard_map/dynamic_slice | solution.py:152
  86.8 1.0 %gather_fusion.1 = bf16[204,192]{1,0:T(8,128)(2,1)S(1)} fusion(bf16[256,192]{1,0:T(8,128)(2,1)S(1)} %dynamic_slice.10, s32[1024]{0:T(1024)S(1)} %pad_clamp_fusion.1), kind=kCustom, calls=%fused_computation.1 | custom fusion | bytes 157488 | tf_op jit(solution)/shard_map/gather | solution.py:153
  88.5 1.6 %collective-permute-done.4 = bf16[51,1024]{1,0:T(8,128)(2,1)S(1)} collective-permute-done((bf16[51,1024]{1,0:T(8,128)(2,1)S(1)}, bf16[51,1024]{1,0:T(8,128)(2,1)S(1)}, u32[]{:S(2)}, u32[]{:S(2)}) %collective-permute-start.4) | collective-permute-done | bytes 104480 | tf_op jit(solution)/shard_map/ppermute | solution.py:90
  90.1 1.3 %collective-permute-done.5 = bf16[51,1024]{1,0:T(8,128)(2,1)S(1)} collective-permute-done((bf16[51,1024]{1,0:T(8,128)(2,1)S(1)}, bf16[51,1024]{1,0:T(8,128)(2,1)S(1)}, u32[]{:S(2)}, u32[]{:S(2)}) %collective-permute-start.5) | collective-permute-done | bytes 104480 | tf_op jit(solution)/shard_map/ppermute | solution.py:90
  91.4 1.2 %fusion.61 = f32[192,1024]{1,0:T(8,128)} fusion(bf16[204,192]{1,0:T(8,128)(2,1)S(1)} %gather_fusion.1, bf16[51,1024]{1,0:T(8,128)(2,1)S(1)} %collective-permute-done.5, bf16[51,1024]{1,0:T(8,128)(2,1)S(1)} %collective-permute-done.4, bf16[51,1024]{1,0:T(8,128)(2,1)S(1)} %collective-permute-done.3, bf16[51,1024]{1,0:T(8,128)(2,1)S(1)} %fusion.104), kind=kOutput, calls=%fused_computation.132 | convolution fusion | flops 81887232 | bytes 1282560 | tf_op jit(solution)/shard_map/vc,vd->cd/dot_general | solution.py:154
  (142 shorter events, 24.1 us)
Async XLA Ops:
  0.6 35.6 %copy-start = (bf16[1024,1024]{1,0:T(8,128)(2,1)S(1)}, bf16[1024,1024]{1,0:T(8,128)(2,1)}, u32[]{:S(2)}) copy-start(bf16[1024,1024]{1,0:T(8,128)(2,1)} %param.13) | copy-start | bytes 6291460
  0.6 9.0 %copy-start.22 = (bf16[1024]{0:T(1024)(128)(2,1)S(1)}, bf16[1024]{0:T(1024)(128)(2,1)}, u32[]{:S(2)}) copy-start(bf16[1024]{0:T(1024)(128)(2,1)} %param.14) | copy-start | bytes 6148
  0.7 12.5 %collective-permute-start = (bf16[64,768]{1,0:T(8,128)(2,1)}, bf16[64,768]{1,0:T(8,128)(2,1)}, u32[]{:S(2)}, u32[]{:S(2)}) collective-permute-start(bf16[64,768]{1,0:T(8,128)(2,1)} %param.9), channel_id=1, source_target_pairs={{0,3},{1,0},{2,1},{3,2},{4,7},{5,4},{6,5},{7,6},{8,11},{9,8},{10,9... | collective-permute-start | bytes 294920 | tf_op jit(solution)/shard_map/ppermute | solution.py:90
  4.6 9.4 %collective-permute-start.1 = (bf16[64,768]{1,0:T(8,128)(2,1)}, bf16[64,768]{1,0:T(8,128)(2,1)}, u32[]{:S(2)}, u32[]{:S(2)}) collective-permute-start(bf16[64,768]{1,0:T(8,128)(2,1)} %param.9), channel_id=1, source_target_pairs={{0,2},{1,3},{2,0},{3,1},{4,6},{5,7},{6,4},{7,5},{8,10},{9,11},{10,... | collective-permute-start | bytes 294920 | tf_op jit(solution)/shard_map/ppermute | solution.py:90
  5.1 9.8 %collective-permute-start.2 = (bf16[64,768]{1,0:T(8,128)(2,1)}, bf16[64,768]{1,0:T(8,128)(2,1)}, u32[]{:S(2)}, u32[]{:S(2)}) collective-permute-start(bf16[64,768]{1,0:T(8,128)(2,1)} %param.9), channel_id=1, source_target_pairs={{0,1},{1,2},{2,3},{3,0},{4,5},{5,6},{6,7},{7,4},{8,9},{9,10},{10,1... | collective-permute-start | bytes 294920 | tf_op jit(solution)/shard_map/ppermute | solution.py:90
  6.4 4.1 %copy-start.23 = (s32[51]{0:T(128)}, s32[51]{0:T(128)S(1)}, u32[]{:S(2)}) copy-start(s32[51]{0:T(128)S(1)} %fusion.114) | copy-start | bytes 616
  8.8 3.1 %copy-start.18 = (s32[4,51]{1,0:T(4,128)S(1)}, s32[4,51]{1,0:T(4,128)}, u32[]{:S(2)}) copy-start(s32[4,51]{1,0:T(4,128)} %param.10) | copy-start | bytes 2452
  8.8 4.3 %copy-start.17 = (bf16[64,768]{1,0:T(8,128)(2,1)S(1)}, bf16[64,768]{1,0:T(8,128)(2,1)}, u32[]{:S(2)}) copy-start(bf16[64,768]{1,0:T(8,128)(2,1)} %param.9) | copy-start | bytes 294916
  9.5 11.4 %copy-start.5 = (u32[51,1024]{1,0:T(8,128)}, u32[51,1024]{1,0:T(8,128)S(1)}, u32[]{:S(2)}) copy-start(u32[51,1024]{1,0:T(8,128)S(1)} %gather_fusion.2) | copy-start | bytes 626692
  18.6 2.4 %copy-start.19 = (bf16[512,768]{1,0:T(8,128)(2,1)}, bf16[512,768]{1,0:T(8,128)(2,1)S(1)}, u32[]{:S(2)}) copy-start(bf16[512,768]{1,0:T(8,128)(2,1)S(1)} %constant_dynamic-update-slice_fusion) | copy-start | bytes 2359300
  31.8 6.9 %slice-start = ((s8[6291456]{0:T(1024)(128)(4,1)}), s8[4194304]{0:T(1024)(128)(4,1)S(1)}, s32[]{:S(2)}) async-start(s8[6291456]{0:T(1024)(128)(4,1)} %bitcast.167), calls=%async_computation | async-start | bytes 8388608
  34.2 4.5 %slice-start.1 = ((s8[6291456]{0:T(1024)(128)(4,1)}), s8[2097152]{0:T(1024)(128)(4,1)S(1)}, s32[]{:S(2)}) async-start(s8[6291456]{0:T(1024)(128)(4,1)} %bitcast.167), calls=%async_computation.1 | async-start | bytes 4194304
  40.5 1.3 %copy-start.9 = (bf16[51,1,16,64]{3,2,1,0:T(8,128)(2,1)}, bf16[51,1,16,64]{3,2,1,0:T(8,128)(2,1)S(1)}, u32[]{:S(2)}) copy-start(bf16[51,1,16,64]{3,2,1,0:T(8,128)(2,1)S(1)} %get-tuple-element.10) | copy-start | bytes 313348
  40.5 1.3 %copy-start.12 = (bf16[51,1,16,64]{3,2,1,0:T(8,128)(2,1)}, bf16[51,1,16,64]{3,2,1,0:T(8,128)(2,1)S(1)}, u32[]{:S(2)}) copy-start(bf16[51,1,16,64]{3,2,1,0:T(8,128)(2,1)S(1)} %get-tuple-element.8) | copy-start | bytes 313348
  42.2 1.0 %copy-start.24 = (s32[51]{0:T(128)S(1)}, s32[51]{0:T(128)}, u32[]{:S(2)}) copy-start(s32[51]{0:T(128)} %copy-done.23) | copy-start | bytes 616
  51.2 2.7 %copy-start.26 = (f32[256]{0:T(256)S(1)}, f32[256]{0:T(256)}, u32[]{:S(2)}) copy-start(f32[256]{0:T(256)} %get-tuple-element.12) | copy-start | bytes 3076
  52.6 1.4 %copy-start.16 = (bf16[256,768]{1,0:T(8,128)(2,1)S(1)}, bf16[256,768]{1,0:T(8,128)(2,1)}, u32[]{:S(2)}) copy-start(bf16[256,768]{1,0:T(8,128)(2,1)} %convolution_convert_fusion.8) | copy-start | bytes 1179652
  54.0 5.2 %copy-start.3 = (f32[256,768]{1,0:T(8,128)S(1)}, f32[256,768]{1,0:T(8,128)}, u32[]{:S(2)}) copy-start(f32[256,768]{1,0:T(8,128)} %copy.61) | copy-start | bytes 2359300
  54.0 5.2 %copy-start.25 = (f32[256]{0:T(256)S(1)}, f32[256]{0:T(256)}, u32[]{:S(2)}) copy-start(f32[256]{0:T(256)} %get-tuple-element.11) | copy-start | bytes 3076
  54.0 5.2 %copy-start.27 = (bf16[768,1024]{1,0:T(8,128)(2,1)S(1)}, bf16[768,1024]{1,0:T(8,128)(2,1)}, u32[]{:S(2)}) copy-start(bf16[768,1024]{1,0:T(8,128)(2,1)} %param.17) | copy-start | bytes 4718596
  62.5 2.6 %copy-start.11 = (bf16[256,768]{1,0:T(8,128)(2,1)}, bf16[256,768]{1,0:T(8,128)(2,1)S(1)}, u32[]{:S(2)}) copy-start(bf16[256,768]{1,0:T(8,128)(2,1)S(1)} %get-tuple-element.24) | copy-start | bytes 1179652
  62.5 4.6 %copy-start.4 = (bf16[3,16,48,48]{3,2,1,0:T(8,128)(2,1)S(1)}, bf16[3,16,48,48]{3,2,1,0:T(8,128)(2,1)}, u32[]{:S(2)}) copy-start(bf16[3,16,48,48]{3,2,1,0:T(8,128)(2,1)} %param.16) | copy-start | bytes 663556
  68.4 2.8 %copy-start.20 = (pred[51]{0:T(512)(128)(4,1)S(1)}, pred[51]{0:T(512)(128)(4,1)}, u32[]{:S(2)}) copy-start(pred[51]{0:T(512)(128)(4,1)} %get-tuple-element.4) | copy-start | bytes 157
  71.3 2.4 %copy-start.13 = (bf16[51,1,16,64]{3,2,1,0:T(8,128)(2,1)S(1)}, bf16[51,1,16,64]{3,2,1,0:T(8,128)(2,1)}, u32[]{:S(2)}) copy-start(bf16[51,1,16,64]{3,2,1,0:T(8,128)(2,1)} %copy-done.12) | copy-start | bytes 313348
  72.0 1.9 %copy-start.8 = (bf16[51,1,16,64]{3,2,1,0:T(8,128)(2,1)S(1)}, bf16[51,1,16,64]{3,2,1,0:T(8,128)(2,1)}, u32[]{:S(2)}) copy-start(bf16[51,1,16,64]{3,2,1,0:T(8,128)(2,1)} %copy-done.7) | copy-start | bytes 313348
  72.1 1.9 %copy-start.10 = (bf16[51,1,16,64]{3,2,1,0:T(8,128)(2,1)S(1)}, bf16[51,1,16,64]{3,2,1,0:T(8,128)(2,1)}, u32[]{:S(2)}) copy-start(bf16[51,1,16,64]{3,2,1,0:T(8,128)(2,1)} %copy-done.9) | copy-start | bytes 313348
  72.3 1.4 %copy-start.15 = (f32[16,51,51]{1,2,0:T(8,128)S(1)}, f32[16,51,51]{1,2,0:T(8,128)}, u32[]{:S(2)}) copy-start(f32[16,51,51]{1,2,0:T(8,128)} %copy-done.14) | copy-start | bytes 499396
  76.4 5.3 %copy-start.6 = (u32[51,1024]{1,0:T(8,128)S(1)}, u32[51,1024]{1,0:T(8,128)}, u32[]{:S(2)}) copy-start(u32[51,1024]{1,0:T(8,128)} %copy-done.5) | copy-start | bytes 626692
  76.4 9.4 %copy-start.21 = (s32[204,1]{0,1:T(1,128)S(1)}, s32[204,1]{0,1:T(1,128)}, u32[]{:S(2)}) copy-start(s32[204,1]{0,1:T(1,128)} %compare_select_fusion.1) | copy-start | bytes 2452
  81.8 6.7 %collective-permute-start.3 = (bf16[51,1024]{1,0:T(8,128)(2,1)S(1)}, bf16[51,1024]{1,0:T(8,128)(2,1)S(1)}, u32[]{:S(2)}, u32[]{:S(2)}) collective-permute-start(bf16[51,1024]{1,0:T(8,128)(2,1)S(1)} %fusion.104), channel_id=1, source_target_pairs={{0,3},{1,0},{2,1},{3,2},{4,7},{5,4},{6,5},{7,6},{8,11},{9,8},{10,9... | collective-permute-start | bytes 313352 | tf_op jit(solution)/shard_map/ppermute | solution.py:90
  84.2 5.9 %collective-permute-start.4 = (bf16[51,1024]{1,0:T(8,128)(2,1)S(1)}, bf16[51,1024]{1,0:T(8,128)(2,1)S(1)}, u32[]{:S(2)}, u32[]{:S(2)}) collective-permute-start(bf16[51,1024]{1,0:T(8,128)(2,1)S(1)} %fusion.104), channel_id=1, source_target_pairs={{0,2},{1,3},{2,0},{3,1},{4,6},{5,7},{6,4},{7,5},{8,10},{9,11},{10,... | collective-permute-start | bytes 313352 | tf_op jit(solution)/shard_map/ppermute | solution.py:90
  85.7 5.7 %collective-permute-start.5 = (bf16[51,1024]{1,0:T(8,128)(2,1)S(1)}, bf16[51,1024]{1,0:T(8,128)(2,1)S(1)}, u32[]{:S(2)}, u32[]{:S(2)}) collective-permute-start(bf16[51,1024]{1,0:T(8,128)(2,1)S(1)} %fusion.104), channel_id=1, source_target_pairs={{0,1},{1,2},{2,3},{3,0},{4,5},{5,6},{6,7},{7,4},{8,9},{9,10},{10,1... | collective-permute-start | bytes 313352 | tf_op jit(solution)/shard_map/ppermute | solution.py:90
  (4 other events, 3.8 us)

commit v2 on v1

--- a/solution.py
+++ b/solution.py
@@ -45,22 +45,49 @@
 
 def attention_branch(inputs, w_qkv, w_out):
     row_count = inputs.shape[0]
+    head_dim = D // HEADS
     normed = row_norm(inputs.astype(jnp.float32)).astype(jnp.bfloat16)
-    projected = jnp.dot(normed, w_qkv, preferred_element_type=jnp.float32).astype(jnp.bfloat16)
-    context = split_project(projected.reshape(row_count, 3, HEADS, D // HEADS))
+    projected = jnp.einsum(
+        "sd,dk->ks", normed, w_qkv, preferred_element_type=jnp.float32
+    ).astype(jnp.bfloat16)
+    projected = projected.reshape(3, HEADS, head_dim, row_count)
+    queries = head_norm_cols(projected[0].astype(jnp.float32)).astype(jnp.bfloat16)
+    key_rows = head_norm_cols(projected[1].astype(jnp.float32)).astype(jnp.bfloat16)
+    score_scale = 1.0 / math.sqrt(head_dim)
+    scores = (
+        jnp.einsum("hdq,hdk->hqk", queries, key_rows, preferred_element_type=jnp.float32)
+        * score_scale
+    )
+    exponent = jnp.exp(scores)
+    weights = (exponent / jnp.sum(exponent, axis=-1, keepdims=True)).astype(jnp.bfloat16)
+    context = jnp.einsum(
+        "hqk,hdk->qhd", weights, projected[2], preferred_element_type=jnp.float32
+    ).astype(jnp.bfloat16)
     return jnp.dot(context.reshape(row_count, D), w_out, preferred_element_type=jnp.float32)
 
 
-def decoder_output(visible_out, positions, total_rows, mask_embed, dec_in, conv_w, dec_out):
+def head_norm_cols(values):
+    return values * lax.rsqrt(jnp.mean(values * values, axis=-2, keepdims=True) + EPSILON)
+
+
+def decoder_output(visible_out, positions, true_rows, mask_embed, dec_in, conv_w, dec_out):
+    total_rows = true_rows.shape[0]
     canvas = jnp.broadcast_to(mask_embed, (total_rows, D)).at[positions].set(visible_out)
     lowered = jnp.dot(canvas, dec_in, preferred_element_type=jnp.float32).astype(jnp.bfloat16)
     grouped = lowered.reshape(total_rows, GROUPS, DD // GROUPS)
-    padded = jnp.pad(grouped, ((1, 1), (0, 0), (0, 0)))
+    has_prev = (true_rows > 0)[:, None, None]
+    has_next = (true_rows < total_rows - 1)[:, None, None]
+    zero = jnp.zeros_like(grouped)
+    shifted = (
+        jnp.where(has_prev, jnp.roll(grouped, 1, axis=0), zero),
+        grouped,
+        jnp.where(has_next, jnp.roll(grouped, -1, axis=0), zero),
+    )
     convolved = jnp.zeros((total_rows, GROUPS, DD // GROUPS), jnp.float32)
     for offset in range(3):
         convolved = convolved + jnp.einsum(
             "pgi,gio->pgo",
-            padded[offset : offset + total_rows],
+            shifted[offset],
             conv_w[offset],
             preferred_element_type=jnp.float32,
         )
@@ -69,13 +96,15 @@
     return jnp.dot(hidden, dec_out, preferred_element_type=jnp.float32)
 
 
-def copy_terms(visible_in, positions, targets, w_qkv, w_out, mask_embed, dec_in, conv_w, dec_out):
+def copy_terms(
+    visible_in, positions, true_rows, targets, w_qkv, w_out, mask_embed, dec_in, conv_w, dec_out
+):
     total_rows = targets.shape[0]
     visible_out = (
         visible_in.astype(jnp.float32) + attention_branch(visible_in, w_qkv, w_out)
     ).astype(jnp.bfloat16)
     predicted = decoder_output(
-        visible_out, positions, total_rows, mask_embed, dec_in, conv_w, dec_out
+        visible_out, positions, true_rows, mask_embed, dec_in, conv_w, dec_out
     )
     slot_ids = jnp.arange(total_rows, dtype=jnp.int32)
     seen = jnp.max((slot_ids[:, None] == positions[None, :]).astype(jnp.float32), axis=1)
@@ -89,13 +118,6 @@
         pairs = [(source, (source - shift) % group_size) for source in range(group_size)]
         parts.append(lax.ppermute(values, "mask", pairs))
     return jnp.concatenate(parts, axis=0)
-
-
-def unroll_blocks(rotated, own_index, block_rows):
-    total_rows = rotated.shape[0]
-    doubled = jnp.concatenate([rotated, rotated], axis=0)
-    start = total_rows - own_index * block_rows
-    return lax.dynamic_slice_in_dim(doubled, start, total_rows, 0)
 
 
 def split_teacher(embedded, w_qkv, w_out, own_index, group_size):
@@ -126,8 +148,11 @@
     visible_count = visible_index.shape[1]
     total_rows = tok_rows * group_size
     col_width = patches.shape[1] // group_size
-    positions = lax.dynamic_index_in_dim(visible_index, own_index, 0, keepdims=False)
-    clip_pixels = unroll_blocks(ring_gather(patches, group_size), own_index, tok_rows)
+    offset = own_index * tok_rows
+    true_rows = (jnp.arange(total_rows, dtype=jnp.int32) + offset) % total_rows
+    rotated_index = (visible_index - offset) % total_rows
+    positions = lax.dynamic_index_in_dim(rotated_index, own_index, 0, keepdims=False)
+    clip_pixels = ring_gather(patches, group_size)
     embedded = jnp.dot(clip_pixels, embed_w, preferred_element_type=jnp.float32).astype(
         jnp.bfloat16
     )
@@ -140,7 +165,7 @@
 
     def objective(rows_in):
         return copy_terms(
-            rows_in, positions, all_targets, w_qkv, w_out, mask_embed, dec_in, conv_w, dec_out
+            rows_in, positions, true_rows, all_targets, w_qkv, w_out, mask_embed, dec_in, conv_w, dec_out
         )
 
     squares, pullback = jax.vjp(objective, visible_in)
@@ -148,7 +173,7 @@
     (grad_in,) = pullback(jnp.ones_like(squares) * factor)
     copy_loss = jnp.reshape(squares / ((total_rows - visible_count) * D), (1,))
     slot_copy = (own_index + jnp.arange(group_size, dtype=jnp.int32)) % group_size
-    flat_index = visible_index[slot_copy].reshape(copies * visible_count)
+    flat_index = rotated_index[slot_copy].reshape(copies * visible_count)
     own_cols = lax.dynamic_slice_in_dim(clip_pixels, own_index * col_width, col_width, 1)
     gathered = own_cols[flat_index]
     embed_grad = jnp.einsum(

time: 94.5 us -> 113 us (1.20)
  local copies, waits for them, and re-layouts: 20.8 us -> 33.1 us
  matrix products: 43.5 us -> 48.7 us
    slice x1 -> x7, local copies, waits for them, and re-layouts: 0.11 us -> 6.25 us  [the longest x4 3 us: decoder_output(): jnp.roll(grouped, -1, axis=0)]
    dot_general x17, matrix products: 24.6 us -> 28.8 us  [the longest x3 13.7 us: attention_branch(): jnp.einsum('sd,dk->ks', normed, w_qkv, preferred_element_type=jnp.float32)]
    unnamed x67 -> x101, local copies, waits for them, and re-layouts: 6.37 us -> 8.26 us
    convert_element_type x2 -> x5, local copies, waits for them, and re-layouts: 2.62 us -> 4.43 us  [the longest x2 2.72 us: attention_branch(): projected[0].astype(jnp.float32)]
    reshape x2, local copies, waits for them, and re-layouts: 0.35 us -> 2.04 us  [attention_branch(): context.reshape(row_count, D)]
    convert_element_type x0 -> x1, other arithmetic: none -> 1.6 us  [attention_branch(): projected[1].astype(jnp.float32)]
    scatter-add x1, other arithmetic: 1.53 us -> 2.91 us  [decoder_output(): jnp.broadcast_to(mask_embed, (total_rows, D)).at[positions].set(visible_out)]
where the time goes in v2:
time: 113 us; the launch traced here: 112 us
  matrix products  48.7 us (43%)
  local copies, waits for them, and re-layouts  33.1 us (29%)
  other arithmetic  15.4 us (14%)
  starting transfers between devices  8.98 us (8%)
  between operations  3.32 us (3%)
  waiting for transfers between devices  2.84 us (3%)
    dot_general x3, matrix products, attention_branch(): jnp.einsum('sd,dk->ks', normed, w_qkv, preferred_element_type=jnp.float32)  13.7 us
    ppermute x6, starting transfers between devices, ring_gather(): parts.append(lax.ppermute(values, 'mask', pairs))  8.98 us
    dot_general x2, matrix products, decoder_output(): return jnp.dot(hidden, dec_out, preferred_element_type=jnp.float32)  8.72 us
    unnamed x101, local copies, waits for them, and re-layouts  8.26 us
    dot_general x6, matrix products, decoder_output(): jnp.einsum('pgi,gio->pgo', shifted[offset], conv_w[offset], preferred_ele...  7.67 us
    dot_general x2, matrix products, decoder_output(): jnp.dot(canvas, dec_in, preferred_element_type=jnp.float32)  4.46 us
    dot_general x4, matrix products, attention_branch(): jnp.einsum('hdq,hdk->hqk', queries, key_rows, preferred_element_type=jnp....  3.79 us
    dot_general x4, matrix products, attention_branch(): jnp.einsum('hqk,hdk->qhd', weights, projected[2], preferred_element_type=...  3.7 us
  transfers between devices with their start and end apart: 6, of which 2 were waited for; matrix products, arithmetic and copies ran while one was open for 12% of the time, Pallas kernels for 0%

profile of v2, /device:TPU:0, one launch (start us, length us, event | category | flops | bytes accessed | tf_op | source)
XLA Modules:
  0.0 112.4 jit_solution(5056874926023706446)
XLA Ops:
  0.7 4.0 %collective-permute-start = (bf16[64,768]{1,0:T(8,128)(2,1)}, bf16[64,768]{1,0:T(8,128)(2,1)}, u32[]{:S(2)}, u32[]{:S(2)}) collective-permute-start(bf16[64,768]{1,0:T(8,128)(2,1)} %param.9), channel_id=1, source_target_pairs={{0,3},{1,0},{2,1},{3,2},{4,7},{5,4},{6,5},{7,6},{8,11},{9,8},{10,9... | collective-permute-start | bytes 294920 | tf_op jit(solution)/shard_map/ppermute | solution.py:119
  5.7 1.6 %constant_dynamic-update-slice_fusion.3 = bf16[256,768]{1,0:T(8,128)(2,1)} fusion(bf16[64,768]{1,0:T(8,128)(2,1)} %param.9), kind=kLoop, calls=%fused_computation.191 | loop fusion | bytes 196608
  13.9 1.5 %constant_dynamic-update-slice_fusion.2 = bf16[256,768]{1,0:T(8,128)(2,1)} fusion(bf16[256,768]{1,0:T(8,128)(2,1)} %constant_dynamic-update-slice_fusion.3, bf16[64,768]{1,0:T(8,128)(2,1)} %collective-permute-done), kind=kLoop, calls=%fused_computation.190 | loop fusion | bytes 196608
  15.4 1.5 %constant_dynamic-update-slice_fusion.1 = bf16[256,768]{1,0:T(8,128)(2,1)} fusion(bf16[256,768]{1,0:T(8,128)(2,1)} %constant_dynamic-update-slice_fusion.2, bf16[64,768]{1,0:T(8,128)(2,1)} %collective-permute-done.1), kind=kLoop, calls=%fused_computation.189 | loop fusion | bytes 196608
  17.0 1.5 %constant_dynamic-update-slice_fusion = bf16[256,768]{1,0:T(8,128)(2,1)} fusion(bf16[256,768]{1,0:T(8,128)(2,1)} %constant_dynamic-update-slice_fusion.1, bf16[64,768]{1,0:T(8,128)(2,1)} %collective-permute-done.2), kind=kLoop, calls=%fused_computation.188 | loop fusion | bytes 196608 | tf_op jit(solution)/shard_map/concatenate | solution.py:120
  18.5 2.8 %convert_reduce_fusion = (f32[256]{0:T(256)}, bf16[256,1024]{1,0:T(8,128)(2,1)S(1)}) fusion(bf16[256,768]{1,0:T(8,128)(2,1)} %constant_dynamic-update-slice_fusion, bf16[768,1024]{1,0:T(8,128)(2,1)} %param.11), kind=kOutput, calls=%fused_computation.18 | convolution fusion | flops 403439360 | bytes 2491392 | tf_op jit(solution)/shard_map/dot_general | solution.py:156
  23.4 4.0 %fusion.2 = bf16[3072,51]{0,1:T(8,128)(2,1)S(1)} fusion(bf16[1024,3072]{1,0:T(8,128)(2,1)} %param.12, bf16[51,1024]{1,0:T(8,128)(2,1)S(1)} %gather_fusion.3, f32[51]{0:T(128)S(1)} %fusion.114, f32[51]{0:T(128)S(1)} %broadcast_multiply_fusion.4), kind=kOutput, calls=%fused_computation.13 | convolution fusion | flops 321229824 | bytes 6709656 | tf_op jit(solution)/shard_map/jvp(sd,dk->ks)/dot_general | solution.py:50
  30.9 2.9 %scatter_fusion = bf16[256,1024]{1,0:T(8,128)(2,1)} fusion(bf16[256,1024]{1,0:T(8,128)(2,1)} %compare_select_fusion, s32[51]{0:T(128)S(1)} %copy-done.40, bf16[51,1024]{1,0:T(8,128)(2,1)S(1)} %fusion.23), kind=kCustom, calls=%fused_computation.6 | custom fusion | flops 52224 | bytes 313548 | tf_op jit(solution)/shard_map/jvp()/scatter-add | solution.py:75
  33.8 2.2 %convolution_convert_fusion.8 = bf16[256,768]{1,0:T(8,128)(2,1)S(1)} fusion(bf16[256,1024]{1,0:T(8,128)(2,1)} %scatter_fusion, bf16[1024,768]{1,0:T(8,128)(2,1)} %param.15), kind=kOutput, calls=%fused_computation.28 | convolution fusion | flops 402849792 | bytes 2490368 | tf_op jit(solution)/shard_map/jvp()/dot_general | solution.py:76
  38.3 4.7 %fusion = bf16[3072,256]{0,1:T(8,128)(2,1)S(1)} fusion(bf16[1024,3072]{1,0:T(8,128)(2,1)} %param.12, bf16[256,1024]{1,0:T(8,128)(2,1)S(1)} %copy-done.7, f32[256]{0:T(256)S(1)} %add_rsqrt_fusion.3, f32[256]{0:T(256)S(1)} %broadcast_multiply_fusion.2), kind=kOutput, calls=%fused_computation.10 | convolution fusion | flops 1612447744 | bytes 8390656 | tf_op jit(solution)/shard_map/sd,dk->ks/dot_general | solution.py:50
  43.0 1.6 %slice_convert_fusion = (f32[1024,256]{0,1:T(8,128)}, f32[1024,256]{0,1:T(8,128)}, bf16[1024,256]{0,1:T(8,128)(2,1)}) fusion(bf16[3072,256]{0,1:T(8,128)(2,1)S(1)} %fusion), kind=kLoop, calls=%fused_computation.101 | loop fusion | flops 524288 | bytes 4194304 | tf_op jit(solution)/shard_map/convert_element_type | solution.py:55
  44.6 1.6 %copy.198 = f32[1024,256]{1,0:T(8,128)S(1)} copy(f32[1024,256]{0,1:T(8,128)} %get-tuple-element.8) | data formatting | bytes 2097152 | tf_op jit(solution)/shard_map/convert_element_type | solution.py:55
  46.3 2.6 %copy.197 = f32[1024,256]{1,0:T(8,128)} copy(f32[1024,256]{0,1:T(8,128)} %get-tuple-element.9) | data formatting | bytes 2097152 | tf_op jit(solution)/shard_map/convert_element_type | solution.py:54
  48.9 1.3 %multiply_reduce_fusion.3 = f32[16,256]{1,0:T(8,128)S(1)} fusion(f32[1024,256]{1,0:T(8,128)} %copy.197), kind=kLoop, calls=%fused_computation.68 | loop fusion | flops 520192 | bytes 1064960 | tf_op jit(solution)/shard_map/reduce_sum | solution.py:70
  50.2 2.0 %copy.196 = bf16[1024,256]{1,0:T(8,128)(2,1)} copy(bf16[1024,256]{0,1:T(8,128)(2,1)} %get-tuple-element.10) | data formatting | bytes 1048576 | tf_op jit(solution)/shard_map/slice | solution.py:64
  52.3 2.2 %fusion.1 = (f32[16,256]{1,0:T(8,128)S(1)}, f32[16,256,256]{1,2,0:T(8,128)S(1)}) fusion(f32[16,64,256]{2,1,0:T(8,128)S(1)} %bitcast.119, f32[16,256]{1,0:T(8,128)S(1)} %get-tuple-element.44, f32[16,64,256]{2,1,0:T(8,128)} %bitcast.120, f32[16,256]{1,0:T(8,128)S(1)} %get-tuple-element.45), kind=kOutput, calls=%fused_computation.11 | convolution fusion | flops 137359360 | bytes 6340608 | tf_op jit(solution)/shard_map/hdq,hdk->hqk/dot_general | solution.py:58
  60.7 1.5 %fusion.61 = f32[16,256,48]{1,2,0:T(8,128)S(1)} fusion(bf16[255,16,48]{0,2,1:T(8,128)(2,1)S(1)} %bitcast.123, bf16[1,16,48]{0,2,1:T(8,128)(2,1)} %slice.78, pred[256]{0:T(512)(128)(4,1)S(1)} %copy-done.47, bf16[3,16,48,48]{3,2,1,0:T(8,128)(2,1)} %param.16), kind=kOutput, calls=%fused_computation.130 | convolution fusion | flops 19857408 | bytes 1571584 | tf_op jit(solution)/shard_map/jvp(pgi,gio->pgo)/dot_general | solution.py:88
  62.1 1.2 %convolution_add_fusion.1 = f32[16,256,48]{1,2,0:T(8,128)S(1)} fusion(f32[16,256,48]{1,2,0:T(8,128)S(1)} %fusion.61, bf16[256,16,48]{0,2,1:T(8,128)(2,1)S(1)} %bitcast.124, bf16[3,16,48,48]{3,2,1,0:T(8,128)(2,1)} %param.16), kind=kOutput, calls=%fused_computation.21 | convolution fusion | flops 19070976 | bytes 2162688 | tf_op jit(solution)/shard_map/jvp(pgi,gio->pgo)/dot_general | solution.py:88
  63.4 1.4 %fusion.131 = (f32[256]{0:T(256)S(1)}, f32[16,256,48]{1,2,0:T(8,128)S(1)}) fusion(f32[16,256,48]{1,2,0:T(8,128)S(1)} %convolution_add_fusion.1, bf16[1,16,48]{0,2,1:T(8,128)(2,1)S(1)} %copy-done.23, bf16[255,16,48]{0,2,1:T(8,128)(2,1)S(1)} %bitcast.122, pred[256]{0:T(512)(128)(4,1)S(1)} %copy-done.46, bf16[3,16,48,48]{3,2,1,0:T(8,128)(2,1)} %param.16), kind=kOutput, calls=%fused_computation.259 | convolution fusion | flops 20250368 | bytes 2163968 | tf_op jit(solution)/shard_map/jvp(pgi,gio->pgo)/dot_general | solution.py:88
  66.1 5.2 %multiply_reduce_fusion = (f32[]{:T(128)}, f32[256,1024]{1,0:T(8,128)S(1)}) fusion(f32[256]{0:T(256)S(1)} %copy-done.42, f32[256]{0:T(256)S(1)} %add_rsqrt_fusion.2, f32[256,1024]{1,0:T(8,128)} %copy-done.5, f32[256]{0:T(256)S(1)} %broadcast_multiply_fusion.1, bf16[768,1024]{1,0:T(8,128)(2,1)} %param.17, bf16[256,768]{1,0:T(8,128)(2,1)S(1)} %copy-done.9, ...), kind=kOutput, calls=%fused_computation.62 | convolution fusion | flops 418709504 | bytes 4854788 | tf_op jit(solution)/shard_map/jvp()/dot_general | solution.py:96
  71.4 3.5 %multiply_reduce_fusion.4 = (f32[256]{0:T(256)S(1)}, bf16[256,768]{1,0:T(8,128)(2,1)S(1)}) fusion(f32[256,768]{1,0:T(8,128)S(1)} %copy-done.10, f32[256]{0:T(256)S(1)} %broadcast_multiply_fusion.3, f32[256]{0:T(256)S(1)} %fusion.110, bf16[768,1024]{1,0:T(8,128)(2,1)S(1)} %copy-done.48, f32[256,1024]{1,0:T(8,128)S(1)} %get-tuple-element.39, ...), kind=kOutput, calls=%fused_computation.82 | convolution fusion | flops 419495680 | bytes 3805184 | tf_op jit(solution)/shard_map/transpose(jvp())/dot_general | solution.py:96
  74.9 2.5 %fusion.126 = (f32[256]{0:T(256)S(1)}, f32[256,768]{1,0:T(8,128)S(1)}) fusion(f32[256]{0:T(256)S(1)} %multiply_multiply_fusion.8, bf16[256,768]{1,0:T(8,128)(2,1)S(1)} %get-tuple-element.29, f32[256]{0:T(256)S(1)} %fusion.110, f32[256,768]{1,0:T(8,128)S(1)} %copy-done.10, f32[256]{0:T(256)S(1)} %broadcast_multiply_fusion.3), kind=kLoop, calls=%fused_computation.254 | loop fusion | flops 15531776 | bytes 1970176 | tf_op jit(solution)/shard_map/transpose(jvp())/reduce_sum | solution.py:19
  80.5 1.3 %fusion.15 = bf16[256,16,48]{0,2,1:T(8,128)(2,1)S(1)} fusion(bf16[16,48,256]{2,1,0:T(8,128)(2,1)S(1)} %bitcast.127, bf16[1,16,48]{0,2,1:T(8,128)(2,1)S(1)} %split.23, bf16[255,16,48]{0,2,1:T(8,128)(2,1)S(1)} %split.22, bf16[255,16,48]{0,2,1:T(8,128)(2,1)S(1)} %bitcast.129, bf16[1,16,48]{0,2,1:T(8,128)(2,1)S(1)} %split.20, bf16[3,16,48,48]{3,2,1,0:T(8,128)(2,1)} %param.16), kind=kOutput, calls=%fused_computation.39 | convolution fusion | flops 20840448 | bytes 1769472 | tf_op jit(solution)/shard_map/transpose(jvp(pgi,gio->pgo))/dot_general | solution.py:88
  82.7 2.3 %convolution_convert_fusion.2 = bf16[256,1024]{1,0:T(8,128)(2,1)S(1)} fusion(bf16[1024,768]{1,0:T(8,128)(2,1)} %param.15, bf16[256,768]{1,0:T(8,128)(2,1)} %copy-done.19, bf16[256,768]{1,0:T(8,128)(2,1)} %copy.204), kind=kOutput, calls=%fused_computation.22 | convolution fusion | flops 403111936 | bytes 2883584 | tf_op jit(solution)/shard_map/transpose(jvp())/dot_general | solution.py:76
  86.6 1.4 %convolution_convert_fusion.15 = bf16[51,1024]{1,0:T(8,128)(2,1)} fusion(bf16[1024,1024]{1,0:T(8,128)(2,1)S(1)} %copy-done, pred[51,1024]{1,0:T(8,128)(4,1)S(1)} %copy-done.26, bf16[51,1024]{1,0:T(8,128)(2,1)S(1)} %gather_fusion.4, pred[51]{0:T(512)(128)(4,1)S(1)} %copy-done.36), kind=kOutput, calls=%fused_computation.56 | convolution fusion | flops 107111424 | bytes 2358323 | tf_op jit(solution)/shard_map/transpose(jvp())/dot_general | solution.py:66
  88.0 1.9 %reshape.338 = bf16[51,16,64]{2,1,0:T(8,128)(2,1)} reshape(bf16[51,1024]{1,0:T(8,128)(2,1)} %convolution_convert_fusion.15) | data formatting | bytes 208896 | tf_op jit(solution)/shard_map/transpose(jvp())/reshape | solution.py:66
  91.1 1.3 %multiply_reduce_fusion.7 = (f32[16,51]{1,0:T(8,128)S(1)}, f32[16,51,51]{1,2,0:T(8,128)S(1)}) fusion(f32[16,51,51]{1,2,0:T(8,128)S(1)} %copy-done.14, f32[16,51]{1,0:T(8,128)S(1)} %multiply_divide_fusion, bf16[16,64,51]{1,0,2:T(8,128)(2,1)} %copy-done.22, bf16[51,16,64]{2,1,0:T(8,128)(2,1)} %reshape.338), kind=kOutput, calls=%fused_computation.115 | convolution fusion | flops 5534112 | bytes 548352 | tf_op jit(solution)/shard_map/transpose(jvp(hqk,hdk->qhd))/dot_general | solution.py:63
  95.0 5.0 %fusion.78 = (f32[51]{0:T(128)S(1)}, f32[51,1024]{1,0:T(8,128)S(1)}) fusion(bf16[51,1024]{1,0:T(8,128)(2,1)S(1)} %gather_fusion.3, f32[51]{0:T(128)S(1)} %copy-done.30, bf16[3072,51]{0,1:T(8,128)(2,1)S(1)} %reshape.339, bf16[1024,3072]{1,0:T(8,128)(2,1)} %param.12), kind=kOutput, calls=%fused_computation.152 | convolution fusion | flops 321177536 | bytes 6918552 | tf_op jit(solution)/shard_map/transpose(jvp(sd,dk->ks))/dot_general | solution.py:50
  100.4 2.4 %collective-permute-start.3 = (bf16[51,1024]{1,0:T(8,128)(2,1)S(1)}, bf16[51,1024]{1,0:T(8,128)(2,1)S(1)}, u32[]{:S(2)}, u32[]{:S(2)}) collective-permute-start(bf16[51,1024]{1,0:T(8,128)(2,1)S(1)} %fusion.101), channel_id=1, source_target_pairs={{0,3},{1,0},{2,1},{3,2},{4,7},{5,4},{6,5},{7,6},{8,11},{9,8},{10,9... | collective-permute-start | bytes 313352 | tf_op jit(solution)/shard_map/ppermute | solution.py:119
  102.8 1.5 %collective-permute-start.4 = (bf16[51,1024]{1,0:T(8,128)(2,1)S(1)}, bf16[51,1024]{1,0:T(8,128)(2,1)S(1)}, u32[]{:S(2)}, u32[]{:S(2)}) collective-permute-start(bf16[51,1024]{1,0:T(8,128)(2,1)S(1)} %fusion.101), channel_id=1, source_target_pairs={{0,2},{1,3},{2,0},{3,1},{4,6},{5,7},{6,4},{7,5},{8,10},{9,11},{10,... | collective-permute-start | bytes 313352 | tf_op jit(solution)/shard_map/ppermute | solution.py:119
  107.2 1.5 %collective-permute-done.4 = bf16[51,1024]{1,0:T(8,128)(2,1)S(1)} collective-permute-done((bf16[51,1024]{1,0:T(8,128)(2,1)S(1)}, bf16[51,1024]{1,0:T(8,128)(2,1)S(1)}, u32[]{:S(2)}, u32[]{:S(2)}) %collective-permute-start.4) | collective-permute-done | bytes 104480 | tf_op jit(solution)/shard_map/ppermute | solution.py:119
  108.7 1.3 %collective-permute-done.5 = bf16[51,1024]{1,0:T(8,128)(2,1)S(1)} collective-permute-done((bf16[51,1024]{1,0:T(8,128)(2,1)S(1)}, bf16[51,1024]{1,0:T(8,128)(2,1)S(1)}, u32[]{:S(2)}, u32[]{:S(2)}) %collective-permute-start.5) | collective-permute-done | bytes 104480 | tf_op jit(solution)/shard_map/ppermute | solution.py:119
  (193 shorter events, 35.7 us)
Async XLA Ops:
  0.6 29.7 %copy-start = (bf16[1024,1024]{1,0:T(8,128)(2,1)S(1)}, bf16[1024,1024]{1,0:T(8,128)(2,1)}, u32[]{:S(2)}) copy-start(bf16[1024,1024]{1,0:T(8,128)(2,1)} %param.13) | copy-start | bytes 6291460
  0.6 9.8 %copy-start.38 = (bf16[1024]{0:T(1024)(128)(2,1)S(1)}, bf16[1024]{0:T(1024)(128)(2,1)}, u32[]{:S(2)}) copy-start(bf16[1024]{0:T(1024)(128)(2,1)} %param.14) | copy-start | bytes 6148
  0.7 13.2 %collective-permute-start = (bf16[64,768]{1,0:T(8,128)(2,1)}, bf16[64,768]{1,0:T(8,128)(2,1)}, u32[]{:S(2)}, u32[]{:S(2)}) collective-permute-start(bf16[64,768]{1,0:T(8,128)(2,1)} %param.9), channel_id=1, source_target_pairs={{0,3},{1,0},{2,1},{3,2},{4,7},{5,4},{6,5},{7,6},{8,11},{9,8},{10,9... | collective-permute-start | bytes 294920 | tf_op jit(solution)/shard_map/ppermute | solution.py:119
  4.6 10.8 %collective-permute-start.1 = (bf16[64,768]{1,0:T(8,128)(2,1)}, bf16[64,768]{1,0:T(8,128)(2,1)}, u32[]{:S(2)}, u32[]{:S(2)}) collective-permute-start(bf16[64,768]{1,0:T(8,128)(2,1)} %param.9), channel_id=1, source_target_pairs={{0,2},{1,3},{2,0},{3,1},{4,6},{5,7},{6,4},{7,5},{8,10},{9,11},{10,... | collective-permute-start | bytes 294920 | tf_op jit(solution)/shard_map/ppermute | solution.py:119
  5.1 11.8 %collective-permute-start.2 = (bf16[64,768]{1,0:T(8,128)(2,1)}, bf16[64,768]{1,0:T(8,128)(2,1)}, u32[]{:S(2)}, u32[]{:S(2)}) collective-permute-start(bf16[64,768]{1,0:T(8,128)(2,1)} %param.9), channel_id=1, source_target_pairs={{0,1},{1,2},{2,3},{3,0},{4,5},{5,6},{6,7},{7,4},{8,9},{9,10},{10,1... | collective-permute-start | bytes 294920 | tf_op jit(solution)/shard_map/ppermute | solution.py:119
  7.3 4.1 %copy-start.32 = (u32[51]{0:T(128)}, u32[51]{0:T(128)S(1)}, u32[]{:S(2)}) copy-start(u32[51]{0:T(128)S(1)} %iota_add_fusion) | copy-start | bytes 616
  8.6 12.7 %copy-start.31 = (s32[1024]{0:T(1024)}, s32[1024]{0:T(1024)S(1)}, u32[]{:S(2)}) copy-start(s32[1024]{0:T(1024)S(1)} %pad_clamp_fusion) | copy-start | bytes 12292
  10.4 10.9 %copy-start.11 = (u32[51,1024]{1,0:T(8,128)}, u32[51,1024]{1,0:T(8,128)S(1)}, u32[]{:S(2)}) copy-start(u32[51,1024]{1,0:T(8,128)S(1)} %gather_fusion.2) | copy-start | bytes 626692
  10.5 19.9 %copy-start.25 = (pred[51,1024]{1,0:T(8,128)(4,1)}, pred[51,1024]{1,0:T(8,128)(4,1)S(1)}, u32[]{:S(2)}) copy-start(pred[51,1024]{1,0:T(8,128)(4,1)S(1)} %broadcast_compare_fusion) | copy-start | bytes 156676
  21.3 6.1 %copy-start.6 = (bf16[256,1024]{1,0:T(8,128)(2,1)}, bf16[256,1024]{1,0:T(8,128)(2,1)S(1)}, u32[]{:S(2)}) copy-start(bf16[256,1024]{1,0:T(8,128)(2,1)S(1)} %get-tuple-element.19) | copy-start | bytes 1572868
  33.8 4.2 %copy-start.43 = (f32[256]{0:T(256)S(1)}, f32[256]{0:T(256)}, u32[]{:S(2)}) copy-start(f32[256]{0:T(256)} %get-tuple-element.18) | copy-start | bytes 3076
  33.8 4.2 %copy-start.7 = (bf16[256,1024]{1,0:T(8,128)(2,1)S(1)}, bf16[256,1024]{1,0:T(8,128)(2,1)}, u32[]{:S(2)}) copy-start(bf16[256,1024]{1,0:T(8,128)(2,1)} %copy-done.6) | copy-start | bytes 1572868
  36.0 7.0 %copy-start.8 = (bf16[256,768]{1,0:T(8,128)(2,1)}, bf16[256,768]{1,0:T(8,128)(2,1)S(1)}, u32[]{:S(2)}) copy-start(bf16[256,768]{1,0:T(8,128)(2,1)S(1)} %convolution_convert_fusion.8) | copy-start | bytes 1179652
  56.2 4.4 %copy-start.47 = (pred[256]{0:T(512)(128)(4,1)S(1)}, pred[256]{0:T(512)(128)(4,1)}, u32[]{:S(2)}) copy-start(pred[256]{0:T(512)(128)(4,1)} %get-tuple-element.41) | copy-start | bytes 772
  57.7 4.5 %copy-start.18 = (bf16[256,768]{0,1:T(8,128)(2,1)S(1)}, bf16[256,768]{0,1:T(8,128)(2,1)}, u32[]{:S(2)}) copy-start(bf16[256,768]{0,1:T(8,128)(2,1)} %copy.190) | copy-start | bytes 1179652
  66.1 5.2 %copy-start.10 = (f32[256,768]{1,0:T(8,128)S(1)}, f32[256,768]{1,0:T(8,128)}, u32[]{:S(2)}) copy-start(f32[256,768]{1,0:T(8,128)} %copy.195) | copy-start | bytes 2359300
  66.1 5.2 %copy-start.41 = (f32[256]{0:T(256)S(1)}, f32[256]{0:T(256)}, u32[]{:S(2)}) copy-start(f32[256]{0:T(256)} %get-tuple-element.16) | copy-start | bytes 3076
  66.1 5.2 %copy-start.48 = (bf16[768,1024]{1,0:T(8,128)(2,1)S(1)}, bf16[768,1024]{1,0:T(8,128)(2,1)}, u32[]{:S(2)}) copy-start(bf16[768,1024]{1,0:T(8,128)(2,1)} %param.17) | copy-start | bytes 4718596
  82.7 3.9 %copy-start.26 = (pred[51,1024]{1,0:T(8,128)(4,1)S(1)}, pred[51,1024]{1,0:T(8,128)(4,1)}, u32[]{:S(2)}) copy-start(pred[51,1024]{1,0:T(8,128)(4,1)} %copy-done.25) | copy-start | bytes 156676
  82.7 3.9 %copy-start.36 = (pred[51]{0:T(512)(128)(4,1)S(1)}, pred[51]{0:T(512)(128)(4,1)}, u32[]{:S(2)}) copy-start(pred[51]{0:T(512)(128)(4,1)} %get-tuple-element.4) | copy-start | bytes 157
  85.0 4.9 %copy-start.14 = (f32[16,51,51]{1,2,0:T(8,128)S(1)}, f32[16,51,51]{1,2,0:T(8,128)}, u32[]{:S(2)}) copy-start(f32[16,51,51]{1,2,0:T(8,128)} %copy-done.13) | copy-start | bytes 499396
  88.0 4.4 %copy-start.2 = (f32[16,64,51]{1,0,2:T(8,128)S(1)}, f32[16,64,51]{1,0,2:T(8,128)}, u32[]{:S(2)}) copy-start(f32[16,64,51]{1,0,2:T(8,128)} %copy-done.1) | copy-start | bytes 626692
  88.0 4.4 %copy-start.4 = (f32[16,64,51]{1,0,2:T(8,128)S(1)}, f32[16,64,51]{1,0,2:T(8,128)}, u32[]{:S(2)}) copy-start(f32[16,64,51]{1,0,2:T(8,128)} %copy-done.3) | copy-start | bytes 626692
  94.9 5.1 %copy-start.45 = (f32[51]{0:T(128)S(1)}, f32[51]{0:T(128)}, u32[]{:S(2)}) copy-start(f32[51]{0:T(128)} %copy-done.44) | copy-start | bytes 616
  94.9 5.1 %copy-start.35 = (f32[51]{0:T(128)S(1)}, f32[51]{0:T(128)}, u32[]{:S(2)}) copy-start(f32[51]{0:T(128)} %copy-done.34) | copy-start | bytes 616
  94.9 5.3 %copy-start.12 = (u32[51,1024]{1,0:T(8,128)S(1)}, u32[51,1024]{1,0:T(8,128)}, u32[]{:S(2)}) copy-start(u32[51,1024]{1,0:T(8,128)} %copy-done.11) | copy-start | bytes 626692
  94.9 5.3 %copy-start.21 = (bf16[51,1024]{1,0:T(8,128)(2,1)S(1)}, bf16[51,1024]{1,0:T(8,128)(2,1)}, u32[]{:S(2)}) copy-start(bf16[51,1024]{1,0:T(8,128)(2,1)} %copy-done.20) | copy-start | bytes 313348
  94.9 5.3 %copy-start.33 = (u32[51]{0:T(128)S(1)}, u32[51]{0:T(128)}, u32[]{:S(2)}) copy-start(u32[51]{0:T(128)} %copy-done.32) | copy-start | bytes 616
  94.9 5.3 %copy-start.37 = (pred[51]{0:T(512)(128)(4,1)S(1)}, pred[51]{0:T(512)(128)(4,1)}, u32[]{:S(2)}) copy-start(pred[51]{0:T(512)(128)(4,1)} %get-tuple-element.4) | copy-start | bytes 157
  100.4 6.8 %collective-permute-start.3 = (bf16[51,1024]{1,0:T(8,128)(2,1)S(1)}, bf16[51,1024]{1,0:T(8,128)(2,1)S(1)}, u32[]{:S(2)}, u32[]{:S(2)}) collective-permute-start(bf16[51,1024]{1,0:T(8,128)(2,1)S(1)} %fusion.101), channel_id=1, source_target_pairs={{0,3},{1,0},{2,1},{3,2},{4,7},{5,4},{6,5},{7,6},{8,11},{9,8},{10,9... | collective-permute-start | bytes 313352 | tf_op jit(solution)/shard_map/ppermute | solution.py:119
  102.8 5.9 %collective-permute-start.4 = (bf16[51,1024]{1,0:T(8,128)(2,1)S(1)}, bf16[51,1024]{1,0:T(8,128)(2,1)S(1)}, u32[]{:S(2)}, u32[]{:S(2)}) collective-permute-start(bf16[51,1024]{1,0:T(8,128)(2,1)S(1)} %fusion.101), channel_id=1, source_target_pairs={{0,2},{1,3},{2,0},{3,1},{4,6},{5,7},{6,4},{7,5},{8,10},{9,11},{10,... | collective-permute-start | bytes 313352 | tf_op jit(solution)/shard_map/ppermute | solution.py:119
  104.4 5.7 %collective-permute-start.5 = (bf16[51,1024]{1,0:T(8,128)(2,1)S(1)}, bf16[51,1024]{1,0:T(8,128)(2,1)S(1)}, u32[]{:S(2)}, u32[]{:S(2)}) collective-permute-start(bf16[51,1024]{1,0:T(8,128)(2,1)S(1)} %fusion.101), channel_id=1, source_target_pairs={{0,1},{1,2},{2,3},{3,0},{4,5},{5,6},{6,7},{7,4},{8,9},{9,10},{10,1... | collective-permute-start | bytes 313352 | tf_op jit(solution)/shard_map/ppermute | solution.py:119
  (23 other events, 41.8 us)

commit v3 on v2

--- a/solution.py
+++ b/solution.py
@@ -45,29 +45,10 @@
 
 def attention_branch(inputs, w_qkv, w_out):
     row_count = inputs.shape[0]
-    head_dim = D // HEADS
     normed = row_norm(inputs.astype(jnp.float32)).astype(jnp.bfloat16)
-    projected = jnp.einsum(
-        "sd,dk->ks", normed, w_qkv, preferred_element_type=jnp.float32
-    ).astype(jnp.bfloat16)
-    projected = projected.reshape(3, HEADS, head_dim, row_count)
-    queries = head_norm_cols(projected[0].astype(jnp.float32)).astype(jnp.bfloat16)
-    key_rows = head_norm_cols(projected[1].astype(jnp.float32)).astype(jnp.bfloat16)
-    score_scale = 1.0 / math.sqrt(head_dim)
-    scores = (
-        jnp.einsum("hdq,hdk->hqk", queries, key_rows, preferred_element_type=jnp.float32)
-        * score_scale
-    )
-    exponent = jnp.exp(scores)
-    weights = (exponent / jnp.sum(exponent, axis=-1, keepdims=True)).astype(jnp.bfloat16)
-    context = jnp.einsum(
-        "hqk,hdk->qhd", weights, projected[2], preferred_element_type=jnp.float32
-    ).astype(jnp.bfloat16)
+    projected = jnp.dot(normed, w_qkv, preferred_element_type=jnp.float32).astype(jnp.bfloat16)
+    context = split_project(projected.reshape(row_count, 3, HEADS, D // HEADS))
     return jnp.dot(context.reshape(row_count, D), w_out, preferred_element_type=jnp.float32)
-
-
-def head_norm_cols(values):
-    return values * lax.rsqrt(jnp.mean(values * values, axis=-2, keepdims=True) + EPSILON)
 
 
 def decoder_output(visible_out, positions, true_rows, mask_embed, dec_in, conv_w, dec_out):

time: 113 us -> 109 us (0.965)
  local copies, waits for them, and re-layouts: 33.1 us -> 28.2 us
  matrix products: 48.7 us -> 51.1 us
  other arithmetic: 15.4 us -> 13.8 us
    dot_general x11, matrix products: 21.2 us -> 23.1 us  [the longest x3 15.5 us: attention_branch(): jnp.dot(normed, w_qkv, preferred_element_type=jnp.float32)]
    slice x1, local copies, waits for them, and re-layouts: 2.04 us -> 0.11 us  [split_project(): return mix_heads(queries, key_rows, projected[:, 2])]
    convert_element_type x5 -> x2, local copies, waits for them, and re-layouts: 4.43 us -> 2.62 us  [the longest x1 2.59 us: attention_branch(): jnp.dot(normed, w_qkv, preferred_element_type=jnp.float32)]
    convert_element_type x1 -> x0, other arithmetic: 1.6 us -> none  [attention_branch(): projected[1].astype(jnp.float32)]
    scatter-add x1, other arithmetic: 2.91 us -> 1.35 us  [decoder_output(): jnp.broadcast_to(mask_embed, (total_rows, D)).at[positions].set(visible_out)]
    reshape x1 -> x2, local copies, waits for them, and re-layouts: 0.47 us -> 1.89 us  [attention_branch(): context = split_project(projected.reshape(row_count, 3, HEADS, D // HEADS))]
    unnamed x101 -> x105, local copies, waits for them, and re-layouts: 8.26 us -> 8.73 us
  transfers between devices with their start and end apart: 6 -> 6, of which waited for: 2 -> 2; matrix products, arithmetic and copies ran while one was open for 12% -> 13% of each run, Pallas kernels for 0% -> 0%
where the time goes in v3:
time: 109 us; the launch traced here: 108 us
  matrix products  51.1 us (47%)
  local copies, waits for them, and re-layouts  28.2 us (26%)
  other arithmetic  13.8 us (13%)
  starting transfers between devices  8.98 us (8%)
  between operations  3.39 us (3%)
  waiting for transfers between devices  2.84 us (3%)
    dot_general x3, matrix products, attention_branch(): jnp.dot(normed, w_qkv, preferred_element_type=jnp.float32)  15.5 us
    ppermute x6, starting transfers between devices, ring_gather(): parts.append(lax.ppermute(values, 'mask', pairs))  8.98 us
    unnamed x105, local copies, waits for them, and re-layouts  8.73 us
    dot_general x2, matrix products, decoder_output(): return jnp.dot(hidden, dec_out, preferred_element_type=jnp.float32)  8.54 us
    dot_general x6, matrix products, decoder_output(): jnp.einsum('pgi,gio->pgo', shifted[offset], conv_w[offset], preferred_ele...  7.67 us
    dot_general x2, matrix products, decoder_output(): jnp.dot(canvas, dec_in, preferred_element_type=jnp.float32)  3.99 us
    dot_general x4, matrix products, mix_heads(): jnp.einsum('hqk,khd->qhd', weights, values, preferred_element_type=jnp.fl...  3.87 us
    dot_general x3, matrix products, attention_branch(): jnp.dot(context.reshape(row_count, D), w_out, preferred_element_type=jnp....  3.82 us
  transfers between devices with their start and end apart: 6, of which 2 were waited for; matrix products, arithmetic and copies ran while one was open for 13% of the time, Pallas kernels for 0%

profile of v3, /device:TPU:0, one launch (start us, length us, event | category | flops | bytes accessed | tf_op | source)
XLA Modules:
  0.0 108.3 jit_solution(11692576893353995262)
XLA Ops:
  0.7 4.0 %collective-permute-start = (bf16[64,768]{1,0:T(8,128)(2,1)}, bf16[64,768]{1,0:T(8,128)(2,1)}, u32[]{:S(2)}, u32[]{:S(2)}) collective-permute-start(bf16[64,768]{1,0:T(8,128)(2,1)} %param.9), channel_id=1, source_target_pairs={{0,3},{1,0},{2,1},{3,2},{4,7},{5,4},{6,5},{7,6},{8,11},{9,8},{10,9... | collective-permute-start | bytes 294920 | tf_op jit(solution)/shard_map/ppermute | solution.py:100
  5.7 1.6 %constant_dynamic-update-slice_fusion.3 = bf16[256,768]{1,0:T(8,128)(2,1)} fusion(bf16[64,768]{1,0:T(8,128)(2,1)} %param.9), kind=kLoop, calls=%fused_computation.203 | loop fusion | bytes 196608
  14.6 1.5 %constant_dynamic-update-slice_fusion.2 = bf16[256,768]{1,0:T(8,128)(2,1)} fusion(bf16[256,768]{1,0:T(8,128)(2,1)} %constant_dynamic-update-slice_fusion.3, bf16[64,768]{1,0:T(8,128)(2,1)} %collective-permute-done), kind=kLoop, calls=%fused_computation.202 | loop fusion | bytes 196608
  16.1 1.5 %constant_dynamic-update-slice_fusion.1 = bf16[256,768]{1,0:T(8,128)(2,1)} fusion(bf16[256,768]{1,0:T(8,128)(2,1)} %constant_dynamic-update-slice_fusion.2, bf16[64,768]{1,0:T(8,128)(2,1)} %collective-permute-done.1), kind=kLoop, calls=%fused_computation.201 | loop fusion | bytes 196608
  18.3 2.8 %convert_reduce_fusion = (f32[256]{0:T(256)}, bf16[256,1024]{1,0:T(8,128)(2,1)S(1)}) fusion(bf16[256,768]{1,0:T(8,128)(2,1)} %constant_dynamic-update-slice_fusion, bf16[768,1024]{1,0:T(8,128)(2,1)} %param.11), kind=kOutput, calls=%fused_computation.20 | convolution fusion | flops 403439360 | bytes 2491392 | tf_op jit(solution)/shard_map/dot_general | solution.py:137
  23.1 4.7 %convolution_convert_fusion.1 = bf16[51,3072]{1,0:T(8,128)(2,1)} fusion(bf16[1024,3072]{1,0:T(8,128)(2,1)} %param.12, bf16[51,1024]{1,0:T(8,128)(2,1)S(1)} %gather_fusion.3, f32[51]{0:T(128)S(1)} %fusion.128, f32[51]{0:T(128)S(1)} %broadcast_multiply_fusion.4), kind=kOutput, calls=%fused_computation.11 | convolution fusion | flops 321229824 | bytes 6709656 | tf_op jit(solution)/shard_map/jvp()/dot_general | solution.py:49
  27.9 1.4 %reshape.324 = bf16[51,3,16,64]{3,2,1,0:T(8,128)(2,1)S(1)} reshape(bf16[51,3072]{1,0:T(8,128)(2,1)} %convolution_convert_fusion.1) | data formatting | bytes 626688 | tf_op jit(solution)/shard_map/jvp()/reshape | solution.py:50
  32.9 1.4 %fusion.23 = bf16[51,1024]{1,0:T(8,128)(2,1)S(1)} fusion(pred[51,1024]{1,0:T(8,128)(4,1)S(1)} %broadcast_compare_fusion, bf16[51,1024]{1,0:T(8,128)(2,1)} %reshape.325, bf16[1024,1024]{1,0:T(8,128)(2,1)S(1)} %copy-done, bf16[51,1024]{1,0:T(8,128)(2,1)S(1)} %gather_fusion.3), kind=kOutput, calls=%fused_computation.61 | convolution fusion | flops 107163648 | bytes 2462720 | tf_op jit(solution)/shard_map/jvp()/dot_general | solution.py:51
  34.3 1.4 %scatter_fusion = bf16[256,1024]{1,0:T(8,128)(2,1)S(1)} fusion(bf16[256,1024]{1,0:T(8,128)(2,1)S(1)} %copy-done.2, s32[51]{0:T(128)S(1)} %copy-done.39, bf16[51,1024]{1,0:T(8,128)(2,1)S(1)} %fusion.23), kind=kCustom, calls=%fused_computation.6 | custom fusion | flops 52224 | bytes 313548 | tf_op jit(solution)/shard_map/jvp()/scatter-add | solution.py:56
  35.7 2.0 %convolution_convert_fusion.8 = bf16[256,768]{1,0:T(8,128)(2,1)S(1)} fusion(bf16[256,1024]{1,0:T(8,128)(2,1)S(1)} %scatter_fusion, bf16[1024,768]{1,0:T(8,128)(2,1)} %param.15), kind=kOutput, calls=%fused_computation.30 | convolution fusion | flops 402849792 | bytes 2490368 | tf_op jit(solution)/shard_map/jvp()/dot_general | solution.py:57
  38.5 1.9 %copy.67 = bf16[256,768]{0,1:T(8,128)(2,1)} copy(bf16[256,768]{1,0:T(8,128)(2,1)} %copy-done.3) | data formatting | bytes 786432 | tf_op jit(solution)/shard_map/jvp()/convert_element_type | solution.py:57
  40.7 5.8 %convolution_convert_fusion = bf16[256,3072]{1,0:T(8,128)(2,1)} fusion(bf16[1024,3072]{1,0:T(8,128)(2,1)} %param.12, bf16[256,1024]{1,0:T(8,128)(2,1)S(1)} %get-tuple-element.18, f32[256]{0:T(256)S(1)} %add_rsqrt_fusion.3, f32[256]{0:T(256)S(1)} %broadcast_multiply_fusion.2), kind=kOutput, calls=%fused_computation.9 | convolution fusion | flops 1612447744 | bytes 8390656 | tf_op jit(solution)/shard_map/dot_general | solution.py:49
  46.5 2.6 %copy.73 = bf16[256,3072]{0,1:T(8,128)(2,1)} copy(bf16[256,3072]{1,0:T(8,128)(2,1)} %convolution_convert_fusion) | data formatting | bytes 3145728 | tf_op jit(solution)/shard_map/convert_element_type | solution.py:49
  49.1 1.5 %fusion.26 = (f32[256,16]{0,1:T(8,128)S(1)}, f32[256,16]{0,1:T(8,128)S(1)}) fusion(bf16[256,3,16,64]{0,3,2,1:T(8,128)(2,1)} %bitcast.175), kind=kLoop, calls=%fused_computation.64 | loop fusion | flops 1564672 | bytes 1081344 | tf_op jit(solution)/shard_map/reduce_sum | solution.py:25
  50.6 2.2 %fusion = (f32[16,256]{1,0:T(8,128)S(1)}, f32[16,256,256]{1,2,0:T(8,128)S(1)}) fusion(f32[256,16]{0,1:T(8,128)S(1)} %get-tuple-element.43, bf16[256,3,16,64]{0,3,2,1:T(8,128)(2,1)} %bitcast.176, f32[256,16]{0,1:T(8,128)S(1)} %get-tuple-element.44), kind=kOutput, calls=%fused_computation.10 | convolution fusion | flops 137883648 | bytes 5292032 | tf_op jit(solution)/shard_map/qhd,khd->hqk/dot_general | solution.py:31
  52.8 1.9 %fusion.3 = bf16[16,64,256]{2,1,0:T(8,128)(2,1)S(1)} fusion(f32[16,256,256]{1,2,0:T(8,128)S(1)} %get-tuple-element.20, f32[16,256]{1,0:T(8,128)S(1)} %get-tuple-element.19, bf16[256,3,16,64]{0,3,2,1:T(8,128)(2,1)} %bitcast.177), kind=kOutput, calls=%fused_computation.21 | convolution fusion | flops 137625600 | bytes 5259264 | tf_op jit(solution)/shard_map/hqk,khd->qhd/dot_general | solution.py:36
  60.6 1.5 %fusion.73 = f32[16,256,48]{1,2,0:T(8,128)S(1)} fusion(bf16[255,16,48]{0,2,1:T(8,128)(2,1)S(1)} %bitcast.180, bf16[1,16,48]{0,2,1:T(8,128)(2,1)} %slice.72, pred[256]{0:T(512)(128)(4,1)S(1)} %copy-done.48, bf16[3,16,48,48]{3,2,1,0:T(8,128)(2,1)} %param.16), kind=kOutput, calls=%fused_computation.143 | convolution fusion | flops 19857408 | bytes 1571584 | tf_op jit(solution)/shard_map/jvp(pgi,gio->pgo)/dot_general | solution.py:69
  62.0 1.2 %convolution_add_fusion.1 = f32[16,256,48]{1,2,0:T(8,128)S(1)} fusion(f32[16,256,48]{1,2,0:T(8,128)S(1)} %fusion.73, bf16[256,16,48]{0,2,1:T(8,128)(2,1)S(1)} %bitcast.181, bf16[3,16,48,48]{3,2,1,0:T(8,128)(2,1)} %param.16), kind=kOutput, calls=%fused_computation.23 | convolution fusion | flops 19070976 | bytes 2162688 | tf_op jit(solution)/shard_map/jvp(pgi,gio->pgo)/dot_general | solution.py:69
  63.4 1.4 %fusion.145 = (f32[256]{0:T(256)S(1)}, f32[16,256,48]{1,2,0:T(8,128)S(1)}) fusion(f32[16,256,48]{1,2,0:T(8,128)S(1)} %convolution_add_fusion.1, bf16[1,16,48]{0,2,1:T(8,128)(2,1)S(1)} %copy-done.16, bf16[255,16,48]{0,2,1:T(8,128)(2,1)S(1)} %bitcast.179, pred[256]{0:T(512)(128)(4,1)S(1)} %copy-done.46, bf16[3,16,48,48]{3,2,1,0:T(8,128)(2,1)} %param.16), kind=kOutput, calls=%fused_computation.271 | convolution fusion | flops 20250368 | bytes 2163968 | tf_op jit(solution)/shard_map/jvp(pgi,gio->pgo)/dot_general | solution.py:69
  66.1 5.2 %multiply_reduce_fusion = (f32[]{:T(128)}, f32[256,1024]{1,0:T(8,128)S(1)}) fusion(f32[256]{0:T(256)S(1)} %copy-done.41, f32[256]{0:T(256)S(1)} %copy-done.43, f32[256,1024]{1,0:T(8,128)} %copy-done.1, f32[256]{0:T(256)S(1)} %broadcast_multiply_fusion.1, bf16[768,1024]{1,0:T(8,128)(2,1)} %param.17, bf16[256,768]{1,0:T(8,128)(2,1)S(1)} %copy-done.4, ...), kind=kOutput, calls=%fused_computation.70 | convolution fusion | flops 418709504 | bytes 4854788 | tf_op jit(solution)/shard_map/jvp()/dot_general | solution.py:77
  71.3 3.3 %multiply_reduce_fusion.2 = (f32[256]{0:T(256)S(1)}, bf16[256,768]{1,0:T(8,128)(2,1)S(1)}) fusion(f32[256,768]{1,0:T(8,128)S(1)} %copy-done.5, f32[256]{0:T(256)S(1)} %broadcast_multiply_fusion.3, f32[256]{0:T(256)S(1)} %fusion.124, bf16[768,1024]{1,0:T(8,128)(2,1)S(1)} %copy-done.50, f32[256,1024]{1,0:T(8,128)S(1)} %get-tuple-element.38, f32[256]{0:T(256)S(1)} %copy-done.40), kind=kOutput, calls=%fused_computation.94 | convolution fusion | flops 419495680 | bytes 3805184 | tf_op jit(solution)/shard_map/transpose(jvp())/dot_general | solution.py:77
  74.7 2.8 %fusion.140 = (f32[256]{0:T(256)S(1)}, f32[256,768]{1,0:T(8,128)S(1)}) fusion(f32[256]{0:T(256)S(1)} %multiply_multiply_fusion.8, bf16[256,768]{1,0:T(8,128)(2,1)S(1)} %get-tuple-element.28, f32[256]{0:T(256)S(1)} %fusion.124, f32[256,768]{1,0:T(8,128)S(1)} %copy-done.5, f32[256]{0:T(256)S(1)} %broadcast_multiply_fusion.3), kind=kLoop, calls=%fused_computation.266 | loop fusion | flops 15531776 | bytes 1970176 | tf_op jit(solution)/shard_map/transpose(jvp())/reduce_sum | solution.py:19
  80.5 1.3 %fusion.13 = bf16[256,16,48]{0,2,1:T(8,128)(2,1)S(1)} fusion(bf16[16,48,256]{2,1,0:T(8,128)(2,1)S(1)} %bitcast.184, bf16[1,16,48]{0,2,1:T(8,128)(2,1)S(1)} %split.23, bf16[255,16,48]{0,2,1:T(8,128)(2,1)S(1)} %split.22, bf16[255,16,48]{0,2,1:T(8,128)(2,1)S(1)} %bitcast.186, bf16[1,16,48]{0,2,1:T(8,128)(2,1)S(1)} %split.20, bf16[3,16,48,48]{3,2,1,0:T(8,128)(2,1)} %param.16), kind=kOutput, calls=%fused_computation.41 | convolution fusion | flops 20840448 | bytes 1769472 | tf_op jit(solution)/shard_map/transpose(jvp(pgi,gio->pgo))/dot_general | solution.py:69
  82.0 2.0 %convolution_convert_fusion.2 = bf16[256,1024]{1,0:T(8,128)(2,1)S(1)} fusion(bf16[1024,768]{1,0:T(8,128)(2,1)} %param.15, bf16[256,768]{1,0:T(8,128)(2,1)S(1)} %get-tuple-element.28, bf16[256,768]{1,0:T(8,128)(2,1)S(1)} %copy.79), kind=kOutput, calls=%fused_computation.24 | convolution fusion | flops 403111936 | bytes 2883584 | tf_op jit(solution)/shard_map/transpose(jvp())/dot_general | solution.py:57
  84.8 1.6 %convolution_convert_fusion.15 = bf16[51,1024]{1,0:T(8,128)(2,1)S(1)} fusion(bf16[1024,1024]{1,0:T(8,128)(2,1)S(1)} %copy-done, pred[51,1024]{1,0:T(8,128)(4,1)} %copy-done.17, bf16[51,1024]{1,0:T(8,128)(2,1)S(1)} %gather_fusion.4, pred[51]{0:T(512)(128)(4,1)S(1)} %copy-done.35), kind=kOutput, calls=%fused_computation.60 | convolution fusion | flops 107111424 | bytes 2358323 | tf_op jit(solution)/shard_map/transpose(jvp())/dot_general | solution.py:51
  86.6 1.4 %fusion.20 = bf16[51,1,16,64]{3,0,2,1:T(8,128)(2,1)S(1)} fusion(bf16[51,16,64]{2,1,0:T(8,128)(2,1)S(1)} %reshape.332, f32[16,51,51]{1,2,0:T(8,128)} %copy-done.18, f32[16,51]{1,0:T(8,128)S(1)} %copy-done.29), kind=kOutput, calls=%fused_computation.55 | convolution fusion | flops 5462304 | bytes 378624 | tf_op jit(solution)/shard_map/transpose(jvp(hqk,khd->qhd))/dot_general | solution.py:36
  90.9 5.0 %fusion.90 = (f32[51]{0:T(128)S(1)}, f32[51,1024]{1,0:T(8,128)S(1)}) fusion(bf16[51,1024]{1,0:T(8,128)(2,1)S(1)} %gather_fusion.3, f32[51]{0:T(128)S(1)} %copy-done.27, bf16[51,3072]{1,0:T(8,128)(2,1)S(1)} %reshape.333, bf16[1024,3072]{1,0:T(8,128)(2,1)} %param.12), kind=kOutput, calls=%fused_computation.165 | convolution fusion | flops 321177536 | bytes 6918552 | tf_op jit(solution)/shard_map/transpose(jvp())/dot_general | solution.py:49
  96.4 2.4 %collective-permute-start.3 = (bf16[51,1024]{1,0:T(8,128)(2,1)S(1)}, bf16[51,1024]{1,0:T(8,128)(2,1)S(1)}, u32[]{:S(2)}, u32[]{:S(2)}) collective-permute-start(bf16[51,1024]{1,0:T(8,128)(2,1)S(1)} %fusion.115), channel_id=1, source_target_pairs={{0,3},{1,0},{2,1},{3,2},{4,7},{5,4},{6,5},{7,6},{8,11},{9,8},{10,9... | collective-permute-start | bytes 313352 | tf_op jit(solution)/shard_map/ppermute | solution.py:100
  98.7 1.5 %collective-permute-start.4 = (bf16[51,1024]{1,0:T(8,128)(2,1)S(1)}, bf16[51,1024]{1,0:T(8,128)(2,1)S(1)}, u32[]{:S(2)}, u32[]{:S(2)}) collective-permute-start(bf16[51,1024]{1,0:T(8,128)(2,1)S(1)} %fusion.115), channel_id=1, source_target_pairs={{0,2},{1,3},{2,0},{3,1},{4,6},{5,7},{6,4},{7,5},{8,10},{9,11},{10,... | collective-permute-start | bytes 313352 | tf_op jit(solution)/shard_map/ppermute | solution.py:100
  103.1 1.5 %collective-permute-done.4 = bf16[51,1024]{1,0:T(8,128)(2,1)S(1)} collective-permute-done((bf16[51,1024]{1,0:T(8,128)(2,1)S(1)}, bf16[51,1024]{1,0:T(8,128)(2,1)S(1)}, u32[]{:S(2)}, u32[]{:S(2)}) %collective-permute-start.4) | collective-permute-done | bytes 104480 | tf_op jit(solution)/shard_map/ppermute | solution.py:100
  104.7 1.3 %collective-permute-done.5 = bf16[51,1024]{1,0:T(8,128)(2,1)S(1)} collective-permute-done((bf16[51,1024]{1,0:T(8,128)(2,1)S(1)}, bf16[51,1024]{1,0:T(8,128)(2,1)S(1)}, u32[]{:S(2)}, u32[]{:S(2)}) %collective-permute-start.5) | collective-permute-done | bytes 104480 | tf_op jit(solution)/shard_map/ppermute | solution.py:100
  106.0 1.2 %fusion.65 = f32[192,1024]{1,0:T(8,128)} fusion(bf16[204,192]{1,0:T(8,128)(2,1)S(1)} %gather_fusion.1, bf16[51,1024]{1,0:T(8,128)(2,1)S(1)} %collective-permute-done.5, bf16[51,1024]{1,0:T(8,128)(2,1)S(1)} %collective-permute-done.4, bf16[51,1024]{1,0:T(8,128)(2,1)S(1)} %collective-permute-done.3, bf16[51,1024]{1,0:T(8,128)(2,1)S(1)} %fusion.115), kind=kOutput, calls=%fused_computation.134 | convolution fusion | flops 81887232 | bytes 1282560 | tf_op jit(solution)/shard_map/vc,vd->cd/dot_general | solution.py:160
  (189 shorter events, 32.2 us)
Async XLA Ops:
  0.6 32.3 %copy-start = (bf16[1024,1024]{1,0:T(8,128)(2,1)S(1)}, bf16[1024,1024]{1,0:T(8,128)(2,1)}, u32[]{:S(2)}) copy-start(bf16[1024,1024]{1,0:T(8,128)(2,1)} %param.13) | copy-start | bytes 6291460
  0.6 9.8 %copy-start.37 = (bf16[1024]{0:T(1024)(128)(2,1)S(1)}, bf16[1024]{0:T(1024)(128)(2,1)}, u32[]{:S(2)}) copy-start(bf16[1024]{0:T(1024)(128)(2,1)} %param.14) | copy-start | bytes 6148
  0.7 14.0 %collective-permute-start = (bf16[64,768]{1,0:T(8,128)(2,1)}, bf16[64,768]{1,0:T(8,128)(2,1)}, u32[]{:S(2)}, u32[]{:S(2)}) collective-permute-start(bf16[64,768]{1,0:T(8,128)(2,1)} %param.9), channel_id=1, source_target_pairs={{0,3},{1,0},{2,1},{3,2},{4,7},{5,4},{6,5},{7,6},{8,11},{9,8},{10,9... | collective-permute-start | bytes 294920 | tf_op jit(solution)/shard_map/ppermute | solution.py:100
  4.6 11.5 %collective-permute-start.1 = (bf16[64,768]{1,0:T(8,128)(2,1)}, bf16[64,768]{1,0:T(8,128)(2,1)}, u32[]{:S(2)}, u32[]{:S(2)}) collective-permute-start(bf16[64,768]{1,0:T(8,128)(2,1)} %param.9), channel_id=1, source_target_pairs={{0,2},{1,3},{2,0},{3,1},{4,6},{5,7},{6,4},{7,5},{8,10},{9,11},{10,... | collective-permute-start | bytes 294920 | tf_op jit(solution)/shard_map/ppermute | solution.py:100
  5.1 12.5 %collective-permute-start.2 = (bf16[64,768]{1,0:T(8,128)(2,1)}, bf16[64,768]{1,0:T(8,128)(2,1)S(1)}, u32[]{:S(2)}, u32[]{:S(2)}) collective-permute-start(bf16[64,768]{1,0:T(8,128)(2,1)} %param.9), channel_id=1, source_target_pairs={{0,1},{1,2},{2,3},{3,0},{4,5},{5,6},{6,7},{7,4},{8,9},{9,10},{10,1... | collective-permute-start | bytes 294920 | tf_op jit(solution)/shard_map/ppermute | solution.py:100
  7.3 4.1 %copy-start.31 = (u32[51]{0:T(128)}, u32[51]{0:T(128)S(1)}, u32[]{:S(2)}) copy-start(u32[51]{0:T(128)S(1)} %iota_add_fusion) | copy-start | bytes 616
  8.0 3.4 %copy-start.38 = (s32[51]{0:T(128)}, s32[51]{0:T(128)S(1)}, u32[]{:S(2)}) copy-start(s32[51]{0:T(128)S(1)} %fusion.127) | copy-start | bytes 616
  8.6 12.5 %copy-start.30 = (s32[1024]{0:T(1024)}, s32[1024]{0:T(1024)S(1)}, u32[]{:S(2)}) copy-start(s32[1024]{0:T(1024)S(1)} %pad_clamp_fusion) | copy-start | bytes 12292
  10.4 10.7 %copy-start.6 = (u32[51,1024]{1,0:T(8,128)}, u32[51,1024]{1,0:T(8,128)S(1)}, u32[]{:S(2)}) copy-start(u32[51,1024]{1,0:T(8,128)S(1)} %gather_fusion.2) | copy-start | bytes 626692
  10.5 22.4 %copy-start.17 = (pred[51,1024]{1,0:T(8,128)(4,1)}, pred[51,1024]{1,0:T(8,128)(4,1)S(1)}, u32[]{:S(2)}) copy-start(pred[51,1024]{1,0:T(8,128)(4,1)S(1)} %broadcast_compare_fusion) | copy-start | bytes 156676
  35.7 4.7 %copy-start.42 = (f32[256]{0:T(256)S(1)}, f32[256]{0:T(256)}, u32[]{:S(2)}) copy-start(f32[256]{0:T(256)} %get-tuple-element.17) | copy-start | bytes 3076
  55.5 5.0 %copy-start.48 = (pred[256]{0:T(512)(128)(4,1)S(1)}, pred[256]{0:T(512)(128)(4,1)}, u32[]{:S(2)}) copy-start(pred[256]{0:T(512)(128)(4,1)} %get-tuple-element.40) | copy-start | bytes 772
  57.6 4.5 %copy-start.13 = (bf16[256,768]{0,1:T(8,128)(2,1)S(1)}, bf16[256,768]{0,1:T(8,128)(2,1)}, u32[]{:S(2)}) copy-start(bf16[256,768]{0,1:T(8,128)(2,1)} %copy.67) | copy-start | bytes 1179652
  59.5 3.8 %copy-start.46 = (pred[256]{0:T(512)(128)(4,1)S(1)}, pred[256]{0:T(512)(128)(4,1)}, u32[]{:S(2)}) copy-start(pred[256]{0:T(512)(128)(4,1)} %get-tuple-element.39) | copy-start | bytes 772
  60.6 2.8 %copy-start.12 = (bf16[255,768]{0,1:T(8,128)(2,1)S(1)}, bf16[255,768]{0,1:T(8,128)(2,1)}, u32[]{:S(2)}) copy-start(bf16[255,768]{0,1:T(8,128)(2,1)} %copy.69) | copy-start | bytes 1175044
  60.6 2.8 %copy-start.16 = (bf16[1,16,48]{0,2,1:T(8,128)(2,1)S(1)}, bf16[1,16,48]{0,2,1:T(8,128)(2,1)}, u32[]{:S(2)}) copy-start(bf16[1,16,48]{0,2,1:T(8,128)(2,1)} %slice.73) | copy-start | bytes 4612
  66.0 5.3 %copy-start.5 = (f32[256,768]{1,0:T(8,128)S(1)}, f32[256,768]{1,0:T(8,128)}, u32[]{:S(2)}) copy-start(f32[256,768]{1,0:T(8,128)} %copy.72) | copy-start | bytes 2359300
  66.0 5.3 %copy-start.40 = (f32[256]{0:T(256)S(1)}, f32[256]{0:T(256)}, u32[]{:S(2)}) copy-start(f32[256]{0:T(256)} %get-tuple-element.15) | copy-start | bytes 3076
  66.1 5.3 %copy-start.50 = (bf16[768,1024]{1,0:T(8,128)(2,1)S(1)}, bf16[768,1024]{1,0:T(8,128)(2,1)}, u32[]{:S(2)}) copy-start(bf16[768,1024]{1,0:T(8,128)(2,1)} %param.17) | copy-start | bytes 4718596
  74.6 3.1 %copy-start.49 = (pred[256]{0:T(512)(128)(4,1)S(1)}, pred[256]{0:T(512)(128)(4,1)}, u32[]{:S(2)}) copy-start(pred[256]{0:T(512)(128)(4,1)} %get-tuple-element.40) | copy-start | bytes 772
  74.7 4.3 %copy-start.47 = (pred[256]{0:T(512)(128)(4,1)S(1)}, pred[256]{0:T(512)(128)(4,1)}, u32[]{:S(2)}) copy-start(pred[256]{0:T(512)(128)(4,1)} %get-tuple-element.39) | copy-start | bytes 772
  77.6 2.8 %copy-start.29 = (f32[16,51]{1,0:T(8,128)S(1)}, f32[16,51]{1,0:T(8,128)}, u32[]{:S(2)}) copy-start(f32[16,51]{1,0:T(8,128)} %copy-done.28) | copy-start | bytes 9796
  81.9 2.8 %copy-start.35 = (pred[51]{0:T(512)(128)(4,1)S(1)}, pred[51]{0:T(512)(128)(4,1)}, u32[]{:S(2)}) copy-start(pred[51]{0:T(512)(128)(4,1)} %get-tuple-element.6) | copy-start | bytes 157
  84.8 3.2 %copy-start.15 = (bf16[51,1,16,64]{3,2,1,0:T(8,128)(2,1)S(1)}, bf16[51,1,16,64]{3,2,1,0:T(8,128)(2,1)}, u32[]{:S(2)}) copy-start(bf16[51,1,16,64]{3,2,1,0:T(8,128)(2,1)} %copy-done.14) | copy-start | bytes 313348
  90.8 5.0 %copy-start.45 = (f32[51]{0:T(128)S(1)}, f32[51]{0:T(128)}, u32[]{:S(2)}) copy-start(f32[51]{0:T(128)} %copy-done.44) | copy-start | bytes 616
  90.8 5.1 %copy-start.34 = (f32[51]{0:T(128)S(1)}, f32[51]{0:T(128)}, u32[]{:S(2)}) copy-start(f32[51]{0:T(128)} %copy-done.33) | copy-start | bytes 616
  90.9 5.3 %copy-start.7 = (u32[51,1024]{1,0:T(8,128)S(1)}, u32[51,1024]{1,0:T(8,128)}, u32[]{:S(2)}) copy-start(u32[51,1024]{1,0:T(8,128)} %copy-done.6) | copy-start | bytes 626692
  90.9 5.3 %copy-start.32 = (u32[51]{0:T(128)S(1)}, u32[51]{0:T(128)}, u32[]{:S(2)}) copy-start(u32[51]{0:T(128)} %copy-done.31) | copy-start | bytes 616
  90.9 5.3 %copy-start.36 = (pred[51]{0:T(512)(128)(4,1)S(1)}, pred[51]{0:T(512)(128)(4,1)}, u32[]{:S(2)}) copy-start(pred[51]{0:T(512)(128)(4,1)} %get-tuple-element.6) | copy-start | bytes 157
  96.4 6.8 %collective-permute-start.3 = (bf16[51,1024]{1,0:T(8,128)(2,1)S(1)}, bf16[51,1024]{1,0:T(8,128)(2,1)S(1)}, u32[]{:S(2)}, u32[]{:S(2)}) collective-permute-start(bf16[51,1024]{1,0:T(8,128)(2,1)S(1)} %fusion.115), channel_id=1, source_target_pairs={{0,3},{1,0},{2,1},{3,2},{4,7},{5,4},{6,5},{7,6},{8,11},{9,8},{10,9... | collective-permute-start | bytes 313352 | tf_op jit(solution)/shard_map/ppermute | solution.py:100
  98.7 5.9 %collective-permute-start.4 = (bf16[51,1024]{1,0:T(8,128)(2,1)S(1)}, bf16[51,1024]{1,0:T(8,128)(2,1)S(1)}, u32[]{:S(2)}, u32[]{:S(2)}) collective-permute-start(bf16[51,1024]{1,0:T(8,128)(2,1)S(1)} %fusion.115), channel_id=1, source_target_pairs={{0,2},{1,3},{2,0},{3,1},{4,6},{5,7},{6,4},{7,5},{8,10},{9,11},{10,... | collective-permute-start | bytes 313352 | tf_op jit(solution)/shard_map/ppermute | solution.py:100
  100.3 5.7 %collective-permute-start.5 = (bf16[51,1024]{1,0:T(8,128)(2,1)S(1)}, bf16[51,1024]{1,0:T(8,128)(2,1)S(1)}, u32[]{:S(2)}, u32[]{:S(2)}) collective-permute-start(bf16[51,1024]{1,0:T(8,128)(2,1)S(1)} %fusion.115), channel_id=1, source_target_pairs={{0,1},{1,2},{2,3},{3,0},{4,5},{5,6},{6,7},{7,4},{8,9},{9,10},{10,1... | collective-permute-start | bytes 313352 | tf_op jit(solution)/shard_map/ppermute | solution.py:100
  (25 other events, 36.6 us)

commit v4 on v1

--- a/solution.py
+++ b/solution.py
@@ -52,8 +52,17 @@
 
 
 def decoder_output(visible_out, positions, total_rows, mask_embed, dec_in, conv_w, dec_out):
-    canvas = jnp.broadcast_to(mask_embed, (total_rows, D)).at[positions].set(visible_out)
-    lowered = jnp.dot(canvas, dec_in, preferred_element_type=jnp.float32).astype(jnp.bfloat16)
+    slot_ids = jnp.arange(total_rows, dtype=jnp.int32)
+    picks = (slot_ids[:, None] == positions[None, :]).astype(jnp.bfloat16)
+    seen = jnp.max(picks, axis=1, keepdims=True)
+    lowered_visible = jnp.dot(visible_out, dec_in, preferred_element_type=jnp.float32).astype(
+        jnp.bfloat16
+    )
+    lowered_mask = jnp.dot(
+        mask_embed[None, :], dec_in, preferred_element_type=jnp.float32
+    ).astype(jnp.bfloat16)
+    placed = jnp.dot(picks, lowered_visible, preferred_element_type=jnp.float32)
+    lowered = jnp.where(seen > 0, placed, lowered_mask.astype(jnp.float32)).astype(jnp.bfloat16)
     grouped = lowered.reshape(total_rows, GROUPS, DD // GROUPS)
     padded = jnp.pad(grouped, ((1, 1), (0, 0), (0, 0)))
     convolved = jnp.zeros((total_rows, GROUPS, DD // GROUPS), jnp.float32)
@@ -88,14 +97,19 @@
     for shift in range(1, group_size):
         pairs = [(source, (source - shift) % group_size) for source in range(group_size)]
         parts.append(lax.ppermute(values, "mask", pairs))
-    return jnp.concatenate(parts, axis=0)
+    return parts
 
 
-def unroll_blocks(rotated, own_index, block_rows):
-    total_rows = rotated.shape[0]
-    doubled = jnp.concatenate([rotated, rotated], axis=0)
-    start = total_rows - own_index * block_rows
-    return lax.dynamic_slice_in_dim(doubled, start, total_rows, 0)
+def in_mask_order(parts, own_index):
+    group_size = len(parts)
+    blocks = []
+    for block in range(group_size):
+        slot = (block - own_index) % group_size
+        chosen = parts[0]
+        for other in range(1, group_size):
+            chosen = jnp.where(slot == other, parts[other], chosen)
+        blocks.append(chosen)
+    return jnp.concatenate(blocks, axis=0)
 
 
 def split_teacher(embedded, w_qkv, w_out, own_index, group_size):
@@ -127,7 +141,7 @@
     total_rows = tok_rows * group_size
     col_width = patches.shape[1] // group_size
     positions = lax.dynamic_index_in_dim(visible_index, own_index, 0, keepdims=False)
-    clip_pixels = unroll_blocks(ring_gather(patches, group_size), own_index, tok_rows)
+    clip_pixels = in_mask_order(ring_gather(patches, group_size), own_index)
     embedded = jnp.dot(clip_pixels, embed_w, preferred_element_type=jnp.float32).astype(
         jnp.bfloat16
     )
@@ -154,7 +168,7 @@
     embed_grad = jnp.einsum(
         "vc,vd->cd",
         gathered,
-        ring_gather(grad_in, group_size),
+        jnp.concatenate(ring_gather(grad_in, group_size), axis=0),
         preferred_element_type=jnp.float32,
     )
     return (embed_grad, copy_loss)

time: 94.5 us -> 87.3 us (0.924)
  local copies, waits for them, and re-layouts: 20.8 us -> 13.3 us
  matrix products: 43.5 us -> 47.3 us
  other arithmetic: 14.3 us -> 10.8 us
    unnamed x67 -> x61, local copies, waits for them, and re-layouts: 6.37 us -> 2.82 us
    dot_general x3, matrix products: 12.1 us -> 14.8 us  [attention_branch(): jnp.dot(normed, w_qkv, preferred_element_type=jnp.float32)]
    dot_general x3 -> x5, matrix products: 6.06 us -> 7.79 us  [the longest x2 4.51 us: decoder_output(): jnp.dot(visible_out, dec_in, preferred_element_type=jnp.float32)]
    scatter-add x1 -> x0, other arithmetic: 1.53 us -> none  [decoder_output(): jnp.broadcast_to(mask_embed, (total_rows, D)).at[positions].set(visible_out)]
    gather x2 -> x0, local copies, waits for them, and re-layouts: 1.34 us -> none  [decoder_output(): jnp.broadcast_to(mask_embed, (total_rows, D)).at[positions].set(visible_out)]
    and x1 -> x0, other arithmetic: 1.23 us -> none  [decoder_output(): jnp.broadcast_to(mask_embed, (total_rows, D)).at[positions].set(visible_out)]
    scatter x1 -> x0, local copies, waits for them, and re-layouts: 1.1 us -> none  [decoder_output(): jnp.broadcast_to(mask_embed, (total_rows, D)).at[positions].set(visible_out)]
    convert_element_type x1, local copies, waits for them, and re-layouts: 1.16 us -> 0.17 us  [decoder_output(): jnp.where(seen > 0, placed, lowered_mask.astype(jnp.float32))]
  transfers between devices with their start and end apart: 6 -> 6, of which waited for: 2 -> 3; matrix products, arithmetic and copies ran while one was open for 12% -> 8% of each run, Pallas kernels for 0% -> 0%
where the time goes in v4:
time: 87.3 us; the launch traced here: 86.6 us
  matrix products  47.3 us (54%)
  local copies, waits for them, and re-layouts  13.3 us (15%)
  other arithmetic  10.8 us (12%)
  starting transfers between devices  8.16 us (9%)
  waiting for transfers between devices  3.77 us (4%)
  between operations  3.17 us (4%)
    dot_general x3, matrix products, attention_branch(): jnp.dot(normed, w_qkv, preferred_element_type=jnp.float32)  14.8 us
    dot_general x2, matrix products, decoder_output(): return jnp.dot(hidden, dec_out, preferred_element_type=jnp.float32)  8.7 us
    ppermute x6, starting transfers between devices, ring_gather(): parts.append(lax.ppermute(values, 'mask', pairs))  8.16 us
    dot_general x6, matrix products, decoder_output(): jnp.einsum('pgi,gio->pgo', padded[offset:offset + total_rows], conv_w[off...  4.61 us
    dot_general x2, matrix products, decoder_output(): jnp.dot(visible_out, dec_in, preferred_element_type=jnp.float32)  4.51 us
    dot_general x4, matrix products, mix_heads(): jnp.einsum('hqk,khd->qhd', weights, values, preferred_element_type=jnp.fl...  3.88 us
    ppermute x6, waiting for transfers between devices, ring_gather(): parts.append(lax.ppermute(values, 'mask', pairs))  3.77 us
    dot_general x4, matrix products, mix_heads(): jnp.einsum('qhd,khd->hqk', queries, key_rows, preferred_element_type=jnp....  3.71 us
  transfers between devices with their start and end apart: 6, of which 3 were waited for; matrix products, arithmetic and copies ran while one was open for 8% of the time, Pallas kernels for 0%

profile of v4, /device:TPU:0, one launch (start us, length us, event | category | flops | bytes accessed | tf_op | source)
XLA Modules:
  0.0 86.6 jit_solution(1157546131260529301)
XLA Ops:
  0.6 3.0 %collective-permute-start = (bf16[64,768]{1,0:T(8,128)(2,1)}, bf16[64,768]{1,0:T(8,128)(2,1)S(1)}, u32[]{:S(2)}, u32[]{:S(2)}) collective-permute-start(bf16[64,768]{1,0:T(8,128)(2,1)} %param.9), channel_id=1, source_target_pairs={{0,1},{1,2},{2,3},{3,0},{4,5},{5,6},{6,7},{7,4},{8,9},{9,10},{10,1... | collective-permute-start | bytes 294920 | tf_op jit(solution)/shard_map/ppermute | solution.py:99
  3.7 1.5 %collective-permute-start.1 = (bf16[64,768]{1,0:T(8,128)(2,1)}, bf16[64,768]{1,0:T(8,128)(2,1)S(1)}, u32[]{:S(2)}, u32[]{:S(2)}) collective-permute-start(bf16[64,768]{1,0:T(8,128)(2,1)} %param.9), channel_id=1, source_target_pairs={{0,2},{1,3},{2,0},{3,1},{4,6},{5,7},{6,4},{7,5},{8,10},{9,11},{10,... | collective-permute-start | bytes 294920 | tf_op jit(solution)/shard_map/ppermute | solution.py:99
  5.2 1.4 %collective-permute-start.2 = (bf16[64,768]{1,0:T(8,128)(2,1)}, bf16[64,768]{1,0:T(8,128)(2,1)S(1)}, u32[]{:S(2)}, u32[]{:S(2)}) collective-permute-start(bf16[64,768]{1,0:T(8,128)(2,1)} %param.9), channel_id=1, source_target_pairs={{0,3},{1,0},{2,1},{3,2},{4,7},{5,4},{6,5},{7,6},{8,11},{9,8},{10,9... | collective-permute-start | bytes 294920 | tf_op jit(solution)/shard_map/ppermute | solution.py:99
  9.5 1.2 %gather_fusion = s32[4,51]{1,0:T(4,128)S(1)} fusion(s32[4,51]{1,0:T(4,128)} %param.10, s32[1024]{0:T(1024)S(1)} %pad_clamp_fusion.2), kind=kCustom, calls=%fused_computation | custom fusion | bytes 1648 | tf_op jit(solution)/shard_map/gather | solution.py:165
  10.9 1.7 %convolution_reduce_fusion = bf16[768]{0:T(1024)(128)(2,1)S(1)} fusion(bf16[1024,1]{0,1:T(2,128)(2,1)S(1)} %reshape.343, bf16[1024,768]{1,0:T(8,128)(2,1)} %param.15), kind=kOutput, calls=%fused_computation.56 | convolution fusion | flops 1572864 | bytes 1576448 | tf_op jit(solution)/shard_map/jvp()/dot_general | solution.py:61
  12.6 1.0 %select_select_fusion.3 = (bf16[64,768]{1,0:T(8,128)(2,1)S(1)}, bf16[64,768]{1,0:T(8,128)(2,1)S(1)}, bf16[64,768]{1,0:T(8,128)(2,1)S(1)}, bf16[64,768]{1,0:T(8,128)(2,1)S(1)}) fusion(bf16[64,768]{1,0:T(8,128)(2,1)S(1)} %collective-permute-done, bf16[64,768]{1,0:T(8,128)(2,1)S(1)} %collective-permute-done.1, bf16[64,768]{1,0:T(8,128)(2,1)S(1)} %collective-permute-done.2, ...), kind=kLoop, calls=%fused_computation.188 | loop fusion | flops 589824 | bytes 786444 | tf_op jit(solution)/shard_map/jit(_where)/select_n | solution.py:110
  13.6 2.2 %convert_reduce_fusion = (f32[256]{0:T(256)S(1)}, bf16[256,1024]{1,0:T(8,128)(2,1)S(1)}) fusion(bf16[768,1024]{1,0:T(8,128)(2,1)} %param.11, bf16[64,768]{1,0:T(8,128)(2,1)S(1)} %get-tuple-element.10, bf16[64,768]{1,0:T(8,128)(2,1)S(1)} %get-tuple-element.11, bf16[64,768]{1,0:T(8,128)(2,1)S(1)} %get-tuple-element.12, bf16[64,768]{1,0:T(8,128)(2,1)S(1)} %get-tuple-element.9), kind=kOutput, calls=%fused_computation.16 | convolution fusion | flops 405012224 | bytes 2491392 | tf_op jit(solution)/shard_map/dot_general | solution.py:145
  16.1 5.8 %convolution_convert_fusion = bf16[256,3072]{1,0:T(8,128)(2,1)} fusion(bf16[1024,3072]{1,0:T(8,128)(2,1)} %param.12, bf16[256,1024]{1,0:T(8,128)(2,1)S(1)} %get-tuple-element.16, f32[256]{0:T(256)S(1)} %add_rsqrt_fusion.3, f32[256]{0:T(256)S(1)} %broadcast_multiply_fusion.2), kind=kOutput, calls=%fused_computation.5 | convolution fusion | flops 1612447744 | bytes 8390656 | tf_op jit(solution)/shard_map/dot_general | solution.py:49
  22.0 2.6 %copy.62 = bf16[256,3072]{0,1:T(8,128)(2,1)} copy(bf16[256,3072]{1,0:T(8,128)(2,1)} %convolution_convert_fusion) | data formatting | bytes 3145728 | tf_op jit(solution)/shard_map/convert_element_type | solution.py:49
  24.5 1.5 %fusion.22 = (f32[256,16]{0,1:T(8,128)S(1)}, f32[256,16]{0,1:T(8,128)S(1)}) fusion(bf16[256,3,16,64]{0,3,2,1:T(8,128)(2,1)} %bitcast.169), kind=kLoop, calls=%fused_computation.59 | loop fusion | flops 1564672 | bytes 1081344 | tf_op jit(solution)/shard_map/reduce_sum | solution.py:25
  26.0 2.2 %fusion = (f32[16,256]{1,0:T(8,128)S(1)}, f32[16,256,256]{1,2,0:T(8,128)S(1)}) fusion(f32[256,16]{0,1:T(8,128)S(1)} %get-tuple-element.39, bf16[256,3,16,64]{0,3,2,1:T(8,128)(2,1)} %bitcast.170, f32[256,16]{0,1:T(8,128)S(1)} %get-tuple-element.40), kind=kOutput, calls=%fused_computation.6 | convolution fusion | flops 137883648 | bytes 5292032 | tf_op jit(solution)/shard_map/qhd,khd->hqk/dot_general | solution.py:31
  28.2 1.9 %fusion.3 = bf16[16,64,256]{2,1,0:T(8,128)(2,1)S(1)} fusion(f32[16,256,256]{1,2,0:T(8,128)S(1)} %get-tuple-element.18, f32[16,256]{1,0:T(8,128)S(1)} %get-tuple-element.17, bf16[256,3,16,64]{0,3,2,1:T(8,128)(2,1)} %bitcast.171), kind=kOutput, calls=%fused_computation.17 | convolution fusion | flops 137625600 | bytes 5259264 | tf_op jit(solution)/shard_map/hqk,khd->qhd/dot_general | solution.py:36
  33.5 4.0 %convolution_convert_fusion.1 = bf16[51,3072]{1,0:T(8,128)(2,1)S(1)} fusion(bf16[1024,3072]{1,0:T(8,128)(2,1)} %param.12, bf16[51,1024]{1,0:T(8,128)(2,1)S(1)} %gather_fusion.2, f32[51]{0:T(128)S(1)} %fusion.126, f32[51]{0:T(128)S(1)} %broadcast_multiply_fusion.4), kind=kOutput, calls=%fused_computation.7 | convolution fusion | flops 321229824 | bytes 6709656 | tf_op jit(solution)/shard_map/jvp()/dot_general | solution.py:49
  40.3 2.2 %convolution_convert_fusion.16 = bf16[51,768]{1,0:T(8,128)(2,1)S(1)} fusion(bf16[1024,768]{1,0:T(8,128)(2,1)} %param.15, bf16[51,1024]{1,0:T(8,128)(2,1)S(1)} %reshape.305, bf16[1024,1024]{1,0:T(8,128)(2,1)S(1)} %copy-done, bf16[51,1024]{1,0:T(8,128)(2,1)S(1)} %gather_fusion.2), kind=kOutput, calls=%fused_computation.55 | convolution fusion | flops 187366656 | bytes 3957248 | tf_op jit(solution)/shard_map/jvp()/dot_general | solution.py:58
  43.7 1.3 %fusion.71 = f32[16,256,48]{1,2,0:T(8,128)S(1)} fusion(bf16[256,16,48]{0,2,1:T(8,128)(2,1)S(1)} %bitcast.176, bf16[3,16,48,48]{3,2,1,0:T(8,128)(2,1)} %param.16), kind=kOutput, calls=%fused_computation.138 | convolution fusion | flops 18874368 | bytes 1376256 | tf_op jit(solution)/shard_map/jvp(pgi,gio->pgo)/dot_general | solution.py:70
  45.0 1.2 %convolution_add_fusion.1 = f32[16,256,48]{1,2,0:T(8,128)S(1)} fusion(f32[16,256,48]{1,2,0:T(8,128)S(1)} %fusion.71, bf16[256,16,48]{0,2,1:T(8,128)(2,1)S(1)} %bitcast.177, bf16[3,16,48,48]{3,2,1,0:T(8,128)(2,1)} %param.16), kind=kOutput, calls=%fused_computation.19 | convolution fusion | flops 19070976 | bytes 2162688 | tf_op jit(solution)/shard_map/jvp(pgi,gio->pgo)/dot_general | solution.py:70
  46.2 1.4 %fusion.140 = (f32[256]{0:T(256)S(1)}, f32[16,256,48]{1,2,0:T(8,128)S(1)}) fusion(f32[16,256,48]{1,2,0:T(8,128)S(1)} %convolution_add_fusion.1, bf16[256,16,48]{0,2,1:T(8,128)(2,1)S(1)} %bitcast.178, bf16[3,16,48,48]{3,2,1,0:T(8,128)(2,1)} %param.16), kind=kOutput, calls=%fused_computation.248 | convolution fusion | flops 19267328 | bytes 2163712 | tf_op jit(solution)/shard_map/jvp(pgi,gio->pgo)/dot_general | solution.py:70
  47.8 1.2 %copy.61 = f32[256,768]{1,0:T(8,128)} copy(f32[256,768]{0,1:T(8,128)S(1)} %bitcast.172) | data formatting | bytes 1572864 | tf_op jit(solution)/shard_map/jvp()/reshape | solution.py:76
  48.9 5.2 %multiply_reduce_fusion = (f32[]{:T(128)}, f32[256,1024]{1,0:T(8,128)S(1)}) fusion(f32[256]{0:T(256)} %get-tuple-element.14, f32[256]{0:T(256)} %add_rsqrt_fusion.2, f32[256,1024]{1,0:T(8,128)} %copy-done.1, f32[256]{0:T(256)} %copy-done.21, bf16[768,1024]{1,0:T(8,128)(2,1)} %param.17, bf16[256,768]{1,0:T(8,128)(2,1)S(1)} %copy-done.20, ...), kind=kOutput, calls=%fused_computation.65 | convolution fusion | flops 418709504 | bytes 4854788 | tf_op jit(solution)/shard_map/jvp()/dot_general | solution.py:78
  54.1 3.5 %multiply_reduce_fusion.2 = (f32[256]{0:T(256)S(1)}, bf16[256,768]{1,0:T(8,128)(2,1)S(1)}) fusion(f32[256,768]{1,0:T(8,128)S(1)} %copy-done.2, f32[256]{0:T(256)S(1)} %broadcast_multiply_fusion.3, f32[256]{0:T(256)S(1)} %fusion.122, bf16[768,1024]{1,0:T(8,128)(2,1)S(1)} %copy-done.29, f32[256,1024]{1,0:T(8,128)S(1)} %get-tuple-element.36, f32[256]{0:T(256)S(1)} %copy-done.22), kind=kOutput, calls=%fused_computation.90 | convolution fusion | flops 419495680 | bytes 3805184 | tf_op jit(solution)/shard_map/transpose(jvp())/dot_general | solution.py:78
  57.7 2.5 %fusion.136 = (f32[256]{0:T(256)S(1)}, f32[256,768]{1,0:T(8,128)S(1)}) fusion(f32[256]{0:T(256)S(1)} %multiply_multiply_fusion.8, bf16[256,768]{1,0:T(8,128)(2,1)S(1)} %get-tuple-element.26, f32[256]{0:T(256)S(1)} %fusion.122, f32[256,768]{1,0:T(8,128)S(1)} %copy-done.2, f32[256]{0:T(256)S(1)} %broadcast_multiply_fusion.3), kind=kLoop, calls=%fused_computation.244 | loop fusion | flops 15531776 | bytes 1970176 | tf_op jit(solution)/shard_map/transpose(jvp())/reduce_sum | solution.py:19
  60.3 0.8 broadcast_add_fusion
  61.1 1.2 %copy.64 = bf16[256,768]{0,1:T(8,128)(2,1)S(1)} copy(bf16[256,768]{1,0:T(8,128)(2,1)} %broadcast_add_fusion) | data formatting | bytes 786432 | tf_op jit(solution)/shard_map/transpose(jvp())/add_any | solution.py:18
  63.6 2.3 %convolution_convert_fusion.13 = bf16[51,1024]{1,0:T(8,128)(2,1)S(1)} fusion(bf16[1024,768]{1,0:T(8,128)(2,1)} %param.15, bf16[256,768]{1,0:T(8,128)(2,1)} %copy-done.8, bf16[256,768]{1,0:T(8,128)(2,1)S(1)} %copy.68, pred[256]{0:T(512)(128)(4,1)S(1)} %copy-done.26, s32[51]{0:T(128)S(1)} %copy-done.24), kind=kOutput, calls=%fused_computation.51 | convolution fusion | flops 100964352 | bytes 2464204 | tf_op jit(solution)/shard_map/transpose(jvp())/dot_general | solution.py:58
  66.9 1.4 %fusion.17 = bf16[51,1,16,64]{3,0,2,1:T(8,128)(2,1)S(1)} fusion(bf16[51,16,64]{2,1,0:T(8,128)(2,1)S(1)} %reshape.312, f32[16,51,51]{1,2,0:T(8,128)} %copy-done.11, f32[16,51]{1,0:T(8,128)S(1)} %get-tuple-element.21), kind=kOutput, calls=%fused_computation.47 | convolution fusion | flops 5462304 | bytes 378624 | tf_op jit(solution)/shard_map/transpose(jvp(hqk,khd->qhd))/dot_general | solution.py:36
  71.0 5.0 %fusion.88 = (f32[51]{0:T(128)S(1)}, f32[51,1024]{1,0:T(8,128)S(1)}) fusion(bf16[51,1024]{1,0:T(8,128)(2,1)S(1)} %gather_fusion.2, f32[51]{0:T(128)S(1)} %broadcast_multiply_fusion.4, bf16[51,3072]{1,0:T(8,128)(2,1)S(1)} %reshape.313, bf16[1024,3072]{1,0:T(8,128)(2,1)} %param.12), kind=kOutput, calls=%fused_computation.159 | convolution fusion | flops 321177536 | bytes 6918552 | tf_op jit(solution)/shard_map/transpose(jvp())/dot_general | solution.py:49
  77.0 1.5 %collective-permute-start.4 = (bf16[51,1024]{1,0:T(8,128)(2,1)S(1)}, bf16[51,1024]{1,0:T(8,128)(2,1)S(1)}, u32[]{:S(2)}, u32[]{:S(2)}) collective-permute-start(bf16[51,1024]{1,0:T(8,128)(2,1)S(1)} %fusion.111), channel_id=1, source_target_pairs={{0,2},{1,3},{2,0},{3,1},{4,6},{5,7},{6,4},{7,5},{8,10},{9,11},{10,... | collective-permute-start | bytes 313352 | tf_op jit(solution)/shard_map/ppermute | solution.py:99
  78.8 1.0 %gather_fusion.1 = bf16[204,192]{1,0:T(8,128)(2,1)S(1)} fusion(bf16[256,192]{1,0:T(8,128)(2,1)S(1)} %constant_dynamic-slice_fusion.1, s32[1024]{0:T(1024)S(1)} %pad_clamp_fusion.1), kind=kCustom, calls=%fused_computation.1 | custom fusion | bytes 157488 | tf_op jit(solution)/shard_map/gather | solution.py:167
  80.5 1.5 %collective-permute-done.3 = bf16[51,1024]{1,0:T(8,128)(2,1)S(1)} collective-permute-done((bf16[51,1024]{1,0:T(8,128)(2,1)S(1)}, bf16[51,1024]{1,0:T(8,128)(2,1)S(1)}, u32[]{:S(2)}, u32[]{:S(2)}) %collective-permute-start.3) | collective-permute-done | bytes 104480 | tf_op jit(solution)/shard_map/ppermute | solution.py:99
  82.0 1.0 %collective-permute-done.4 = bf16[51,1024]{1,0:T(8,128)(2,1)S(1)} collective-permute-done((bf16[51,1024]{1,0:T(8,128)(2,1)S(1)}, bf16[51,1024]{1,0:T(8,128)(2,1)S(1)}, u32[]{:S(2)}, u32[]{:S(2)}) %collective-permute-start.4) | collective-permute-done | bytes 104480 | tf_op jit(solution)/shard_map/ppermute | solution.py:99
  83.0 1.2 %collective-permute-done.5 = bf16[51,1024]{1,0:T(8,128)(2,1)S(1)} collective-permute-done((bf16[51,1024]{1,0:T(8,128)(2,1)S(1)}, bf16[51,1024]{1,0:T(8,128)(2,1)S(1)}, u32[]{:S(2)}, u32[]{:S(2)}) %collective-permute-start.5) | collective-permute-done | bytes 104480 | tf_op jit(solution)/shard_map/ppermute | solution.py:99
  84.2 1.2 %fusion.63 = f32[192,1024]{1,0:T(8,128)} fusion(bf16[204,192]{1,0:T(8,128)(2,1)S(1)} %gather_fusion.1, bf16[51,1024]{1,0:T(8,128)(2,1)S(1)} %collective-permute-done.5, bf16[51,1024]{1,0:T(8,128)(2,1)S(1)} %collective-permute-done.4, bf16[51,1024]{1,0:T(8,128)(2,1)S(1)} %collective-permute-done.3, bf16[51,1024]{1,0:T(8,128)(2,1)S(1)} %fusion.111), kind=kOutput, calls=%fused_computation.130 | convolution fusion | flops 81887232 | bytes 1282560 | tf_op jit(solution)/shard_map/vc,vd->cd/dot_general | solution.py:168
  (132 shorter events, 16.7 us)
Async XLA Ops:
  0.6 29.5 %copy-start = (bf16[1024,1024]{1,0:T(8,128)(2,1)S(1)}, bf16[1024,1024]{1,0:T(8,128)(2,1)}, u32[]{:S(2)}) copy-start(bf16[1024,1024]{1,0:T(8,128)(2,1)} %param.13) | copy-start | bytes 6291460
  0.6 12.0 %collective-permute-start = (bf16[64,768]{1,0:T(8,128)(2,1)}, bf16[64,768]{1,0:T(8,128)(2,1)S(1)}, u32[]{:S(2)}, u32[]{:S(2)}) collective-permute-start(bf16[64,768]{1,0:T(8,128)(2,1)} %param.9), channel_id=1, source_target_pairs={{0,1},{1,2},{2,3},{3,0},{4,5},{5,6},{6,7},{7,4},{8,9},{9,10},{10,1... | collective-permute-start | bytes 294920 | tf_op jit(solution)/shard_map/ppermute | solution.py:99
  3.7 9.0 %collective-permute-start.1 = (bf16[64,768]{1,0:T(8,128)(2,1)}, bf16[64,768]{1,0:T(8,128)(2,1)S(1)}, u32[]{:S(2)}, u32[]{:S(2)}) collective-permute-start(bf16[64,768]{1,0:T(8,128)(2,1)} %param.9), channel_id=1, source_target_pairs={{0,2},{1,3},{2,0},{3,1},{4,6},{5,7},{6,4},{7,5},{8,10},{9,11},{10,... | collective-permute-start | bytes 294920 | tf_op jit(solution)/shard_map/ppermute | solution.py:99
  5.2 7.5 %collective-permute-start.2 = (bf16[64,768]{1,0:T(8,128)(2,1)}, bf16[64,768]{1,0:T(8,128)(2,1)S(1)}, u32[]{:S(2)}, u32[]{:S(2)}) collective-permute-start(bf16[64,768]{1,0:T(8,128)(2,1)} %param.9), channel_id=1, source_target_pairs={{0,3},{1,0},{2,1},{3,2},{4,7},{5,4},{6,5},{7,6},{8,11},{9,8},{10,9... | collective-permute-start | bytes 294920 | tf_op jit(solution)/shard_map/ppermute | solution.py:99
  8.0 34.5 %copy-start.23 = (s32[51]{0:T(128)}, s32[51]{0:T(128)S(1)}, u32[]{:S(2)}) copy-start(s32[51]{0:T(128)S(1)} %fusion.127) | copy-start | bytes 616
  8.2 34.3 %copy-start.25 = (pred[256]{0:T(512)(128)(4,1)}, pred[256]{0:T(512)(128)(4,1)S(1)}, u32[]{:S(2)}) copy-start(pred[256]{0:T(512)(128)(4,1)S(1)} %broadcast_compare_fusion) | copy-start | bytes 772
  13.6 2.5 %copy-start.13 = (bf16[64,768]{1,0:T(8,128)(2,1)}, bf16[64,768]{1,0:T(8,128)(2,1)S(1)}, u32[]{:S(2)}) copy-start(bf16[64,768]{1,0:T(8,128)(2,1)S(1)} %get-tuple-element.10) | copy-start | bytes 294916
  13.6 2.5 %copy-start.15 = (bf16[64,768]{1,0:T(8,128)(2,1)}, bf16[64,768]{1,0:T(8,128)(2,1)S(1)}, u32[]{:S(2)}) copy-start(bf16[64,768]{1,0:T(8,128)(2,1)S(1)} %get-tuple-element.11) | copy-start | bytes 294916
  13.6 2.5 %copy-start.17 = (bf16[64,768]{1,0:T(8,128)(2,1)}, bf16[64,768]{1,0:T(8,128)(2,1)S(1)}, u32[]{:S(2)}) copy-start(bf16[64,768]{1,0:T(8,128)(2,1)S(1)} %get-tuple-element.12) | copy-start | bytes 294916
  31.0 6.6 %copy-start.21 = (f32[256]{0:T(256)}, f32[256]{0:T(256)S(1)}, u32[]{:S(2)}) copy-start(f32[256]{0:T(256)S(1)} %broadcast_multiply_fusion.1) | copy-start | bytes 3076
  33.5 4.1 %copy-start.27 = (f32[51]{0:T(128)}, f32[51]{0:T(128)S(1)}, u32[]{:S(2)}) copy-start(f32[51]{0:T(128)S(1)} %fusion.86) | copy-start | bytes 616
  38.1 1.2 %copy-start.6 = (bf16[51,1,16,64]{3,2,1,0:T(8,128)(2,1)}, bf16[51,1,16,64]{3,2,1,0:T(8,128)(2,1)S(1)}, u32[]{:S(2)}) copy-start(bf16[51,1,16,64]{3,2,1,0:T(8,128)(2,1)S(1)} %get-tuple-element.8) | copy-start | bytes 313348
  38.1 1.2 %copy-start.9 = (bf16[51,1,16,64]{3,2,1,0:T(8,128)(2,1)}, bf16[51,1,16,64]{3,2,1,0:T(8,128)(2,1)S(1)}, u32[]{:S(2)}) copy-start(bf16[51,1,16,64]{3,2,1,0:T(8,128)(2,1)S(1)} %get-tuple-element.7) | copy-start | bytes 313348
  47.6 1.3 %copy-start.20 = (bf16[256,768]{1,0:T(8,128)(2,1)S(1)}, bf16[256,768]{1,0:T(8,128)(2,1)}, u32[]{:S(2)}) copy-start(bf16[256,768]{1,0:T(8,128)(2,1)} %copy-done.19) | copy-start | bytes 1179652
  48.9 5.2 %copy-start.2 = (f32[256,768]{1,0:T(8,128)S(1)}, f32[256,768]{1,0:T(8,128)}, u32[]{:S(2)}) copy-start(f32[256,768]{1,0:T(8,128)} %copy.61) | copy-start | bytes 2359300
  48.9 5.2 %copy-start.22 = (f32[256]{0:T(256)S(1)}, f32[256]{0:T(256)}, u32[]{:S(2)}) copy-start(f32[256]{0:T(256)} %get-tuple-element.13) | copy-start | bytes 3076
  48.9 5.2 %copy-start.29 = (bf16[768,1024]{1,0:T(8,128)(2,1)S(1)}, bf16[768,1024]{1,0:T(8,128)(2,1)}, u32[]{:S(2)}) copy-start(bf16[768,1024]{1,0:T(8,128)(2,1)} %param.17) | copy-start | bytes 4718596
  57.7 2.6 %copy-start.8 = (bf16[256,768]{1,0:T(8,128)(2,1)}, bf16[256,768]{1,0:T(8,128)(2,1)S(1)}, u32[]{:S(2)}) copy-start(bf16[256,768]{1,0:T(8,128)(2,1)S(1)} %get-tuple-element.26) | copy-start | bytes 1179652
  57.7 4.6 %copy-start.3 = (bf16[3,16,48,48]{3,2,1,0:T(8,128)(2,1)S(1)}, bf16[3,16,48,48]{3,2,1,0:T(8,128)(2,1)}, u32[]{:S(2)}) copy-start(bf16[3,16,48,48]{3,2,1,0:T(8,128)(2,1)} %param.16) | copy-start | bytes 663556
  62.5 1.0 %copy-start.24 = (s32[51]{0:T(128)S(1)}, s32[51]{0:T(128)}, u32[]{:S(2)}) copy-start(s32[51]{0:T(128)} %copy-done.23) | copy-start | bytes 616
  62.6 1.0 %copy-start.26 = (pred[256]{0:T(512)(128)(4,1)S(1)}, pred[256]{0:T(512)(128)(4,1)}, u32[]{:S(2)}) copy-start(pred[256]{0:T(512)(128)(4,1)} %copy-done.25) | copy-start | bytes 772
  65.9 2.3 %copy-start.10 = (bf16[51,1,16,64]{3,2,1,0:T(8,128)(2,1)S(1)}, bf16[51,1,16,64]{3,2,1,0:T(8,128)(2,1)}, u32[]{:S(2)}) copy-start(bf16[51,1,16,64]{3,2,1,0:T(8,128)(2,1)} %copy-done.9) | copy-start | bytes 313348
  66.7 1.9 %copy-start.5 = (bf16[51,1,16,64]{3,2,1,0:T(8,128)(2,1)S(1)}, bf16[51,1,16,64]{3,2,1,0:T(8,128)(2,1)}, u32[]{:S(2)}) copy-start(bf16[51,1,16,64]{3,2,1,0:T(8,128)(2,1)} %copy-done.4) | copy-start | bytes 313348
  66.7 1.9 %copy-start.7 = (bf16[51,1,16,64]{3,2,1,0:T(8,128)(2,1)S(1)}, bf16[51,1,16,64]{3,2,1,0:T(8,128)(2,1)}, u32[]{:S(2)}) copy-start(bf16[51,1,16,64]{3,2,1,0:T(8,128)(2,1)} %copy-done.6) | copy-start | bytes 313348
  66.9 1.4 %copy-start.12 = (f32[16,51,51]{1,2,0:T(8,128)S(1)}, f32[16,51,51]{1,2,0:T(8,128)}, u32[]{:S(2)}) copy-start(f32[16,51,51]{1,2,0:T(8,128)} %copy-done.11) | copy-start | bytes 499396
  71.0 5.0 %copy-start.28 = (f32[51]{0:T(128)S(1)}, f32[51]{0:T(128)}, u32[]{:S(2)}) copy-start(f32[51]{0:T(128)} %copy-done.27) | copy-start | bytes 616
  71.0 7.6 %copy-start.14 = (bf16[64,768]{1,0:T(8,128)(2,1)S(1)}, bf16[64,768]{1,0:T(8,128)(2,1)}, u32[]{:S(2)}) copy-start(bf16[64,768]{1,0:T(8,128)(2,1)} %copy-done.13) | copy-start | bytes 294916
  71.0 7.6 %copy-start.16 = (bf16[64,768]{1,0:T(8,128)(2,1)S(1)}, bf16[64,768]{1,0:T(8,128)(2,1)}, u32[]{:S(2)}) copy-start(bf16[64,768]{1,0:T(8,128)(2,1)} %copy-done.15) | copy-start | bytes 294916
  71.0 7.6 %copy-start.18 = (bf16[64,768]{1,0:T(8,128)(2,1)S(1)}, bf16[64,768]{1,0:T(8,128)(2,1)}, u32[]{:S(2)}) copy-start(bf16[64,768]{1,0:T(8,128)(2,1)} %copy-done.17) | copy-start | bytes 294916
  76.4 5.5 %collective-permute-start.3 = (bf16[51,1024]{1,0:T(8,128)(2,1)S(1)}, bf16[51,1024]{1,0:T(8,128)(2,1)S(1)}, u32[]{:S(2)}, u32[]{:S(2)}) collective-permute-start(bf16[51,1024]{1,0:T(8,128)(2,1)S(1)} %fusion.111), channel_id=1, source_target_pairs={{0,3},{1,0},{2,1},{3,2},{4,7},{5,4},{6,5},{7,6},{8,11},{9,8},{10,9... | collective-permute-start | bytes 313352 | tf_op jit(solution)/shard_map/ppermute | solution.py:99
  77.0 6.0 %collective-permute-start.4 = (bf16[51,1024]{1,0:T(8,128)(2,1)S(1)}, bf16[51,1024]{1,0:T(8,128)(2,1)S(1)}, u32[]{:S(2)}, u32[]{:S(2)}) collective-permute-start(bf16[51,1024]{1,0:T(8,128)(2,1)S(1)} %fusion.111), channel_id=1, source_target_pairs={{0,2},{1,3},{2,0},{3,1},{4,6},{5,7},{6,4},{7,5},{8,10},{9,11},{10,... | collective-permute-start | bytes 313352 | tf_op jit(solution)/shard_map/ppermute | solution.py:99
  78.6 5.7 %collective-permute-start.5 = (bf16[51,1024]{1,0:T(8,128)(2,1)S(1)}, bf16[51,1024]{1,0:T(8,128)(2,1)S(1)}, u32[]{:S(2)}, u32[]{:S(2)}) collective-permute-start(bf16[51,1024]{1,0:T(8,128)(2,1)S(1)} %fusion.111), channel_id=1, source_target_pairs={{0,1},{1,2},{2,3},{3,0},{4,5},{5,6},{6,7},{7,4},{8,9},{9,10},{10,1... | collective-permute-start | bytes 313352 | tf_op jit(solution)/shard_map/ppermute | solution.py:99
  (4 other events, 3.2 us)

commit v5 on v4

--- a/solution.py
+++ b/solution.py
@@ -43,12 +43,44 @@
     return mix_heads(queries, key_rows, projected[:, 2])
 
 
-def attention_branch(inputs, w_qkv, w_out):
+def project_heads(inputs, w_qkv):
     row_count = inputs.shape[0]
     normed = row_norm(inputs.astype(jnp.float32)).astype(jnp.bfloat16)
     projected = jnp.dot(normed, w_qkv, preferred_element_type=jnp.float32).astype(jnp.bfloat16)
-    context = split_project(projected.reshape(row_count, 3, HEADS, D // HEADS))
+    projected = projected.reshape(row_count, 3, HEADS, D // HEADS)
+    queries = head_norm(projected[:, 0].astype(jnp.float32)).astype(jnp.bfloat16)
+    key_rows = head_norm(projected[:, 1].astype(jnp.float32)).astype(jnp.bfloat16)
+    return queries, key_rows, projected[:, 2]
+
+
+def attention_from(heads, w_out):
+    context = mix_heads(*heads)
+    row_count = context.shape[0]
     return jnp.dot(context.reshape(row_count, D), w_out, preferred_element_type=jnp.float32)
+
+
+def attention_branch(inputs, w_qkv, w_out):
+    return attention_from(project_heads(inputs, w_qkv), w_out)
+
+
+@jax.custom_vjp
+def reuse_heads(inputs, w_qkv, heads):
+    return heads
+
+
+def reuse_heads_fwd(inputs, w_qkv, heads):
+    return heads, (inputs, w_qkv)
+
+
+def reuse_heads_bwd(saved, cotangents):
+    inputs, w_qkv = saved
+    _, pullback = jax.vjp(lambda rows: project_heads(rows, w_qkv), inputs)
+    (d_inputs,) = pullback(cotangents)
+    zeros = tuple(jnp.zeros_like(part) for part in cotangents)
+    return d_inputs, jnp.zeros_like(w_qkv), zeros
+
+
+reuse_heads.defvjp(reuse_heads_fwd, reuse_heads_bwd)
 
 
 def decoder_output(visible_out, positions, total_rows, mask_embed, dec_in, conv_w, dec_out):
@@ -78,11 +110,15 @@
     return jnp.dot(hidden, dec_out, preferred_element_type=jnp.float32)
 
 
-def copy_terms(visible_in, positions, targets, w_qkv, w_out, mask_embed, dec_in, conv_w, dec_out):
+def copy_terms(
+    visible_in, positions, targets, w_qkv, w_out, mask_embed, dec_in, conv_w, dec_out, heads
+):
     total_rows = targets.shape[0]
-    visible_out = (
-        visible_in.astype(jnp.float32) + attention_branch(visible_in, w_qkv, w_out)
-    ).astype(jnp.bfloat16)
+    if heads is None:
+        branch = attention_branch(visible_in, w_qkv, w_out)
+    else:
+        branch = attention_from(reuse_heads(visible_in, w_qkv, heads), w_out)
+    visible_out = (visible_in.astype(jnp.float32) + branch).astype(jnp.bfloat16)
     predicted = decoder_output(
         visible_out, positions, total_rows, mask_embed, dec_in, conv_w, dec_out
     )
@@ -147,14 +183,26 @@
     )
     visible_in = embedded[positions]
     if HEADS * total_rows * total_rows * 4 <= (1 << 24):
-        branch = attention_branch(embedded, w_qkv, w_out)
+        clip_heads = project_heads(embedded, w_qkv)
+        branch = attention_from(clip_heads, w_out)
+        visible_heads = tuple(part[positions] for part in clip_heads)
     else:
         branch = split_teacher(embedded, w_qkv, w_out, own_index, group_size)
+        visible_heads = None
     all_targets = row_norm(branch).astype(jnp.bfloat16)
 
     def objective(rows_in):
         return copy_terms(
-            rows_in, positions, all_targets, w_qkv, w_out, mask_embed, dec_in, conv_w, dec_out
+            rows_in,
+            positions,
+            all_targets,
+            w_qkv,
+            w_out,
+            mask_embed,
+            dec_in,
+            conv_w,
+            dec_out,
+            visible_heads,
         )
 
     squares, pullback = jax.vjp(objective, visible_in)

time: 87.3 us -> 114 us (1.31)
  local copies, waits for them, and re-layouts: 13.3 us -> 32 us
  other arithmetic: 10.8 us -> 14.9 us
  matrix products: 47.3 us -> 51 us
    unnamed x61 -> x67, local copies, waits for them, and re-layouts: 2.82 us -> 10.1 us
    gather x0 -> x3, local copies, waits for them, and re-layouts: none -> 5.6 us  [on_device(): visible_heads = tuple((part[positions] for part in clip_heads))]
    squeeze x0 -> x2, local copies, waits for them, and re-layouts: none -> 4.48 us  [project_heads(): return (queries, key_rows, projected[:, 2])]
    convert_element_type x0 -> x1, other arithmetic: none -> 3.24 us  [project_heads(): head_norm(projected[:, 0].astype(jnp.float32)).astype(jnp.bfloat16)]
    dot_general x4, matrix products: 3.88 us -> 5.53 us  [mix_heads(): jnp.einsum('hqk,khd->qhd', weights, values, preferred_element_type=jnp.fl...]
    dot_general x4, matrix products: 3.71 us -> 5.23 us  [mix_heads(): jnp.einsum('qhd,khd->hqk', queries, key_rows, preferred_element_type=jnp....]
    reduce_sum x2 -> x1, other arithmetic: 2.76 us -> 2.76 us  [row_norm(): centred = values - average]
  transfers between devices with their start and end apart: 6 -> 6, of which waited for: 3 -> 3; matrix products, arithmetic and copies ran while one was open for 8% -> 7% of each run, Pallas kernels for 0% -> 0%
where the time goes in v5:
time: 114 us; the launch traced here: 113 us
  matrix products  51 us (45%)
  local copies, waits for them, and re-layouts  32 us (28%)
  other arithmetic  14.9 us (13%)
  starting transfers between devices  8.15 us (7%)
  waiting for transfers between devices  3.77 us (3%)
  between operations  3.18 us (3%)
    unnamed x67, local copies, waits for them, and re-layouts  10.1 us
    dot_general x2, matrix products, copy_terms(): branch = attention_from(reuse_heads(visible_in, w_qkv, heads), w_out)  9.72 us
    dot_general x2, matrix products, decoder_output(): return jnp.dot(hidden, dec_out, preferred_element_type=jnp.float32)  8.46 us
    ppermute x6, starting transfers between devices, ring_gather(): parts.append(lax.ppermute(values, 'mask', pairs))  8.15 us
    dot_general x1, matrix products, project_heads(): jnp.dot(normed, w_qkv, preferred_element_type=jnp.float32)  5.84 us
    gather x3, local copies, waits for them, and re-layouts, on_device(): visible_heads = tuple((part[positions] for part in clip_heads))  5.6 us
    dot_general x4, matrix products, mix_heads(): jnp.einsum('hqk,khd->qhd', weights, values, preferred_element_type=jnp.fl...  5.53 us
    dot_general x4, matrix products, mix_heads(): jnp.einsum('qhd,khd->hqk', queries, key_rows, preferred_element_type=jnp....  5.23 us
  transfers between devices with their start and end apart: 6, of which 3 were waited for; matrix products, arithmetic and copies ran while one was open for 7% of the time, Pallas kernels for 0%

profile of v5, /device:TPU:0, one launch (start us, length us, event | category | flops | bytes accessed | tf_op | source)
XLA Modules:
  0.0 113.0 jit_solution(17626459318786486899)
XLA Ops:
  0.6 3.0 %collective-permute-start = (bf16[64,768]{1,0:T(8,128)(2,1)}, bf16[64,768]{1,0:T(8,128)(2,1)S(1)}, u32[]{:S(2)}, u32[]{:S(2)}) collective-permute-start(bf16[64,768]{1,0:T(8,128)(2,1)} %param.9), channel_id=1, source_target_pairs={{0,1},{1,2},{2,3},{3,0},{4,5},{5,6},{6,7},{7,4},{8,9},{9,10},{10,1... | collective-permute-start | bytes 294920 | tf_op jit(solution)/shard_map/ppermute | solution.py:135
  3.7 1.5 %collective-permute-start.1 = (bf16[64,768]{1,0:T(8,128)(2,1)}, bf16[64,768]{1,0:T(8,128)(2,1)S(1)}, u32[]{:S(2)}, u32[]{:S(2)}) collective-permute-start(bf16[64,768]{1,0:T(8,128)(2,1)} %param.9), channel_id=1, source_target_pairs={{0,2},{1,3},{2,0},{3,1},{4,6},{5,7},{6,4},{7,5},{8,10},{9,11},{10,... | collective-permute-start | bytes 294920 | tf_op jit(solution)/shard_map/ppermute | solution.py:135
  5.2 1.4 %collective-permute-start.2 = (bf16[64,768]{1,0:T(8,128)(2,1)}, bf16[64,768]{1,0:T(8,128)(2,1)S(1)}, u32[]{:S(2)}, u32[]{:S(2)}) collective-permute-start(bf16[64,768]{1,0:T(8,128)(2,1)} %param.9), channel_id=1, source_target_pairs={{0,3},{1,0},{2,1},{3,2},{4,7},{5,4},{6,5},{7,6},{8,11},{9,8},{10,9... | collective-permute-start | bytes 294920 | tf_op jit(solution)/shard_map/ppermute | solution.py:135
  11.6 1.7 %convolution_reduce_fusion = bf16[768]{0:T(1024)(128)(2,1)S(1)} fusion(bf16[1024,1]{0,1:T(2,128)(2,1)S(1)} %reshape.367, bf16[1024,768]{1,0:T(8,128)(2,1)} %param.15), kind=kOutput, calls=%fused_computation.63 | convolution fusion | flops 1572864 | bytes 1576448 | tf_op jit(solution)/shard_map/jvp()/dot_general | solution.py:93
  14.3 2.2 %convert_reduce_fusion = (f32[256]{0:T(256)S(1)}, bf16[256,1024]{1,0:T(8,128)(2,1)S(1)}) fusion(bf16[768,1024]{1,0:T(8,128)(2,1)} %param.11, bf16[64,768]{1,0:T(8,128)(2,1)S(1)} %get-tuple-element.14, bf16[64,768]{1,0:T(8,128)(2,1)S(1)} %get-tuple-element.15, bf16[64,768]{1,0:T(8,128)(2,1)S(1)} %get-tuple-element.16, bf16[64,768]{1,0:T(8,128)(2,1)S(1)} %get-tuple-element.13), kind=kOutput, calls=%fused_computation.23 | convolution fusion | flops 405012224 | bytes 2491392 | tf_op jit(solution)/shard_map/dot_general | solution.py:181
  17.3 5.8 %convolution_convert_fusion = bf16[256,3072]{1,0:T(8,128)(2,1)} fusion(bf16[1024,3072]{1,0:T(8,128)(2,1)} %param.12, bf16[256,1024]{1,0:T(8,128)(2,1)S(1)} %get-tuple-element.24, f32[256]{0:T(256)S(1)} %add_rsqrt_fusion.3, f32[256]{0:T(256)S(1)} %broadcast_multiply_fusion.3), kind=kOutput, calls=%fused_computation.8 | convolution fusion | flops 1612447744 | bytes 8390656 | tf_op jit(solution)/shard_map/dot_general | solution.py:49
  23.1 2.6 %copy.123 = bf16[256,3072]{0,1:T(8,128)(2,1)} copy(bf16[256,3072]{1,0:T(8,128)(2,1)} %convolution_convert_fusion) | data formatting | bytes 3145728 | tf_op jit(solution)/shard_map/convert_element_type | solution.py:49
  25.7 2.6 %slice_bitcast_fusion = (bf16[256,16,64]{0,2,1:T(8,128)(2,1)}, bf16[256,1,16,64]{0,3,2,1:T(8,128)(2,1)}, bf16[256,1,16,64]{0,3,2,1:T(8,128)(2,1)}) fusion(bf16[256,3,16,64]{0,3,2,1:T(8,128)(2,1)} %bitcast.132), kind=kLoop, calls=%fused_computation.114 | loop fusion | bytes 3145728 | tf_op jit(solution)/shard_map/squeeze | solution.py:53
  28.3 2.0 %copy.163 = bf16[256,1,16,64]{3,2,0,1:T(8,128)(2,1)S(1)} copy(bf16[256,1,16,64]{0,3,2,1:T(8,128)(2,1)} %get-tuple-element.9) | data formatting | bytes 1048576
  31.1 2.9 %copy.164 = bf16[256,1,16,64]{3,2,0,1:T(8,128)(2,1)} copy(bf16[256,1,16,64]{0,3,2,1:T(8,128)(2,1)} %get-tuple-element.10) | data formatting | bytes 1048576
  34.0 1.8 %fusion.3 = f32[256,16]{1,0:T(8,128)S(1)} fusion(bf16[256,1,16,64]{3,2,0,1:T(8,128)(2,1)} %copy.164), kind=kLoop, calls=%fused_computation.17 | loop fusion | flops 782336 | bytes 540672 | tf_op jit(solution)/shard_map/reduce_sum | solution.py:25
  36.1 3.2 %fusion.2 = (bf16[256,16,64]{2,1,0:T(8,128)(2,1)S(1)}, bf16[256,16,64]{2,1,0:T(8,128)(2,1)S(1)}) fusion(bf16[256,1,16,64]{3,2,0,1:T(8,128)(2,1)S(1)} %copy.163, f32[256,16]{1,0:T(8,128)S(1)} %copy.127, f32[256,16]{1,0:T(8,128)S(1)} %copy.130, bf16[256,1,16,64]{3,2,0,1:T(8,128)(2,1)} %copy.164), kind=kLoop, calls=%fused_computation.16 | loop fusion | flops 1572864 | bytes 2129920 | tf_op jit(solution)/shard_map/convert_element_type | solution.py:51
  40.6 2.9 %fusion = (f32[16,256]{1,0:T(8,128)S(1)}, f32[16,256,256]{1,2,0:T(8,128)}) fusion(bf16[256,16,64]{2,1,0:T(8,128)(2,1)S(1)} %get-tuple-element.44, bf16[256,16,64]{2,1,0:T(8,128)(2,1)S(1)} %get-tuple-element.43), kind=kOutput, calls=%fused_computation.9 | convolution fusion | flops 136310784 | bytes 5259264 | tf_op jit(solution)/shard_map/qhd,khd->hqk/dot_general | solution.py:31
  43.5 1.8 %gather_fusion.4 = bf16[51,16,64]{2,1,0:T(8,128)(2,1)S(1)} fusion(bf16[256,16,64]{2,1,0:T(8,128)(2,1)} %copy-done.2, s32[1024]{0:T(1024)S(1)} %pad_clamp_fusion), kind=kCustom, calls=%fused_computation.4 | custom fusion | bytes 209100 | tf_op jit(solution)/shard_map/gather | solution.py:188
  45.4 1.9 %gather_fusion.5 = bf16[51,16,64]{2,1,0:T(8,128)(2,1)S(1)} fusion(bf16[256,16,64]{2,1,0:T(8,128)(2,1)} %copy-done.1, s32[1024]{0:T(1024)S(1)} %pad_clamp_fusion), kind=kCustom, calls=%fused_computation.5 | custom fusion | bytes 209100 | tf_op jit(solution)/shard_map/gather | solution.py:188
  48.0 3.2 %fusion.7 = bf16[16,64,256]{2,1,0:T(8,128)(2,1)S(1)} fusion(f32[16,256,256]{1,2,0:T(8,128)} %get-tuple-element.26, f32[16,256]{1,0:T(8,128)S(1)} %get-tuple-element.25, bf16[256,3,16,64]{0,3,2,1:T(8,128)(2,1)} %bitcast.133), kind=kOutput, calls=%fused_computation.24 | convolution fusion | flops 137625600 | bytes 5259264 | tf_op jit(solution)/shard_map/hqk,khd->qhd/dot_general | solution.py:36
  53.3 1.9 %copy.124 = bf16[256,16,64]{2,1,0:T(8,128)(2,1)} copy(bf16[256,16,64]{0,2,1:T(8,128)(2,1)S(1)} %copy-done.8) | data formatting | bytes 1048576 | tf_op jit(solution)/shard_map/squeeze | solution.py:53
  55.2 1.8 %gather_fusion.3 = bf16[51,16,64]{2,1,0:T(8,128)(2,1)S(1)} fusion(bf16[256,16,64]{2,1,0:T(8,128)(2,1)} %copy.124, s32[1024]{0:T(1024)S(1)} %pad_clamp_fusion), kind=kCustom, calls=%fused_computation.3 | custom fusion | bytes 209100 | tf_op jit(solution)/shard_map/gather | solution.py:188
  58.7 2.2 %convolution_convert_fusion.16 = bf16[51,768]{1,0:T(8,128)(2,1)S(1)} fusion(bf16[1024,768]{1,0:T(8,128)(2,1)} %param.15, bf16[51,1024]{1,0:T(8,128)(2,1)S(1)} %reshape.305, bf16[1024,1024]{1,0:T(8,128)(2,1)S(1)} %copy-done, bf16[51,1024]{1,0:T(8,128)(2,1)S(1)} %gather_fusion.2), kind=kOutput, calls=%fused_computation.62 | convolution fusion | flops 187366656 | bytes 3957248 | tf_op jit(solution)/shard_map/jvp()/dot_general | solution.py:90
  62.1 1.3 %fusion.67 = f32[16,256,48]{1,2,0:T(8,128)S(1)} fusion(bf16[256,16,48]{0,2,1:T(8,128)(2,1)S(1)} %bitcast.137, bf16[3,16,48,48]{3,2,1,0:T(8,128)(2,1)} %param.16), kind=kOutput, calls=%fused_computation.135 | convolution fusion | flops 18874368 | bytes 1376256 | tf_op jit(solution)/shard_map/jvp(pgi,gio->pgo)/dot_general | solution.py:102
  64.7 1.4 %fusion.138 = (f32[256]{0:T(256)S(1)}, f32[16,256,48]{1,2,0:T(8,128)S(1)}) fusion(f32[16,256,48]{1,2,0:T(8,128)S(1)} %convolution_add_fusion.1, bf16[256,16,48]{0,2,1:T(8,128)(2,1)S(1)} %bitcast.139, bf16[3,16,48,48]{3,2,1,0:T(8,128)(2,1)} %param.16), kind=kOutput, calls=%fused_computation.250 | convolution fusion | flops 19267328 | bytes 2163712 | tf_op jit(solution)/shard_map/jvp(pgi,gio->pgo)/dot_general | solution.py:102
  67.4 5.2 %multiply_reduce_fusion = (f32[]{:T(128)}, f32[256,1024]{1,0:T(8,128)S(1)}) fusion(f32[256]{0:T(256)S(1)} %copy-done.27, f32[256]{0:T(256)S(1)} %add_rsqrt_fusion.2, f32[256,1024]{1,0:T(8,128)} %copy-done.3, f32[256]{0:T(256)S(1)} %broadcast_multiply_fusion.2, bf16[768,1024]{1,0:T(8,128)(2,1)} %param.17, bf16[256,768]{1,0:T(8,128)(2,1)S(1)} %copy-done.25, ...), kind=kOutput, calls=%fused_computation.71 | convolution fusion | flops 418709504 | bytes 4854788 | tf_op jit(solution)/shard_map/jvp()/dot_general | solution.py:110
  72.6 3.3 %multiply_reduce_fusion.2 = (f32[256]{0:T(256)S(1)}, bf16[256,768]{1,0:T(8,128)(2,1)S(1)}) fusion(f32[256,768]{1,0:T(8,128)S(1)} %copy-done.6, f32[256]{0:T(256)S(1)} %broadcast_multiply_fusion.1, f32[256]{0:T(256)S(1)} %fusion.120, bf16[768,1024]{1,0:T(8,128)(2,1)S(1)} %copy-done.31, f32[256,1024]{1,0:T(8,128)S(1)} %get-tuple-element.42, ...), kind=kOutput, calls=%fused_computation.88 | convolution fusion | flops 419495680 | bytes 3805184 | tf_op jit(solution)/shard_map/transpose(jvp())/dot_general | solution.py:110
  75.9 2.8 %fusion.134 = (f32[256]{0:T(256)S(1)}, f32[256,768]{1,0:T(8,128)S(1)}) fusion(f32[256]{0:T(256)S(1)} %multiply_multiply_fusion.8, bf16[256,768]{1,0:T(8,128)(2,1)S(1)} %get-tuple-element.34, f32[256]{0:T(256)S(1)} %fusion.120, f32[256,768]{1,0:T(8,128)S(1)} %copy-done.6, f32[256]{0:T(256)S(1)} %broadcast_multiply_fusion.1), kind=kLoop, calls=%fused_computation.246 | loop fusion | flops 15531776 | bytes 1970176 | tf_op jit(solution)/shard_map/transpose(jvp())/reduce_sum | solution.py:19
  82.1 2.3 %convolution_convert_fusion.13 = bf16[51,1024]{1,0:T(8,128)(2,1)S(1)} fusion(bf16[1024,768]{1,0:T(8,128)(2,1)} %param.15, bf16[256,768]{1,0:T(8,128)(2,1)} %copy-done.11, bf16[256,768]{1,0:T(8,128)(2,1)S(1)} %copy.148, pred[256]{0:T(512)(128)(4,1)S(1)} %copy-done.30, s32[51]{0:T(128)S(1)} %copy-done.29), kind=kOutput, calls=%fused_computation.58 | convolution fusion | flops 100964352 | bytes 2464204 | tf_op jit(solution)/shard_map/transpose(jvp())/dot_general | solution.py:90
  87.6 4.7 %convolution_convert_fusion.1 = bf16[51,3072]{1,0:T(8,128)(2,1)} fusion(bf16[1024,3072]{1,0:T(8,128)(2,1)} %param.12, bf16[51,1024]{1,0:T(8,128)(2,1)S(1)} %gather_fusion.2, f32[51]{0:T(128)S(1)} %fusion.124, f32[51]{0:T(128)S(1)} %broadcast_multiply_fusion.4), kind=kOutput, calls=%fused_computation.10 | convolution fusion | flops 321229824 | bytes 6709656 | tf_op jit(solution)/shard_map/transpose(jvp(jvp()))/dot_general | solution.py:120
  92.4 1.4 %reshape.312 = bf16[51,3,16,64]{3,2,1,0:T(8,128)(2,1)S(1)} reshape(bf16[51,3072]{1,0:T(8,128)(2,1)} %convolution_convert_fusion.1) | data formatting | bytes 626688 | tf_op jit(solution)/shard_map/transpose(jvp(jvp()))/reshape | solution.py:120
  93.9 1.6 %fusion.55 = (f32[51,16]{0,1:T(8,128)S(1)}, f32[51,16]{0,1:T(8,128)S(1)}, f32[51,16,64]{2,0,1:T(8,128)S(1)}) fusion(bf16[51,1,16,64]{3,2,1,0:T(8,128)(2,1)S(1)} %get-tuple-element.11, bf16[51,16,64]{2,1,0:T(8,128)(2,1)} %copy-done.14, f32[16,51,51]{1,2,0:T(8,128)S(1)} %copy-done.10, f32[16,51,51]{1,2,0:T(8,128)} %get-tuple-element.36, ...), kind=kOutput, calls=%fused_computation.120 | convolution fusion | flops 5857248 | bytes 763776 | tf_op jit(solution)/shard_map/transpose(jvp(qhd,khd->hqk))/dot_general | solution.py:31
  97.4 5.0 %fusion.84 = (f32[51]{0:T(128)S(1)}, f32[51,1024]{1,0:T(8,128)S(1)}) fusion(bf16[51,1024]{1,0:T(8,128)(2,1)S(1)} %gather_fusion.2, f32[51]{0:T(128)S(1)} %broadcast_multiply_fusion.4, bf16[51,3072]{1,0:T(8,128)(2,1)S(1)} %reshape.313, bf16[1024,3072]{1,0:T(8,128)(2,1)} %param.12), kind=kOutput, calls=%fused_computation.156 | convolution fusion | flops 321177536 | bytes 6918552 | tf_op jit(solution)/shard_map/transpose(jvp(transpose(jvp())))/dot_general | solution.py:120
  103.4 1.5 %collective-permute-start.4 = (bf16[51,1024]{1,0:T(8,128)(2,1)S(1)}, bf16[51,1024]{1,0:T(8,128)(2,1)S(1)}, u32[]{:S(2)}, u32[]{:S(2)}) collective-permute-start(bf16[51,1024]{1,0:T(8,128)(2,1)S(1)} %fusion.109), channel_id=1, source_target_pairs={{0,2},{1,3},{2,0},{3,1},{4,6},{5,7},{6,4},{7,5},{8,10},{9,11},{10,... | collective-permute-start | bytes 313352 | tf_op jit(solution)/shard_map/ppermute | solution.py:135
  106.9 1.5 %collective-permute-done.3 = bf16[51,1024]{1,0:T(8,128)(2,1)S(1)} collective-permute-done((bf16[51,1024]{1,0:T(8,128)(2,1)S(1)}, bf16[51,1024]{1,0:T(8,128)(2,1)S(1)}, u32[]{:S(2)}, u32[]{:S(2)}) %collective-permute-start.3) | collective-permute-done | bytes 104480 | tf_op jit(solution)/shard_map/ppermute | solution.py:135
  109.4 1.2 %collective-permute-done.5 = bf16[51,1024]{1,0:T(8,128)(2,1)S(1)} collective-permute-done((bf16[51,1024]{1,0:T(8,128)(2,1)S(1)}, bf16[51,1024]{1,0:T(8,128)(2,1)S(1)}, u32[]{:S(2)}, u32[]{:S(2)}) %collective-permute-start.5) | collective-permute-done | bytes 104480 | tf_op jit(solution)/shard_map/ppermute | solution.py:135
  (147 shorter events, 29.9 us)
Async XLA Ops:
  0.6 50.5 %copy-start = (bf16[1024,1024]{1,0:T(8,128)(2,1)S(1)}, bf16[1024,1024]{1,0:T(8,128)(2,1)}, u32[]{:S(2)}) copy-start(bf16[1024,1024]{1,0:T(8,128)(2,1)} %param.13) | copy-start | bytes 6291460
  0.6 12.7 %collective-permute-start = (bf16[64,768]{1,0:T(8,128)(2,1)}, bf16[64,768]{1,0:T(8,128)(2,1)S(1)}, u32[]{:S(2)}, u32[]{:S(2)}) collective-permute-start(bf16[64,768]{1,0:T(8,128)(2,1)} %param.9), channel_id=1, source_target_pairs={{0,1},{1,2},{2,3},{3,0},{4,5},{5,6},{6,7},{7,4},{8,9},{9,10},{10,1... | collective-permute-start | bytes 294920 | tf_op jit(solution)/shard_map/ppermute | solution.py:135
  3.7 9.7 %collective-permute-start.1 = (bf16[64,768]{1,0:T(8,128)(2,1)}, bf16[64,768]{1,0:T(8,128)(2,1)S(1)}, u32[]{:S(2)}, u32[]{:S(2)}) collective-permute-start(bf16[64,768]{1,0:T(8,128)(2,1)} %param.9), channel_id=1, source_target_pairs={{0,2},{1,3},{2,0},{3,1},{4,6},{5,7},{6,4},{7,5},{8,10},{9,11},{10,... | collective-permute-start | bytes 294920 | tf_op jit(solution)/shard_map/ppermute | solution.py:135
  5.2 8.2 %collective-permute-start.2 = (bf16[64,768]{1,0:T(8,128)(2,1)}, bf16[64,768]{1,0:T(8,128)(2,1)S(1)}, u32[]{:S(2)}, u32[]{:S(2)}) collective-permute-start(bf16[64,768]{1,0:T(8,128)(2,1)} %param.9), channel_id=1, source_target_pairs={{0,3},{1,0},{2,1},{3,2},{4,7},{5,4},{6,5},{7,6},{8,11},{9,8},{10,9... | collective-permute-start | bytes 294920 | tf_op jit(solution)/shard_map/ppermute | solution.py:135
  14.3 2.5 %copy-start.18 = (bf16[64,768]{1,0:T(8,128)(2,1)}, bf16[64,768]{1,0:T(8,128)(2,1)S(1)}, u32[]{:S(2)}) copy-start(bf16[64,768]{1,0:T(8,128)(2,1)S(1)} %get-tuple-element.14) | copy-start | bytes 294916
  14.3 2.5 %copy-start.20 = (bf16[64,768]{1,0:T(8,128)(2,1)}, bf16[64,768]{1,0:T(8,128)(2,1)S(1)}, u32[]{:S(2)}) copy-start(bf16[64,768]{1,0:T(8,128)(2,1)S(1)} %get-tuple-element.15) | copy-start | bytes 294916
  14.3 2.5 %copy-start.22 = (bf16[64,768]{1,0:T(8,128)(2,1)}, bf16[64,768]{1,0:T(8,128)(2,1)S(1)}, u32[]{:S(2)}) copy-start(bf16[64,768]{1,0:T(8,128)(2,1)S(1)} %get-tuple-element.16) | copy-start | bytes 294916
  39.3 1.3 %copy-start.2 = (bf16[256,16,64]{2,1,0:T(8,128)(2,1)}, bf16[256,16,64]{2,1,0:T(8,128)(2,1)S(1)}, u32[]{:S(2)}) copy-start(bf16[256,16,64]{2,1,0:T(8,128)(2,1)S(1)} %get-tuple-element.43) | copy-start | bytes 1572868
  40.6 6.6 %copy-start.5 = (bf16[256,1024]{1,0:T(8,128)(2,1)S(1)}, bf16[256,1024]{1,0:T(8,128)(2,1)}, u32[]{:S(2)}) copy-start(bf16[256,1024]{1,0:T(8,128)(2,1)} %copy-done.4) | copy-start | bytes 1572868
  45.3 11.7 %copy-start.14 = (bf16[51,16,64]{2,1,0:T(8,128)(2,1)}, bf16[51,16,64]{2,1,0:T(8,128)(2,1)S(1)}, u32[]{:S(2)}) copy-start(bf16[51,16,64]{2,1,0:T(8,128)(2,1)S(1)} %gather_fusion.4) | copy-start | bytes 313348
  47.3 9.8 %copy-start.12 = (bf16[51,16,64]{2,1,0:T(8,128)(2,1)}, bf16[51,16,64]{2,1,0:T(8,128)(2,1)S(1)}, u32[]{:S(2)}) copy-start(bf16[51,16,64]{2,1,0:T(8,128)(2,1)S(1)} %gather_fusion.5) | copy-start | bytes 313348
  51.2 2.1 %copy-start.8 = (bf16[256,16,64]{0,2,1:T(8,128)(2,1)S(1)}, bf16[256,16,64]{0,2,1:T(8,128)(2,1)}, u32[]{:S(2)}) copy-start(bf16[256,16,64]{0,2,1:T(8,128)(2,1)} %get-tuple-element.8) | copy-start | bytes 1572868
  57.1 3.9 %copy-start.15 = (bf16[51,16,64]{2,1,0:T(8,128)(2,1)}, bf16[51,16,64]{2,1,0:T(8,128)(2,1)S(1)}, u32[]{:S(2)}) copy-start(bf16[51,16,64]{2,1,0:T(8,128)(2,1)S(1)} %gather_fusion.3) | copy-start | bytes 313348
  58.5 2.4 %copy-start.29 = (s32[51]{0:T(128)S(1)}, s32[51]{0:T(128)}, u32[]{:S(2)}) copy-start(s32[51]{0:T(128)} %copy-done.28) | copy-start | bytes 616
  58.5 2.4 %copy-start.30 = (pred[256]{0:T(512)(128)(4,1)S(1)}, pred[256]{0:T(512)(128)(4,1)}, u32[]{:S(2)}) copy-start(pred[256]{0:T(512)(128)(4,1)} %broadcast_compare_fusion) | copy-start | bytes 772
  64.7 2.7 %copy-start.27 = (f32[256]{0:T(256)S(1)}, f32[256]{0:T(256)}, u32[]{:S(2)}) copy-start(f32[256]{0:T(256)} %get-tuple-element.22) | copy-start | bytes 3076
  66.0 1.3 %copy-start.25 = (bf16[256,768]{1,0:T(8,128)(2,1)S(1)}, bf16[256,768]{1,0:T(8,128)(2,1)}, u32[]{:S(2)}) copy-start(bf16[256,768]{1,0:T(8,128)(2,1)} %copy-done.24) | copy-start | bytes 1179652
  67.4 5.2 %copy-start.6 = (f32[256,768]{1,0:T(8,128)S(1)}, f32[256,768]{1,0:T(8,128)}, u32[]{:S(2)}) copy-start(f32[256,768]{1,0:T(8,128)} %copy.140) | copy-start | bytes 2359300
  67.4 5.2 %copy-start.31 = (bf16[768,1024]{1,0:T(8,128)(2,1)S(1)}, bf16[768,1024]{1,0:T(8,128)(2,1)}, u32[]{:S(2)}) copy-start(bf16[768,1024]{1,0:T(8,128)(2,1)} %param.17) | copy-start | bytes 4718596
  75.9 2.8 %copy-start.11 = (bf16[256,768]{1,0:T(8,128)(2,1)}, bf16[256,768]{1,0:T(8,128)(2,1)S(1)}, u32[]{:S(2)}) copy-start(bf16[256,768]{1,0:T(8,128)(2,1)S(1)} %get-tuple-element.34) | copy-start | bytes 1179652
  75.9 4.8 %copy-start.7 = (bf16[3,16,48,48]{3,2,1,0:T(8,128)(2,1)S(1)}, bf16[3,16,48,48]{3,2,1,0:T(8,128)(2,1)}, u32[]{:S(2)}) copy-start(bf16[3,16,48,48]{3,2,1,0:T(8,128)(2,1)} %param.16) | copy-start | bytes 663556
  82.1 3.3 %copy-start.10 = (f32[16,51,51]{1,2,0:T(8,128)S(1)}, f32[16,51,51]{1,2,0:T(8,128)}, u32[]{:S(2)}) copy-start(f32[16,51,51]{1,2,0:T(8,128)} %copy-done.9) | copy-start | bytes 499396
  84.5 1.9 %copy-start.16 = (bf16[51,16,64]{2,1,0:T(8,128)(2,1)S(1)}, bf16[51,16,64]{2,1,0:T(8,128)(2,1)}, u32[]{:S(2)}) copy-start(bf16[51,16,64]{2,1,0:T(8,128)(2,1)} %copy-done.15) | copy-start | bytes 313348
  93.8 1.7 %copy-start.13 = (bf16[51,16,64]{2,1,0:T(8,128)(2,1)S(1)}, bf16[51,16,64]{2,1,0:T(8,128)(2,1)}, u32[]{:S(2)}) copy-start(bf16[51,16,64]{2,1,0:T(8,128)(2,1)} %copy-done.12) | copy-start | bytes 313348
  93.8 1.7 %copy-start.17 = (f32[16,51,51]{1,2,0:T(8,128)S(1)}, f32[16,51,51]{1,2,0:T(8,128)}, u32[]{:S(2)}) copy-start(f32[16,51,51]{1,2,0:T(8,128)} %get-tuple-element.36) | copy-start | bytes 499396
  95.5 1.1 %copy-start.26 = (bf16[51,1,16,64]{3,0,2,1:T(8,128)(2,1)S(1)}, bf16[51,1,16,64]{3,0,2,1:T(8,128)(2,1)}, u32[]{:S(2)}) copy-start(bf16[51,1,16,64]{3,0,2,1:T(8,128)(2,1)} %fusion.21) | copy-start | bytes 313348
  97.4 7.6 %copy-start.19 = (bf16[64,768]{1,0:T(8,128)(2,1)S(1)}, bf16[64,768]{1,0:T(8,128)(2,1)}, u32[]{:S(2)}) copy-start(bf16[64,768]{1,0:T(8,128)(2,1)} %copy-done.18) | copy-start | bytes 294916
  97.4 7.6 %copy-start.21 = (bf16[64,768]{1,0:T(8,128)(2,1)S(1)}, bf16[64,768]{1,0:T(8,128)(2,1)}, u32[]{:S(2)}) copy-start(bf16[64,768]{1,0:T(8,128)(2,1)} %copy-done.20) | copy-start | bytes 294916
  97.4 7.6 %copy-start.23 = (bf16[64,768]{1,0:T(8,128)(2,1)S(1)}, bf16[64,768]{1,0:T(8,128)(2,1)}, u32[]{:S(2)}) copy-start(bf16[64,768]{1,0:T(8,128)(2,1)} %copy-done.22) | copy-start | bytes 294916
  102.8 5.5 %collective-permute-start.3 = (bf16[51,1024]{1,0:T(8,128)(2,1)S(1)}, bf16[51,1024]{1,0:T(8,128)(2,1)S(1)}, u32[]{:S(2)}, u32[]{:S(2)}) collective-permute-start(bf16[51,1024]{1,0:T(8,128)(2,1)S(1)} %fusion.109), channel_id=1, source_target_pairs={{0,3},{1,0},{2,1},{3,2},{4,7},{5,4},{6,5},{7,6},{8,11},{9,8},{10,9... | collective-permute-start | bytes 313352 | tf_op jit(solution)/shard_map/ppermute | solution.py:135
  103.4 6.0 %collective-permute-start.4 = (bf16[51,1024]{1,0:T(8,128)(2,1)S(1)}, bf16[51,1024]{1,0:T(8,128)(2,1)S(1)}, u32[]{:S(2)}, u32[]{:S(2)}) collective-permute-start(bf16[51,1024]{1,0:T(8,128)(2,1)S(1)} %fusion.109), channel_id=1, source_target_pairs={{0,2},{1,3},{2,0},{3,1},{4,6},{5,7},{6,4},{7,5},{8,10},{9,11},{10,... | collective-permute-start | bytes 313352 | tf_op jit(solution)/shard_map/ppermute | solution.py:135
  104.9 5.7 %collective-permute-start.5 = (bf16[51,1024]{1,0:T(8,128)(2,1)S(1)}, bf16[51,1024]{1,0:T(8,128)(2,1)S(1)}, u32[]{:S(2)}, u32[]{:S(2)}) collective-permute-start(bf16[51,1024]{1,0:T(8,128)(2,1)S(1)} %fusion.109), channel_id=1, source_target_pairs={{0,1},{1,2},{2,3},{3,0},{4,5},{5,6},{6,7},{7,4},{8,9},{9,10},{10,1... | collective-permute-start | bytes 313352 | tf_op jit(solution)/shard_map/ppermute | solution.py:135
  (6 other events, 4.8 us)

commit v6 on v4

--- a/solution.py
+++ b/solution.py
@@ -43,12 +43,38 @@
     return mix_heads(queries, key_rows, projected[:, 2])
 
 
-def attention_branch(inputs, w_qkv, w_out):
-    row_count = inputs.shape[0]
+def project_rows(inputs, w_qkv):
     normed = row_norm(inputs.astype(jnp.float32)).astype(jnp.bfloat16)
-    projected = jnp.dot(normed, w_qkv, preferred_element_type=jnp.float32).astype(jnp.bfloat16)
+    return jnp.dot(normed, w_qkv, preferred_element_type=jnp.float32).astype(jnp.bfloat16)
+
+
+def attention_from(projected, w_out):
+    row_count = projected.shape[0]
     context = split_project(projected.reshape(row_count, 3, HEADS, D // HEADS))
     return jnp.dot(context.reshape(row_count, D), w_out, preferred_element_type=jnp.float32)
+
+
+def attention_branch(inputs, w_qkv, w_out):
+    return attention_from(project_rows(inputs, w_qkv), w_out)
+
+
+@jax.custom_vjp
+def reuse_rows(inputs, w_qkv, projected):
+    return projected
+
+
+def reuse_rows_fwd(inputs, w_qkv, projected):
+    return projected, (inputs, w_qkv)
+
+
+def reuse_rows_bwd(saved, cotangent):
+    inputs, w_qkv = saved
+    _, pullback = jax.vjp(lambda rows: project_rows(rows, w_qkv), inputs)
+    (d_inputs,) = pullback(cotangent)
+    return d_inputs, jnp.zeros_like(w_qkv), jnp.zeros_like(cotangent)
+
+
+reuse_rows.defvjp(reuse_rows_fwd, reuse_rows_bwd)
 
 
 def decoder_output(visible_out, positions, total_rows, mask_embed, dec_in, conv_w, dec_out):
@@ -78,11 +104,15 @@
     return jnp.dot(hidden, dec_out, preferred_element_type=jnp.float32)
 
 
-def copy_terms(visible_in, positions, targets, w_qkv, w_out, mask_embed, dec_in, conv_w, dec_out):
+def copy_terms(
+    visible_in, positions, targets, w_qkv, w_out, mask_embed, dec_in, conv_w, dec_out, projected
+):
     total_rows = targets.shape[0]
-    visible_out = (
-        visible_in.astype(jnp.float32) + attention_branch(visible_in, w_qkv, w_out)
-    ).astype(jnp.bfloat16)
+    if projected is None:
+        branch = attention_branch(visible_in, w_qkv, w_out)
+    else:
+        branch = attention_from(reuse_rows(visible_in, w_qkv, projected), w_out)
+    visible_out = (visible_in.astype(jnp.float32) + branch).astype(jnp.bfloat16)
     predicted = decoder_output(
         visible_out, positions, total_rows, mask_embed, dec_in, conv_w, dec_out
     )
@@ -147,14 +177,26 @@
     )
     visible_in = embedded[positions]
     if HEADS * total_rows * total_rows * 4 <= (1 << 24):
-        branch = attention_branch(embedded, w_qkv, w_out)
+        clip_projected = project_rows(embedded, w_qkv)
+        branch = attention_from(clip_projected, w_out)
+        visible_projected = clip_projected[positions]
     else:
         branch = split_teacher(embedded, w_qkv, w_out, own_index, group_size)
+        visible_projected = None
     all_targets = row_norm(branch).astype(jnp.bfloat16)
 
     def objective(rows_in):
         return copy_terms(
-            rows_in, positions, all_targets, w_qkv, w_out, mask_embed, dec_in, conv_w, dec_out
+            rows_in,
+            positions,
+            all_targets,
+            w_qkv,
+            w_out,
+            mask_embed,
+            dec_in,
+            conv_w,
+            dec_out,
+            visible_projected,
         )
 
     squares, pullback = jax.vjp(objective, visible_in)

time: 87.3 us -> 86.5 us (level)
  matrix products: 47.3 us -> 43.7 us
  local copies, waits for them, and re-layouts: 13.3 us -> 16.4 us
    dot_general x5 -> x4, matrix products: 16.4 us -> 12.4 us  [the longest x1 5.83 us: project_rows(): jnp.dot(normed, w_qkv, preferred_element_type=jnp.float32)]
    gather x0 -> x1, local copies, waits for them, and re-layouts: none -> 2.66 us  [on_device(): visible_projected = clip_projected[positions]]
    dot_general x6, matrix products: 4.61 us -> 2.78 us  [decoder_output(): jnp.einsum('pgi,gio->pgo', padded[offset:offset + total_rows], conv_w[off...]
    dot_general x1, matrix products: 0.37 us -> 2.01 us  [decoder_output(): placed = jnp.dot(picks, lowered_visible, preferred_element_type=jnp.float32)]
    convert_element_type x1, local copies, waits for them, and re-layouts: 0.17 us -> 1.16 us  [decoder_output(): jnp.where(seen > 0, placed, lowered_mask.astype(jnp.float32))]
    unnamed x61 -> x53, local copies, waits for them, and re-layouts: 2.82 us -> 2.2 us
    reduce_sum x2 -> x1, other arithmetic: 2.76 us -> 2.54 us  [row_norm(): centred = values - average]
where the time goes in v6:
time: 86.5 us; the launch traced here: 85.8 us
  matrix products  43.7 us (51%)
  local copies, waits for them, and re-layouts  16.4 us (19%)
  other arithmetic  10.7 us (12%)
  starting transfers between devices  8.16 us (9%)
  waiting for transfers between devices  3.77 us (4%)
  between operations  3.11 us (4%)
    dot_general x2, matrix products, decoder_output(): return jnp.dot(hidden, dec_out, preferred_element_type=jnp.float32)  8.69 us
    ppermute x6, starting transfers between devices, ring_gather(): parts.append(lax.ppermute(values, 'mask', pairs))  8.16 us
    dot_general x1, matrix products, project_rows(): jnp.dot(normed, w_qkv, preferred_element_type=jnp.float32)  5.83 us
    dot_general x2, matrix products, decoder_output(): jnp.dot(visible_out, dec_in, preferred_element_type=jnp.float32)  5.21 us
    dot_general x1, matrix products, copy_terms(): branch = attention_from(reuse_rows(visible_in, w_qkv, projected), w_out)  4.97 us
    dot_general x4, matrix products, mix_heads(): jnp.einsum('hqk,khd->qhd', weights, values, preferred_element_type=jnp.fl...  3.87 us
    ppermute x6, waiting for transfers between devices, ring_gather(): parts.append(lax.ppermute(values, 'mask', pairs))  3.77 us
    dot_general x4, matrix products, mix_heads(): jnp.einsum('qhd,khd->hqk', queries, key_rows, preferred_element_type=jnp....  3.72 us
  transfers between devices with their start and end apart: 6, of which 3 were waited for; matrix products, arithmetic and copies ran while one was open for 8% of the time, Pallas kernels for 0%

profile of v6, /device:TPU:0, one launch (start us, length us, event | category | flops | bytes accessed | tf_op | source)
XLA Modules:
  0.0 85.8 jit_solution(7323303930402355236)
XLA Ops:
  0.6 3.0 %collective-permute-start = (bf16[64,768]{1,0:T(8,128)(2,1)}, bf16[64,768]{1,0:T(8,128)(2,1)S(1)}, u32[]{:S(2)}, u32[]{:S(2)}) collective-permute-start(bf16[64,768]{1,0:T(8,128)(2,1)} %param.9), channel_id=1, source_target_pairs={{0,1},{1,2},{2,3},{3,0},{4,5},{5,6},{6,7},{7,4},{8,9},{9,10},{10,1... | collective-permute-start | bytes 294920 | tf_op jit(solution)/shard_map/ppermute | solution.py:129
  3.7 1.5 %collective-permute-start.1 = (bf16[64,768]{1,0:T(8,128)(2,1)}, bf16[64,768]{1,0:T(8,128)(2,1)S(1)}, u32[]{:S(2)}, u32[]{:S(2)}) collective-permute-start(bf16[64,768]{1,0:T(8,128)(2,1)} %param.9), channel_id=1, source_target_pairs={{0,2},{1,3},{2,0},{3,1},{4,6},{5,7},{6,4},{7,5},{8,10},{9,11},{10,... | collective-permute-start | bytes 294920 | tf_op jit(solution)/shard_map/ppermute | solution.py:129
  5.2 1.4 %collective-permute-start.2 = (bf16[64,768]{1,0:T(8,128)(2,1)}, bf16[64,768]{1,0:T(8,128)(2,1)S(1)}, u32[]{:S(2)}, u32[]{:S(2)}) collective-permute-start(bf16[64,768]{1,0:T(8,128)(2,1)} %param.9), channel_id=1, source_target_pairs={{0,3},{1,0},{2,1},{3,2},{4,7},{5,4},{6,5},{7,6},{8,11},{9,8},{10,9... | collective-permute-start | bytes 294920 | tf_op jit(solution)/shard_map/ppermute | solution.py:129
  9.5 1.2 %gather_fusion = s32[4,51]{1,0:T(4,128)S(1)} fusion(s32[4,51]{1,0:T(4,128)} %param.10, s32[1024]{0:T(1024)S(1)} %pad_clamp_fusion.2), kind=kCustom, calls=%fused_computation | custom fusion | bytes 1648 | tf_op jit(solution)/shard_map/gather | solution.py:207
  10.9 1.7 %convolution_reduce_fusion = bf16[768]{0:T(1024)(128)(2,1)S(1)} fusion(bf16[1024,1]{0,1:T(2,128)(2,1)S(1)} %reshape.351, bf16[1024,768]{1,0:T(8,128)(2,1)} %param.15), kind=kOutput, calls=%fused_computation.56 | convolution fusion | flops 1572864 | bytes 1576448 | tf_op jit(solution)/shard_map/jvp()/dot_general | solution.py:87
  12.6 1.0 %select_select_fusion.3 = (bf16[64,768]{1,0:T(8,128)(2,1)S(1)}, bf16[64,768]{1,0:T(8,128)(2,1)S(1)}, bf16[64,768]{1,0:T(8,128)(2,1)S(1)}, bf16[64,768]{1,0:T(8,128)(2,1)S(1)}) fusion(bf16[64,768]{1,0:T(8,128)(2,1)S(1)} %collective-permute-done, bf16[64,768]{1,0:T(8,128)(2,1)S(1)} %collective-permute-done.1, bf16[64,768]{1,0:T(8,128)(2,1)S(1)} %collective-permute-done.2, ...), kind=kLoop, calls=%fused_computation.184 | loop fusion | flops 589824 | bytes 786444 | tf_op jit(solution)/shard_map/jit(_where)/select_n | solution.py:140
  13.6 2.2 %convert_reduce_fusion = (f32[256]{0:T(256)S(1)}, bf16[256,1024]{1,0:T(8,128)(2,1)S(1)}) fusion(bf16[768,1024]{1,0:T(8,128)(2,1)} %param.11, bf16[64,768]{1,0:T(8,128)(2,1)S(1)} %get-tuple-element.12, bf16[64,768]{1,0:T(8,128)(2,1)S(1)} %get-tuple-element.13, bf16[64,768]{1,0:T(8,128)(2,1)S(1)} %get-tuple-element.14, bf16[64,768]{1,0:T(8,128)(2,1)S(1)} %get-tuple-element.11), kind=kOutput, calls=%fused_computation.16 | convolution fusion | flops 405012224 | bytes 2491392 | tf_op jit(solution)/shard_map/dot_general | solution.py:175
  16.1 5.8 %convolution_convert_fusion = bf16[256,3072]{1,0:T(8,128)(2,1)} fusion(bf16[1024,3072]{1,0:T(8,128)(2,1)} %param.12, bf16[256,1024]{1,0:T(8,128)(2,1)S(1)} %get-tuple-element.20, f32[256]{0:T(256)S(1)} %add_rsqrt_fusion.3, f32[256]{0:T(256)S(1)} %broadcast_multiply_fusion.3), kind=kOutput, calls=%fused_computation.6 | convolution fusion | flops 1612447744 | bytes 8390656 | tf_op jit(solution)/shard_map/dot_general | solution.py:48
  22.0 2.6 %copy.59 = bf16[256,3072]{0,1:T(8,128)(2,1)} copy(bf16[256,3072]{1,0:T(8,128)(2,1)} %convolution_convert_fusion) | data formatting | bytes 3145728 | tf_op jit(solution)/shard_map/convert_element_type | solution.py:48
  24.5 2.7 %gather_fusion.3 = bf16[51,3072]{1,0:T(8,128)(2,1)S(1)} fusion(bf16[256,3072]{1,0:T(8,128)(2,1)} %convolution_convert_fusion, s32[1024]{0:T(1024)S(1)} %pad_clamp_fusion), kind=kCustom, calls=%fused_computation.3 | custom fusion | bytes 626892 | tf_op jit(solution)/shard_map/gather | solution.py:182
  27.9 1.5 %fusion.22 = (f32[256,16]{0,1:T(8,128)S(1)}, f32[256,16]{0,1:T(8,128)S(1)}) fusion(bf16[256,3,16,64]{0,3,2,1:T(8,128)(2,1)} %bitcast.168), kind=kLoop, calls=%fused_computation.59 | loop fusion | flops 1564672 | bytes 1081344 | tf_op jit(solution)/shard_map/reduce_sum | solution.py:25
  29.4 2.2 %fusion = (f32[16,256]{1,0:T(8,128)S(1)}, f32[16,256,256]{1,2,0:T(8,128)S(1)}) fusion(f32[256,16]{0,1:T(8,128)S(1)} %get-tuple-element.42, bf16[256,3,16,64]{0,3,2,1:T(8,128)(2,1)} %bitcast.169, f32[256,16]{0,1:T(8,128)S(1)} %get-tuple-element.43), kind=kOutput, calls=%fused_computation.7 | convolution fusion | flops 137883648 | bytes 5292032 | tf_op jit(solution)/shard_map/qhd,khd->hqk/dot_general | solution.py:31
  31.6 1.9 %fusion.3 = bf16[16,64,256]{2,1,0:T(8,128)(2,1)S(1)} fusion(f32[16,256,256]{1,2,0:T(8,128)S(1)} %get-tuple-element.22, f32[16,256]{1,0:T(8,128)S(1)} %get-tuple-element.21, bf16[256,3,16,64]{0,3,2,1:T(8,128)(2,1)} %bitcast.170), kind=kOutput, calls=%fused_computation.17 | convolution fusion | flops 137625600 | bytes 5259264 | tf_op jit(solution)/shard_map/hqk,khd->qhd/dot_general | solution.py:36
  34.3 1.0 %copy-done.1 = f32[256,1024]{1,0:T(8,128)} copy-done((f32[256,1024]{1,0:T(8,128)}, f32[256,1024]{1,0:T(8,128)S(1)}, u32[]{:S(2)}) %copy-start.1) | copy-done | bytes 1048600
  38.6 2.9 %convolution_convert_fusion.15 = bf16[51,768]{1,0:T(8,128)(2,1)} fusion(bf16[1024,768]{1,0:T(8,128)(2,1)} %param.15, bf16[51,1024]{1,0:T(8,128)(2,1)S(1)} %reshape.305, bf16[1024,1024]{1,0:T(8,128)(2,1)S(1)} %copy-done, bf16[51,1024]{1,0:T(8,128)(2,1)S(1)} %gather_fusion.2), kind=kOutput, calls=%fused_computation.55 | convolution fusion | flops 187366656 | bytes 3957248 | tf_op jit(solution)/shard_map/jvp()/dot_general | solution.py:84
  41.5 2.0 %fusion.4 = bf16[256,768]{1,0:T(8,128)(2,1)} fusion(bf16[51,768]{1,0:T(8,128)(2,1)} %convolution_convert_fusion.15, bf16[768]{0:T(1024)(128)(2,1)S(1)} %convolution_reduce_fusion, pred[256]{0:T(512)(128)(4,1)S(1)} %broadcast_compare_fusion, s32[51]{0:T(128)S(1)} %fusion.122), kind=kOutput, calls=%fused_computation.22 | convolution fusion | flops 20263680 | bytes 473548 | tf_op jit(solution)/shard_map/jvp()/dot_general | solution.py:90
  43.5 1.2 %copy.54 = bf16[256,768]{0,1:T(8,128)(2,1)S(1)} copy(bf16[256,768]{1,0:T(8,128)(2,1)} %fusion.4) | data formatting | bytes 786432 | tf_op jit(solution)/shard_map/jvp()/convert_element_type | solution.py:91
  45.4 1.4 %fusion.135 = (f32[256]{0:T(256)S(1)}, f32[16,256,48]{1,2,0:T(8,128)S(1)}) fusion(f32[16,256,48]{1,2,0:T(8,128)S(1)} %convolution_add_fusion.1, bf16[256,16,48]{0,2,1:T(8,128)(2,1)S(1)} %bitcast.177, bf16[3,16,48,48]{3,2,1,0:T(8,128)(2,1)} %param.16), kind=kOutput, calls=%fused_computation.244 | convolution fusion | flops 19267328 | bytes 2163712 | tf_op jit(solution)/shard_map/jvp(pgi,gio->pgo)/dot_general | solution.py:96
  46.9 1.2 %copy.58 = f32[256,768]{1,0:T(8,128)} copy(f32[256,768]{0,1:T(8,128)S(1)} %bitcast.171) | data formatting | bytes 1572864 | tf_op jit(solution)/shard_map/jvp()/reshape | solution.py:102
  48.1 5.2 %multiply_reduce_fusion = (f32[]{:T(128)}, f32[256,1024]{1,0:T(8,128)S(1)}) fusion(f32[256]{0:T(256)} %get-tuple-element.16, f32[256]{0:T(256)} %add_rsqrt_fusion.2, f32[256,1024]{1,0:T(8,128)} %copy-done.1, f32[256]{0:T(256)S(1)} %broadcast_multiply_fusion.2, bf16[768,1024]{1,0:T(8,128)(2,1)} %param.17, bf16[256,768]{1,0:T(8,128)(2,1)S(1)} %copy-done.20, ...), kind=kOutput, calls=%fused_computation.65 | convolution fusion | flops 418709504 | bytes 4854788 | tf_op jit(solution)/shard_map/jvp()/dot_general | solution.py:104
  53.3 3.5 %multiply_reduce_fusion.2 = (f32[256]{0:T(256)S(1)}, bf16[256,768]{1,0:T(8,128)(2,1)S(1)}) fusion(f32[256,768]{1,0:T(8,128)S(1)} %copy-done.2, f32[256]{0:T(256)S(1)} %broadcast_multiply_fusion.1, f32[256]{0:T(256)S(1)} %fusion.117, bf16[768,1024]{1,0:T(8,128)(2,1)S(1)} %copy-done.25, f32[256,1024]{1,0:T(8,128)S(1)} %get-tuple-element.39, ...), kind=kOutput, calls=%fused_computation.90 | convolution fusion | flops 419495680 | bytes 3805184 | tf_op jit(solution)/shard_map/transpose(jvp())/dot_general | solution.py:104
  56.8 2.5 %fusion.131 = (f32[256]{0:T(256)S(1)}, f32[256,768]{1,0:T(8,128)S(1)}) fusion(f32[256]{0:T(256)S(1)} %multiply_multiply_fusion.8, bf16[256,768]{1,0:T(8,128)(2,1)S(1)} %get-tuple-element.30, f32[256]{0:T(256)S(1)} %fusion.117, f32[256,768]{1,0:T(8,128)S(1)} %copy-done.2, f32[256]{0:T(256)S(1)} %broadcast_multiply_fusion.1), kind=kLoop, calls=%fused_computation.240 | loop fusion | flops 15531776 | bytes 1970176 | tf_op jit(solution)/shard_map/transpose(jvp())/reduce_sum | solution.py:19
  60.3 1.2 %copy.61 = bf16[256,768]{0,1:T(8,128)(2,1)S(1)} copy(bf16[256,768]{1,0:T(8,128)(2,1)} %broadcast_add_fusion) | data formatting | bytes 786432 | tf_op jit(solution)/shard_map/transpose(jvp())/add_any | solution.py:18
  62.7 2.3 %convolution_convert_fusion.12 = bf16[51,1024]{1,0:T(8,128)(2,1)S(1)} fusion(bf16[1024,768]{1,0:T(8,128)(2,1)} %param.15, bf16[256,768]{1,0:T(8,128)(2,1)} %copy-done.9, bf16[256,768]{1,0:T(8,128)(2,1)S(1)} %copy.65, pred[256]{0:T(512)(128)(4,1)S(1)} %copy-done.24, s32[51]{0:T(128)S(1)} %copy-done.22), kind=kOutput, calls=%fused_computation.51 | convolution fusion | flops 100964352 | bytes 2464204 | tf_op jit(solution)/shard_map/transpose(jvp())/dot_general | solution.py:84
  66.0 1.4 %fusion.17 = bf16[51,1,16,64]{3,0,2,1:T(8,128)(2,1)S(1)} fusion(bf16[51,16,64]{2,1,0:T(8,128)(2,1)S(1)} %reshape.312, f32[16,51,51]{1,2,0:T(8,128)} %copy-done.12, f32[16,51]{1,0:T(8,128)S(1)} %get-tuple-element.25), kind=kOutput, calls=%fused_computation.47 | convolution fusion | flops 5462304 | bytes 378624 | tf_op jit(solution)/shard_map/transpose(jvp(hqk,khd->qhd))/dot_general | solution.py:36
  70.3 5.0 %fusion.85 = (f32[51]{0:T(128)S(1)}, f32[51]{0:T(128)S(1)}, f32[51,1024]{1,0:T(8,128)S(1)}) fusion(bf16[51,1024]{1,0:T(8,128)(2,1)S(1)} %gather_fusion.2, f32[51]{0:T(128)S(1)} %broadcast_multiply_fusion.4, bf16[51,3072]{1,0:T(8,128)(2,1)S(1)} %reshape.313, bf16[1024,3072]{1,0:T(8,128)(2,1)} %param.12), kind=kOutput, calls=%fused_computation.156 | convolution fusion | flops 321281920 | bytes 6918756 | tf_op jit(solution)/shard_map/transpose(jvp(transpose(jvp())))/dot_general | solution.py:114
  76.3 1.5 %collective-permute-start.4 = (bf16[51,1024]{1,0:T(8,128)(2,1)S(1)}, bf16[51,1024]{1,0:T(8,128)(2,1)S(1)}, u32[]{:S(2)}, u32[]{:S(2)}) collective-permute-start(bf16[51,1024]{1,0:T(8,128)(2,1)S(1)} %fusion.109), channel_id=1, source_target_pairs={{0,2},{1,3},{2,0},{3,1},{4,6},{5,7},{6,4},{7,5},{8,10},{9,11},{10,... | collective-permute-start | bytes 313352 | tf_op jit(solution)/shard_map/ppermute | solution.py:129
  78.0 1.0 %gather_fusion.1 = bf16[204,192]{1,0:T(8,128)(2,1)S(1)} fusion(bf16[256,192]{1,0:T(8,128)(2,1)S(1)} %constant_dynamic-slice_fusion.1, s32[1024]{0:T(1024)S(1)} %pad_clamp_fusion.1), kind=kCustom, calls=%fused_computation.1 | custom fusion | bytes 157488 | tf_op jit(solution)/shard_map/gather | solution.py:209
  79.7 1.5 %collective-permute-done.3 = bf16[51,1024]{1,0:T(8,128)(2,1)S(1)} collective-permute-done((bf16[51,1024]{1,0:T(8,128)(2,1)S(1)}, bf16[51,1024]{1,0:T(8,128)(2,1)S(1)}, u32[]{:S(2)}, u32[]{:S(2)}) %collective-permute-start.3) | collective-permute-done | bytes 104480 | tf_op jit(solution)/shard_map/ppermute | solution.py:129
  81.2 1.0 %collective-permute-done.4 = bf16[51,1024]{1,0:T(8,128)(2,1)S(1)} collective-permute-done((bf16[51,1024]{1,0:T(8,128)(2,1)S(1)}, bf16[51,1024]{1,0:T(8,128)(2,1)S(1)}, u32[]{:S(2)}, u32[]{:S(2)}) %collective-permute-start.4) | collective-permute-done | bytes 104480 | tf_op jit(solution)/shard_map/ppermute | solution.py:129
  82.2 1.2 %collective-permute-done.5 = bf16[51,1024]{1,0:T(8,128)(2,1)S(1)} collective-permute-done((bf16[51,1024]{1,0:T(8,128)(2,1)S(1)}, bf16[51,1024]{1,0:T(8,128)(2,1)S(1)}, u32[]{:S(2)}, u32[]{:S(2)}) %collective-permute-start.5) | collective-permute-done | bytes 104480 | tf_op jit(solution)/shard_map/ppermute | solution.py:129
  83.5 1.2 %fusion.63 = f32[192,1024]{1,0:T(8,128)} fusion(bf16[204,192]{1,0:T(8,128)(2,1)S(1)} %gather_fusion.1, bf16[51,1024]{1,0:T(8,128)(2,1)S(1)} %collective-permute-done.5, bf16[51,1024]{1,0:T(8,128)(2,1)S(1)} %collective-permute-done.4, bf16[51,1024]{1,0:T(8,128)(2,1)S(1)} %collective-permute-done.3, bf16[51,1024]{1,0:T(8,128)(2,1)S(1)} %fusion.109), kind=kOutput, calls=%fused_computation.130 | convolution fusion | flops 81887232 | bytes 1282560 | tf_op jit(solution)/shard_map/vc,vd->cd/dot_general | solution.py:210
  (122 shorter events, 15.9 us)
Async XLA Ops:
  0.6 32.9 %copy-start = (bf16[1024,1024]{1,0:T(8,128)(2,1)S(1)}, bf16[1024,1024]{1,0:T(8,128)(2,1)}, u32[]{:S(2)}) copy-start(bf16[1024,1024]{1,0:T(8,128)(2,1)} %param.13) | copy-start | bytes 6291460
  0.6 12.0 %collective-permute-start = (bf16[64,768]{1,0:T(8,128)(2,1)}, bf16[64,768]{1,0:T(8,128)(2,1)S(1)}, u32[]{:S(2)}, u32[]{:S(2)}) collective-permute-start(bf16[64,768]{1,0:T(8,128)(2,1)} %param.9), channel_id=1, source_target_pairs={{0,1},{1,2},{2,3},{3,0},{4,5},{5,6},{6,7},{7,4},{8,9},{9,10},{10,1... | collective-permute-start | bytes 294920 | tf_op jit(solution)/shard_map/ppermute | solution.py:129
  3.7 9.0 %collective-permute-start.1 = (bf16[64,768]{1,0:T(8,128)(2,1)}, bf16[64,768]{1,0:T(8,128)(2,1)S(1)}, u32[]{:S(2)}, u32[]{:S(2)}) collective-permute-start(bf16[64,768]{1,0:T(8,128)(2,1)} %param.9), channel_id=1, source_target_pairs={{0,2},{1,3},{2,0},{3,1},{4,6},{5,7},{6,4},{7,5},{8,10},{9,11},{10,... | collective-permute-start | bytes 294920 | tf_op jit(solution)/shard_map/ppermute | solution.py:129
  5.2 7.5 %collective-permute-start.2 = (bf16[64,768]{1,0:T(8,128)(2,1)}, bf16[64,768]{1,0:T(8,128)(2,1)S(1)}, u32[]{:S(2)}, u32[]{:S(2)}) collective-permute-start(bf16[64,768]{1,0:T(8,128)(2,1)} %param.9), channel_id=1, source_target_pairs={{0,3},{1,0},{2,1},{3,2},{4,7},{5,4},{6,5},{7,6},{8,11},{9,8},{10,9... | collective-permute-start | bytes 294920 | tf_op jit(solution)/shard_map/ppermute | solution.py:129
  8.0 33.5 %copy-start.21 = (s32[51]{0:T(128)}, s32[51]{0:T(128)S(1)}, u32[]{:S(2)}) copy-start(s32[51]{0:T(128)S(1)} %fusion.122) | copy-start | bytes 616
  8.2 33.3 %copy-start.23 = (pred[256]{0:T(512)(128)(4,1)}, pred[256]{0:T(512)(128)(4,1)S(1)}, u32[]{:S(2)}) copy-start(pred[256]{0:T(512)(128)(4,1)S(1)} %broadcast_compare_fusion) | copy-start | bytes 772
  13.6 2.5 %copy-start.14 = (bf16[64,768]{1,0:T(8,128)(2,1)}, bf16[64,768]{1,0:T(8,128)(2,1)S(1)}, u32[]{:S(2)}) copy-start(bf16[64,768]{1,0:T(8,128)(2,1)S(1)} %get-tuple-element.12) | copy-start | bytes 294916
  13.6 2.5 %copy-start.16 = (bf16[64,768]{1,0:T(8,128)(2,1)}, bf16[64,768]{1,0:T(8,128)(2,1)S(1)}, u32[]{:S(2)}) copy-start(bf16[64,768]{1,0:T(8,128)(2,1)S(1)} %get-tuple-element.13) | copy-start | bytes 294916
  13.6 2.5 %copy-start.18 = (bf16[64,768]{1,0:T(8,128)(2,1)}, bf16[64,768]{1,0:T(8,128)(2,1)S(1)}, u32[]{:S(2)}) copy-start(bf16[64,768]{1,0:T(8,128)(2,1)S(1)} %get-tuple-element.14) | copy-start | bytes 294916
  34.3 1.0 %copy-start.1 = (f32[256,1024]{1,0:T(8,128)}, f32[256,1024]{1,0:T(8,128)S(1)}, u32[]{:S(2)}) copy-start(f32[256,1024]{1,0:T(8,128)S(1)} %get-tuple-element.24) | copy-start | bytes 3145732
  36.6 0.9 %copy-start.10 = (bf16[51,1,16,64]{3,2,1,0:T(8,128)(2,1)}, bf16[51,1,16,64]{3,2,1,0:T(8,128)(2,1)S(1)}, u32[]{:S(2)}) copy-start(bf16[51,1,16,64]{3,2,1,0:T(8,128)(2,1)S(1)} %get-tuple-element.9) | copy-start | bytes 313348
  36.6 1.9 %copy-start.5 = (bf16[51,1,16,64]{3,2,1,0:T(8,128)(2,1)}, bf16[51,1,16,64]{3,2,1,0:T(8,128)(2,1)S(1)}, u32[]{:S(2)}) copy-start(bf16[51,1,16,64]{3,2,1,0:T(8,128)(2,1)S(1)} %get-tuple-element.8) | copy-start | bytes 313348
  36.6 1.9 %copy-start.7 = (bf16[51,1,16,64]{3,2,1,0:T(8,128)(2,1)}, bf16[51,1,16,64]{3,2,1,0:T(8,128)(2,1)S(1)}, u32[]{:S(2)}) copy-start(bf16[51,1,16,64]{3,2,1,0:T(8,128)(2,1)S(1)} %get-tuple-element.10) | copy-start | bytes 313348
  37.5 0.8 copy-start.12
  38.6 6.1 %copy-start.3 = (bf16[3,16,48,48]{3,2,1,0:T(8,128)(2,1)S(1)}, bf16[3,16,48,48]{3,2,1,0:T(8,128)(2,1)}, u32[]{:S(2)}) copy-start(bf16[3,16,48,48]{3,2,1,0:T(8,128)(2,1)} %param.16) | copy-start | bytes 663556
  46.8 1.3 %copy-start.20 = (bf16[256,768]{1,0:T(8,128)(2,1)S(1)}, bf16[256,768]{1,0:T(8,128)(2,1)}, u32[]{:S(2)}) copy-start(bf16[256,768]{1,0:T(8,128)(2,1)} %fusion.4) | copy-start | bytes 1179652
  48.1 5.2 %copy-start.2 = (f32[256,768]{1,0:T(8,128)S(1)}, f32[256,768]{1,0:T(8,128)}, u32[]{:S(2)}) copy-start(f32[256,768]{1,0:T(8,128)} %copy.58) | copy-start | bytes 2359300
  48.1 5.2 %copy-start.25 = (bf16[768,1024]{1,0:T(8,128)(2,1)S(1)}, bf16[768,1024]{1,0:T(8,128)(2,1)}, u32[]{:S(2)}) copy-start(bf16[768,1024]{1,0:T(8,128)(2,1)} %param.17) | copy-start | bytes 4718596
  56.8 2.6 %copy-start.9 = (bf16[256,768]{1,0:T(8,128)(2,1)}, bf16[256,768]{1,0:T(8,128)(2,1)S(1)}, u32[]{:S(2)}) copy-start(bf16[256,768]{1,0:T(8,128)(2,1)S(1)} %get-tuple-element.30) | copy-start | bytes 1179652
  56.8 4.6 %copy-start.4 = (bf16[3,16,48,48]{3,2,1,0:T(8,128)(2,1)S(1)}, bf16[3,16,48,48]{3,2,1,0:T(8,128)(2,1)}, u32[]{:S(2)}) copy-start(bf16[3,16,48,48]{3,2,1,0:T(8,128)(2,1)} %param.16) | copy-start | bytes 663556
  61.7 1.0 %copy-start.22 = (s32[51]{0:T(128)S(1)}, s32[51]{0:T(128)}, u32[]{:S(2)}) copy-start(s32[51]{0:T(128)} %copy-done.21) | copy-start | bytes 616
  61.7 1.0 %copy-start.24 = (pred[256]{0:T(512)(128)(4,1)S(1)}, pred[256]{0:T(512)(128)(4,1)}, u32[]{:S(2)}) copy-start(pred[256]{0:T(512)(128)(4,1)} %copy-done.23) | copy-start | bytes 772
  65.0 2.3 %copy-start.11 = (bf16[51,1,16,64]{3,2,1,0:T(8,128)(2,1)S(1)}, bf16[51,1,16,64]{3,2,1,0:T(8,128)(2,1)}, u32[]{:S(2)}) copy-start(bf16[51,1,16,64]{3,2,1,0:T(8,128)(2,1)} %copy-done.10) | copy-start | bytes 313348
  65.8 1.9 %copy-start.6 = (bf16[51,1,16,64]{3,2,1,0:T(8,128)(2,1)S(1)}, bf16[51,1,16,64]{3,2,1,0:T(8,128)(2,1)}, u32[]{:S(2)}) copy-start(bf16[51,1,16,64]{3,2,1,0:T(8,128)(2,1)} %copy-done.5) | copy-start | bytes 313348
  65.8 1.9 %copy-start.8 = (bf16[51,1,16,64]{3,2,1,0:T(8,128)(2,1)S(1)}, bf16[51,1,16,64]{3,2,1,0:T(8,128)(2,1)}, u32[]{:S(2)}) copy-start(bf16[51,1,16,64]{3,2,1,0:T(8,128)(2,1)} %copy-done.7) | copy-start | bytes 313348
  66.0 1.4 %copy-start.13 = (f32[16,51,51]{1,2,0:T(8,128)S(1)}, f32[16,51,51]{1,2,0:T(8,128)}, u32[]{:S(2)}) copy-start(f32[16,51,51]{1,2,0:T(8,128)} %copy-done.12) | copy-start | bytes 499396
  70.3 7.6 %copy-start.15 = (bf16[64,768]{1,0:T(8,128)(2,1)S(1)}, bf16[64,768]{1,0:T(8,128)(2,1)}, u32[]{:S(2)}) copy-start(bf16[64,768]{1,0:T(8,128)(2,1)} %copy-done.14) | copy-start | bytes 294916
  70.3 7.6 %copy-start.17 = (bf16[64,768]{1,0:T(8,128)(2,1)S(1)}, bf16[64,768]{1,0:T(8,128)(2,1)}, u32[]{:S(2)}) copy-start(bf16[64,768]{1,0:T(8,128)(2,1)} %copy-done.16) | copy-start | bytes 294916
  70.3 7.6 %copy-start.19 = (bf16[64,768]{1,0:T(8,128)(2,1)S(1)}, bf16[64,768]{1,0:T(8,128)(2,1)}, u32[]{:S(2)}) copy-start(bf16[64,768]{1,0:T(8,128)(2,1)} %copy-done.18) | copy-start | bytes 294916
  75.7 5.5 %collective-permute-start.3 = (bf16[51,1024]{1,0:T(8,128)(2,1)S(1)}, bf16[51,1024]{1,0:T(8,128)(2,1)S(1)}, u32[]{:S(2)}, u32[]{:S(2)}) collective-permute-start(bf16[51,1024]{1,0:T(8,128)(2,1)S(1)} %fusion.109), channel_id=1, source_target_pairs={{0,3},{1,0},{2,1},{3,2},{4,7},{5,4},{6,5},{7,6},{8,11},{9,8},{10,9... | collective-permute-start | bytes 313352 | tf_op jit(solution)/shard_map/ppermute | solution.py:129
  76.3 6.0 %collective-permute-start.4 = (bf16[51,1024]{1,0:T(8,128)(2,1)S(1)}, bf16[51,1024]{1,0:T(8,128)(2,1)S(1)}, u32[]{:S(2)}, u32[]{:S(2)}) collective-permute-start(bf16[51,1024]{1,0:T(8,128)(2,1)S(1)} %fusion.109), channel_id=1, source_target_pairs={{0,2},{1,3},{2,0},{3,1},{4,6},{5,7},{6,4},{7,5},{8,10},{9,11},{10,... | collective-permute-start | bytes 313352 | tf_op jit(solution)/shard_map/ppermute | solution.py:129
  77.8 5.7 %collective-permute-start.5 = (bf16[51,1024]{1,0:T(8,128)(2,1)S(1)}, bf16[51,1024]{1,0:T(8,128)(2,1)S(1)}, u32[]{:S(2)}, u32[]{:S(2)}) collective-permute-start(bf16[51,1024]{1,0:T(8,128)(2,1)S(1)} %fusion.109), channel_id=1, source_target_pairs={{0,1},{1,2},{2,3},{3,0},{4,5},{5,6},{6,7},{7,4},{8,9},{9,10},{10,1... | collective-permute-start | bytes 313352 | tf_op jit(solution)/shard_map/ppermute | solution.py:129

commit v7 on v6

--- a/solution.py
+++ b/solution.py
@@ -69,8 +69,11 @@
 
 def reuse_rows_bwd(saved, cotangent):
     inputs, w_qkv = saved
-    _, pullback = jax.vjp(lambda rows: project_rows(rows, w_qkv), inputs)
-    (d_inputs,) = pullback(cotangent)
+    _, pullback = jax.vjp(
+        lambda rows: row_norm(rows.astype(jnp.float32)).astype(jnp.bfloat16), inputs
+    )
+    d_normed = jnp.dot(w_qkv, cotangent.T, preferred_element_type=jnp.float32).T
+    (d_inputs,) = pullback(d_normed.astype(jnp.bfloat16))
     return d_inputs, jnp.zeros_like(w_qkv), jnp.zeros_like(cotangent)
 
 
@@ -101,7 +104,9 @@
         )
     activated = jax.nn.gelu(row_norm(convolved.reshape(total_rows, DD)), approximate=False)
     hidden = (lowered.astype(jnp.float32) + activated).astype(jnp.bfloat16)
-    return jnp.dot(hidden, dec_out, preferred_element_type=jnp.float32)
+    return lax.optimization_barrier(
+        jnp.dot(hidden, dec_out, preferred_element_type=jnp.float32)
+    )
 
 
 def copy_terms(
@@ -175,11 +180,17 @@
     embedded = jnp.dot(clip_pixels, embed_w, preferred_element_type=jnp.float32).astype(
         jnp.bfloat16
     )
-    visible_in = embedded[positions]
+    clip_ids = jnp.arange(total_rows, dtype=jnp.int32)
+    own_picks = (positions[:, None] == clip_ids[None, :]).astype(jnp.bfloat16)
+    visible_in = jnp.dot(own_picks, embedded, preferred_element_type=jnp.float32).astype(
+        jnp.bfloat16
+    )
     if HEADS * total_rows * total_rows * 4 <= (1 << 24):
         clip_projected = project_rows(embedded, w_qkv)
         branch = attention_from(clip_projected, w_out)
-        visible_projected = clip_projected[positions]
+        visible_projected = jnp.dot(
+            own_picks, clip_projected, preferred_element_type=jnp.float32
+        ).astype(jnp.bfloat16)
     else:
         branch = split_teacher(embedded, w_qkv, w_out, own_index, group_size)
         visible_projected = None
@@ -206,7 +217,10 @@
     slot_copy = (own_index + jnp.arange(group_size, dtype=jnp.int32)) % group_size
     flat_index = visible_index[slot_copy].reshape(copies * visible_count)
     own_cols = lax.dynamic_slice_in_dim(clip_pixels, own_index * col_width, col_width, 1)
-    gathered = own_cols[flat_index]
+    all_picks = (flat_index[:, None] == clip_ids[None, :]).astype(jnp.bfloat16)
+    gathered = jnp.dot(all_picks, own_cols, preferred_element_type=jnp.float32).astype(
+        jnp.bfloat16
+    )
     embed_grad = jnp.einsum(
         "vc,vd->cd",
         gathered,

time: 86.5 us -> 89.2 us (1.031)
  matrix products: 43.7 us -> 39.8 us
  other arithmetic: 10.7 us -> 13.5 us
  local copies, waits for them, and re-layouts: 16.4 us -> 18.6 us
  waiting for transfers between devices: 3.77 us -> 4.93 us
    gather x3 -> x0, local copies, waits for them, and re-layouts: 4.37 us -> none  [the longest x1 2.66 us: on_device(): visible_projected = clip_projected[positions]]
    another operation x0 -> x1, other arithmetic: none -> 3.03 us  [decoder_output(): jax.nn.gelu(row_norm(convolved.reshape(total_rows, DD)), approximate=False)]
    dot_general x1, matrix products: 5.83 us -> 3.1 us  [project_rows(): jnp.dot(normed, w_qkv, preferred_element_type=jnp.float32)]
    dot_general x2 -> x4, matrix products: 8.69 us -> 6.67 us  [the longest x2 3.13 us: decoder_output(): jnp.dot(hidden, dec_out, preferred_element_type=jnp.float32)]
    reshape x2, local copies, waits for them, and re-layouts: 0.87 us -> 2.73 us  [attention_from(): context = split_project(projected.reshape(row_count, 3, HEADS, D // HEADS))]
    dot_general x6, matrix products: 2.78 us -> 4.62 us  [decoder_output(): jnp.einsum('pgi,gio->pgo', padded[offset:offset + total_rows], conv_w[off...]
    unnamed x53 -> x105, local copies, waits for them, and re-layouts: 2.2 us -> 3.64 us
    dot_general x4, matrix products: 3.72 us -> 2.5 us  [mix_heads(): jnp.einsum('qhd,khd->hqk', queries, key_rows, preferred_element_type=jnp....]
  transfers between devices with their start and end apart: 6 -> 6, of which waited for: 3 -> 3; matrix products, arithmetic and copies ran while one was open for 8% -> 7% of each run, Pallas kernels for 0% -> 0%
where the time goes in v7:
time: 89.2 us; the launch traced here: 88.5 us
  matrix products  39.8 us (45%)
  local copies, waits for them, and re-layouts  18.6 us (21%)
  other arithmetic  13.5 us (15%)
  starting transfers between devices  8.15 us (9%)
  waiting for transfers between devices  4.93 us (6%)
  between operations  3.41 us (4%)
    ppermute x6, starting transfers between devices, ring_gather(): parts.append(lax.ppermute(values, 'mask', pairs))  8.15 us
    dot_general x1, matrix products, copy_terms(): branch = attention_from(reuse_rows(visible_in, w_qkv, projected), w_out)  5.01 us
    dot_general x2, matrix products, decoder_output(): jnp.dot(visible_out, dec_in, preferred_element_type=jnp.float32)  5.01 us
    ppermute x6, waiting for transfers between devices, ring_gather(): parts.append(lax.ppermute(values, 'mask', pairs))  4.93 us
    dot_general x6, matrix products, decoder_output(): jnp.einsum('pgi,gio->pgo', padded[offset:offset + total_rows], conv_w[off...  4.62 us
    dot_general x4, matrix products, mix_heads(): jnp.einsum('hqk,khd->qhd', weights, values, preferred_element_type=jnp.fl...  3.84 us
    unnamed x105, local copies, waits for them, and re-layouts  3.64 us
    dot_general x2, matrix products, decoder_output(): jnp.dot(hidden, dec_out, preferred_element_type=jnp.float32)  3.13 us
  transfers between devices with their start and end apart: 6, of which 3 were waited for; matrix products, arithmetic and copies ran while one was open for 7% of the time, Pallas kernels for 0%

profile of v7, /device:TPU:0, one launch (start us, length us, event | category | flops | bytes accessed | tf_op | source)
XLA Modules:
  0.0 88.5 jit_solution(11436291288225895864)
XLA Ops:
  0.6 3.0 %collective-permute-start = (bf16[64,768]{1,0:T(8,128)(2,1)}, bf16[64,768]{1,0:T(8,128)(2,1)S(1)}, u32[]{:S(2)}, u32[]{:S(2)}) collective-permute-start(bf16[64,768]{1,0:T(8,128)(2,1)} %param.9), channel_id=1, source_target_pairs={{0,1},{1,2},{2,3},{3,0},{4,5},{5,6},{6,7},{7,4},{8,9},{9,10},{10,1... | collective-permute-start | bytes 294920 | tf_op jit(solution)/shard_map/ppermute | solution.py:134
  3.7 1.5 %collective-permute-start.1 = (bf16[64,768]{1,0:T(8,128)(2,1)}, bf16[64,768]{1,0:T(8,128)(2,1)S(1)}, u32[]{:S(2)}, u32[]{:S(2)}) collective-permute-start(bf16[64,768]{1,0:T(8,128)(2,1)} %param.9), channel_id=1, source_target_pairs={{0,2},{1,3},{2,0},{3,1},{4,6},{5,7},{6,4},{7,5},{8,10},{9,11},{10,... | collective-permute-start | bytes 294920 | tf_op jit(solution)/shard_map/ppermute | solution.py:134
  5.2 1.4 %collective-permute-start.2 = (bf16[64,768]{1,0:T(8,128)(2,1)}, bf16[64,768]{1,0:T(8,128)(2,1)S(1)}, u32[]{:S(2)}, u32[]{:S(2)}) collective-permute-start(bf16[64,768]{1,0:T(8,128)(2,1)} %param.9), channel_id=1, source_target_pairs={{0,3},{1,0},{2,1},{3,2},{4,7},{5,4},{6,5},{7,6},{8,11},{9,8},{10,9... | collective-permute-start | bytes 294920 | tf_op jit(solution)/shard_map/ppermute | solution.py:134
  8.8 1.2 %gather_fusion = s32[4,51]{1,0:T(4,128)S(1)} fusion(s32[4,51]{1,0:T(4,128)} %param.10, s32[1024]{0:T(1024)S(1)} %pad_clamp_fusion), kind=kCustom, calls=%fused_computation | custom fusion | bytes 1648 | tf_op jit(solution)/shard_map/gather | solution.py:218
  10.7 1.9 %convolution_reduce_fusion = bf16[768]{0:T(1024)(128)(2,1)S(1)} fusion(bf16[1024,1]{0,1:T(2,128)(2,1)S(1)} %reshape.270, bf16[1024,768]{1,0:T(8,128)(2,1)} %param.15), kind=kOutput, calls=%fused_computation.56 | convolution fusion | flops 1572864 | bytes 1576448 | tf_op jit(solution)/shard_map/jvp()/dot_general | solution.py:90
  12.6 1.3 %select_select_fusion.3 = (bf16[64,768]{1,0:T(8,128)(2,1)S(1)}, bf16[64,768]{1,0:T(8,128)(2,1)S(1)}, bf16[64,768]{1,0:T(8,128)(2,1)S(1)}, bf16[64,768]{1,0:T(8,128)(2,1)S(1)}) fusion(bf16[64,768]{1,0:T(8,128)(2,1)S(1)} %collective-permute-done, bf16[64,768]{1,0:T(8,128)(2,1)S(1)} %collective-permute-done.1, bf16[64,768]{1,0:T(8,128)(2,1)S(1)} %collective-permute-done.2, ...), kind=kLoop, calls=%fused_computation.180 | loop fusion | flops 589824 | bytes 786444 | tf_op jit(solution)/shard_map/jit(_where)/select_n | solution.py:145
  13.9 2.2 %convert_reduce_fusion = (f32[256]{0:T(256)S(1)}, bf16[256,1024]{1,0:T(8,128)(2,1)S(1)}) fusion(bf16[768,1024]{1,0:T(8,128)(2,1)} %param.11, bf16[64,768]{1,0:T(8,128)(2,1)S(1)} %get-tuple-element.14, bf16[64,768]{1,0:T(8,128)(2,1)S(1)} %get-tuple-element.15, bf16[64,768]{1,0:T(8,128)(2,1)S(1)} %get-tuple-element.16, bf16[64,768]{1,0:T(8,128)(2,1)S(1)} %get-tuple-element.13), kind=kOutput, calls=%fused_computation.12 | convolution fusion | flops 405012224 | bytes 2491392 | tf_op jit(solution)/shard_map/dot_general | solution.py:180
  16.5 3.1 %convolution_convert_fusion = bf16[256,3072]{1,0:T(8,128)(2,1)} fusion(bf16[1024,3072]{1,0:T(8,128)(2,1)S(1)} %copy-done.4, bf16[256,1024]{1,0:T(8,128)(2,1)S(1)} %get-tuple-element.22, f32[256]{0:T(256)S(1)} %add_rsqrt_fusion.3, f32[256]{0:T(256)S(1)} %broadcast_multiply_fusion.3), kind=kOutput, calls=%fused_computation.3 | convolution fusion | flops 1612447744 | bytes 8390656 | tf_op jit(solution)/shard_map/dot_general | solution.py:48
  19.6 2.6 %copy.62 = bf16[256,3072]{0,1:T(8,128)(2,1)} copy(bf16[256,3072]{1,0:T(8,128)(2,1)} %convolution_convert_fusion) | data formatting | bytes 3145728 | tf_op jit(solution)/shard_map/convert_element_type | solution.py:48
  22.2 2.7 %convolution_convert_fusion.1 = bf16[51,3072]{1,0:T(8,128)(2,1)} fusion(bf16[256,3072]{1,0:T(8,128)(2,1)} %convolution_convert_fusion, s32[51]{0:T(128)S(1)} %dynamic-slice_bitcast_fusion), kind=kOutput, calls=%fused_computation.5 | convolution fusion | flops 80385792 | bytes 1886412 | tf_op jit(solution)/shard_map/dot_general | solution.py:191
  30.1 2.3 %reshape.247 = bf16[51,3,16,64]{3,2,1,0:T(8,128)(2,1)} reshape(bf16[51,3072]{1,0:T(8,128)(2,1)} %convolution_convert_fusion.1) | data formatting | bytes 626688 | tf_op jit(solution)/shard_map/jvp()/reshape | solution.py:53
  32.3 1.3 %fusion.130 = (bf16[51,1,16,64]{3,2,1,0:T(8,128)(2,1)S(1)}, bf16[51,1,16,64]{3,2,1,0:T(8,128)(2,1)S(1)}, bf16[51,1,16,64]{3,2,1,0:T(8,128)(2,1)S(1)}) fusion(bf16[51,3,16,64]{3,2,1,0:T(8,128)(2,1)} %reshape.247), kind=kLoop, calls=%fused_computation.234 | loop fusion | bytes 626688 | tf_op jit(solution)/shard_map/jvp()/slice | solution.py:41
  36.3 1.1 %reshape.248 = bf16[51,1024]{1,0:T(8,128)(2,1)S(1)} reshape(bf16[51,16,64]{2,1,0:T(8,128)(2,1)} %copy.56) | data formatting | bytes 208896 | tf_op jit(solution)/shard_map/jvp()/reshape | solution.py:54
  37.4 2.8 %convolution_convert_fusion.18 = bf16[51,768]{1,0:T(8,128)(2,1)} fusion(bf16[1024,768]{1,0:T(8,128)(2,1)} %param.15, f32[51,1024]{1,0:T(8,128)S(1)} %get-tuple-element.34, bf16[51,1024]{1,0:T(8,128)(2,1)S(1)} %reshape.248, bf16[1024,1024]{1,0:T(8,128)(2,1)S(1)} %copy-done), kind=kOutput, calls=%fused_computation.54 | convolution fusion | flops 187314432 | bytes 4061696 | tf_op jit(solution)/shard_map/jvp()/dot_general | solution.py:87
  40.3 2.0 %fusion.3 = bf16[256,768]{1,0:T(8,128)(2,1)} fusion(bf16[51,768]{1,0:T(8,128)(2,1)} %convolution_convert_fusion.18, bf16[768]{0:T(1024)(128)(2,1)S(1)} %convolution_reduce_fusion, pred[256]{0:T(512)(128)(4,1)S(1)} %broadcast_compare_fusion, s32[51]{0:T(128)S(1)} %dynamic-slice_bitcast_fusion), kind=kOutput, calls=%fused_computation.18 | convolution fusion | flops 20263680 | bytes 473548 | tf_op jit(solution)/shard_map/jvp()/dot_general | solution.py:93
  42.3 1.2 %copy.57 = bf16[256,768]{0,1:T(8,128)(2,1)S(1)} copy(bf16[256,768]{1,0:T(8,128)(2,1)} %fusion.3) | data formatting | bytes 786432 | tf_op jit(solution)/shard_map/jvp()/convert_element_type | solution.py:94
  43.5 1.3 %fusion.68 = f32[16,256,48]{1,2,0:T(8,128)S(1)} fusion(bf16[256,16,48]{0,2,1:T(8,128)(2,1)S(1)} %bitcast.172, bf16[3,16,48,48]{3,2,1,0:T(8,128)(2,1)} %param.16), kind=kOutput, calls=%fused_computation.136 | convolution fusion | flops 18874368 | bytes 1376256 | tf_op jit(solution)/shard_map/jvp(pgi,gio->pgo)/dot_general | solution.py:99
  44.8 1.2 %convolution_add_fusion.1 = f32[16,256,48]{1,2,0:T(8,128)S(1)} fusion(f32[16,256,48]{1,2,0:T(8,128)S(1)} %fusion.68, bf16[256,16,48]{0,2,1:T(8,128)(2,1)S(1)} %bitcast.173, bf16[3,16,48,48]{3,2,1,0:T(8,128)(2,1)} %param.16), kind=kOutput, calls=%fused_computation.15 | convolution fusion | flops 19070976 | bytes 2162688 | tf_op jit(solution)/shard_map/jvp(pgi,gio->pgo)/dot_general | solution.py:99
  46.0 1.4 %fusion.132 = (f32[256]{0:T(256)S(1)}, f32[16,256,48]{1,2,0:T(8,128)S(1)}) fusion(f32[16,256,48]{1,2,0:T(8,128)S(1)} %convolution_add_fusion.1, bf16[256,16,48]{0,2,1:T(8,128)(2,1)S(1)} %bitcast.174, bf16[3,16,48,48]{3,2,1,0:T(8,128)(2,1)} %param.16), kind=kOutput, calls=%fused_computation.236 | convolution fusion | flops 19267328 | bytes 2163712 | tf_op jit(solution)/shard_map/jvp(pgi,gio->pgo)/dot_general | solution.py:99
  49.0 2.3 %copy.61 = f32[256,768]{1,0:T(8,128)} copy(f32[256,768]{0,1:T(8,128)} %bitcast.168) | data formatting | bytes 1572864 | tf_op jit(solution)/shard_map/jvp()/reshape | solution.py:105
  51.3 3.0 %fusion.33 = f32[256,768]{1,0:T(8,128)S(1)} fusion(f32[256,768]{1,0:T(8,128)} %copy.61, f32[256]{0:T(256)} %fusion.115, f32[256]{0:T(256)} %copy-done.34), kind=kLoop, calls=%fused_computation.84 | loop fusion | flops 12582912 | bytes 1574912 | tf_op jit(solution)/shard_map/jvp()/erfc | solution.py:105
  54.4 2.1 %fusion.69 = f32[256,1024]{1,0:T(8,128)S(1)} fusion(bf16[768,1024]{1,0:T(8,128)(2,1)} %param.17, f32[256,768]{1,0:T(8,128)S(1)} %fusion.33, bf16[256,768]{1,0:T(8,128)(2,1)S(1)} %copy-done.12, f32[256,768]{1,0:T(8,128)S(1)} %copy-done.1, f32[256]{0:T(256)} %fusion.115, f32[256]{0:T(256)} %copy-done.34), kind=kOutput, calls=%fused_computation.137 | convolution fusion | flops 404029440 | bytes 4589568 | tf_op jit(solution)/shard_map/jvp()/dot_general | solution.py:108
  56.6 1.1 %multiply_reduce_fusion = f32[]{:T(128)} fusion(f32[256,1024]{1,0:T(8,128)S(1)} %fusion.69, f32[256]{0:T(256)S(1)} %copy-done.39, f32[256]{0:T(256)S(1)} %copy-done.40, f32[256,1024]{1,0:T(8,128)S(1)} %get-tuple-element.30, f32[256]{0:T(256)S(1)} %copy-done.37), kind=kLoop, calls=%fused_computation.64 | loop fusion | flops 2097151 | bytes 2100228 | tf_op jit(solution)/shard_map/jvp()/reduce_sum | solution.py:127
  59.2 2.8 %fusion.129 = (f32[256]{0:T(256)S(1)}, f32[256,768]{1,0:T(8,128)S(1)}) fusion(f32[256]{0:T(256)S(1)} %multiply_multiply_fusion.8, bf16[256,768]{1,0:T(8,128)(2,1)S(1)} %get-tuple-element.32, f32[256]{0:T(256)S(1)} %copy-done.38, f32[256,768]{1,0:T(8,128)S(1)} %copy-done.1, f32[256]{0:T(256)S(1)} %copy-done.35), kind=kLoop, calls=%fused_computation.233 | loop fusion | flops 15531776 | bytes 1970176 | tf_op jit(solution)/shard_map/transpose(jvp())/reduce_sum | solution.py:19
  63.7 2.2 %convolution_convert_fusion.13 = bf16[51,1024]{1,0:T(8,128)(2,1)S(1)} fusion(bf16[1024,768]{1,0:T(8,128)(2,1)} %param.15, bf16[256,768]{1,0:T(8,128)(2,1)S(1)} %copy-done.15, bf16[256,768]{1,0:T(8,128)(2,1)S(1)} %copy.68, pred[256]{0:T(512)(128)(4,1)S(1)} %copy-done.50, s32[51]{0:T(128)S(1)} %copy-done.46), kind=kOutput, calls=%fused_computation.47 | convolution fusion | flops 100964352 | bytes 2464204 | tf_op jit(solution)/shard_map/transpose(jvp())/dot_general | solution.py:87
  67.5 1.4 %fusion.16 = bf16[51,1,16,64]{3,0,2,1:T(8,128)(2,1)S(1)} fusion(bf16[51,16,64]{2,1,0:T(8,128)(2,1)S(1)} %reshape.255, f32[16,51,51]{1,2,0:T(8,128)} %copy-done.20, f32[16,51]{1,0:T(8,128)S(1)} %copy-done.44), kind=kOutput, calls=%fused_computation.43 | convolution fusion | flops 5462304 | bytes 378624 | tf_op jit(solution)/shard_map/transpose(jvp(hqk,khd->qhd))/dot_general | solution.py:36
  68.8 1.3 %multiply_reduce_fusion.3 = (f32[16,51]{1,0:T(8,128)S(1)}, f32[16,51,51]{1,2,0:T(8,128)S(1)}) fusion(f32[16,51,51]{1,2,0:T(8,128)} %copy-done.20, f32[16,51]{1,0:T(8,128)S(1)} %multiply_divide_fusion, bf16[51,1,16,64]{3,2,1,0:T(8,128)(2,1)S(1)} %copy-done.19, bf16[51,16,64]{2,1,0:T(8,128)(2,1)S(1)} %reshape.255), kind=kOutput, calls=%fused_computation.127 | convolution fusion | flops 5534112 | bytes 548352 | tf_op jit(solution)/shard_map/transpose(jvp(hqk,khd->qhd))/dot_general | solution.py:36
  72.7 5.0 %multiply_reduce_fusion.5 = (f32[51]{0:T(128)S(1)}, f32[51]{0:T(128)S(1)}, f32[51,1024]{1,0:T(8,128)S(1)}) fusion(f32[51,1024]{1,0:T(8,128)S(1)} %copy-done.6, f32[51]{0:T(128)S(1)} %broadcast_multiply_fusion.4, bf16[51,3072]{1,0:T(8,128)(2,1)S(1)} %reshape.256, bf16[1024,3072]{1,0:T(8,128)(2,1)} %param.12), kind=kOutput, calls=%fused_computation.158 | convolution fusion | flops 321229696 | bytes 7023204 | tf_op jit(solution)/shard_map/transpose(jvp())/dot_general | solution.py:119
  78.7 1.5 %collective-permute-start.4 = (bf16[51,1024]{1,0:T(8,128)(2,1)S(1)}, bf16[51,1024]{1,0:T(8,128)(2,1)S(1)}, u32[]{:S(2)}, u32[]{:S(2)}) collective-permute-start(bf16[51,1024]{1,0:T(8,128)(2,1)S(1)} %fusion.103), channel_id=1, source_target_pairs={{0,2},{1,3},{2,0},{3,1},{4,6},{5,7},{6,4},{7,5},{8,10},{9,11},{10,... | collective-permute-start | bytes 313352 | tf_op jit(solution)/shard_map/ppermute | solution.py:134
  81.0 2.7 %collective-permute-done.3 = bf16[51,1024]{1,0:T(8,128)(2,1)S(1)} collective-permute-done((bf16[51,1024]{1,0:T(8,128)(2,1)S(1)}, bf16[51,1024]{1,0:T(8,128)(2,1)S(1)}, u32[]{:S(2)}, u32[]{:S(2)}) %collective-permute-start.3) | collective-permute-done | bytes 104480 | tf_op jit(solution)/shard_map/ppermute | solution.py:134
  84.7 1.2 %collective-permute-done.5 = bf16[51,1024]{1,0:T(8,128)(2,1)S(1)} collective-permute-done((bf16[51,1024]{1,0:T(8,128)(2,1)S(1)}, bf16[51,1024]{1,0:T(8,128)(2,1)S(1)}, u32[]{:S(2)}, u32[]{:S(2)}) %collective-permute-start.5) | collective-permute-done | bytes 104480 | tf_op jit(solution)/shard_map/ppermute | solution.py:134
  85.9 1.4 %fusion.20 = f32[192,1024]{1,0:T(8,128)} fusion(bf16[51,1024]{1,0:T(8,128)(2,1)S(1)} %collective-permute-done.5, bf16[51,1024]{1,0:T(8,128)(2,1)S(1)} %collective-permute-done.4, bf16[51,1024]{1,0:T(8,128)(2,1)S(1)} %collective-permute-done.3, bf16[51,1024]{1,0:T(8,128)(2,1)S(1)} %fusion.103, bf16[256,768]{1,0:T(8,128)(2,1)S(1)} %pad_maximum_fusion, ...), kind=kOutput, calls=%fused_computation.55 | convolution fusion | flops 102032640 | bytes 1377284 | tf_op jit(solution)/shard_map/vc,vd->cd/dot_general | solution.py:224
  (170 shorter events, 21.6 us)
Async XLA Ops:
  0.6 27.2 %copy-start = (bf16[1024,1024]{1,0:T(8,128)(2,1)S(1)}, bf16[1024,1024]{1,0:T(8,128)(2,1)}, u32[]{:S(2)}) copy-start(bf16[1024,1024]{1,0:T(8,128)(2,1)} %param.13) | copy-start | bytes 6291460
  0.6 11.9 %collective-permute-start = (bf16[64,768]{1,0:T(8,128)(2,1)}, bf16[64,768]{1,0:T(8,128)(2,1)S(1)}, u32[]{:S(2)}, u32[]{:S(2)}) collective-permute-start(bf16[64,768]{1,0:T(8,128)(2,1)} %param.9), channel_id=1, source_target_pairs={{0,1},{1,2},{2,3},{3,0},{4,5},{5,6},{6,7},{7,4},{8,9},{9,10},{10,1... | collective-permute-start | bytes 294920 | tf_op jit(solution)/shard_map/ppermute | solution.py:134
  3.7 8.9 %collective-permute-start.1 = (bf16[64,768]{1,0:T(8,128)(2,1)}, bf16[64,768]{1,0:T(8,128)(2,1)S(1)}, u32[]{:S(2)}, u32[]{:S(2)}) collective-permute-start(bf16[64,768]{1,0:T(8,128)(2,1)} %param.9), channel_id=1, source_target_pairs={{0,2},{1,3},{2,0},{3,1},{4,6},{5,7},{6,4},{7,5},{8,10},{9,11},{10,... | collective-permute-start | bytes 294920 | tf_op jit(solution)/shard_map/ppermute | solution.py:134
  5.2 7.4 %collective-permute-start.2 = (bf16[64,768]{1,0:T(8,128)(2,1)}, bf16[64,768]{1,0:T(8,128)(2,1)S(1)}, u32[]{:S(2)}, u32[]{:S(2)}) collective-permute-start(bf16[64,768]{1,0:T(8,128)(2,1)} %param.9), channel_id=1, source_target_pairs={{0,3},{1,0},{2,1},{3,2},{4,7},{5,4},{6,5},{7,6},{8,11},{9,8},{10,9... | collective-permute-start | bytes 294920 | tf_op jit(solution)/shard_map/ppermute | solution.py:134
  7.3 33.0 %copy-start.45 = (s32[51]{0:T(128)}, s32[51]{0:T(128)S(1)}, u32[]{:S(2)}) copy-start(s32[51]{0:T(128)S(1)} %dynamic-slice_bitcast_fusion) | copy-start | bytes 616
  7.5 32.8 %copy-start.49 = (pred[256]{0:T(512)(128)(4,1)}, pred[256]{0:T(512)(128)(4,1)S(1)}, u32[]{:S(2)}) copy-start(pred[256]{0:T(512)(128)(4,1)S(1)} %broadcast_compare_fusion) | copy-start | bytes 772
  10.7 5.8 %copy-start.4 = (bf16[1024,3072]{1,0:T(8,128)(2,1)S(1)}, bf16[1024,3072]{1,0:T(8,128)(2,1)}, u32[]{:S(2)}) copy-start(bf16[1024,3072]{1,0:T(8,128)(2,1)} %param.12) | copy-start | bytes 18874372
  13.9 2.5 %copy-start.22 = (bf16[64,768]{1,0:T(8,128)(2,1)}, bf16[64,768]{1,0:T(8,128)(2,1)S(1)}, u32[]{:S(2)}) copy-start(bf16[64,768]{1,0:T(8,128)(2,1)S(1)} %get-tuple-element.13) | copy-start | bytes 294916
  13.9 2.5 %copy-start.24 = (bf16[64,768]{1,0:T(8,128)(2,1)}, bf16[64,768]{1,0:T(8,128)(2,1)S(1)}, u32[]{:S(2)}) copy-start(bf16[64,768]{1,0:T(8,128)(2,1)S(1)} %get-tuple-element.14) | copy-start | bytes 294916
  13.9 2.5 %copy-start.26 = (bf16[64,768]{1,0:T(8,128)(2,1)}, bf16[64,768]{1,0:T(8,128)(2,1)S(1)}, u32[]{:S(2)}) copy-start(bf16[64,768]{1,0:T(8,128)(2,1)S(1)} %get-tuple-element.15) | copy-start | bytes 294916
  13.9 2.5 %copy-start.28 = (bf16[64,768]{1,0:T(8,128)(2,1)}, bf16[64,768]{1,0:T(8,128)(2,1)S(1)}, u32[]{:S(2)}) copy-start(bf16[64,768]{1,0:T(8,128)(2,1)S(1)} %get-tuple-element.16) | copy-start | bytes 294916
  22.2 3.5 %copy-start.2 = (bf16[256,3072]{0,1:T(8,128)(2,1)S(1)}, bf16[256,3072]{0,1:T(8,128)(2,1)}, u32[]{:S(2)}) copy-start(bf16[256,3072]{0,1:T(8,128)(2,1)} %copy.62) | copy-start | bytes 4718596
  25.7 11.7 %copy-start.5 = (f32[51,1024]{1,0:T(8,128)}, f32[51,1024]{1,0:T(8,128)S(1)}, u32[]{:S(2)}) copy-start(f32[51,1024]{1,0:T(8,128)S(1)} %get-tuple-element.34) | copy-start | bytes 626692
  47.4 7.0 %copy-start.12 = (bf16[256,768]{1,0:T(8,128)(2,1)S(1)}, bf16[256,768]{1,0:T(8,128)(2,1)}, u32[]{:S(2)}) copy-start(bf16[256,768]{1,0:T(8,128)(2,1)} %fusion.3) | copy-start | bytes 1179652
  51.3 3.0 %copy-start.1 = (f32[256,768]{1,0:T(8,128)S(1)}, f32[256,768]{1,0:T(8,128)}, u32[]{:S(2)}) copy-start(f32[256,768]{1,0:T(8,128)} %copy.61) | copy-start | bytes 2359300
  54.4 2.2 %copy-start.37 = (f32[256]{0:T(256)S(1)}, f32[256]{0:T(256)}, u32[]{:S(2)}) copy-start(f32[256]{0:T(256)} %copy-done.36) | copy-start | bytes 3076
  59.2 2.8 %copy-start.14 = (bf16[256,768]{1,0:T(8,128)(2,1)}, bf16[256,768]{1,0:T(8,128)(2,1)S(1)}, u32[]{:S(2)}) copy-start(bf16[256,768]{1,0:T(8,128)(2,1)S(1)} %get-tuple-element.32) | copy-start | bytes 1179652
  59.2 3.1 %copy-start.7 = (bf16[3,16,48,48]{3,2,1,0:T(8,128)(2,1)S(1)}, bf16[3,16,48,48]{3,2,1,0:T(8,128)(2,1)}, u32[]{:S(2)}) copy-start(bf16[3,16,48,48]{3,2,1,0:T(8,128)(2,1)} %param.16) | copy-start | bytes 663556
  66.5 2.3 %copy-start.19 = (bf16[51,1,16,64]{3,2,1,0:T(8,128)(2,1)S(1)}, bf16[51,1,16,64]{3,2,1,0:T(8,128)(2,1)}, u32[]{:S(2)}) copy-start(bf16[51,1,16,64]{3,2,1,0:T(8,128)(2,1)} %copy-done.18) | copy-start | bytes 313348
  67.2 2.9 %copy-start.9 = (bf16[51,1,16,64]{3,2,1,0:T(8,128)(2,1)S(1)}, bf16[51,1,16,64]{3,2,1,0:T(8,128)(2,1)}, u32[]{:S(2)}) copy-start(bf16[51,1,16,64]{3,2,1,0:T(8,128)(2,1)} %copy-done.8) | copy-start | bytes 313348
  67.2 2.9 %copy-start.11 = (bf16[51,1,16,64]{3,2,1,0:T(8,128)(2,1)S(1)}, bf16[51,1,16,64]{3,2,1,0:T(8,128)(2,1)}, u32[]{:S(2)}) copy-start(bf16[51,1,16,64]{3,2,1,0:T(8,128)(2,1)} %copy-done.10) | copy-start | bytes 313348
  67.2 2.9 %copy-start.31 = (f32[51,16]{0,1:T(8,128)S(1)}, f32[51,16]{0,1:T(8,128)}, u32[]{:S(2)}) copy-start(f32[51,16]{0,1:T(8,128)} %copy-done.30) | copy-start | bytes 9796
  67.4 2.7 %copy-start.21 = (f32[16,51,51]{1,2,0:T(8,128)S(1)}, f32[16,51,51]{1,2,0:T(8,128)}, u32[]{:S(2)}) copy-start(f32[16,51,51]{1,2,0:T(8,128)} %copy-done.20) | copy-start | bytes 499396
  72.7 5.3 %copy-start.17 = (bf16[51,1024]{1,0:T(8,128)(2,1)S(1)}, bf16[51,1024]{1,0:T(8,128)(2,1)}, u32[]{:S(2)}) copy-start(bf16[51,1024]{1,0:T(8,128)(2,1)} %copy-done.16) | copy-start | bytes 313348
  72.7 8.2 %copy-start.23 = (bf16[64,768]{1,0:T(8,128)(2,1)S(1)}, bf16[64,768]{1,0:T(8,128)(2,1)}, u32[]{:S(2)}) copy-start(bf16[64,768]{1,0:T(8,128)(2,1)} %copy-done.22) | copy-start | bytes 294916
  72.7 8.2 %copy-start.25 = (bf16[64,768]{1,0:T(8,128)(2,1)S(1)}, bf16[64,768]{1,0:T(8,128)(2,1)}, u32[]{:S(2)}) copy-start(bf16[64,768]{1,0:T(8,128)(2,1)} %copy-done.24) | copy-start | bytes 294916
  72.7 8.2 %copy-start.27 = (bf16[64,768]{1,0:T(8,128)(2,1)S(1)}, bf16[64,768]{1,0:T(8,128)(2,1)}, u32[]{:S(2)}) copy-start(bf16[64,768]{1,0:T(8,128)(2,1)} %copy-done.26) | copy-start | bytes 294916
  72.7 8.2 %copy-start.29 = (bf16[64,768]{1,0:T(8,128)(2,1)S(1)}, bf16[64,768]{1,0:T(8,128)(2,1)}, u32[]{:S(2)}) copy-start(bf16[64,768]{1,0:T(8,128)(2,1)} %copy-done.28) | copy-start | bytes 294916
  72.7 13.2 %copy-start.48 = (s32[204]{0:T(256)S(1)}, s32[204]{0:T(256)}, u32[]{:S(2)}) copy-start(s32[204]{0:T(256)} %eq.93) | copy-start | bytes 2452
  78.1 5.5 %collective-permute-start.3 = (bf16[51,1024]{1,0:T(8,128)(2,1)S(1)}, bf16[51,1024]{1,0:T(8,128)(2,1)S(1)}, u32[]{:S(2)}, u32[]{:S(2)}) collective-permute-start(bf16[51,1024]{1,0:T(8,128)(2,1)S(1)} %fusion.103), channel_id=1, source_target_pairs={{0,3},{1,0},{2,1},{3,2},{4,7},{5,4},{6,5},{7,6},{8,11},{9,8},{10,9... | collective-permute-start | bytes 313352 | tf_op jit(solution)/shard_map/ppermute | solution.py:134
  78.7 6.0 %collective-permute-start.4 = (bf16[51,1024]{1,0:T(8,128)(2,1)S(1)}, bf16[51,1024]{1,0:T(8,128)(2,1)S(1)}, u32[]{:S(2)}, u32[]{:S(2)}) collective-permute-start(bf16[51,1024]{1,0:T(8,128)(2,1)S(1)} %fusion.103), channel_id=1, source_target_pairs={{0,2},{1,3},{2,0},{3,1},{4,6},{5,7},{6,4},{7,5},{8,10},{9,11},{10,... | collective-permute-start | bytes 313352 | tf_op jit(solution)/shard_map/ppermute | solution.py:134
  80.2 5.7 %collective-permute-start.5 = (bf16[51,1024]{1,0:T(8,128)(2,1)S(1)}, bf16[51,1024]{1,0:T(8,128)(2,1)S(1)}, u32[]{:S(2)}, u32[]{:S(2)}) collective-permute-start(bf16[51,1024]{1,0:T(8,128)(2,1)S(1)} %fusion.103), channel_id=1, source_target_pairs={{0,1},{1,2},{2,3},{3,0},{4,5},{5,6},{6,7},{7,4},{8,9},{9,10},{10,1... | collective-permute-start | bytes 313352 | tf_op jit(solution)/shard_map/ppermute | solution.py:134
  (26 other events, 29.9 us)

commit v8 on v4

--- a/solution.py
+++ b/solution.py
@@ -3,6 +3,8 @@
 import jax
 import jax.numpy as jnp
 from jax import lax
+from jax.experimental import pallas as pl
+from jax.experimental.pallas import tpu as pltpu
 from jax.sharding import PartitionSpec as P
 
 D = 1024
@@ -92,6 +94,69 @@
     return jnp.sum(mismatch * mismatch)
 
 
+def teacher_kernel(pixels_ref, embed_w_ref, w_qkv_ref, w_out_ref, embedded_ref, targets_ref,
+                   context_ref):
+    rows = pixels_ref.shape[0]
+    head_dim = D // HEADS
+    embedded = jnp.dot(pixels_ref[...], embed_w_ref[...], preferred_element_type=jnp.float32)
+    embedded = embedded.astype(jnp.bfloat16)
+    embedded_ref[...] = embedded
+    values = embedded.astype(jnp.float32)
+    average = jnp.mean(values, axis=-1, keepdims=True)
+    centred = values - average
+    spread = jnp.mean(centred * centred, axis=-1, keepdims=True)
+    normed = (centred * lax.rsqrt(spread + EPSILON)).astype(jnp.bfloat16)
+    lane = lax.broadcasted_iota(jnp.int32, (rows, 2 * head_dim), 1)
+    first = lane < head_dim
+    score_scale = 1.0 / math.sqrt(head_dim)
+
+    def pair_norm(block):
+        squares = block * block
+        low = jnp.sum(jnp.where(first, squares, 0.0), axis=-1, keepdims=True) / head_dim
+        high = jnp.sum(jnp.where(first, 0.0, squares), axis=-1, keepdims=True) / head_dim
+        scale = jnp.where(first, lax.rsqrt(low + EPSILON), lax.rsqrt(high + EPSILON))
+        return (block * scale).astype(jnp.bfloat16)
+
+    for pair in range(HEADS // 2):
+        width = 2 * head_dim
+        cols = slice(pair * width, (pair + 1) * width)
+        q_block = jnp.dot(normed, w_qkv_ref[:, pair * width:(pair + 1) * width],
+                          preferred_element_type=jnp.float32).astype(jnp.bfloat16)
+        k_block = jnp.dot(normed, w_qkv_ref[:, D + pair * width:D + (pair + 1) * width],
+                          preferred_element_type=jnp.float32).astype(jnp.bfloat16)
+        v_block = jnp.dot(normed, w_qkv_ref[:, 2 * D + pair * width:2 * D + (pair + 1) * width],
+                          preferred_element_type=jnp.float32).astype(jnp.bfloat16)
+        queries = pair_norm(q_block.astype(jnp.float32))
+        key_rows = pair_norm(k_block.astype(jnp.float32))
+        zero = jnp.zeros_like(queries)
+        mixed = []
+        for half in range(2):
+            chosen = first if half == 0 else jnp.logical_not(first)
+            scores = lax.dot_general(
+                jnp.where(chosen, queries, zero), key_rows,
+                (((1,), (1,)), ((), ())), preferred_element_type=jnp.float32) * score_scale
+            exponent = jnp.exp(scores)
+            weights = (exponent / jnp.sum(exponent, axis=-1, keepdims=True)).astype(jnp.bfloat16)
+            mixed.append(jnp.dot(weights, v_block, preferred_element_type=jnp.float32))
+        context = jnp.where(first, mixed[0], mixed[1]).astype(jnp.bfloat16)
+        context_ref[:, cols] = context
+    branch = jnp.dot(context_ref[...], w_out_ref[...], preferred_element_type=jnp.float32)
+    average = jnp.mean(branch, axis=-1, keepdims=True)
+    centred = branch - average
+    spread = jnp.mean(centred * centred, axis=-1, keepdims=True)
+    targets_ref[...] = (centred * lax.rsqrt(spread + EPSILON)).astype(jnp.bfloat16)
+
+
+def teacher(pixels, embed_w, w_qkv, w_out):
+    rows = pixels.shape[0]
+    return pl.pallas_call(
+        teacher_kernel,
+        out_shape=(jax.ShapeDtypeStruct((rows, D), jnp.bfloat16),
+                   jax.ShapeDtypeStruct((rows, D), jnp.bfloat16)),
+        scratch_shapes=[pltpu.VMEM((rows, D), jnp.bfloat16)],
+    )(pixels, embed_w, w_qkv, w_out)
+
+
 def ring_gather(values, group_size):
     parts = [values]
     for shift in range(1, group_size):
@@ -142,15 +207,15 @@
     col_width = patches.shape[1] // group_size
     positions = lax.dynamic_index_in_dim(visible_index, own_index, 0, keepdims=False)
     clip_pixels = in_mask_order(ring_gather(patches, group_size), own_index)
-    embedded = jnp.dot(clip_pixels, embed_w, preferred_element_type=jnp.float32).astype(
-        jnp.bfloat16
-    )
+    if total_rows <= 256:
+        embedded, all_targets = teacher(clip_pixels, embed_w, w_qkv, w_out)
+    else:
+        embedded = jnp.dot(clip_pixels, embed_w, preferred_element_type=jnp.float32).astype(
+            jnp.bfloat16
+        )
+        branch = split_teacher(embedded, w_qkv, w_out, own_index, group_size)
+        all_targets = row_norm(branch).astype(jnp.bfloat16)
     visible_in = embedded[positions]
-    if HEADS * total_rows * total_rows * 4 <= (1 << 24):
-        branch = attention_branch(embedded, w_qkv, w_out)
-    else:
-        branch = split_teacher(embedded, w_qkv, w_out, own_index, group_size)
-    all_targets = row_norm(branch).astype(jnp.bfloat16)
 
     def objective(rows_in):
         return copy_terms(

time: 87.3 us -> 102 us (1.17)
  Pallas kernels: 0 us -> 13.4 us
  local copies, waits for them, and re-layouts: 13.3 us -> 22.8 us
  matrix products: 47.3 us -> 40.9 us
  waiting for transfers between devices: 3.77 us -> 1.04 us
    pallas_call x0 -> x1, Pallas kernels: none -> 13.4 us  [teacher(): pl.pallas_call(teacher_kernel, out_shape=(jax.ShapeDtypeStruct((rows, D),...]
    dot_general x3 -> x2, matrix products: 14.8 us -> 8.98 us  [attention_branch(): jnp.dot(normed, w_qkv, preferred_element_type=jnp.float32)]
    dot_general x6, matrix products: 4.61 us -> 8.77 us  [decoder_output(): jnp.einsum('pgi,gio->pgo', padded[offset:offset + total_rows], conv_w[off...]
    dot_general x4 -> x3, matrix products: 3.88 us -> 0.89 us  [mix_heads(): jnp.einsum('hqk,khd->qhd', weights, values, preferred_element_type=jnp.fl...]
    ppermute x6, waiting for transfers between devices: 3.77 us -> 1.04 us  [ring_gather(): parts.append(lax.ppermute(values, 'mask', pairs))]
    convert_element_type x1 -> x0, local copies, waits for them, and re-layouts: 2.59 us -> none  [attention_branch(): jnp.dot(normed, w_qkv, preferred_element_type=jnp.float32)]
    dot_general x4 -> x3, matrix products: 3.71 us -> 1.53 us  [mix_heads(): jnp.einsum('qhd,khd->hqk', queries, key_rows, preferred_element_type=jnp....]
    unnamed x61 -> x73, local copies, waits for them, and re-layouts: 2.82 us -> 5 us
  transfers between devices with their start and end apart: 6 -> 6, of which waited for: 3 -> 2; matrix products, arithmetic and copies ran while one was open for 8% -> 10% of each run, Pallas kernels for 0% -> 0%
where the time goes in v8:
time: 102 us; the launch traced here: 101 us
  matrix products  40.9 us (40%)
  local copies, waits for them, and re-layouts  22.8 us (22%)
  Pallas kernels  13.4 us (13%)
  other arithmetic  11.1 us (11%)
  starting transfers between devices  9.05 us (9%)
  between operations  2.94 us (3%)
  waiting for transfers between devices  1.04 us (1%)
    pallas_call x1, Pallas kernels, teacher(): pl.pallas_call(teacher_kernel, out_shape=(jax.ShapeDtypeStruct((rows, D),...  13.4 us
    ppermute x6, starting transfers between devices, ring_gather(): parts.append(lax.ppermute(values, 'mask', pairs))  9.05 us
    dot_general x2, matrix products, attention_branch(): jnp.dot(normed, w_qkv, preferred_element_type=jnp.float32)  8.98 us
    dot_general x6, matrix products, decoder_output(): jnp.einsum('pgi,gio->pgo', padded[offset:offset + total_rows], conv_w[off...  8.77 us
    dot_general x2, matrix products, decoder_output(): return jnp.dot(hidden, dec_out, preferred_element_type=jnp.float32)  7.78 us
    dot_general x2, matrix products, decoder_output(): jnp.dot(visible_out, dec_in, preferred_element_type=jnp.float32)  5.13 us
    unnamed x73, local copies, waits for them, and re-layouts  5 us
    reduce_sum x2, other arithmetic, row_norm(): centred = values - average  2.76 us
  transfers between devices with their start and end apart: 6, of which 2 were waited for; matrix products, arithmetic and copies ran while one was open for 10% of the time, Pallas kernels for 0%

profile of v8, /device:TPU:0, one launch (start us, length us, event | category | flops | bytes accessed | tf_op | source)
XLA Modules:
  0.0 101.2 jit_solution(7689505971965770528)
XLA Ops:
  0.7 3.0 %collective-permute-start = (bf16[64,768]{1,0:T(8,128)(2,1)}, bf16[64,768]{1,0:T(8,128)(2,1)S(1)}, u32[]{:S(2)}, u32[]{:S(2)}) collective-permute-start(bf16[64,768]{1,0:T(8,128)(2,1)} %param.9), channel_id=1, source_target_pairs={{0,1},{1,2},{2,3},{3,0},{4,5},{5,6},{6,7},{7,4},{8,9},{9,10},{10,1... | collective-permute-start | bytes 294920 | tf_op jit(solution)/shard_map/ppermute | solution.py:164
  3.7 1.5 %collective-permute-start.1 = (bf16[64,768]{1,0:T(8,128)(2,1)}, bf16[64,768]{1,0:T(8,128)(2,1)S(1)}, u32[]{:S(2)}, u32[]{:S(2)}) collective-permute-start(bf16[64,768]{1,0:T(8,128)(2,1)} %param.9), channel_id=1, source_target_pairs={{0,2},{1,3},{2,0},{3,1},{4,6},{5,7},{6,4},{7,5},{8,10},{9,11},{10,... | collective-permute-start | bytes 294920 | tf_op jit(solution)/shard_map/ppermute | solution.py:164
  5.2 1.4 %collective-permute-start.2 = (bf16[64,768]{1,0:T(8,128)(2,1)}, bf16[64,768]{1,0:T(8,128)(2,1)S(1)}, u32[]{:S(2)}, u32[]{:S(2)}) collective-permute-start(bf16[64,768]{1,0:T(8,128)(2,1)} %param.9), channel_id=1, source_target_pairs={{0,3},{1,0},{2,1},{3,2},{4,7},{5,4},{6,5},{7,6},{8,11},{9,8},{10,9... | collective-permute-start | bytes 294920 | tf_op jit(solution)/shard_map/ppermute | solution.py:164
  8.5 1.2 %gather_fusion = s32[4,51]{1,0:T(4,128)S(1)} fusion(s32[4,51]{1,0:T(4,128)} %param.10, s32[1024]{0:T(1024)S(1)} %pad_clamp_fusion.2), kind=kCustom, calls=%fused_computation | custom fusion | bytes 1648 | tf_op jit(solution)/shard_map/gather | solution.py:230
  12.3 2.3 %convolution_reduce_fusion = bf16[768]{0:T(1024)(128)(2,1)} fusion(bf16[1024,1]{0,1:T(2,128)(2,1)S(1)} %reshape.288, bf16[1024,768]{1,0:T(8,128)(2,1)} %param.15), kind=kOutput, calls=%fused_computation.41 | convolution fusion | flops 1572864 | bytes 1576448 | tf_op jit(solution)/shard_map/jvp()/dot_general | solution.py:63
  15.5 13.4 %shard_map.104 = (bf16[256,1024]{1,0:T(8,128)(2,1)}, bf16[256,1024]{1,0:T(8,128)(2,1)}) custom-call(bf16[256,768]{1,0:T(8,128)(2,1)} %pad_maximum_fusion.pixels_ref, bf16[768,1024]{1,0:T(8,128)(2,1)} %embed_w_ref.1, bf16[1024,3072]{1,0:T(8,128)(2,1)} %w_qkv_ref.1, bf16[1024,1024]{1,0:T(8,128)(2,1)} %w_out_ref.1), custom_call_target="tpu_custom_call" | custom-call | tf_op jit(solution)/shard_map/pallas_call | solution.py:152
  28.9 1.9 %gather_fusion.2 = bf16[51,1024]{1,0:T(8,128)(2,1)S(1)} fusion(bf16[256,1024]{1,0:T(8,128)(2,1)} %get-tuple-element.4, s32[1024]{0:T(1024)S(1)} %pad_clamp_fusion), kind=kCustom, calls=%fused_computation.2 | custom fusion | bytes 209100 | tf_op jit(solution)/shard_map/gather | solution.py:218
  32.2 4.0 %convolution_convert_fusion = bf16[51,3072]{1,0:T(8,128)(2,1)S(1)} fusion(bf16[1024,3072]{1,0:T(8,128)(2,1)} %w_qkv_ref.1, bf16[51,1024]{1,0:T(8,128)(2,1)S(1)} %gather_fusion.2, f32[51]{0:T(128)S(1)} %fusion.107, f32[51]{0:T(128)S(1)} %broadcast_multiply_fusion.2), kind=kOutput, calls=%fused_computation.3 | convolution fusion | flops 321229824 | bytes 6709656 | tf_op jit(solution)/shard_map/jvp()/dot_general | solution.py:51
  40.7 1.8 %reshape.254 = bf16[51,1024]{1,0:T(8,128)(2,1)} reshape(bf16[51,16,64]{2,1,0:T(8,128)(2,1)} %copy.50) | data formatting | bytes 208896 | tf_op jit(solution)/shard_map/jvp()/reshape | solution.py:53
  42.5 2.6 %convolution_convert_fusion.14 = bf16[51,768]{1,0:T(8,128)(2,1)S(1)} fusion(bf16[1024,768]{1,0:T(8,128)(2,1)S(1)} %copy-done.1, bf16[51,1024]{1,0:T(8,128)(2,1)} %reshape.254, bf16[1024,1024]{1,0:T(8,128)(2,1)} %w_out_ref.1, bf16[51,1024]{1,0:T(8,128)(2,1)S(1)} %gather_fusion.2), kind=kOutput, calls=%fused_computation.40 | convolution fusion | flops 187366656 | bytes 3957248 | tf_op jit(solution)/shard_map/jvp()/dot_general | solution.py:60
  45.1 1.8 %fusion.1 = bf16[256,768]{1,0:T(8,128)(2,1)} fusion(bf16[51,768]{1,0:T(8,128)(2,1)S(1)} %convolution_convert_fusion.14, bf16[768]{0:T(1024)(128)(2,1)} %convolution_reduce_fusion, pred[256]{0:T(512)(128)(4,1)} %broadcast_compare_fusion, s32[51]{0:T(128)} %copy-done.31), kind=kOutput, calls=%fused_computation.9 | convolution fusion | flops 20263680 | bytes 473548 | tf_op jit(solution)/shard_map/jvp()/dot_general | solution.py:66
  46.9 1.9 %copy.51 = bf16[256,768]{0,1:T(8,128)(2,1)} copy(bf16[256,768]{1,0:T(8,128)(2,1)} %fusion.1) | data formatting | bytes 786432 | tf_op jit(solution)/shard_map/jvp()/convert_element_type | solution.py:67
  48.8 1.5 %fusion.52 = f32[16,256,48]{1,2,0:T(8,128)S(1)} fusion(bf16[256,16,48]{0,2,1:T(8,128)(2,1)} %bitcast.142, bf16[3,16,48,48]{3,2,1,0:T(8,128)(2,1)} %param.16), kind=kOutput, calls=%fused_computation.107 | convolution fusion | flops 18874368 | bytes 1376256 | tf_op jit(solution)/shard_map/jvp(pgi,gio->pgo)/dot_general | solution.py:72
  50.4 1.2 %convolution_add_fusion.1 = f32[16,256,48]{1,2,0:T(8,128)S(1)} fusion(f32[16,256,48]{1,2,0:T(8,128)S(1)} %fusion.52, bf16[256,16,48]{0,2,1:T(8,128)(2,1)S(1)} %bitcast.143, bf16[3,16,48,48]{3,2,1,0:T(8,128)(2,1)} %param.16), kind=kOutput, calls=%fused_computation.7 | convolution fusion | flops 19070976 | bytes 2162688 | tf_op jit(solution)/shard_map/jvp(pgi,gio->pgo)/dot_general | solution.py:72
  51.6 2.2 %fusion.119 = (f32[256]{0:T(256)S(1)}, f32[16,256,48]{1,2,0:T(8,128)}) fusion(f32[16,256,48]{1,2,0:T(8,128)S(1)} %convolution_add_fusion.1, bf16[256,16,48]{0,2,1:T(8,128)(2,1)S(1)} %bitcast.144, bf16[3,16,48,48]{3,2,1,0:T(8,128)(2,1)} %param.16), kind=kOutput, calls=%fused_computation.209 | convolution fusion | flops 19267328 | bytes 2163712 | tf_op jit(solution)/shard_map/jvp(pgi,gio->pgo)/dot_general | solution.py:72
  53.8 2.3 %copy.55 = f32[256,768]{1,0:T(8,128)} copy(f32[256,768]{0,1:T(8,128)} %bitcast.138) | data formatting | bytes 1572864 | tf_op jit(solution)/shard_map/jvp()/reshape | solution.py:78
  56.1 1.3 %fusion.25 = f32[256]{0:T(256)S(1)} fusion(f32[16,256,48]{1,2,0:T(8,128)} %get-tuple-element.20, f32[256]{0:T(256)S(1)} %broadcast_multiply_fusion.1), kind=kLoop, calls=%fused_computation.64 | loop fusion | flops 589568 | bytes 788480 | tf_op jit(solution)/shard_map/jvp()/reduce_sum | solution.py:22
  57.4 4.5 %multiply_reduce_fusion = (f32[]{:T(128)}, f32[256,1024]{1,0:T(8,128)S(1)}) fusion(f32[256]{0:T(256)S(1)} %copy-done.30, bf16[256,1024]{1,0:T(8,128)(2,1)} %get-tuple-element.5, bf16[768,1024]{1,0:T(8,128)(2,1)S(1)} %copy-done, bf16[256,768]{1,0:T(8,128)(2,1)} %fusion.1, f32[256,768]{1,0:T(8,128)} %copy.55, f32[256]{0:T(256)S(1)} %fusion.103, ...), kind=kOutput, calls=%fused_computation.44 | convolution fusion | flops 417923072 | bytes 4328452 | tf_op jit(solution)/shard_map/jvp()/dot_general | solution.py:80
  62.0 3.3 %multiply_reduce_fusion.1 = (f32[256]{0:T(256)S(1)}, bf16[256,768]{1,0:T(8,128)(2,1)S(1)}) fusion(f32[256,768]{1,0:T(8,128)S(1)} %copy-done.4, f32[256]{0:T(256)S(1)} %broadcast_multiply_fusion.1, f32[256]{0:T(256)S(1)} %fusion.103, bf16[768,1024]{1,0:T(8,128)(2,1)S(1)} %copy-done, f32[256,1024]{1,0:T(8,128)S(1)} %get-tuple-element.32, f32[256]{0:T(256)S(1)} %copy-done.29), kind=kOutput, calls=%fused_computation.67 | convolution fusion | flops 419495680 | bytes 3805184 | tf_op jit(solution)/shard_map/transpose(jvp())/dot_general | solution.py:80
  65.3 2.5 %fusion.116 = (f32[256]{0:T(256)S(1)}, f32[256,768]{1,0:T(8,128)S(1)}) fusion(f32[256]{0:T(256)S(1)} %multiply_multiply_fusion.8, bf16[256,768]{1,0:T(8,128)(2,1)S(1)} %get-tuple-element.22, f32[256]{0:T(256)S(1)} %fusion.103, f32[256,768]{1,0:T(8,128)S(1)} %copy-done.4, f32[256]{0:T(256)S(1)} %broadcast_multiply_fusion.1), kind=kLoop, calls=%fused_computation.206 | loop fusion | flops 15531776 | bytes 1970176 | tf_op jit(solution)/shard_map/transpose(jvp())/reduce_sum | solution.py:21
  68.7 1.9 %copy.56 = bf16[256,768]{0,1:T(8,128)(2,1)} copy(bf16[256,768]{1,0:T(8,128)(2,1)} %broadcast_add_fusion) | data formatting | bytes 786432 | tf_op jit(solution)/shard_map/transpose(jvp())/add_any | solution.py:20
  70.6 1.3 %fusion.5 = bf16[256,16,48]{0,2,1:T(8,128)(2,1)S(1)} fusion(bf16[16,48,256]{2,1,0:T(8,128)(2,1)} %bitcast.139, bf16[3,16,48,48]{3,2,1,0:T(8,128)(2,1)} %param.16), kind=kOutput, calls=%fused_computation.18 | convolution fusion | flops 18874368 | bytes 983040 | tf_op jit(solution)/shard_map/transpose(jvp(pgi,gio->pgo))/dot_general | solution.py:72
  72.0 1.3 %fusion.4 = bf16[256,16,48]{0,2,1:T(8,128)(2,1)S(1)} fusion(bf16[16,48,256]{2,1,0:T(8,128)(2,1)} %bitcast.140, bf16[3,16,48,48]{3,2,1,0:T(8,128)(2,1)} %param.16), kind=kOutput, calls=%fused_computation.17 | convolution fusion | flops 18874368 | bytes 983040 | tf_op jit(solution)/shard_map/transpose(jvp(pgi,gio->pgo))/dot_general | solution.py:72
  73.3 1.2 %fusion.3 = bf16[256,16,48]{0,2,1:T(8,128)(2,1)S(1)} fusion(bf16[16,48,256]{2,1,0:T(8,128)(2,1)S(1)} %bitcast.141, bf16[3,16,48,48]{3,2,1,0:T(8,128)(2,1)} %param.16), kind=kOutput, calls=%fused_computation.16 | convolution fusion | flops 18874368 | bytes 983040 | tf_op jit(solution)/shard_map/transpose(jvp(pgi,gio->pgo))/dot_general | solution.py:72
  74.5 1.1 %pad_add_fusion.1 = bf16[256,16,48]{0,2,1:T(8,128)(2,1)} fusion(bf16[256,16,48]{0,2,1:T(8,128)(2,1)S(1)} %fusion.5, bf16[256,16,48]{0,2,1:T(8,128)(2,1)S(1)} %fusion.4, bf16[256,16,48]{0,2,1:T(8,128)(2,1)S(1)} %fusion.3), kind=kLoop, calls=%fused_computation.108 | loop fusion | flops 1179648 | bytes 1572864 | tf_op jit(solution)/shard_map/transpose(jvp())/add_any | solution.py:74
  75.6 1.9 %copy.60 = bf16[256,768]{1,0:T(8,128)(2,1)} copy(bf16[256,768]{0,1:T(8,128)(2,1)} %bitcast.145) | data formatting | bytes 786432 | tf_op jit(solution)/shard_map/transpose(jvp())/reshape | solution.py:68
  77.5 2.5 %convolution_convert_fusion.11 = bf16[51,1024]{1,0:T(8,128)(2,1)} fusion(bf16[1024,768]{1,0:T(8,128)(2,1)S(1)} %copy-done.1, bf16[256,768]{1,0:T(8,128)(2,1)} %copy-done.7, bf16[256,768]{1,0:T(8,128)(2,1)} %copy.60, pred[256]{0:T(512)(128)(4,1)S(1)} %copy-done.33, s32[51]{0:T(128)S(1)} %copy-done.32), kind=kOutput, calls=%fused_computation.36 | convolution fusion | flops 100964352 | bytes 2464204 | tf_op jit(solution)/shard_map/transpose(jvp())/dot_general | solution.py:60
  80.0 2.5 %convolution_convert_fusion.12 = bf16[51,1024]{1,0:T(8,128)(2,1)S(1)} fusion(bf16[51,1024]{1,0:T(8,128)(2,1)} %convolution_convert_fusion.11, bf16[1024,1024]{1,0:T(8,128)(2,1)} %w_out_ref.1), kind=kOutput, calls=%fused_computation.38 | convolution fusion | flops 107006976 | bytes 2306048 | tf_op jit(solution)/shard_map/transpose(jvp())/dot_general | solution.py:53
  86.7 5.0 %fusion.69 = (f32[51]{0:T(128)S(1)}, f32[51,1024]{1,0:T(8,128)S(1)}) fusion(bf16[51,1024]{1,0:T(8,128)(2,1)S(1)} %gather_fusion.2, f32[51]{0:T(128)S(1)} %copy-done.24, bf16[51,3072]{1,0:T(8,128)(2,1)S(1)} %reshape.260, bf16[1024,3072]{1,0:T(8,128)(2,1)} %w_qkv_ref.1), kind=kOutput, calls=%fused_computation.128 | convolution fusion | flops 321177536 | bytes 6918552 | tf_op jit(solution)/shard_map/transpose(jvp())/dot_general | solution.py:51
  93.2 1.9 %collective-permute-start.3 = (bf16[51,1024]{1,0:T(8,128)(2,1)S(1)}, bf16[51,1024]{1,0:T(8,128)(2,1)S(1)}, u32[]{:S(2)}, u32[]{:S(2)}) collective-permute-start(bf16[51,1024]{1,0:T(8,128)(2,1)S(1)} %fusion.92), channel_id=1, source_target_pairs={{0,3},{1,0},{2,1},{3,2},{4,7},{5,4},{6,5},{7,6},{8,11},{9,8},{10,9... | collective-permute-start | bytes 313352 | tf_op jit(solution)/shard_map/ppermute | solution.py:164
  96.2 1.2 %gather_fusion.1 = bf16[204,192]{1,0:T(8,128)(2,1)S(1)} fusion(bf16[256,192]{1,0:T(8,128)(2,1)S(1)} %constant_dynamic-slice_fusion.1, s32[1024]{0:T(1024)} %pad_clamp_fusion.1), kind=kCustom, calls=%fused_computation.1 | custom fusion | bytes 157488 | tf_op jit(solution)/shard_map/gather | solution.py:232
  98.9 1.2 %fusion.44 = f32[192,1024]{1,0:T(8,128)} fusion(bf16[204,192]{1,0:T(8,128)(2,1)S(1)} %gather_fusion.1, bf16[51,1024]{1,0:T(8,128)(2,1)S(1)} %collective-permute-done.5, bf16[51,1024]{1,0:T(8,128)(2,1)S(1)} %collective-permute-done.4, bf16[51,1024]{1,0:T(8,128)(2,1)S(1)} %collective-permute-done.3, bf16[51,1024]{1,0:T(8,128)(2,1)S(1)} %fusion.92), kind=kOutput, calls=%fused_computation.99 | convolution fusion | flops 81887232 | bytes 1282560 | tf_op jit(solution)/shard_map/vc,vd->cd/dot_general | solution.py:233
  (131 shorter events, 19.6 us)
Async XLA Ops:
  0.6 56.8 %copy-start = (bf16[768,1024]{1,0:T(8,128)(2,1)S(1)}, bf16[768,1024]{1,0:T(8,128)(2,1)}, u32[]{:S(2)}) copy-start(bf16[768,1024]{1,0:T(8,128)(2,1)} %param.17) | copy-start | bytes 4718596
  0.6 14.0 %copy-start.14 = (bf16[64,768]{1,0:T(8,128)(2,1)S(1)}, bf16[64,768]{1,0:T(8,128)(2,1)}, u32[]{:S(2)}) copy-start(bf16[64,768]{1,0:T(8,128)(2,1)} %param.9) | copy-start | bytes 294916
  0.7 13.9 %collective-permute-start = (bf16[64,768]{1,0:T(8,128)(2,1)}, bf16[64,768]{1,0:T(8,128)(2,1)S(1)}, u32[]{:S(2)}, u32[]{:S(2)}) collective-permute-start(bf16[64,768]{1,0:T(8,128)(2,1)} %param.9), channel_id=1, source_target_pairs={{0,1},{1,2},{2,3},{3,0},{4,5},{5,6},{6,7},{7,4},{8,9},{9,10},{10,1... | collective-permute-start | bytes 294920 | tf_op jit(solution)/shard_map/ppermute | solution.py:164
  3.7 10.9 %collective-permute-start.1 = (bf16[64,768]{1,0:T(8,128)(2,1)}, bf16[64,768]{1,0:T(8,128)(2,1)S(1)}, u32[]{:S(2)}, u32[]{:S(2)}) collective-permute-start(bf16[64,768]{1,0:T(8,128)(2,1)} %param.9), channel_id=1, source_target_pairs={{0,2},{1,3},{2,0},{3,1},{4,6},{5,7},{6,4},{7,5},{8,10},{9,11},{10,... | collective-permute-start | bytes 294920 | tf_op jit(solution)/shard_map/ppermute | solution.py:164
  5.2 9.4 %collective-permute-start.2 = (bf16[64,768]{1,0:T(8,128)(2,1)}, bf16[64,768]{1,0:T(8,128)(2,1)S(1)}, u32[]{:S(2)}, u32[]{:S(2)}) collective-permute-start(bf16[64,768]{1,0:T(8,128)(2,1)} %param.9), channel_id=1, source_target_pairs={{0,3},{1,0},{2,1},{3,2},{4,7},{5,4},{6,5},{7,6},{8,11},{9,8},{10,9... | collective-permute-start | bytes 294920 | tf_op jit(solution)/shard_map/ppermute | solution.py:164
  30.9 0.8 copy-start.23
  36.7 3.3 %copy-start.9 = (bf16[51,1,16,64]{3,2,1,0:T(8,128)(2,1)}, bf16[51,1,16,64]{3,2,1,0:T(8,128)(2,1)S(1)}, u32[]{:S(2)}) copy-start(bf16[51,1,16,64]{3,2,1,0:T(8,128)(2,1)S(1)} %get-tuple-element.9) | copy-start | bytes 313348
  38.8 0.8 copy-start.11
  38.9 1.2 %copy-start.25 = (f32[16,51]{1,0:T(8,128)}, f32[16,51]{1,0:T(8,128)S(1)}, u32[]{:S(2)}) copy-start(f32[16,51]{1,0:T(8,128)S(1)} %get-tuple-element.17) | copy-start | bytes 9796
  38.9 3.6 %copy-start.1 = (bf16[1024,768]{1,0:T(8,128)(2,1)S(1)}, bf16[1024,768]{1,0:T(8,128)(2,1)}, u32[]{:S(2)}) copy-start(bf16[1024,768]{1,0:T(8,128)(2,1)} %param.15) | copy-start | bytes 4718596
  48.8 1.5 %copy-start.3 = (bf16[256,768]{0,1:T(8,128)(2,1)S(1)}, bf16[256,768]{0,1:T(8,128)(2,1)}, u32[]{:S(2)}) copy-start(bf16[256,768]{0,1:T(8,128)(2,1)} %copy.51) | copy-start | bytes 1179652
  53.8 3.6 %copy-start.30 = (f32[256]{0:T(256)S(1)}, f32[256]{0:T(256)}, u32[]{:S(2)}) copy-start(f32[256]{0:T(256)} %get-tuple-element.16) | copy-start | bytes 3076
  57.4 4.5 %copy-start.4 = (f32[256,768]{1,0:T(8,128)S(1)}, f32[256,768]{1,0:T(8,128)}, u32[]{:S(2)}) copy-start(f32[256,768]{1,0:T(8,128)} %copy.55) | copy-start | bytes 2359300
  57.4 4.5 %copy-start.29 = (f32[256]{0:T(256)S(1)}, f32[256]{0:T(256)}, u32[]{:S(2)}) copy-start(f32[256]{0:T(256)} %get-tuple-element.15) | copy-start | bytes 3076
  65.2 2.6 %copy-start.7 = (bf16[256,768]{1,0:T(8,128)(2,1)}, bf16[256,768]{1,0:T(8,128)(2,1)S(1)}, u32[]{:S(2)}) copy-start(bf16[256,768]{1,0:T(8,128)(2,1)S(1)} %get-tuple-element.22) | copy-start | bytes 1179652
  70.6 2.6 %copy-start.2 = (bf16[256,768]{0,1:T(8,128)(2,1)S(1)}, bf16[256,768]{0,1:T(8,128)(2,1)}, u32[]{:S(2)}) copy-start(bf16[256,768]{0,1:T(8,128)(2,1)} %copy.56) | copy-start | bytes 1179652
  70.6 3.8 %copy-start.26 = (f32[16,51]{1,0:T(8,128)S(1)}, f32[16,51]{1,0:T(8,128)}, u32[]{:S(2)}) copy-start(f32[16,51]{1,0:T(8,128)} %copy-done.25) | copy-start | bytes 9796
  73.3 4.2 %copy-start.32 = (s32[51]{0:T(128)S(1)}, s32[51]{0:T(128)}, u32[]{:S(2)}) copy-start(s32[51]{0:T(128)} %copy-done.31) | copy-start | bytes 616
  73.3 4.2 %copy-start.33 = (pred[256]{0:T(512)(128)(4,1)S(1)}, pred[256]{0:T(512)(128)(4,1)}, u32[]{:S(2)}) copy-start(pred[256]{0:T(512)(128)(4,1)} %broadcast_compare_fusion) | copy-start | bytes 772
  80.0 2.7 %copy-start.10 = (bf16[51,1,16,64]{3,2,1,0:T(8,128)(2,1)S(1)}, bf16[51,1,16,64]{3,2,1,0:T(8,128)(2,1)}, u32[]{:S(2)}) copy-start(bf16[51,1,16,64]{3,2,1,0:T(8,128)(2,1)} %copy-done.9) | copy-start | bytes 313348
  80.0 2.7 %copy-start.12 = (f32[16,51,51]{1,2,0:T(8,128)S(1)}, f32[16,51,51]{1,2,0:T(8,128)}, u32[]{:S(2)}) copy-start(f32[16,51,51]{1,2,0:T(8,128)} %copy-done.11) | copy-start | bytes 499396
  80.0 3.0 %copy-start.6 = (bf16[51,1,16,64]{3,2,1,0:T(8,128)(2,1)S(1)}, bf16[51,1,16,64]{3,2,1,0:T(8,128)(2,1)}, u32[]{:S(2)}) copy-start(bf16[51,1,16,64]{3,2,1,0:T(8,128)(2,1)} %copy-done.5) | copy-start | bytes 313348
  80.0 3.0 %copy-start.20 = (f32[51,16]{0,1:T(8,128)S(1)}, f32[51,16]{0,1:T(8,128)}, u32[]{:S(2)}) copy-start(f32[51,16]{0,1:T(8,128)} %copy-done.19) | copy-start | bytes 9796
  83.0 1.0 %copy-start.13 = (f32[16,51,51]{1,2,0:T(8,128)S(1)}, f32[16,51,51]{1,2,0:T(8,128)}, u32[]{:S(2)}) copy-start(f32[16,51,51]{1,2,0:T(8,128)} %copy-done.11) | copy-start | bytes 499396
  83.0 1.0 %copy-start.22 = (f32[51,16]{0,1:T(8,128)S(1)}, f32[51,16]{0,1:T(8,128)}, u32[]{:S(2)}) copy-start(f32[51,16]{0,1:T(8,128)} %copy-done.21) | copy-start | bytes 9796
  85.9 0.8 copy-start.24
  86.6 5.0 %copy-start.35 = (f32[51]{0:T(128)S(1)}, f32[51]{0:T(128)}, u32[]{:S(2)}) copy-start(f32[51]{0:T(128)} %copy-done.34) | copy-start | bytes 616
  86.6 5.0 %copy-start.28 = (f32[51]{0:T(128)S(1)}, f32[51]{0:T(128)}, u32[]{:S(2)}) copy-start(f32[51]{0:T(128)} %copy-done.27) | copy-start | bytes 616
  86.7 5.3 %copy-start.8 = (bf16[51,1024]{1,0:T(8,128)(2,1)S(1)}, bf16[51,1024]{1,0:T(8,128)(2,1)}, u32[]{:S(2)}) copy-start(bf16[51,1024]{1,0:T(8,128)(2,1)} %convolution_convert_fusion.11) | copy-start | bytes 313348
  92.1 6.4 %collective-permute-start.5 = (bf16[51,1024]{1,0:T(8,128)(2,1)S(1)}, bf16[51,1024]{1,0:T(8,128)(2,1)S(1)}, u32[]{:S(2)}, u32[]{:S(2)}) collective-permute-start(bf16[51,1024]{1,0:T(8,128)(2,1)S(1)} %fusion.92), channel_id=1, source_target_pairs={{0,1},{1,2},{2,3},{3,0},{4,5},{5,6},{6,7},{7,4},{8,9},{9,10},{10,1... | collective-permute-start | bytes 313352 | tf_op jit(solution)/shard_map/ppermute | solution.py:164
  92.7 6.2 %collective-permute-start.4 = (bf16[51,1024]{1,0:T(8,128)(2,1)S(1)}, bf16[51,1024]{1,0:T(8,128)(2,1)S(1)}, u32[]{:S(2)}, u32[]{:S(2)}) collective-permute-start(bf16[51,1024]{1,0:T(8,128)(2,1)S(1)} %fusion.92), channel_id=1, source_target_pairs={{0,2},{1,3},{2,0},{3,1},{4,6},{5,7},{6,4},{7,5},{8,10},{9,11},{10,... | collective-permute-start | bytes 313352 | tf_op jit(solution)/shard_map/ppermute | solution.py:164
  93.2 5.7 %collective-permute-start.3 = (bf16[51,1024]{1,0:T(8,128)(2,1)S(1)}, bf16[51,1024]{1,0:T(8,128)(2,1)S(1)}, u32[]{:S(2)}, u32[]{:S(2)}) collective-permute-start(bf16[51,1024]{1,0:T(8,128)(2,1)S(1)} %fusion.92), channel_id=1, source_target_pairs={{0,3},{1,0},{2,1},{3,2},{4,7},{5,4},{6,5},{7,6},{8,11},{9,8},{10,9... | collective-permute-start | bytes 313352 | tf_op jit(solution)/shard_map/ppermute | solution.py:164
  (10 other events, 6.1 us)

commit v9 on v4

--- a/solution.py
+++ b/solution.py
@@ -3,6 +3,8 @@
 import jax
 import jax.numpy as jnp
 from jax import lax
+from jax.experimental import pallas as pl
+from jax.experimental.pallas import tpu as pltpu
 from jax.sharding import PartitionSpec as P
 
 D = 1024
@@ -92,6 +94,87 @@
     return jnp.sum(mismatch * mismatch)
 
 
+def teacher_kernel(embedded_ref, q_ref, k_ref, v_ref, w_out_ref, targets_ref, normed_ref, acc_ref):
+    pair = pl.program_id(0)
+    rows = embedded_ref.shape[0]
+    head_dim = D // HEADS
+
+    @pl.when(pair == 0)
+    def _():
+        values = embedded_ref[...].astype(jnp.float32)
+        average = jnp.mean(values, axis=-1, keepdims=True)
+        centred = values - average
+        spread = jnp.mean(centred * centred, axis=-1, keepdims=True)
+        normed_ref[...] = (centred * lax.rsqrt(spread + EPSILON)).astype(jnp.bfloat16)
+
+    normed = normed_ref[...]
+    lane = lax.broadcasted_iota(jnp.int32, (rows, 2 * head_dim), 1)
+    first = lane < head_dim
+    score_scale = 1.0 / math.sqrt(head_dim)
+
+    def pair_norm(block):
+        squares = block * block
+        low = jnp.sum(jnp.where(first, squares, 0.0), axis=-1, keepdims=True) / head_dim
+        high = jnp.sum(jnp.where(first, 0.0, squares), axis=-1, keepdims=True) / head_dim
+        scale = jnp.where(first, lax.rsqrt(low + EPSILON), lax.rsqrt(high + EPSILON))
+        return (block * scale).astype(jnp.bfloat16)
+
+    def project(w_ref):
+        return jnp.dot(normed, w_ref[...], preferred_element_type=jnp.float32).astype(jnp.bfloat16)
+
+    queries = pair_norm(project(q_ref).astype(jnp.float32))
+    key_rows = pair_norm(project(k_ref).astype(jnp.float32))
+    v_block = project(v_ref)
+    zero = jnp.zeros_like(queries)
+    mixed = []
+    for half in range(2):
+        chosen = first if half == 0 else jnp.logical_not(first)
+        scores = lax.dot_general(
+            jnp.where(chosen, queries, zero), key_rows,
+            (((1,), (1,)), ((), ())), preferred_element_type=jnp.float32) * score_scale
+        exponent = jnp.exp(scores)
+        weights = (exponent / jnp.sum(exponent, axis=-1, keepdims=True)).astype(jnp.bfloat16)
+        mixed.append(jnp.dot(weights, v_block, preferred_element_type=jnp.float32))
+    context = jnp.where(first, mixed[0], mixed[1]).astype(jnp.bfloat16)
+    part = jnp.dot(context, w_out_ref[...], preferred_element_type=jnp.float32)
+
+    @pl.when(pair == 0)
+    def _():
+        acc_ref[...] = part
+
+    @pl.when(pair > 0)
+    def _():
+        acc_ref[...] += part
+
+    @pl.when(pair == pl.num_programs(0) - 1)
+    def _():
+        branch = acc_ref[...]
+        average = jnp.mean(branch, axis=-1, keepdims=True)
+        centred = branch - average
+        spread = jnp.mean(centred * centred, axis=-1, keepdims=True)
+        targets_ref[...] = (centred * lax.rsqrt(spread + EPSILON)).astype(jnp.bfloat16)
+
+
+def teacher(embedded, w_qkv, w_out):
+    rows = embedded.shape[0]
+    width = 2 * (D // HEADS)
+    pairs = HEADS // 2
+    return pl.pallas_call(
+        teacher_kernel,
+        grid=(pairs,),
+        in_specs=[
+            pl.BlockSpec((rows, D), lambda p: (0, 0)),
+            pl.BlockSpec((D, width), lambda p: (0, p)),
+            pl.BlockSpec((D, width), lambda p: (0, pairs + p)),
+            pl.BlockSpec((D, width), lambda p: (0, 2 * pairs + p)),
+            pl.BlockSpec((width, D), lambda p: (p, 0)),
+        ],
+        out_specs=pl.BlockSpec((rows, D), lambda p: (0, 0)),
+        out_shape=jax.ShapeDtypeStruct((rows, D), jnp.bfloat16),
+        scratch_shapes=[pltpu.VMEM((rows, D), jnp.bfloat16), pltpu.VMEM((rows, D), jnp.float32)],
+    )(embedded, w_qkv, w_qkv, w_qkv, w_out)
+
+
 def ring_gather(values, group_size):
     parts = [values]
     for shift in range(1, group_size):
@@ -146,11 +229,11 @@
         jnp.bfloat16
     )
     visible_in = embedded[positions]
-    if HEADS * total_rows * total_rows * 4 <= (1 << 24):
-        branch = attention_branch(embedded, w_qkv, w_out)
+    if total_rows <= 256:
+        all_targets = teacher(embedded, w_qkv, w_out)
     else:
         branch = split_teacher(embedded, w_qkv, w_out, own_index, group_size)
-    all_targets = row_norm(branch).astype(jnp.bfloat16)
+        all_targets = row_norm(branch).astype(jnp.bfloat16)
 
     def objective(rows_in):
         return copy_terms(

time: 87.3 us -> 99.7 us (1.14)
  Pallas kernels: 0 us -> 13.7 us
  local copies, waits for them, and re-layouts: 13.3 us -> 19.4 us
  matrix products: 47.3 us -> 41.4 us
  waiting for transfers between devices: 3.77 us -> 0.96 us
    pallas_call x0 -> x1, Pallas kernels: none -> 13.7 us  [teacher(): pl.pallas_call(teacher_kernel, grid=(pairs,), in_specs=[pl.BlockSpec((row...]
    dot_general x3 -> x2, matrix products: 14.8 us -> 8.98 us  [attention_branch(): jnp.dot(normed, w_qkv, preferred_element_type=jnp.float32)]
    dot_general x6, matrix products: 4.61 us -> 8.77 us  [decoder_output(): jnp.einsum('pgi,gio->pgo', padded[offset:offset + total_rows], conv_w[off...]
    dot_general x4 -> x3, matrix products: 3.88 us -> 0.89 us  [mix_heads(): jnp.einsum('hqk,khd->qhd', weights, values, preferred_element_type=jnp.fl...]
    ppermute x6, waiting for transfers between devices: 3.77 us -> 0.96 us  [ring_gather(): parts.append(lax.ppermute(values, 'mask', pairs))]
    convert_element_type x1 -> x0, local copies, waits for them, and re-layouts: 2.59 us -> none  [attention_branch(): jnp.dot(normed, w_qkv, preferred_element_type=jnp.float32)]
    dot_general x4 -> x3, matrix products: 3.71 us -> 1.53 us  [mix_heads(): jnp.einsum('qhd,khd->hqk', queries, key_rows, preferred_element_type=jnp....]
    reshape x1, local copies, waits for them, and re-layouts: 0.17 us -> 1.92 us  [decoder_output(): grouped = lowered.reshape(total_rows, GROUPS, DD // GROUPS)]
  transfers between devices with their start and end apart: 6 -> 6, of which waited for: 3 -> 2; matrix products, arithmetic and copies ran while one was open for 8% -> 10% of each run, Pallas kernels for 0% -> 0%
where the time goes in v9:
time: 99.7 us; the launch traced here: 98.9 us
  matrix products  41.4 us (42%)
  local copies, waits for them, and re-layouts  19.4 us (19%)
  Pallas kernels  13.7 us (14%)
  other arithmetic  11.3 us (11%)
  starting transfers between devices  9.05 us (9%)
  between operations  3.05 us (3%)
    pallas_call x1, Pallas kernels, teacher(): pl.pallas_call(teacher_kernel, grid=(pairs,), in_specs=[pl.BlockSpec((row...  13.7 us
    ppermute x6, starting transfers between devices, ring_gather(): parts.append(lax.ppermute(values, 'mask', pairs))  9.05 us
    dot_general x2, matrix products, attention_branch(): jnp.dot(normed, w_qkv, preferred_element_type=jnp.float32)  8.98 us
    dot_general x6, matrix products, decoder_output(): jnp.einsum('pgi,gio->pgo', padded[offset:offset + total_rows], conv_w[off...  8.77 us
    dot_general x2, matrix products, decoder_output(): return jnp.dot(hidden, dec_out, preferred_element_type=jnp.float32)  7.83 us
    dot_general x2, matrix products, decoder_output(): jnp.dot(visible_out, dec_in, preferred_element_type=jnp.float32)  4.97 us
    unnamed x77, local copies, waits for them, and re-layouts  4.36 us
    reduce_sum x2, other arithmetic, row_norm(): centred = values - average  2.98 us
  transfers between devices with their start and end apart: 6, of which 2 were waited for; matrix products, arithmetic and copies ran while one was open for 10% of the time, Pallas kernels for 0%

profile of v9, /device:TPU:0, one launch (start us, length us, event | category | flops | bytes accessed | tf_op | source)
XLA Modules:
  0.0 98.9 jit_solution(17545450232015528347)
XLA Ops:
  0.7 3.0 %collective-permute-start = (bf16[64,768]{1,0:T(8,128)(2,1)}, bf16[64,768]{1,0:T(8,128)(2,1)S(1)}, u32[]{:S(2)}, u32[]{:S(2)}) collective-permute-start(bf16[64,768]{1,0:T(8,128)(2,1)} %param.9), channel_id=1, source_target_pairs={{0,1},{1,2},{2,3},{3,0},{4,5},{5,6},{6,7},{7,4},{8,9},{9,10},{10,1... | collective-permute-start | bytes 294920 | tf_op jit(solution)/shard_map/ppermute | solution.py:182
  3.7 1.5 %collective-permute-start.1 = (bf16[64,768]{1,0:T(8,128)(2,1)}, bf16[64,768]{1,0:T(8,128)(2,1)S(1)}, u32[]{:S(2)}, u32[]{:S(2)}) collective-permute-start(bf16[64,768]{1,0:T(8,128)(2,1)} %param.9), channel_id=1, source_target_pairs={{0,2},{1,3},{2,0},{3,1},{4,6},{5,7},{6,4},{7,5},{8,10},{9,11},{10,... | collective-permute-start | bytes 294920 | tf_op jit(solution)/shard_map/ppermute | solution.py:182
  5.2 1.4 %collective-permute-start.2 = (bf16[64,768]{1,0:T(8,128)(2,1)}, bf16[64,768]{1,0:T(8,128)(2,1)S(1)}, u32[]{:S(2)}, u32[]{:S(2)}) collective-permute-start(bf16[64,768]{1,0:T(8,128)(2,1)} %param.9), channel_id=1, source_target_pairs={{0,3},{1,0},{2,1},{3,2},{4,7},{5,4},{6,5},{7,6},{8,11},{9,8},{10,9... | collective-permute-start | bytes 294920 | tf_op jit(solution)/shard_map/ppermute | solution.py:182
  8.6 1.2 %gather_fusion = s32[4,51]{1,0:T(4,128)S(1)} fusion(s32[4,51]{1,0:T(4,128)} %param.10, s32[1024]{0:T(1024)S(1)} %pad_clamp_fusion.2), kind=kCustom, calls=%fused_computation | custom fusion | bytes 1648 | tf_op jit(solution)/shard_map/gather | solution.py:248
  12.3 2.4 %convolution_reduce_fusion = bf16[768]{0:T(1024)(128)(2,1)} fusion(bf16[1024,1]{0,1:T(2,128)(2,1)S(1)} %reshape.288, bf16[1024,768]{1,0:T(8,128)(2,1)} %param.15), kind=kOutput, calls=%fused_computation.42 | convolution fusion | flops 1572864 | bytes 1576448 | tf_op jit(solution)/shard_map/jvp()/dot_general | solution.py:63
  18.2 4.0 %convolution_convert_fusion = bf16[51,3072]{1,0:T(8,128)(2,1)S(1)} fusion(bf16[1024,3072]{1,0:T(8,128)(2,1)} %v_ref.1, bf16[51,1024]{1,0:T(8,128)(2,1)S(1)} %gather_fusion.2, f32[51]{0:T(128)S(1)} %fusion.107, f32[51]{0:T(128)S(1)} %broadcast_multiply_fusion.2), kind=kOutput, calls=%fused_computation.3 | convolution fusion | flops 321229824 | bytes 6709656 | tf_op jit(solution)/shard_map/jvp()/dot_general | solution.py:51
  26.3 13.7 %shard_map.104 = bf16[256,1024]{1,0:T(8,128)(2,1)} custom-call(bf16[256,1024]{1,0:T(8,128)(2,1)} %copy-done.4, bf16[1024,3072]{1,0:T(8,128)(2,1)} %v_ref.1, bf16[1024,3072]{1,0:T(8,128)(2,1)} %v_ref.1, bf16[1024,3072]{1,0:T(8,128)(2,1)} %v_ref.1, bf16[1024,1024]{1,0:T(8,128)(2,1)} %w_out_ref.1), custom_call_target="tpu_custom_call" | custom-call | tf_op jit(solution)/shard_map/pallas_call | solution.py:162
  40.0 2.5 %convolution_convert_fusion.15 = bf16[51,768]{1,0:T(8,128)(2,1)S(1)} fusion(bf16[1024,768]{1,0:T(8,128)(2,1)S(1)} %copy-done.1, bf16[51,1024]{1,0:T(8,128)(2,1)} %reshape.254, bf16[1024,1024]{1,0:T(8,128)(2,1)} %w_out_ref.1, bf16[51,1024]{1,0:T(8,128)(2,1)S(1)} %gather_fusion.2), kind=kOutput, calls=%fused_computation.41 | convolution fusion | flops 187366656 | bytes 3957248 | tf_op jit(solution)/shard_map/jvp()/dot_general | solution.py:60
  42.5 1.8 %fusion.1 = bf16[256,768]{1,0:T(8,128)(2,1)} fusion(bf16[51,768]{1,0:T(8,128)(2,1)S(1)} %convolution_convert_fusion.15, bf16[768]{0:T(1024)(128)(2,1)} %convolution_reduce_fusion, pred[256]{0:T(512)(128)(4,1)} %broadcast_compare_fusion, s32[51]{0:T(128)} %copy-done.32), kind=kOutput, calls=%fused_computation.10 | convolution fusion | flops 20263680 | bytes 473548 | tf_op jit(solution)/shard_map/jvp()/dot_general | solution.py:66
  44.3 1.9 %copy.51 = bf16[256,768]{0,1:T(8,128)(2,1)} copy(bf16[256,768]{1,0:T(8,128)(2,1)} %fusion.1) | data formatting | bytes 786432 | tf_op jit(solution)/shard_map/jvp()/convert_element_type | solution.py:67
  46.2 1.5 %fusion.52 = f32[16,256,48]{1,2,0:T(8,128)S(1)} fusion(bf16[256,16,48]{0,2,1:T(8,128)(2,1)} %bitcast.143, bf16[3,16,48,48]{3,2,1,0:T(8,128)(2,1)} %param.16), kind=kOutput, calls=%fused_computation.108 | convolution fusion | flops 18874368 | bytes 1376256 | tf_op jit(solution)/shard_map/jvp(pgi,gio->pgo)/dot_general | solution.py:72
  47.7 1.2 %convolution_add_fusion.1 = f32[16,256,48]{1,2,0:T(8,128)S(1)} fusion(f32[16,256,48]{1,2,0:T(8,128)S(1)} %fusion.52, bf16[256,16,48]{0,2,1:T(8,128)(2,1)S(1)} %bitcast.144, bf16[3,16,48,48]{3,2,1,0:T(8,128)(2,1)} %param.16), kind=kOutput, calls=%fused_computation.7 | convolution fusion | flops 19070976 | bytes 2162688 | tf_op jit(solution)/shard_map/jvp(pgi,gio->pgo)/dot_general | solution.py:72
  49.0 2.2 %fusion.119 = (f32[256]{0:T(256)S(1)}, f32[16,256,48]{1,2,0:T(8,128)}) fusion(f32[16,256,48]{1,2,0:T(8,128)S(1)} %convolution_add_fusion.1, bf16[256,16,48]{0,2,1:T(8,128)(2,1)S(1)} %bitcast.145, bf16[3,16,48,48]{3,2,1,0:T(8,128)(2,1)} %param.16), kind=kOutput, calls=%fused_computation.210 | convolution fusion | flops 19267328 | bytes 2163712 | tf_op jit(solution)/shard_map/jvp(pgi,gio->pgo)/dot_general | solution.py:72
  51.2 2.3 %copy.55 = f32[256,768]{1,0:T(8,128)} copy(f32[256,768]{0,1:T(8,128)} %bitcast.139) | data formatting | bytes 1572864 | tf_op jit(solution)/shard_map/jvp()/reshape | solution.py:78
  53.5 1.3 %fusion.25 = f32[256]{0:T(256)S(1)} fusion(f32[16,256,48]{1,2,0:T(8,128)} %get-tuple-element.16, f32[256]{0:T(256)S(1)} %broadcast_multiply_fusion.1), kind=kLoop, calls=%fused_computation.65 | loop fusion | flops 589568 | bytes 788480 | tf_op jit(solution)/shard_map/jvp()/reduce_sum | solution.py:22
  54.8 4.6 %multiply_reduce_fusion = (f32[]{:T(128)}, f32[256,1024]{1,0:T(8,128)S(1)}) fusion(f32[256]{0:T(256)S(1)} %copy-done.31, bf16[256,1024]{1,0:T(8,128)(2,1)} %shard_map.104, bf16[768,1024]{1,0:T(8,128)(2,1)S(1)} %copy-done, bf16[256,768]{1,0:T(8,128)(2,1)} %fusion.1, f32[256,768]{1,0:T(8,128)} %copy.55, f32[256]{0:T(256)S(1)} %fusion.103, ...), kind=kOutput, calls=%fused_computation.45 | convolution fusion | flops 417923072 | bytes 4328452 | tf_op jit(solution)/shard_map/jvp()/dot_general | solution.py:80
  59.4 3.3 %multiply_reduce_fusion.1 = (f32[256]{0:T(256)S(1)}, bf16[256,768]{1,0:T(8,128)(2,1)S(1)}) fusion(f32[256,768]{1,0:T(8,128)S(1)} %copy-done.5, f32[256]{0:T(256)S(1)} %broadcast_multiply_fusion.1, f32[256]{0:T(256)S(1)} %fusion.103, bf16[768,1024]{1,0:T(8,128)(2,1)S(1)} %copy-done, f32[256,1024]{1,0:T(8,128)S(1)} %get-tuple-element.28, f32[256]{0:T(256)S(1)} %copy-done.30), kind=kOutput, calls=%fused_computation.68 | convolution fusion | flops 419495680 | bytes 3805184 | tf_op jit(solution)/shard_map/transpose(jvp())/dot_general | solution.py:80
  62.7 2.8 %fusion.116 = (f32[256]{0:T(256)S(1)}, f32[256,768]{1,0:T(8,128)S(1)}) fusion(f32[256]{0:T(256)S(1)} %multiply_multiply_fusion.8, bf16[256,768]{1,0:T(8,128)(2,1)S(1)} %get-tuple-element.18, f32[256]{0:T(256)S(1)} %fusion.103, f32[256,768]{1,0:T(8,128)S(1)} %copy-done.5, f32[256]{0:T(256)S(1)} %broadcast_multiply_fusion.1), kind=kLoop, calls=%fused_computation.207 | loop fusion | flops 15531776 | bytes 1970176 | tf_op jit(solution)/shard_map/transpose(jvp())/reduce_sum | solution.py:21
  65.5 0.9 broadcast_add_fusion
  66.3 1.9 %copy.56 = bf16[256,768]{0,1:T(8,128)(2,1)} copy(bf16[256,768]{1,0:T(8,128)(2,1)} %broadcast_add_fusion) | data formatting | bytes 786432 | tf_op jit(solution)/shard_map/transpose(jvp())/add_any | solution.py:20
  68.2 1.3 %fusion.5 = bf16[256,16,48]{0,2,1:T(8,128)(2,1)S(1)} fusion(bf16[16,48,256]{2,1,0:T(8,128)(2,1)} %bitcast.140, bf16[3,16,48,48]{3,2,1,0:T(8,128)(2,1)} %param.16), kind=kOutput, calls=%fused_computation.19 | convolution fusion | flops 18874368 | bytes 983040 | tf_op jit(solution)/shard_map/transpose(jvp(pgi,gio->pgo))/dot_general | solution.py:72
  69.6 1.3 %fusion.4 = bf16[256,16,48]{0,2,1:T(8,128)(2,1)S(1)} fusion(bf16[16,48,256]{2,1,0:T(8,128)(2,1)} %bitcast.141, bf16[3,16,48,48]{3,2,1,0:T(8,128)(2,1)} %param.16), kind=kOutput, calls=%fused_computation.18 | convolution fusion | flops 18874368 | bytes 983040 | tf_op jit(solution)/shard_map/transpose(jvp(pgi,gio->pgo))/dot_general | solution.py:72
  70.9 1.2 %fusion.3 = bf16[256,16,48]{0,2,1:T(8,128)(2,1)S(1)} fusion(bf16[16,48,256]{2,1,0:T(8,128)(2,1)S(1)} %bitcast.142, bf16[3,16,48,48]{3,2,1,0:T(8,128)(2,1)} %param.16), kind=kOutput, calls=%fused_computation.17 | convolution fusion | flops 18874368 | bytes 983040 | tf_op jit(solution)/shard_map/transpose(jvp(pgi,gio->pgo))/dot_general | solution.py:72
  72.1 1.1 %pad_add_fusion.1 = bf16[256,16,48]{0,2,1:T(8,128)(2,1)} fusion(bf16[256,16,48]{0,2,1:T(8,128)(2,1)S(1)} %fusion.5, bf16[256,16,48]{0,2,1:T(8,128)(2,1)S(1)} %fusion.4, bf16[256,16,48]{0,2,1:T(8,128)(2,1)S(1)} %fusion.3), kind=kLoop, calls=%fused_computation.109 | loop fusion | flops 1179648 | bytes 1572864 | tf_op jit(solution)/shard_map/transpose(jvp())/add_any | solution.py:74
  73.2 1.9 %copy.60 = bf16[256,768]{1,0:T(8,128)(2,1)} copy(bf16[256,768]{0,1:T(8,128)(2,1)} %bitcast.146) | data formatting | bytes 786432 | tf_op jit(solution)/shard_map/transpose(jvp())/reshape | solution.py:68
  75.1 2.5 %convolution_convert_fusion.12 = bf16[51,1024]{1,0:T(8,128)(2,1)} fusion(bf16[1024,768]{1,0:T(8,128)(2,1)S(1)} %copy-done.1, bf16[256,768]{1,0:T(8,128)(2,1)} %copy-done.8, bf16[256,768]{1,0:T(8,128)(2,1)} %copy.60, pred[256]{0:T(512)(128)(4,1)S(1)} %copy-done.36, s32[51]{0:T(128)S(1)} %copy-done.33), kind=kOutput, calls=%fused_computation.37 | convolution fusion | flops 100964352 | bytes 2464204 | tf_op jit(solution)/shard_map/transpose(jvp())/dot_general | solution.py:60
  77.6 2.5 %convolution_convert_fusion.13 = bf16[51,1024]{1,0:T(8,128)(2,1)S(1)} fusion(bf16[51,1024]{1,0:T(8,128)(2,1)} %convolution_convert_fusion.12, bf16[1024,1024]{1,0:T(8,128)(2,1)} %w_out_ref.1), kind=kOutput, calls=%fused_computation.39 | convolution fusion | flops 107006976 | bytes 2306048 | tf_op jit(solution)/shard_map/transpose(jvp())/dot_general | solution.py:53
  84.3 5.0 %fusion.69 = (f32[51]{0:T(128)S(1)}, f32[51,1024]{1,0:T(8,128)S(1)}) fusion(bf16[51,1024]{1,0:T(8,128)(2,1)S(1)} %gather_fusion.2, f32[51]{0:T(128)S(1)} %copy-done.25, bf16[51,3072]{1,0:T(8,128)(2,1)S(1)} %reshape.260, bf16[1024,3072]{1,0:T(8,128)(2,1)} %v_ref.1), kind=kOutput, calls=%fused_computation.129 | convolution fusion | flops 321177536 | bytes 6918552 | tf_op jit(solution)/shard_map/transpose(jvp())/dot_general | solution.py:51
  90.8 1.9 %collective-permute-start.3 = (bf16[51,1024]{1,0:T(8,128)(2,1)S(1)}, bf16[51,1024]{1,0:T(8,128)(2,1)S(1)}, u32[]{:S(2)}, u32[]{:S(2)}) collective-permute-start(bf16[51,1024]{1,0:T(8,128)(2,1)S(1)} %fusion.92), channel_id=1, source_target_pairs={{0,3},{1,0},{2,1},{3,2},{4,7},{5,4},{6,5},{7,6},{8,11},{9,8},{10,9... | collective-permute-start | bytes 313352 | tf_op jit(solution)/shard_map/ppermute | solution.py:182
  92.8 1.0 %constant_dynamic-slice_fusion.1 = bf16[256,192]{1,0:T(8,128)(2,1)S(1)} fusion(bf16[256,768]{1,0:T(8,128)(2,1)} %pad_maximum_fusion, s32[]{:T(128)S(6)} %select_n.179), kind=kLoop, calls=%fused_computation.196 | loop fusion | bytes 196612 | tf_op jit(solution)/shard_map/dynamic_slice | solution.py:249
  93.8 1.2 %gather_fusion.1 = bf16[204,192]{1,0:T(8,128)(2,1)S(1)} fusion(bf16[256,192]{1,0:T(8,128)(2,1)S(1)} %constant_dynamic-slice_fusion.1, s32[1024]{0:T(1024)} %pad_clamp_fusion.1), kind=kCustom, calls=%fused_computation.1 | custom fusion | bytes 157488 | tf_op jit(solution)/shard_map/gather | solution.py:250
  96.5 1.2 %fusion.44 = f32[192,1024]{1,0:T(8,128)} fusion(bf16[204,192]{1,0:T(8,128)(2,1)S(1)} %gather_fusion.1, bf16[51,1024]{1,0:T(8,128)(2,1)S(1)} %collective-permute-done.5, bf16[51,1024]{1,0:T(8,128)(2,1)S(1)} %collective-permute-done.4, bf16[51,1024]{1,0:T(8,128)(2,1)S(1)} %collective-permute-done.3, bf16[51,1024]{1,0:T(8,128)(2,1)S(1)} %fusion.92), kind=kOutput, calls=%fused_computation.100 | convolution fusion | flops 81887232 | bytes 1282560 | tf_op jit(solution)/shard_map/vc,vd->cd/dot_general | solution.py:251
  (136 shorter events, 18.3 us)
Async XLA Ops:
  0.6 54.1 %copy-start = (bf16[768,1024]{1,0:T(8,128)(2,1)S(1)}, bf16[768,1024]{1,0:T(8,128)(2,1)}, u32[]{:S(2)}) copy-start(bf16[768,1024]{1,0:T(8,128)(2,1)} %param.17) | copy-start | bytes 4718596
  0.6 14.1 %copy-start.15 = (bf16[64,768]{1,0:T(8,128)(2,1)S(1)}, bf16[64,768]{1,0:T(8,128)(2,1)}, u32[]{:S(2)}) copy-start(bf16[64,768]{1,0:T(8,128)(2,1)} %param.9) | copy-start | bytes 294916
  0.7 14.1 %collective-permute-start = (bf16[64,768]{1,0:T(8,128)(2,1)}, bf16[64,768]{1,0:T(8,128)(2,1)S(1)}, u32[]{:S(2)}, u32[]{:S(2)}) collective-permute-start(bf16[64,768]{1,0:T(8,128)(2,1)} %param.9), channel_id=1, source_target_pairs={{0,1},{1,2},{2,3},{3,0},{4,5},{5,6},{6,7},{7,4},{8,9},{9,10},{10,1... | collective-permute-start | bytes 294920 | tf_op jit(solution)/shard_map/ppermute | solution.py:182
  3.7 11.1 %collective-permute-start.1 = (bf16[64,768]{1,0:T(8,128)(2,1)}, bf16[64,768]{1,0:T(8,128)(2,1)S(1)}, u32[]{:S(2)}, u32[]{:S(2)}) collective-permute-start(bf16[64,768]{1,0:T(8,128)(2,1)} %param.9), channel_id=1, source_target_pairs={{0,2},{1,3},{2,0},{3,1},{4,6},{5,7},{6,4},{7,5},{8,10},{9,11},{10,... | collective-permute-start | bytes 294920 | tf_op jit(solution)/shard_map/ppermute | solution.py:182
  5.2 9.6 %collective-permute-start.2 = (bf16[64,768]{1,0:T(8,128)(2,1)}, bf16[64,768]{1,0:T(8,128)(2,1)S(1)}, u32[]{:S(2)}, u32[]{:S(2)}) collective-permute-start(bf16[64,768]{1,0:T(8,128)(2,1)} %param.9), channel_id=1, source_target_pairs={{0,3},{1,0},{2,1},{3,2},{4,7},{5,4},{6,5},{7,6},{8,11},{9,8},{10,9... | collective-permute-start | bytes 294920 | tf_op jit(solution)/shard_map/ppermute | solution.py:182
  12.3 3.3 %copy-start.37 = (bf16[768,1024]{1,0:T(8,128)(2,1)S(1)}, bf16[768,1024]{1,0:T(8,128)(2,1)}, u32[]{:S(2)}) copy-start(bf16[768,1024]{1,0:T(8,128)(2,1)} %param.11) | copy-start | bytes 4718596
  16.2 6.1 %copy-start.4 = (bf16[256,1024]{1,0:T(8,128)(2,1)}, bf16[256,1024]{1,0:T(8,128)(2,1)S(1)}, u32[]{:S(2)}) copy-start(bf16[256,1024]{1,0:T(8,128)(2,1)S(1)} %convolution_convert_fusion.1.embedded_ref) | copy-start | bytes 1572868
  22.8 2.7 %copy-start.6 = (bf16[51,1,16,64]{3,2,1,0:T(8,128)(2,1)}, bf16[51,1,16,64]{3,2,1,0:T(8,128)(2,1)S(1)}, u32[]{:S(2)}) copy-start(bf16[51,1,16,64]{3,2,1,0:T(8,128)(2,1)S(1)} %get-tuple-element.4) | copy-start | bytes 313348
  22.8 2.7 %copy-start.10 = (bf16[51,1,16,64]{3,2,1,0:T(8,128)(2,1)}, bf16[51,1,16,64]{3,2,1,0:T(8,128)(2,1)S(1)}, u32[]{:S(2)}) copy-start(bf16[51,1,16,64]{3,2,1,0:T(8,128)(2,1)S(1)} %get-tuple-element.5) | copy-start | bytes 313348
  23.2 1.2 %copy-start.20 = (f32[51,16]{0,1:T(8,128)}, f32[51,16]{0,1:T(8,128)S(1)}, u32[]{:S(2)}) copy-start(f32[51,16]{0,1:T(8,128)S(1)} %fusion.102) | copy-start | bytes 9796
  24.3 1.2 %copy-start.26 = (f32[16,51]{1,0:T(8,128)}, f32[16,51]{1,0:T(8,128)S(1)}, u32[]{:S(2)}) copy-start(f32[16,51]{1,0:T(8,128)S(1)} %get-tuple-element.13) | copy-start | bytes 9796
  26.3 13.7 %copy-start.1 = (bf16[1024,768]{1,0:T(8,128)(2,1)S(1)}, bf16[1024,768]{1,0:T(8,128)(2,1)}, u32[]{:S(2)}) copy-start(bf16[1024,768]{1,0:T(8,128)(2,1)} %param.15) | copy-start | bytes 4718596
  46.2 1.5 %copy-start.3 = (bf16[256,768]{0,1:T(8,128)(2,1)S(1)}, bf16[256,768]{0,1:T(8,128)(2,1)}, u32[]{:S(2)}) copy-start(bf16[256,768]{0,1:T(8,128)(2,1)} %copy.51) | copy-start | bytes 1179652
  51.2 3.6 %copy-start.31 = (f32[256]{0:T(256)S(1)}, f32[256]{0:T(256)}, u32[]{:S(2)}) copy-start(f32[256]{0:T(256)} %get-tuple-element.12) | copy-start | bytes 3076
  54.8 4.6 %copy-start.5 = (f32[256,768]{1,0:T(8,128)S(1)}, f32[256,768]{1,0:T(8,128)}, u32[]{:S(2)}) copy-start(f32[256,768]{1,0:T(8,128)} %copy.55) | copy-start | bytes 2359300
  54.8 4.6 %copy-start.30 = (f32[256]{0:T(256)S(1)}, f32[256]{0:T(256)}, u32[]{:S(2)}) copy-start(f32[256]{0:T(256)} %get-tuple-element.11) | copy-start | bytes 3076
  62.6 2.8 %copy-start.8 = (bf16[256,768]{1,0:T(8,128)(2,1)}, bf16[256,768]{1,0:T(8,128)(2,1)S(1)}, u32[]{:S(2)}) copy-start(bf16[256,768]{1,0:T(8,128)(2,1)S(1)} %get-tuple-element.18) | copy-start | bytes 1179652
  68.2 2.6 %copy-start.2 = (bf16[256,768]{0,1:T(8,128)(2,1)S(1)}, bf16[256,768]{0,1:T(8,128)(2,1)}, u32[]{:S(2)}) copy-start(bf16[256,768]{0,1:T(8,128)(2,1)} %copy.56) | copy-start | bytes 1179652
  68.2 3.8 %copy-start.27 = (f32[16,51]{1,0:T(8,128)S(1)}, f32[16,51]{1,0:T(8,128)}, u32[]{:S(2)}) copy-start(f32[16,51]{1,0:T(8,128)} %copy-done.26) | copy-start | bytes 9796
  70.9 4.2 %copy-start.33 = (s32[51]{0:T(128)S(1)}, s32[51]{0:T(128)}, u32[]{:S(2)}) copy-start(s32[51]{0:T(128)} %copy-done.32) | copy-start | bytes 616
  70.9 4.2 %copy-start.36 = (pred[256]{0:T(512)(128)(4,1)S(1)}, pred[256]{0:T(512)(128)(4,1)}, u32[]{:S(2)}) copy-start(pred[256]{0:T(512)(128)(4,1)} %broadcast_compare_fusion) | copy-start | bytes 772
  77.6 2.7 %copy-start.11 = (bf16[51,1,16,64]{3,2,1,0:T(8,128)(2,1)S(1)}, bf16[51,1,16,64]{3,2,1,0:T(8,128)(2,1)}, u32[]{:S(2)}) copy-start(bf16[51,1,16,64]{3,2,1,0:T(8,128)(2,1)} %copy-done.10) | copy-start | bytes 313348
  77.6 2.7 %copy-start.13 = (f32[16,51,51]{1,2,0:T(8,128)S(1)}, f32[16,51,51]{1,2,0:T(8,128)}, u32[]{:S(2)}) copy-start(f32[16,51,51]{1,2,0:T(8,128)} %copy-done.12) | copy-start | bytes 499396
  77.6 3.0 %copy-start.7 = (bf16[51,1,16,64]{3,2,1,0:T(8,128)(2,1)S(1)}, bf16[51,1,16,64]{3,2,1,0:T(8,128)(2,1)}, u32[]{:S(2)}) copy-start(bf16[51,1,16,64]{3,2,1,0:T(8,128)(2,1)} %copy-done.6) | copy-start | bytes 313348
  77.6 3.0 %copy-start.21 = (f32[51,16]{0,1:T(8,128)S(1)}, f32[51,16]{0,1:T(8,128)}, u32[]{:S(2)}) copy-start(f32[51,16]{0,1:T(8,128)} %copy-done.20) | copy-start | bytes 9796
  80.6 1.0 %copy-start.14 = (f32[16,51,51]{1,2,0:T(8,128)S(1)}, f32[16,51,51]{1,2,0:T(8,128)}, u32[]{:S(2)}) copy-start(f32[16,51,51]{1,2,0:T(8,128)} %copy-done.12) | copy-start | bytes 499396
  84.2 5.0 %copy-start.35 = (f32[51]{0:T(128)S(1)}, f32[51]{0:T(128)}, u32[]{:S(2)}) copy-start(f32[51]{0:T(128)} %copy-done.34) | copy-start | bytes 616
  84.3 5.0 %copy-start.29 = (f32[51]{0:T(128)S(1)}, f32[51]{0:T(128)}, u32[]{:S(2)}) copy-start(f32[51]{0:T(128)} %copy-done.28) | copy-start | bytes 616
  84.3 5.3 %copy-start.9 = (bf16[51,1024]{1,0:T(8,128)(2,1)S(1)}, bf16[51,1024]{1,0:T(8,128)(2,1)}, u32[]{:S(2)}) copy-start(bf16[51,1024]{1,0:T(8,128)(2,1)} %convolution_convert_fusion.12) | copy-start | bytes 313348
  89.7 6.4 %collective-permute-start.5 = (bf16[51,1024]{1,0:T(8,128)(2,1)S(1)}, bf16[51,1024]{1,0:T(8,128)(2,1)S(1)}, u32[]{:S(2)}, u32[]{:S(2)}) collective-permute-start(bf16[51,1024]{1,0:T(8,128)(2,1)S(1)} %fusion.92), channel_id=1, source_target_pairs={{0,1},{1,2},{2,3},{3,0},{4,5},{5,6},{6,7},{7,4},{8,9},{9,10},{10,1... | collective-permute-start | bytes 313352 | tf_op jit(solution)/shard_map/ppermute | solution.py:182
  90.3 6.2 %collective-permute-start.4 = (bf16[51,1024]{1,0:T(8,128)(2,1)S(1)}, bf16[51,1024]{1,0:T(8,128)(2,1)S(1)}, u32[]{:S(2)}, u32[]{:S(2)}) collective-permute-start(bf16[51,1024]{1,0:T(8,128)(2,1)S(1)} %fusion.92), channel_id=1, source_target_pairs={{0,2},{1,3},{2,0},{3,1},{4,6},{5,7},{6,4},{7,5},{8,10},{9,11},{10,... | collective-permute-start | bytes 313352 | tf_op jit(solution)/shard_map/ppermute | solution.py:182
  90.8 5.7 %collective-permute-start.3 = (bf16[51,1024]{1,0:T(8,128)(2,1)S(1)}, bf16[51,1024]{1,0:T(8,128)(2,1)S(1)}, u32[]{:S(2)}, u32[]{:S(2)}) collective-permute-start(bf16[51,1024]{1,0:T(8,128)(2,1)S(1)} %fusion.92), channel_id=1, source_target_pairs={{0,3},{1,0},{2,1},{3,2},{4,7},{5,4},{6,5},{7,6},{8,11},{9,8},{10,9... | collective-permute-start | bytes 313352 | tf_op jit(solution)/shard_map/ppermute | solution.py:182
  (12 other events, 8.1 us)

commit v10 on v6

--- a/solution.py
+++ b/solution.py
@@ -89,17 +89,22 @@
     ).astype(jnp.bfloat16)
     placed = jnp.dot(picks, lowered_visible, preferred_element_type=jnp.float32)
     lowered = jnp.where(seen > 0, placed, lowered_mask.astype(jnp.float32)).astype(jnp.bfloat16)
-    grouped = lowered.reshape(total_rows, GROUPS, DD // GROUPS)
-    padded = jnp.pad(grouped, ((1, 1), (0, 0), (0, 0)))
-    convolved = jnp.zeros((total_rows, GROUPS, DD // GROUPS), jnp.float32)
+    padded = jnp.pad(lowered, ((1, 1), (0, 0)))
+    group_width = DD // GROUPS
+    same_group = (
+        jnp.arange(GROUPS)[:, None, None, None] == jnp.arange(GROUPS)[None, None, :, None]
+    )
+    convolved = jnp.zeros((total_rows, DD), jnp.float32)
     for offset in range(3):
-        convolved = convolved + jnp.einsum(
-            "pgi,gio->pgo",
+        spread_w = jnp.where(
+            same_group, conv_w[offset][:, :, None, :], jnp.zeros((), conv_w.dtype)
+        ).reshape(DD, DD)
+        convolved = convolved + jnp.dot(
             padded[offset : offset + total_rows],
-            conv_w[offset],
+            spread_w,
             preferred_element_type=jnp.float32,
         )
-    activated = jax.nn.gelu(row_norm(convolved.reshape(total_rows, DD)), approximate=False)
+    activated = jax.nn.gelu(row_norm(convolved), approximate=False)
     hidden = (lowered.astype(jnp.float32) + activated).astype(jnp.bfloat16)
     return jnp.dot(hidden, dec_out, preferred_element_type=jnp.float32)
 

time: 86.5 us -> 109 us (1.26)
  local copies, waits for them, and re-layouts: 16.4 us -> 38 us
  other arithmetic: 10.7 us -> 14.4 us
  waiting for transfers between devices: 3.77 us -> 0.9 us
  matrix products: 43.7 us -> 42.2 us
    select_n x0 -> x3, local copies, waits for them, and re-layouts: none -> 15.8 us  [decoder_output(): jnp.where(same_group, conv_w[offset][:, :, None, :], jnp.zeros((), conv_w...]
    select_n x0 -> x1, other arithmetic: none -> 3.94 us  [decoder_output(): jnp.where(same_group, conv_w[offset][:, :, None, :], jnp.zeros((), conv_w...]
    dot_general x6, matrix products: 2.78 us -> 6.65 us  [decoder_output(): jnp.dot(padded[offset:offset + total_rows], spread_w, preferred_element_t...]
    ppermute x6, waiting for transfers between devices: 3.77 us -> 0.9 us  [ring_gather(): parts.append(lax.ppermute(values, 'mask', pairs))]
    dot_general x2, matrix products: 8.69 us -> 6.5 us  [decoder_output(): return jnp.dot(hidden, dec_out, preferred_element_type=jnp.float32)]
    reshape x2, local copies, waits for them, and re-layouts: 0.87 us -> 2.73 us  [attention_from(): context = split_project(projected.reshape(row_count, 3, HEADS, D // HEADS))]
    dot_general x1, matrix products: 2.16 us -> 0.65 us  [on_device(): jnp.dot(clip_pixels, embed_w, preferred_element_type=jnp.float32)]
    reshape x2 -> x0, local copies, waits for them, and re-layouts: 1.32 us -> none  [the longest x1 1.15 us: decoder_output(): convolved.reshape(total_rows, DD)]
  transfers between devices with their start and end apart: 6 -> 6, of which waited for: 3 -> 2; matrix products, arithmetic and copies ran while one was open for 8% -> 27% of each run, Pallas kernels for 0% -> 0%
where the time goes in v10:
time: 109 us; the launch traced here: 108 us
  matrix products  42.2 us (39%)
  local copies, waits for them, and re-layouts  38 us (35%)
  other arithmetic  14.4 us (13%)
  starting transfers between devices  9.04 us (8%)
  between operations  3.02 us (3%)
    select_n x3, local copies, waits for them, and re-layouts, decoder_output(): jnp.where(same_group, conv_w[offset][:, :, None, :], jnp.zeros((), conv_w...  15.8 us
    ppermute x6, starting transfers between devices, ring_gather(): parts.append(lax.ppermute(values, 'mask', pairs))  9.04 us
    dot_general x6, matrix products, decoder_output(): jnp.dot(padded[offset:offset + total_rows], spread_w, preferred_element_t...  6.65 us
    dot_general x2, matrix products, decoder_output(): return jnp.dot(hidden, dec_out, preferred_element_type=jnp.float32)  6.5 us
    dot_general x1, matrix products, project_rows(): jnp.dot(normed, w_qkv, preferred_element_type=jnp.float32)  6.01 us
    dot_general x2, matrix products, decoder_output(): jnp.dot(visible_out, dec_in, preferred_element_type=jnp.float32)  5.28 us
    dot_general x1, matrix products, copy_terms(): branch = attention_from(reuse_rows(visible_in, w_qkv, projected), w_out)  4.93 us
    select_n x1, other arithmetic, decoder_output(): jnp.where(same_group, conv_w[offset][:, :, None, :], jnp.zeros((), conv_w...  3.94 us
  transfers between devices with their start and end apart: 6, of which 2 were waited for; matrix products, arithmetic and copies ran while one was open for 27% of the time, Pallas kernels for 0%

profile of v10, /device:TPU:0, one launch (start us, length us, event | category | flops | bytes accessed | tf_op | source)
XLA Modules:
  0.0 107.6 jit_solution(17627086225168508930)
XLA Ops:
  0.6 3.0 %collective-permute-start = (bf16[64,768]{1,0:T(8,128)(2,1)}, bf16[64,768]{1,0:T(8,128)(2,1)S(1)}, u32[]{:S(2)}, u32[]{:S(2)}) collective-permute-start(bf16[64,768]{1,0:T(8,128)(2,1)} %param.9), channel_id=1, source_target_pairs={{0,1},{1,2},{2,3},{3,0},{4,5},{5,6},{6,7},{7,4},{8,9},{9,10},{10,1... | collective-permute-start | bytes 294920 | tf_op jit(solution)/shard_map/ppermute | solution.py:134
  3.7 1.5 %collective-permute-start.1 = (bf16[64,768]{1,0:T(8,128)(2,1)}, bf16[64,768]{1,0:T(8,128)(2,1)}, u32[]{:S(2)}, u32[]{:S(2)}) collective-permute-start(bf16[64,768]{1,0:T(8,128)(2,1)} %param.9), channel_id=1, source_target_pairs={{0,2},{1,3},{2,0},{3,1},{4,6},{5,7},{6,4},{7,5},{8,10},{9,11},{10,... | collective-permute-start | bytes 294920 | tf_op jit(solution)/shard_map/ppermute | solution.py:134
  5.2 1.4 %collective-permute-start.2 = (bf16[64,768]{1,0:T(8,128)(2,1)}, bf16[64,768]{1,0:T(8,128)(2,1)}, u32[]{:S(2)}, u32[]{:S(2)}) collective-permute-start(bf16[64,768]{1,0:T(8,128)(2,1)} %param.9), channel_id=1, source_target_pairs={{0,3},{1,0},{2,1},{3,2},{4,7},{5,4},{6,5},{7,6},{8,11},{9,8},{10,9... | collective-permute-start | bytes 294920 | tf_op jit(solution)/shard_map/ppermute | solution.py:134
  8.2 1.2 %gather_fusion = s32[4,51]{1,0:T(4,128)S(1)} fusion(s32[4,51]{1,0:T(4,128)} %param.10, s32[1024]{0:T(1024)S(1)} %pad_clamp_fusion.2), kind=kCustom, calls=%fused_computation | custom fusion | bytes 1648 | tf_op jit(solution)/shard_map/gather | solution.py:212
  10.2 1.2 %slice_bitcast_fusion.6 = (bf16[16,48,48]{2,1,0:T(8,128)(2,1)S(1)}, bf16[16,48,48]{2,1,0:T(8,128)(2,1)S(1)}, bf16[16,48,48]{2,1,0:T(8,128)(2,1)S(1)}) fusion(bf16[3,16,48,48]{3,2,1,0:T(8,128)(2,1)} %param.16), kind=kLoop, calls=%fused_computation.174 | loop fusion | bytes 442368 | tf_op jit(solution)/shard_map/jvp(jit(_where))/broadcast_in_dim | solution.py:99
  11.3 3.9 %broadcast_select_fusion = (bf16[16,48,16,48]{3,2,1,0:T(8,128)(2,1)}, bf16[16,48,16,48]{3,2,1,0:T(8,128)(2,1)}, bf16[16,48,16,48]{3,2,1,0:T(8,128)(2,1)}) fusion(pred[16,16]{1,0:T(8,128)(4,1)S(1)} %iota_compare_fusion.4, bf16[16,48,48]{2,1,0:T(8,128)(2,1)S(1)} %get-tuple-element.11, bf16[16,48,48]{2,1,0:T(8,128)(2,1)S(1)} %get-tuple-element.13, ...), kind=kLoop, calls=%fused_computation.8 | loop fusion | flops 1769472 | bytes 3760384 | tf_op jit(solution)/shard_map/jvp(jit(_where))/select_n | solution.py:99
  15.3 5.5 %select_n.210 = bf16[768,768]{1,0:T(8,128)(2,1)} reshape(bf16[16,48,16,48]{3,2,1,0:T(8,128)(2,1)} %get-tuple-element.20) | data formatting | bytes 2359296 | tf_op jit(solution)/shard_map/jvp(jit(_where))/select_n | solution.py:99
  21.3 4.7 %select_n.212 = bf16[768,768]{1,0:T(8,128)(2,1)S(1)} reshape(bf16[16,48,16,48]{3,2,1,0:T(8,128)(2,1)} %get-tuple-element.19) | data formatting | bytes 2359296 | tf_op jit(solution)/shard_map/jvp(jit(_where))/select_n | solution.py:99
  26.0 5.5 %select_n.214 = bf16[768,768]{1,0:T(8,128)(2,1)} reshape(bf16[16,48,16,48]{3,2,1,0:T(8,128)(2,1)} %get-tuple-element.18) | data formatting | bytes 2359296 | tf_op jit(solution)/shard_map/jvp(jit(_where))/select_n | solution.py:99
  32.2 1.9 %convolution_reduce_fusion = bf16[768]{0:T(1024)(128)(2,1)S(1)} fusion(bf16[1024,1]{0,1:T(2,128)(2,1)S(1)} %reshape.363, bf16[1024,768]{1,0:T(8,128)(2,1)} %param.15), kind=kOutput, calls=%fused_computation.56 | convolution fusion | flops 1572864 | bytes 1576448 | tf_op jit(solution)/shard_map/jvp()/dot_general | solution.py:87
  37.3 1.9 %gather_fusion.2 = bf16[51,1024]{1,0:T(8,128)(2,1)S(1)} fusion(bf16[256,1024]{1,0:T(8,128)(2,1)} %copy-done.4, s32[1024]{0:T(1024)S(1)} %pad_clamp_fusion), kind=kCustom, calls=%fused_computation.2 | custom fusion | bytes 209100 | tf_op jit(solution)/shard_map/gather | solution.py:183
  39.2 6.0 %convolution_convert_fusion = bf16[256,3072]{1,0:T(8,128)(2,1)} fusion(bf16[1024,3072]{1,0:T(8,128)(2,1)} %param.12, bf16[256,1024]{1,0:T(8,128)(2,1)} %copy-done.4, f32[256]{0:T(256)S(1)} %add_rsqrt_fusion.3, f32[256]{0:T(256)S(1)} %broadcast_multiply_fusion.3), kind=kOutput, calls=%fused_computation.6 | convolution fusion | flops 1612447744 | bytes 8390656 | tf_op jit(solution)/shard_map/dot_general | solution.py:48
  45.2 3.4 %gather_fusion.3 = bf16[51,3072]{1,0:T(8,128)(2,1)} fusion(bf16[256,3072]{1,0:T(8,128)(2,1)} %convolution_convert_fusion, s32[1024]{0:T(1024)S(1)} %pad_clamp_fusion), kind=kCustom, calls=%fused_computation.3 | custom fusion | bytes 626892 | tf_op jit(solution)/shard_map/gather | solution.py:187
  48.6 2.6 %copy.33 = bf16[256,3072]{0,1:T(8,128)(2,1)} copy(bf16[256,3072]{1,0:T(8,128)(2,1)} %convolution_convert_fusion) | data formatting | bytes 3145728 | tf_op jit(solution)/shard_map/convert_element_type | solution.py:48
  51.2 2.3 %reshape.320 = bf16[51,3,16,64]{3,2,1,0:T(8,128)(2,1)} reshape(bf16[51,3072]{1,0:T(8,128)(2,1)} %gather_fusion.3) | data formatting | bytes 626688 | tf_op jit(solution)/shard_map/jvp()/reshape | solution.py:53
  53.4 1.3 %fusion.130 = (bf16[51,1,16,64]{3,2,1,0:T(8,128)(2,1)S(1)}, bf16[51,1,16,64]{3,2,1,0:T(8,128)(2,1)S(1)}, bf16[51,1,16,64]{3,2,1,0:T(8,128)(2,1)S(1)}) fusion(bf16[51,3,16,64]{3,2,1,0:T(8,128)(2,1)} %reshape.320), kind=kLoop, calls=%fused_computation.240 | loop fusion | bytes 626688 | tf_op jit(solution)/shard_map/jvp()/slice | solution.py:41
  58.2 2.8 %convolution_convert_fusion.15 = bf16[51,768]{1,0:T(8,128)(2,1)} fusion(bf16[1024,768]{1,0:T(8,128)(2,1)} %param.15, bf16[51,1024]{1,0:T(8,128)(2,1)S(1)} %reshape.321, bf16[1024,1024]{1,0:T(8,128)(2,1)S(1)} %copy-done, bf16[51,1024]{1,0:T(8,128)(2,1)S(1)} %gather_fusion.2), kind=kOutput, calls=%fused_computation.55 | convolution fusion | flops 187366656 | bytes 3957248 | tf_op jit(solution)/shard_map/jvp()/dot_general | solution.py:84
  61.1 1.3 %fusion.4 = bf16[256,768]{1,0:T(8,128)(2,1)S(1)} fusion(bf16[51,768]{1,0:T(8,128)(2,1)} %convolution_convert_fusion.15, bf16[768]{0:T(1024)(128)(2,1)S(1)} %convolution_reduce_fusion, pred[256]{0:T(512)(128)(4,1)} %broadcast_compare_fusion, s32[51]{0:T(128)S(1)} %fusion.118), kind=kOutput, calls=%fused_computation.25 | convolution fusion | flops 20263680 | bytes 473548 | tf_op jit(solution)/shard_map/jvp()/dot_general | solution.py:90
  62.3 1.8 %fusion.83 = f32[256,768]{1,0:T(8,128)S(1)} fusion(bf16[768,768]{1,0:T(8,128)(2,1)} %select_n.210, bf16[256,768]{1,0:T(8,128)(2,1)S(1)} %fusion.4), kind=kOutput, calls=%fused_computation.150 | convolution fusion | flops 301989888 | bytes 2359296 | tf_op jit(solution)/shard_map/jvp()/dot_general | solution.py:102
  70.3 3.2 %multiply_reduce_fusion = (f32[]{:T(128)}, f32[256,1024]{1,0:T(8,128)S(1)}) fusion(f32[256]{0:T(256)S(1)} %copy-done.20, f32[256]{0:T(256)S(1)} %add_rsqrt_fusion.2, f32[256,1024]{1,0:T(8,128)S(1)} %get-tuple-element.30, f32[256]{0:T(256)S(1)} %broadcast_multiply_fusion.2, bf16[768,1024]{1,0:T(8,128)(2,1)S(1)} %copy-done.24, ...), kind=kOutput, calls=%fused_computation.65 | convolution fusion | flops 418709504 | bytes 4854788 | tf_op jit(solution)/shard_map/jvp()/dot_general | solution.py:109
  73.5 3.3 %multiply_reduce_fusion.2 = (f32[256]{0:T(256)S(1)}, bf16[256,768]{1,0:T(8,128)(2,1)S(1)}) fusion(f32[256,768]{1,0:T(8,128)S(1)} %get-tuple-element.34, f32[256]{0:T(256)S(1)} %broadcast_multiply_fusion.1, f32[256]{0:T(256)S(1)} %fusion.113, bf16[768,1024]{1,0:T(8,128)(2,1)S(1)} %copy-done.24, f32[256,1024]{1,0:T(8,128)S(1)} %get-tuple-element.45, ...), kind=kOutput, calls=%fused_computation.87 | convolution fusion | flops 419495680 | bytes 3805184 | tf_op jit(solution)/shard_map/transpose(jvp())/dot_general | solution.py:109
  76.9 2.8 %fusion.129 = (f32[256]{0:T(256)S(1)}, f32[256,768]{1,0:T(8,128)S(1)}) fusion(f32[256]{0:T(256)S(1)} %multiply_multiply_fusion.8, bf16[256,768]{1,0:T(8,128)(2,1)S(1)} %get-tuple-element.36, f32[256]{0:T(256)S(1)} %fusion.113, f32[256,768]{1,0:T(8,128)S(1)} %get-tuple-element.34, f32[256]{0:T(256)S(1)} %broadcast_multiply_fusion.1), kind=kLoop, calls=%fused_computation.239 | loop fusion | flops 15531776 | bytes 1970176 | tf_op jit(solution)/shard_map/transpose(jvp())/reduce_sum | solution.py:19
  79.7 1.3 %convolution_convert_fusion.2 = bf16[256,768]{1,0:T(8,128)(2,1)} fusion(bf16[768,768]{1,0:T(8,128)(2,1)S(1)} %copy-done.1, f32[256,768]{1,0:T(8,128)S(1)} %get-tuple-element.7, f32[256]{0:T(256)S(1)} %negate_multiply_fusion.1), kind=kOutput, calls=%fused_computation.26 | convolution fusion | flops 302383104 | bytes 2360320 | tf_op jit(solution)/shard_map/transpose(jvp())/dot_general | solution.py:102
  80.9 1.3 %convolution_convert_fusion.3 = bf16[256,768]{1,0:T(8,128)(2,1)} fusion(bf16[768,768]{1,0:T(8,128)(2,1)S(1)} %select_n.212, f32[256,768]{1,0:T(8,128)S(1)} %get-tuple-element.7, f32[256]{0:T(256)S(1)} %negate_multiply_fusion.1), kind=kOutput, calls=%fused_computation.27 | convolution fusion | flops 302383104 | bytes 2360320 | tf_op jit(solution)/shard_map/transpose(jvp())/dot_general | solution.py:102
  82.2 1.3 %convolution_convert_fusion.4 = bf16[256,768]{1,0:T(8,128)(2,1)} fusion(bf16[768,768]{1,0:T(8,128)(2,1)S(1)} %copy-done.2, f32[256,768]{1,0:T(8,128)S(1)} %get-tuple-element.7, f32[256]{0:T(256)S(1)} %negate_multiply_fusion.1), kind=kOutput, calls=%fused_computation.28 | convolution fusion | flops 302383104 | bytes 2360320 | tf_op jit(solution)/shard_map/transpose(jvp())/dot_general | solution.py:102
  84.2 2.5 %convolution_convert_fusion.12 = bf16[51,1024]{1,0:T(8,128)(2,1)S(1)} fusion(bf16[1024,768]{1,0:T(8,128)(2,1)} %param.15, bf16[256,768]{1,0:T(8,128)(2,1)S(1)} %copy-done.10, bf16[256,768]{1,0:T(8,128)(2,1)S(1)} %copy-done.11, bf16[256,768]{1,0:T(8,128)(2,1)S(1)} %copy-done.12, bf16[256,768]{1,0:T(8,128)(2,1)} %convolution_convert_fusion.4, ...), kind=kOutput, calls=%fused_computation.51 | convolution fusion | flops 102144000 | bytes 3250636 | tf_op jit(solution)/shard_map/transpose(jvp())/dot_general | solution.py:84
  87.6 1.3 %multiply_reduce_fusion.4 = (f32[16,51]{1,0:T(8,128)S(1)}, f32[16,51,51]{1,2,0:T(8,128)S(1)}) fusion(f32[16,51,51]{1,2,0:T(8,128)} %copy-done.15, f32[16,51]{1,0:T(8,128)S(1)} %multiply_divide_fusion, bf16[51,1,16,64]{3,2,1,0:T(8,128)(2,1)S(1)} %copy-done.14, bf16[51,16,64]{2,1,0:T(8,128)(2,1)S(1)} %reshape.324), kind=kOutput, calls=%fused_computation.127 | convolution fusion | flops 5534112 | bytes 548352 | tf_op jit(solution)/shard_map/transpose(jvp(hqk,khd->qhd))/dot_general | solution.py:36
  89.0 1.6 %fusion.57 = (f32[51,16]{0,1:T(8,128)S(1)}, f32[51,16,64]{2,0,1:T(8,128)S(1)}) fusion(bf16[51,1,16,64]{3,2,1,0:T(8,128)(2,1)S(1)} %copy-done.8, f32[51,16]{0,1:T(8,128)S(1)} %fusion.112, bf16[51,1,16,64]{3,2,1,0:T(8,128)(2,1)S(1)} %copy-done.6, f32[16,51,51]{1,2,0:T(8,128)} %copy-done.15, f32[16,51,51]{1,2,0:T(8,128)S(1)} %get-tuple-element.38, ...), kind=kOutput, calls=%fused_computation.122 | convolution fusion | flops 5910288 | bytes 763776 | tf_op jit(solution)/shard_map/transpose(jvp(qhd,khd->hqk))/dot_general | solution.py:31
  93.1 4.9 %fusion.93 = (f32[51]{0:T(128)S(1)}, f32[51]{0:T(128)S(1)}, f32[51,1024]{1,0:T(8,128)S(1)}) fusion(bf16[51,1024]{1,0:T(8,128)(2,1)S(1)} %gather_fusion.2, f32[51]{0:T(128)S(1)} %broadcast_multiply_fusion.4, bf16[51,3072]{1,0:T(8,128)(2,1)S(1)} %reshape.325, bf16[1024,3072]{1,0:T(8,128)(2,1)} %param.12), kind=kOutput, calls=%fused_computation.162 | convolution fusion | flops 321281920 | bytes 6918756 | tf_op jit(solution)/shard_map/transpose(jvp(transpose(jvp())))/dot_general | solution.py:119
  99.6 1.9 %collective-permute-start.3 = (bf16[51,1024]{1,0:T(8,128)(2,1)S(1)}, bf16[51,1024]{1,0:T(8,128)(2,1)S(1)}, u32[]{:S(2)}, u32[]{:S(2)}) collective-permute-start(bf16[51,1024]{1,0:T(8,128)(2,1)S(1)} %fusion.105), channel_id=1, source_target_pairs={{0,3},{1,0},{2,1},{3,2},{4,7},{5,4},{6,5},{7,6},{8,11},{9,8},{10,9... | collective-permute-start | bytes 313352 | tf_op jit(solution)/shard_map/ppermute | solution.py:134
  102.5 1.2 %gather_fusion.1 = bf16[204,192]{1,0:T(8,128)(2,1)S(1)} fusion(bf16[256,192]{1,0:T(8,128)(2,1)S(1)} %constant_dynamic-slice_fusion.1, s32[1024]{0:T(1024)} %pad_clamp_fusion.1), kind=kCustom, calls=%fused_computation.1 | custom fusion | bytes 157488 | tf_op jit(solution)/shard_map/gather | solution.py:214
  105.3 1.2 %fusion.61 = f32[192,1024]{1,0:T(8,128)} fusion(bf16[204,192]{1,0:T(8,128)(2,1)S(1)} %gather_fusion.1, bf16[51,1024]{1,0:T(8,128)(2,1)S(1)} %collective-permute-done.5, bf16[51,1024]{1,0:T(8,128)(2,1)S(1)} %collective-permute-done.4, bf16[51,1024]{1,0:T(8,128)(2,1)S(1)} %collective-permute-done.3, bf16[51,1024]{1,0:T(8,128)(2,1)S(1)} %fusion.105), kind=kOutput, calls=%fused_computation.129 | convolution fusion | flops 81887232 | bytes 1282560 | tf_op jit(solution)/shard_map/vc,vd->cd/dot_general | solution.py:215
  (120 shorter events, 23.7 us)
Async XLA Ops:
  0.6 57.6 %copy-start = (bf16[1024,1024]{1,0:T(8,128)(2,1)S(1)}, bf16[1024,1024]{1,0:T(8,128)(2,1)}, u32[]{:S(2)}) copy-start(bf16[1024,1024]{1,0:T(8,128)(2,1)} %param.13) | copy-start | bytes 6291460
  0.6 33.4 %collective-permute-start = (bf16[64,768]{1,0:T(8,128)(2,1)}, bf16[64,768]{1,0:T(8,128)(2,1)S(1)}, u32[]{:S(2)}, u32[]{:S(2)}) collective-permute-start(bf16[64,768]{1,0:T(8,128)(2,1)} %param.9), channel_id=1, source_target_pairs={{0,1},{1,2},{2,3},{3,0},{4,5},{5,6},{6,7},{7,4},{8,9},{9,10},{10,1... | collective-permute-start | bytes 294920 | tf_op jit(solution)/shard_map/ppermute | solution.py:134
  3.7 30.4 %collective-permute-start.1 = (bf16[64,768]{1,0:T(8,128)(2,1)}, bf16[64,768]{1,0:T(8,128)(2,1)}, u32[]{:S(2)}, u32[]{:S(2)}) collective-permute-start(bf16[64,768]{1,0:T(8,128)(2,1)} %param.9), channel_id=1, source_target_pairs={{0,2},{1,3},{2,0},{3,1},{4,6},{5,7},{6,4},{7,5},{8,10},{9,11},{10,... | collective-permute-start | bytes 294920 | tf_op jit(solution)/shard_map/ppermute | solution.py:134
  5.2 28.9 %collective-permute-start.2 = (bf16[64,768]{1,0:T(8,128)(2,1)}, bf16[64,768]{1,0:T(8,128)(2,1)}, u32[]{:S(2)}, u32[]{:S(2)}) collective-permute-start(bf16[64,768]{1,0:T(8,128)(2,1)} %param.9), channel_id=1, source_target_pairs={{0,3},{1,0},{2,1},{3,2},{4,7},{5,4},{6,5},{7,6},{8,11},{9,8},{10,9... | collective-permute-start | bytes 294920 | tf_op jit(solution)/shard_map/ppermute | solution.py:134
  8.0 53.0 %copy-start.21 = (s32[51]{0:T(128)}, s32[51]{0:T(128)S(1)}, u32[]{:S(2)}) copy-start(s32[51]{0:T(128)S(1)} %fusion.118) | copy-start | bytes 616
  15.3 5.5 %copy-start.18 = (bf16[1024]{0:T(1024)(128)(2,1)S(1)}, bf16[1024]{0:T(1024)(128)(2,1)}, u32[]{:S(2)}) copy-start(bf16[1024]{0:T(1024)(128)(2,1)} %param.14) | copy-start | bytes 6148
  31.6 2.5 %copy-start.17 = (bf16[64,768]{1,0:T(8,128)(2,1)S(1)}, bf16[64,768]{1,0:T(8,128)(2,1)}, u32[]{:S(2)}) copy-start(bf16[64,768]{1,0:T(8,128)(2,1)} %param.9) | copy-start | bytes 294916
  32.2 3.7 %copy-start.23 = (bf16[768,1024]{1,0:T(8,128)(2,1)S(1)}, bf16[768,1024]{1,0:T(8,128)(2,1)}, u32[]{:S(2)}) copy-start(bf16[768,1024]{1,0:T(8,128)(2,1)} %param.11) | copy-start | bytes 4718596
  36.5 0.8 copy-start.4
  54.7 1.3 %copy-start.5 = (bf16[51,1,16,64]{3,2,1,0:T(8,128)(2,1)}, bf16[51,1,16,64]{3,2,1,0:T(8,128)(2,1)S(1)}, u32[]{:S(2)}) copy-start(bf16[51,1,16,64]{3,2,1,0:T(8,128)(2,1)S(1)} %get-tuple-element.10) | copy-start | bytes 313348
  54.7 1.3 %copy-start.7 = (bf16[51,1,16,64]{3,2,1,0:T(8,128)(2,1)}, bf16[51,1,16,64]{3,2,1,0:T(8,128)(2,1)S(1)}, u32[]{:S(2)}) copy-start(bf16[51,1,16,64]{3,2,1,0:T(8,128)(2,1)S(1)} %get-tuple-element.8) | copy-start | bytes 313348
  54.7 1.3 %copy-start.13 = (bf16[51,1,16,64]{3,2,1,0:T(8,128)(2,1)}, bf16[51,1,16,64]{3,2,1,0:T(8,128)(2,1)S(1)}, u32[]{:S(2)}) copy-start(bf16[51,1,16,64]{3,2,1,0:T(8,128)(2,1)S(1)} %get-tuple-element.9) | copy-start | bytes 313348
  55.6 0.8 copy-start.15
  64.1 1.3 %copy-start.2 = (bf16[768,768]{1,0:T(8,128)(2,1)S(1)}, bf16[768,768]{1,0:T(8,128)(2,1)}, u32[]{:S(2)}) copy-start(bf16[768,768]{1,0:T(8,128)(2,1)} %select_n.214) | copy-start | bytes 3538948
  65.4 1.4 %copy-start.3 = (bf16[256,3072]{0,1:T(8,128)(2,1)S(1)}, bf16[256,3072]{0,1:T(8,128)(2,1)}, u32[]{:S(2)}) copy-start(bf16[256,3072]{0,1:T(8,128)(2,1)} %copy.33) | copy-start | bytes 4718596
  68.9 1.1 %copy-start.20 = (f32[256]{0:T(256)S(1)}, f32[256]{0:T(256)}, u32[]{:S(2)}) copy-start(f32[256]{0:T(256)} %get-tuple-element.22) | copy-start | bytes 3076
  68.9 1.4 %copy-start.24 = (bf16[768,1024]{1,0:T(8,128)(2,1)S(1)}, bf16[768,1024]{1,0:T(8,128)(2,1)}, u32[]{:S(2)}) copy-start(bf16[768,1024]{1,0:T(8,128)(2,1)} %param.17) | copy-start | bytes 4718596
  70.3 3.2 %copy-start.19 = (f32[256]{0:T(256)S(1)}, f32[256]{0:T(256)}, u32[]{:S(2)}) copy-start(f32[256]{0:T(256)} %get-tuple-element.21) | copy-start | bytes 3076
  76.8 4.1 %copy-start.9 = (bf16[256,768]{1,0:T(8,128)(2,1)}, bf16[256,768]{1,0:T(8,128)(2,1)S(1)}, u32[]{:S(2)}) copy-start(bf16[256,768]{1,0:T(8,128)(2,1)S(1)} %get-tuple-element.36) | copy-start | bytes 1179652
  76.8 2.8 %copy-start.1 = (bf16[768,768]{1,0:T(8,128)(2,1)S(1)}, bf16[768,768]{1,0:T(8,128)(2,1)}, u32[]{:S(2)}) copy-start(bf16[768,768]{1,0:T(8,128)(2,1)} %select_n.210) | copy-start | bytes 3538948
  82.2 1.9 %copy-start.10 = (bf16[256,768]{1,0:T(8,128)(2,1)S(1)}, bf16[256,768]{1,0:T(8,128)(2,1)}, u32[]{:S(2)}) copy-start(bf16[256,768]{1,0:T(8,128)(2,1)} %copy-done.9) | copy-start | bytes 1179652
  82.2 1.9 %copy-start.11 = (bf16[256,768]{1,0:T(8,128)(2,1)S(1)}, bf16[256,768]{1,0:T(8,128)(2,1)}, u32[]{:S(2)}) copy-start(bf16[256,768]{1,0:T(8,128)(2,1)} %convolution_convert_fusion.2) | copy-start | bytes 1179652
  82.2 1.9 %copy-start.12 = (bf16[256,768]{1,0:T(8,128)(2,1)S(1)}, bf16[256,768]{1,0:T(8,128)(2,1)}, u32[]{:S(2)}) copy-start(bf16[256,768]{1,0:T(8,128)(2,1)} %convolution_convert_fusion.3) | copy-start | bytes 1179652
  86.6 1.0 copy-start.14
  86.6 2.3 %copy-start.6 = (bf16[51,1,16,64]{3,2,1,0:T(8,128)(2,1)S(1)}, bf16[51,1,16,64]{3,2,1,0:T(8,128)(2,1)}, u32[]{:S(2)}) copy-start(bf16[51,1,16,64]{3,2,1,0:T(8,128)(2,1)} %copy-done.5) | copy-start | bytes 313348
  86.6 2.3 %copy-start.8 = (bf16[51,1,16,64]{3,2,1,0:T(8,128)(2,1)S(1)}, bf16[51,1,16,64]{3,2,1,0:T(8,128)(2,1)}, u32[]{:S(2)}) copy-start(bf16[51,1,16,64]{3,2,1,0:T(8,128)(2,1)} %copy-done.7) | copy-start | bytes 313348
  88.9 1.7 %copy-start.16 = (f32[16,51,51]{1,2,0:T(8,128)S(1)}, f32[16,51,51]{1,2,0:T(8,128)}, u32[]{:S(2)}) copy-start(f32[16,51,51]{1,2,0:T(8,128)} %copy-done.15) | copy-start | bytes 499396
  91.0 0.6 copy-start.22
  98.4 6.4 %collective-permute-start.5 = (bf16[51,1024]{1,0:T(8,128)(2,1)S(1)}, bf16[51,1024]{1,0:T(8,128)(2,1)S(1)}, u32[]{:S(2)}, u32[]{:S(2)}) collective-permute-start(bf16[51,1024]{1,0:T(8,128)(2,1)S(1)} %fusion.105), channel_id=1, source_target_pairs={{0,1},{1,2},{2,3},{3,0},{4,5},{5,6},{6,7},{7,4},{8,9},{9,10},{10,1... | collective-permute-start | bytes 313352 | tf_op jit(solution)/shard_map/ppermute | solution.py:134
  99.1 6.2 %collective-permute-start.4 = (bf16[51,1024]{1,0:T(8,128)(2,1)S(1)}, bf16[51,1024]{1,0:T(8,128)(2,1)S(1)}, u32[]{:S(2)}, u32[]{:S(2)}) collective-permute-start(bf16[51,1024]{1,0:T(8,128)(2,1)S(1)} %fusion.105), channel_id=1, source_target_pairs={{0,2},{1,3},{2,0},{3,1},{4,6},{5,7},{6,4},{7,5},{8,10},{9,11},{10,... | collective-permute-start | bytes 313352 | tf_op jit(solution)/shard_map/ppermute | solution.py:134
  99.6 5.7 %collective-permute-start.3 = (bf16[51,1024]{1,0:T(8,128)(2,1)S(1)}, bf16[51,1024]{1,0:T(8,128)(2,1)S(1)}, u32[]{:S(2)}, u32[]{:S(2)}) collective-permute-start(bf16[51,1024]{1,0:T(8,128)(2,1)S(1)} %fusion.105), channel_id=1, source_target_pairs={{0,3},{1,0},{2,1},{3,2},{4,7},{5,4},{6,5},{7,6},{8,11},{9,8},{10,9... | collective-permute-start | bytes 313352 | tf_op jit(solution)/shard_map/ppermute | solution.py:134

commit v11 on v7

--- a/solution.py
+++ b/solution.py
@@ -69,11 +69,8 @@
 
 def reuse_rows_bwd(saved, cotangent):
     inputs, w_qkv = saved
-    _, pullback = jax.vjp(
-        lambda rows: row_norm(rows.astype(jnp.float32)).astype(jnp.bfloat16), inputs
-    )
-    d_normed = jnp.dot(w_qkv, cotangent.T, preferred_element_type=jnp.float32).T
-    (d_inputs,) = pullback(d_normed.astype(jnp.bfloat16))
+    _, pullback = jax.vjp(lambda rows: project_rows(rows, w_qkv), inputs)
+    (d_inputs,) = pullback(cotangent)
     return d_inputs, jnp.zeros_like(w_qkv), jnp.zeros_like(cotangent)
 
 
@@ -104,9 +101,7 @@
         )
     activated = jax.nn.gelu(row_norm(convolved.reshape(total_rows, DD)), approximate=False)
     hidden = (lowered.astype(jnp.float32) + activated).astype(jnp.bfloat16)
-    return lax.optimization_barrier(
-        jnp.dot(hidden, dec_out, preferred_element_type=jnp.float32)
-    )
+    return jnp.dot(hidden, dec_out, preferred_element_type=jnp.float32)
 
 
 def copy_terms(

time: 89.2 us -> 79.1 us (0.89)
  local copies, waits for them, and re-layouts: 18.6 us -> 12.4 us
  other arithmetic: 13.5 us -> 9.67 us
    dot_general x2, matrix products: 3.13 us -> 8.57 us  [decoder_output(): return jnp.dot(hidden, dec_out, preferred_element_type=jnp.float32)]
    another operation x1 -> x0, other arithmetic: 3.03 us -> none  [decoder_output(): jax.nn.gelu(row_norm(convolved.reshape(total_rows, DD)), approximate=False)]
    dot_general x6, matrix products: 4.62 us -> 2.76 us  [decoder_output(): jnp.einsum('pgi,gio->pgo', padded[offset:offset + total_rows], conv_w[off...]
    reshape x2, local copies, waits for them, and re-layouts: 2.73 us -> 0.87 us  [attention_from(): context = split_project(projected.reshape(row_count, 3, HEADS, D // HEADS))]
    unnamed x105 -> x71, local copies, waits for them, and re-layouts: 3.64 us -> 2.23 us
    slice x1, local copies, waits for them, and re-layouts: 1.25 us -> 0.11 us  [split_project(): projected[:, 0].astype(jnp.float32)]
    reshape x1, local copies, waits for them, and re-layouts: 2.29 us -> 1.15 us  [decoder_output(): convolved.reshape(total_rows, DD)]
    reduce_sum x1 -> x0, other arithmetic: 1.11 us -> none  [copy_terms(): return jnp.sum(mismatch * mismatch)]
where the time goes in v11:
time: 79.1 us; the launch traced here: 78.7 us
  matrix products  40.3 us (51%)
  local copies, waits for them, and re-layouts  12.4 us (16%)
  other arithmetic  9.67 us (12%)
  starting transfers between devices  8.16 us (10%)
  waiting for transfers between devices  4.92 us (6%)
  between operations  3.2 us (4%)
    dot_general x2, matrix products, decoder_output(): return jnp.dot(hidden, dec_out, preferred_element_type=jnp.float32)  8.57 us
    ppermute x6, starting transfers between devices, ring_gather(): parts.append(lax.ppermute(values, 'mask', pairs))  8.16 us
    dot_general x1, matrix products, copy_terms(): branch = attention_from(reuse_rows(visible_in, w_qkv, projected), w_out)  5 us
    ppermute x6, waiting for transfers between devices, ring_gather(): parts.append(lax.ppermute(values, 'mask', pairs))  4.92 us
    dot_general x2, matrix products, decoder_output(): jnp.dot(visible_out, dec_in, preferred_element_type=jnp.float32)  4.57 us
    dot_general x1, matrix products, project_rows(): jnp.dot(normed, w_qkv, preferred_element_type=jnp.float32)  3.1 us
    dot_general x4, matrix products, mix_heads(): jnp.einsum('hqk,khd->qhd', weights, values, preferred_element_type=jnp.fl...  2.83 us
    reduce_sum x1, other arithmetic, row_norm(): centred = values - average  2.76 us
  transfers between devices with their start and end apart: 6, of which 3 were waited for; matrix products, arithmetic and copies ran while one was open for 7% of the time, Pallas kernels for 0%

profile of v11, /device:TPU:0, one launch (start us, length us, event | category | flops | bytes accessed | tf_op | source)
XLA Modules:
  0.0 78.7 jit_solution(624255757404109492)
XLA Ops:
  0.6 3.0 %collective-permute-start = (bf16[64,768]{1,0:T(8,128)(2,1)}, bf16[64,768]{1,0:T(8,128)(2,1)S(1)}, u32[]{:S(2)}, u32[]{:S(2)}) collective-permute-start(bf16[64,768]{1,0:T(8,128)(2,1)} %param.9), channel_id=1, source_target_pairs={{0,1},{1,2},{2,3},{3,0},{4,5},{5,6},{6,7},{7,4},{8,9},{9,10},{10,1... | collective-permute-start | bytes 294920 | tf_op jit(solution)/shard_map/ppermute | solution.py:129
  3.7 1.5 %collective-permute-start.1 = (bf16[64,768]{1,0:T(8,128)(2,1)}, bf16[64,768]{1,0:T(8,128)(2,1)S(1)}, u32[]{:S(2)}, u32[]{:S(2)}) collective-permute-start(bf16[64,768]{1,0:T(8,128)(2,1)} %param.9), channel_id=1, source_target_pairs={{0,2},{1,3},{2,0},{3,1},{4,6},{5,7},{6,4},{7,5},{8,10},{9,11},{10,... | collective-permute-start | bytes 294920 | tf_op jit(solution)/shard_map/ppermute | solution.py:129
  5.2 1.4 %collective-permute-start.2 = (bf16[64,768]{1,0:T(8,128)(2,1)}, bf16[64,768]{1,0:T(8,128)(2,1)S(1)}, u32[]{:S(2)}, u32[]{:S(2)}) collective-permute-start(bf16[64,768]{1,0:T(8,128)(2,1)} %param.9), channel_id=1, source_target_pairs={{0,3},{1,0},{2,1},{3,2},{4,7},{5,4},{6,5},{7,6},{8,11},{9,8},{10,9... | collective-permute-start | bytes 294920 | tf_op jit(solution)/shard_map/ppermute | solution.py:129
  8.8 1.2 %gather_fusion = s32[4,51]{1,0:T(4,128)S(1)} fusion(s32[4,51]{1,0:T(4,128)} %param.10, s32[1024]{0:T(1024)S(1)} %pad_clamp_fusion), kind=kCustom, calls=%fused_computation | custom fusion | bytes 1648 | tf_op jit(solution)/shard_map/gather | solution.py:213
  10.6 1.9 %convolution_reduce_fusion = bf16[768]{0:T(1024)(128)(2,1)S(1)} fusion(bf16[1024,1]{0,1:T(2,128)(2,1)S(1)} %reshape.270, bf16[1024,768]{1,0:T(8,128)(2,1)} %param.15), kind=kOutput, calls=%fused_computation.58 | convolution fusion | flops 1572864 | bytes 1576448 | tf_op jit(solution)/shard_map/jvp()/dot_general | solution.py:87
  12.5 1.3 %select_select_fusion.3 = (bf16[64,768]{1,0:T(8,128)(2,1)S(1)}, bf16[64,768]{1,0:T(8,128)(2,1)S(1)}, bf16[64,768]{1,0:T(8,128)(2,1)S(1)}, bf16[64,768]{1,0:T(8,128)(2,1)S(1)}) fusion(bf16[64,768]{1,0:T(8,128)(2,1)S(1)} %collective-permute-done, bf16[64,768]{1,0:T(8,128)(2,1)S(1)} %collective-permute-done.1, bf16[64,768]{1,0:T(8,128)(2,1)S(1)} %collective-permute-done.2, ...), kind=kLoop, calls=%fused_computation.182 | loop fusion | flops 589824 | bytes 786444 | tf_op jit(solution)/shard_map/jit(_where)/select_n | solution.py:140
  13.9 2.2 %convert_reduce_fusion = (f32[256]{0:T(256)S(1)}, bf16[256,1024]{1,0:T(8,128)(2,1)S(1)}) fusion(bf16[768,1024]{1,0:T(8,128)(2,1)} %param.11, bf16[64,768]{1,0:T(8,128)(2,1)S(1)} %get-tuple-element.14, bf16[64,768]{1,0:T(8,128)(2,1)S(1)} %get-tuple-element.15, bf16[64,768]{1,0:T(8,128)(2,1)S(1)} %get-tuple-element.16, bf16[64,768]{1,0:T(8,128)(2,1)S(1)} %get-tuple-element.13), kind=kOutput, calls=%fused_computation.14 | convolution fusion | flops 405012224 | bytes 2491392 | tf_op jit(solution)/shard_map/dot_general | solution.py:175
  16.4 3.1 %convolution_convert_fusion = bf16[256,3072]{1,0:T(8,128)(2,1)} fusion(bf16[1024,3072]{1,0:T(8,128)(2,1)S(1)} %copy-done.2, bf16[256,1024]{1,0:T(8,128)(2,1)S(1)} %get-tuple-element.22, f32[256]{0:T(256)S(1)} %add_rsqrt_fusion.3, f32[256]{0:T(256)S(1)} %broadcast_multiply_fusion.3), kind=kOutput, calls=%fused_computation.3 | convolution fusion | flops 1612447744 | bytes 8390656 | tf_op jit(solution)/shard_map/dot_general | solution.py:48
  19.5 2.6 %copy.62 = bf16[256,3072]{0,1:T(8,128)(2,1)} copy(bf16[256,3072]{1,0:T(8,128)(2,1)} %convolution_convert_fusion) | data formatting | bytes 3145728 | tf_op jit(solution)/shard_map/convert_element_type | solution.py:48
  22.1 1.9 %convolution_convert_fusion.1 = bf16[51,3072]{1,0:T(8,128)(2,1)S(1)} fusion(bf16[256,3072]{1,0:T(8,128)(2,1)} %convolution_convert_fusion, s32[51]{0:T(128)S(1)} %dynamic-slice_bitcast_fusion), kind=kOutput, calls=%fused_computation.5 | convolution fusion | flops 80385792 | bytes 1886412 | tf_op jit(solution)/shard_map/dot_general | solution.py:186
  24.0 0.9 %fusion.137 = (f32[51]{0:T(128)}, f32[51,1024]{1,0:T(8,128)S(1)}) fusion(bf16[256,1024]{1,0:T(8,128)(2,1)S(1)} %get-tuple-element.22, s32[51]{0:T(128)S(1)} %dynamic-slice_bitcast_fusion), kind=kOutput, calls=%fused_computation.240 | convolution fusion | flops 26908364 | bytes 733592 | tf_op jit(solution)/shard_map/dot_general | solution.py:180
  25.2 1.0 %fusion = (f32[16,256]{1,0:T(8,128)S(1)}, f32[16,256,256]{1,2,0:T(8,128)S(1)}) fusion(f32[256,16]{0,1:T(8,128)S(1)} %get-tuple-element.46, bf16[256,3,16,64]{0,3,2,1:T(8,128)(2,1)S(1)} %bitcast.165, f32[256,16]{0,1:T(8,128)S(1)} %get-tuple-element.47), kind=kOutput, calls=%fused_computation.4 | convolution fusion | flops 137883648 | bytes 5292032 | tf_op jit(solution)/shard_map/qhd,khd->hqk/dot_general | solution.py:31
  26.2 0.9 %fusion.3 = bf16[16,64,256]{2,1,0:T(8,128)(2,1)S(1)} fusion(f32[16,256,256]{1,2,0:T(8,128)S(1)} %get-tuple-element.24, f32[16,256]{1,0:T(8,128)S(1)} %get-tuple-element.23, bf16[256,3,16,64]{0,3,2,1:T(8,128)(2,1)S(1)} %bitcast.166), kind=kOutput, calls=%fused_computation.15 | convolution fusion | flops 137625600 | bytes 5259264 | tf_op jit(solution)/shard_map/hqk,khd->qhd/dot_general | solution.py:36
  27.9 1.0 %copy-done.3 = f32[256,1024]{1,0:T(8,128)} copy-done((f32[256,1024]{1,0:T(8,128)}, f32[256,1024]{1,0:T(8,128)S(1)}, u32[]{:S(2)}) %copy-start.3) | copy-done | bytes 1048600
  32.1 2.3 %convolution_convert_fusion.18 = bf16[51,768]{1,0:T(8,128)(2,1)S(1)} fusion(bf16[1024,768]{1,0:T(8,128)(2,1)} %param.15, f32[51,1024]{1,0:T(8,128)S(1)} %get-tuple-element.34, bf16[51,1024]{1,0:T(8,128)(2,1)S(1)} %reshape.248, bf16[1024,1024]{1,0:T(8,128)(2,1)S(1)} %copy-done), kind=kOutput, calls=%fused_computation.56 | convolution fusion | flops 187314432 | bytes 4061696 | tf_op jit(solution)/shard_map/jvp()/dot_general | solution.py:84
  34.4 1.1 %fusion.4 = bf16[256,768]{1,0:T(8,128)(2,1)} fusion(bf16[51,768]{1,0:T(8,128)(2,1)S(1)} %convolution_convert_fusion.18, bf16[768]{0:T(1024)(128)(2,1)S(1)} %convolution_reduce_fusion, pred[256]{0:T(512)(128)(4,1)S(1)} %broadcast_compare_fusion, s32[51]{0:T(128)S(1)} %dynamic-slice_bitcast_fusion), kind=kOutput, calls=%fused_computation.20 | convolution fusion | flops 20263680 | bytes 473548 | tf_op jit(solution)/shard_map/jvp()/dot_general | solution.py:90
  35.5 1.2 %copy.57 = bf16[256,768]{0,1:T(8,128)(2,1)S(1)} copy(bf16[256,768]{1,0:T(8,128)(2,1)} %fusion.4) | data formatting | bytes 786432 | tf_op jit(solution)/shard_map/jvp()/convert_element_type | solution.py:91
  37.4 1.4 %fusion.136 = (f32[256]{0:T(256)S(1)}, f32[16,256,48]{1,2,0:T(8,128)S(1)}) fusion(f32[16,256,48]{1,2,0:T(8,128)S(1)} %convolution_add_fusion.1, bf16[256,16,48]{0,2,1:T(8,128)(2,1)S(1)} %bitcast.173, bf16[3,16,48,48]{3,2,1,0:T(8,128)(2,1)} %param.16), kind=kOutput, calls=%fused_computation.239 | convolution fusion | flops 19267328 | bytes 2163712 | tf_op jit(solution)/shard_map/jvp(pgi,gio->pgo)/dot_general | solution.py:96
  39.5 1.1 %copy.61 = f32[256,768]{1,0:T(8,128)} copy(f32[256,768]{0,1:T(8,128)S(1)} %bitcast.167) | data formatting | bytes 1572864 | tf_op jit(solution)/shard_map/jvp()/reshape | solution.py:102
  40.7 5.2 %multiply_reduce_fusion = (f32[]{:T(128)}, f32[256,1024]{1,0:T(8,128)S(1)}) fusion(f32[256]{0:T(256)} %get-tuple-element.18, f32[256]{0:T(256)} %add_rsqrt_fusion.2, f32[256,1024]{1,0:T(8,128)} %copy-done.3, f32[256]{0:T(256)} %copy-done.28, bf16[768,1024]{1,0:T(8,128)(2,1)} %param.17, bf16[256,768]{1,0:T(8,128)(2,1)S(1)} %copy-done.24, ...), kind=kOutput, calls=%fused_computation.67 | convolution fusion | flops 418709504 | bytes 4854788 | tf_op jit(solution)/shard_map/jvp()/dot_general | solution.py:104
  46.0 3.3 %multiply_reduce_fusion.2 = (f32[256]{0:T(256)S(1)}, bf16[256,768]{1,0:T(8,128)(2,1)S(1)}) fusion(f32[256,768]{1,0:T(8,128)S(1)} %copy-done.4, f32[256]{0:T(256)S(1)} %broadcast_multiply_fusion.1, f32[256]{0:T(256)S(1)} %copy-done.27, bf16[768,1024]{1,0:T(8,128)(2,1)S(1)} %copy-done.34, f32[256,1024]{1,0:T(8,128)S(1)} %get-tuple-element.43, ...), kind=kOutput, calls=%fused_computation.92 | convolution fusion | flops 419495680 | bytes 3805184 | tf_op jit(solution)/shard_map/transpose(jvp())/dot_general | solution.py:104
  49.3 2.8 %fusion.132 = (f32[256]{0:T(256)S(1)}, f32[256,768]{1,0:T(8,128)S(1)}) fusion(f32[256]{0:T(256)S(1)} %multiply_multiply_fusion.8, bf16[256,768]{1,0:T(8,128)(2,1)S(1)} %get-tuple-element.32, f32[256]{0:T(256)S(1)} %copy-done.27, f32[256,768]{1,0:T(8,128)S(1)} %copy-done.4, f32[256]{0:T(256)S(1)} %broadcast_multiply_fusion.1), kind=kLoop, calls=%fused_computation.235 | loop fusion | flops 15531776 | bytes 1970176 | tf_op jit(solution)/shard_map/transpose(jvp())/reduce_sum | solution.py:19
  52.1 0.8 %broadcast_add_fusion = bf16[256,768]{1,0:T(8,128)(2,1)} fusion(f32[256,768]{1,0:T(8,128)S(1)} %get-tuple-element.9, f32[256]{0:T(256)S(1)} %negate_multiply_fusion.1), kind=kLoop, calls=%fused_computation.144 | loop fusion | flops 393216 | bytes 1180672 | tf_op jit(solution)/shard_map/transpose(jvp())/add_any | solution.py:18
  53.0 1.2 %copy.64 = bf16[256,768]{0,1:T(8,128)(2,1)S(1)} copy(bf16[256,768]{1,0:T(8,128)(2,1)} %broadcast_add_fusion) | data formatting | bytes 786432 | tf_op jit(solution)/shard_map/transpose(jvp())/add_any | solution.py:18
  55.5 2.3 %convolution_convert_fusion.13 = bf16[51,1024]{1,0:T(8,128)(2,1)S(1)} fusion(bf16[1024,768]{1,0:T(8,128)(2,1)} %param.15, bf16[256,768]{1,0:T(8,128)(2,1)} %copy-done.11, bf16[256,768]{1,0:T(8,128)(2,1)S(1)} %copy.68, pred[256]{0:T(512)(128)(4,1)S(1)} %copy-done.32, s32[51]{0:T(128)S(1)} %copy-done.26), kind=kOutput, calls=%fused_computation.49 | convolution fusion | flops 100964352 | bytes 2464204 | tf_op jit(solution)/shard_map/transpose(jvp())/dot_general | solution.py:84
  58.8 1.4 %fusion.17 = bf16[51,1,16,64]{3,0,2,1:T(8,128)(2,1)S(1)} fusion(bf16[51,16,64]{2,1,0:T(8,128)(2,1)S(1)} %reshape.255, f32[16,51,51]{1,2,0:T(8,128)} %copy-done.14, f32[16,51]{1,0:T(8,128)S(1)} %get-tuple-element.27), kind=kOutput, calls=%fused_computation.45 | convolution fusion | flops 5462304 | bytes 378624 | tf_op jit(solution)/shard_map/transpose(jvp(hqk,khd->qhd))/dot_general | solution.py:36
  63.0 5.0 %multiply_reduce_fusion.5 = (f32[51]{0:T(128)S(1)}, f32[51]{0:T(128)S(1)}, f32[51,1024]{1,0:T(8,128)S(1)}) fusion(f32[51,1024]{1,0:T(8,128)S(1)} %get-tuple-element.34, f32[51]{0:T(128)S(1)} %broadcast_multiply_fusion.4, bf16[51,3072]{1,0:T(8,128)(2,1)S(1)} %reshape.256, bf16[1024,3072]{1,0:T(8,128)(2,1)} %param.12), kind=kOutput, calls=%fused_computation.160 | convolution fusion | flops 321229696 | bytes 7023204 | tf_op jit(solution)/shard_map/transpose(jvp(transpose(jvp())))/dot_general | solution.py:114
  68.9 1.5 %collective-permute-start.4 = (bf16[51,1024]{1,0:T(8,128)(2,1)S(1)}, bf16[51,1024]{1,0:T(8,128)(2,1)S(1)}, u32[]{:S(2)}, u32[]{:S(2)}) collective-permute-start(bf16[51,1024]{1,0:T(8,128)(2,1)S(1)} %fusion.106), channel_id=1, source_target_pairs={{0,2},{1,3},{2,0},{3,1},{4,6},{5,7},{6,4},{7,5},{8,10},{9,11},{10,... | collective-permute-start | bytes 313352 | tf_op jit(solution)/shard_map/ppermute | solution.py:129
  71.2 2.6 %collective-permute-done.3 = bf16[51,1024]{1,0:T(8,128)(2,1)S(1)} collective-permute-done((bf16[51,1024]{1,0:T(8,128)(2,1)S(1)}, bf16[51,1024]{1,0:T(8,128)(2,1)S(1)}, u32[]{:S(2)}, u32[]{:S(2)}) %collective-permute-start.3) | collective-permute-done | bytes 104480 | tf_op jit(solution)/shard_map/ppermute | solution.py:129
  73.9 1.0 %collective-permute-done.4 = bf16[51,1024]{1,0:T(8,128)(2,1)S(1)} collective-permute-done((bf16[51,1024]{1,0:T(8,128)(2,1)S(1)}, bf16[51,1024]{1,0:T(8,128)(2,1)S(1)}, u32[]{:S(2)}, u32[]{:S(2)}) %collective-permute-start.4) | collective-permute-done | bytes 104480 | tf_op jit(solution)/shard_map/ppermute | solution.py:129
  74.9 1.3 %collective-permute-done.5 = bf16[51,1024]{1,0:T(8,128)(2,1)S(1)} collective-permute-done((bf16[51,1024]{1,0:T(8,128)(2,1)S(1)}, bf16[51,1024]{1,0:T(8,128)(2,1)S(1)}, u32[]{:S(2)}, u32[]{:S(2)}) %collective-permute-start.5) | collective-permute-done | bytes 104480 | tf_op jit(solution)/shard_map/ppermute | solution.py:129
  76.1 1.4 %fusion.21 = f32[192,1024]{1,0:T(8,128)} fusion(bf16[51,1024]{1,0:T(8,128)(2,1)S(1)} %collective-permute-done.5, bf16[51,1024]{1,0:T(8,128)(2,1)S(1)} %collective-permute-done.4, bf16[51,1024]{1,0:T(8,128)(2,1)S(1)} %collective-permute-done.3, bf16[51,1024]{1,0:T(8,128)(2,1)S(1)} %fusion.106, bf16[256,768]{1,0:T(8,128)(2,1)S(1)} %pad_maximum_fusion, ...), kind=kOutput, calls=%fused_computation.57 | convolution fusion | flops 102032640 | bytes 1377284 | tf_op jit(solution)/shard_map/vc,vd->cd/dot_general | solution.py:219
  (133 shorter events, 14.7 us)
Async XLA Ops:
  0.6 26.4 %copy-start = (bf16[1024,1024]{1,0:T(8,128)(2,1)S(1)}, bf16[1024,1024]{1,0:T(8,128)(2,1)}, u32[]{:S(2)}) copy-start(bf16[1024,1024]{1,0:T(8,128)(2,1)} %param.13) | copy-start | bytes 6291460
  0.6 11.8 %collective-permute-start = (bf16[64,768]{1,0:T(8,128)(2,1)}, bf16[64,768]{1,0:T(8,128)(2,1)S(1)}, u32[]{:S(2)}, u32[]{:S(2)}) collective-permute-start(bf16[64,768]{1,0:T(8,128)(2,1)} %param.9), channel_id=1, source_target_pairs={{0,1},{1,2},{2,3},{3,0},{4,5},{5,6},{6,7},{7,4},{8,9},{9,10},{10,1... | collective-permute-start | bytes 294920 | tf_op jit(solution)/shard_map/ppermute | solution.py:129
  3.7 8.8 %collective-permute-start.1 = (bf16[64,768]{1,0:T(8,128)(2,1)}, bf16[64,768]{1,0:T(8,128)(2,1)S(1)}, u32[]{:S(2)}, u32[]{:S(2)}) collective-permute-start(bf16[64,768]{1,0:T(8,128)(2,1)} %param.9), channel_id=1, source_target_pairs={{0,2},{1,3},{2,0},{3,1},{4,6},{5,7},{6,4},{7,5},{8,10},{9,11},{10,... | collective-permute-start | bytes 294920 | tf_op jit(solution)/shard_map/ppermute | solution.py:129
  5.2 7.3 %collective-permute-start.2 = (bf16[64,768]{1,0:T(8,128)(2,1)}, bf16[64,768]{1,0:T(8,128)(2,1)S(1)}, u32[]{:S(2)}, u32[]{:S(2)}) collective-permute-start(bf16[64,768]{1,0:T(8,128)(2,1)} %param.9), channel_id=1, source_target_pairs={{0,3},{1,0},{2,1},{3,2},{4,7},{5,4},{6,5},{7,6},{8,11},{9,8},{10,9... | collective-permute-start | bytes 294920 | tf_op jit(solution)/shard_map/ppermute | solution.py:129
  7.3 27.1 %copy-start.25 = (s32[51]{0:T(128)}, s32[51]{0:T(128)S(1)}, u32[]{:S(2)}) copy-start(s32[51]{0:T(128)S(1)} %dynamic-slice_bitcast_fusion) | copy-start | bytes 616
  7.5 26.9 %copy-start.31 = (pred[256]{0:T(512)(128)(4,1)}, pred[256]{0:T(512)(128)(4,1)S(1)}, u32[]{:S(2)}) copy-start(pred[256]{0:T(512)(128)(4,1)S(1)} %broadcast_compare_fusion) | copy-start | bytes 772
  10.6 5.8 %copy-start.2 = (bf16[1024,3072]{1,0:T(8,128)(2,1)S(1)}, bf16[1024,3072]{1,0:T(8,128)(2,1)}, u32[]{:S(2)}) copy-start(bf16[1024,3072]{1,0:T(8,128)(2,1)} %param.12) | copy-start | bytes 18874372
  13.8 2.5 %copy-start.16 = (bf16[64,768]{1,0:T(8,128)(2,1)}, bf16[64,768]{1,0:T(8,128)(2,1)S(1)}, u32[]{:S(2)}) copy-start(bf16[64,768]{1,0:T(8,128)(2,1)S(1)} %get-tuple-element.13) | copy-start | bytes 294916
  13.8 2.5 %copy-start.18 = (bf16[64,768]{1,0:T(8,128)(2,1)}, bf16[64,768]{1,0:T(8,128)(2,1)S(1)}, u32[]{:S(2)}) copy-start(bf16[64,768]{1,0:T(8,128)(2,1)S(1)} %get-tuple-element.14) | copy-start | bytes 294916
  13.8 2.5 %copy-start.20 = (bf16[64,768]{1,0:T(8,128)(2,1)}, bf16[64,768]{1,0:T(8,128)(2,1)S(1)}, u32[]{:S(2)}) copy-start(bf16[64,768]{1,0:T(8,128)(2,1)S(1)} %get-tuple-element.15) | copy-start | bytes 294916
  13.9 2.5 %copy-start.22 = (bf16[64,768]{1,0:T(8,128)(2,1)}, bf16[64,768]{1,0:T(8,128)(2,1)S(1)}, u32[]{:S(2)}) copy-start(bf16[64,768]{1,0:T(8,128)(2,1)S(1)} %get-tuple-element.16) | copy-start | bytes 294916
  22.1 2.8 %copy-start.1 = (bf16[256,3072]{0,1:T(8,128)(2,1)S(1)}, bf16[256,3072]{0,1:T(8,128)(2,1)}, u32[]{:S(2)}) copy-start(bf16[256,3072]{0,1:T(8,128)(2,1)} %copy.62) | copy-start | bytes 4718596
  27.9 2.3 %copy-start.28 = (f32[256]{0:T(256)}, f32[256]{0:T(256)S(1)}, u32[]{:S(2)}) copy-start(f32[256]{0:T(256)S(1)} %broadcast_multiply_fusion.2) | copy-start | bytes 3076
  30.2 1.9 %copy-start.7 = (bf16[51,1,16,64]{3,2,1,0:T(8,128)(2,1)}, bf16[51,1,16,64]{3,2,1,0:T(8,128)(2,1)S(1)}, u32[]{:S(2)}) copy-start(bf16[51,1,16,64]{3,2,1,0:T(8,128)(2,1)S(1)} %get-tuple-element.10) | copy-start | bytes 313348
  30.2 1.9 %copy-start.9 = (bf16[51,1,16,64]{3,2,1,0:T(8,128)(2,1)}, bf16[51,1,16,64]{3,2,1,0:T(8,128)(2,1)S(1)}, u32[]{:S(2)}) copy-start(bf16[51,1,16,64]{3,2,1,0:T(8,128)(2,1)S(1)} %get-tuple-element.12) | copy-start | bytes 313348
  32.1 4.6 %copy-start.5 = (bf16[3,16,48,48]{3,2,1,0:T(8,128)(2,1)S(1)}, bf16[3,16,48,48]{3,2,1,0:T(8,128)(2,1)}, u32[]{:S(2)}) copy-start(bf16[3,16,48,48]{3,2,1,0:T(8,128)(2,1)} %param.16) | copy-start | bytes 663556
  38.8 1.9 %copy-start.24 = (bf16[256,768]{1,0:T(8,128)(2,1)S(1)}, bf16[256,768]{1,0:T(8,128)(2,1)}, u32[]{:S(2)}) copy-start(bf16[256,768]{1,0:T(8,128)(2,1)} %fusion.4) | copy-start | bytes 1179652
  40.7 5.3 %copy-start.4 = (f32[256,768]{1,0:T(8,128)S(1)}, f32[256,768]{1,0:T(8,128)}, u32[]{:S(2)}) copy-start(f32[256,768]{1,0:T(8,128)} %copy.61) | copy-start | bytes 2359300
  40.7 5.3 %copy-start.27 = (f32[256]{0:T(256)S(1)}, f32[256]{0:T(256)}, u32[]{:S(2)}) copy-start(f32[256]{0:T(256)} %fusion.118) | copy-start | bytes 3076
  40.7 5.3 %copy-start.30 = (f32[256]{0:T(256)S(1)}, f32[256]{0:T(256)}, u32[]{:S(2)}) copy-start(f32[256]{0:T(256)} %get-tuple-element.17) | copy-start | bytes 3076
  40.7 5.3 %copy-start.34 = (bf16[768,1024]{1,0:T(8,128)(2,1)S(1)}, bf16[768,1024]{1,0:T(8,128)(2,1)}, u32[]{:S(2)}) copy-start(bf16[768,1024]{1,0:T(8,128)(2,1)} %param.17) | copy-start | bytes 4718596
  49.3 2.8 %copy-start.11 = (bf16[256,768]{1,0:T(8,128)(2,1)}, bf16[256,768]{1,0:T(8,128)(2,1)S(1)}, u32[]{:S(2)}) copy-start(bf16[256,768]{1,0:T(8,128)(2,1)S(1)} %get-tuple-element.32) | copy-start | bytes 1179652
  49.3 4.8 %copy-start.6 = (bf16[3,16,48,48]{3,2,1,0:T(8,128)(2,1)S(1)}, bf16[3,16,48,48]{3,2,1,0:T(8,128)(2,1)}, u32[]{:S(2)}) copy-start(bf16[3,16,48,48]{3,2,1,0:T(8,128)(2,1)} %param.16) | copy-start | bytes 663556
  57.8 2.3 %copy-start.13 = (bf16[51,1,16,64]{3,2,1,0:T(8,128)(2,1)S(1)}, bf16[51,1,16,64]{3,2,1,0:T(8,128)(2,1)}, u32[]{:S(2)}) copy-start(bf16[51,1,16,64]{3,2,1,0:T(8,128)(2,1)} %copy-done.12) | copy-start | bytes 313348
  62.9 8.2 %copy-start.17 = (bf16[64,768]{1,0:T(8,128)(2,1)S(1)}, bf16[64,768]{1,0:T(8,128)(2,1)}, u32[]{:S(2)}) copy-start(bf16[64,768]{1,0:T(8,128)(2,1)} %copy-done.16) | copy-start | bytes 294916
  62.9 8.2 %copy-start.19 = (bf16[64,768]{1,0:T(8,128)(2,1)S(1)}, bf16[64,768]{1,0:T(8,128)(2,1)}, u32[]{:S(2)}) copy-start(bf16[64,768]{1,0:T(8,128)(2,1)} %copy-done.18) | copy-start | bytes 294916
  62.9 8.2 %copy-start.21 = (bf16[64,768]{1,0:T(8,128)(2,1)S(1)}, bf16[64,768]{1,0:T(8,128)(2,1)}, u32[]{:S(2)}) copy-start(bf16[64,768]{1,0:T(8,128)(2,1)} %copy-done.20) | copy-start | bytes 294916
  62.9 8.2 %copy-start.23 = (bf16[64,768]{1,0:T(8,128)(2,1)S(1)}, bf16[64,768]{1,0:T(8,128)(2,1)}, u32[]{:S(2)}) copy-start(bf16[64,768]{1,0:T(8,128)(2,1)} %copy-done.22) | copy-start | bytes 294916
  62.9 13.2 %copy-start.29 = (s32[204]{0:T(256)S(1)}, s32[204]{0:T(256)}, u32[]{:S(2)}) copy-start(s32[204]{0:T(256)} %eq.93) | copy-start | bytes 2452
  68.3 5.5 %collective-permute-start.3 = (bf16[51,1024]{1,0:T(8,128)(2,1)S(1)}, bf16[51,1024]{1,0:T(8,128)(2,1)S(1)}, u32[]{:S(2)}, u32[]{:S(2)}) collective-permute-start(bf16[51,1024]{1,0:T(8,128)(2,1)S(1)} %fusion.106), channel_id=1, source_target_pairs={{0,3},{1,0},{2,1},{3,2},{4,7},{5,4},{6,5},{7,6},{8,11},{9,8},{10,9... | collective-permute-start | bytes 313352 | tf_op jit(solution)/shard_map/ppermute | solution.py:129
  68.9 6.0 %collective-permute-start.4 = (bf16[51,1024]{1,0:T(8,128)(2,1)S(1)}, bf16[51,1024]{1,0:T(8,128)(2,1)S(1)}, u32[]{:S(2)}, u32[]{:S(2)}) collective-permute-start(bf16[51,1024]{1,0:T(8,128)(2,1)S(1)} %fusion.106), channel_id=1, source_target_pairs={{0,2},{1,3},{2,0},{3,1},{4,6},{5,7},{6,4},{7,5},{8,10},{9,11},{10,... | collective-permute-start | bytes 313352 | tf_op jit(solution)/shard_map/ppermute | solution.py:129
  70.4 5.7 %collective-permute-start.5 = (bf16[51,1024]{1,0:T(8,128)(2,1)S(1)}, bf16[51,1024]{1,0:T(8,128)(2,1)S(1)}, u32[]{:S(2)}, u32[]{:S(2)}) collective-permute-start(bf16[51,1024]{1,0:T(8,128)(2,1)S(1)} %fusion.106), channel_id=1, source_target_pairs={{0,1},{1,2},{2,3},{3,0},{4,5},{5,6},{6,7},{7,4},{8,9},{9,10},{10,1... | collective-permute-start | bytes 313352 | tf_op jit(solution)/shard_map/ppermute | solution.py:129
  (9 other events, 11.1 us)

commit v12 on v11

--- a/solution.py
+++ b/solution.py
@@ -80,15 +80,15 @@
 def decoder_output(visible_out, positions, total_rows, mask_embed, dec_in, conv_w, dec_out):
     slot_ids = jnp.arange(total_rows, dtype=jnp.int32)
     picks = (slot_ids[:, None] == positions[None, :]).astype(jnp.bfloat16)
-    seen = jnp.max(picks, axis=1, keepdims=True)
-    lowered_visible = jnp.dot(visible_out, dec_in, preferred_element_type=jnp.float32).astype(
-        jnp.bfloat16
-    )
-    lowered_mask = jnp.dot(
-        mask_embed[None, :], dec_in, preferred_element_type=jnp.float32
-    ).astype(jnp.bfloat16)
-    placed = jnp.dot(picks, lowered_visible, preferred_element_type=jnp.float32)
-    lowered = jnp.where(seen > 0, placed, lowered_mask.astype(jnp.float32)).astype(jnp.bfloat16)
+    unseen = 1.0 - jnp.max(picks, axis=1, keepdims=True)
+    picks = jnp.concatenate([picks, unseen], axis=1)
+    distinct_rows = jnp.concatenate([visible_out, mask_embed[None, :]], axis=0)
+    lowered_rows = jnp.dot(distinct_rows, dec_in, preferred_element_type=jnp.float32).astype(
+        jnp.bfloat16
+    )
+    lowered = jnp.dot(picks, lowered_rows, preferred_element_type=jnp.float32).astype(
+        jnp.bfloat16
+    )
     grouped = lowered.reshape(total_rows, GROUPS, DD // GROUPS)
     padded = jnp.pad(grouped, ((1, 1), (0, 0), (0, 0)))
     convolved = jnp.zeros((total_rows, GROUPS, DD // GROUPS), jnp.float32)
@@ -210,7 +210,13 @@
     (grad_in,) = pullback(jnp.ones_like(squares) * factor)
     copy_loss = jnp.reshape(squares / ((total_rows - visible_count) * D), (1,))
     slot_copy = (own_index + jnp.arange(group_size, dtype=jnp.int32)) % group_size
-    flat_index = visible_index[slot_copy].reshape(copies * visible_count)
+    slot_rows = []
+    for slot in range(group_size):
+        chosen = visible_index[0]
+        for copy_id in range(1, copies):
+            chosen = jnp.where(slot_copy[slot] == copy_id, visible_index[copy_id], chosen)
+        slot_rows.append(chosen)
+    flat_index = jnp.concatenate(slot_rows, axis=0)
     own_cols = lax.dynamic_slice_in_dim(clip_pixels, own_index * col_width, col_width, 1)
     all_picks = (flat_index[:, None] == clip_ids[None, :]).astype(jnp.bfloat16)
     gathered = jnp.dot(all_picks, own_cols, preferred_element_type=jnp.float32).astype(

time: 79.1 us -> 88.5 us (1.12)
  between operations: 3.2 us -> 10.9 us
  other arithmetic: 9.67 us -> 11.8 us
  local copies, waits for them, and re-layouts: 12.4 us -> 11.2 us
    dot_general x1, matrix products: 3.1 us -> 5.83 us  [project_rows(): jnp.dot(normed, w_qkv, preferred_element_type=jnp.float32)]
    dot_general x4 -> x2, matrix products: 7.57 us -> 5 us  [the longest x1 2.79 us: decoder_output(): jnp.dot(picks, lowered_rows, preferred_element_type=jnp.float32)]
    select_n x1 -> x3, other arithmetic: 0.01 us -> 1.72 us  [the longest x2 1.71 us: on_device(): jnp.where(slot_copy[slot] == copy_id, visible_index[copy_id], chosen)]
    eq x2 -> x0, local copies, waits for them, and re-layouts: 1.28 us -> none  [the longest x1 0.69 us: decoder_output(): picks = (slot_ids[:, None] == positions[None, :]).astype(jnp.bfloat16)]
    gather x1 -> x0, local copies, waits for them, and re-layouts: 1.24 us -> none  [on_device(): flat_index = visible_index[slot_copy].reshape(copies * visible_count)]
    dot_general x2 -> x3, matrix products: 1.57 us -> 2.06 us  [attention_from(): jnp.dot(context.reshape(row_count, D), w_out, preferred_element_type=jnp....]
    unnamed x71 -> x80, local copies, waits for them, and re-layouts: 2.23 us -> 2.11 us
  transfers between devices with their start and end apart: 6 -> 6, of which waited for: 3 -> 3; matrix products, arithmetic and copies ran while one was open for 7% -> 5% of each run, Pallas kernels for 0% -> 0%
where the time goes in v12:
time: 88.5 us; the launch traced here: 87.9 us
  matrix products  41 us (46%)
  other arithmetic  11.8 us (13%)
  local copies, waits for them, and re-layouts  11.2 us (13%)
  between operations  10.9 us (12%)
  starting transfers between devices  8.15 us (9%)
  waiting for transfers between devices  4.92 us (6%)
    dot_general x2, matrix products, decoder_output(): return jnp.dot(hidden, dec_out, preferred_element_type=jnp.float32)  8.57 us
    ppermute x6, starting transfers between devices, ring_gather(): parts.append(lax.ppermute(values, 'mask', pairs))  8.15 us
    dot_general x1, matrix products, project_rows(): jnp.dot(normed, w_qkv, preferred_element_type=jnp.float32)  5.83 us
    dot_general x1, matrix products, copy_terms(): branch = attention_from(reuse_rows(visible_in, w_qkv, projected), w_out)  5 us
    ppermute x6, waiting for transfers between devices, ring_gather(): parts.append(lax.ppermute(values, 'mask', pairs))  4.92 us
    dot_general x4, matrix products, mix_heads(): jnp.einsum('hqk,khd->qhd', weights, values, preferred_element_type=jnp.fl...  2.82 us
    dot_general x1, matrix products, decoder_output(): jnp.dot(picks, lowered_rows, preferred_element_type=jnp.float32)  2.79 us
    dot_general x6, matrix products, decoder_output(): jnp.einsum('pgi,gio->pgo', padded[offset:offset + total_rows], conv_w[off...  2.76 us
  transfers between devices with their start and end apart: 6, of which 3 were waited for; matrix products, arithmetic and copies ran while one was open for 5% of the time, Pallas kernels for 0%

profile of v12, /device:TPU:0, one launch (start us, length us, event | category | flops | bytes accessed | tf_op | source)
XLA Modules:
  0.0 87.9 jit_solution(14950220552273793098)
XLA Ops:
  0.6 3.0 %collective-permute-start = (bf16[64,768]{1,0:T(8,128)(2,1)}, bf16[64,768]{1,0:T(8,128)(2,1)S(1)}, u32[]{:S(2)}, u32[]{:S(2)}) collective-permute-start(bf16[64,768]{1,0:T(8,128)(2,1)} %param.9), channel_id=1, source_target_pairs={{0,1},{1,2},{2,3},{3,0},{4,5},{5,6},{6,7},{7,4},{8,9},{9,10},{10,1... | collective-permute-start | bytes 294920 | tf_op jit(solution)/shard_map/ppermute | solution.py:129
  3.7 1.5 %collective-permute-start.1 = (bf16[64,768]{1,0:T(8,128)(2,1)}, bf16[64,768]{1,0:T(8,128)(2,1)S(1)}, u32[]{:S(2)}, u32[]{:S(2)}) collective-permute-start(bf16[64,768]{1,0:T(8,128)(2,1)} %param.9), channel_id=1, source_target_pairs={{0,2},{1,3},{2,0},{3,1},{4,6},{5,7},{6,4},{7,5},{8,10},{9,11},{10,... | collective-permute-start | bytes 294920 | tf_op jit(solution)/shard_map/ppermute | solution.py:129
  5.2 1.4 %collective-permute-start.2 = (bf16[64,768]{1,0:T(8,128)(2,1)}, bf16[64,768]{1,0:T(8,128)(2,1)S(1)}, u32[]{:S(2)}, u32[]{:S(2)}) collective-permute-start(bf16[64,768]{1,0:T(8,128)(2,1)} %param.9), channel_id=1, source_target_pairs={{0,3},{1,0},{2,1},{3,2},{4,7},{5,4},{6,5},{7,6},{8,11},{9,8},{10,9... | collective-permute-start | bytes 294920 | tf_op jit(solution)/shard_map/ppermute | solution.py:129
  10.9 0.9 fusion.114
  17.4 0.8 fusion.116
  18.8 1.0 %select_select_fusion.3 = (bf16[64,768]{1,0:T(8,128)(2,1)S(1)}, bf16[64,768]{1,0:T(8,128)(2,1)S(1)}, bf16[64,768]{1,0:T(8,128)(2,1)S(1)}, bf16[64,768]{1,0:T(8,128)(2,1)S(1)}) fusion(bf16[64,768]{1,0:T(8,128)(2,1)S(1)} %collective-permute-done, bf16[64,768]{1,0:T(8,128)(2,1)S(1)} %collective-permute-done.1, bf16[64,768]{1,0:T(8,128)(2,1)S(1)} %collective-permute-done.2, ...), kind=kLoop, calls=%fused_computation.179 | loop fusion | flops 589824 | bytes 786444 | tf_op jit(solution)/shard_map/jit(_where)/select_n | solution.py:140
  19.8 2.2 %convert_reduce_fusion = (f32[256]{0:T(256)S(1)}, bf16[256,1024]{1,0:T(8,128)(2,1)S(1)}) fusion(bf16[768,1024]{1,0:T(8,128)(2,1)} %param.11, bf16[64,768]{1,0:T(8,128)(2,1)S(1)} %get-tuple-element.14, bf16[64,768]{1,0:T(8,128)(2,1)S(1)} %get-tuple-element.15, bf16[64,768]{1,0:T(8,128)(2,1)S(1)} %get-tuple-element.16, bf16[64,768]{1,0:T(8,128)(2,1)S(1)} %get-tuple-element.13), kind=kOutput, calls=%fused_computation.13 | convolution fusion | flops 405012224 | bytes 2491392 | tf_op jit(solution)/shard_map/dot_general | solution.py:175
  22.4 5.8 %convolution_convert_fusion = bf16[256,3072]{1,0:T(8,128)(2,1)} fusion(bf16[1024,3072]{1,0:T(8,128)(2,1)} %param.12, bf16[256,1024]{1,0:T(8,128)(2,1)S(1)} %get-tuple-element.33, f32[256]{0:T(256)S(1)} %add_rsqrt_fusion.3, f32[256]{0:T(256)S(1)} %broadcast_multiply_fusion.3), kind=kOutput, calls=%fused_computation.2 | convolution fusion | flops 1612447744 | bytes 8390656 | tf_op jit(solution)/shard_map/dot_general | solution.py:48
  28.2 2.6 %copy.63 = bf16[256,3072]{0,1:T(8,128)(2,1)} copy(bf16[256,3072]{1,0:T(8,128)(2,1)} %convolution_convert_fusion) | data formatting | bytes 3145728 | tf_op jit(solution)/shard_map/convert_element_type | solution.py:48
  30.8 1.9 %convolution_convert_fusion.1 = bf16[51,3072]{1,0:T(8,128)(2,1)S(1)} fusion(bf16[256,3072]{1,0:T(8,128)(2,1)} %convolution_convert_fusion, s32[51]{0:T(128)S(1)} %get-tuple-element.19), kind=kOutput, calls=%fused_computation.4 | convolution fusion | flops 80385792 | bytes 1886412 | tf_op jit(solution)/shard_map/dot_general | solution.py:186
  32.7 0.9 fusion.135
  33.9 1.0 %fusion = (f32[16,256]{1,0:T(8,128)S(1)}, f32[16,256,256]{1,2,0:T(8,128)S(1)}) fusion(f32[256,16]{0,1:T(8,128)S(1)} %get-tuple-element.55, bf16[256,3,16,64]{0,3,2,1:T(8,128)(2,1)S(1)} %bitcast.179, f32[256,16]{0,1:T(8,128)S(1)} %get-tuple-element.56), kind=kOutput, calls=%fused_computation.3 | convolution fusion | flops 137883648 | bytes 5292032 | tf_op jit(solution)/shard_map/qhd,khd->hqk/dot_general | solution.py:31
  34.9 0.8 fusion.3
  35.7 0.8 fusion.136
  36.6 1.0 %copy-done.2 = f32[256,1024]{1,0:T(8,128)} copy-done((f32[256,1024]{1,0:T(8,128)}, f32[256,1024]{1,0:T(8,128)S(1)}, u32[]{:S(2)}) %copy-start.2) | copy-done | bytes 1048600
  41.4 2.8 %convolution_convert_fusion.7 = bf16[256,768]{1,0:T(8,128)(2,1)} fusion(bf16[1024,768]{1,0:T(8,128)(2,1)} %param.15, bf16[1,1024]{1,0:T(2,128)(2,1)S(1)} %broadcast_in_dim.26, bf16[51,1024]{1,0:T(8,128)(2,1)S(1)} %fusion.17, bf16[256,1]{0,1:T(2,128)(2,1)S(1)} %sub.85, bf16[256,51]{0,1:T(8,128)(2,1)S(1)} %fusion.107), kind=kOutput, calls=%fused_computation.22 | convolution fusion | flops 102738944 | bytes 2099200 | tf_op jit(solution)/shard_map/jvp()/dot_general | solution.py:89
  44.2 1.2 %copy.58 = bf16[256,768]{0,1:T(8,128)(2,1)S(1)} copy(bf16[256,768]{1,0:T(8,128)(2,1)} %convolution_convert_fusion.7) | data formatting | bytes 786432 | tf_op jit(solution)/shard_map/jvp()/convert_element_type | solution.py:89
  46.1 1.4 %fusion.138 = (f32[256]{0:T(256)S(1)}, f32[16,256,48]{1,2,0:T(8,128)S(1)}) fusion(f32[16,256,48]{1,2,0:T(8,128)S(1)} %convolution_add_fusion.1, bf16[256,16,48]{0,2,1:T(8,128)(2,1)S(1)} %bitcast.187, bf16[3,16,48,48]{3,2,1,0:T(8,128)(2,1)} %param.16), kind=kOutput, calls=%fused_computation.251 | convolution fusion | flops 19267328 | bytes 2163712 | tf_op jit(solution)/shard_map/jvp(pgi,gio->pgo)/dot_general | solution.py:96
  48.8 1.1 %copy.62 = f32[256,768]{1,0:T(8,128)} copy(f32[256,768]{0,1:T(8,128)S(1)} %bitcast.181) | data formatting | bytes 1572864 | tf_op jit(solution)/shard_map/jvp()/reshape | solution.py:102
  49.9 5.2 %multiply_reduce_fusion = (f32[]{:T(128)}, f32[256,1024]{1,0:T(8,128)S(1)}) fusion(f32[256]{0:T(256)} %get-tuple-element.23, f32[256]{0:T(256)} %add_rsqrt_fusion.2, f32[256,1024]{1,0:T(8,128)} %copy-done.2, f32[256]{0:T(256)} %copy-done.35, bf16[768,1024]{1,0:T(8,128)(2,1)} %param.17, bf16[256,768]{1,0:T(8,128)(2,1)S(1)} %copy-done.11, ...), kind=kOutput, calls=%fused_computation.64 | convolution fusion | flops 418709504 | bytes 4854788 | tf_op jit(solution)/shard_map/jvp()/dot_general | solution.py:104
  55.2 3.3 %multiply_reduce_fusion.2 = (f32[256]{0:T(256)S(1)}, bf16[256,768]{1,0:T(8,128)(2,1)S(1)}) fusion(f32[256,768]{1,0:T(8,128)S(1)} %copy-done.3, f32[256]{0:T(256)S(1)} %broadcast_multiply_fusion.1, f32[256]{0:T(256)S(1)} %copy-done.34, bf16[768,1024]{1,0:T(8,128)(2,1)S(1)} %copy-done.39, f32[256,1024]{1,0:T(8,128)S(1)} %get-tuple-element.52, ...), kind=kOutput, calls=%fused_computation.87 | convolution fusion | flops 419495680 | bytes 3805184 | tf_op jit(solution)/shard_map/transpose(jvp())/dot_general | solution.py:104
  58.6 2.8 %fusion.132 = (f32[256]{0:T(256)S(1)}, f32[256,768]{1,0:T(8,128)S(1)}) fusion(f32[256]{0:T(256)S(1)} %multiply_multiply_fusion.8, bf16[256,768]{1,0:T(8,128)(2,1)S(1)} %get-tuple-element.43, f32[256]{0:T(256)S(1)} %copy-done.34, f32[256,768]{1,0:T(8,128)S(1)} %copy-done.3, f32[256]{0:T(256)S(1)} %broadcast_multiply_fusion.1), kind=kLoop, calls=%fused_computation.245 | loop fusion | flops 15531776 | bytes 1970176 | tf_op jit(solution)/shard_map/transpose(jvp())/reduce_sum | solution.py:19
  61.4 0.8 broadcast_add_fusion
  62.2 1.2 %copy.65 = bf16[256,768]{0,1:T(8,128)(2,1)S(1)} copy(bf16[256,768]{1,0:T(8,128)(2,1)} %broadcast_add_fusion) | data formatting | bytes 786432 | tf_op jit(solution)/shard_map/transpose(jvp())/add_any | solution.py:18
  64.7 2.2 %fusion.21 = bf16[52,1024]{1,0:T(8,128)(2,1)S(1)} fusion(bf16[1024,768]{1,0:T(8,128)(2,1)} %param.15, bf16[256,768]{1,0:T(8,128)(2,1)} %copy-done.10, bf16[256,768]{1,0:T(8,128)(2,1)S(1)} %copy.69, bf16[256,1]{0,1:T(2,128)(2,1)S(1)} %copy-done.33, bf16[256,51]{0,1:T(8,128)(2,1)S(1)} %fusion.107), kind=kOutput, calls=%fused_computation.55 | convolution fusion | flops 102525952 | bytes 2492416 | tf_op jit(solution)/shard_map/transpose(jvp())/dot_general | solution.py:86
  67.9 1.4 %fusion.16 = bf16[51,1,16,64]{3,0,2,1:T(8,128)(2,1)S(1)} fusion(bf16[51,16,64]{2,1,0:T(8,128)(2,1)S(1)} %reshape.254, f32[16,51,51]{1,2,0:T(8,128)} %copy-done.14, f32[16,51]{1,0:T(8,128)S(1)} %copy-done.31), kind=kOutput, calls=%fused_computation.43 | convolution fusion | flops 5462304 | bytes 378624 | tf_op jit(solution)/shard_map/transpose(jvp(hqk,khd->qhd))/dot_general | solution.py:36
  72.2 5.0 %multiply_reduce_fusion.5 = (f32[51]{0:T(128)S(1)}, f32[51]{0:T(128)S(1)}, f32[51,1024]{1,0:T(8,128)S(1)}) fusion(f32[51,1024]{1,0:T(8,128)S(1)} %get-tuple-element.31, f32[51]{0:T(128)S(1)} %broadcast_multiply_fusion.4, bf16[51,3072]{1,0:T(8,128)(2,1)S(1)} %reshape.255, bf16[1024,3072]{1,0:T(8,128)(2,1)} %param.12), kind=kOutput, calls=%fused_computation.154 | convolution fusion | flops 321229696 | bytes 7023204 | tf_op jit(solution)/shard_map/transpose(jvp(transpose(jvp())))/dot_general | solution.py:114
  78.1 1.5 %collective-permute-start.4 = (bf16[51,1024]{1,0:T(8,128)(2,1)S(1)}, bf16[51,1024]{1,0:T(8,128)(2,1)S(1)}, u32[]{:S(2)}, u32[]{:S(2)}) collective-permute-start(bf16[51,1024]{1,0:T(8,128)(2,1)S(1)} %fusion.98), channel_id=1, source_target_pairs={{0,2},{1,3},{2,0},{3,1},{4,6},{5,7},{6,4},{7,5},{8,10},{9,11},{10,... | collective-permute-start | bytes 313352 | tf_op jit(solution)/shard_map/ppermute | solution.py:129
  80.4 2.6 %collective-permute-done.3 = bf16[51,1024]{1,0:T(8,128)(2,1)S(1)} collective-permute-done((bf16[51,1024]{1,0:T(8,128)(2,1)S(1)}, bf16[51,1024]{1,0:T(8,128)(2,1)S(1)}, u32[]{:S(2)}, u32[]{:S(2)}) %collective-permute-start.3) | collective-permute-done | bytes 104480 | tf_op jit(solution)/shard_map/ppermute | solution.py:129
  83.1 1.0 %collective-permute-done.4 = bf16[51,1024]{1,0:T(8,128)(2,1)S(1)} collective-permute-done((bf16[51,1024]{1,0:T(8,128)(2,1)S(1)}, bf16[51,1024]{1,0:T(8,128)(2,1)S(1)}, u32[]{:S(2)}, u32[]{:S(2)}) %collective-permute-start.4) | collective-permute-done | bytes 104480 | tf_op jit(solution)/shard_map/ppermute | solution.py:129
  84.1 1.3 %collective-permute-done.5 = bf16[51,1024]{1,0:T(8,128)(2,1)S(1)} collective-permute-done((bf16[51,1024]{1,0:T(8,128)(2,1)S(1)}, bf16[51,1024]{1,0:T(8,128)(2,1)S(1)}, u32[]{:S(2)}, u32[]{:S(2)}) %collective-permute-start.5) | collective-permute-done | bytes 104480 | tf_op jit(solution)/shard_map/ppermute | solution.py:129
  85.3 1.4 %fusion.20 = f32[192,1024]{1,0:T(8,128)} fusion(bf16[51,1024]{1,0:T(8,128)(2,1)S(1)} %collective-permute-done.5, bf16[51,1024]{1,0:T(8,128)(2,1)S(1)} %collective-permute-done.4, bf16[51,1024]{1,0:T(8,128)(2,1)S(1)} %collective-permute-done.3, bf16[51,1024]{1,0:T(8,128)(2,1)S(1)} %fusion.98, bf16[256,768]{1,0:T(8,128)(2,1)S(1)} %pad_maximum_fusion, ...), kind=kOutput, calls=%fused_computation.54 | convolution fusion | flops 102032640 | bytes 1377284 | tf_op jit(solution)/shard_map/vc,vd->cd/dot_general | solution.py:225
  (144 shorter events, 15.1 us)
Async XLA Ops:
  0.6 35.1 %copy-start = (bf16[1024,1024]{1,0:T(8,128)(2,1)S(1)}, bf16[1024,1024]{1,0:T(8,128)(2,1)}, u32[]{:S(2)}) copy-start(bf16[1024,1024]{1,0:T(8,128)(2,1)} %param.13) | copy-start | bytes 6291460
  0.6 18.2 %collective-permute-start = (bf16[64,768]{1,0:T(8,128)(2,1)}, bf16[64,768]{1,0:T(8,128)(2,1)S(1)}, u32[]{:S(2)}, u32[]{:S(2)}) collective-permute-start(bf16[64,768]{1,0:T(8,128)(2,1)} %param.9), channel_id=1, source_target_pairs={{0,1},{1,2},{2,3},{3,0},{4,5},{5,6},{6,7},{7,4},{8,9},{9,10},{10,1... | collective-permute-start | bytes 294920 | tf_op jit(solution)/shard_map/ppermute | solution.py:129
  3.7 15.2 %collective-permute-start.1 = (bf16[64,768]{1,0:T(8,128)(2,1)}, bf16[64,768]{1,0:T(8,128)(2,1)S(1)}, u32[]{:S(2)}, u32[]{:S(2)}) collective-permute-start(bf16[64,768]{1,0:T(8,128)(2,1)} %param.9), channel_id=1, source_target_pairs={{0,2},{1,3},{2,0},{3,1},{4,6},{5,7},{6,4},{7,5},{8,10},{9,11},{10,... | collective-permute-start | bytes 294920 | tf_op jit(solution)/shard_map/ppermute | solution.py:129
  5.2 13.7 %collective-permute-start.2 = (bf16[64,768]{1,0:T(8,128)(2,1)}, bf16[64,768]{1,0:T(8,128)(2,1)S(1)}, u32[]{:S(2)}, u32[]{:S(2)}) collective-permute-start(bf16[64,768]{1,0:T(8,128)(2,1)} %param.9), channel_id=1, source_target_pairs={{0,3},{1,0},{2,1},{3,2},{4,7},{5,4},{6,5},{7,6},{8,11},{9,8},{10,9... | collective-permute-start | bytes 294920 | tf_op jit(solution)/shard_map/ppermute | solution.py:129
  16.1 25.3 %copy-start.32 = (bf16[256,1]{0,1:T(2,128)(2,1)}, bf16[256,1]{0,1:T(2,128)(2,1)S(1)}, u32[]{:S(2)}) copy-start(bf16[256,1]{0,1:T(2,128)(2,1)S(1)} %sub.85) | copy-start | bytes 1540
  19.8 2.5 %copy-start.16 = (bf16[64,768]{1,0:T(8,128)(2,1)}, bf16[64,768]{1,0:T(8,128)(2,1)S(1)}, u32[]{:S(2)}) copy-start(bf16[64,768]{1,0:T(8,128)(2,1)S(1)} %get-tuple-element.13) | copy-start | bytes 294916
  19.8 2.5 %copy-start.18 = (bf16[64,768]{1,0:T(8,128)(2,1)}, bf16[64,768]{1,0:T(8,128)(2,1)S(1)}, u32[]{:S(2)}) copy-start(bf16[64,768]{1,0:T(8,128)(2,1)S(1)} %get-tuple-element.14) | copy-start | bytes 294916
  19.8 2.5 %copy-start.20 = (bf16[64,768]{1,0:T(8,128)(2,1)}, bf16[64,768]{1,0:T(8,128)(2,1)S(1)}, u32[]{:S(2)}) copy-start(bf16[64,768]{1,0:T(8,128)(2,1)S(1)} %get-tuple-element.15) | copy-start | bytes 294916
  19.8 2.5 %copy-start.22 = (bf16[64,768]{1,0:T(8,128)(2,1)}, bf16[64,768]{1,0:T(8,128)(2,1)S(1)}, u32[]{:S(2)}) copy-start(bf16[64,768]{1,0:T(8,128)(2,1)S(1)} %get-tuple-element.16) | copy-start | bytes 294916
  30.8 2.8 %copy-start.1 = (bf16[256,3072]{0,1:T(8,128)(2,1)S(1)}, bf16[256,3072]{0,1:T(8,128)(2,1)}, u32[]{:S(2)}) copy-start(bf16[256,3072]{0,1:T(8,128)(2,1)} %copy.63) | copy-start | bytes 4718596
  36.6 3.3 %copy-start.35 = (f32[256]{0:T(256)}, f32[256]{0:T(256)S(1)}, u32[]{:S(2)}) copy-start(f32[256]{0:T(256)S(1)} %broadcast_multiply_fusion.2) | copy-start | bytes 3076
  38.9 1.9 %copy-start.6 = (bf16[51,1,16,64]{3,2,1,0:T(8,128)(2,1)}, bf16[51,1,16,64]{3,2,1,0:T(8,128)(2,1)S(1)}, u32[]{:S(2)}) copy-start(bf16[51,1,16,64]{3,2,1,0:T(8,128)(2,1)S(1)} %get-tuple-element.11) | copy-start | bytes 313348
  38.9 1.9 %copy-start.8 = (bf16[51,1,16,64]{3,2,1,0:T(8,128)(2,1)}, bf16[51,1,16,64]{3,2,1,0:T(8,128)(2,1)S(1)}, u32[]{:S(2)}) copy-start(bf16[51,1,16,64]{3,2,1,0:T(8,128)(2,1)S(1)} %get-tuple-element.12) | copy-start | bytes 313348
  40.9 4.5 %copy-start.4 = (bf16[3,16,48,48]{3,2,1,0:T(8,128)(2,1)S(1)}, bf16[3,16,48,48]{3,2,1,0:T(8,128)(2,1)}, u32[]{:S(2)}) copy-start(bf16[3,16,48,48]{3,2,1,0:T(8,128)(2,1)} %param.16) | copy-start | bytes 663556
  47.4 2.5 %copy-start.11 = (bf16[256,768]{1,0:T(8,128)(2,1)S(1)}, bf16[256,768]{1,0:T(8,128)(2,1)}, u32[]{:S(2)}) copy-start(bf16[256,768]{1,0:T(8,128)(2,1)} %convolution_convert_fusion.7) | copy-start | bytes 1179652
  49.9 5.3 %copy-start.3 = (f32[256,768]{1,0:T(8,128)S(1)}, f32[256,768]{1,0:T(8,128)}, u32[]{:S(2)}) copy-start(f32[256,768]{1,0:T(8,128)} %copy.62) | copy-start | bytes 2359300
  49.9 5.3 %copy-start.34 = (f32[256]{0:T(256)S(1)}, f32[256]{0:T(256)}, u32[]{:S(2)}) copy-start(f32[256]{0:T(256)} %fusion.113) | copy-start | bytes 3076
  49.9 5.3 %copy-start.37 = (f32[256]{0:T(256)S(1)}, f32[256]{0:T(256)}, u32[]{:S(2)}) copy-start(f32[256]{0:T(256)} %get-tuple-element.22) | copy-start | bytes 3076
  49.9 5.3 %copy-start.39 = (bf16[768,1024]{1,0:T(8,128)(2,1)S(1)}, bf16[768,1024]{1,0:T(8,128)(2,1)}, u32[]{:S(2)}) copy-start(bf16[768,1024]{1,0:T(8,128)(2,1)} %param.17) | copy-start | bytes 4718596
  55.2 3.4 %copy-start.29 = (f32[256]{0:T(256)S(1)}, f32[256]{0:T(256)}, u32[]{:S(2)}) copy-start(f32[256]{0:T(256)} %copy-done.28) | copy-start | bytes 3076
  58.5 2.8 %copy-start.10 = (bf16[256,768]{1,0:T(8,128)(2,1)}, bf16[256,768]{1,0:T(8,128)(2,1)S(1)}, u32[]{:S(2)}) copy-start(bf16[256,768]{1,0:T(8,128)(2,1)S(1)} %get-tuple-element.43) | copy-start | bytes 1179652
  58.5 4.9 %copy-start.5 = (bf16[3,16,48,48]{3,2,1,0:T(8,128)(2,1)S(1)}, bf16[3,16,48,48]{3,2,1,0:T(8,128)(2,1)}, u32[]{:S(2)}) copy-start(bf16[3,16,48,48]{3,2,1,0:T(8,128)(2,1)} %param.16) | copy-start | bytes 663556
  62.2 1.9 %copy-start.31 = (f32[16,51]{1,0:T(8,128)S(1)}, f32[16,51]{1,0:T(8,128)}, u32[]{:S(2)}) copy-start(f32[16,51]{1,0:T(8,128)} %copy-done.30) | copy-start | bytes 9796
  66.9 2.4 %copy-start.13 = (bf16[51,1,16,64]{3,2,1,0:T(8,128)(2,1)S(1)}, bf16[51,1,16,64]{3,2,1,0:T(8,128)(2,1)}, u32[]{:S(2)}) copy-start(bf16[51,1,16,64]{3,2,1,0:T(8,128)(2,1)} %copy-done.12) | copy-start | bytes 313348
  72.1 8.2 %copy-start.17 = (bf16[64,768]{1,0:T(8,128)(2,1)S(1)}, bf16[64,768]{1,0:T(8,128)(2,1)}, u32[]{:S(2)}) copy-start(bf16[64,768]{1,0:T(8,128)(2,1)} %copy-done.16) | copy-start | bytes 294916
  72.1 8.2 %copy-start.19 = (bf16[64,768]{1,0:T(8,128)(2,1)S(1)}, bf16[64,768]{1,0:T(8,128)(2,1)}, u32[]{:S(2)}) copy-start(bf16[64,768]{1,0:T(8,128)(2,1)} %copy-done.18) | copy-start | bytes 294916
  72.1 8.2 %copy-start.21 = (bf16[64,768]{1,0:T(8,128)(2,1)S(1)}, bf16[64,768]{1,0:T(8,128)(2,1)}, u32[]{:S(2)}) copy-start(bf16[64,768]{1,0:T(8,128)(2,1)} %copy-done.20) | copy-start | bytes 294916
  72.1 8.2 %copy-start.23 = (bf16[64,768]{1,0:T(8,128)(2,1)S(1)}, bf16[64,768]{1,0:T(8,128)(2,1)}, u32[]{:S(2)}) copy-start(bf16[64,768]{1,0:T(8,128)(2,1)} %copy-done.22) | copy-start | bytes 294916
  72.2 13.2 %copy-start.36 = (s32[204]{0:T(256)S(1)}, s32[204]{0:T(256)}, u32[]{:S(2)}) copy-start(s32[204]{0:T(256)} %pad_add_fusion.3) | copy-start | bytes 2452
  77.5 5.5 %collective-permute-start.3 = (bf16[51,1024]{1,0:T(8,128)(2,1)S(1)}, bf16[51,1024]{1,0:T(8,128)(2,1)S(1)}, u32[]{:S(2)}, u32[]{:S(2)}) collective-permute-start(bf16[51,1024]{1,0:T(8,128)(2,1)S(1)} %fusion.98), channel_id=1, source_target_pairs={{0,3},{1,0},{2,1},{3,2},{4,7},{5,4},{6,5},{7,6},{8,11},{9,8},{10,9... | collective-permute-start | bytes 313352 | tf_op jit(solution)/shard_map/ppermute | solution.py:129
  78.1 6.0 %collective-permute-start.4 = (bf16[51,1024]{1,0:T(8,128)(2,1)S(1)}, bf16[51,1024]{1,0:T(8,128)(2,1)S(1)}, u32[]{:S(2)}, u32[]{:S(2)}) collective-permute-start(bf16[51,1024]{1,0:T(8,128)(2,1)S(1)} %fusion.98), channel_id=1, source_target_pairs={{0,2},{1,3},{2,0},{3,1},{4,6},{5,7},{6,4},{7,5},{8,10},{9,11},{10,... | collective-permute-start | bytes 313352 | tf_op jit(solution)/shard_map/ppermute | solution.py:129
  79.6 5.7 %collective-permute-start.5 = (bf16[51,1024]{1,0:T(8,128)(2,1)S(1)}, bf16[51,1024]{1,0:T(8,128)(2,1)S(1)}, u32[]{:S(2)}, u32[]{:S(2)}) collective-permute-start(bf16[51,1024]{1,0:T(8,128)(2,1)S(1)} %fusion.98), channel_id=1, source_target_pairs={{0,1},{1,2},{2,3},{3,0},{4,5},{5,6},{6,7},{7,4},{8,9},{9,10},{10,1... | collective-permute-start | bytes 313352 | tf_op jit(solution)/shard_map/ppermute | solution.py:129
  (14 other events, 16.8 us)

commit v13 on v11

--- a/solution.py
+++ b/solution.py
@@ -210,7 +210,13 @@
     (grad_in,) = pullback(jnp.ones_like(squares) * factor)
     copy_loss = jnp.reshape(squares / ((total_rows - visible_count) * D), (1,))
     slot_copy = (own_index + jnp.arange(group_size, dtype=jnp.int32)) % group_size
-    flat_index = visible_index[slot_copy].reshape(copies * visible_count)
+    slot_rows = []
+    for slot in range(group_size):
+        chosen = visible_index[0]
+        for copy_id in range(1, copies):
+            chosen = jnp.where(slot_copy[slot] == copy_id, visible_index[copy_id], chosen)
+        slot_rows.append(chosen)
+    flat_index = jnp.concatenate(slot_rows, axis=0)
     own_cols = lax.dynamic_slice_in_dim(clip_pixels, own_index * col_width, col_width, 1)
     all_picks = (flat_index[:, None] == clip_ids[None, :]).astype(jnp.bfloat16)
     gathered = jnp.dot(all_picks, own_cols, preferred_element_type=jnp.float32).astype(

time: 79.1 us -> 89.6 us (1.13)
  between operations: 3.2 us -> 10.8 us
  matrix products: 40.3 us -> 42.9 us
  other arithmetic: 9.67 us -> 11.6 us
  local copies, waits for them, and re-layouts: 12.4 us -> 10.6 us
    dot_general x1, matrix products: 3.1 us -> 5.83 us  [project_rows(): jnp.dot(normed, w_qkv, preferred_element_type=jnp.float32)]
    select_n x1 -> x3, other arithmetic: 0.01 us -> 1.73 us  [the longest x2 1.72 us: on_device(): jnp.where(slot_copy[slot] == copy_id, visible_index[copy_id], chosen)]
    eq x2 -> x0, local copies, waits for them, and re-layouts: 1.28 us -> none  [the longest x1 0.69 us: decoder_output(): picks = (slot_ids[:, None] == positions[None, :]).astype(jnp.bfloat16)]
    gather x1 -> x0, local copies, waits for them, and re-layouts: 1.24 us -> none  [on_device(): flat_index = visible_index[slot_copy].reshape(copies * visible_count)]
    unnamed x71 -> x69, local copies, waits for them, and re-layouts: 2.23 us -> 2.23 us
where the time goes in v13:
time: 89.6 us; the launch traced here: 89 us
  matrix products  42.9 us (48%)
  other arithmetic  11.6 us (13%)
  between operations  10.8 us (12%)
  local copies, waits for them, and re-layouts  10.6 us (12%)
  starting transfers between devices  8.16 us (9%)
  waiting for transfers between devices  4.91 us (5%)
    dot_general x2, matrix products, decoder_output(): return jnp.dot(hidden, dec_out, preferred_element_type=jnp.float32)  8.57 us
    ppermute x6, starting transfers between devices, ring_gather(): parts.append(lax.ppermute(values, 'mask', pairs))  8.16 us
    dot_general x1, matrix products, project_rows(): jnp.dot(normed, w_qkv, preferred_element_type=jnp.float32)  5.83 us
    dot_general x1, matrix products, copy_terms(): branch = attention_from(reuse_rows(visible_in, w_qkv, projected), w_out)  5 us
    ppermute x6, waiting for transfers between devices, ring_gather(): parts.append(lax.ppermute(values, 'mask', pairs))  4.91 us
    dot_general x2, matrix products, decoder_output(): jnp.dot(visible_out, dec_in, preferred_element_type=jnp.float32)  4.57 us
    dot_general x4, matrix products, mix_heads(): jnp.einsum('hqk,khd->qhd', weights, values, preferred_element_type=jnp.fl...  2.82 us
    reduce_sum x1, other arithmetic, row_norm(): centred = values - average  2.76 us
  transfers between devices with their start and end apart: 6, of which 3 were waited for; matrix products, arithmetic and copies ran while one was open for 7% of the time, Pallas kernels for 0%

profile of v13, /device:TPU:0, one launch (start us, length us, event | category | flops | bytes accessed | tf_op | source)
XLA Modules:
  0.0 89.0 jit_solution(5457065186004385894)
XLA Ops:
  0.6 3.0 %collective-permute-start = (bf16[64,768]{1,0:T(8,128)(2,1)}, bf16[64,768]{1,0:T(8,128)(2,1)S(1)}, u32[]{:S(2)}, u32[]{:S(2)}) collective-permute-start(bf16[64,768]{1,0:T(8,128)(2,1)} %param.9), channel_id=1, source_target_pairs={{0,1},{1,2},{2,3},{3,0},{4,5},{5,6},{6,7},{7,4},{8,9},{9,10},{10,1... | collective-permute-start | bytes 294920 | tf_op jit(solution)/shard_map/ppermute | solution.py:129
  3.7 1.5 %collective-permute-start.1 = (bf16[64,768]{1,0:T(8,128)(2,1)}, bf16[64,768]{1,0:T(8,128)(2,1)S(1)}, u32[]{:S(2)}, u32[]{:S(2)}) collective-permute-start(bf16[64,768]{1,0:T(8,128)(2,1)} %param.9), channel_id=1, source_target_pairs={{0,2},{1,3},{2,0},{3,1},{4,6},{5,7},{6,4},{7,5},{8,10},{9,11},{10,... | collective-permute-start | bytes 294920 | tf_op jit(solution)/shard_map/ppermute | solution.py:129
  5.2 1.4 %collective-permute-start.2 = (bf16[64,768]{1,0:T(8,128)(2,1)}, bf16[64,768]{1,0:T(8,128)(2,1)S(1)}, u32[]{:S(2)}, u32[]{:S(2)}) collective-permute-start(bf16[64,768]{1,0:T(8,128)(2,1)} %param.9), channel_id=1, source_target_pairs={{0,3},{1,0},{2,1},{3,2},{4,7},{5,4},{6,5},{7,6},{8,11},{9,8},{10,9... | collective-permute-start | bytes 294920 | tf_op jit(solution)/shard_map/ppermute | solution.py:129
  10.9 0.9 fusion.119
  17.3 1.7 %convolution_reduce_fusion = bf16[768]{0:T(1024)(128)(2,1)S(1)} fusion(bf16[1024,1]{0,1:T(2,128)(2,1)S(1)} %reshape.261, bf16[1024,768]{1,0:T(8,128)(2,1)} %param.15), kind=kOutput, calls=%fused_computation.57 | convolution fusion | flops 1572864 | bytes 1576448 | tf_op jit(solution)/shard_map/jvp()/dot_general | solution.py:87
  20.4 1.0 %select_select_fusion.3 = (bf16[64,768]{1,0:T(8,128)(2,1)S(1)}, bf16[64,768]{1,0:T(8,128)(2,1)S(1)}, bf16[64,768]{1,0:T(8,128)(2,1)S(1)}, bf16[64,768]{1,0:T(8,128)(2,1)S(1)}) fusion(bf16[64,768]{1,0:T(8,128)(2,1)S(1)} %collective-permute-done, bf16[64,768]{1,0:T(8,128)(2,1)S(1)} %collective-permute-done.1, bf16[64,768]{1,0:T(8,128)(2,1)S(1)} %collective-permute-done.2, ...), kind=kLoop, calls=%fused_computation.181 | loop fusion | flops 589824 | bytes 786444 | tf_op jit(solution)/shard_map/jit(_where)/select_n | solution.py:140
  21.4 2.2 %convert_reduce_fusion = (f32[256]{0:T(256)S(1)}, bf16[256,1024]{1,0:T(8,128)(2,1)S(1)}) fusion(bf16[768,1024]{1,0:T(8,128)(2,1)} %param.11, bf16[64,768]{1,0:T(8,128)(2,1)S(1)} %get-tuple-element.14, bf16[64,768]{1,0:T(8,128)(2,1)S(1)} %get-tuple-element.15, bf16[64,768]{1,0:T(8,128)(2,1)S(1)} %get-tuple-element.16, bf16[64,768]{1,0:T(8,128)(2,1)S(1)} %get-tuple-element.13), kind=kOutput, calls=%fused_computation.13 | convolution fusion | flops 405012224 | bytes 2491392 | tf_op jit(solution)/shard_map/dot_general | solution.py:175
  24.0 5.8 %convolution_convert_fusion = bf16[256,3072]{1,0:T(8,128)(2,1)} fusion(bf16[1024,3072]{1,0:T(8,128)(2,1)} %param.12, bf16[256,1024]{1,0:T(8,128)(2,1)S(1)} %get-tuple-element.31, f32[256]{0:T(256)S(1)} %add_rsqrt_fusion.3, f32[256]{0:T(256)S(1)} %broadcast_multiply_fusion.3), kind=kOutput, calls=%fused_computation.2 | convolution fusion | flops 1612447744 | bytes 8390656 | tf_op jit(solution)/shard_map/dot_general | solution.py:48
  29.8 2.6 %copy.62 = bf16[256,3072]{0,1:T(8,128)(2,1)} copy(bf16[256,3072]{1,0:T(8,128)(2,1)} %convolution_convert_fusion) | data formatting | bytes 3145728 | tf_op jit(solution)/shard_map/convert_element_type | solution.py:48
  32.4 1.9 %convolution_convert_fusion.1 = bf16[51,3072]{1,0:T(8,128)(2,1)S(1)} fusion(bf16[256,3072]{1,0:T(8,128)(2,1)} %convolution_convert_fusion, s32[51]{0:T(128)S(1)} %get-tuple-element.19), kind=kOutput, calls=%fused_computation.4 | convolution fusion | flops 80385792 | bytes 1886412 | tf_op jit(solution)/shard_map/dot_general | solution.py:186
  34.3 0.9 fusion.141
  35.5 1.0 %fusion = (f32[16,256]{1,0:T(8,128)S(1)}, f32[16,256,256]{1,2,0:T(8,128)S(1)}) fusion(f32[256,16]{0,1:T(8,128)S(1)} %get-tuple-element.55, bf16[256,3,16,64]{0,3,2,1:T(8,128)(2,1)S(1)} %bitcast.183, f32[256,16]{0,1:T(8,128)S(1)} %get-tuple-element.56), kind=kOutput, calls=%fused_computation.3 | convolution fusion | flops 137883648 | bytes 5292032 | tf_op jit(solution)/shard_map/qhd,khd->hqk/dot_general | solution.py:31
  36.5 0.8 fusion.3
  38.2 1.0 %copy-done.2 = f32[256,1024]{1,0:T(8,128)} copy-done((f32[256,1024]{1,0:T(8,128)}, f32[256,1024]{1,0:T(8,128)S(1)}, u32[]{:S(2)}) %copy-start.2) | copy-done | bytes 1048600
  42.4 2.3 %convolution_convert_fusion.18 = bf16[51,768]{1,0:T(8,128)(2,1)S(1)} fusion(bf16[1024,768]{1,0:T(8,128)(2,1)} %param.15, f32[51,1024]{1,0:T(8,128)S(1)} %get-tuple-element.43, bf16[51,1024]{1,0:T(8,128)(2,1)S(1)} %reshape.247, bf16[1024,1024]{1,0:T(8,128)(2,1)S(1)} %copy-done), kind=kOutput, calls=%fused_computation.55 | convolution fusion | flops 187314432 | bytes 4061696 | tf_op jit(solution)/shard_map/jvp()/dot_general | solution.py:84
  44.7 1.1 %fusion.4 = bf16[256,768]{1,0:T(8,128)(2,1)} fusion(bf16[51,768]{1,0:T(8,128)(2,1)S(1)} %convolution_convert_fusion.18, bf16[768]{0:T(1024)(128)(2,1)S(1)} %convolution_reduce_fusion, pred[256]{0:T(512)(128)(4,1)S(1)} %broadcast_compare_fusion, s32[51]{0:T(128)S(1)} %get-tuple-element.19), kind=kOutput, calls=%fused_computation.19 | convolution fusion | flops 20263680 | bytes 473548 | tf_op jit(solution)/shard_map/jvp()/dot_general | solution.py:90
  45.8 1.2 %copy.57 = bf16[256,768]{0,1:T(8,128)(2,1)S(1)} copy(bf16[256,768]{1,0:T(8,128)(2,1)} %fusion.4) | data formatting | bytes 786432 | tf_op jit(solution)/shard_map/jvp()/convert_element_type | solution.py:91
  47.7 1.4 %fusion.140 = (f32[256]{0:T(256)S(1)}, f32[16,256,48]{1,2,0:T(8,128)S(1)}) fusion(f32[16,256,48]{1,2,0:T(8,128)S(1)} %convolution_add_fusion.1, bf16[256,16,48]{0,2,1:T(8,128)(2,1)S(1)} %bitcast.191, bf16[3,16,48,48]{3,2,1,0:T(8,128)(2,1)} %param.16), kind=kOutput, calls=%fused_computation.253 | convolution fusion | flops 19267328 | bytes 2163712 | tf_op jit(solution)/shard_map/jvp(pgi,gio->pgo)/dot_general | solution.py:96
  49.8 1.1 %copy.61 = f32[256,768]{1,0:T(8,128)} copy(f32[256,768]{0,1:T(8,128)S(1)} %bitcast.185) | data formatting | bytes 1572864 | tf_op jit(solution)/shard_map/jvp()/reshape | solution.py:102
  51.0 5.2 %multiply_reduce_fusion = (f32[]{:T(128)}, f32[256,1024]{1,0:T(8,128)S(1)}) fusion(f32[256]{0:T(256)} %get-tuple-element.23, f32[256]{0:T(256)} %add_rsqrt_fusion.2, f32[256,1024]{1,0:T(8,128)} %copy-done.2, f32[256]{0:T(256)} %copy-done.27, bf16[768,1024]{1,0:T(8,128)(2,1)} %param.17, bf16[256,768]{1,0:T(8,128)(2,1)S(1)} %copy-done.23, ...), kind=kOutput, calls=%fused_computation.66 | convolution fusion | flops 418709504 | bytes 4854788 | tf_op jit(solution)/shard_map/jvp()/dot_general | solution.py:104
  56.3 3.3 %multiply_reduce_fusion.2 = (f32[256]{0:T(256)S(1)}, bf16[256,768]{1,0:T(8,128)(2,1)S(1)}) fusion(f32[256,768]{1,0:T(8,128)S(1)} %copy-done.3, f32[256]{0:T(256)S(1)} %broadcast_multiply_fusion.1, f32[256]{0:T(256)S(1)} %copy-done.26, bf16[768,1024]{1,0:T(8,128)(2,1)S(1)} %copy-done.33, f32[256,1024]{1,0:T(8,128)S(1)} %get-tuple-element.52, ...), kind=kOutput, calls=%fused_computation.91 | convolution fusion | flops 419495680 | bytes 3805184 | tf_op jit(solution)/shard_map/transpose(jvp())/dot_general | solution.py:104
  59.6 2.8 %fusion.135 = (f32[256]{0:T(256)S(1)}, f32[256,768]{1,0:T(8,128)S(1)}) fusion(f32[256]{0:T(256)S(1)} %multiply_multiply_fusion.8, bf16[256,768]{1,0:T(8,128)(2,1)S(1)} %get-tuple-element.41, f32[256]{0:T(256)S(1)} %copy-done.26, f32[256,768]{1,0:T(8,128)S(1)} %copy-done.3, f32[256]{0:T(256)S(1)} %broadcast_multiply_fusion.1), kind=kLoop, calls=%fused_computation.248 | loop fusion | flops 15531776 | bytes 1970176 | tf_op jit(solution)/shard_map/transpose(jvp())/reduce_sum | solution.py:19
  62.4 0.8 broadcast_add_fusion
  63.3 1.2 %copy.64 = bf16[256,768]{0,1:T(8,128)(2,1)S(1)} copy(bf16[256,768]{1,0:T(8,128)(2,1)} %broadcast_add_fusion) | data formatting | bytes 786432 | tf_op jit(solution)/shard_map/transpose(jvp())/add_any | solution.py:18
  65.8 2.3 %convolution_convert_fusion.13 = bf16[51,1024]{1,0:T(8,128)(2,1)S(1)} fusion(bf16[1024,768]{1,0:T(8,128)(2,1)} %param.15, bf16[256,768]{1,0:T(8,128)(2,1)} %copy-done.10, bf16[256,768]{1,0:T(8,128)(2,1)S(1)} %copy.68, pred[256]{0:T(512)(128)(4,1)S(1)} %copy-done.31, s32[51]{0:T(128)S(1)} %copy-done.25), kind=kOutput, calls=%fused_computation.48 | convolution fusion | flops 100964352 | bytes 2464204 | tf_op jit(solution)/shard_map/transpose(jvp())/dot_general | solution.py:84
  69.0 1.4 %fusion.17 = bf16[51,1,16,64]{3,0,2,1:T(8,128)(2,1)S(1)} fusion(bf16[51,16,64]{2,1,0:T(8,128)(2,1)S(1)} %reshape.254, f32[16,51,51]{1,2,0:T(8,128)} %copy-done.13, f32[16,51]{1,0:T(8,128)S(1)} %get-tuple-element.36), kind=kOutput, calls=%fused_computation.44 | convolution fusion | flops 5462304 | bytes 378624 | tf_op jit(solution)/shard_map/transpose(jvp(hqk,khd->qhd))/dot_general | solution.py:36
  73.2 5.0 %multiply_reduce_fusion.5 = (f32[51]{0:T(128)S(1)}, f32[51]{0:T(128)S(1)}, f32[51,1024]{1,0:T(8,128)S(1)}) fusion(f32[51,1024]{1,0:T(8,128)S(1)} %get-tuple-element.43, f32[51]{0:T(128)S(1)} %broadcast_multiply_fusion.4, bf16[51,3072]{1,0:T(8,128)(2,1)S(1)} %reshape.255, bf16[1024,3072]{1,0:T(8,128)(2,1)} %param.12), kind=kOutput, calls=%fused_computation.159 | convolution fusion | flops 321229696 | bytes 7023204 | tf_op jit(solution)/shard_map/transpose(jvp(transpose(jvp())))/dot_general | solution.py:114
  79.2 1.5 %collective-permute-start.4 = (bf16[51,1024]{1,0:T(8,128)(2,1)S(1)}, bf16[51,1024]{1,0:T(8,128)(2,1)S(1)}, u32[]{:S(2)}, u32[]{:S(2)}) collective-permute-start(bf16[51,1024]{1,0:T(8,128)(2,1)S(1)} %fusion.106), channel_id=1, source_target_pairs={{0,2},{1,3},{2,0},{3,1},{4,6},{5,7},{6,4},{7,5},{8,10},{9,11},{10,... | collective-permute-start | bytes 313352 | tf_op jit(solution)/shard_map/ppermute | solution.py:129
  81.5 2.6 %collective-permute-done.3 = bf16[51,1024]{1,0:T(8,128)(2,1)S(1)} collective-permute-done((bf16[51,1024]{1,0:T(8,128)(2,1)S(1)}, bf16[51,1024]{1,0:T(8,128)(2,1)S(1)}, u32[]{:S(2)}, u32[]{:S(2)}) %collective-permute-start.3) | collective-permute-done | bytes 104480 | tf_op jit(solution)/shard_map/ppermute | solution.py:129
  84.1 1.0 %collective-permute-done.4 = bf16[51,1024]{1,0:T(8,128)(2,1)S(1)} collective-permute-done((bf16[51,1024]{1,0:T(8,128)(2,1)S(1)}, bf16[51,1024]{1,0:T(8,128)(2,1)S(1)}, u32[]{:S(2)}, u32[]{:S(2)}) %collective-permute-start.4) | collective-permute-done | bytes 104480 | tf_op jit(solution)/shard_map/ppermute | solution.py:129
  85.2 1.2 %collective-permute-done.5 = bf16[51,1024]{1,0:T(8,128)(2,1)S(1)} collective-permute-done((bf16[51,1024]{1,0:T(8,128)(2,1)S(1)}, bf16[51,1024]{1,0:T(8,128)(2,1)S(1)}, u32[]{:S(2)}, u32[]{:S(2)}) %collective-permute-start.5) | collective-permute-done | bytes 104480 | tf_op jit(solution)/shard_map/ppermute | solution.py:129
  86.4 1.4 %fusion.21 = f32[192,1024]{1,0:T(8,128)} fusion(bf16[51,1024]{1,0:T(8,128)(2,1)S(1)} %collective-permute-done.5, bf16[51,1024]{1,0:T(8,128)(2,1)S(1)} %collective-permute-done.4, bf16[51,1024]{1,0:T(8,128)(2,1)S(1)} %collective-permute-done.3, bf16[51,1024]{1,0:T(8,128)(2,1)S(1)} %fusion.106, bf16[256,768]{1,0:T(8,128)(2,1)S(1)} %pad_maximum_fusion, ...), kind=kOutput, calls=%fused_computation.56 | convolution fusion | flops 102032640 | bytes 1377284 | tf_op jit(solution)/shard_map/vc,vd->cd/dot_general | solution.py:225
  (131 shorter events, 15.6 us)
Async XLA Ops:
  0.6 36.7 %copy-start = (bf16[1024,1024]{1,0:T(8,128)(2,1)S(1)}, bf16[1024,1024]{1,0:T(8,128)(2,1)}, u32[]{:S(2)}) copy-start(bf16[1024,1024]{1,0:T(8,128)(2,1)} %param.13) | copy-start | bytes 6291460
  0.6 19.8 %collective-permute-start = (bf16[64,768]{1,0:T(8,128)(2,1)}, bf16[64,768]{1,0:T(8,128)(2,1)S(1)}, u32[]{:S(2)}, u32[]{:S(2)}) collective-permute-start(bf16[64,768]{1,0:T(8,128)(2,1)} %param.9), channel_id=1, source_target_pairs={{0,1},{1,2},{2,3},{3,0},{4,5},{5,6},{6,7},{7,4},{8,9},{9,10},{10,1... | collective-permute-start | bytes 294920 | tf_op jit(solution)/shard_map/ppermute | solution.py:129
  3.7 16.8 %collective-permute-start.1 = (bf16[64,768]{1,0:T(8,128)(2,1)}, bf16[64,768]{1,0:T(8,128)(2,1)S(1)}, u32[]{:S(2)}, u32[]{:S(2)}) collective-permute-start(bf16[64,768]{1,0:T(8,128)(2,1)} %param.9), channel_id=1, source_target_pairs={{0,2},{1,3},{2,0},{3,1},{4,6},{5,7},{6,4},{7,5},{8,10},{9,11},{10,... | collective-permute-start | bytes 294920 | tf_op jit(solution)/shard_map/ppermute | solution.py:129
  5.2 15.2 %collective-permute-start.2 = (bf16[64,768]{1,0:T(8,128)(2,1)}, bf16[64,768]{1,0:T(8,128)(2,1)S(1)}, u32[]{:S(2)}, u32[]{:S(2)}) collective-permute-start(bf16[64,768]{1,0:T(8,128)(2,1)} %param.9), channel_id=1, source_target_pairs={{0,3},{1,0},{2,1},{3,2},{4,7},{5,4},{6,5},{7,6},{8,11},{9,8},{10,9... | collective-permute-start | bytes 294920 | tf_op jit(solution)/shard_map/ppermute | solution.py:129
  11.8 32.9 %copy-start.24 = (s32[51]{0:T(128)}, s32[51]{0:T(128)S(1)}, u32[]{:S(2)}) copy-start(s32[51]{0:T(128)S(1)} %get-tuple-element.19) | copy-start | bytes 616
  16.0 28.7 %copy-start.30 = (pred[256]{0:T(512)(128)(4,1)}, pred[256]{0:T(512)(128)(4,1)S(1)}, u32[]{:S(2)}) copy-start(pred[256]{0:T(512)(128)(4,1)S(1)} %broadcast_compare_fusion) | copy-start | bytes 772
  21.4 2.5 %copy-start.15 = (bf16[64,768]{1,0:T(8,128)(2,1)}, bf16[64,768]{1,0:T(8,128)(2,1)S(1)}, u32[]{:S(2)}) copy-start(bf16[64,768]{1,0:T(8,128)(2,1)S(1)} %get-tuple-element.13) | copy-start | bytes 294916
  21.4 2.5 %copy-start.17 = (bf16[64,768]{1,0:T(8,128)(2,1)}, bf16[64,768]{1,0:T(8,128)(2,1)S(1)}, u32[]{:S(2)}) copy-start(bf16[64,768]{1,0:T(8,128)(2,1)S(1)} %get-tuple-element.14) | copy-start | bytes 294916
  21.4 2.5 %copy-start.19 = (bf16[64,768]{1,0:T(8,128)(2,1)}, bf16[64,768]{1,0:T(8,128)(2,1)S(1)}, u32[]{:S(2)}) copy-start(bf16[64,768]{1,0:T(8,128)(2,1)S(1)} %get-tuple-element.15) | copy-start | bytes 294916
  21.4 2.5 %copy-start.21 = (bf16[64,768]{1,0:T(8,128)(2,1)}, bf16[64,768]{1,0:T(8,128)(2,1)S(1)}, u32[]{:S(2)}) copy-start(bf16[64,768]{1,0:T(8,128)(2,1)S(1)} %get-tuple-element.16) | copy-start | bytes 294916
  32.4 2.8 %copy-start.1 = (bf16[256,3072]{0,1:T(8,128)(2,1)S(1)}, bf16[256,3072]{0,1:T(8,128)(2,1)}, u32[]{:S(2)}) copy-start(bf16[256,3072]{0,1:T(8,128)(2,1)} %copy.62) | copy-start | bytes 4718596
  38.1 2.3 %copy-start.27 = (f32[256]{0:T(256)}, f32[256]{0:T(256)S(1)}, u32[]{:S(2)}) copy-start(f32[256]{0:T(256)S(1)} %broadcast_multiply_fusion.2) | copy-start | bytes 3076
  40.5 1.9 %copy-start.6 = (bf16[51,1,16,64]{3,2,1,0:T(8,128)(2,1)}, bf16[51,1,16,64]{3,2,1,0:T(8,128)(2,1)S(1)}, u32[]{:S(2)}) copy-start(bf16[51,1,16,64]{3,2,1,0:T(8,128)(2,1)S(1)} %get-tuple-element.10) | copy-start | bytes 313348
  40.5 1.9 %copy-start.8 = (bf16[51,1,16,64]{3,2,1,0:T(8,128)(2,1)}, bf16[51,1,16,64]{3,2,1,0:T(8,128)(2,1)S(1)}, u32[]{:S(2)}) copy-start(bf16[51,1,16,64]{3,2,1,0:T(8,128)(2,1)S(1)} %get-tuple-element.12) | copy-start | bytes 313348
  42.4 4.6 %copy-start.4 = (bf16[3,16,48,48]{3,2,1,0:T(8,128)(2,1)S(1)}, bf16[3,16,48,48]{3,2,1,0:T(8,128)(2,1)}, u32[]{:S(2)}) copy-start(bf16[3,16,48,48]{3,2,1,0:T(8,128)(2,1)} %param.16) | copy-start | bytes 663556
  49.1 1.9 %copy-start.23 = (bf16[256,768]{1,0:T(8,128)(2,1)S(1)}, bf16[256,768]{1,0:T(8,128)(2,1)}, u32[]{:S(2)}) copy-start(bf16[256,768]{1,0:T(8,128)(2,1)} %fusion.4) | copy-start | bytes 1179652
  51.0 5.3 %copy-start.3 = (f32[256,768]{1,0:T(8,128)S(1)}, f32[256,768]{1,0:T(8,128)}, u32[]{:S(2)}) copy-start(f32[256,768]{1,0:T(8,128)} %copy.61) | copy-start | bytes 2359300
  51.0 5.3 %copy-start.26 = (f32[256]{0:T(256)S(1)}, f32[256]{0:T(256)}, u32[]{:S(2)}) copy-start(f32[256]{0:T(256)} %fusion.118) | copy-start | bytes 3076
  51.0 5.3 %copy-start.29 = (f32[256]{0:T(256)S(1)}, f32[256]{0:T(256)}, u32[]{:S(2)}) copy-start(f32[256]{0:T(256)} %get-tuple-element.22) | copy-start | bytes 3076
  51.0 5.3 %copy-start.33 = (bf16[768,1024]{1,0:T(8,128)(2,1)S(1)}, bf16[768,1024]{1,0:T(8,128)(2,1)}, u32[]{:S(2)}) copy-start(bf16[768,1024]{1,0:T(8,128)(2,1)} %param.17) | copy-start | bytes 4718596
  59.6 2.8 %copy-start.10 = (bf16[256,768]{1,0:T(8,128)(2,1)}, bf16[256,768]{1,0:T(8,128)(2,1)S(1)}, u32[]{:S(2)}) copy-start(bf16[256,768]{1,0:T(8,128)(2,1)S(1)} %get-tuple-element.41) | copy-start | bytes 1179652
  59.6 4.8 %copy-start.5 = (bf16[3,16,48,48]{3,2,1,0:T(8,128)(2,1)S(1)}, bf16[3,16,48,48]{3,2,1,0:T(8,128)(2,1)}, u32[]{:S(2)}) copy-start(bf16[3,16,48,48]{3,2,1,0:T(8,128)(2,1)} %param.16) | copy-start | bytes 663556
  68.0 2.3 %copy-start.12 = (bf16[51,1,16,64]{3,2,1,0:T(8,128)(2,1)S(1)}, bf16[51,1,16,64]{3,2,1,0:T(8,128)(2,1)}, u32[]{:S(2)}) copy-start(bf16[51,1,16,64]{3,2,1,0:T(8,128)(2,1)} %copy-done.11) | copy-start | bytes 313348
  68.8 1.9 %copy-start.7 = (bf16[51,1,16,64]{3,2,1,0:T(8,128)(2,1)S(1)}, bf16[51,1,16,64]{3,2,1,0:T(8,128)(2,1)}, u32[]{:S(2)}) copy-start(bf16[51,1,16,64]{3,2,1,0:T(8,128)(2,1)} %copy-done.6) | copy-start | bytes 313348
  73.2 8.2 %copy-start.16 = (bf16[64,768]{1,0:T(8,128)(2,1)S(1)}, bf16[64,768]{1,0:T(8,128)(2,1)}, u32[]{:S(2)}) copy-start(bf16[64,768]{1,0:T(8,128)(2,1)} %copy-done.15) | copy-start | bytes 294916
  73.2 8.2 %copy-start.18 = (bf16[64,768]{1,0:T(8,128)(2,1)S(1)}, bf16[64,768]{1,0:T(8,128)(2,1)}, u32[]{:S(2)}) copy-start(bf16[64,768]{1,0:T(8,128)(2,1)} %copy-done.17) | copy-start | bytes 294916
  73.2 8.2 %copy-start.20 = (bf16[64,768]{1,0:T(8,128)(2,1)S(1)}, bf16[64,768]{1,0:T(8,128)(2,1)}, u32[]{:S(2)}) copy-start(bf16[64,768]{1,0:T(8,128)(2,1)} %copy-done.19) | copy-start | bytes 294916
  73.2 8.2 %copy-start.22 = (bf16[64,768]{1,0:T(8,128)(2,1)S(1)}, bf16[64,768]{1,0:T(8,128)(2,1)}, u32[]{:S(2)}) copy-start(bf16[64,768]{1,0:T(8,128)(2,1)} %copy-done.21) | copy-start | bytes 294916
  73.2 13.2 %copy-start.28 = (s32[204]{0:T(256)S(1)}, s32[204]{0:T(256)}, u32[]{:S(2)}) copy-start(s32[204]{0:T(256)} %pad_add_fusion.3) | copy-start | bytes 2452
  78.6 5.5 %collective-permute-start.3 = (bf16[51,1024]{1,0:T(8,128)(2,1)S(1)}, bf16[51,1024]{1,0:T(8,128)(2,1)S(1)}, u32[]{:S(2)}, u32[]{:S(2)}) collective-permute-start(bf16[51,1024]{1,0:T(8,128)(2,1)S(1)} %fusion.106), channel_id=1, source_target_pairs={{0,3},{1,0},{2,1},{3,2},{4,7},{5,4},{6,5},{7,6},{8,11},{9,8},{10,9... | collective-permute-start | bytes 313352 | tf_op jit(solution)/shard_map/ppermute | solution.py:129
  79.2 6.0 %collective-permute-start.4 = (bf16[51,1024]{1,0:T(8,128)(2,1)S(1)}, bf16[51,1024]{1,0:T(8,128)(2,1)S(1)}, u32[]{:S(2)}, u32[]{:S(2)}) collective-permute-start(bf16[51,1024]{1,0:T(8,128)(2,1)S(1)} %fusion.106), channel_id=1, source_target_pairs={{0,2},{1,3},{2,0},{3,1},{4,6},{5,7},{6,4},{7,5},{8,10},{9,11},{10,... | collective-permute-start | bytes 313352 | tf_op jit(solution)/shard_map/ppermute | solution.py:129
  80.7 5.7 %collective-permute-start.5 = (bf16[51,1024]{1,0:T(8,128)(2,1)S(1)}, bf16[51,1024]{1,0:T(8,128)(2,1)S(1)}, u32[]{:S(2)}, u32[]{:S(2)}) collective-permute-start(bf16[51,1024]{1,0:T(8,128)(2,1)S(1)} %fusion.106), channel_id=1, source_target_pairs={{0,1},{1,2},{2,3},{3,0},{4,5},{5,6},{6,7},{7,4},{8,9},{9,10},{10,1... | collective-permute-start | bytes 313352 | tf_op jit(solution)/shard_map/ppermute | solution.py:129
  (8 other events, 9.2 us)

commit v14 on v7

--- a/solution.py
+++ b/solution.py
@@ -104,9 +104,7 @@
         )
     activated = jax.nn.gelu(row_norm(convolved.reshape(total_rows, DD)), approximate=False)
     hidden = (lowered.astype(jnp.float32) + activated).astype(jnp.bfloat16)
-    return lax.optimization_barrier(
-        jnp.dot(hidden, dec_out, preferred_element_type=jnp.float32)
-    )
+    return jnp.dot(hidden, dec_out, preferred_element_type=jnp.float32)
 
 
 def copy_terms(

time: 89.2 us -> 79.1 us (0.89)
  local copies, waits for them, and re-layouts: 18.6 us -> 12.4 us
  other arithmetic: 13.5 us -> 9.67 us
    dot_general x2, matrix products: 3.13 us -> 8.57 us  [decoder_output(): return jnp.dot(hidden, dec_out, preferred_element_type=jnp.float32)]
    another operation x1 -> x0, other arithmetic: 3.03 us -> none  [decoder_output(): jax.nn.gelu(row_norm(convolved.reshape(total_rows, DD)), approximate=False)]
    dot_general x6, matrix products: 4.62 us -> 2.76 us  [decoder_output(): jnp.einsum('pgi,gio->pgo', padded[offset:offset + total_rows], conv_w[off...]
    reshape x2, local copies, waits for them, and re-layouts: 2.73 us -> 0.87 us  [attention_from(): context = split_project(projected.reshape(row_count, 3, HEADS, D // HEADS))]
    unnamed x105 -> x71, local copies, waits for them, and re-layouts: 3.64 us -> 2.23 us
    slice x1, local copies, waits for them, and re-layouts: 1.25 us -> 0.11 us  [split_project(): projected[:, 0].astype(jnp.float32)]
    reshape x1, local copies, waits for them, and re-layouts: 2.29 us -> 1.15 us  [decoder_output(): convolved.reshape(total_rows, DD)]
    reduce_sum x1 -> x0, other arithmetic: 1.11 us -> none  [copy_terms(): return jnp.sum(mismatch * mismatch)]
where the time goes in v14:
time: 79.1 us; the launch traced here: 78.7 us
  matrix products  40.3 us (51%)
  local copies, waits for them, and re-layouts  12.4 us (16%)
  other arithmetic  9.67 us (12%)
  starting transfers between devices  8.16 us (10%)
  waiting for transfers between devices  4.92 us (6%)
  between operations  3.2 us (4%)
    dot_general x2, matrix products, decoder_output(): return jnp.dot(hidden, dec_out, preferred_element_type=jnp.float32)  8.57 us
    ppermute x6, starting transfers between devices, ring_gather(): parts.append(lax.ppermute(values, 'mask', pairs))  8.16 us
    dot_general x1, matrix products, copy_terms(): branch = attention_from(reuse_rows(visible_in, w_qkv, projected), w_out)  5 us
    ppermute x6, waiting for transfers between devices, ring_gather(): parts.append(lax.ppermute(values, 'mask', pairs))  4.92 us
    dot_general x2, matrix products, decoder_output(): jnp.dot(visible_out, dec_in, preferred_element_type=jnp.float32)  4.57 us
    dot_general x1, matrix products, project_rows(): jnp.dot(normed, w_qkv, preferred_element_type=jnp.float32)  3.1 us
    dot_general x4, matrix products, mix_heads(): jnp.einsum('hqk,khd->qhd', weights, values, preferred_element_type=jnp.fl...  2.83 us
    reduce_sum x1, other arithmetic, row_norm(): centred = values - average  2.76 us
  transfers between devices with their start and end apart: 6, of which 3 were waited for; matrix products, arithmetic and copies ran while one was open for 7% of the time, Pallas kernels for 0%

profile of v14, /device:TPU:0, one launch (start us, length us, event | category | flops | bytes accessed | tf_op | source)
XLA Modules:
  0.0 78.7 jit_solution(624255757404109492)
XLA Ops:
  0.6 3.0 %collective-permute-start = (bf16[64,768]{1,0:T(8,128)(2,1)}, bf16[64,768]{1,0:T(8,128)(2,1)S(1)}, u32[]{:S(2)}, u32[]{:S(2)}) collective-permute-start(bf16[64,768]{1,0:T(8,128)(2,1)} %param.9), channel_id=1, source_target_pairs={{0,1},{1,2},{2,3},{3,0},{4,5},{5,6},{6,7},{7,4},{8,9},{9,10},{10,1... | collective-permute-start | bytes 294920 | tf_op jit(solution)/shard_map/ppermute | solution.py:132
  3.7 1.5 %collective-permute-start.1 = (bf16[64,768]{1,0:T(8,128)(2,1)}, bf16[64,768]{1,0:T(8,128)(2,1)S(1)}, u32[]{:S(2)}, u32[]{:S(2)}) collective-permute-start(bf16[64,768]{1,0:T(8,128)(2,1)} %param.9), channel_id=1, source_target_pairs={{0,2},{1,3},{2,0},{3,1},{4,6},{5,7},{6,4},{7,5},{8,10},{9,11},{10,... | collective-permute-start | bytes 294920 | tf_op jit(solution)/shard_map/ppermute | solution.py:132
  5.2 1.4 %collective-permute-start.2 = (bf16[64,768]{1,0:T(8,128)(2,1)}, bf16[64,768]{1,0:T(8,128)(2,1)S(1)}, u32[]{:S(2)}, u32[]{:S(2)}) collective-permute-start(bf16[64,768]{1,0:T(8,128)(2,1)} %param.9), channel_id=1, source_target_pairs={{0,3},{1,0},{2,1},{3,2},{4,7},{5,4},{6,5},{7,6},{8,11},{9,8},{10,9... | collective-permute-start | bytes 294920 | tf_op jit(solution)/shard_map/ppermute | solution.py:132
  8.8 1.2 %gather_fusion = s32[4,51]{1,0:T(4,128)S(1)} fusion(s32[4,51]{1,0:T(4,128)} %param.10, s32[1024]{0:T(1024)S(1)} %pad_clamp_fusion), kind=kCustom, calls=%fused_computation | custom fusion | bytes 1648 | tf_op jit(solution)/shard_map/gather | solution.py:216
  10.6 1.9 %convolution_reduce_fusion = bf16[768]{0:T(1024)(128)(2,1)S(1)} fusion(bf16[1024,1]{0,1:T(2,128)(2,1)S(1)} %reshape.270, bf16[1024,768]{1,0:T(8,128)(2,1)} %param.15), kind=kOutput, calls=%fused_computation.58 | convolution fusion | flops 1572864 | bytes 1576448 | tf_op jit(solution)/shard_map/jvp()/dot_general | solution.py:90
  12.5 1.3 %select_select_fusion.3 = (bf16[64,768]{1,0:T(8,128)(2,1)S(1)}, bf16[64,768]{1,0:T(8,128)(2,1)S(1)}, bf16[64,768]{1,0:T(8,128)(2,1)S(1)}, bf16[64,768]{1,0:T(8,128)(2,1)S(1)}) fusion(bf16[64,768]{1,0:T(8,128)(2,1)S(1)} %collective-permute-done, bf16[64,768]{1,0:T(8,128)(2,1)S(1)} %collective-permute-done.1, bf16[64,768]{1,0:T(8,128)(2,1)S(1)} %collective-permute-done.2, ...), kind=kLoop, calls=%fused_computation.182 | loop fusion | flops 589824 | bytes 786444 | tf_op jit(solution)/shard_map/jit(_where)/select_n | solution.py:143
  13.9 2.2 %convert_reduce_fusion = (f32[256]{0:T(256)S(1)}, bf16[256,1024]{1,0:T(8,128)(2,1)S(1)}) fusion(bf16[768,1024]{1,0:T(8,128)(2,1)} %param.11, bf16[64,768]{1,0:T(8,128)(2,1)S(1)} %get-tuple-element.14, bf16[64,768]{1,0:T(8,128)(2,1)S(1)} %get-tuple-element.15, bf16[64,768]{1,0:T(8,128)(2,1)S(1)} %get-tuple-element.16, bf16[64,768]{1,0:T(8,128)(2,1)S(1)} %get-tuple-element.13), kind=kOutput, calls=%fused_computation.14 | convolution fusion | flops 405012224 | bytes 2491392 | tf_op jit(solution)/shard_map/dot_general | solution.py:178
  16.4 3.1 %convolution_convert_fusion = bf16[256,3072]{1,0:T(8,128)(2,1)} fusion(bf16[1024,3072]{1,0:T(8,128)(2,1)S(1)} %copy-done.2, bf16[256,1024]{1,0:T(8,128)(2,1)S(1)} %get-tuple-element.22, f32[256]{0:T(256)S(1)} %add_rsqrt_fusion.3, f32[256]{0:T(256)S(1)} %broadcast_multiply_fusion.3), kind=kOutput, calls=%fused_computation.3 | convolution fusion | flops 1612447744 | bytes 8390656 | tf_op jit(solution)/shard_map/dot_general | solution.py:48
  19.5 2.6 %copy.62 = bf16[256,3072]{0,1:T(8,128)(2,1)} copy(bf16[256,3072]{1,0:T(8,128)(2,1)} %convolution_convert_fusion) | data formatting | bytes 3145728 | tf_op jit(solution)/shard_map/convert_element_type | solution.py:48
  22.1 1.9 %convolution_convert_fusion.1 = bf16[51,3072]{1,0:T(8,128)(2,1)S(1)} fusion(bf16[256,3072]{1,0:T(8,128)(2,1)} %convolution_convert_fusion, s32[51]{0:T(128)S(1)} %dynamic-slice_bitcast_fusion), kind=kOutput, calls=%fused_computation.5 | convolution fusion | flops 80385792 | bytes 1886412 | tf_op jit(solution)/shard_map/dot_general | solution.py:189
  24.0 0.9 %fusion.137 = (f32[51]{0:T(128)}, f32[51,1024]{1,0:T(8,128)S(1)}) fusion(bf16[256,1024]{1,0:T(8,128)(2,1)S(1)} %get-tuple-element.22, s32[51]{0:T(128)S(1)} %dynamic-slice_bitcast_fusion), kind=kOutput, calls=%fused_computation.240 | convolution fusion | flops 26908364 | bytes 733592 | tf_op jit(solution)/shard_map/dot_general | solution.py:183
  25.2 1.0 %fusion = (f32[16,256]{1,0:T(8,128)S(1)}, f32[16,256,256]{1,2,0:T(8,128)S(1)}) fusion(f32[256,16]{0,1:T(8,128)S(1)} %get-tuple-element.46, bf16[256,3,16,64]{0,3,2,1:T(8,128)(2,1)S(1)} %bitcast.165, f32[256,16]{0,1:T(8,128)S(1)} %get-tuple-element.47), kind=kOutput, calls=%fused_computation.4 | convolution fusion | flops 137883648 | bytes 5292032 | tf_op jit(solution)/shard_map/qhd,khd->hqk/dot_general | solution.py:31
  26.2 0.9 %fusion.3 = bf16[16,64,256]{2,1,0:T(8,128)(2,1)S(1)} fusion(f32[16,256,256]{1,2,0:T(8,128)S(1)} %get-tuple-element.24, f32[16,256]{1,0:T(8,128)S(1)} %get-tuple-element.23, bf16[256,3,16,64]{0,3,2,1:T(8,128)(2,1)S(1)} %bitcast.166), kind=kOutput, calls=%fused_computation.15 | convolution fusion | flops 137625600 | bytes 5259264 | tf_op jit(solution)/shard_map/hqk,khd->qhd/dot_general | solution.py:36
  27.9 1.0 %copy-done.3 = f32[256,1024]{1,0:T(8,128)} copy-done((f32[256,1024]{1,0:T(8,128)}, f32[256,1024]{1,0:T(8,128)S(1)}, u32[]{:S(2)}) %copy-start.3) | copy-done | bytes 1048600
  32.1 2.3 %convolution_convert_fusion.18 = bf16[51,768]{1,0:T(8,128)(2,1)S(1)} fusion(bf16[1024,768]{1,0:T(8,128)(2,1)} %param.15, f32[51,1024]{1,0:T(8,128)S(1)} %get-tuple-element.34, bf16[51,1024]{1,0:T(8,128)(2,1)S(1)} %reshape.248, bf16[1024,1024]{1,0:T(8,128)(2,1)S(1)} %copy-done), kind=kOutput, calls=%fused_computation.56 | convolution fusion | flops 187314432 | bytes 4061696 | tf_op jit(solution)/shard_map/jvp()/dot_general | solution.py:87
  34.4 1.1 %fusion.4 = bf16[256,768]{1,0:T(8,128)(2,1)} fusion(bf16[51,768]{1,0:T(8,128)(2,1)S(1)} %convolution_convert_fusion.18, bf16[768]{0:T(1024)(128)(2,1)S(1)} %convolution_reduce_fusion, pred[256]{0:T(512)(128)(4,1)S(1)} %broadcast_compare_fusion, s32[51]{0:T(128)S(1)} %dynamic-slice_bitcast_fusion), kind=kOutput, calls=%fused_computation.20 | convolution fusion | flops 20263680 | bytes 473548 | tf_op jit(solution)/shard_map/jvp()/dot_general | solution.py:93
  35.5 1.2 %copy.57 = bf16[256,768]{0,1:T(8,128)(2,1)S(1)} copy(bf16[256,768]{1,0:T(8,128)(2,1)} %fusion.4) | data formatting | bytes 786432 | tf_op jit(solution)/shard_map/jvp()/convert_element_type | solution.py:94
  37.4 1.4 %fusion.136 = (f32[256]{0:T(256)S(1)}, f32[16,256,48]{1,2,0:T(8,128)S(1)}) fusion(f32[16,256,48]{1,2,0:T(8,128)S(1)} %convolution_add_fusion.1, bf16[256,16,48]{0,2,1:T(8,128)(2,1)S(1)} %bitcast.173, bf16[3,16,48,48]{3,2,1,0:T(8,128)(2,1)} %param.16), kind=kOutput, calls=%fused_computation.239 | convolution fusion | flops 19267328 | bytes 2163712 | tf_op jit(solution)/shard_map/jvp(pgi,gio->pgo)/dot_general | solution.py:99
  39.5 1.1 %copy.61 = f32[256,768]{1,0:T(8,128)} copy(f32[256,768]{0,1:T(8,128)S(1)} %bitcast.167) | data formatting | bytes 1572864 | tf_op jit(solution)/shard_map/jvp()/reshape | solution.py:105
  40.7 5.2 %multiply_reduce_fusion = (f32[]{:T(128)}, f32[256,1024]{1,0:T(8,128)S(1)}) fusion(f32[256]{0:T(256)} %get-tuple-element.18, f32[256]{0:T(256)} %add_rsqrt_fusion.2, f32[256,1024]{1,0:T(8,128)} %copy-done.3, f32[256]{0:T(256)} %copy-done.28, bf16[768,1024]{1,0:T(8,128)(2,1)} %param.17, bf16[256,768]{1,0:T(8,128)(2,1)S(1)} %copy-done.24, ...), kind=kOutput, calls=%fused_computation.67 | convolution fusion | flops 418709504 | bytes 4854788 | tf_op jit(solution)/shard_map/jvp()/dot_general | solution.py:107
  46.0 3.3 %multiply_reduce_fusion.2 = (f32[256]{0:T(256)S(1)}, bf16[256,768]{1,0:T(8,128)(2,1)S(1)}) fusion(f32[256,768]{1,0:T(8,128)S(1)} %copy-done.4, f32[256]{0:T(256)S(1)} %broadcast_multiply_fusion.1, f32[256]{0:T(256)S(1)} %copy-done.27, bf16[768,1024]{1,0:T(8,128)(2,1)S(1)} %copy-done.34, f32[256,1024]{1,0:T(8,128)S(1)} %get-tuple-element.43, ...), kind=kOutput, calls=%fused_computation.92 | convolution fusion | flops 419495680 | bytes 3805184 | tf_op jit(solution)/shard_map/transpose(jvp())/dot_general | solution.py:107
  49.3 2.8 %fusion.132 = (f32[256]{0:T(256)S(1)}, f32[256,768]{1,0:T(8,128)S(1)}) fusion(f32[256]{0:T(256)S(1)} %multiply_multiply_fusion.8, bf16[256,768]{1,0:T(8,128)(2,1)S(1)} %get-tuple-element.32, f32[256]{0:T(256)S(1)} %copy-done.27, f32[256,768]{1,0:T(8,128)S(1)} %copy-done.4, f32[256]{0:T(256)S(1)} %broadcast_multiply_fusion.1), kind=kLoop, calls=%fused_computation.235 | loop fusion | flops 15531776 | bytes 1970176 | tf_op jit(solution)/shard_map/transpose(jvp())/reduce_sum | solution.py:19
  52.1 0.8 %broadcast_add_fusion = bf16[256,768]{1,0:T(8,128)(2,1)} fusion(f32[256,768]{1,0:T(8,128)S(1)} %get-tuple-element.9, f32[256]{0:T(256)S(1)} %negate_multiply_fusion.1), kind=kLoop, calls=%fused_computation.144 | loop fusion | flops 393216 | bytes 1180672 | tf_op jit(solution)/shard_map/transpose(jvp())/add_any | solution.py:18
  53.0 1.2 %copy.64 = bf16[256,768]{0,1:T(8,128)(2,1)S(1)} copy(bf16[256,768]{1,0:T(8,128)(2,1)} %broadcast_add_fusion) | data formatting | bytes 786432 | tf_op jit(solution)/shard_map/transpose(jvp())/add_any | solution.py:18
  55.5 2.3 %convolution_convert_fusion.13 = bf16[51,1024]{1,0:T(8,128)(2,1)S(1)} fusion(bf16[1024,768]{1,0:T(8,128)(2,1)} %param.15, bf16[256,768]{1,0:T(8,128)(2,1)} %copy-done.11, bf16[256,768]{1,0:T(8,128)(2,1)S(1)} %copy.68, pred[256]{0:T(512)(128)(4,1)S(1)} %copy-done.32, s32[51]{0:T(128)S(1)} %copy-done.26), kind=kOutput, calls=%fused_computation.49 | convolution fusion | flops 100964352 | bytes 2464204 | tf_op jit(solution)/shard_map/transpose(jvp())/dot_general | solution.py:87
  58.8 1.4 %fusion.17 = bf16[51,1,16,64]{3,0,2,1:T(8,128)(2,1)S(1)} fusion(bf16[51,16,64]{2,1,0:T(8,128)(2,1)S(1)} %reshape.255, f32[16,51,51]{1,2,0:T(8,128)} %copy-done.14, f32[16,51]{1,0:T(8,128)S(1)} %get-tuple-element.27), kind=kOutput, calls=%fused_computation.45 | convolution fusion | flops 5462304 | bytes 378624 | tf_op jit(solution)/shard_map/transpose(jvp(hqk,khd->qhd))/dot_general | solution.py:36
  63.0 5.0 %multiply_reduce_fusion.5 = (f32[51]{0:T(128)S(1)}, f32[51]{0:T(128)S(1)}, f32[51,1024]{1,0:T(8,128)S(1)}) fusion(f32[51,1024]{1,0:T(8,128)S(1)} %get-tuple-element.34, f32[51]{0:T(128)S(1)} %broadcast_multiply_fusion.4, bf16[51,3072]{1,0:T(8,128)(2,1)S(1)} %reshape.256, bf16[1024,3072]{1,0:T(8,128)(2,1)} %param.12), kind=kOutput, calls=%fused_computation.160 | convolution fusion | flops 321229696 | bytes 7023204 | tf_op jit(solution)/shard_map/transpose(jvp())/dot_general | solution.py:117
  68.9 1.5 %collective-permute-start.4 = (bf16[51,1024]{1,0:T(8,128)(2,1)S(1)}, bf16[51,1024]{1,0:T(8,128)(2,1)S(1)}, u32[]{:S(2)}, u32[]{:S(2)}) collective-permute-start(bf16[51,1024]{1,0:T(8,128)(2,1)S(1)} %fusion.106), channel_id=1, source_target_pairs={{0,2},{1,3},{2,0},{3,1},{4,6},{5,7},{6,4},{7,5},{8,10},{9,11},{10,... | collective-permute-start | bytes 313352 | tf_op jit(solution)/shard_map/ppermute | solution.py:132
  71.2 2.6 %collective-permute-done.3 = bf16[51,1024]{1,0:T(8,128)(2,1)S(1)} collective-permute-done((bf16[51,1024]{1,0:T(8,128)(2,1)S(1)}, bf16[51,1024]{1,0:T(8,128)(2,1)S(1)}, u32[]{:S(2)}, u32[]{:S(2)}) %collective-permute-start.3) | collective-permute-done | bytes 104480 | tf_op jit(solution)/shard_map/ppermute | solution.py:132
  73.9 1.0 %collective-permute-done.4 = bf16[51,1024]{1,0:T(8,128)(2,1)S(1)} collective-permute-done((bf16[51,1024]{1,0:T(8,128)(2,1)S(1)}, bf16[51,1024]{1,0:T(8,128)(2,1)S(1)}, u32[]{:S(2)}, u32[]{:S(2)}) %collective-permute-start.4) | collective-permute-done | bytes 104480 | tf_op jit(solution)/shard_map/ppermute | solution.py:132
  74.9 1.3 %collective-permute-done.5 = bf16[51,1024]{1,0:T(8,128)(2,1)S(1)} collective-permute-done((bf16[51,1024]{1,0:T(8,128)(2,1)S(1)}, bf16[51,1024]{1,0:T(8,128)(2,1)S(1)}, u32[]{:S(2)}, u32[]{:S(2)}) %collective-permute-start.5) | collective-permute-done | bytes 104480 | tf_op jit(solution)/shard_map/ppermute | solution.py:132
  76.1 1.4 %fusion.21 = f32[192,1024]{1,0:T(8,128)} fusion(bf16[51,1024]{1,0:T(8,128)(2,1)S(1)} %collective-permute-done.5, bf16[51,1024]{1,0:T(8,128)(2,1)S(1)} %collective-permute-done.4, bf16[51,1024]{1,0:T(8,128)(2,1)S(1)} %collective-permute-done.3, bf16[51,1024]{1,0:T(8,128)(2,1)S(1)} %fusion.106, bf16[256,768]{1,0:T(8,128)(2,1)S(1)} %pad_maximum_fusion, ...), kind=kOutput, calls=%fused_computation.57 | convolution fusion | flops 102032640 | bytes 1377284 | tf_op jit(solution)/shard_map/vc,vd->cd/dot_general | solution.py:222
  (133 shorter events, 14.7 us)
Async XLA Ops:
  0.6 26.4 %copy-start = (bf16[1024,1024]{1,0:T(8,128)(2,1)S(1)}, bf16[1024,1024]{1,0:T(8,128)(2,1)}, u32[]{:S(2)}) copy-start(bf16[1024,1024]{1,0:T(8,128)(2,1)} %param.13) | copy-start | bytes 6291460
  0.6 11.8 %collective-permute-start = (bf16[64,768]{1,0:T(8,128)(2,1)}, bf16[64,768]{1,0:T(8,128)(2,1)S(1)}, u32[]{:S(2)}, u32[]{:S(2)}) collective-permute-start(bf16[64,768]{1,0:T(8,128)(2,1)} %param.9), channel_id=1, source_target_pairs={{0,1},{1,2},{2,3},{3,0},{4,5},{5,6},{6,7},{7,4},{8,9},{9,10},{10,1... | collective-permute-start | bytes 294920 | tf_op jit(solution)/shard_map/ppermute | solution.py:132
  3.7 8.8 %collective-permute-start.1 = (bf16[64,768]{1,0:T(8,128)(2,1)}, bf16[64,768]{1,0:T(8,128)(2,1)S(1)}, u32[]{:S(2)}, u32[]{:S(2)}) collective-permute-start(bf16[64,768]{1,0:T(8,128)(2,1)} %param.9), channel_id=1, source_target_pairs={{0,2},{1,3},{2,0},{3,1},{4,6},{5,7},{6,4},{7,5},{8,10},{9,11},{10,... | collective-permute-start | bytes 294920 | tf_op jit(solution)/shard_map/ppermute | solution.py:132
  5.2 7.3 %collective-permute-start.2 = (bf16[64,768]{1,0:T(8,128)(2,1)}, bf16[64,768]{1,0:T(8,128)(2,1)S(1)}, u32[]{:S(2)}, u32[]{:S(2)}) collective-permute-start(bf16[64,768]{1,0:T(8,128)(2,1)} %param.9), channel_id=1, source_target_pairs={{0,3},{1,0},{2,1},{3,2},{4,7},{5,4},{6,5},{7,6},{8,11},{9,8},{10,9... | collective-permute-start | bytes 294920 | tf_op jit(solution)/shard_map/ppermute | solution.py:132
  7.3 27.1 %copy-start.25 = (s32[51]{0:T(128)}, s32[51]{0:T(128)S(1)}, u32[]{:S(2)}) copy-start(s32[51]{0:T(128)S(1)} %dynamic-slice_bitcast_fusion) | copy-start | bytes 616
  7.5 26.9 %copy-start.31 = (pred[256]{0:T(512)(128)(4,1)}, pred[256]{0:T(512)(128)(4,1)S(1)}, u32[]{:S(2)}) copy-start(pred[256]{0:T(512)(128)(4,1)S(1)} %broadcast_compare_fusion) | copy-start | bytes 772
  10.6 5.8 %copy-start.2 = (bf16[1024,3072]{1,0:T(8,128)(2,1)S(1)}, bf16[1024,3072]{1,0:T(8,128)(2,1)}, u32[]{:S(2)}) copy-start(bf16[1024,3072]{1,0:T(8,128)(2,1)} %param.12) | copy-start | bytes 18874372
  13.8 2.5 %copy-start.16 = (bf16[64,768]{1,0:T(8,128)(2,1)}, bf16[64,768]{1,0:T(8,128)(2,1)S(1)}, u32[]{:S(2)}) copy-start(bf16[64,768]{1,0:T(8,128)(2,1)S(1)} %get-tuple-element.13) | copy-start | bytes 294916
  13.8 2.5 %copy-start.18 = (bf16[64,768]{1,0:T(8,128)(2,1)}, bf16[64,768]{1,0:T(8,128)(2,1)S(1)}, u32[]{:S(2)}) copy-start(bf16[64,768]{1,0:T(8,128)(2,1)S(1)} %get-tuple-element.14) | copy-start | bytes 294916
  13.8 2.5 %copy-start.20 = (bf16[64,768]{1,0:T(8,128)(2,1)}, bf16[64,768]{1,0:T(8,128)(2,1)S(1)}, u32[]{:S(2)}) copy-start(bf16[64,768]{1,0:T(8,128)(2,1)S(1)} %get-tuple-element.15) | copy-start | bytes 294916
  13.9 2.5 %copy-start.22 = (bf16[64,768]{1,0:T(8,128)(2,1)}, bf16[64,768]{1,0:T(8,128)(2,1)S(1)}, u32[]{:S(2)}) copy-start(bf16[64,768]{1,0:T(8,128)(2,1)S(1)} %get-tuple-element.16) | copy-start | bytes 294916
  22.1 2.8 %copy-start.1 = (bf16[256,3072]{0,1:T(8,128)(2,1)S(1)}, bf16[256,3072]{0,1:T(8,128)(2,1)}, u32[]{:S(2)}) copy-start(bf16[256,3072]{0,1:T(8,128)(2,1)} %copy.62) | copy-start | bytes 4718596
  27.9 2.3 %copy-start.28 = (f32[256]{0:T(256)}, f32[256]{0:T(256)S(1)}, u32[]{:S(2)}) copy-start(f32[256]{0:T(256)S(1)} %broadcast_multiply_fusion.2) | copy-start | bytes 3076
  30.2 1.9 %copy-start.7 = (bf16[51,1,16,64]{3,2,1,0:T(8,128)(2,1)}, bf16[51,1,16,64]{3,2,1,0:T(8,128)(2,1)S(1)}, u32[]{:S(2)}) copy-start(bf16[51,1,16,64]{3,2,1,0:T(8,128)(2,1)S(1)} %get-tuple-element.10) | copy-start | bytes 313348
  30.2 1.9 %copy-start.9 = (bf16[51,1,16,64]{3,2,1,0:T(8,128)(2,1)}, bf16[51,1,16,64]{3,2,1,0:T(8,128)(2,1)S(1)}, u32[]{:S(2)}) copy-start(bf16[51,1,16,64]{3,2,1,0:T(8,128)(2,1)S(1)} %get-tuple-element.12) | copy-start | bytes 313348
  32.1 4.6 %copy-start.5 = (bf16[3,16,48,48]{3,2,1,0:T(8,128)(2,1)S(1)}, bf16[3,16,48,48]{3,2,1,0:T(8,128)(2,1)}, u32[]{:S(2)}) copy-start(bf16[3,16,48,48]{3,2,1,0:T(8,128)(2,1)} %param.16) | copy-start | bytes 663556
  38.8 1.9 %copy-start.24 = (bf16[256,768]{1,0:T(8,128)(2,1)S(1)}, bf16[256,768]{1,0:T(8,128)(2,1)}, u32[]{:S(2)}) copy-start(bf16[256,768]{1,0:T(8,128)(2,1)} %fusion.4) | copy-start | bytes 1179652
  40.7 5.3 %copy-start.4 = (f32[256,768]{1,0:T(8,128)S(1)}, f32[256,768]{1,0:T(8,128)}, u32[]{:S(2)}) copy-start(f32[256,768]{1,0:T(8,128)} %copy.61) | copy-start | bytes 2359300
  40.7 5.3 %copy-start.27 = (f32[256]{0:T(256)S(1)}, f32[256]{0:T(256)}, u32[]{:S(2)}) copy-start(f32[256]{0:T(256)} %fusion.118) | copy-start | bytes 3076
  40.7 5.3 %copy-start.30 = (f32[256]{0:T(256)S(1)}, f32[256]{0:T(256)}, u32[]{:S(2)}) copy-start(f32[256]{0:T(256)} %get-tuple-element.17) | copy-start | bytes 3076
  40.7 5.3 %copy-start.34 = (bf16[768,1024]{1,0:T(8,128)(2,1)S(1)}, bf16[768,1024]{1,0:T(8,128)(2,1)}, u32[]{:S(2)}) copy-start(bf16[768,1024]{1,0:T(8,128)(2,1)} %param.17) | copy-start | bytes 4718596
  49.3 2.8 %copy-start.11 = (bf16[256,768]{1,0:T(8,128)(2,1)}, bf16[256,768]{1,0:T(8,128)(2,1)S(1)}, u32[]{:S(2)}) copy-start(bf16[256,768]{1,0:T(8,128)(2,1)S(1)} %get-tuple-element.32) | copy-start | bytes 1179652
  49.3 4.8 %copy-start.6 = (bf16[3,16,48,48]{3,2,1,0:T(8,128)(2,1)S(1)}, bf16[3,16,48,48]{3,2,1,0:T(8,128)(2,1)}, u32[]{:S(2)}) copy-start(bf16[3,16,48,48]{3,2,1,0:T(8,128)(2,1)} %param.16) | copy-start | bytes 663556
  57.8 2.3 %copy-start.13 = (bf16[51,1,16,64]{3,2,1,0:T(8,128)(2,1)S(1)}, bf16[51,1,16,64]{3,2,1,0:T(8,128)(2,1)}, u32[]{:S(2)}) copy-start(bf16[51,1,16,64]{3,2,1,0:T(8,128)(2,1)} %copy-done.12) | copy-start | bytes 313348
  62.9 8.2 %copy-start.17 = (bf16[64,768]{1,0:T(8,128)(2,1)S(1)}, bf16[64,768]{1,0:T(8,128)(2,1)}, u32[]{:S(2)}) copy-start(bf16[64,768]{1,0:T(8,128)(2,1)} %copy-done.16) | copy-start | bytes 294916
  62.9 8.2 %copy-start.19 = (bf16[64,768]{1,0:T(8,128)(2,1)S(1)}, bf16[64,768]{1,0:T(8,128)(2,1)}, u32[]{:S(2)}) copy-start(bf16[64,768]{1,0:T(8,128)(2,1)} %copy-done.18) | copy-start | bytes 294916
  62.9 8.2 %copy-start.21 = (bf16[64,768]{1,0:T(8,128)(2,1)S(1)}, bf16[64,768]{1,0:T(8,128)(2,1)}, u32[]{:S(2)}) copy-start(bf16[64,768]{1,0:T(8,128)(2,1)} %copy-done.20) | copy-start | bytes 294916
  62.9 8.2 %copy-start.23 = (bf16[64,768]{1,0:T(8,128)(2,1)S(1)}, bf16[64,768]{1,0:T(8,128)(2,1)}, u32[]{:S(2)}) copy-start(bf16[64,768]{1,0:T(8,128)(2,1)} %copy-done.22) | copy-start | bytes 294916
  62.9 13.2 %copy-start.29 = (s32[204]{0:T(256)S(1)}, s32[204]{0:T(256)}, u32[]{:S(2)}) copy-start(s32[204]{0:T(256)} %eq.93) | copy-start | bytes 2452
  68.3 5.5 %collective-permute-start.3 = (bf16[51,1024]{1,0:T(8,128)(2,1)S(1)}, bf16[51,1024]{1,0:T(8,128)(2,1)S(1)}, u32[]{:S(2)}, u32[]{:S(2)}) collective-permute-start(bf16[51,1024]{1,0:T(8,128)(2,1)S(1)} %fusion.106), channel_id=1, source_target_pairs={{0,3},{1,0},{2,1},{3,2},{4,7},{5,4},{6,5},{7,6},{8,11},{9,8},{10,9... | collective-permute-start | bytes 313352 | tf_op jit(solution)/shard_map/ppermute | solution.py:132
  68.9 6.0 %collective-permute-start.4 = (bf16[51,1024]{1,0:T(8,128)(2,1)S(1)}, bf16[51,1024]{1,0:T(8,128)(2,1)S(1)}, u32[]{:S(2)}, u32[]{:S(2)}) collective-permute-start(bf16[51,1024]{1,0:T(8,128)(2,1)S(1)} %fusion.106), channel_id=1, source_target_pairs={{0,2},{1,3},{2,0},{3,1},{4,6},{5,7},{6,4},{7,5},{8,10},{9,11},{10,... | collective-permute-start | bytes 313352 | tf_op jit(solution)/shard_map/ppermute | solution.py:132
  70.4 5.7 %collective-permute-start.5 = (bf16[51,1024]{1,0:T(8,128)(2,1)S(1)}, bf16[51,1024]{1,0:T(8,128)(2,1)S(1)}, u32[]{:S(2)}, u32[]{:S(2)}) collective-permute-start(bf16[51,1024]{1,0:T(8,128)(2,1)S(1)} %fusion.106), channel_id=1, source_target_pairs={{0,1},{1,2},{2,3},{3,0},{4,5},{5,6},{6,7},{7,4},{8,9},{9,10},{10,1... | collective-permute-start | bytes 313352 | tf_op jit(solution)/shard_map/ppermute | solution.py:132
  (9 other events, 11.1 us)

commit v15 on v11

--- a/solution.py
+++ b/solution.py
@@ -56,6 +56,34 @@
 
 def attention_branch(inputs, w_qkv, w_out):
     return attention_from(project_rows(inputs, w_qkv), w_out)
+
+
+def teacher_branch(embedded, w_qkv, w_out):
+    row_count = embedded.shape[0]
+    head_dim = D // HEADS
+    normed = row_norm(embedded.astype(jnp.float32)).astype(jnp.bfloat16)
+    projected_t = jnp.einsum(
+        "sd,dk->ks", normed, w_qkv, preferred_element_type=jnp.float32
+    ).astype(jnp.bfloat16)
+    heads = projected_t.reshape(3, HEADS, head_dim, row_count)
+    queries = head_norm_cols(heads[0].astype(jnp.float32)).astype(jnp.bfloat16)
+    key_rows = head_norm_cols(heads[1].astype(jnp.float32)).astype(jnp.bfloat16)
+    score_scale = 1.0 / math.sqrt(head_dim)
+    scores = (
+        jnp.einsum("hdq,hdk->hqk", queries, key_rows, preferred_element_type=jnp.float32)
+        * score_scale
+    )
+    exponent = jnp.exp(scores)
+    weights = (exponent / jnp.sum(exponent, axis=-1, keepdims=True)).astype(jnp.bfloat16)
+    context = jnp.einsum(
+        "hqk,hdk->qhd", weights, heads[2], preferred_element_type=jnp.float32
+    ).astype(jnp.bfloat16)
+    branch = jnp.dot(context.reshape(row_count, D), w_out, preferred_element_type=jnp.float32)
+    return projected_t, branch
+
+
+def head_norm_cols(values):
+    return values * lax.rsqrt(jnp.mean(values * values, axis=-2, keepdims=True) + EPSILON)
 
 
 @jax.custom_vjp
@@ -181,10 +209,9 @@
         jnp.bfloat16
     )
     if HEADS * total_rows * total_rows * 4 <= (1 << 24):
-        clip_projected = project_rows(embedded, w_qkv)
-        branch = attention_from(clip_projected, w_out)
-        visible_projected = jnp.dot(
-            own_picks, clip_projected, preferred_element_type=jnp.float32
+        projected_t, branch = teacher_branch(embedded, w_qkv, w_out)
+        visible_projected = jnp.einsum(
+            "vs,ks->vk", own_picks, projected_t, preferred_element_type=jnp.float32
         ).astype(jnp.bfloat16)
     else:
         branch = split_teacher(embedded, w_qkv, w_out, own_index, group_size)

time: 79.1 us -> 85 us (1.075)
  local copies, waits for them, and re-layouts: 12.4 us -> 16.1 us
  other arithmetic: 9.67 us -> 12.2 us
    slice x0 -> x1, local copies, waits for them, and re-layouts: none -> 2.04 us  [teacher_branch(): heads[2]]
    dot_general x2 -> x5, matrix products: 5.05 us -> 7 us  [the longest x1 2.24 us: teacher_branch(): jnp.einsum('hdq,hdk->hqk', queries, key_rows, preferred_element_type=jnp....]
    convert_element_type x0 -> x1, other arithmetic: none -> 1.6 us  [teacher_branch(): key_rows = head_norm_cols(heads[1].astype(jnp.float32)).astype(jnp.bfloat16)]
    convert_element_type x1 -> x2, local copies, waits for them, and re-layouts: 2.59 us -> 4.15 us  [the longest x1 2.6 us: teacher_branch(): queries = head_norm_cols(heads[0].astype(jnp.float32)).astype(jnp.bfloat16)]
    reduce_sum x0 -> x2, other arithmetic: none -> 1.43 us  [head_norm_cols(): jnp.mean(values * values, axis=-2, keepdims=True) + EPSILON]
    dot_general x4 -> x3, matrix products: 2.5 us -> 1.52 us  [mix_heads(): jnp.einsum('qhd,khd->hqk', queries, key_rows, preferred_element_type=jnp....]
    dot_general x4 -> x3, matrix products: 2.83 us -> 1.97 us  [mix_heads(): jnp.einsum('hqk,khd->qhd', weights, values, preferred_element_type=jnp.fl...]
    unnamed x71 -> x73, local copies, waits for them, and re-layouts: 2.23 us -> 2.24 us
where the time goes in v15:
time: 85 us; the launch traced here: 84.4 us
  matrix products  39.8 us (47%)
  local copies, waits for them, and re-layouts  16.1 us (19%)
  other arithmetic  12.2 us (14%)
  starting transfers between devices  8.15 us (10%)
  waiting for transfers between devices  4.9 us (6%)
  between operations  3.2 us (4%)
    dot_general x2, matrix products, decoder_output(): return jnp.dot(hidden, dec_out, preferred_element_type=jnp.float32)  8.74 us
    ppermute x6, starting transfers between devices, ring_gather(): parts.append(lax.ppermute(values, 'mask', pairs))  8.15 us
    dot_general x1, matrix products, copy_terms(): branch = attention_from(reuse_rows(visible_in, w_qkv, projected), w_out)  5 us
    ppermute x6, waiting for transfers between devices, ring_gather(): parts.append(lax.ppermute(values, 'mask', pairs))  4.9 us
    dot_general x2, matrix products, decoder_output(): jnp.dot(visible_out, dec_in, preferred_element_type=jnp.float32)  4.57 us
    dot_general x6, matrix products, decoder_output(): jnp.einsum('pgi,gio->pgo', padded[offset:offset + total_rows], conv_w[off...  2.78 us
    convert_element_type x1, local copies, waits for them, and re-layouts, teacher_branch(): queries = head_norm_cols(heads[0].astype(jnp.float32)).astype(jnp.bfloat16)  2.6 us
    reduce_sum x1, other arithmetic, row_norm(): centred = values - average  2.54 us
  transfers between devices with their start and end apart: 6, of which 3 were waited for; matrix products, arithmetic and copies ran while one was open for 7% of the time, Pallas kernels for 0%

profile of v15, /device:TPU:0, one launch (start us, length us, event | category | flops | bytes accessed | tf_op | source)
XLA Modules:
  0.0 84.4 jit_solution(10464275544295322358)
XLA Ops:
  0.6 3.0 %collective-permute-start = (bf16[64,768]{1,0:T(8,128)(2,1)}, bf16[64,768]{1,0:T(8,128)(2,1)S(1)}, u32[]{:S(2)}, u32[]{:S(2)}) collective-permute-start(bf16[64,768]{1,0:T(8,128)(2,1)} %param.9), channel_id=1, source_target_pairs={{0,1},{1,2},{2,3},{3,0},{4,5},{5,6},{6,7},{7,4},{8,9},{9,10},{10,1... | collective-permute-start | bytes 294920 | tf_op jit(solution)/shard_map/ppermute | solution.py:157
  3.7 1.5 %collective-permute-start.1 = (bf16[64,768]{1,0:T(8,128)(2,1)}, bf16[64,768]{1,0:T(8,128)(2,1)S(1)}, u32[]{:S(2)}, u32[]{:S(2)}) collective-permute-start(bf16[64,768]{1,0:T(8,128)(2,1)} %param.9), channel_id=1, source_target_pairs={{0,2},{1,3},{2,0},{3,1},{4,6},{5,7},{6,4},{7,5},{8,10},{9,11},{10,... | collective-permute-start | bytes 294920 | tf_op jit(solution)/shard_map/ppermute | solution.py:157
  5.2 1.4 %collective-permute-start.2 = (bf16[64,768]{1,0:T(8,128)(2,1)}, bf16[64,768]{1,0:T(8,128)(2,1)S(1)}, u32[]{:S(2)}, u32[]{:S(2)}) collective-permute-start(bf16[64,768]{1,0:T(8,128)(2,1)} %param.9), channel_id=1, source_target_pairs={{0,3},{1,0},{2,1},{3,2},{4,7},{5,4},{6,5},{7,6},{8,11},{9,8},{10,9... | collective-permute-start | bytes 294920 | tf_op jit(solution)/shard_map/ppermute | solution.py:157
  8.8 1.2 %gather_fusion = s32[4,51]{1,0:T(4,128)S(1)} fusion(s32[4,51]{1,0:T(4,128)} %param.10, s32[1024]{0:T(1024)S(1)} %pad_clamp_fusion), kind=kCustom, calls=%fused_computation | custom fusion | bytes 1648 | tf_op jit(solution)/shard_map/gather | solution.py:240
  10.7 1.9 %convolution_reduce_fusion = bf16[768]{0:T(1024)(128)(2,1)S(1)} fusion(bf16[1024,1]{0,1:T(2,128)(2,1)S(1)} %reshape.273, bf16[1024,768]{1,0:T(8,128)(2,1)} %param.15), kind=kOutput, calls=%fused_computation.54 | convolution fusion | flops 1572864 | bytes 1576448 | tf_op jit(solution)/shard_map/jvp()/dot_general | solution.py:115
  12.6 1.3 %select_select_fusion.3 = (bf16[64,768]{1,0:T(8,128)(2,1)S(1)}, bf16[64,768]{1,0:T(8,128)(2,1)S(1)}, bf16[64,768]{1,0:T(8,128)(2,1)S(1)}, bf16[64,768]{1,0:T(8,128)(2,1)S(1)}) fusion(bf16[64,768]{1,0:T(8,128)(2,1)S(1)} %collective-permute-done, bf16[64,768]{1,0:T(8,128)(2,1)S(1)} %collective-permute-done.1, bf16[64,768]{1,0:T(8,128)(2,1)S(1)} %collective-permute-done.2, ...), kind=kLoop, calls=%fused_computation.177 | loop fusion | flops 589824 | bytes 786444 | tf_op jit(solution)/shard_map/jit(_where)/select_n | solution.py:168
  13.9 2.2 %convert_reduce_fusion = (f32[256]{0:T(256)S(1)}, bf16[256,1024]{1,0:T(8,128)(2,1)S(1)}) fusion(bf16[768,1024]{1,0:T(8,128)(2,1)} %param.11, bf16[64,768]{1,0:T(8,128)(2,1)S(1)} %get-tuple-element.15, bf16[64,768]{1,0:T(8,128)(2,1)S(1)} %get-tuple-element.16, bf16[64,768]{1,0:T(8,128)(2,1)S(1)} %get-tuple-element.17, bf16[64,768]{1,0:T(8,128)(2,1)S(1)} %get-tuple-element.14), kind=kOutput, calls=%fused_computation.10 | convolution fusion | flops 405012224 | bytes 2491392 | tf_op jit(solution)/shard_map/dot_general | solution.py:203
  17.3 1.9 %convolution_convert_fusion = bf16[256,3072]{1,0:T(8,128)(2,1)S(1)} fusion(bf16[1024,3072]{1,0:T(8,128)(2,1)S(1)} %copy-done.1, bf16[256,1024]{1,0:T(8,128)(2,1)S(1)} %get-tuple-element.23, f32[256]{0:T(256)S(1)} %add_rsqrt_fusion.3, f32[256]{0:T(256)S(1)} %broadcast_multiply_fusion.3), kind=kOutput, calls=%fused_computation.3 | convolution fusion | flops 1612447744 | bytes 8390656 | tf_op jit(solution)/shard_map/sd,dk->ks/dot_general | solution.py:65
  19.2 1.2 %convolution_convert_fusion.1 = bf16[51,3072]{1,0:T(8,128)(2,1)} fusion(bf16[256,3072]{1,0:T(8,128)(2,1)S(1)} %convolution_convert_fusion, s32[51]{0:T(128)S(1)} %dynamic-slice_bitcast_fusion), kind=kOutput, calls=%fused_computation.5 | convolution fusion | flops 80385792 | bytes 1886412 | tf_op jit(solution)/shard_map/vs,ks->vk/dot_general | solution.py:213
  20.4 1.6 %slice_convert_fusion = (f32[1024,256]{0,1:T(8,128)}, f32[1024,256]{0,1:T(8,128)}, bf16[1024,256]{0,1:T(8,128)(2,1)}) fusion(bf16[3072,256]{0,1:T(8,128)(2,1)S(1)} %bitcast.150), kind=kLoop, calls=%fused_computation.109 | loop fusion | flops 524288 | bytes 4194304 | tf_op jit(solution)/shard_map/convert_element_type | solution.py:70
  22.0 1.6 %copy.66 = f32[1024,256]{1,0:T(8,128)S(1)} copy(f32[1024,256]{0,1:T(8,128)} %get-tuple-element.8) | data formatting | bytes 2097152 | tf_op jit(solution)/shard_map/convert_element_type | solution.py:70
  23.7 2.6 %copy.65 = f32[1024,256]{1,0:T(8,128)} copy(f32[1024,256]{0,1:T(8,128)} %get-tuple-element.9) | data formatting | bytes 2097152 | tf_op jit(solution)/shard_map/convert_element_type | solution.py:69
  26.3 1.3 %multiply_reduce_fusion.3 = f32[16,256]{1,0:T(8,128)S(1)} fusion(f32[1024,256]{1,0:T(8,128)} %copy.65), kind=kLoop, calls=%fused_computation.65 | loop fusion | flops 520192 | bytes 1064960 | tf_op jit(solution)/shard_map/reduce_sum | solution.py:86
  27.6 2.0 %copy.64 = bf16[1024,256]{1,0:T(8,128)(2,1)} copy(bf16[1024,256]{0,1:T(8,128)(2,1)} %get-tuple-element.10) | data formatting | bytes 1048576 | tf_op jit(solution)/shard_map/slice | solution.py:79
  29.7 2.2 %fusion = (f32[16,256]{1,0:T(8,128)S(1)}, f32[16,256,256]{1,2,0:T(8,128)S(1)}) fusion(f32[16,64,256]{2,1,0:T(8,128)S(1)} %bitcast.147, f32[16,256]{1,0:T(8,128)S(1)} %get-tuple-element.47, f32[16,64,256]{2,1,0:T(8,128)} %bitcast.148, f32[16,256]{1,0:T(8,128)S(1)} %get-tuple-element.48), kind=kOutput, calls=%fused_computation.4 | convolution fusion | flops 137359360 | bytes 6340608 | tf_op jit(solution)/shard_map/hdq,hdk->hqk/dot_general | solution.py:73
  37.9 2.3 %convolution_convert_fusion.18 = bf16[51,768]{1,0:T(8,128)(2,1)S(1)} fusion(bf16[1024,768]{1,0:T(8,128)(2,1)} %param.15, f32[51,1024]{1,0:T(8,128)S(1)} %get-tuple-element.35, bf16[51,1024]{1,0:T(8,128)(2,1)S(1)} %reshape.252, bf16[1024,1024]{1,0:T(8,128)(2,1)S(1)} %copy-done), kind=kOutput, calls=%fused_computation.52 | convolution fusion | flops 187314432 | bytes 4061696 | tf_op jit(solution)/shard_map/jvp()/dot_general | solution.py:112
  40.2 1.1 %fusion.4 = bf16[256,768]{1,0:T(8,128)(2,1)} fusion(bf16[51,768]{1,0:T(8,128)(2,1)S(1)} %convolution_convert_fusion.18, bf16[768]{0:T(1024)(128)(2,1)S(1)} %convolution_reduce_fusion, pred[256]{0:T(512)(128)(4,1)S(1)} %broadcast_compare_fusion, s32[51]{0:T(128)S(1)} %dynamic-slice_bitcast_fusion), kind=kOutput, calls=%fused_computation.16 | convolution fusion | flops 20263680 | bytes 473548 | tf_op jit(solution)/shard_map/jvp()/dot_general | solution.py:118
  41.3 1.2 %copy.59 = bf16[256,768]{0,1:T(8,128)(2,1)S(1)} copy(bf16[256,768]{1,0:T(8,128)(2,1)} %fusion.4) | data formatting | bytes 786432 | tf_op jit(solution)/shard_map/jvp()/convert_element_type | solution.py:119
  43.2 1.4 %fusion.130 = (f32[256]{0:T(256)S(1)}, f32[16,256,48]{1,2,0:T(8,128)S(1)}) fusion(f32[16,256,48]{1,2,0:T(8,128)S(1)} %convolution_add_fusion.1, bf16[256,16,48]{0,2,1:T(8,128)(2,1)S(1)} %bitcast.156, bf16[3,16,48,48]{3,2,1,0:T(8,128)(2,1)} %param.16), kind=kOutput, calls=%fused_computation.234 | convolution fusion | flops 19267328 | bytes 2163712 | tf_op jit(solution)/shard_map/jvp(pgi,gio->pgo)/dot_general | solution.py:124
  45.3 1.1 %copy.63 = f32[256,768]{1,0:T(8,128)} copy(f32[256,768]{0,1:T(8,128)S(1)} %bitcast.149) | data formatting | bytes 1572864 | tf_op jit(solution)/shard_map/jvp()/reshape | solution.py:130
  46.5 5.4 %multiply_reduce_fusion = (f32[]{:T(128)}, f32[256,1024]{1,0:T(8,128)S(1)}) fusion(f32[256]{0:T(256)} %get-tuple-element.19, f32[256]{0:T(256)} %add_rsqrt_fusion.2, f32[256,1024]{1,0:T(8,128)} %copy-done.2, f32[256]{0:T(256)} %copy-done.29, bf16[768,1024]{1,0:T(8,128)(2,1)} %param.17, bf16[256,768]{1,0:T(8,128)(2,1)S(1)} %copy-done.25, ...), kind=kOutput, calls=%fused_computation.59 | convolution fusion | flops 418709504 | bytes 4854788 | tf_op jit(solution)/shard_map/jvp()/dot_general | solution.py:132
  51.9 3.3 %multiply_reduce_fusion.4 = (f32[256]{0:T(256)S(1)}, bf16[256,768]{1,0:T(8,128)(2,1)S(1)}) fusion(f32[256,768]{1,0:T(8,128)S(1)} %copy-done.3, f32[256]{0:T(256)S(1)} %broadcast_multiply_fusion.1, f32[256]{0:T(256)S(1)} %copy-done.28, bf16[768,1024]{1,0:T(8,128)(2,1)S(1)} %copy-done.35, f32[256,1024]{1,0:T(8,128)S(1)} %get-tuple-element.44, ...), kind=kOutput, calls=%fused_computation.88 | convolution fusion | flops 419495680 | bytes 3805184 | tf_op jit(solution)/shard_map/transpose(jvp())/dot_general | solution.py:132
  55.3 2.5 %fusion.126 = (f32[256]{0:T(256)S(1)}, f32[256,768]{1,0:T(8,128)S(1)}) fusion(f32[256]{0:T(256)S(1)} %multiply_multiply_fusion.8, bf16[256,768]{1,0:T(8,128)(2,1)S(1)} %get-tuple-element.33, f32[256]{0:T(256)S(1)} %copy-done.28, f32[256,768]{1,0:T(8,128)S(1)} %copy-done.3, f32[256]{0:T(256)S(1)} %broadcast_multiply_fusion.1), kind=kLoop, calls=%fused_computation.230 | loop fusion | flops 15531776 | bytes 1970176 | tf_op jit(solution)/shard_map/transpose(jvp())/reduce_sum | solution.py:19
  58.7 1.2 %copy.68 = bf16[256,768]{0,1:T(8,128)(2,1)S(1)} copy(bf16[256,768]{1,0:T(8,128)(2,1)} %broadcast_add_fusion) | data formatting | bytes 786432 | tf_op jit(solution)/shard_map/transpose(jvp())/add_any | solution.py:18
  61.2 2.3 %convolution_convert_fusion.13 = bf16[51,1024]{1,0:T(8,128)(2,1)S(1)} fusion(bf16[1024,768]{1,0:T(8,128)(2,1)} %param.15, bf16[256,768]{1,0:T(8,128)(2,1)} %copy-done.10, bf16[256,768]{1,0:T(8,128)(2,1)S(1)} %copy.72, pred[256]{0:T(512)(128)(4,1)S(1)} %copy-done.33, s32[51]{0:T(128)S(1)} %copy-done.27), kind=kOutput, calls=%fused_computation.45 | convolution fusion | flops 100964352 | bytes 2464204 | tf_op jit(solution)/shard_map/transpose(jvp())/dot_general | solution.py:112
  64.5 1.4 %fusion.17 = bf16[51,1,16,64]{3,0,2,1:T(8,128)(2,1)S(1)} fusion(bf16[51,16,64]{2,1,0:T(8,128)(2,1)S(1)} %reshape.258, f32[16,51,51]{1,2,0:T(8,128)} %copy-done.15, f32[16,51]{1,0:T(8,128)S(1)} %get-tuple-element.28), kind=kOutput, calls=%fused_computation.41 | convolution fusion | flops 5462304 | bytes 378624 | tf_op jit(solution)/shard_map/transpose(jvp(hqk,khd->qhd))/dot_general | solution.py:36
  68.7 5.0 %multiply_reduce_fusion.7 = (f32[51]{0:T(128)S(1)}, f32[51]{0:T(128)S(1)}, f32[51,1024]{1,0:T(8,128)S(1)}) fusion(f32[51,1024]{1,0:T(8,128)S(1)} %get-tuple-element.35, f32[51]{0:T(128)S(1)} %broadcast_multiply_fusion.4, bf16[51,3072]{1,0:T(8,128)(2,1)S(1)} %reshape.259, bf16[1024,3072]{1,0:T(8,128)(2,1)} %param.12), kind=kOutput, calls=%fused_computation.155 | convolution fusion | flops 321229696 | bytes 7023204 | tf_op jit(solution)/shard_map/transpose(jvp(transpose(jvp())))/dot_general | solution.py:142
  74.6 1.5 %collective-permute-start.4 = (bf16[51,1024]{1,0:T(8,128)(2,1)S(1)}, bf16[51,1024]{1,0:T(8,128)(2,1)S(1)}, u32[]{:S(2)}, u32[]{:S(2)}) collective-permute-start(bf16[51,1024]{1,0:T(8,128)(2,1)S(1)} %fusion.100), channel_id=1, source_target_pairs={{0,2},{1,3},{2,0},{3,1},{4,6},{5,7},{6,4},{7,5},{8,10},{9,11},{10,... | collective-permute-start | bytes 313352 | tf_op jit(solution)/shard_map/ppermute | solution.py:157
  76.9 2.6 %collective-permute-done.3 = bf16[51,1024]{1,0:T(8,128)(2,1)S(1)} collective-permute-done((bf16[51,1024]{1,0:T(8,128)(2,1)S(1)}, bf16[51,1024]{1,0:T(8,128)(2,1)S(1)}, u32[]{:S(2)}, u32[]{:S(2)}) %collective-permute-start.3) | collective-permute-done | bytes 104480 | tf_op jit(solution)/shard_map/ppermute | solution.py:157
  79.6 1.0 %collective-permute-done.4 = bf16[51,1024]{1,0:T(8,128)(2,1)S(1)} collective-permute-done((bf16[51,1024]{1,0:T(8,128)(2,1)S(1)}, bf16[51,1024]{1,0:T(8,128)(2,1)S(1)}, u32[]{:S(2)}, u32[]{:S(2)}) %collective-permute-start.4) | collective-permute-done | bytes 104480 | tf_op jit(solution)/shard_map/ppermute | solution.py:157
  80.6 1.2 %collective-permute-done.5 = bf16[51,1024]{1,0:T(8,128)(2,1)S(1)} collective-permute-done((bf16[51,1024]{1,0:T(8,128)(2,1)S(1)}, bf16[51,1024]{1,0:T(8,128)(2,1)S(1)}, u32[]{:S(2)}, u32[]{:S(2)}) %collective-permute-start.5) | collective-permute-done | bytes 104480 | tf_op jit(solution)/shard_map/ppermute | solution.py:157
  81.8 1.4 %fusion.21 = f32[192,1024]{1,0:T(8,128)} fusion(bf16[51,1024]{1,0:T(8,128)(2,1)S(1)} %collective-permute-done.5, bf16[51,1024]{1,0:T(8,128)(2,1)S(1)} %collective-permute-done.4, bf16[51,1024]{1,0:T(8,128)(2,1)S(1)} %collective-permute-done.3, bf16[51,1024]{1,0:T(8,128)(2,1)S(1)} %fusion.100, bf16[256,768]{1,0:T(8,128)(2,1)S(1)} %pad_maximum_fusion, ...), kind=kOutput, calls=%fused_computation.53 | convolution fusion | flops 102032640 | bytes 1377284 | tf_op jit(solution)/shard_map/vc,vd->cd/dot_general | solution.py:246
  (139 shorter events, 18.2 us)
Async XLA Ops:
  0.6 32.2 %copy-start = (bf16[1024,1024]{1,0:T(8,128)(2,1)S(1)}, bf16[1024,1024]{1,0:T(8,128)(2,1)}, u32[]{:S(2)}) copy-start(bf16[1024,1024]{1,0:T(8,128)(2,1)} %param.13) | copy-start | bytes 6291460
  0.6 11.9 %collective-permute-start = (bf16[64,768]{1,0:T(8,128)(2,1)}, bf16[64,768]{1,0:T(8,128)(2,1)S(1)}, u32[]{:S(2)}, u32[]{:S(2)}) collective-permute-start(bf16[64,768]{1,0:T(8,128)(2,1)} %param.9), channel_id=1, source_target_pairs={{0,1},{1,2},{2,3},{3,0},{4,5},{5,6},{6,7},{7,4},{8,9},{9,10},{10,1... | collective-permute-start | bytes 294920 | tf_op jit(solution)/shard_map/ppermute | solution.py:157
  3.7 8.9 %collective-permute-start.1 = (bf16[64,768]{1,0:T(8,128)(2,1)}, bf16[64,768]{1,0:T(8,128)(2,1)S(1)}, u32[]{:S(2)}, u32[]{:S(2)}) collective-permute-start(bf16[64,768]{1,0:T(8,128)(2,1)} %param.9), channel_id=1, source_target_pairs={{0,2},{1,3},{2,0},{3,1},{4,6},{5,7},{6,4},{7,5},{8,10},{9,11},{10,... | collective-permute-start | bytes 294920 | tf_op jit(solution)/shard_map/ppermute | solution.py:157
  5.2 7.4 %collective-permute-start.2 = (bf16[64,768]{1,0:T(8,128)(2,1)}, bf16[64,768]{1,0:T(8,128)(2,1)S(1)}, u32[]{:S(2)}, u32[]{:S(2)}) collective-permute-start(bf16[64,768]{1,0:T(8,128)(2,1)} %param.9), channel_id=1, source_target_pairs={{0,3},{1,0},{2,1},{3,2},{4,7},{5,4},{6,5},{7,6},{8,11},{9,8},{10,9... | collective-permute-start | bytes 294920 | tf_op jit(solution)/shard_map/ppermute | solution.py:157
  7.3 32.9 %copy-start.26 = (s32[51]{0:T(128)}, s32[51]{0:T(128)S(1)}, u32[]{:S(2)}) copy-start(s32[51]{0:T(128)S(1)} %dynamic-slice_bitcast_fusion) | copy-start | bytes 616
  7.5 32.7 %copy-start.32 = (pred[256]{0:T(512)(128)(4,1)}, pred[256]{0:T(512)(128)(4,1)S(1)}, u32[]{:S(2)}) copy-start(pred[256]{0:T(512)(128)(4,1)S(1)} %broadcast_compare_fusion) | copy-start | bytes 772
  10.7 6.6 %copy-start.1 = (bf16[1024,3072]{1,0:T(8,128)(2,1)S(1)}, bf16[1024,3072]{1,0:T(8,128)(2,1)}, u32[]{:S(2)}) copy-start(bf16[1024,3072]{1,0:T(8,128)(2,1)} %param.12) | copy-start | bytes 18874372
  13.9 3.1 %copy-start.17 = (bf16[64,768]{1,0:T(8,128)(2,1)}, bf16[64,768]{1,0:T(8,128)(2,1)S(1)}, u32[]{:S(2)}) copy-start(bf16[64,768]{1,0:T(8,128)(2,1)S(1)} %get-tuple-element.14) | copy-start | bytes 294916
  13.9 3.1 %copy-start.19 = (bf16[64,768]{1,0:T(8,128)(2,1)}, bf16[64,768]{1,0:T(8,128)(2,1)S(1)}, u32[]{:S(2)}) copy-start(bf16[64,768]{1,0:T(8,128)(2,1)S(1)} %get-tuple-element.15) | copy-start | bytes 294916
  13.9 3.1 %copy-start.21 = (bf16[64,768]{1,0:T(8,128)(2,1)}, bf16[64,768]{1,0:T(8,128)(2,1)S(1)}, u32[]{:S(2)}) copy-start(bf16[64,768]{1,0:T(8,128)(2,1)S(1)} %get-tuple-element.16) | copy-start | bytes 294916
  13.9 3.1 %copy-start.23 = (bf16[64,768]{1,0:T(8,128)(2,1)}, bf16[64,768]{1,0:T(8,128)(2,1)S(1)}, u32[]{:S(2)}) copy-start(bf16[64,768]{1,0:T(8,128)(2,1)S(1)} %get-tuple-element.17) | copy-start | bytes 294916
  29.7 2.3 %copy-start.14 = (bf16[1024,256]{1,0:T(8,128)(2,1)S(1)}, bf16[1024,256]{1,0:T(8,128)(2,1)}, u32[]{:S(2)}) copy-start(bf16[1024,256]{1,0:T(8,128)(2,1)} %copy.64) | copy-start | bytes 1572868
  32.8 2.6 %copy-start.11 = (bf16[51,3072]{1,0:T(8,128)(2,1)S(1)}, bf16[51,3072]{1,0:T(8,128)(2,1)}, u32[]{:S(2)}) copy-start(bf16[51,3072]{1,0:T(8,128)(2,1)} %convolution_convert_fusion.1) | copy-start | bytes 940036
  33.6 2.3 %copy-start.29 = (f32[256]{0:T(256)}, f32[256]{0:T(256)S(1)}, u32[]{:S(2)}) copy-start(f32[256]{0:T(256)S(1)} %broadcast_multiply_fusion.2) | copy-start | bytes 3076
  36.0 1.9 %copy-start.6 = (bf16[51,1,16,64]{3,2,1,0:T(8,128)(2,1)}, bf16[51,1,16,64]{3,2,1,0:T(8,128)(2,1)S(1)}, u32[]{:S(2)}) copy-start(bf16[51,1,16,64]{3,2,1,0:T(8,128)(2,1)S(1)} %get-tuple-element.11) | copy-start | bytes 313348
  36.0 1.9 %copy-start.8 = (bf16[51,1,16,64]{3,2,1,0:T(8,128)(2,1)}, bf16[51,1,16,64]{3,2,1,0:T(8,128)(2,1)S(1)}, u32[]{:S(2)}) copy-start(bf16[51,1,16,64]{3,2,1,0:T(8,128)(2,1)S(1)} %get-tuple-element.13) | copy-start | bytes 313348
  37.9 4.6 %copy-start.4 = (bf16[3,16,48,48]{3,2,1,0:T(8,128)(2,1)S(1)}, bf16[3,16,48,48]{3,2,1,0:T(8,128)(2,1)}, u32[]{:S(2)}) copy-start(bf16[3,16,48,48]{3,2,1,0:T(8,128)(2,1)} %param.16) | copy-start | bytes 663556
  46.5 5.4 %copy-start.3 = (f32[256,768]{1,0:T(8,128)S(1)}, f32[256,768]{1,0:T(8,128)}, u32[]{:S(2)}) copy-start(f32[256,768]{1,0:T(8,128)} %copy.63) | copy-start | bytes 2359300
  46.5 5.4 %copy-start.28 = (f32[256]{0:T(256)S(1)}, f32[256]{0:T(256)}, u32[]{:S(2)}) copy-start(f32[256]{0:T(256)} %fusion.112) | copy-start | bytes 3076
  46.5 5.4 %copy-start.31 = (f32[256]{0:T(256)S(1)}, f32[256]{0:T(256)}, u32[]{:S(2)}) copy-start(f32[256]{0:T(256)} %get-tuple-element.18) | copy-start | bytes 3076
  46.5 5.4 %copy-start.35 = (bf16[768,1024]{1,0:T(8,128)(2,1)S(1)}, bf16[768,1024]{1,0:T(8,128)(2,1)}, u32[]{:S(2)}) copy-start(bf16[768,1024]{1,0:T(8,128)(2,1)} %param.17) | copy-start | bytes 4718596
  55.3 2.6 %copy-start.10 = (bf16[256,768]{1,0:T(8,128)(2,1)}, bf16[256,768]{1,0:T(8,128)(2,1)S(1)}, u32[]{:S(2)}) copy-start(bf16[256,768]{1,0:T(8,128)(2,1)S(1)} %get-tuple-element.33) | copy-start | bytes 1179652
  55.3 4.6 %copy-start.5 = (bf16[3,16,48,48]{3,2,1,0:T(8,128)(2,1)S(1)}, bf16[3,16,48,48]{3,2,1,0:T(8,128)(2,1)}, u32[]{:S(2)}) copy-start(bf16[3,16,48,48]{3,2,1,0:T(8,128)(2,1)} %param.16) | copy-start | bytes 663556
  63.5 2.3 %copy-start.13 = (bf16[51,1,16,64]{3,2,1,0:T(8,128)(2,1)S(1)}, bf16[51,1,16,64]{3,2,1,0:T(8,128)(2,1)}, u32[]{:S(2)}) copy-start(bf16[51,1,16,64]{3,2,1,0:T(8,128)(2,1)} %copy-done.12) | copy-start | bytes 313348
  68.6 8.2 %copy-start.18 = (bf16[64,768]{1,0:T(8,128)(2,1)S(1)}, bf16[64,768]{1,0:T(8,128)(2,1)}, u32[]{:S(2)}) copy-start(bf16[64,768]{1,0:T(8,128)(2,1)} %copy-done.17) | copy-start | bytes 294916
  68.6 8.2 %copy-start.20 = (bf16[64,768]{1,0:T(8,128)(2,1)S(1)}, bf16[64,768]{1,0:T(8,128)(2,1)}, u32[]{:S(2)}) copy-start(bf16[64,768]{1,0:T(8,128)(2,1)} %copy-done.19) | copy-start | bytes 294916
  68.7 8.2 %copy-start.22 = (bf16[64,768]{1,0:T(8,128)(2,1)S(1)}, bf16[64,768]{1,0:T(8,128)(2,1)}, u32[]{:S(2)}) copy-start(bf16[64,768]{1,0:T(8,128)(2,1)} %copy-done.21) | copy-start | bytes 294916
  68.7 8.2 %copy-start.24 = (bf16[64,768]{1,0:T(8,128)(2,1)S(1)}, bf16[64,768]{1,0:T(8,128)(2,1)}, u32[]{:S(2)}) copy-start(bf16[64,768]{1,0:T(8,128)(2,1)} %copy-done.23) | copy-start | bytes 294916
  68.7 13.2 %copy-start.30 = (s32[204]{0:T(256)S(1)}, s32[204]{0:T(256)}, u32[]{:S(2)}) copy-start(s32[204]{0:T(256)} %eq.93) | copy-start | bytes 2452
  74.1 5.5 %collective-permute-start.3 = (bf16[51,1024]{1,0:T(8,128)(2,1)S(1)}, bf16[51,1024]{1,0:T(8,128)(2,1)S(1)}, u32[]{:S(2)}, u32[]{:S(2)}) collective-permute-start(bf16[51,1024]{1,0:T(8,128)(2,1)S(1)} %fusion.100), channel_id=1, source_target_pairs={{0,3},{1,0},{2,1},{3,2},{4,7},{5,4},{6,5},{7,6},{8,11},{9,8},{10,9... | collective-permute-start | bytes 313352 | tf_op jit(solution)/shard_map/ppermute | solution.py:157
  74.6 6.0 %collective-permute-start.4 = (bf16[51,1024]{1,0:T(8,128)(2,1)S(1)}, bf16[51,1024]{1,0:T(8,128)(2,1)S(1)}, u32[]{:S(2)}, u32[]{:S(2)}) collective-permute-start(bf16[51,1024]{1,0:T(8,128)(2,1)S(1)} %fusion.100), channel_id=1, source_target_pairs={{0,2},{1,3},{2,0},{3,1},{4,6},{5,7},{6,4},{7,5},{8,10},{9,11},{10,... | collective-permute-start | bytes 313352 | tf_op jit(solution)/shard_map/ppermute | solution.py:157
  76.1 5.7 %collective-permute-start.5 = (bf16[51,1024]{1,0:T(8,128)(2,1)S(1)}, bf16[51,1024]{1,0:T(8,128)(2,1)S(1)}, u32[]{:S(2)}, u32[]{:S(2)}) collective-permute-start(bf16[51,1024]{1,0:T(8,128)(2,1)S(1)} %fusion.100), channel_id=1, source_target_pairs={{0,1},{1,2},{2,3},{3,0},{4,5},{5,6},{6,7},{7,4},{8,9},{9,10},{10,1... | collective-permute-start | bytes 313352 | tf_op jit(solution)/shard_map/ppermute | solution.py:157
  (10 other events, 13.0 us)

commit v16 on v11

--- a/solution.py
+++ b/solution.py
@@ -1,8 +1,10 @@
+import functools
 import math
 
 import jax
 import jax.numpy as jnp
 from jax import lax
+from jax.experimental import pallas as pl
 from jax.sharding import PartitionSpec as P
 
 D = 1024
@@ -100,12 +102,70 @@
             preferred_element_type=jnp.float32,
         )
     activated = jax.nn.gelu(row_norm(convolved.reshape(total_rows, DD)), approximate=False)
-    hidden = (lowered.astype(jnp.float32) + activated).astype(jnp.bfloat16)
-    return jnp.dot(hidden, dec_out, preferred_element_type=jnp.float32)
+    return (lowered.astype(jnp.float32) + activated).astype(jnp.bfloat16)
+
+
+def loss_kernel(hidden_ref, dec_out_ref, targets_ref, keep_ref, squares_ref, d_hidden_ref, *, scale):
+    predicted = jnp.dot(hidden_ref[...], dec_out_ref[...], preferred_element_type=jnp.float32)
+    mismatch = (predicted - targets_ref[...].astype(jnp.float32)) * keep_ref[...]
+    squares_ref[...] = jnp.sum(mismatch * mismatch, keepdims=True)
+    d_predicted = (2.0 * scale * mismatch) * keep_ref[...]
+    d_hidden = lax.dot_general(
+        d_predicted.astype(jnp.bfloat16),
+        dec_out_ref[...],
+        (((1,), (1,)), ((), ())),
+        preferred_element_type=jnp.float32,
+    )
+    d_hidden_ref[...] = d_hidden.astype(jnp.bfloat16)
+
+
+def masked_squares(hidden, dec_out, targets, keep, scale):
+    rows, width = hidden.shape
+    return pl.pallas_call(
+        functools.partial(loss_kernel, scale=scale),
+        out_shape=(
+            jax.ShapeDtypeStruct((1, 1), jnp.float32),
+            jax.ShapeDtypeStruct((rows, width), jnp.bfloat16),
+        ),
+    )(hidden, dec_out, targets, keep)
+
+
+@functools.partial(jax.custom_vjp, nondiff_argnums=(4,))
+def squares_of(hidden, dec_out, targets, keep, scale):
+    return masked_squares(hidden, dec_out, targets, keep, scale)[0][0, 0]
+
+
+def squares_of_fwd(hidden, dec_out, targets, keep, scale):
+    squares, d_hidden = masked_squares(hidden, dec_out, targets, keep, scale)
+    return squares[0, 0], (d_hidden, dec_out, targets, keep)
+
+
+def squares_of_bwd(scale, saved, cotangent):
+    d_hidden, dec_out, targets, keep = saved
+    ratio = (cotangent / scale).astype(jnp.bfloat16)
+    return (
+        d_hidden * ratio,
+        jnp.zeros_like(dec_out),
+        jnp.zeros_like(targets),
+        jnp.zeros_like(keep),
+    )
+
+
+squares_of.defvjp(squares_of_fwd, squares_of_bwd)
 
 
 def copy_terms(
-    visible_in, positions, targets, w_qkv, w_out, mask_embed, dec_in, conv_w, dec_out, projected
+    visible_in,
+    positions,
+    targets,
+    w_qkv,
+    w_out,
+    mask_embed,
+    dec_in,
+    conv_w,
+    dec_out,
+    projected,
+    scale,
 ):
     total_rows = targets.shape[0]
     if projected is None:
@@ -113,13 +173,12 @@
     else:
         branch = attention_from(reuse_rows(visible_in, w_qkv, projected), w_out)
     visible_out = (visible_in.astype(jnp.float32) + branch).astype(jnp.bfloat16)
-    predicted = decoder_output(
+    hidden = decoder_output(
         visible_out, positions, total_rows, mask_embed, dec_in, conv_w, dec_out
     )
     slot_ids = jnp.arange(total_rows, dtype=jnp.int32)
     seen = jnp.max((slot_ids[:, None] == positions[None, :]).astype(jnp.float32), axis=1)
-    mismatch = (predicted - targets.astype(jnp.float32)) * (1.0 - seen)[:, None]
-    return jnp.sum(mismatch * mismatch)
+    return squares_of(hidden, dec_out, targets, (1.0 - seen)[:, None], scale)
 
 
 def ring_gather(values, group_size):
@@ -203,10 +262,11 @@
             conv_w,
             dec_out,
             visible_projected,
+            factor,
         )
 
+    factor = 0.5 / math.sqrt(copies * visible_count)
     squares, pullback = jax.vjp(objective, visible_in)
-    factor = 0.5 / math.sqrt(copies * visible_count)
     (grad_in,) = pullback(jnp.ones_like(squares) * factor)
     copy_loss = jnp.reshape(squares / ((total_rows - visible_count) * D), (1,))
     slot_copy = (own_index + jnp.arange(group_size, dtype=jnp.int32)) % group_size

time: 79.1 us -> 78.8 us (level)
  matrix products: 40.3 us -> 35.7 us
  Pallas kernels: 0 us -> 3.54 us
  other arithmetic: 9.67 us -> 11.2 us
  local copies, waits for them, and re-layouts: 12.4 us -> 11.5 us
    dot_general x2 -> x0, matrix products: 8.57 us -> none  [decoder_output(): return jnp.dot(hidden, dec_out, preferred_element_type=jnp.float32)]
    dot_general x6, matrix products: 2.76 us -> 7.63 us  [decoder_output(): jnp.einsum('pgi,gio->pgo', padded[offset:offset + total_rows], conv_w[off...]
    convert_element_type x0 -> x2, other arithmetic: none -> 3.94 us  [the longest x1 2.97 us: decoder_output(): return (lowered.astype(jnp.float32) + activated).astype(jnp.bfloat16)]
    pallas_call x0 -> x1, Pallas kernels: none -> 3.54 us  [masked_squares(): pl.pallas_call(functools.partial(loss_kernel, scale=scale), out_shape=(ja...]
    reduce_sum x1, other arithmetic: 2.76 us -> 0.74 us  [row_norm(): centred = values - average]
    reduce_sum x0 -> x1, other arithmetic: none -> 2 us  [row_norm(): return centred * lax.rsqrt(spread + EPSILON)]
    rsqrt x3, other arithmetic: 1.14 us -> 0.02 us  [row_norm(): return centred * lax.rsqrt(spread + EPSILON)]
    add_any x1, local copies, waits for them, and re-layouts: 1.16 us -> 0.17 us  [row_norm(): average = jnp.mean(values, axis=-1, keepdims=True)]
  transfers between devices with their start and end apart: 6 -> 6, of which waited for: 3 -> 3; matrix products, arithmetic and copies ran while one was open for 7% -> 8% of each run, Pallas kernels for 0% -> 0%
where the time goes in v16:
time: 78.8 us; the launch traced here: 78.2 us
  matrix products  35.7 us (45%)
  local copies, waits for them, and re-layouts  11.5 us (15%)
  other arithmetic  11.2 us (14%)
  starting transfers between devices  8.15 us (10%)
  waiting for transfers between devices  4.87 us (6%)
  Pallas kernels  3.54 us (4%)
  between operations  3.17 us (4%)
    ppermute x6, starting transfers between devices, ring_gather(): parts.append(lax.ppermute(values, 'mask', pairs))  8.15 us
    dot_general x6, matrix products, decoder_output(): jnp.einsum('pgi,gio->pgo', padded[offset:offset + total_rows], conv_w[off...  7.63 us
    dot_general x1, matrix products, copy_terms(): branch = attention_from(reuse_rows(visible_in, w_qkv, projected), w_out)  5 us
    ppermute x6, waiting for transfers between devices, ring_gather(): parts.append(lax.ppermute(values, 'mask', pairs))  4.87 us
    dot_general x2, matrix products, decoder_output(): jnp.dot(visible_out, dec_in, preferred_element_type=jnp.float32)  4.38 us
    pallas_call x1, Pallas kernels, masked_squares(): pl.pallas_call(functools.partial(loss_kernel, scale=scale), out_shape=(ja...  3.54 us
    dot_general x1, matrix products, project_rows(): jnp.dot(normed, w_qkv, preferred_element_type=jnp.float32)  3.1 us
    convert_element_type x1, other arithmetic, decoder_output(): return (lowered.astype(jnp.float32) + activated).astype(jnp.bfloat16)  2.97 us
  transfers between devices with their start and end apart: 6, of which 3 were waited for; matrix products, arithmetic and copies ran while one was open for 8% of the time, Pallas kernels for 0%

profile of v16, /device:TPU:0, one launch (start us, length us, event | category | flops | bytes accessed | tf_op | source)
XLA Modules:
  0.0 78.2 jit_solution(3988352777425396628)
XLA Ops:
  0.6 3.0 %collective-permute-start = (bf16[64,768]{1,0:T(8,128)(2,1)}, bf16[64,768]{1,0:T(8,128)(2,1)S(1)}, u32[]{:S(2)}, u32[]{:S(2)}) collective-permute-start(bf16[64,768]{1,0:T(8,128)(2,1)} %param.9), channel_id=1, source_target_pairs={{0,1},{1,2},{2,3},{3,0},{4,5},{5,6},{6,7},{7,4},{8,9},{9,10},{10,1... | collective-permute-start | bytes 294920 | tf_op jit(solution)/shard_map/ppermute | solution.py:188
  3.7 1.5 %collective-permute-start.1 = (bf16[64,768]{1,0:T(8,128)(2,1)}, bf16[64,768]{1,0:T(8,128)(2,1)S(1)}, u32[]{:S(2)}, u32[]{:S(2)}) collective-permute-start(bf16[64,768]{1,0:T(8,128)(2,1)} %param.9), channel_id=1, source_target_pairs={{0,2},{1,3},{2,0},{3,1},{4,6},{5,7},{6,4},{7,5},{8,10},{9,11},{10,... | collective-permute-start | bytes 294920 | tf_op jit(solution)/shard_map/ppermute | solution.py:188
  5.2 1.4 %collective-permute-start.2 = (bf16[64,768]{1,0:T(8,128)(2,1)}, bf16[64,768]{1,0:T(8,128)(2,1)S(1)}, u32[]{:S(2)}, u32[]{:S(2)}) collective-permute-start(bf16[64,768]{1,0:T(8,128)(2,1)} %param.9), channel_id=1, source_target_pairs={{0,3},{1,0},{2,1},{3,2},{4,7},{5,4},{6,5},{7,6},{8,11},{9,8},{10,9... | collective-permute-start | bytes 294920 | tf_op jit(solution)/shard_map/ppermute | solution.py:188
  9.0 1.2 %gather_fusion = s32[4,51]{1,0:T(4,128)S(1)} fusion(s32[4,51]{1,0:T(4,128)} %param.10, s32[1024]{0:T(1024)S(1)} %pad_clamp_fusion), kind=kCustom, calls=%fused_computation | custom fusion | bytes 1648 | tf_op jit(solution)/shard_map/gather | solution.py:273
  10.9 1.9 %convolution_reduce_fusion = bf16[768]{0:T(1024)(128)(2,1)S(1)} fusion(bf16[1024,1]{0,1:T(2,128)(2,1)S(1)} %reshape.279, bf16[1024,768]{1,0:T(8,128)(2,1)} %param.15), kind=kOutput, calls=%fused_computation.55 | convolution fusion | flops 1572864 | bytes 1576448 | tf_op jit(solution)/shard_map/jvp()/dot_general | solution.py:89
  12.9 1.3 %select_select_fusion.3 = (bf16[64,768]{1,0:T(8,128)(2,1)S(1)}, bf16[64,768]{1,0:T(8,128)(2,1)S(1)}, bf16[64,768]{1,0:T(8,128)(2,1)S(1)}, bf16[64,768]{1,0:T(8,128)(2,1)S(1)}) fusion(bf16[64,768]{1,0:T(8,128)(2,1)S(1)} %collective-permute-done, bf16[64,768]{1,0:T(8,128)(2,1)S(1)} %collective-permute-done.1, bf16[64,768]{1,0:T(8,128)(2,1)S(1)} %collective-permute-done.2, ...), kind=kLoop, calls=%fused_computation.172 | loop fusion | flops 589824 | bytes 786444 | tf_op jit(solution)/shard_map/jit(_where)/select_n | solution.py:199
  14.2 2.2 %convert_reduce_fusion = (f32[256]{0:T(256)S(1)}, bf16[256,1024]{1,0:T(8,128)(2,1)S(1)}) fusion(bf16[768,1024]{1,0:T(8,128)(2,1)} %param.11, bf16[64,768]{1,0:T(8,128)(2,1)S(1)} %get-tuple-element.20, bf16[64,768]{1,0:T(8,128)(2,1)S(1)} %get-tuple-element.21, bf16[64,768]{1,0:T(8,128)(2,1)S(1)} %get-tuple-element.22, bf16[64,768]{1,0:T(8,128)(2,1)S(1)} %get-tuple-element.19), kind=kOutput, calls=%fused_computation.12 | convolution fusion | flops 405012224 | bytes 2491392 | tf_op jit(solution)/shard_map/dot_general | solution.py:234
  16.8 3.1 %convolution_convert_fusion = bf16[256,3072]{1,0:T(8,128)(2,1)} fusion(bf16[1024,3072]{1,0:T(8,128)(2,1)S(1)} %copy-done.4, bf16[256,1024]{1,0:T(8,128)(2,1)S(1)} %get-tuple-element.26, f32[256]{0:T(256)S(1)} %add_rsqrt_fusion.3, f32[256]{0:T(256)S(1)} %broadcast_multiply_fusion.2), kind=kOutput, calls=%fused_computation.3 | convolution fusion | flops 1612447744 | bytes 8390656 | tf_op jit(solution)/shard_map/dot_general | solution.py:50
  19.8 2.6 %copy.63 = bf16[256,3072]{0,1:T(8,128)(2,1)} copy(bf16[256,3072]{1,0:T(8,128)(2,1)} %convolution_convert_fusion) | data formatting | bytes 3145728 | tf_op jit(solution)/shard_map/convert_element_type | solution.py:50
  22.4 1.9 %convolution_convert_fusion.1 = bf16[51,3072]{1,0:T(8,128)(2,1)S(1)} fusion(bf16[256,3072]{1,0:T(8,128)(2,1)} %convolution_convert_fusion, s32[51]{0:T(128)S(1)} %dynamic-slice_bitcast_fusion), kind=kOutput, calls=%fused_computation.5 | convolution fusion | flops 80385792 | bytes 1886412 | tf_op jit(solution)/shard_map/dot_general | solution.py:245
  24.4 0.9 %fusion.130 = (f32[51]{0:T(128)}, f32[51,1024]{1,0:T(8,128)S(1)}) fusion(bf16[256,1024]{1,0:T(8,128)(2,1)S(1)} %get-tuple-element.26, s32[51]{0:T(128)S(1)} %dynamic-slice_bitcast_fusion), kind=kOutput, calls=%fused_computation.228 | convolution fusion | flops 26908364 | bytes 733592 | tf_op jit(solution)/shard_map/dot_general | solution.py:239
  25.5 1.0 %fusion = (f32[16,256]{1,0:T(8,128)S(1)}, f32[16,256,256]{1,2,0:T(8,128)S(1)}) fusion(f32[256,16]{0,1:T(8,128)S(1)} %get-tuple-element.46, bf16[256,3,16,64]{0,3,2,1:T(8,128)(2,1)S(1)} %bitcast.164, f32[256,16]{0,1:T(8,128)S(1)} %get-tuple-element.47), kind=kOutput, calls=%fused_computation.4 | convolution fusion | flops 137883648 | bytes 5292032 | tf_op jit(solution)/shard_map/qhd,khd->hqk/dot_general | solution.py:33
  28.5 1.0 %multiply_convert_fusion.targets_ref = bf16[256,1024]{1,0:T(8,128)(2,1)} fusion(f32[256,1024]{1,0:T(8,128)S(1)} %get-tuple-element.34, f32[256]{0:T(256)S(1)} %add_rsqrt_fusion.2, f32[256]{0:T(256)S(1)} %broadcast_multiply_fusion.1), kind=kLoop, calls=%fused_computation.62 | loop fusion | flops 786432 | bytes 1574912 | tf_op jit(solution)/shard_map/convert_element_type | solution.py:251
  32.2 2.2 %convolution_convert_fusion.17 = bf16[51,768]{1,0:T(8,128)(2,1)S(1)} fusion(bf16[1024,768]{1,0:T(8,128)(2,1)} %param.15, f32[51,1024]{1,0:T(8,128)S(1)} %get-tuple-element.36, bf16[51,1024]{1,0:T(8,128)(2,1)S(1)} %reshape.257, bf16[1024,1024]{1,0:T(8,128)(2,1)S(1)} %copy-done), kind=kOutput, calls=%fused_computation.53 | convolution fusion | flops 187314432 | bytes 4061696 | tf_op jit(solution)/shard_map/jvp()/dot_general | solution.py:86
  35.0 1.3 %fusion.68 = f32[16,256,48]{1,2,0:T(8,128)S(1)} fusion(bf16[256,16,48]{0,2,1:T(8,128)(2,1)S(1)} %bitcast.170, bf16[3,16,48,48]{3,2,1,0:T(8,128)(2,1)} %param.16), kind=kOutput, calls=%fused_computation.132 | convolution fusion | flops 18874368 | bytes 1376256 | tf_op jit(solution)/shard_map/jvp(pgi,gio->pgo)/dot_general | solution.py:98
  36.3 1.2 %convolution_add_fusion.1 = f32[16,256,48]{1,2,0:T(8,128)S(1)} fusion(f32[16,256,48]{1,2,0:T(8,128)S(1)} %fusion.68, bf16[256,16,48]{0,2,1:T(8,128)(2,1)S(1)} %bitcast.171, bf16[3,16,48,48]{3,2,1,0:T(8,128)(2,1)} %param.16), kind=kOutput, calls=%fused_computation.15 | convolution fusion | flops 19070976 | bytes 2162688 | tf_op jit(solution)/shard_map/jvp(pgi,gio->pgo)/dot_general | solution.py:98
  37.6 1.4 %fusion.128 = (f32[256]{0:T(256)S(1)}, f32[16,256,48]{1,2,0:T(8,128)S(1)}) fusion(f32[16,256,48]{1,2,0:T(8,128)S(1)} %convolution_add_fusion.1, bf16[256,16,48]{0,2,1:T(8,128)(2,1)S(1)} %bitcast.172, bf16[3,16,48,48]{3,2,1,0:T(8,128)(2,1)} %param.16), kind=kOutput, calls=%fused_computation.226 | convolution fusion | flops 19267328 | bytes 2163712 | tf_op jit(solution)/shard_map/jvp(pgi,gio->pgo)/dot_general | solution.py:98
  39.8 1.4 %copy.62 = f32[256,768]{1,0:T(8,128)S(1)} copy(f32[256,768]{0,1:T(8,128)} %bitcast.166) | data formatting | bytes 1572864 | tf_op jit(solution)/shard_map/jvp()/reshape | solution.py:104
  41.2 3.0 %add_convert_fusion = (bf16[256,768]{1,0:T(8,128)(2,1)}, f32[256,768]{1,0:T(8,128)}) fusion(bf16[256,768]{1,0:T(8,128)(2,1)S(1)} %fusion.3, f32[256,768]{1,0:T(8,128)S(1)} %copy.62, f32[256]{0:T(256)S(1)} %fusion.111, f32[256]{0:T(256)S(1)} %broadcast_multiply_fusion), kind=kLoop, calls=%fused_computation.87 | loop fusion | flops 13565952 | bytes 2361344 | tf_op jit(solution)/shard_map/jvp()/convert_element_type | solution.py:105
  44.2 3.5 %jvp__.1 = (f32[1,1]{1,0:T(1,128)}, bf16[256,768]{1,0:T(8,128)(2,1)}) custom-call(bf16[256,768]{1,0:T(8,128)(2,1)} %get-tuple-element.14.hidden_ref, bf16[768,1024]{1,0:T(8,128)(2,1)} %dec_out_ref.1, bf16[256,1024]{1,0:T(8,128)(2,1)} %multiply_convert_fusion.targets_ref, f32[256,1]{1,0:T(8,128)} %copy.65.keep_ref), custom_call_target="tpu_custom_call" | custom-call | tf_op jit(solution)/shard_map/jvp()/pallas_call | solution.py:124
  47.7 2.0 %multiply_reduce_fusion.1 = f32[256]{0:T(256)S(1)} fusion(f32[256,768]{1,0:T(8,128)S(1)} %copy.62, f32[256]{0:T(256)S(1)} %broadcast_multiply_fusion, f32[256,768]{1,0:T(8,128)} %get-tuple-element.15, bf16[256,768]{1,0:T(8,128)(2,1)} %get-tuple-element.4, f32[256]{0:T(256)S(1)} %fusion.111), kind=kLoop, calls=%fused_computation.86 | loop fusion | flops 3538688 | bytes 1969152 | tf_op jit(solution)/shard_map/transpose(jvp())/reduce_sum | solution.py:23
  50.8 1.4 %fusion.7 = bf16[256,16,48]{0,2,1:T(8,128)(2,1)S(1)} fusion(bf16[16,48,256]{2,1,0:T(8,128)(2,1)S(1)} %bitcast.167, bf16[3,16,48,48]{3,2,1,0:T(8,128)(2,1)} %param.16), kind=kOutput, calls=%fused_computation.26 | convolution fusion | flops 18874368 | bytes 983040 | tf_op jit(solution)/shard_map/transpose(jvp(pgi,gio->pgo))/dot_general | solution.py:98
  52.2 1.2 %fusion.8 = bf16[256,16,48]{0,2,1:T(8,128)(2,1)S(1)} fusion(bf16[16,48,256]{2,1,0:T(8,128)(2,1)S(1)} %bitcast.168, bf16[3,16,48,48]{3,2,1,0:T(8,128)(2,1)} %param.16), kind=kOutput, calls=%fused_computation.27 | convolution fusion | flops 18874368 | bytes 983040 | tf_op jit(solution)/shard_map/transpose(jvp(pgi,gio->pgo))/dot_general | solution.py:98
  53.4 1.2 %fusion.9 = bf16[256,16,48]{0,2,1:T(8,128)(2,1)S(1)} fusion(bf16[16,48,256]{2,1,0:T(8,128)(2,1)S(1)} %bitcast.169, bf16[3,16,48,48]{3,2,1,0:T(8,128)(2,1)} %param.16), kind=kOutput, calls=%fused_computation.28 | convolution fusion | flops 18874368 | bytes 983040 | tf_op jit(solution)/shard_map/transpose(jvp(pgi,gio->pgo))/dot_general | solution.py:98
  55.1 2.2 %convolution_convert_fusion.12 = bf16[51,1024]{1,0:T(8,128)(2,1)S(1)} fusion(bf16[1024,768]{1,0:T(8,128)(2,1)} %param.15, bf16[256,768]{1,0:T(8,128)(2,1)S(1)} %copy-done.5, bf16[256,768]{1,0:T(8,128)(2,1)S(1)} %copy.70, pred[256]{0:T(512)(128)(4,1)} %copy-done.26, s32[51]{0:T(128)} %copy-done.24), kind=kOutput, calls=%fused_computation.46 | convolution fusion | flops 100964352 | bytes 2464204 | tf_op jit(solution)/shard_map/transpose(jvp())/dot_general | solution.py:86
  58.2 1.4 %fusion.16 = bf16[51,1,16,64]{3,0,2,1:T(8,128)(2,1)S(1)} fusion(bf16[51,16,64]{2,1,0:T(8,128)(2,1)S(1)} %reshape.264, f32[16,51,51]{1,2,0:T(8,128)} %copy-done.12, f32[16,51]{1,0:T(8,128)S(1)} %copy-done.23), kind=kOutput, calls=%fused_computation.42 | convolution fusion | flops 5462304 | bytes 378624 | tf_op jit(solution)/shard_map/transpose(jvp(hqk,khd->qhd))/dot_general | solution.py:38
  62.5 5.0 %multiply_reduce_fusion.4 = (f32[51]{0:T(128)S(1)}, f32[51]{0:T(128)S(1)}, f32[51,1024]{1,0:T(8,128)S(1)}) fusion(f32[51,1024]{1,0:T(8,128)S(1)} %get-tuple-element.36, f32[51]{0:T(128)S(1)} %broadcast_multiply_fusion.3, bf16[51,3072]{1,0:T(8,128)(2,1)S(1)} %reshape.265, bf16[1024,3072]{1,0:T(8,128)(2,1)} %param.12), kind=kOutput, calls=%fused_computation.150 | convolution fusion | flops 321229696 | bytes 7023204 | tf_op jit(solution)/shard_map/transpose(jvp(transpose(jvp())))/dot_general | solution.py:174
  68.4 1.5 %collective-permute-start.4 = (bf16[51,1024]{1,0:T(8,128)(2,1)S(1)}, bf16[51,1024]{1,0:T(8,128)(2,1)S(1)}, u32[]{:S(2)}, u32[]{:S(2)}) collective-permute-start(bf16[51,1024]{1,0:T(8,128)(2,1)S(1)} %fusion.99), channel_id=1, source_target_pairs={{0,2},{1,3},{2,0},{3,1},{4,6},{5,7},{6,4},{7,5},{8,10},{9,11},{10,... | collective-permute-start | bytes 313352 | tf_op jit(solution)/shard_map/ppermute | solution.py:188
  70.8 2.6 %collective-permute-done.3 = bf16[51,1024]{1,0:T(8,128)(2,1)S(1)} collective-permute-done((bf16[51,1024]{1,0:T(8,128)(2,1)S(1)}, bf16[51,1024]{1,0:T(8,128)(2,1)S(1)}, u32[]{:S(2)}, u32[]{:S(2)}) %collective-permute-start.3) | collective-permute-done | bytes 104480 | tf_op jit(solution)/shard_map/ppermute | solution.py:188
  73.4 1.0 %collective-permute-done.4 = bf16[51,1024]{1,0:T(8,128)(2,1)S(1)} collective-permute-done((bf16[51,1024]{1,0:T(8,128)(2,1)S(1)}, bf16[51,1024]{1,0:T(8,128)(2,1)S(1)}, u32[]{:S(2)}, u32[]{:S(2)}) %collective-permute-start.4) | collective-permute-done | bytes 104480 | tf_op jit(solution)/shard_map/ppermute | solution.py:188
  74.4 1.3 %collective-permute-done.5 = bf16[51,1024]{1,0:T(8,128)(2,1)S(1)} collective-permute-done((bf16[51,1024]{1,0:T(8,128)(2,1)S(1)}, bf16[51,1024]{1,0:T(8,128)(2,1)S(1)}, u32[]{:S(2)}, u32[]{:S(2)}) %collective-permute-start.5) | collective-permute-done | bytes 104480 | tf_op jit(solution)/shard_map/ppermute | solution.py:188
  75.6 1.4 %fusion.20 = f32[192,1024]{1,0:T(8,128)} fusion(bf16[51,1024]{1,0:T(8,128)(2,1)S(1)} %collective-permute-done.5, bf16[51,1024]{1,0:T(8,128)(2,1)S(1)} %collective-permute-done.4, bf16[51,1024]{1,0:T(8,128)(2,1)S(1)} %collective-permute-done.3, bf16[51,1024]{1,0:T(8,128)(2,1)S(1)} %fusion.99, bf16[256,768]{1,0:T(8,128)(2,1)S(1)} %pad_maximum_fusion, ...), kind=kOutput, calls=%fused_computation.54 | convolution fusion | flops 102032640 | bytes 1377284 | tf_op jit(solution)/shard_map/vc,vd->cd/dot_general | solution.py:279
  (122 shorter events, 15.9 us)
Async XLA Ops:
  0.6 26.7 %copy-start = (bf16[1024,1024]{1,0:T(8,128)(2,1)S(1)}, bf16[1024,1024]{1,0:T(8,128)(2,1)}, u32[]{:S(2)}) copy-start(bf16[1024,1024]{1,0:T(8,128)(2,1)} %param.13) | copy-start | bytes 6291460
  0.6 12.2 %collective-permute-start = (bf16[64,768]{1,0:T(8,128)(2,1)}, bf16[64,768]{1,0:T(8,128)(2,1)S(1)}, u32[]{:S(2)}, u32[]{:S(2)}) collective-permute-start(bf16[64,768]{1,0:T(8,128)(2,1)} %param.9), channel_id=1, source_target_pairs={{0,1},{1,2},{2,3},{3,0},{4,5},{5,6},{6,7},{7,4},{8,9},{9,10},{10,1... | collective-permute-start | bytes 294920 | tf_op jit(solution)/shard_map/ppermute | solution.py:188
  3.7 9.2 %collective-permute-start.1 = (bf16[64,768]{1,0:T(8,128)(2,1)}, bf16[64,768]{1,0:T(8,128)(2,1)S(1)}, u32[]{:S(2)}, u32[]{:S(2)}) collective-permute-start(bf16[64,768]{1,0:T(8,128)(2,1)} %param.9), channel_id=1, source_target_pairs={{0,2},{1,3},{2,0},{3,1},{4,6},{5,7},{6,4},{7,5},{8,10},{9,11},{10,... | collective-permute-start | bytes 294920 | tf_op jit(solution)/shard_map/ppermute | solution.py:188
  5.2 7.7 %collective-permute-start.2 = (bf16[64,768]{1,0:T(8,128)(2,1)}, bf16[64,768]{1,0:T(8,128)(2,1)S(1)}, u32[]{:S(2)}, u32[]{:S(2)}) collective-permute-start(bf16[64,768]{1,0:T(8,128)(2,1)} %param.9), channel_id=1, source_target_pairs={{0,3},{1,0},{2,1},{3,2},{4,7},{5,4},{6,5},{7,6},{8,11},{9,8},{10,9... | collective-permute-start | bytes 294920 | tf_op jit(solution)/shard_map/ppermute | solution.py:188
  7.3 27.1 %copy-start.24 = (s32[51]{0:T(128)}, s32[51]{0:T(128)S(1)}, u32[]{:S(2)}) copy-start(s32[51]{0:T(128)S(1)} %dynamic-slice_bitcast_fusion) | copy-start | bytes 616
  7.5 26.9 %copy-start.26 = (pred[256]{0:T(512)(128)(4,1)}, pred[256]{0:T(512)(128)(4,1)S(1)}, u32[]{:S(2)}) copy-start(pred[256]{0:T(512)(128)(4,1)S(1)} %broadcast_compare_fusion) | copy-start | bytes 772
  10.9 5.8 %copy-start.4 = (bf16[1024,3072]{1,0:T(8,128)(2,1)S(1)}, bf16[1024,3072]{1,0:T(8,128)(2,1)}, u32[]{:S(2)}) copy-start(bf16[1024,3072]{1,0:T(8,128)(2,1)} %param.12) | copy-start | bytes 18874372
  14.2 2.5 %copy-start.14 = (bf16[64,768]{1,0:T(8,128)(2,1)}, bf16[64,768]{1,0:T(8,128)(2,1)S(1)}, u32[]{:S(2)}) copy-start(bf16[64,768]{1,0:T(8,128)(2,1)S(1)} %get-tuple-element.19) | copy-start | bytes 294916
  14.2 2.5 %copy-start.16 = (bf16[64,768]{1,0:T(8,128)(2,1)}, bf16[64,768]{1,0:T(8,128)(2,1)S(1)}, u32[]{:S(2)}) copy-start(bf16[64,768]{1,0:T(8,128)(2,1)S(1)} %get-tuple-element.20) | copy-start | bytes 294916
  14.2 2.5 %copy-start.18 = (bf16[64,768]{1,0:T(8,128)(2,1)}, bf16[64,768]{1,0:T(8,128)(2,1)S(1)}, u32[]{:S(2)}) copy-start(bf16[64,768]{1,0:T(8,128)(2,1)S(1)} %get-tuple-element.21) | copy-start | bytes 294916
  14.2 2.5 %copy-start.20 = (bf16[64,768]{1,0:T(8,128)(2,1)}, bf16[64,768]{1,0:T(8,128)(2,1)S(1)}, u32[]{:S(2)}) copy-start(bf16[64,768]{1,0:T(8,128)(2,1)S(1)} %get-tuple-element.22) | copy-start | bytes 294916
  22.4 2.8 %copy-start.1 = (bf16[256,3072]{0,1:T(8,128)(2,1)S(1)}, bf16[256,3072]{0,1:T(8,128)(2,1)}, u32[]{:S(2)}) copy-start(bf16[256,3072]{0,1:T(8,128)(2,1)} %copy.63) | copy-start | bytes 4718596
  30.0 1.2 %copy-start.8 = (bf16[51,1,16,64]{3,2,1,0:T(8,128)(2,1)}, bf16[51,1,16,64]{3,2,1,0:T(8,128)(2,1)S(1)}, u32[]{:S(2)}) copy-start(bf16[51,1,16,64]{3,2,1,0:T(8,128)(2,1)S(1)} %get-tuple-element.18) | copy-start | bytes 313348
  30.0 1.2 %copy-start.10 = (bf16[51,1,16,64]{3,2,1,0:T(8,128)(2,1)}, bf16[51,1,16,64]{3,2,1,0:T(8,128)(2,1)S(1)}, u32[]{:S(2)}) copy-start(bf16[51,1,16,64]{3,2,1,0:T(8,128)(2,1)S(1)} %get-tuple-element.17) | copy-start | bytes 313348
  31.2 1.0 %copy-start.22 = (f32[16,51]{1,0:T(8,128)}, f32[16,51]{1,0:T(8,128)S(1)}, u32[]{:S(2)}) copy-start(f32[16,51]{1,0:T(8,128)S(1)} %get-tuple-element.27) | copy-start | bytes 9796
  38.9 0.9 %copy-start.2 = (f32[16,256,48]{1,2,0:T(8,128)}, f32[16,256,48]{1,2,0:T(8,128)S(1)}, u32[]{:S(2)}) copy-start(f32[16,256,48]{1,2,0:T(8,128)S(1)} %get-tuple-element.30) | copy-start | bytes 2359300
  47.7 2.0 %copy-start.3 = (f32[256,768]{1,0:T(8,128)S(1)}, f32[256,768]{1,0:T(8,128)}, u32[]{:S(2)}) copy-start(f32[256,768]{1,0:T(8,128)} %get-tuple-element.15) | copy-start | bytes 2359300
  47.7 2.0 %copy-start.5 = (bf16[256,768]{1,0:T(8,128)(2,1)S(1)}, bf16[256,768]{1,0:T(8,128)(2,1)}, u32[]{:S(2)}) copy-start(bf16[256,768]{1,0:T(8,128)(2,1)} %get-tuple-element.4) | copy-start | bytes 1179652
  50.6 3.9 %copy-start.23 = (f32[16,51]{1,0:T(8,128)S(1)}, f32[16,51]{1,0:T(8,128)}, u32[]{:S(2)}) copy-start(f32[16,51]{1,0:T(8,128)} %copy-done.22) | copy-start | bytes 9796
  57.3 2.4 %copy-start.11 = (bf16[51,1,16,64]{3,2,1,0:T(8,128)(2,1)S(1)}, bf16[51,1,16,64]{3,2,1,0:T(8,128)(2,1)}, u32[]{:S(2)}) copy-start(bf16[51,1,16,64]{3,2,1,0:T(8,128)(2,1)} %copy-done.10) | copy-start | bytes 313348
  58.0 1.9 %copy-start.7 = (bf16[51,1,16,64]{3,2,1,0:T(8,128)(2,1)S(1)}, bf16[51,1,16,64]{3,2,1,0:T(8,128)(2,1)}, u32[]{:S(2)}) copy-start(bf16[51,1,16,64]{3,2,1,0:T(8,128)(2,1)} %copy-done.6) | copy-start | bytes 313348
  58.0 1.9 %copy-start.9 = (bf16[51,1,16,64]{3,2,1,0:T(8,128)(2,1)S(1)}, bf16[51,1,16,64]{3,2,1,0:T(8,128)(2,1)}, u32[]{:S(2)}) copy-start(bf16[51,1,16,64]{3,2,1,0:T(8,128)(2,1)} %copy-done.8) | copy-start | bytes 313348
  58.2 1.4 %copy-start.13 = (f32[16,51,51]{1,2,0:T(8,128)S(1)}, f32[16,51,51]{1,2,0:T(8,128)}, u32[]{:S(2)}) copy-start(f32[16,51,51]{1,2,0:T(8,128)} %copy-done.12) | copy-start | bytes 499396
  61.3 1.1 %copy-start.27 = (f32[51]{0:T(128)S(1)}, f32[51]{0:T(128)}, u32[]{:S(2)}) copy-start(f32[51]{0:T(128)} %get-tuple-element.35) | copy-start | bytes 616
  62.4 8.3 %copy-start.15 = (bf16[64,768]{1,0:T(8,128)(2,1)S(1)}, bf16[64,768]{1,0:T(8,128)(2,1)}, u32[]{:S(2)}) copy-start(bf16[64,768]{1,0:T(8,128)(2,1)} %copy-done.14) | copy-start | bytes 294916
  62.4 8.3 %copy-start.17 = (bf16[64,768]{1,0:T(8,128)(2,1)S(1)}, bf16[64,768]{1,0:T(8,128)(2,1)}, u32[]{:S(2)}) copy-start(bf16[64,768]{1,0:T(8,128)(2,1)} %copy-done.16) | copy-start | bytes 294916
  62.4 8.3 %copy-start.19 = (bf16[64,768]{1,0:T(8,128)(2,1)S(1)}, bf16[64,768]{1,0:T(8,128)(2,1)}, u32[]{:S(2)}) copy-start(bf16[64,768]{1,0:T(8,128)(2,1)} %copy-done.18) | copy-start | bytes 294916
  62.4 8.3 %copy-start.21 = (bf16[64,768]{1,0:T(8,128)(2,1)S(1)}, bf16[64,768]{1,0:T(8,128)(2,1)}, u32[]{:S(2)}) copy-start(bf16[64,768]{1,0:T(8,128)(2,1)} %copy-done.20) | copy-start | bytes 294916
  62.5 13.2 %copy-start.25 = (s32[204]{0:T(256)S(1)}, s32[204]{0:T(256)}, u32[]{:S(2)}) copy-start(s32[204]{0:T(256)} %eq.93) | copy-start | bytes 2452
  67.8 5.5 %collective-permute-start.3 = (bf16[51,1024]{1,0:T(8,128)(2,1)S(1)}, bf16[51,1024]{1,0:T(8,128)(2,1)S(1)}, u32[]{:S(2)}, u32[]{:S(2)}) collective-permute-start(bf16[51,1024]{1,0:T(8,128)(2,1)S(1)} %fusion.99), channel_id=1, source_target_pairs={{0,3},{1,0},{2,1},{3,2},{4,7},{5,4},{6,5},{7,6},{8,11},{9,8},{10,9... | collective-permute-start | bytes 313352 | tf_op jit(solution)/shard_map/ppermute | solution.py:188
  68.4 6.0 %collective-permute-start.4 = (bf16[51,1024]{1,0:T(8,128)(2,1)S(1)}, bf16[51,1024]{1,0:T(8,128)(2,1)S(1)}, u32[]{:S(2)}, u32[]{:S(2)}) collective-permute-start(bf16[51,1024]{1,0:T(8,128)(2,1)S(1)} %fusion.99), channel_id=1, source_target_pairs={{0,2},{1,3},{2,0},{3,1},{4,6},{5,7},{6,4},{7,5},{8,10},{9,11},{10,... | collective-permute-start | bytes 313352 | tf_op jit(solution)/shard_map/ppermute | solution.py:188
  69.9 5.7 %collective-permute-start.5 = (bf16[51,1024]{1,0:T(8,128)(2,1)S(1)}, bf16[51,1024]{1,0:T(8,128)(2,1)S(1)}, u32[]{:S(2)}, u32[]{:S(2)}) collective-permute-start(bf16[51,1024]{1,0:T(8,128)(2,1)S(1)} %fusion.99), channel_id=1, source_target_pairs={{0,1},{1,2},{2,3},{3,0},{4,5},{5,6},{6,7},{7,4},{8,9},{9,10},{10,1... | collective-permute-start | bytes 313352 | tf_op jit(solution)/shard_map/ppermute | solution.py:188
  (2 other events, 1.5 us)

commit v17 on v16

--- a/solution.py
+++ b/solution.py
@@ -181,6 +181,12 @@
     return squares_of(hidden, dec_out, targets, (1.0 - seen)[:, None], scale)
 
 
+def exchange_gather(values, group_size):
+    copies_out = jnp.broadcast_to(values[None], (group_size,) + values.shape)
+    gathered = lax.all_to_all(copies_out, "mask", split_axis=0, concat_axis=0, tiled=True)
+    return gathered.reshape((group_size * values.shape[0],) + values.shape[1:])
+
+
 def ring_gather(values, group_size):
     parts = [values]
     for shift in range(1, group_size):
@@ -230,7 +236,7 @@
     total_rows = tok_rows * group_size
     col_width = patches.shape[1] // group_size
     positions = lax.dynamic_index_in_dim(visible_index, own_index, 0, keepdims=False)
-    clip_pixels = in_mask_order(ring_gather(patches, group_size), own_index)
+    clip_pixels = exchange_gather(patches, group_size)
     embedded = jnp.dot(clip_pixels, embed_w, preferred_element_type=jnp.float32).astype(
         jnp.bfloat16
     )
@@ -269,8 +275,7 @@
     squares, pullback = jax.vjp(objective, visible_in)
     (grad_in,) = pullback(jnp.ones_like(squares) * factor)
     copy_loss = jnp.reshape(squares / ((total_rows - visible_count) * D), (1,))
-    slot_copy = (own_index + jnp.arange(group_size, dtype=jnp.int32)) % group_size
-    flat_index = visible_index[slot_copy].reshape(copies * visible_count)
+    flat_index = visible_index.reshape(copies * visible_count)
     own_cols = lax.dynamic_slice_in_dim(clip_pixels, own_index * col_width, col_width, 1)
     all_picks = (flat_index[:, None] == clip_ids[None, :]).astype(jnp.bfloat16)
     gathered = jnp.dot(all_picks, own_cols, preferred_element_type=jnp.float32).astype(
@@ -279,7 +284,7 @@
     embed_grad = jnp.einsum(
         "vc,vd->cd",
         gathered,
-        jnp.concatenate(ring_gather(grad_in, group_size), axis=0),
+        exchange_gather(grad_in, group_size),
         preferred_element_type=jnp.float32,
     )
     return (embed_grad, copy_loss)

time: 78.8 us -> 85.7 us (1.088)
  matrix products: 35.7 us -> 39.1 us
  waiting for transfers between devices: 4.87 us -> 8.16 us
  other arithmetic: 11.2 us -> 9.87 us
  local copies, waits for them, and re-layouts: 11.5 us -> 12.4 us
    all_to_all x0 -> x2, starting transfers between devices: none -> 8.66 us  [exchange_gather(): lax.all_to_all(copies_out, 'mask', split_axis=0, concat_axis=0, tiled=True)]
    all_to_all x0 -> x2, waiting for transfers between devices: none -> 8.16 us  [exchange_gather(): lax.all_to_all(copies_out, 'mask', split_axis=0, concat_axis=0, tiled=True)]
    ppermute x6 -> x0, starting transfers between devices: 8.15 us -> none  [ring_gather(): parts.append(lax.ppermute(values, 'mask', pairs))]
    ppermute x6 -> x0, waiting for transfers between devices: 4.87 us -> none  [ring_gather(): parts.append(lax.ppermute(values, 'mask', pairs))]
    dot_general x1, matrix products: 3.1 us -> 5.83 us  [project_rows(): jnp.dot(normed, w_qkv, preferred_element_type=jnp.float32)]
    broadcast_in_dim x0 -> x2, local copies, waits for them, and re-layouts: none -> 2.63 us  [exchange_gather(): copies_out = jnp.broadcast_to(values[None], (group_size,) + values.shape)]
    select_n x2 -> x0, other arithmetic: 1.32 us -> none  [the longest x1 1.31 us: in_mask_order(): chosen = jnp.where(slot == other, parts[other], chosen)]
    gather x1 -> x0, local copies, waits for them, and re-layouts: 1.24 us -> none  [on_device(): flat_index = visible_index[slot_copy].reshape(copies * visible_count)]
  transfers between devices with their start and end apart: 6 -> 2, of which waited for: 3 -> 2; matrix products, arithmetic and copies ran while one was open for 8% -> 5% of each run, Pallas kernels for 0% -> 0%
where the time goes in v17:
time: 85.7 us; the launch traced here: 84.8 us
  matrix products  39.1 us (46%)
  local copies, waits for them, and re-layouts  12.4 us (14%)
  other arithmetic  9.87 us (12%)
  starting transfers between devices  8.66 us (10%)
  waiting for transfers between devices  8.16 us (10%)
  Pallas kernels  3.54 us (4%)
  between operations  3.02 us (4%)
    all_to_all x2, starting transfers between devices, exchange_gather(): lax.all_to_all(copies_out, 'mask', split_axis=0, concat_axis=0, tiled=True)  8.66 us
    all_to_all x2, waiting for transfers between devices, exchange_gather(): lax.all_to_all(copies_out, 'mask', split_axis=0, concat_axis=0, tiled=True)  8.16 us
    dot_general x6, matrix products, decoder_output(): jnp.einsum('pgi,gio->pgo', padded[offset:offset + total_rows], conv_w[off...  7.62 us
    dot_general x1, matrix products, project_rows(): jnp.dot(normed, w_qkv, preferred_element_type=jnp.float32)  5.83 us
    dot_general x1, matrix products, copy_terms(): branch = attention_from(reuse_rows(visible_in, w_qkv, projected), w_out)  4.93 us
    dot_general x2, matrix products, decoder_output(): jnp.dot(visible_out, dec_in, preferred_element_type=jnp.float32)  4.38 us
    pallas_call x1, Pallas kernels, masked_squares(): pl.pallas_call(functools.partial(loss_kernel, scale=scale), out_shape=(ja...  3.54 us
    convert_element_type x1, other arithmetic, decoder_output(): return (lowered.astype(jnp.float32) + activated).astype(jnp.bfloat16)  2.97 us
  transfers between devices with their start and end apart: 2, of which 2 were waited for; matrix products, arithmetic and copies ran while one was open for 5% of the time, Pallas kernels for 0%

profile of v17, /device:TPU:0, one launch (start us, length us, event | category | flops | bytes accessed | tf_op | source)
XLA Modules:
  0.0 84.8 jit_solution(9570176197891735885)
XLA Ops:
  0.6 1.8 %broadcast_in_dim.44 = bf16[4,64,768]{2,1,0:T(8,128)(2,1)} broadcast(bf16[64,768]{1,0:T(8,128)(2,1)} %param.9), dimensions={1,2} | broadcast | bytes 491520 | tf_op jit(solution)/shard_map/broadcast_in_dim | solution.py:185
  2.5 5.2 %all-to-all-start = ((bf16[4,64,768]{2,1,0:T(8,128)(2,1)}), bf16[4,64,768]{2,1,0:T(8,128)(2,1)S(1)}, u32[]{:S(2)}, u32[]{:S(2)}) async-start(bf16[4,64,768]{2,1,0:T(8,128)(2,1)} %broadcast_in_dim.44), calls=%async_computation | async-start | bytes 786432 | tf_op jit(solution)/shard_map/all_to_all | solution.py:186
  9.1 0.8 copy.65.keep_ref
  9.9 1.7 %convolution_reduce_fusion = bf16[768]{0:T(1024)(128)(2,1)S(1)} fusion(bf16[1024,1]{0,1:T(2,128)(2,1)S(1)} %reshape.232, bf16[1024,768]{1,0:T(8,128)(2,1)} %param.15), kind=kOutput, calls=%fused_computation.54 | convolution fusion | flops 1572864 | bytes 1576448 | tf_op jit(solution)/shard_map/jvp()/dot_general | solution.py:89
  11.8 2.5 %all-to-all-done = bf16[4,64,768]{2,1,0:T(8,128)(2,1)S(1)} async-done(((bf16[4,64,768]{2,1,0:T(8,128)(2,1)}), bf16[4,64,768]{2,1,0:T(8,128)(2,1)S(1)}, u32[]{:S(2)}, u32[]{:S(2)}) %all-to-all-start) | async-done | bytes 393248 | tf_op jit(solution)/shard_map/all_to_all | solution.py:186
  14.3 2.2 %convert_reduce_fusion = (f32[256]{0:T(256)S(1)}, bf16[256,1024]{1,0:T(8,128)(2,1)S(1)}) fusion(bf16[256,768]{1,0:T(8,128)(2,1)S(1)} %bitcast.175, bf16[768,1024]{1,0:T(8,128)(2,1)} %param.11), kind=kOutput, calls=%fused_computation.11 | convolution fusion | flops 403439360 | bytes 2491392 | tf_op jit(solution)/shard_map/dot_general | solution.py:240
  16.8 5.8 %convolution_convert_fusion = bf16[256,3072]{1,0:T(8,128)(2,1)} fusion(bf16[1024,3072]{1,0:T(8,128)(2,1)} %param.12, bf16[256,1024]{1,0:T(8,128)(2,1)S(1)} %get-tuple-element.22, f32[256]{0:T(256)S(1)} %add_rsqrt_fusion.3, f32[256]{0:T(256)S(1)} %broadcast_multiply_fusion.2), kind=kOutput, calls=%fused_computation.2 | convolution fusion | flops 1612447744 | bytes 8390656 | tf_op jit(solution)/shard_map/dot_general | solution.py:50
  22.6 2.6 %copy.63 = bf16[256,3072]{0,1:T(8,128)(2,1)} copy(bf16[256,3072]{1,0:T(8,128)(2,1)} %convolution_convert_fusion) | data formatting | bytes 3145728 | tf_op jit(solution)/shard_map/convert_element_type | solution.py:50
  25.2 1.9 %convolution_convert_fusion.1 = bf16[51,3072]{1,0:T(8,128)(2,1)S(1)} fusion(bf16[256,3072]{1,0:T(8,128)(2,1)} %convolution_convert_fusion, s32[51]{0:T(128)S(1)} %dynamic-slice_bitcast_fusion), kind=kOutput, calls=%fused_computation.4 | convolution fusion | flops 80385792 | bytes 1886412 | tf_op jit(solution)/shard_map/dot_general | solution.py:251
  27.2 0.9 %fusion.120 = (f32[51]{0:T(128)}, f32[51,1024]{1,0:T(8,128)S(1)}) fusion(bf16[256,1024]{1,0:T(8,128)(2,1)S(1)} %get-tuple-element.22, s32[51]{0:T(128)S(1)} %dynamic-slice_bitcast_fusion), kind=kOutput, calls=%fused_computation.207 | convolution fusion | flops 26908364 | bytes 733592 | tf_op jit(solution)/shard_map/dot_general | solution.py:245
  28.3 1.0 %fusion = (f32[16,256]{1,0:T(8,128)S(1)}, f32[16,256,256]{1,2,0:T(8,128)S(1)}) fusion(f32[256,16]{0,1:T(8,128)S(1)} %get-tuple-element.42, bf16[256,3,16,64]{0,3,2,1:T(8,128)(2,1)S(1)} %bitcast.165, f32[256,16]{0,1:T(8,128)S(1)} %get-tuple-element.43), kind=kOutput, calls=%fused_computation.3 | convolution fusion | flops 137883648 | bytes 5292032 | tf_op jit(solution)/shard_map/qhd,khd->hqk/dot_general | solution.py:33
  29.3 0.8 fusion.2
  30.1 0.8 fusion.119
  31.2 1.0 %multiply_convert_fusion.targets_ref = bf16[256,1024]{1,0:T(8,128)(2,1)} fusion(f32[256,1024]{1,0:T(8,128)S(1)} %get-tuple-element.30, f32[256]{0:T(256)S(1)} %add_rsqrt_fusion.2, f32[256]{0:T(256)S(1)} %broadcast_multiply_fusion.1), kind=kLoop, calls=%fused_computation.61 | loop fusion | flops 786432 | bytes 1574912 | tf_op jit(solution)/shard_map/convert_element_type | solution.py:257
  35.0 2.2 %convolution_convert_fusion.17 = bf16[51,768]{1,0:T(8,128)(2,1)S(1)} fusion(bf16[1024,768]{1,0:T(8,128)(2,1)} %param.15, f32[51,1024]{1,0:T(8,128)S(1)} %get-tuple-element.32, bf16[51,1024]{1,0:T(8,128)(2,1)S(1)} %reshape.217, bf16[1024,1024]{1,0:T(8,128)(2,1)S(1)} %copy-done), kind=kOutput, calls=%fused_computation.52 | convolution fusion | flops 187314432 | bytes 4061696 | tf_op jit(solution)/shard_map/jvp()/dot_general | solution.py:86
  37.7 1.3 %fusion.61 = f32[16,256,48]{1,2,0:T(8,128)S(1)} fusion(bf16[256,16,48]{0,2,1:T(8,128)(2,1)S(1)} %bitcast.171, bf16[3,16,48,48]{3,2,1,0:T(8,128)(2,1)} %param.16), kind=kOutput, calls=%fused_computation.124 | convolution fusion | flops 18874368 | bytes 1376256 | tf_op jit(solution)/shard_map/jvp(pgi,gio->pgo)/dot_general | solution.py:98
  39.1 1.2 %convolution_add_fusion.1 = f32[16,256,48]{1,2,0:T(8,128)S(1)} fusion(f32[16,256,48]{1,2,0:T(8,128)S(1)} %fusion.61, bf16[256,16,48]{0,2,1:T(8,128)(2,1)S(1)} %bitcast.172, bf16[3,16,48,48]{3,2,1,0:T(8,128)(2,1)} %param.16), kind=kOutput, calls=%fused_computation.14 | convolution fusion | flops 19070976 | bytes 2162688 | tf_op jit(solution)/shard_map/jvp(pgi,gio->pgo)/dot_general | solution.py:98
  40.3 1.4 %fusion.118 = (f32[256]{0:T(256)S(1)}, f32[16,256,48]{1,2,0:T(8,128)S(1)}) fusion(f32[16,256,48]{1,2,0:T(8,128)S(1)} %convolution_add_fusion.1, bf16[256,16,48]{0,2,1:T(8,128)(2,1)S(1)} %bitcast.173, bf16[3,16,48,48]{3,2,1,0:T(8,128)(2,1)} %param.16), kind=kOutput, calls=%fused_computation.205 | convolution fusion | flops 19267328 | bytes 2163712 | tf_op jit(solution)/shard_map/jvp(pgi,gio->pgo)/dot_general | solution.py:98
  42.6 1.4 %copy.62 = f32[256,768]{1,0:T(8,128)S(1)} copy(f32[256,768]{0,1:T(8,128)} %bitcast.167) | data formatting | bytes 1572864 | tf_op jit(solution)/shard_map/jvp()/reshape | solution.py:104
  44.0 3.0 %add_convert_fusion = (bf16[256,768]{1,0:T(8,128)(2,1)}, f32[256,768]{1,0:T(8,128)}) fusion(bf16[256,768]{1,0:T(8,128)(2,1)S(1)} %fusion.3, f32[256,768]{1,0:T(8,128)S(1)} %copy.62, f32[256]{0:T(256)S(1)} %fusion.104, f32[256]{0:T(256)S(1)} %broadcast_multiply_fusion), kind=kLoop, calls=%fused_computation.86 | loop fusion | flops 13565952 | bytes 2361344 | tf_op jit(solution)/shard_map/jvp()/convert_element_type | solution.py:105
  46.9 3.5 %jvp__.1 = (f32[1,1]{1,0:T(1,128)}, bf16[256,768]{1,0:T(8,128)(2,1)}) custom-call(bf16[256,768]{1,0:T(8,128)(2,1)} %get-tuple-element.14.hidden_ref, bf16[768,1024]{1,0:T(8,128)(2,1)} %dec_out_ref.1, bf16[256,1024]{1,0:T(8,128)(2,1)} %multiply_convert_fusion.targets_ref, f32[256,1]{1,0:T(8,128)} %copy.65.keep_ref), custom_call_target="tpu_custom_call" | custom-call | tf_op jit(solution)/shard_map/jvp()/pallas_call | solution.py:124
  50.5 2.0 %multiply_reduce_fusion.1 = f32[256]{0:T(256)S(1)} fusion(f32[256,768]{1,0:T(8,128)S(1)} %copy.62, f32[256]{0:T(256)S(1)} %broadcast_multiply_fusion, f32[256,768]{1,0:T(8,128)} %get-tuple-element.15, bf16[256,768]{1,0:T(8,128)(2,1)} %get-tuple-element.4, f32[256]{0:T(256)S(1)} %fusion.104), kind=kLoop, calls=%fused_computation.85 | loop fusion | flops 3538688 | bytes 1969152 | tf_op jit(solution)/shard_map/transpose(jvp())/reduce_sum | solution.py:23
  53.6 1.4 %fusion.7 = bf16[256,16,48]{0,2,1:T(8,128)(2,1)S(1)} fusion(bf16[16,48,256]{2,1,0:T(8,128)(2,1)S(1)} %bitcast.168, bf16[3,16,48,48]{3,2,1,0:T(8,128)(2,1)} %param.16), kind=kOutput, calls=%fused_computation.25 | convolution fusion | flops 18874368 | bytes 983040 | tf_op jit(solution)/shard_map/transpose(jvp(pgi,gio->pgo))/dot_general | solution.py:98
  55.0 1.2 %fusion.8 = bf16[256,16,48]{0,2,1:T(8,128)(2,1)S(1)} fusion(bf16[16,48,256]{2,1,0:T(8,128)(2,1)S(1)} %bitcast.169, bf16[3,16,48,48]{3,2,1,0:T(8,128)(2,1)} %param.16), kind=kOutput, calls=%fused_computation.26 | convolution fusion | flops 18874368 | bytes 983040 | tf_op jit(solution)/shard_map/transpose(jvp(pgi,gio->pgo))/dot_general | solution.py:98
  56.1 1.2 %fusion.9 = bf16[256,16,48]{0,2,1:T(8,128)(2,1)S(1)} fusion(bf16[16,48,256]{2,1,0:T(8,128)(2,1)S(1)} %bitcast.170, bf16[3,16,48,48]{3,2,1,0:T(8,128)(2,1)} %param.16), kind=kOutput, calls=%fused_computation.27 | convolution fusion | flops 18874368 | bytes 983040 | tf_op jit(solution)/shard_map/transpose(jvp(pgi,gio->pgo))/dot_general | solution.py:98
  57.8 2.2 %convolution_convert_fusion.12 = bf16[51,1024]{1,0:T(8,128)(2,1)S(1)} fusion(bf16[1024,768]{1,0:T(8,128)(2,1)} %param.15, bf16[256,768]{1,0:T(8,128)(2,1)S(1)} %copy-done.4, bf16[256,768]{1,0:T(8,128)(2,1)S(1)} %copy.70, pred[256]{0:T(512)(128)(4,1)} %copy-done.18, s32[51]{0:T(128)} %copy-done.16), kind=kOutput, calls=%fused_computation.45 | convolution fusion | flops 100964352 | bytes 2464204 | tf_op jit(solution)/shard_map/transpose(jvp())/dot_general | solution.py:86
  61.0 1.4 %fusion.16 = bf16[51,1,16,64]{3,0,2,1:T(8,128)(2,1)S(1)} fusion(bf16[51,16,64]{2,1,0:T(8,128)(2,1)S(1)} %reshape.224, f32[16,51,51]{1,2,0:T(8,128)} %copy-done.12, f32[16,51]{1,0:T(8,128)S(1)} %copy-done.15), kind=kOutput, calls=%fused_computation.41 | convolution fusion | flops 5462304 | bytes 378624 | tf_op jit(solution)/shard_map/transpose(jvp(hqk,khd->qhd))/dot_general | solution.py:38
  65.2 4.9 %multiply_reduce_fusion.4 = (f32[51]{0:T(128)S(1)}, f32[51]{0:T(128)S(1)}, f32[51,1024]{1,0:T(8,128)S(1)}) fusion(f32[51,1024]{1,0:T(8,128)S(1)} %get-tuple-element.32, f32[51]{0:T(128)S(1)} %broadcast_multiply_fusion.3, bf16[51,3072]{1,0:T(8,128)(2,1)S(1)} %reshape.225, bf16[1024,3072]{1,0:T(8,128)(2,1)} %param.12), kind=kOutput, calls=%fused_computation.141 | convolution fusion | flops 321229696 | bytes 7023204 | tf_op jit(solution)/shard_map/transpose(jvp(transpose(jvp())))/dot_general | solution.py:174
  70.5 0.8 broadcast_in_dim.101
  71.3 3.5 %all-to-all-start.1 = ((bf16[4,51,1024]{2,1,0:T(8,128)(2,1)}), bf16[4,51,1024]{2,1,0:T(8,128)(2,1)S(1)}, u32[]{:S(2)}, u32[]{:S(2)}) async-start(bf16[4,51,1024]{2,1,0:T(8,128)(2,1)} %broadcast_in_dim.101), calls=%async_computation.1 | async-start | bytes 917504 | tf_op jit(solution)/shard_map/all_to_all | solution.py:186
  75.5 5.7 %all-to-all-done.1 = bf16[4,51,1024]{2,1,0:T(8,128)(2,1)S(1)} async-done(((bf16[4,51,1024]{2,1,0:T(8,128)(2,1)}), bf16[4,51,1024]{2,1,0:T(8,128)(2,1)S(1)}, u32[]{:S(2)}, u32[]{:S(2)}) %all-to-all-start.1) | async-done | bytes 417824 | tf_op jit(solution)/shard_map/all_to_all | solution.py:186
  81.3 2.4 %fusion.20 = f32[192,1024]{1,0:T(8,128)} fusion(bf16[204,1024]{1,0:T(8,128)(2,1)S(1)} %reshape.226, bf16[256,768]{1,0:T(8,128)(2,1)} %bitcast.176, s32[]{:T(128)S(6)} %select_n.15, s32[204]{0:T(256)S(1)} %eq.22), kind=kOutput, calls=%fused_computation.53 | convolution fusion | flops 100361472 | bytes 1336116 | tf_op jit(solution)/shard_map/vc,vd->cd/dot_general | solution.py:284
  (96 shorter events, 12.2 us)
Async XLA Ops:
  0.6 29.5 %copy-start = (bf16[1024,1024]{1,0:T(8,128)(2,1)S(1)}, bf16[1024,1024]{1,0:T(8,128)(2,1)}, u32[]{:S(2)}) copy-start(bf16[1024,1024]{1,0:T(8,128)(2,1)} %param.13) | copy-start | bytes 6291460
  2.5 11.8 %all-to-all-start = ((bf16[4,64,768]{2,1,0:T(8,128)(2,1)}), bf16[4,64,768]{2,1,0:T(8,128)(2,1)S(1)}, u32[]{:S(2)}, u32[]{:S(2)}) async-start(bf16[4,64,768]{2,1,0:T(8,128)(2,1)} %broadcast_in_dim.44), calls=%async_computation | async-start | bytes 786432 | tf_op jit(solution)/shard_map/all_to_all | solution.py:186
  9.0 28.2 %copy-start.16 = (s32[51]{0:T(128)}, s32[51]{0:T(128)S(1)}, u32[]{:S(2)}) copy-start(s32[51]{0:T(128)S(1)} %dynamic-slice_bitcast_fusion) | copy-start | bytes 616
  11.8 25.4 %copy-start.18 = (pred[256]{0:T(512)(128)(4,1)}, pred[256]{0:T(512)(128)(4,1)S(1)}, u32[]{:S(2)}) copy-start(pred[256]{0:T(512)(128)(4,1)S(1)} %broadcast_compare_fusion) | copy-start | bytes 772
  14.3 8.3 %copy-start.11 = (bf16[4,64,768]{2,1,0:T(8,128)(2,1)}, bf16[4,64,768]{2,1,0:T(8,128)(2,1)S(1)}, u32[]{:S(2)}) copy-start(bf16[4,64,768]{2,1,0:T(8,128)(2,1)S(1)} %all-to-all-done) | copy-start | bytes 1179652
  25.2 2.8 %copy-start.1 = (bf16[256,3072]{0,1:T(8,128)(2,1)S(1)}, bf16[256,3072]{0,1:T(8,128)(2,1)}, u32[]{:S(2)}) copy-start(bf16[256,3072]{0,1:T(8,128)(2,1)} %copy.63) | copy-start | bytes 4718596
  32.7 0.7 copy-start.5
  32.7 1.2 %copy-start.7 = (bf16[51,1,16,64]{3,2,1,0:T(8,128)(2,1)}, bf16[51,1,16,64]{3,2,1,0:T(8,128)(2,1)S(1)}, u32[]{:S(2)}) copy-start(bf16[51,1,16,64]{3,2,1,0:T(8,128)(2,1)S(1)} %get-tuple-element.18) | copy-start | bytes 313348
  32.7 1.2 %copy-start.9 = (bf16[51,1,16,64]{3,2,1,0:T(8,128)(2,1)}, bf16[51,1,16,64]{3,2,1,0:T(8,128)(2,1)S(1)}, u32[]{:S(2)}) copy-start(bf16[51,1,16,64]{3,2,1,0:T(8,128)(2,1)S(1)} %get-tuple-element.17) | copy-start | bytes 313348
  34.0 0.8 copy-start.12
  34.0 1.0 %copy-start.14 = (f32[16,51]{1,0:T(8,128)}, f32[16,51]{1,0:T(8,128)S(1)}, u32[]{:S(2)}) copy-start(f32[16,51]{1,0:T(8,128)S(1)} %get-tuple-element.23) | copy-start | bytes 9796
  41.7 0.9 %copy-start.2 = (f32[16,256,48]{1,2,0:T(8,128)}, f32[16,256,48]{1,2,0:T(8,128)S(1)}, u32[]{:S(2)}) copy-start(f32[16,256,48]{1,2,0:T(8,128)S(1)} %get-tuple-element.26) | copy-start | bytes 2359300
  50.5 2.0 %copy-start.3 = (f32[256,768]{1,0:T(8,128)S(1)}, f32[256,768]{1,0:T(8,128)}, u32[]{:S(2)}) copy-start(f32[256,768]{1,0:T(8,128)} %get-tuple-element.15) | copy-start | bytes 2359300
  50.5 2.0 %copy-start.4 = (bf16[256,768]{1,0:T(8,128)(2,1)S(1)}, bf16[256,768]{1,0:T(8,128)(2,1)}, u32[]{:S(2)}) copy-start(bf16[256,768]{1,0:T(8,128)(2,1)} %get-tuple-element.4) | copy-start | bytes 1179652
  53.4 3.9 %copy-start.15 = (f32[16,51]{1,0:T(8,128)S(1)}, f32[16,51]{1,0:T(8,128)}, u32[]{:S(2)}) copy-start(f32[16,51]{1,0:T(8,128)} %copy-done.14) | copy-start | bytes 9796
  60.0 2.4 %copy-start.10 = (bf16[51,1,16,64]{3,2,1,0:T(8,128)(2,1)S(1)}, bf16[51,1,16,64]{3,2,1,0:T(8,128)(2,1)}, u32[]{:S(2)}) copy-start(bf16[51,1,16,64]{3,2,1,0:T(8,128)(2,1)} %copy-done.9) | copy-start | bytes 313348
  60.8 1.9 %copy-start.6 = (bf16[51,1,16,64]{3,2,1,0:T(8,128)(2,1)S(1)}, bf16[51,1,16,64]{3,2,1,0:T(8,128)(2,1)}, u32[]{:S(2)}) copy-start(bf16[51,1,16,64]{3,2,1,0:T(8,128)(2,1)} %copy-done.5) | copy-start | bytes 313348
  60.8 1.9 %copy-start.8 = (bf16[51,1,16,64]{3,2,1,0:T(8,128)(2,1)S(1)}, bf16[51,1,16,64]{3,2,1,0:T(8,128)(2,1)}, u32[]{:S(2)}) copy-start(bf16[51,1,16,64]{3,2,1,0:T(8,128)(2,1)} %copy-done.7) | copy-start | bytes 313348
  61.0 1.4 %copy-start.13 = (f32[16,51,51]{1,2,0:T(8,128)S(1)}, f32[16,51,51]{1,2,0:T(8,128)}, u32[]{:S(2)}) copy-start(f32[16,51,51]{1,2,0:T(8,128)} %copy-done.12) | copy-start | bytes 499396
  64.1 1.1 %copy-start.19 = (f32[51]{0:T(128)S(1)}, f32[51]{0:T(128)}, u32[]{:S(2)}) copy-start(f32[51]{0:T(128)} %get-tuple-element.31) | copy-start | bytes 616
  70.1 4.7 %copy-start.17 = (s32[4,51]{1,0:T(4,128)S(1)}, s32[4,51]{1,0:T(4,128)}, u32[]{:S(2)}) copy-start(s32[4,51]{1,0:T(4,128)} %param.10) | copy-start | bytes 2452
  71.3 9.9 %all-to-all-start.1 = ((bf16[4,51,1024]{2,1,0:T(8,128)(2,1)}), bf16[4,51,1024]{2,1,0:T(8,128)(2,1)S(1)}, u32[]{:S(2)}, u32[]{:S(2)}) async-start(bf16[4,51,1024]{2,1,0:T(8,128)(2,1)} %broadcast_in_dim.101), calls=%async_computation.1 | async-start | bytes 917504 | tf_op jit(solution)/shard_map/all_to_all | solution.py:186

commit v18 on v16

--- a/solution.py
+++ b/solution.py
@@ -71,8 +71,12 @@
 
 def reuse_rows_bwd(saved, cotangent):
     inputs, w_qkv = saved
-    _, pullback = jax.vjp(lambda rows: project_rows(rows, w_qkv), inputs)
-    (d_inputs,) = pullback(cotangent)
+    _, pullback = jax.vjp(
+        lambda rows: row_norm(rows.astype(jnp.float32)).astype(jnp.bfloat16), inputs
+    )
+    d_normed = jnp.dot(cotangent, w_qkv.T, preferred_element_type=jnp.float32)
+    d_normed = lax.optimization_barrier(d_normed.astype(jnp.bfloat16))
+    (d_inputs,) = pullback(d_normed)
     return d_inputs, jnp.zeros_like(w_qkv), jnp.zeros_like(cotangent)
 
 

time: 78.8 us -> 78.9 us (level)
  no operation moved by 1% of the time
where the time goes in v18:
time: 78.9 us; the launch traced here: 78.3 us
  matrix products  35.6 us (45%)
  local copies, waits for them, and re-layouts  11.5 us (15%)
  other arithmetic  11.5 us (15%)
  starting transfers between devices  8.15 us (10%)
  waiting for transfers between devices  4.87 us (6%)
  Pallas kernels  3.54 us (4%)
  between operations  3.16 us (4%)
    ppermute x6, starting transfers between devices, ring_gather(): parts.append(lax.ppermute(values, 'mask', pairs))  8.15 us
    dot_general x6, matrix products, decoder_output(): jnp.einsum('pgi,gio->pgo', padded[offset:offset + total_rows], conv_w[off...  7.63 us
    dot_general x1, matrix products, copy_terms(): branch = attention_from(reuse_rows(visible_in, w_qkv, projected), w_out)  4.89 us
    ppermute x6, waiting for transfers between devices, ring_gather(): parts.append(lax.ppermute(values, 'mask', pairs))  4.87 us
    dot_general x2, matrix products, decoder_output(): jnp.dot(visible_out, dec_in, preferred_element_type=jnp.float32)  4.38 us
    pallas_call x1, Pallas kernels, masked_squares(): pl.pallas_call(functools.partial(loss_kernel, scale=scale), out_shape=(ja...  3.54 us
    dot_general x1, matrix products, project_rows(): jnp.dot(normed, w_qkv, preferred_element_type=jnp.float32)  3.1 us
    convert_element_type x1, other arithmetic, decoder_output(): return (lowered.astype(jnp.float32) + activated).astype(jnp.bfloat16)  2.97 us
  transfers between devices with their start and end apart: 6, of which 3 were waited for; matrix products, arithmetic and copies ran while one was open for 8% of the time, Pallas kernels for 0%

profile of v18, /device:TPU:0, one launch (start us, length us, event | category | flops | bytes accessed | tf_op | source)
XLA Modules:
  0.0 78.3 jit_solution(2270507882491561907)
XLA Ops:
  0.6 3.0 %collective-permute-start = (bf16[64,768]{1,0:T(8,128)(2,1)}, bf16[64,768]{1,0:T(8,128)(2,1)S(1)}, u32[]{:S(2)}, u32[]{:S(2)}) collective-permute-start(bf16[64,768]{1,0:T(8,128)(2,1)} %param.9), channel_id=1, source_target_pairs={{0,1},{1,2},{2,3},{3,0},{4,5},{5,6},{6,7},{7,4},{8,9},{9,10},{10,1... | collective-permute-start | bytes 294920 | tf_op jit(solution)/shard_map/ppermute | solution.py:192
  3.7 1.5 %collective-permute-start.1 = (bf16[64,768]{1,0:T(8,128)(2,1)}, bf16[64,768]{1,0:T(8,128)(2,1)S(1)}, u32[]{:S(2)}, u32[]{:S(2)}) collective-permute-start(bf16[64,768]{1,0:T(8,128)(2,1)} %param.9), channel_id=1, source_target_pairs={{0,2},{1,3},{2,0},{3,1},{4,6},{5,7},{6,4},{7,5},{8,10},{9,11},{10,... | collective-permute-start | bytes 294920 | tf_op jit(solution)/shard_map/ppermute | solution.py:192
  5.2 1.4 %collective-permute-start.2 = (bf16[64,768]{1,0:T(8,128)(2,1)}, bf16[64,768]{1,0:T(8,128)(2,1)S(1)}, u32[]{:S(2)}, u32[]{:S(2)}) collective-permute-start(bf16[64,768]{1,0:T(8,128)(2,1)} %param.9), channel_id=1, source_target_pairs={{0,3},{1,0},{2,1},{3,2},{4,7},{5,4},{6,5},{7,6},{8,11},{9,8},{10,9... | collective-permute-start | bytes 294920 | tf_op jit(solution)/shard_map/ppermute | solution.py:192
  9.0 1.2 %gather_fusion = s32[4,51]{1,0:T(4,128)S(1)} fusion(s32[4,51]{1,0:T(4,128)} %param.10, s32[1024]{0:T(1024)S(1)} %pad_clamp_fusion), kind=kCustom, calls=%fused_computation | custom fusion | bytes 1648 | tf_op jit(solution)/shard_map/gather | solution.py:277
  10.9 1.9 %convolution_reduce_fusion = bf16[768]{0:T(1024)(128)(2,1)S(1)} fusion(bf16[1024,1]{0,1:T(2,128)(2,1)S(1)} %reshape.279, bf16[1024,768]{1,0:T(8,128)(2,1)} %param.15), kind=kOutput, calls=%fused_computation.54 | convolution fusion | flops 1572864 | bytes 1576448 | tf_op jit(solution)/shard_map/jvp()/dot_general | solution.py:93
  12.9 1.3 %select_select_fusion.3 = (bf16[64,768]{1,0:T(8,128)(2,1)S(1)}, bf16[64,768]{1,0:T(8,128)(2,1)S(1)}, bf16[64,768]{1,0:T(8,128)(2,1)S(1)}, bf16[64,768]{1,0:T(8,128)(2,1)S(1)}) fusion(bf16[64,768]{1,0:T(8,128)(2,1)S(1)} %collective-permute-done, bf16[64,768]{1,0:T(8,128)(2,1)S(1)} %collective-permute-done.1, bf16[64,768]{1,0:T(8,128)(2,1)S(1)} %collective-permute-done.2, ...), kind=kLoop, calls=%fused_computation.173 | loop fusion | flops 589824 | bytes 786444 | tf_op jit(solution)/shard_map/jit(_where)/select_n | solution.py:203
  14.2 2.2 %convert_reduce_fusion = (f32[256]{0:T(256)S(1)}, bf16[256,1024]{1,0:T(8,128)(2,1)S(1)}) fusion(bf16[768,1024]{1,0:T(8,128)(2,1)} %param.11, bf16[64,768]{1,0:T(8,128)(2,1)S(1)} %get-tuple-element.18, bf16[64,768]{1,0:T(8,128)(2,1)S(1)} %get-tuple-element.19, bf16[64,768]{1,0:T(8,128)(2,1)S(1)} %get-tuple-element.20, bf16[64,768]{1,0:T(8,128)(2,1)S(1)} %get-tuple-element.17), kind=kOutput, calls=%fused_computation.12 | convolution fusion | flops 405012224 | bytes 2491392 | tf_op jit(solution)/shard_map/dot_general | solution.py:238
  16.8 3.1 %convolution_convert_fusion = bf16[256,3072]{1,0:T(8,128)(2,1)} fusion(bf16[1024,3072]{1,0:T(8,128)(2,1)S(1)} %copy-done.4, bf16[256,1024]{1,0:T(8,128)(2,1)S(1)} %get-tuple-element.24, f32[256]{0:T(256)S(1)} %add_rsqrt_fusion.3, f32[256]{0:T(256)S(1)} %broadcast_multiply_fusion.2), kind=kOutput, calls=%fused_computation.3 | convolution fusion | flops 1612447744 | bytes 8390656 | tf_op jit(solution)/shard_map/dot_general | solution.py:50
  19.8 2.6 %copy.63 = bf16[256,3072]{0,1:T(8,128)(2,1)} copy(bf16[256,3072]{1,0:T(8,128)(2,1)} %convolution_convert_fusion) | data formatting | bytes 3145728 | tf_op jit(solution)/shard_map/convert_element_type | solution.py:50
  22.4 1.9 %convolution_convert_fusion.1 = bf16[51,3072]{1,0:T(8,128)(2,1)S(1)} fusion(bf16[256,3072]{1,0:T(8,128)(2,1)} %convolution_convert_fusion, s32[51]{0:T(128)S(1)} %dynamic-slice_bitcast_fusion), kind=kOutput, calls=%fused_computation.5 | convolution fusion | flops 80385792 | bytes 1886412 | tf_op jit(solution)/shard_map/dot_general | solution.py:249
  24.4 0.9 %fusion.130 = (f32[51]{0:T(128)}, f32[51,1024]{1,0:T(8,128)S(1)}) fusion(bf16[256,1024]{1,0:T(8,128)(2,1)S(1)} %get-tuple-element.24, s32[51]{0:T(128)S(1)} %dynamic-slice_bitcast_fusion), kind=kOutput, calls=%fused_computation.229 | convolution fusion | flops 26908364 | bytes 733592 | tf_op jit(solution)/shard_map/dot_general | solution.py:243
  25.5 1.0 %fusion = (f32[16,256]{1,0:T(8,128)S(1)}, f32[16,256,256]{1,2,0:T(8,128)S(1)}) fusion(f32[256,16]{0,1:T(8,128)S(1)} %get-tuple-element.43, bf16[256,3,16,64]{0,3,2,1:T(8,128)(2,1)S(1)} %bitcast.164, f32[256,16]{0,1:T(8,128)S(1)} %get-tuple-element.44), kind=kOutput, calls=%fused_computation.4 | convolution fusion | flops 137883648 | bytes 5292032 | tf_op jit(solution)/shard_map/qhd,khd->hqk/dot_general | solution.py:33
  28.5 1.0 %multiply_convert_fusion.targets_ref = bf16[256,1024]{1,0:T(8,128)(2,1)} fusion(f32[256,1024]{1,0:T(8,128)S(1)} %get-tuple-element.32, f32[256]{0:T(256)S(1)} %add_rsqrt_fusion.2, f32[256]{0:T(256)S(1)} %broadcast_multiply_fusion.1), kind=kLoop, calls=%fused_computation.61 | loop fusion | flops 786432 | bytes 1574912 | tf_op jit(solution)/shard_map/convert_element_type | solution.py:255
  32.2 2.2 %convolution_convert_fusion.17 = bf16[51,768]{1,0:T(8,128)(2,1)S(1)} fusion(bf16[1024,768]{1,0:T(8,128)(2,1)} %param.15, f32[51,1024]{1,0:T(8,128)S(1)} %get-tuple-element.34, bf16[51,1024]{1,0:T(8,128)(2,1)S(1)} %reshape.257, bf16[1024,1024]{1,0:T(8,128)(2,1)S(1)} %copy-done), kind=kOutput, calls=%fused_computation.52 | convolution fusion | flops 187314432 | bytes 4061696 | tf_op jit(solution)/shard_map/jvp()/dot_general | solution.py:90
  35.0 1.3 %fusion.67 = f32[16,256,48]{1,2,0:T(8,128)S(1)} fusion(bf16[256,16,48]{0,2,1:T(8,128)(2,1)S(1)} %bitcast.170, bf16[3,16,48,48]{3,2,1,0:T(8,128)(2,1)} %param.16), kind=kOutput, calls=%fused_computation.131 | convolution fusion | flops 18874368 | bytes 1376256 | tf_op jit(solution)/shard_map/jvp(pgi,gio->pgo)/dot_general | solution.py:102
  36.3 1.2 %convolution_add_fusion.1 = f32[16,256,48]{1,2,0:T(8,128)S(1)} fusion(f32[16,256,48]{1,2,0:T(8,128)S(1)} %fusion.67, bf16[256,16,48]{0,2,1:T(8,128)(2,1)S(1)} %bitcast.171, bf16[3,16,48,48]{3,2,1,0:T(8,128)(2,1)} %param.16), kind=kOutput, calls=%fused_computation.15 | convolution fusion | flops 19070976 | bytes 2162688 | tf_op jit(solution)/shard_map/jvp(pgi,gio->pgo)/dot_general | solution.py:102
  37.6 1.4 %fusion.128 = (f32[256]{0:T(256)S(1)}, f32[16,256,48]{1,2,0:T(8,128)S(1)}) fusion(f32[16,256,48]{1,2,0:T(8,128)S(1)} %convolution_add_fusion.1, bf16[256,16,48]{0,2,1:T(8,128)(2,1)S(1)} %bitcast.172, bf16[3,16,48,48]{3,2,1,0:T(8,128)(2,1)} %param.16), kind=kOutput, calls=%fused_computation.227 | convolution fusion | flops 19267328 | bytes 2163712 | tf_op jit(solution)/shard_map/jvp(pgi,gio->pgo)/dot_general | solution.py:102
  39.8 1.4 %copy.62 = f32[256,768]{1,0:T(8,128)S(1)} copy(f32[256,768]{0,1:T(8,128)} %bitcast.166) | data formatting | bytes 1572864 | tf_op jit(solution)/shard_map/jvp()/reshape | solution.py:108
  41.2 3.0 %add_convert_fusion = (bf16[256,768]{1,0:T(8,128)(2,1)}, f32[256,768]{1,0:T(8,128)}) fusion(bf16[256,768]{1,0:T(8,128)(2,1)S(1)} %fusion.3, f32[256,768]{1,0:T(8,128)S(1)} %copy.62, f32[256]{0:T(256)S(1)} %fusion.111, f32[256]{0:T(256)S(1)} %broadcast_multiply_fusion), kind=kLoop, calls=%fused_computation.86 | loop fusion | flops 13565952 | bytes 2361344 | tf_op jit(solution)/shard_map/jvp()/convert_element_type | solution.py:109
  44.2 3.5 %jvp__.1 = (f32[1,1]{1,0:T(1,128)}, bf16[256,768]{1,0:T(8,128)(2,1)}) custom-call(bf16[256,768]{1,0:T(8,128)(2,1)} %get-tuple-element.12.hidden_ref, bf16[768,1024]{1,0:T(8,128)(2,1)} %dec_out_ref.1, bf16[256,1024]{1,0:T(8,128)(2,1)} %multiply_convert_fusion.targets_ref, f32[256,1]{1,0:T(8,128)} %copy.65.keep_ref), custom_call_target="tpu_custom_call" | custom-call | tf_op jit(solution)/shard_map/jvp()/pallas_call | solution.py:128
  47.7 2.0 %multiply_reduce_fusion.1 = f32[256]{0:T(256)S(1)} fusion(f32[256,768]{1,0:T(8,128)S(1)} %copy.62, f32[256]{0:T(256)S(1)} %broadcast_multiply_fusion, f32[256,768]{1,0:T(8,128)} %get-tuple-element.13, bf16[256,768]{1,0:T(8,128)(2,1)} %get-tuple-element.4, f32[256]{0:T(256)S(1)} %fusion.111), kind=kLoop, calls=%fused_computation.85 | loop fusion | flops 3538688 | bytes 1969152 | tf_op jit(solution)/shard_map/transpose(jvp())/reduce_sum | solution.py:23
  50.8 1.4 %fusion.7 = bf16[256,16,48]{0,2,1:T(8,128)(2,1)S(1)} fusion(bf16[16,48,256]{2,1,0:T(8,128)(2,1)S(1)} %bitcast.167, bf16[3,16,48,48]{3,2,1,0:T(8,128)(2,1)} %param.16), kind=kOutput, calls=%fused_computation.26 | convolution fusion | flops 18874368 | bytes 983040 | tf_op jit(solution)/shard_map/transpose(jvp(pgi,gio->pgo))/dot_general | solution.py:102
  52.2 1.2 %fusion.8 = bf16[256,16,48]{0,2,1:T(8,128)(2,1)S(1)} fusion(bf16[16,48,256]{2,1,0:T(8,128)(2,1)S(1)} %bitcast.168, bf16[3,16,48,48]{3,2,1,0:T(8,128)(2,1)} %param.16), kind=kOutput, calls=%fused_computation.27 | convolution fusion | flops 18874368 | bytes 983040 | tf_op jit(solution)/shard_map/transpose(jvp(pgi,gio->pgo))/dot_general | solution.py:102
  53.4 1.2 %fusion.9 = bf16[256,16,48]{0,2,1:T(8,128)(2,1)S(1)} fusion(bf16[16,48,256]{2,1,0:T(8,128)(2,1)S(1)} %bitcast.169, bf16[3,16,48,48]{3,2,1,0:T(8,128)(2,1)} %param.16), kind=kOutput, calls=%fused_computation.28 | convolution fusion | flops 18874368 | bytes 983040 | tf_op jit(solution)/shard_map/transpose(jvp(pgi,gio->pgo))/dot_general | solution.py:102
  55.1 2.2 %convolution_convert_fusion.12 = bf16[51,1024]{1,0:T(8,128)(2,1)S(1)} fusion(bf16[1024,768]{1,0:T(8,128)(2,1)} %param.15, bf16[256,768]{1,0:T(8,128)(2,1)S(1)} %copy-done.5, bf16[256,768]{1,0:T(8,128)(2,1)S(1)} %copy.70, pred[256]{0:T(512)(128)(4,1)} %copy-done.26, s32[51]{0:T(128)} %copy-done.24), kind=kOutput, calls=%fused_computation.46 | convolution fusion | flops 100964352 | bytes 2464204 | tf_op jit(solution)/shard_map/transpose(jvp())/dot_general | solution.py:90
  58.2 1.4 %fusion.16 = bf16[51,1,16,64]{3,0,2,1:T(8,128)(2,1)S(1)} fusion(bf16[51,16,64]{2,1,0:T(8,128)(2,1)S(1)} %reshape.264, f32[16,51,51]{1,2,0:T(8,128)} %copy-done.12, f32[16,51]{1,0:T(8,128)S(1)} %copy-done.23), kind=kOutput, calls=%fused_computation.42 | convolution fusion | flops 5462304 | bytes 378624 | tf_op jit(solution)/shard_map/transpose(jvp(hqk,khd->qhd))/dot_general | solution.py:38
  62.4 4.9 %convolution_convert_fusion.11 = bf16[51,1024]{1,0:T(8,128)(2,1)S(1)} fusion(bf16[51,3072]{1,0:T(8,128)(2,1)S(1)} %reshape.265, bf16[1024,3072]{1,0:T(8,128)(2,1)} %param.12), kind=kOutput, calls=%fused_computation.45 | convolution fusion | flops 320916480 | bytes 6709248 | tf_op jit(solution)/shard_map/transpose(jvp())/dot_general | solution.py:178
  68.6 1.5 %collective-permute-start.4 = (bf16[51,1024]{1,0:T(8,128)(2,1)S(1)}, bf16[51,1024]{1,0:T(8,128)(2,1)S(1)}, u32[]{:S(2)}, u32[]{:S(2)}) collective-permute-start(bf16[51,1024]{1,0:T(8,128)(2,1)S(1)} %fusion.99), channel_id=1, source_target_pairs={{0,2},{1,3},{2,0},{3,1},{4,6},{5,7},{6,4},{7,5},{8,10},{9,11},{10,... | collective-permute-start | bytes 313352 | tf_op jit(solution)/shard_map/ppermute | solution.py:192
  70.9 2.6 %collective-permute-done.3 = bf16[51,1024]{1,0:T(8,128)(2,1)S(1)} collective-permute-done((bf16[51,1024]{1,0:T(8,128)(2,1)S(1)}, bf16[51,1024]{1,0:T(8,128)(2,1)S(1)}, u32[]{:S(2)}, u32[]{:S(2)}) %collective-permute-start.3) | collective-permute-done | bytes 104480 | tf_op jit(solution)/shard_map/ppermute | solution.py:192
  73.5 1.0 %collective-permute-done.4 = bf16[51,1024]{1,0:T(8,128)(2,1)S(1)} collective-permute-done((bf16[51,1024]{1,0:T(8,128)(2,1)S(1)}, bf16[51,1024]{1,0:T(8,128)(2,1)S(1)}, u32[]{:S(2)}, u32[]{:S(2)}) %collective-permute-start.4) | collective-permute-done | bytes 104480 | tf_op jit(solution)/shard_map/ppermute | solution.py:192
  74.5 1.3 %collective-permute-done.5 = bf16[51,1024]{1,0:T(8,128)(2,1)S(1)} collective-permute-done((bf16[51,1024]{1,0:T(8,128)(2,1)S(1)}, bf16[51,1024]{1,0:T(8,128)(2,1)S(1)}, u32[]{:S(2)}, u32[]{:S(2)}) %collective-permute-start.5) | collective-permute-done | bytes 104480 | tf_op jit(solution)/shard_map/ppermute | solution.py:192
  75.8 1.4 %fusion.19 = f32[192,1024]{1,0:T(8,128)} fusion(bf16[51,1024]{1,0:T(8,128)(2,1)S(1)} %collective-permute-done.5, bf16[51,1024]{1,0:T(8,128)(2,1)S(1)} %collective-permute-done.4, bf16[51,1024]{1,0:T(8,128)(2,1)S(1)} %collective-permute-done.3, bf16[51,1024]{1,0:T(8,128)(2,1)S(1)} %fusion.99, bf16[256,768]{1,0:T(8,128)(2,1)S(1)} %pad_maximum_fusion, ...), kind=kOutput, calls=%fused_computation.53 | convolution fusion | flops 102032640 | bytes 1377284 | tf_op jit(solution)/shard_map/vc,vd->cd/dot_general | solution.py:283
  (123 shorter events, 16.2 us)
Async XLA Ops:
  0.6 26.7 %copy-start = (bf16[1024,1024]{1,0:T(8,128)(2,1)S(1)}, bf16[1024,1024]{1,0:T(8,128)(2,1)}, u32[]{:S(2)}) copy-start(bf16[1024,1024]{1,0:T(8,128)(2,1)} %param.13) | copy-start | bytes 6291460
  0.6 12.2 %collective-permute-start = (bf16[64,768]{1,0:T(8,128)(2,1)}, bf16[64,768]{1,0:T(8,128)(2,1)S(1)}, u32[]{:S(2)}, u32[]{:S(2)}) collective-permute-start(bf16[64,768]{1,0:T(8,128)(2,1)} %param.9), channel_id=1, source_target_pairs={{0,1},{1,2},{2,3},{3,0},{4,5},{5,6},{6,7},{7,4},{8,9},{9,10},{10,1... | collective-permute-start | bytes 294920 | tf_op jit(solution)/shard_map/ppermute | solution.py:192
  3.7 9.2 %collective-permute-start.1 = (bf16[64,768]{1,0:T(8,128)(2,1)}, bf16[64,768]{1,0:T(8,128)(2,1)S(1)}, u32[]{:S(2)}, u32[]{:S(2)}) collective-permute-start(bf16[64,768]{1,0:T(8,128)(2,1)} %param.9), channel_id=1, source_target_pairs={{0,2},{1,3},{2,0},{3,1},{4,6},{5,7},{6,4},{7,5},{8,10},{9,11},{10,... | collective-permute-start | bytes 294920 | tf_op jit(solution)/shard_map/ppermute | solution.py:192
  5.2 7.7 %collective-permute-start.2 = (bf16[64,768]{1,0:T(8,128)(2,1)}, bf16[64,768]{1,0:T(8,128)(2,1)S(1)}, u32[]{:S(2)}, u32[]{:S(2)}) collective-permute-start(bf16[64,768]{1,0:T(8,128)(2,1)} %param.9), channel_id=1, source_target_pairs={{0,3},{1,0},{2,1},{3,2},{4,7},{5,4},{6,5},{7,6},{8,11},{9,8},{10,9... | collective-permute-start | bytes 294920 | tf_op jit(solution)/shard_map/ppermute | solution.py:192
  7.3 27.1 %copy-start.24 = (s32[51]{0:T(128)}, s32[51]{0:T(128)S(1)}, u32[]{:S(2)}) copy-start(s32[51]{0:T(128)S(1)} %dynamic-slice_bitcast_fusion) | copy-start | bytes 616
  7.5 26.9 %copy-start.26 = (pred[256]{0:T(512)(128)(4,1)}, pred[256]{0:T(512)(128)(4,1)S(1)}, u32[]{:S(2)}) copy-start(pred[256]{0:T(512)(128)(4,1)S(1)} %broadcast_compare_fusion) | copy-start | bytes 772
  10.9 5.8 %copy-start.4 = (bf16[1024,3072]{1,0:T(8,128)(2,1)S(1)}, bf16[1024,3072]{1,0:T(8,128)(2,1)}, u32[]{:S(2)}) copy-start(bf16[1024,3072]{1,0:T(8,128)(2,1)} %param.12) | copy-start | bytes 18874372
  14.2 2.5 %copy-start.14 = (bf16[64,768]{1,0:T(8,128)(2,1)}, bf16[64,768]{1,0:T(8,128)(2,1)S(1)}, u32[]{:S(2)}) copy-start(bf16[64,768]{1,0:T(8,128)(2,1)S(1)} %get-tuple-element.17) | copy-start | bytes 294916
  14.2 2.5 %copy-start.16 = (bf16[64,768]{1,0:T(8,128)(2,1)}, bf16[64,768]{1,0:T(8,128)(2,1)S(1)}, u32[]{:S(2)}) copy-start(bf16[64,768]{1,0:T(8,128)(2,1)S(1)} %get-tuple-element.18) | copy-start | bytes 294916
  14.2 2.5 %copy-start.18 = (bf16[64,768]{1,0:T(8,128)(2,1)}, bf16[64,768]{1,0:T(8,128)(2,1)S(1)}, u32[]{:S(2)}) copy-start(bf16[64,768]{1,0:T(8,128)(2,1)S(1)} %get-tuple-element.19) | copy-start | bytes 294916
  14.2 2.5 %copy-start.20 = (bf16[64,768]{1,0:T(8,128)(2,1)}, bf16[64,768]{1,0:T(8,128)(2,1)S(1)}, u32[]{:S(2)}) copy-start(bf16[64,768]{1,0:T(8,128)(2,1)S(1)} %get-tuple-element.20) | copy-start | bytes 294916
  22.4 2.8 %copy-start.1 = (bf16[256,3072]{0,1:T(8,128)(2,1)S(1)}, bf16[256,3072]{0,1:T(8,128)(2,1)}, u32[]{:S(2)}) copy-start(bf16[256,3072]{0,1:T(8,128)(2,1)} %copy.63) | copy-start | bytes 4718596
  30.0 1.2 %copy-start.8 = (bf16[51,1,16,64]{3,2,1,0:T(8,128)(2,1)}, bf16[51,1,16,64]{3,2,1,0:T(8,128)(2,1)S(1)}, u32[]{:S(2)}) copy-start(bf16[51,1,16,64]{3,2,1,0:T(8,128)(2,1)S(1)} %get-tuple-element.16) | copy-start | bytes 313348
  30.0 1.2 %copy-start.10 = (bf16[51,1,16,64]{3,2,1,0:T(8,128)(2,1)}, bf16[51,1,16,64]{3,2,1,0:T(8,128)(2,1)S(1)}, u32[]{:S(2)}) copy-start(bf16[51,1,16,64]{3,2,1,0:T(8,128)(2,1)S(1)} %get-tuple-element.15) | copy-start | bytes 313348
  31.2 1.0 %copy-start.22 = (f32[16,51]{1,0:T(8,128)}, f32[16,51]{1,0:T(8,128)S(1)}, u32[]{:S(2)}) copy-start(f32[16,51]{1,0:T(8,128)S(1)} %get-tuple-element.25) | copy-start | bytes 9796
  38.9 0.9 %copy-start.2 = (f32[16,256,48]{1,2,0:T(8,128)}, f32[16,256,48]{1,2,0:T(8,128)S(1)}, u32[]{:S(2)}) copy-start(f32[16,256,48]{1,2,0:T(8,128)S(1)} %get-tuple-element.28) | copy-start | bytes 2359300
  47.7 2.0 %copy-start.3 = (f32[256,768]{1,0:T(8,128)S(1)}, f32[256,768]{1,0:T(8,128)}, u32[]{:S(2)}) copy-start(f32[256,768]{1,0:T(8,128)} %get-tuple-element.13) | copy-start | bytes 2359300
  47.7 2.0 %copy-start.5 = (bf16[256,768]{1,0:T(8,128)(2,1)S(1)}, bf16[256,768]{1,0:T(8,128)(2,1)}, u32[]{:S(2)}) copy-start(bf16[256,768]{1,0:T(8,128)(2,1)} %get-tuple-element.4) | copy-start | bytes 1179652
  50.6 3.9 %copy-start.23 = (f32[16,51]{1,0:T(8,128)S(1)}, f32[16,51]{1,0:T(8,128)}, u32[]{:S(2)}) copy-start(f32[16,51]{1,0:T(8,128)} %copy-done.22) | copy-start | bytes 9796
  57.3 2.4 %copy-start.11 = (bf16[51,1,16,64]{3,2,1,0:T(8,128)(2,1)S(1)}, bf16[51,1,16,64]{3,2,1,0:T(8,128)(2,1)}, u32[]{:S(2)}) copy-start(bf16[51,1,16,64]{3,2,1,0:T(8,128)(2,1)} %copy-done.10) | copy-start | bytes 313348
  58.0 1.9 %copy-start.7 = (bf16[51,1,16,64]{3,2,1,0:T(8,128)(2,1)S(1)}, bf16[51,1,16,64]{3,2,1,0:T(8,128)(2,1)}, u32[]{:S(2)}) copy-start(bf16[51,1,16,64]{3,2,1,0:T(8,128)(2,1)} %copy-done.6) | copy-start | bytes 313348
  58.0 1.9 %copy-start.9 = (bf16[51,1,16,64]{3,2,1,0:T(8,128)(2,1)S(1)}, bf16[51,1,16,64]{3,2,1,0:T(8,128)(2,1)}, u32[]{:S(2)}) copy-start(bf16[51,1,16,64]{3,2,1,0:T(8,128)(2,1)} %copy-done.8) | copy-start | bytes 313348
  58.2 1.4 %copy-start.13 = (f32[16,51,51]{1,2,0:T(8,128)S(1)}, f32[16,51,51]{1,2,0:T(8,128)}, u32[]{:S(2)}) copy-start(f32[16,51,51]{1,2,0:T(8,128)} %copy-done.12) | copy-start | bytes 499396
  62.4 5.0 %copy-start.27 = (f32[51]{0:T(128)S(1)}, f32[51]{0:T(128)}, u32[]{:S(2)}) copy-start(f32[51]{0:T(128)} %get-tuple-element.33) | copy-start | bytes 616
  62.4 8.5 %copy-start.15 = (bf16[64,768]{1,0:T(8,128)(2,1)S(1)}, bf16[64,768]{1,0:T(8,128)(2,1)}, u32[]{:S(2)}) copy-start(bf16[64,768]{1,0:T(8,128)(2,1)} %copy-done.14) | copy-start | bytes 294916
  62.4 8.5 %copy-start.17 = (bf16[64,768]{1,0:T(8,128)(2,1)S(1)}, bf16[64,768]{1,0:T(8,128)(2,1)}, u32[]{:S(2)}) copy-start(bf16[64,768]{1,0:T(8,128)(2,1)} %copy-done.16) | copy-start | bytes 294916
  62.4 8.5 %copy-start.19 = (bf16[64,768]{1,0:T(8,128)(2,1)S(1)}, bf16[64,768]{1,0:T(8,128)(2,1)}, u32[]{:S(2)}) copy-start(bf16[64,768]{1,0:T(8,128)(2,1)} %copy-done.18) | copy-start | bytes 294916
  62.4 8.5 %copy-start.21 = (bf16[64,768]{1,0:T(8,128)(2,1)S(1)}, bf16[64,768]{1,0:T(8,128)(2,1)}, u32[]{:S(2)}) copy-start(bf16[64,768]{1,0:T(8,128)(2,1)} %copy-done.20) | copy-start | bytes 294916
  62.4 13.4 %copy-start.25 = (s32[204]{0:T(256)S(1)}, s32[204]{0:T(256)}, u32[]{:S(2)}) copy-start(s32[204]{0:T(256)} %eq.93) | copy-start | bytes 2452
  68.0 5.5 %collective-permute-start.3 = (bf16[51,1024]{1,0:T(8,128)(2,1)S(1)}, bf16[51,1024]{1,0:T(8,128)(2,1)S(1)}, u32[]{:S(2)}, u32[]{:S(2)}) collective-permute-start(bf16[51,1024]{1,0:T(8,128)(2,1)S(1)} %fusion.99), channel_id=1, source_target_pairs={{0,3},{1,0},{2,1},{3,2},{4,7},{5,4},{6,5},{7,6},{8,11},{9,8},{10,9... | collective-permute-start | bytes 313352 | tf_op jit(solution)/shard_map/ppermute | solution.py:192
  68.6 6.0 %collective-permute-start.4 = (bf16[51,1024]{1,0:T(8,128)(2,1)S(1)}, bf16[51,1024]{1,0:T(8,128)(2,1)S(1)}, u32[]{:S(2)}, u32[]{:S(2)}) collective-permute-start(bf16[51,1024]{1,0:T(8,128)(2,1)S(1)} %fusion.99), channel_id=1, source_target_pairs={{0,2},{1,3},{2,0},{3,1},{4,6},{5,7},{6,4},{7,5},{8,10},{9,11},{10,... | collective-permute-start | bytes 313352 | tf_op jit(solution)/shard_map/ppermute | solution.py:192
  70.1 5.7 %collective-permute-start.5 = (bf16[51,1024]{1,0:T(8,128)(2,1)S(1)}, bf16[51,1024]{1,0:T(8,128)(2,1)S(1)}, u32[]{:S(2)}, u32[]{:S(2)}) collective-permute-start(bf16[51,1024]{1,0:T(8,128)(2,1)S(1)} %fusion.99), channel_id=1, source_target_pairs={{0,1},{1,2},{2,3},{3,0},{4,5},{5,6},{6,7},{7,4},{8,9},{9,10},{10,1... | collective-permute-start | bytes 313352 | tf_op jit(solution)/shard_map/ppermute | solution.py:192
  (2 other events, 1.5 us)

commit v19 on v18

--- a/solution.py
+++ b/solution.py
@@ -60,6 +60,40 @@
     return attention_from(project_rows(inputs, w_qkv), w_out)
 
 
+def transposed_product_kernel(rows_ref, weight_ref, out_ref):
+    step = pl.program_id(0)
+    part = lax.dot_general(
+        rows_ref[...],
+        weight_ref[...],
+        (((1,), (1,)), ((), ())),
+        preferred_element_type=jnp.float32,
+    )
+
+    @pl.when(step == 0)
+    def _():
+        out_ref[...] = part
+
+    @pl.when(step > 0)
+    def _():
+        out_ref[...] += part
+
+
+def transposed_product(rows, weight):
+    count, inner = rows.shape
+    outer = weight.shape[0]
+    block = 512 if inner % 512 == 0 else inner
+    return pl.pallas_call(
+        transposed_product_kernel,
+        grid=(inner // block,),
+        in_specs=[
+            pl.BlockSpec((count, block), lambda k: (0, k)),
+            pl.BlockSpec((outer, block), lambda k: (0, k)),
+        ],
+        out_specs=pl.BlockSpec((count, outer), lambda k: (0, 0)),
+        out_shape=jax.ShapeDtypeStruct((count, outer), jnp.float32),
+    )(rows, weight)
+
+
 @jax.custom_vjp
 def reuse_rows(inputs, w_qkv, projected):
     return projected
@@ -74,9 +108,8 @@
     _, pullback = jax.vjp(
         lambda rows: row_norm(rows.astype(jnp.float32)).astype(jnp.bfloat16), inputs
     )
-    d_normed = jnp.dot(cotangent, w_qkv.T, preferred_element_type=jnp.float32)
-    d_normed = lax.optimization_barrier(d_normed.astype(jnp.bfloat16))
-    (d_inputs,) = pullback(d_normed)
+    d_normed = transposed_product(cotangent, w_qkv)
+    (d_inputs,) = pullback(d_normed.astype(jnp.bfloat16))
     return d_inputs, jnp.zeros_like(w_qkv), jnp.zeros_like(cotangent)
 
 

time: 78.9 us -> 83.2 us (1.054)
  Pallas kernels: 3.54 us -> 10 us
  matrix products: 35.6 us -> 30.7 us
  other arithmetic: 11.5 us -> 13.3 us
    pallas_call x0 -> x1, Pallas kernels: none -> 6.5 us  [copy_terms(): branch = attention_from(reuse_rows(visible_in, w_qkv, projected), w_out)]
    dot_general x1 -> x0, matrix products: 4.89 us -> none  [copy_terms(): branch = attention_from(reuse_rows(visible_in, w_qkv, projected), w_out)]
    reduce_sum x2, other arithmetic: 0.44 us -> 2.32 us  [copy_terms(): branch = attention_from(reuse_rows(visible_in, w_qkv, projected), w_out)]
where the time goes in v19:
time: 83.2 us; the launch traced here: 82.5 us
  matrix products  30.7 us (37%)
  other arithmetic  13.3 us (16%)
  local copies, waits for them, and re-layouts  12.3 us (15%)
  Pallas kernels  10 us (12%)
  starting transfers between devices  8.15 us (10%)
  waiting for transfers between devices  4.87 us (6%)
  between operations  3.13 us (4%)
    ppermute x6, starting transfers between devices, ring_gather(): parts.append(lax.ppermute(values, 'mask', pairs))  8.15 us
    dot_general x6, matrix products, decoder_output(): jnp.einsum('pgi,gio->pgo', padded[offset:offset + total_rows], conv_w[off...  7.63 us
    pallas_call x1, Pallas kernels, copy_terms(): branch = attention_from(reuse_rows(visible_in, w_qkv, projected), w_out)  6.5 us
    ppermute x6, waiting for transfers between devices, ring_gather(): parts.append(lax.ppermute(values, 'mask', pairs))  4.87 us
    dot_general x2, matrix products, decoder_output(): jnp.dot(visible_out, dec_in, preferred_element_type=jnp.float32)  4.38 us
    pallas_call x1, Pallas kernels, masked_squares(): pl.pallas_call(functools.partial(loss_kernel, scale=scale), out_shape=(ja...  3.54 us
    dot_general x1, matrix products, project_rows(): jnp.dot(normed, w_qkv, preferred_element_type=jnp.float32)  3.1 us
    convert_element_type x1, other arithmetic, decoder_output(): return (lowered.astype(jnp.float32) + activated).astype(jnp.bfloat16)  2.97 us
  transfers between devices with their start and end apart: 6, of which 3 were waited for; matrix products, arithmetic and copies ran while one was open for 8% of the time, Pallas kernels for 0%

profile of v19, /device:TPU:0, one launch (start us, length us, event | category | flops | bytes accessed | tf_op | source)
XLA Modules:
  0.0 82.5 jit_solution(18265750071023603631)
XLA Ops:
  0.6 3.0 %collective-permute-start = (bf16[64,768]{1,0:T(8,128)(2,1)}, bf16[64,768]{1,0:T(8,128)(2,1)S(1)}, u32[]{:S(2)}, u32[]{:S(2)}) collective-permute-start(bf16[64,768]{1,0:T(8,128)(2,1)} %param.9), channel_id=1, source_target_pairs={{0,1},{1,2},{2,3},{3,0},{4,5},{5,6},{6,7},{7,4},{8,9},{9,10},{10,1... | collective-permute-start | bytes 294920 | tf_op jit(solution)/shard_map/ppermute | solution.py:225
  3.7 1.5 %collective-permute-start.1 = (bf16[64,768]{1,0:T(8,128)(2,1)}, bf16[64,768]{1,0:T(8,128)(2,1)S(1)}, u32[]{:S(2)}, u32[]{:S(2)}) collective-permute-start(bf16[64,768]{1,0:T(8,128)(2,1)} %param.9), channel_id=1, source_target_pairs={{0,2},{1,3},{2,0},{3,1},{4,6},{5,7},{6,4},{7,5},{8,10},{9,11},{10,... | collective-permute-start | bytes 294920 | tf_op jit(solution)/shard_map/ppermute | solution.py:225
  5.2 1.4 %collective-permute-start.2 = (bf16[64,768]{1,0:T(8,128)(2,1)}, bf16[64,768]{1,0:T(8,128)(2,1)S(1)}, u32[]{:S(2)}, u32[]{:S(2)}) collective-permute-start(bf16[64,768]{1,0:T(8,128)(2,1)} %param.9), channel_id=1, source_target_pairs={{0,3},{1,0},{2,1},{3,2},{4,7},{5,4},{6,5},{7,6},{8,11},{9,8},{10,9... | collective-permute-start | bytes 294920 | tf_op jit(solution)/shard_map/ppermute | solution.py:225
  9.0 1.2 %gather_fusion = s32[4,51]{1,0:T(4,128)S(1)} fusion(s32[4,51]{1,0:T(4,128)} %param.10, s32[1024]{0:T(1024)S(1)} %pad_clamp_fusion), kind=kCustom, calls=%fused_computation | custom fusion | bytes 1648 | tf_op jit(solution)/shard_map/gather | solution.py:310
  10.9 1.9 %convolution_reduce_fusion = bf16[768]{0:T(1024)(128)(2,1)S(1)} fusion(bf16[1024,1]{0,1:T(2,128)(2,1)S(1)} %reshape.279, bf16[1024,768]{1,0:T(8,128)(2,1)} %param.15), kind=kOutput, calls=%fused_computation.53 | convolution fusion | flops 1572864 | bytes 1576448 | tf_op jit(solution)/shard_map/jvp()/dot_general | solution.py:126
  12.9 1.3 %select_select_fusion.3 = (bf16[64,768]{1,0:T(8,128)(2,1)S(1)}, bf16[64,768]{1,0:T(8,128)(2,1)S(1)}, bf16[64,768]{1,0:T(8,128)(2,1)S(1)}, bf16[64,768]{1,0:T(8,128)(2,1)S(1)}) fusion(bf16[64,768]{1,0:T(8,128)(2,1)S(1)} %collective-permute-done, bf16[64,768]{1,0:T(8,128)(2,1)S(1)} %collective-permute-done.1, bf16[64,768]{1,0:T(8,128)(2,1)S(1)} %collective-permute-done.2, ...), kind=kLoop, calls=%fused_computation.172 | loop fusion | flops 589824 | bytes 786444 | tf_op jit(solution)/shard_map/jit(_where)/select_n | solution.py:236
  14.2 2.2 %convert_reduce_fusion = (f32[256]{0:T(256)S(1)}, bf16[256,1024]{1,0:T(8,128)(2,1)S(1)}) fusion(bf16[768,1024]{1,0:T(8,128)(2,1)} %param.11, bf16[64,768]{1,0:T(8,128)(2,1)S(1)} %get-tuple-element.20, bf16[64,768]{1,0:T(8,128)(2,1)S(1)} %get-tuple-element.21, bf16[64,768]{1,0:T(8,128)(2,1)S(1)} %get-tuple-element.22, bf16[64,768]{1,0:T(8,128)(2,1)S(1)} %get-tuple-element.19), kind=kOutput, calls=%fused_computation.12 | convolution fusion | flops 405012224 | bytes 2491392 | tf_op jit(solution)/shard_map/dot_general | solution.py:271
  16.8 3.1 %convolution_convert_fusion = bf16[256,3072]{1,0:T(8,128)(2,1)} fusion(bf16[1024,3072]{1,0:T(8,128)(2,1)S(1)} %copy-done.4, bf16[256,1024]{1,0:T(8,128)(2,1)S(1)} %get-tuple-element.26, f32[256]{0:T(256)S(1)} %add_rsqrt_fusion.3, f32[256]{0:T(256)S(1)} %broadcast_multiply_fusion.2), kind=kOutput, calls=%fused_computation.3 | convolution fusion | flops 1612447744 | bytes 8390656 | tf_op jit(solution)/shard_map/dot_general | solution.py:50
  19.8 2.6 %copy.64 = bf16[256,3072]{0,1:T(8,128)(2,1)} copy(bf16[256,3072]{1,0:T(8,128)(2,1)} %convolution_convert_fusion) | data formatting | bytes 3145728 | tf_op jit(solution)/shard_map/convert_element_type | solution.py:50
  22.4 1.9 %convolution_convert_fusion.1 = bf16[51,3072]{1,0:T(8,128)(2,1)S(1)} fusion(bf16[256,3072]{1,0:T(8,128)(2,1)} %convolution_convert_fusion, s32[51]{0:T(128)S(1)} %dynamic-slice_bitcast_fusion), kind=kOutput, calls=%fused_computation.5 | convolution fusion | flops 80385792 | bytes 1886412 | tf_op jit(solution)/shard_map/dot_general | solution.py:282
  32.2 2.2 %convolution_convert_fusion.16 = bf16[51,768]{1,0:T(8,128)(2,1)S(1)} fusion(bf16[1024,768]{1,0:T(8,128)(2,1)} %param.15, f32[51,1024]{1,0:T(8,128)S(1)} %get-tuple-element.36, bf16[51,1024]{1,0:T(8,128)(2,1)S(1)} %reshape.257, bf16[1024,1024]{1,0:T(8,128)(2,1)S(1)} %copy-done), kind=kOutput, calls=%fused_computation.51 | convolution fusion | flops 187314432 | bytes 4061696 | tf_op jit(solution)/shard_map/jvp()/dot_general | solution.py:123
  35.0 1.3 %fusion.67 = f32[16,256,48]{1,2,0:T(8,128)S(1)} fusion(bf16[256,16,48]{0,2,1:T(8,128)(2,1)S(1)} %bitcast.168, bf16[3,16,48,48]{3,2,1,0:T(8,128)(2,1)} %param.16), kind=kOutput, calls=%fused_computation.130 | convolution fusion | flops 18874368 | bytes 1376256 | tf_op jit(solution)/shard_map/jvp(pgi,gio->pgo)/dot_general | solution.py:135
  36.3 1.2 %convolution_add_fusion.1 = f32[16,256,48]{1,2,0:T(8,128)S(1)} fusion(f32[16,256,48]{1,2,0:T(8,128)S(1)} %fusion.67, bf16[256,16,48]{0,2,1:T(8,128)(2,1)S(1)} %bitcast.169, bf16[3,16,48,48]{3,2,1,0:T(8,128)(2,1)} %param.16), kind=kOutput, calls=%fused_computation.15 | convolution fusion | flops 19070976 | bytes 2162688 | tf_op jit(solution)/shard_map/jvp(pgi,gio->pgo)/dot_general | solution.py:135
  37.6 1.4 %fusion.128 = (f32[256]{0:T(256)S(1)}, f32[16,256,48]{1,2,0:T(8,128)S(1)}) fusion(f32[16,256,48]{1,2,0:T(8,128)S(1)} %convolution_add_fusion.1, bf16[256,16,48]{0,2,1:T(8,128)(2,1)S(1)} %bitcast.170, bf16[3,16,48,48]{3,2,1,0:T(8,128)(2,1)} %param.16), kind=kOutput, calls=%fused_computation.226 | convolution fusion | flops 19267328 | bytes 2163712 | tf_op jit(solution)/shard_map/jvp(pgi,gio->pgo)/dot_general | solution.py:135
  39.8 1.4 %copy.63 = f32[256,768]{1,0:T(8,128)S(1)} copy(f32[256,768]{0,1:T(8,128)} %bitcast.164) | data formatting | bytes 1572864 | tf_op jit(solution)/shard_map/jvp()/reshape | solution.py:141
  41.2 3.0 %add_convert_fusion = (bf16[256,768]{1,0:T(8,128)(2,1)}, f32[256,768]{1,0:T(8,128)}) fusion(bf16[256,768]{1,0:T(8,128)(2,1)S(1)} %fusion.3, f32[256,768]{1,0:T(8,128)S(1)} %copy.63, f32[256]{0:T(256)S(1)} %fusion.111, f32[256]{0:T(256)S(1)} %broadcast_multiply_fusion), kind=kLoop, calls=%fused_computation.85 | loop fusion | flops 13565952 | bytes 2361344 | tf_op jit(solution)/shard_map/jvp()/convert_element_type | solution.py:142
  44.2 3.5 %jvp__.1 = (f32[1,1]{1,0:T(1,128)}, bf16[256,768]{1,0:T(8,128)(2,1)}) custom-call(bf16[256,768]{1,0:T(8,128)(2,1)} %get-tuple-element.14.hidden_ref, bf16[768,1024]{1,0:T(8,128)(2,1)} %dec_out_ref.1, bf16[256,1024]{1,0:T(8,128)(2,1)} %multiply_convert_fusion.targets_ref, f32[256,1]{1,0:T(8,128)} %copy.66.keep_ref), custom_call_target="tpu_custom_call" | custom-call | tf_op jit(solution)/shard_map/jvp()/pallas_call | solution.py:161
  47.7 2.0 %multiply_reduce_fusion.1 = f32[256]{0:T(256)S(1)} fusion(f32[256,768]{1,0:T(8,128)S(1)} %copy.63, f32[256]{0:T(256)S(1)} %broadcast_multiply_fusion, f32[256,768]{1,0:T(8,128)} %get-tuple-element.15, bf16[256,768]{1,0:T(8,128)(2,1)} %get-tuple-element.4, f32[256]{0:T(256)S(1)} %fusion.111), kind=kLoop, calls=%fused_computation.84 | loop fusion | flops 3538688 | bytes 1969152 | tf_op jit(solution)/shard_map/transpose(jvp())/reduce_sum | solution.py:23
  50.8 1.4 %fusion.7 = bf16[256,16,48]{0,2,1:T(8,128)(2,1)S(1)} fusion(bf16[16,48,256]{2,1,0:T(8,128)(2,1)S(1)} %bitcast.165, bf16[3,16,48,48]{3,2,1,0:T(8,128)(2,1)} %param.16), kind=kOutput, calls=%fused_computation.26 | convolution fusion | flops 18874368 | bytes 983040 | tf_op jit(solution)/shard_map/transpose(jvp(pgi,gio->pgo))/dot_general | solution.py:135
  52.2 1.2 %fusion.8 = bf16[256,16,48]{0,2,1:T(8,128)(2,1)S(1)} fusion(bf16[16,48,256]{2,1,0:T(8,128)(2,1)S(1)} %bitcast.166, bf16[3,16,48,48]{3,2,1,0:T(8,128)(2,1)} %param.16), kind=kOutput, calls=%fused_computation.27 | convolution fusion | flops 18874368 | bytes 983040 | tf_op jit(solution)/shard_map/transpose(jvp(pgi,gio->pgo))/dot_general | solution.py:135
  53.4 1.2 %fusion.9 = bf16[256,16,48]{0,2,1:T(8,128)(2,1)S(1)} fusion(bf16[16,48,256]{2,1,0:T(8,128)(2,1)S(1)} %bitcast.167, bf16[3,16,48,48]{3,2,1,0:T(8,128)(2,1)} %param.16), kind=kOutput, calls=%fused_computation.28 | convolution fusion | flops 18874368 | bytes 983040 | tf_op jit(solution)/shard_map/transpose(jvp(pgi,gio->pgo))/dot_general | solution.py:135
  55.1 2.2 %convolution_convert_fusion.11 = bf16[51,1024]{1,0:T(8,128)(2,1)S(1)} fusion(bf16[1024,768]{1,0:T(8,128)(2,1)} %param.15, bf16[256,768]{1,0:T(8,128)(2,1)S(1)} %copy-done.5, bf16[256,768]{1,0:T(8,128)(2,1)S(1)} %copy.71, pred[256]{0:T(512)(128)(4,1)} %copy-done.26, s32[51]{0:T(128)} %copy-done.24), kind=kOutput, calls=%fused_computation.45 | convolution fusion | flops 100964352 | bytes 2464204 | tf_op jit(solution)/shard_map/transpose(jvp())/dot_general | solution.py:123
  58.2 1.4 %fusion.16 = bf16[51,1,16,64]{3,0,2,1:T(8,128)(2,1)S(1)} fusion(bf16[51,16,64]{2,1,0:T(8,128)(2,1)S(1)} %reshape.264, f32[16,51,51]{1,2,0:T(8,128)} %copy-done.12, f32[16,51]{1,0:T(8,128)S(1)} %copy-done.23), kind=kOutput, calls=%fused_computation.42 | convolution fusion | flops 5462304 | bytes 378624 | tf_op jit(solution)/shard_map/transpose(jvp(hqk,khd->qhd))/dot_general | solution.py:38
  61.9 1.2 %reshape.265.rows_ref = bf16[51,3072]{1,0:T(8,128)(2,1)} reshape(bf16[51,3,16,64]{3,2,1,0:T(8,128)(2,1)S(1)} %copy.74) | data formatting | bytes 626688 | tf_op jit(solution)/shard_map/transpose(jvp())/reshape | solution.py:55
  63.1 6.5 %transpose_jvp___.1 = f32[51,1024]{1,0:T(8,128)} custom-call(bf16[51,3072]{1,0:T(8,128)(2,1)} %reshape.265.rows_ref, bf16[1024,3072]{1,0:T(8,128)(2,1)} %weight_ref.1), custom_call_target="tpu_custom_call" | custom-call | tf_op jit(solution)/shard_map/transpose(jvp())/pallas_call | solution.py:211
  69.6 1.1 %multiply_reduce_fusion.3 = (f32[51]{0:T(128)S(1)}, f32[51]{0:T(128)S(1)}) fusion(f32[51,1024]{1,0:T(8,128)S(1)} %get-tuple-element.36, f32[51]{0:T(128)S(1)} %broadcast_multiply_fusion.3, f32[51,1024]{1,0:T(8,128)} %transpose_jvp___.1), kind=kLoop, calls=%fused_computation.150 | loop fusion | flops 365466 | bytes 418404 | tf_op jit(solution)/shard_map/transpose(jvp(jvp()))/reduce_sum | solution.py:211
  70.8 1.2 %fusion.123 = (f32[51]{0:T(128)S(1)}, f32[51,1024]{1,0:T(8,128)S(1)}) fusion(f32[51]{0:T(128)S(1)} %get-tuple-element.24, f32[51,1024]{1,0:T(8,128)S(1)} %get-tuple-element.36, f32[51]{0:T(128)S(1)} %broadcast_multiply_fusion.3, f32[51]{0:T(128)S(1)} %get-tuple-element.23, f32[51,1024]{1,0:T(8,128)} %transpose_jvp___.1), kind=kLoop, calls=%fused_computation.222 | loop fusion | flops 417741 | bytes 627504 | tf_op jit(solution)/shard_map/transpose(jvp(transpose(jvp())))/reduce_sum | solution.py:211
  72.7 1.5 %collective-permute-start.4 = (bf16[51,1024]{1,0:T(8,128)(2,1)S(1)}, bf16[51,1024]{1,0:T(8,128)(2,1)S(1)}, u32[]{:S(2)}, u32[]{:S(2)}) collective-permute-start(bf16[51,1024]{1,0:T(8,128)(2,1)S(1)} %fusion.99), channel_id=1, source_target_pairs={{0,2},{1,3},{2,0},{3,1},{4,6},{5,7},{6,4},{7,5},{8,10},{9,11},{10,... | collective-permute-start | bytes 313352 | tf_op jit(solution)/shard_map/ppermute | solution.py:225
  75.0 2.6 %collective-permute-done.3 = bf16[51,1024]{1,0:T(8,128)(2,1)S(1)} collective-permute-done((bf16[51,1024]{1,0:T(8,128)(2,1)S(1)}, bf16[51,1024]{1,0:T(8,128)(2,1)S(1)}, u32[]{:S(2)}, u32[]{:S(2)}) %collective-permute-start.3) | collective-permute-done | bytes 104480 | tf_op jit(solution)/shard_map/ppermute | solution.py:225
  77.6 1.0 %collective-permute-done.4 = bf16[51,1024]{1,0:T(8,128)(2,1)S(1)} collective-permute-done((bf16[51,1024]{1,0:T(8,128)(2,1)S(1)}, bf16[51,1024]{1,0:T(8,128)(2,1)S(1)}, u32[]{:S(2)}, u32[]{:S(2)}) %collective-permute-start.4) | collective-permute-done | bytes 104480 | tf_op jit(solution)/shard_map/ppermute | solution.py:225
  78.6 1.3 %collective-permute-done.5 = bf16[51,1024]{1,0:T(8,128)(2,1)S(1)} collective-permute-done((bf16[51,1024]{1,0:T(8,128)(2,1)S(1)}, bf16[51,1024]{1,0:T(8,128)(2,1)S(1)}, u32[]{:S(2)}, u32[]{:S(2)}) %collective-permute-start.5) | collective-permute-done | bytes 104480 | tf_op jit(solution)/shard_map/ppermute | solution.py:225
  79.9 1.4 %fusion.19 = f32[192,1024]{1,0:T(8,128)} fusion(bf16[51,1024]{1,0:T(8,128)(2,1)S(1)} %collective-permute-done.5, bf16[51,1024]{1,0:T(8,128)(2,1)S(1)} %collective-permute-done.4, bf16[51,1024]{1,0:T(8,128)(2,1)S(1)} %collective-permute-done.3, bf16[51,1024]{1,0:T(8,128)(2,1)S(1)} %fusion.99, bf16[256,768]{1,0:T(8,128)(2,1)S(1)} %pad_maximum_fusion, ...), kind=kOutput, calls=%fused_computation.52 | convolution fusion | flops 102032640 | bytes 1377284 | tf_op jit(solution)/shard_map/vc,vd->cd/dot_general | solution.py:316
  (123 shorter events, 18.0 us)
Async XLA Ops:
  0.6 26.7 %copy-start = (bf16[1024,1024]{1,0:T(8,128)(2,1)S(1)}, bf16[1024,1024]{1,0:T(8,128)(2,1)}, u32[]{:S(2)}) copy-start(bf16[1024,1024]{1,0:T(8,128)(2,1)} %param.13) | copy-start | bytes 6291460
  0.6 12.2 %collective-permute-start = (bf16[64,768]{1,0:T(8,128)(2,1)}, bf16[64,768]{1,0:T(8,128)(2,1)S(1)}, u32[]{:S(2)}, u32[]{:S(2)}) collective-permute-start(bf16[64,768]{1,0:T(8,128)(2,1)} %param.9), channel_id=1, source_target_pairs={{0,1},{1,2},{2,3},{3,0},{4,5},{5,6},{6,7},{7,4},{8,9},{9,10},{10,1... | collective-permute-start | bytes 294920 | tf_op jit(solution)/shard_map/ppermute | solution.py:225
  3.7 9.2 %collective-permute-start.1 = (bf16[64,768]{1,0:T(8,128)(2,1)}, bf16[64,768]{1,0:T(8,128)(2,1)S(1)}, u32[]{:S(2)}, u32[]{:S(2)}) collective-permute-start(bf16[64,768]{1,0:T(8,128)(2,1)} %param.9), channel_id=1, source_target_pairs={{0,2},{1,3},{2,0},{3,1},{4,6},{5,7},{6,4},{7,5},{8,10},{9,11},{10,... | collective-permute-start | bytes 294920 | tf_op jit(solution)/shard_map/ppermute | solution.py:225
  5.2 7.7 %collective-permute-start.2 = (bf16[64,768]{1,0:T(8,128)(2,1)}, bf16[64,768]{1,0:T(8,128)(2,1)S(1)}, u32[]{:S(2)}, u32[]{:S(2)}) collective-permute-start(bf16[64,768]{1,0:T(8,128)(2,1)} %param.9), channel_id=1, source_target_pairs={{0,3},{1,0},{2,1},{3,2},{4,7},{5,4},{6,5},{7,6},{8,11},{9,8},{10,9... | collective-permute-start | bytes 294920 | tf_op jit(solution)/shard_map/ppermute | solution.py:225
  7.3 27.1 %copy-start.24 = (s32[51]{0:T(128)}, s32[51]{0:T(128)S(1)}, u32[]{:S(2)}) copy-start(s32[51]{0:T(128)S(1)} %dynamic-slice_bitcast_fusion) | copy-start | bytes 616
  7.5 26.9 %copy-start.26 = (pred[256]{0:T(512)(128)(4,1)}, pred[256]{0:T(512)(128)(4,1)S(1)}, u32[]{:S(2)}) copy-start(pred[256]{0:T(512)(128)(4,1)S(1)} %broadcast_compare_fusion) | copy-start | bytes 772
  10.9 5.8 %copy-start.4 = (bf16[1024,3072]{1,0:T(8,128)(2,1)S(1)}, bf16[1024,3072]{1,0:T(8,128)(2,1)}, u32[]{:S(2)}) copy-start(bf16[1024,3072]{1,0:T(8,128)(2,1)} %weight_ref.1) | copy-start | bytes 18874372
  14.2 2.5 %copy-start.14 = (bf16[64,768]{1,0:T(8,128)(2,1)}, bf16[64,768]{1,0:T(8,128)(2,1)S(1)}, u32[]{:S(2)}) copy-start(bf16[64,768]{1,0:T(8,128)(2,1)S(1)} %get-tuple-element.19) | copy-start | bytes 294916
  14.2 2.5 %copy-start.16 = (bf16[64,768]{1,0:T(8,128)(2,1)}, bf16[64,768]{1,0:T(8,128)(2,1)S(1)}, u32[]{:S(2)}) copy-start(bf16[64,768]{1,0:T(8,128)(2,1)S(1)} %get-tuple-element.20) | copy-start | bytes 294916
  14.2 2.5 %copy-start.18 = (bf16[64,768]{1,0:T(8,128)(2,1)}, bf16[64,768]{1,0:T(8,128)(2,1)S(1)}, u32[]{:S(2)}) copy-start(bf16[64,768]{1,0:T(8,128)(2,1)S(1)} %get-tuple-element.21) | copy-start | bytes 294916
  14.2 2.5 %copy-start.20 = (bf16[64,768]{1,0:T(8,128)(2,1)}, bf16[64,768]{1,0:T(8,128)(2,1)S(1)}, u32[]{:S(2)}) copy-start(bf16[64,768]{1,0:T(8,128)(2,1)S(1)} %get-tuple-element.22) | copy-start | bytes 294916
  22.4 2.8 %copy-start.1 = (bf16[256,3072]{0,1:T(8,128)(2,1)S(1)}, bf16[256,3072]{0,1:T(8,128)(2,1)}, u32[]{:S(2)}) copy-start(bf16[256,3072]{0,1:T(8,128)(2,1)} %copy.64) | copy-start | bytes 4718596
  30.0 1.2 %copy-start.8 = (bf16[51,1,16,64]{3,2,1,0:T(8,128)(2,1)}, bf16[51,1,16,64]{3,2,1,0:T(8,128)(2,1)S(1)}, u32[]{:S(2)}) copy-start(bf16[51,1,16,64]{3,2,1,0:T(8,128)(2,1)S(1)} %get-tuple-element.18) | copy-start | bytes 313348
  30.0 1.2 %copy-start.10 = (bf16[51,1,16,64]{3,2,1,0:T(8,128)(2,1)}, bf16[51,1,16,64]{3,2,1,0:T(8,128)(2,1)S(1)}, u32[]{:S(2)}) copy-start(bf16[51,1,16,64]{3,2,1,0:T(8,128)(2,1)S(1)} %get-tuple-element.17) | copy-start | bytes 313348
  31.2 1.0 %copy-start.22 = (f32[16,51]{1,0:T(8,128)}, f32[16,51]{1,0:T(8,128)S(1)}, u32[]{:S(2)}) copy-start(f32[16,51]{1,0:T(8,128)S(1)} %get-tuple-element.27) | copy-start | bytes 9796
  38.9 0.9 %copy-start.2 = (f32[16,256,48]{1,2,0:T(8,128)}, f32[16,256,48]{1,2,0:T(8,128)S(1)}, u32[]{:S(2)}) copy-start(f32[16,256,48]{1,2,0:T(8,128)S(1)} %get-tuple-element.30) | copy-start | bytes 2359300
  47.7 2.0 %copy-start.3 = (f32[256,768]{1,0:T(8,128)S(1)}, f32[256,768]{1,0:T(8,128)}, u32[]{:S(2)}) copy-start(f32[256,768]{1,0:T(8,128)} %get-tuple-element.15) | copy-start | bytes 2359300
  47.7 2.0 %copy-start.5 = (bf16[256,768]{1,0:T(8,128)(2,1)S(1)}, bf16[256,768]{1,0:T(8,128)(2,1)}, u32[]{:S(2)}) copy-start(bf16[256,768]{1,0:T(8,128)(2,1)} %get-tuple-element.4) | copy-start | bytes 1179652
  50.6 3.9 %copy-start.23 = (f32[16,51]{1,0:T(8,128)S(1)}, f32[16,51]{1,0:T(8,128)}, u32[]{:S(2)}) copy-start(f32[16,51]{1,0:T(8,128)} %copy-done.22) | copy-start | bytes 9796
  57.3 2.4 %copy-start.11 = (bf16[51,1,16,64]{3,2,1,0:T(8,128)(2,1)S(1)}, bf16[51,1,16,64]{3,2,1,0:T(8,128)(2,1)}, u32[]{:S(2)}) copy-start(bf16[51,1,16,64]{3,2,1,0:T(8,128)(2,1)} %copy-done.10) | copy-start | bytes 313348
  58.0 1.9 %copy-start.7 = (bf16[51,1,16,64]{3,2,1,0:T(8,128)(2,1)S(1)}, bf16[51,1,16,64]{3,2,1,0:T(8,128)(2,1)}, u32[]{:S(2)}) copy-start(bf16[51,1,16,64]{3,2,1,0:T(8,128)(2,1)} %copy-done.6) | copy-start | bytes 313348
  58.0 1.9 %copy-start.9 = (bf16[51,1,16,64]{3,2,1,0:T(8,128)(2,1)S(1)}, bf16[51,1,16,64]{3,2,1,0:T(8,128)(2,1)}, u32[]{:S(2)}) copy-start(bf16[51,1,16,64]{3,2,1,0:T(8,128)(2,1)} %copy-done.8) | copy-start | bytes 313348
  58.2 1.4 %copy-start.13 = (f32[16,51,51]{1,2,0:T(8,128)S(1)}, f32[16,51,51]{1,2,0:T(8,128)}, u32[]{:S(2)}) copy-start(f32[16,51,51]{1,2,0:T(8,128)} %copy-done.12) | copy-start | bytes 499396
  63.1 6.5 %copy-start.27 = (f32[51]{0:T(128)S(1)}, f32[51]{0:T(128)}, u32[]{:S(2)}) copy-start(f32[51]{0:T(128)} %get-tuple-element.35) | copy-start | bytes 616
  63.1 11.9 %copy-start.15 = (bf16[64,768]{1,0:T(8,128)(2,1)S(1)}, bf16[64,768]{1,0:T(8,128)(2,1)}, u32[]{:S(2)}) copy-start(bf16[64,768]{1,0:T(8,128)(2,1)} %copy-done.14) | copy-start | bytes 294916
  63.1 11.9 %copy-start.17 = (bf16[64,768]{1,0:T(8,128)(2,1)S(1)}, bf16[64,768]{1,0:T(8,128)(2,1)}, u32[]{:S(2)}) copy-start(bf16[64,768]{1,0:T(8,128)(2,1)} %copy-done.16) | copy-start | bytes 294916
  63.1 11.9 %copy-start.19 = (bf16[64,768]{1,0:T(8,128)(2,1)S(1)}, bf16[64,768]{1,0:T(8,128)(2,1)}, u32[]{:S(2)}) copy-start(bf16[64,768]{1,0:T(8,128)(2,1)} %copy-done.18) | copy-start | bytes 294916
  63.1 11.9 %copy-start.21 = (bf16[64,768]{1,0:T(8,128)(2,1)S(1)}, bf16[64,768]{1,0:T(8,128)(2,1)}, u32[]{:S(2)}) copy-start(bf16[64,768]{1,0:T(8,128)(2,1)} %copy-done.20) | copy-start | bytes 294916
  69.6 10.3 %copy-start.25 = (s32[204]{0:T(256)S(1)}, s32[204]{0:T(256)}, u32[]{:S(2)}) copy-start(s32[204]{0:T(256)} %eq.93) | copy-start | bytes 2452
  72.1 5.5 %collective-permute-start.3 = (bf16[51,1024]{1,0:T(8,128)(2,1)S(1)}, bf16[51,1024]{1,0:T(8,128)(2,1)S(1)}, u32[]{:S(2)}, u32[]{:S(2)}) collective-permute-start(bf16[51,1024]{1,0:T(8,128)(2,1)S(1)} %fusion.99), channel_id=1, source_target_pairs={{0,3},{1,0},{2,1},{3,2},{4,7},{5,4},{6,5},{7,6},{8,11},{9,8},{10,9... | collective-permute-start | bytes 313352 | tf_op jit(solution)/shard_map/ppermute | solution.py:225
  72.7 6.0 %collective-permute-start.4 = (bf16[51,1024]{1,0:T(8,128)(2,1)S(1)}, bf16[51,1024]{1,0:T(8,128)(2,1)S(1)}, u32[]{:S(2)}, u32[]{:S(2)}) collective-permute-start(bf16[51,1024]{1,0:T(8,128)(2,1)S(1)} %fusion.99), channel_id=1, source_target_pairs={{0,2},{1,3},{2,0},{3,1},{4,6},{5,7},{6,4},{7,5},{8,10},{9,11},{10,... | collective-permute-start | bytes 313352 | tf_op jit(solution)/shard_map/ppermute | solution.py:225
  74.2 5.7 %collective-permute-start.5 = (bf16[51,1024]{1,0:T(8,128)(2,1)S(1)}, bf16[51,1024]{1,0:T(8,128)(2,1)S(1)}, u32[]{:S(2)}, u32[]{:S(2)}) collective-permute-start(bf16[51,1024]{1,0:T(8,128)(2,1)S(1)} %fusion.99), channel_id=1, source_target_pairs={{0,1},{1,2},{2,3},{3,0},{4,5},{5,6},{6,7},{7,4},{8,9},{9,10},{10,1... | collective-permute-start | bytes 313352 | tf_op jit(solution)/shard_map/ppermute | solution.py:225
  (2 other events, 1.5 us)

commit v20 on v18

--- a/solution.py
+++ b/solution.py
@@ -280,12 +280,15 @@
     gathered = jnp.dot(all_picks, own_cols, preferred_element_type=jnp.float32).astype(
         jnp.bfloat16
     )
-    embed_grad = jnp.einsum(
-        "vc,vd->cd",
-        gathered,
-        jnp.concatenate(ring_gather(grad_in, group_size), axis=0),
-        preferred_element_type=jnp.float32,
-    )
+    embed_grad = None
+    for slot, rows in enumerate(ring_gather(grad_in, group_size)):
+        term = jnp.einsum(
+            "vc,vd->cd",
+            gathered[slot * visible_count : (slot + 1) * visible_count],
+            rows,
+            preferred_element_type=jnp.float32,
+        )
+        embed_grad = term if embed_grad is None else embed_grad + term
     return (embed_grad, copy_loss)
 
 

time: 78.9 us -> 79.4 us (level)
  waiting for transfers between devices: 4.87 us -> 2.76 us
  matrix products: 35.6 us -> 37.3 us
    ppermute x6, waiting for transfers between devices: 4.87 us -> 2.76 us  [ring_gather(): parts.append(lax.ppermute(values, 'mask', pairs))]
    dot_general x1 -> x5, matrix products: 1.42 us -> 3.24 us  [the longest x4 2.01 us: on_device(): jnp.einsum('vc,vd->cd', gathered[slot * visible_count:(slot + 1) * visibl...]
  transfers between devices with their start and end apart: 6 -> 6, of which waited for: 3 -> 3; matrix products, arithmetic and copies ran while one was open for 8% -> 10% of each run, Pallas kernels for 0% -> 0%
where the time goes in v20:
time: 79.4 us; the launch traced here: 78.7 us
  matrix products  37.3 us (47%)
  other arithmetic  12.2 us (15%)
  local copies, waits for them, and re-layouts  11.5 us (14%)
  starting transfers between devices  8.15 us (10%)
  Pallas kernels  3.54 us (4%)
  between operations  3.18 us (4%)
  waiting for transfers between devices  2.76 us (3%)
    ppermute x6, starting transfers between devices, ring_gather(): parts.append(lax.ppermute(values, 'mask', pairs))  8.15 us
    dot_general x6, matrix products, decoder_output(): jnp.einsum('pgi,gio->pgo', padded[offset:offset + total_rows], conv_w[off...  7.63 us
    dot_general x1, matrix products, copy_terms(): branch = attention_from(reuse_rows(visible_in, w_qkv, projected), w_out)  4.81 us
    dot_general x2, matrix products, decoder_output(): jnp.dot(visible_out, dec_in, preferred_element_type=jnp.float32)  4.38 us
    pallas_call x1, Pallas kernels, masked_squares(): pl.pallas_call(functools.partial(loss_kernel, scale=scale), out_shape=(ja...  3.54 us
    dot_general x1, matrix products, project_rows(): jnp.dot(normed, w_qkv, preferred_element_type=jnp.float32)  3.1 us
    convert_element_type x1, other arithmetic, decoder_output(): return (lowered.astype(jnp.float32) + activated).astype(jnp.bfloat16)  2.97 us
    dot_general x4, matrix products, mix_heads(): jnp.einsum('hqk,khd->qhd', weights, values, preferred_element_type=jnp.fl...  2.82 us
  transfers between devices with their start and end apart: 6, of which 3 were waited for; matrix products, arithmetic and copies ran while one was open for 10% of the time, Pallas kernels for 0%

profile of v20, /device:TPU:0, one launch (start us, length us, event | category | flops | bytes accessed | tf_op | source)
XLA Modules:
  0.0 78.7 jit_solution(17619555916106290233)
XLA Ops:
  0.6 3.0 %collective-permute-start = (bf16[64,768]{1,0:T(8,128)(2,1)}, bf16[64,768]{1,0:T(8,128)(2,1)S(1)}, u32[]{:S(2)}, u32[]{:S(2)}) collective-permute-start(bf16[64,768]{1,0:T(8,128)(2,1)} %param.9), channel_id=1, source_target_pairs={{0,1},{1,2},{2,3},{3,0},{4,5},{5,6},{6,7},{7,4},{8,9},{9,10},{10,1... | collective-permute-start | bytes 294920 | tf_op jit(solution)/shard_map/ppermute | solution.py:192
  3.7 1.5 %collective-permute-start.1 = (bf16[64,768]{1,0:T(8,128)(2,1)}, bf16[64,768]{1,0:T(8,128)(2,1)S(1)}, u32[]{:S(2)}, u32[]{:S(2)}) collective-permute-start(bf16[64,768]{1,0:T(8,128)(2,1)} %param.9), channel_id=1, source_target_pairs={{0,2},{1,3},{2,0},{3,1},{4,6},{5,7},{6,4},{7,5},{8,10},{9,11},{10,... | collective-permute-start | bytes 294920 | tf_op jit(solution)/shard_map/ppermute | solution.py:192
  5.2 1.4 %collective-permute-start.2 = (bf16[64,768]{1,0:T(8,128)(2,1)}, bf16[64,768]{1,0:T(8,128)(2,1)S(1)}, u32[]{:S(2)}, u32[]{:S(2)}) collective-permute-start(bf16[64,768]{1,0:T(8,128)(2,1)} %param.9), channel_id=1, source_target_pairs={{0,3},{1,0},{2,1},{3,2},{4,7},{5,4},{6,5},{7,6},{8,11},{9,8},{10,9... | collective-permute-start | bytes 294920 | tf_op jit(solution)/shard_map/ppermute | solution.py:192
  9.0 1.2 %gather_fusion = s32[4,51]{1,0:T(4,128)S(1)} fusion(s32[4,51]{1,0:T(4,128)} %param.10, s32[1024]{0:T(1024)S(1)} %pad_clamp_fusion), kind=kCustom, calls=%fused_computation | custom fusion | bytes 1648 | tf_op jit(solution)/shard_map/gather | solution.py:277
  10.9 1.9 %convolution_reduce_fusion = bf16[768]{0:T(1024)(128)(2,1)S(1)} fusion(bf16[1024,1]{0,1:T(2,128)(2,1)S(1)} %reshape.279, bf16[1024,768]{1,0:T(8,128)(2,1)} %param.15), kind=kOutput, calls=%fused_computation.56 | convolution fusion | flops 1572864 | bytes 1576448 | tf_op jit(solution)/shard_map/jvp()/dot_general | solution.py:93
  12.9 1.3 %select_select_fusion.3 = (bf16[64,768]{1,0:T(8,128)(2,1)S(1)}, bf16[64,768]{1,0:T(8,128)(2,1)S(1)}, bf16[64,768]{1,0:T(8,128)(2,1)S(1)}, bf16[64,768]{1,0:T(8,128)(2,1)S(1)}) fusion(bf16[64,768]{1,0:T(8,128)(2,1)S(1)} %collective-permute-done, bf16[64,768]{1,0:T(8,128)(2,1)S(1)} %collective-permute-done.1, bf16[64,768]{1,0:T(8,128)(2,1)S(1)} %collective-permute-done.2, ...), kind=kLoop, calls=%fused_computation.168 | loop fusion | flops 589824 | bytes 786444 | tf_op jit(solution)/shard_map/jit(_where)/select_n | solution.py:203
  14.2 2.2 %convert_reduce_fusion = (f32[256]{0:T(256)S(1)}, bf16[256,1024]{1,0:T(8,128)(2,1)S(1)}) fusion(bf16[768,1024]{1,0:T(8,128)(2,1)} %param.11, bf16[64,768]{1,0:T(8,128)(2,1)S(1)} %get-tuple-element.18, bf16[64,768]{1,0:T(8,128)(2,1)S(1)} %get-tuple-element.19, bf16[64,768]{1,0:T(8,128)(2,1)S(1)} %get-tuple-element.20, bf16[64,768]{1,0:T(8,128)(2,1)S(1)} %get-tuple-element.17), kind=kOutput, calls=%fused_computation.12 | convolution fusion | flops 405012224 | bytes 2491392 | tf_op jit(solution)/shard_map/dot_general | solution.py:238
  16.8 3.1 %convolution_convert_fusion = bf16[256,3072]{1,0:T(8,128)(2,1)} fusion(bf16[1024,3072]{1,0:T(8,128)(2,1)S(1)} %copy-done.4, bf16[256,1024]{1,0:T(8,128)(2,1)S(1)} %get-tuple-element.24, f32[256]{0:T(256)S(1)} %add_rsqrt_fusion.3, f32[256]{0:T(256)S(1)} %broadcast_multiply_fusion.2), kind=kOutput, calls=%fused_computation.3 | convolution fusion | flops 1612447744 | bytes 8390656 | tf_op jit(solution)/shard_map/dot_general | solution.py:50
  19.8 2.6 %copy.63 = bf16[256,3072]{0,1:T(8,128)(2,1)} copy(bf16[256,3072]{1,0:T(8,128)(2,1)} %convolution_convert_fusion) | data formatting | bytes 3145728 | tf_op jit(solution)/shard_map/convert_element_type | solution.py:50
  22.4 1.9 %convolution_convert_fusion.1 = bf16[51,3072]{1,0:T(8,128)(2,1)S(1)} fusion(bf16[256,3072]{1,0:T(8,128)(2,1)} %convolution_convert_fusion, s32[51]{0:T(128)S(1)} %dynamic-slice_bitcast_fusion), kind=kOutput, calls=%fused_computation.5 | convolution fusion | flops 80385792 | bytes 1886412 | tf_op jit(solution)/shard_map/dot_general | solution.py:249
  24.4 0.9 %fusion.125 = (f32[51]{0:T(128)}, f32[51,1024]{1,0:T(8,128)S(1)}) fusion(bf16[256,1024]{1,0:T(8,128)(2,1)S(1)} %get-tuple-element.24, s32[51]{0:T(128)S(1)} %dynamic-slice_bitcast_fusion), kind=kOutput, calls=%fused_computation.229 | convolution fusion | flops 26908364 | bytes 733592 | tf_op jit(solution)/shard_map/dot_general | solution.py:243
  25.5 1.0 %fusion = (f32[16,256]{1,0:T(8,128)S(1)}, f32[16,256,256]{1,2,0:T(8,128)S(1)}) fusion(f32[256,16]{0,1:T(8,128)S(1)} %get-tuple-element.43, bf16[256,3,16,64]{0,3,2,1:T(8,128)(2,1)S(1)} %bitcast.168, f32[256,16]{0,1:T(8,128)S(1)} %get-tuple-element.44), kind=kOutput, calls=%fused_computation.4 | convolution fusion | flops 137883648 | bytes 5292032 | tf_op jit(solution)/shard_map/qhd,khd->hqk/dot_general | solution.py:33
  28.5 1.0 %multiply_convert_fusion.targets_ref = bf16[256,1024]{1,0:T(8,128)(2,1)} fusion(f32[256,1024]{1,0:T(8,128)S(1)} %get-tuple-element.32, f32[256]{0:T(256)S(1)} %add_rsqrt_fusion.2, f32[256]{0:T(256)S(1)} %broadcast_multiply_fusion.1), kind=kLoop, calls=%fused_computation.63 | loop fusion | flops 786432 | bytes 1574912 | tf_op jit(solution)/shard_map/convert_element_type | solution.py:255
  32.2 2.2 %convolution_convert_fusion.17 = bf16[51,768]{1,0:T(8,128)(2,1)S(1)} fusion(bf16[1024,768]{1,0:T(8,128)(2,1)} %param.15, f32[51,1024]{1,0:T(8,128)S(1)} %get-tuple-element.34, bf16[51,1024]{1,0:T(8,128)(2,1)S(1)} %reshape.257, bf16[1024,1024]{1,0:T(8,128)(2,1)S(1)} %copy-done), kind=kOutput, calls=%fused_computation.55 | convolution fusion | flops 187314432 | bytes 4061696 | tf_op jit(solution)/shard_map/jvp()/dot_general | solution.py:90
  35.0 1.3 %fusion.60 = f32[16,256,48]{1,2,0:T(8,128)S(1)} fusion(bf16[256,16,48]{0,2,1:T(8,128)(2,1)S(1)} %bitcast.174, bf16[3,16,48,48]{3,2,1,0:T(8,128)(2,1)} %param.16), kind=kOutput, calls=%fused_computation.126 | convolution fusion | flops 18874368 | bytes 1376256 | tf_op jit(solution)/shard_map/jvp(pgi,gio->pgo)/dot_general | solution.py:102
  36.3 1.2 %convolution_add_fusion.1 = f32[16,256,48]{1,2,0:T(8,128)S(1)} fusion(f32[16,256,48]{1,2,0:T(8,128)S(1)} %fusion.60, bf16[256,16,48]{0,2,1:T(8,128)(2,1)S(1)} %bitcast.175, bf16[3,16,48,48]{3,2,1,0:T(8,128)(2,1)} %param.16), kind=kOutput, calls=%fused_computation.15 | convolution fusion | flops 19070976 | bytes 2162688 | tf_op jit(solution)/shard_map/jvp(pgi,gio->pgo)/dot_general | solution.py:102
  37.6 1.4 %fusion.123 = (f32[256]{0:T(256)S(1)}, f32[16,256,48]{1,2,0:T(8,128)S(1)}) fusion(f32[16,256,48]{1,2,0:T(8,128)S(1)} %convolution_add_fusion.1, bf16[256,16,48]{0,2,1:T(8,128)(2,1)S(1)} %bitcast.176, bf16[3,16,48,48]{3,2,1,0:T(8,128)(2,1)} %param.16), kind=kOutput, calls=%fused_computation.227 | convolution fusion | flops 19267328 | bytes 2163712 | tf_op jit(solution)/shard_map/jvp(pgi,gio->pgo)/dot_general | solution.py:102
  39.8 1.4 %copy.62 = f32[256,768]{1,0:T(8,128)S(1)} copy(f32[256,768]{0,1:T(8,128)} %bitcast.170) | data formatting | bytes 1572864 | tf_op jit(solution)/shard_map/jvp()/reshape | solution.py:108
  41.2 3.0 %add_convert_fusion = (bf16[256,768]{1,0:T(8,128)(2,1)}, f32[256,768]{1,0:T(8,128)}) fusion(bf16[256,768]{1,0:T(8,128)(2,1)S(1)} %fusion.4, f32[256,768]{1,0:T(8,128)S(1)} %copy.62, f32[256]{0:T(256)S(1)} %fusion.108, f32[256]{0:T(256)S(1)} %broadcast_multiply_fusion), kind=kLoop, calls=%fused_computation.88 | loop fusion | flops 13565952 | bytes 2361344 | tf_op jit(solution)/shard_map/jvp()/convert_element_type | solution.py:109
  44.2 3.5 %jvp__.1 = (f32[1,1]{1,0:T(1,128)}, bf16[256,768]{1,0:T(8,128)(2,1)}) custom-call(bf16[256,768]{1,0:T(8,128)(2,1)} %get-tuple-element.12.hidden_ref, bf16[768,1024]{1,0:T(8,128)(2,1)} %dec_out_ref.1, bf16[256,1024]{1,0:T(8,128)(2,1)} %multiply_convert_fusion.targets_ref, f32[256,1]{1,0:T(8,128)} %copy.65.keep_ref), custom_call_target="tpu_custom_call" | custom-call | tf_op jit(solution)/shard_map/jvp()/pallas_call | solution.py:128
  47.7 2.0 %multiply_reduce_fusion.1 = f32[256]{0:T(256)S(1)} fusion(f32[256,768]{1,0:T(8,128)S(1)} %copy.62, f32[256]{0:T(256)S(1)} %broadcast_multiply_fusion, f32[256,768]{1,0:T(8,128)} %get-tuple-element.13, bf16[256,768]{1,0:T(8,128)(2,1)} %get-tuple-element.4, f32[256]{0:T(256)S(1)} %fusion.108), kind=kLoop, calls=%fused_computation.87 | loop fusion | flops 3538688 | bytes 1969152 | tf_op jit(solution)/shard_map/transpose(jvp())/reduce_sum | solution.py:23
  50.8 1.4 %fusion.10 = bf16[256,16,48]{0,2,1:T(8,128)(2,1)S(1)} fusion(bf16[16,48,256]{2,1,0:T(8,128)(2,1)S(1)} %bitcast.171, bf16[3,16,48,48]{3,2,1,0:T(8,128)(2,1)} %param.16), kind=kOutput, calls=%fused_computation.31 | convolution fusion | flops 18874368 | bytes 983040 | tf_op jit(solution)/shard_map/transpose(jvp(pgi,gio->pgo))/dot_general | solution.py:102
  52.2 1.2 %fusion.8 = bf16[256,16,48]{0,2,1:T(8,128)(2,1)S(1)} fusion(bf16[16,48,256]{2,1,0:T(8,128)(2,1)S(1)} %bitcast.172, bf16[3,16,48,48]{3,2,1,0:T(8,128)(2,1)} %param.16), kind=kOutput, calls=%fused_computation.29 | convolution fusion | flops 18874368 | bytes 983040 | tf_op jit(solution)/shard_map/transpose(jvp(pgi,gio->pgo))/dot_general | solution.py:102
  53.4 1.2 %fusion.9 = bf16[256,16,48]{0,2,1:T(8,128)(2,1)S(1)} fusion(bf16[16,48,256]{2,1,0:T(8,128)(2,1)S(1)} %bitcast.173, bf16[3,16,48,48]{3,2,1,0:T(8,128)(2,1)} %param.16), kind=kOutput, calls=%fused_computation.30 | convolution fusion | flops 18874368 | bytes 983040 | tf_op jit(solution)/shard_map/transpose(jvp(pgi,gio->pgo))/dot_general | solution.py:102
  55.1 2.2 %convolution_convert_fusion.12 = bf16[51,1024]{1,0:T(8,128)(2,1)S(1)} fusion(bf16[1024,768]{1,0:T(8,128)(2,1)} %param.15, bf16[256,768]{1,0:T(8,128)(2,1)S(1)} %copy-done.5, bf16[256,768]{1,0:T(8,128)(2,1)S(1)} %copy.70, pred[256]{0:T(512)(128)(4,1)} %copy-done.26, s32[51]{0:T(128)} %copy-done.24), kind=kOutput, calls=%fused_computation.49 | convolution fusion | flops 100964352 | bytes 2464204 | tf_op jit(solution)/shard_map/transpose(jvp())/dot_general | solution.py:90
  58.2 1.4 %fusion.17 = bf16[51,1,16,64]{3,0,2,1:T(8,128)(2,1)S(1)} fusion(bf16[51,16,64]{2,1,0:T(8,128)(2,1)S(1)} %reshape.264, f32[16,51,51]{1,2,0:T(8,128)} %copy-done.12, f32[16,51]{1,0:T(8,128)S(1)} %copy-done.23), kind=kOutput, calls=%fused_computation.45 | convolution fusion | flops 5462304 | bytes 378624 | tf_op jit(solution)/shard_map/transpose(jvp(hqk,khd->qhd))/dot_general | solution.py:38
  63.2 4.8 %convolution_convert_fusion.11 = bf16[51,1024]{1,0:T(8,128)(2,1)S(1)} fusion(bf16[51,3072]{1,0:T(8,128)(2,1)S(1)} %reshape.265, bf16[1024,3072]{1,0:T(8,128)(2,1)} %param.12), kind=kOutput, calls=%fused_computation.48 | convolution fusion | flops 320916480 | bytes 6709248 | tf_op jit(solution)/shard_map/transpose(jvp())/dot_general | solution.py:178
  69.3 1.5 %collective-permute-start.5 = (bf16[51,1024]{1,0:T(8,128)(2,1)S(1)}, bf16[51,1024]{1,0:T(8,128)(2,1)S(1)}, u32[]{:S(2)}, u32[]{:S(2)}) collective-permute-start(bf16[51,1024]{1,0:T(8,128)(2,1)S(1)} %fusion.91), channel_id=1, source_target_pairs={{0,1},{1,2},{2,3},{3,0},{4,5},{5,6},{6,7},{7,4},{8,9},{9,10},{10,1... | collective-permute-start | bytes 313352 | tf_op jit(solution)/shard_map/ppermute | solution.py:192
  70.9 1.2 %convolution_convert_fusion.15 = bf16[204,192]{0,1:T(8,128)(2,1)S(1)} fusion(bf16[256,768]{1,0:T(8,128)(2,1)} %pad_maximum_fusion, s32[]{:T(128)S(6)} %select_n.161, s32[204]{0:T(256)S(1)} %copy-done.25), kind=kOutput, calls=%fused_computation.53 | convolution fusion | flops 20145408 | bytes 210228 | tf_op jit(solution)/shard_map/dot_general | solution.py:280
  73.1 1.0 %collective-permute-done.3 = bf16[51,1024]{1,0:T(8,128)(2,1)S(1)} collective-permute-done((bf16[51,1024]{1,0:T(8,128)(2,1)S(1)}, bf16[51,1024]{1,0:T(8,128)(2,1)S(1)}, u32[]{:S(2)}, u32[]{:S(2)}) %collective-permute-start.3) | collective-permute-done | bytes 104480 | tf_op jit(solution)/shard_map/ppermute | solution.py:192
  75.5 0.9 %collective-permute-done.4 = bf16[51,1024]{1,0:T(8,128)(2,1)S(1)} collective-permute-done((bf16[51,1024]{1,0:T(8,128)(2,1)S(1)}, bf16[51,1024]{1,0:T(8,128)(2,1)S(1)}, u32[]{:S(2)}, u32[]{:S(2)}) %collective-permute-start.4) | collective-permute-done | bytes 104480 | tf_op jit(solution)/shard_map/ppermute | solution.py:192
  76.4 1.2 %fusion.3 = f32[192,1024]{1,0:T(8,128)} fusion(f32[192,1024]{1,0:T(8,128)S(1)} %fusion.94, f32[192,1024]{1,0:T(8,128)S(1)} %convolution_add_fusion.3, bf16[51,1024]{1,0:T(8,128)(2,1)S(1)} %collective-permute-done.4, bf16[204,192]{0,1:T(8,128)(2,1)S(1)} %convolution_convert_fusion.15), kind=kOutput, calls=%fused_computation.17 | convolution fusion | flops 20447232 | bytes 2523136 | tf_op jit(solution)/shard_map/vc,vd->cd/dot_general | solution.py:285
  (127 shorter events, 18.6 us)
Async XLA Ops:
  0.6 26.7 %copy-start = (bf16[1024,1024]{1,0:T(8,128)(2,1)S(1)}, bf16[1024,1024]{1,0:T(8,128)(2,1)}, u32[]{:S(2)}) copy-start(bf16[1024,1024]{1,0:T(8,128)(2,1)} %param.13) | copy-start | bytes 6291460
  0.6 12.2 %collective-permute-start = (bf16[64,768]{1,0:T(8,128)(2,1)}, bf16[64,768]{1,0:T(8,128)(2,1)S(1)}, u32[]{:S(2)}, u32[]{:S(2)}) collective-permute-start(bf16[64,768]{1,0:T(8,128)(2,1)} %param.9), channel_id=1, source_target_pairs={{0,1},{1,2},{2,3},{3,0},{4,5},{5,6},{6,7},{7,4},{8,9},{9,10},{10,1... | collective-permute-start | bytes 294920 | tf_op jit(solution)/shard_map/ppermute | solution.py:192
  3.7 9.2 %collective-permute-start.1 = (bf16[64,768]{1,0:T(8,128)(2,1)}, bf16[64,768]{1,0:T(8,128)(2,1)S(1)}, u32[]{:S(2)}, u32[]{:S(2)}) collective-permute-start(bf16[64,768]{1,0:T(8,128)(2,1)} %param.9), channel_id=1, source_target_pairs={{0,2},{1,3},{2,0},{3,1},{4,6},{5,7},{6,4},{7,5},{8,10},{9,11},{10,... | collective-permute-start | bytes 294920 | tf_op jit(solution)/shard_map/ppermute | solution.py:192
  5.2 7.7 %collective-permute-start.2 = (bf16[64,768]{1,0:T(8,128)(2,1)}, bf16[64,768]{1,0:T(8,128)(2,1)S(1)}, u32[]{:S(2)}, u32[]{:S(2)}) collective-permute-start(bf16[64,768]{1,0:T(8,128)(2,1)} %param.9), channel_id=1, source_target_pairs={{0,3},{1,0},{2,1},{3,2},{4,7},{5,4},{6,5},{7,6},{8,11},{9,8},{10,9... | collective-permute-start | bytes 294920 | tf_op jit(solution)/shard_map/ppermute | solution.py:192
  7.3 27.1 %copy-start.24 = (s32[51]{0:T(128)}, s32[51]{0:T(128)S(1)}, u32[]{:S(2)}) copy-start(s32[51]{0:T(128)S(1)} %dynamic-slice_bitcast_fusion) | copy-start | bytes 616
  7.5 26.9 %copy-start.26 = (pred[256]{0:T(512)(128)(4,1)}, pred[256]{0:T(512)(128)(4,1)S(1)}, u32[]{:S(2)}) copy-start(pred[256]{0:T(512)(128)(4,1)S(1)} %broadcast_compare_fusion) | copy-start | bytes 772
  10.9 5.8 %copy-start.4 = (bf16[1024,3072]{1,0:T(8,128)(2,1)S(1)}, bf16[1024,3072]{1,0:T(8,128)(2,1)}, u32[]{:S(2)}) copy-start(bf16[1024,3072]{1,0:T(8,128)(2,1)} %param.12) | copy-start | bytes 18874372
  14.2 2.5 %copy-start.14 = (bf16[64,768]{1,0:T(8,128)(2,1)}, bf16[64,768]{1,0:T(8,128)(2,1)S(1)}, u32[]{:S(2)}) copy-start(bf16[64,768]{1,0:T(8,128)(2,1)S(1)} %get-tuple-element.17) | copy-start | bytes 294916
  14.2 2.5 %copy-start.16 = (bf16[64,768]{1,0:T(8,128)(2,1)}, bf16[64,768]{1,0:T(8,128)(2,1)S(1)}, u32[]{:S(2)}) copy-start(bf16[64,768]{1,0:T(8,128)(2,1)S(1)} %get-tuple-element.18) | copy-start | bytes 294916
  14.2 2.5 %copy-start.18 = (bf16[64,768]{1,0:T(8,128)(2,1)}, bf16[64,768]{1,0:T(8,128)(2,1)S(1)}, u32[]{:S(2)}) copy-start(bf16[64,768]{1,0:T(8,128)(2,1)S(1)} %get-tuple-element.19) | copy-start | bytes 294916
  14.2 2.5 %copy-start.20 = (bf16[64,768]{1,0:T(8,128)(2,1)}, bf16[64,768]{1,0:T(8,128)(2,1)S(1)}, u32[]{:S(2)}) copy-start(bf16[64,768]{1,0:T(8,128)(2,1)S(1)} %get-tuple-element.20) | copy-start | bytes 294916
  22.4 2.8 %copy-start.1 = (bf16[256,3072]{0,1:T(8,128)(2,1)S(1)}, bf16[256,3072]{0,1:T(8,128)(2,1)}, u32[]{:S(2)}) copy-start(bf16[256,3072]{0,1:T(8,128)(2,1)} %copy.63) | copy-start | bytes 4718596
  30.0 1.2 %copy-start.8 = (bf16[51,1,16,64]{3,2,1,0:T(8,128)(2,1)}, bf16[51,1,16,64]{3,2,1,0:T(8,128)(2,1)S(1)}, u32[]{:S(2)}) copy-start(bf16[51,1,16,64]{3,2,1,0:T(8,128)(2,1)S(1)} %get-tuple-element.16) | copy-start | bytes 313348
  30.0 1.2 %copy-start.10 = (bf16[51,1,16,64]{3,2,1,0:T(8,128)(2,1)}, bf16[51,1,16,64]{3,2,1,0:T(8,128)(2,1)S(1)}, u32[]{:S(2)}) copy-start(bf16[51,1,16,64]{3,2,1,0:T(8,128)(2,1)S(1)} %get-tuple-element.15) | copy-start | bytes 313348
  31.2 1.0 %copy-start.22 = (f32[16,51]{1,0:T(8,128)}, f32[16,51]{1,0:T(8,128)S(1)}, u32[]{:S(2)}) copy-start(f32[16,51]{1,0:T(8,128)S(1)} %get-tuple-element.25) | copy-start | bytes 9796
  38.9 0.9 %copy-start.2 = (f32[16,256,48]{1,2,0:T(8,128)}, f32[16,256,48]{1,2,0:T(8,128)S(1)}, u32[]{:S(2)}) copy-start(f32[16,256,48]{1,2,0:T(8,128)S(1)} %get-tuple-element.28) | copy-start | bytes 2359300
  47.7 2.0 %copy-start.3 = (f32[256,768]{1,0:T(8,128)S(1)}, f32[256,768]{1,0:T(8,128)}, u32[]{:S(2)}) copy-start(f32[256,768]{1,0:T(8,128)} %get-tuple-element.13) | copy-start | bytes 2359300
  47.7 2.0 %copy-start.5 = (bf16[256,768]{1,0:T(8,128)(2,1)S(1)}, bf16[256,768]{1,0:T(8,128)(2,1)}, u32[]{:S(2)}) copy-start(bf16[256,768]{1,0:T(8,128)(2,1)} %get-tuple-element.4) | copy-start | bytes 1179652
  50.6 3.9 %copy-start.23 = (f32[16,51]{1,0:T(8,128)S(1)}, f32[16,51]{1,0:T(8,128)}, u32[]{:S(2)}) copy-start(f32[16,51]{1,0:T(8,128)} %copy-done.22) | copy-start | bytes 9796
  57.3 2.4 %copy-start.11 = (bf16[51,1,16,64]{3,2,1,0:T(8,128)(2,1)S(1)}, bf16[51,1,16,64]{3,2,1,0:T(8,128)(2,1)}, u32[]{:S(2)}) copy-start(bf16[51,1,16,64]{3,2,1,0:T(8,128)(2,1)} %copy-done.10) | copy-start | bytes 313348
  58.0 1.9 %copy-start.7 = (bf16[51,1,16,64]{3,2,1,0:T(8,128)(2,1)S(1)}, bf16[51,1,16,64]{3,2,1,0:T(8,128)(2,1)}, u32[]{:S(2)}) copy-start(bf16[51,1,16,64]{3,2,1,0:T(8,128)(2,1)} %copy-done.6) | copy-start | bytes 313348
  58.0 1.9 %copy-start.9 = (bf16[51,1,16,64]{3,2,1,0:T(8,128)(2,1)S(1)}, bf16[51,1,16,64]{3,2,1,0:T(8,128)(2,1)}, u32[]{:S(2)}) copy-start(bf16[51,1,16,64]{3,2,1,0:T(8,128)(2,1)} %copy-done.8) | copy-start | bytes 313348
  58.2 1.4 %copy-start.13 = (f32[16,51,51]{1,2,0:T(8,128)S(1)}, f32[16,51,51]{1,2,0:T(8,128)}, u32[]{:S(2)}) copy-start(f32[16,51,51]{1,2,0:T(8,128)} %copy-done.12) | copy-start | bytes 499396
  60.0 1.0 %copy-start.15 = (bf16[64,768]{1,0:T(8,128)(2,1)S(1)}, bf16[64,768]{1,0:T(8,128)(2,1)}, u32[]{:S(2)}) copy-start(bf16[64,768]{1,0:T(8,128)(2,1)} %copy-done.14) | copy-start | bytes 294916
  60.0 1.0 %copy-start.17 = (bf16[64,768]{1,0:T(8,128)(2,1)S(1)}, bf16[64,768]{1,0:T(8,128)(2,1)}, u32[]{:S(2)}) copy-start(bf16[64,768]{1,0:T(8,128)(2,1)} %copy-done.16) | copy-start | bytes 294916
  60.0 1.0 %copy-start.19 = (bf16[64,768]{1,0:T(8,128)(2,1)S(1)}, bf16[64,768]{1,0:T(8,128)(2,1)}, u32[]{:S(2)}) copy-start(bf16[64,768]{1,0:T(8,128)(2,1)} %copy-done.18) | copy-start | bytes 294916
  60.0 1.0 %copy-start.21 = (bf16[64,768]{1,0:T(8,128)(2,1)S(1)}, bf16[64,768]{1,0:T(8,128)(2,1)}, u32[]{:S(2)}) copy-start(bf16[64,768]{1,0:T(8,128)(2,1)} %copy-done.20) | copy-start | bytes 294916
  63.2 4.8 %copy-start.27 = (f32[51]{0:T(128)S(1)}, f32[51]{0:T(128)}, u32[]{:S(2)}) copy-start(f32[51]{0:T(128)} %get-tuple-element.33) | copy-start | bytes 616
  63.2 7.7 %copy-start.25 = (s32[204]{0:T(256)S(1)}, s32[204]{0:T(256)}, u32[]{:S(2)}) copy-start(s32[204]{0:T(256)} %eq.93) | copy-start | bytes 2452
  68.7 5.3 %collective-permute-start.3 = (bf16[51,1024]{1,0:T(8,128)(2,1)S(1)}, bf16[51,1024]{1,0:T(8,128)(2,1)S(1)}, u32[]{:S(2)}, u32[]{:S(2)}) collective-permute-start(bf16[51,1024]{1,0:T(8,128)(2,1)S(1)} %fusion.91), channel_id=1, source_target_pairs={{0,3},{1,0},{2,1},{3,2},{4,7},{5,4},{6,5},{7,6},{8,11},{9,8},{10,9... | collective-permute-start | bytes 313352 | tf_op jit(solution)/shard_map/ppermute | solution.py:192
  69.3 5.9 %collective-permute-start.5 = (bf16[51,1024]{1,0:T(8,128)(2,1)S(1)}, bf16[51,1024]{1,0:T(8,128)(2,1)S(1)}, u32[]{:S(2)}, u32[]{:S(2)}) collective-permute-start(bf16[51,1024]{1,0:T(8,128)(2,1)S(1)} %fusion.91), channel_id=1, source_target_pairs={{0,1},{1,2},{2,3},{3,0},{4,5},{5,6},{6,7},{7,4},{8,9},{9,10},{10,1... | collective-permute-start | bytes 313352 | tf_op jit(solution)/shard_map/ppermute | solution.py:192
  70.8 5.6 %collective-permute-start.4 = (bf16[51,1024]{1,0:T(8,128)(2,1)S(1)}, bf16[51,1024]{1,0:T(8,128)(2,1)S(1)}, u32[]{:S(2)}, u32[]{:S(2)}) collective-permute-start(bf16[51,1024]{1,0:T(8,128)(2,1)S(1)} %fusion.91), channel_id=1, source_target_pairs={{0,2},{1,3},{2,0},{3,1},{4,6},{5,7},{6,4},{7,5},{8,10},{9,11},{10,... | collective-permute-start | bytes 313352 | tf_op jit(solution)/shard_map/ppermute | solution.py:192
  (2 other events, 1.5 us)

commit v21 on v18

--- a/solution.py
+++ b/solution.py
@@ -2,6 +2,7 @@
 import math
 
 import jax
+import numpy as np
 import jax.numpy as jnp
 from jax import lax
 from jax.experimental import pallas as pl
@@ -110,10 +111,14 @@
 
 
 def loss_kernel(hidden_ref, dec_out_ref, targets_ref, keep_ref, squares_ref, d_hidden_ref, *, scale):
+    rows = hidden_ref.shape[0]
+    slot_ids = lax.broadcasted_iota(jnp.int32, (rows, keep_ref.shape[1]), 0)
+    seen = jnp.max((slot_ids == keep_ref[...]).astype(jnp.float32), axis=1, keepdims=True)
+    keep = 1.0 - seen
     predicted = jnp.dot(hidden_ref[...], dec_out_ref[...], preferred_element_type=jnp.float32)
-    mismatch = (predicted - targets_ref[...].astype(jnp.float32)) * keep_ref[...]
+    mismatch = (predicted - targets_ref[...].astype(jnp.float32)) * keep
     squares_ref[...] = jnp.sum(mismatch * mismatch, keepdims=True)
-    d_predicted = (2.0 * scale * mismatch) * keep_ref[...]
+    d_predicted = (2.0 * scale * mismatch) * keep
     d_hidden = lax.dot_general(
         d_predicted.astype(jnp.bfloat16),
         dec_out_ref[...],
@@ -151,7 +156,7 @@
         d_hidden * ratio,
         jnp.zeros_like(dec_out),
         jnp.zeros_like(targets),
-        jnp.zeros_like(keep),
+        np.zeros(keep.shape, jax.dtypes.float0),
     )
 
 
@@ -180,9 +185,7 @@
     hidden = decoder_output(
         visible_out, positions, total_rows, mask_embed, dec_in, conv_w, dec_out
     )
-    slot_ids = jnp.arange(total_rows, dtype=jnp.int32)
-    seen = jnp.max((slot_ids[:, None] == positions[None, :]).astype(jnp.float32), axis=1)
-    return squares_of(hidden, dec_out, targets, (1.0 - seen)[:, None], scale)
+    return squares_of(hidden, dec_out, targets, positions[None, :], scale)
 
 
 def ring_gather(values, group_size):

time: 78.9 us -> 81.5 us (1.033)
  matrix products: 35.6 us -> 38.1 us
    dot_general x1, matrix products: 3.1 us -> 5.83 us  [project_rows(): jnp.dot(normed, w_qkv, preferred_element_type=jnp.float32)]
    dynamic_slice x0 -> x1, local copies, waits for them, and re-layouts: none -> 1.22 us  [on_device(): lax.dynamic_index_in_dim(visible_index, own_index, 0, keepdims=False)]
    unnamed x57 -> x55, local copies, waits for them, and re-layouts: 2.21 us -> 2.21 us
where the time goes in v21:
time: 81.5 us; the launch traced here: 80.8 us
  matrix products  38.1 us (47%)
  local copies, waits for them, and re-layouts  11.9 us (15%)
  other arithmetic  11 us (13%)
  starting transfers between devices  8.15 us (10%)
  waiting for transfers between devices  4.87 us (6%)
  Pallas kernels  3.54 us (4%)
  between operations  3.13 us (4%)
    ppermute x6, starting transfers between devices, ring_gather(): parts.append(lax.ppermute(values, 'mask', pairs))  8.15 us
    dot_general x6, matrix products, decoder_output(): jnp.einsum('pgi,gio->pgo', padded[offset:offset + total_rows], conv_w[off...  7.62 us
    dot_general x1, matrix products, project_rows(): jnp.dot(normed, w_qkv, preferred_element_type=jnp.float32)  5.83 us
    dot_general x1, matrix products, copy_terms(): branch = attention_from(reuse_rows(visible_in, w_qkv, projected), w_out)  4.89 us
    ppermute x6, waiting for transfers between devices, ring_gather(): parts.append(lax.ppermute(values, 'mask', pairs))  4.87 us
    dot_general x2, matrix products, decoder_output(): jnp.dot(visible_out, dec_in, preferred_element_type=jnp.float32)  4.38 us
    pallas_call x1, Pallas kernels, masked_squares(): pl.pallas_call(functools.partial(loss_kernel, scale=scale), out_shape=(ja...  3.54 us
    convert_element_type x1, other arithmetic, decoder_output(): return (lowered.astype(jnp.float32) + activated).astype(jnp.bfloat16)  2.97 us
  transfers between devices with their start and end apart: 6, of which 3 were waited for; matrix products, arithmetic and copies ran while one was open for 8% of the time, Pallas kernels for 0%

profile of v21, /device:TPU:0, one launch (start us, length us, event | category | flops | bytes accessed | tf_op | source)
XLA Modules:
  0.0 80.8 jit_solution(15142453607641480251)
XLA Ops:
  0.6 3.0 %collective-permute-start = (bf16[64,768]{1,0:T(8,128)(2,1)}, bf16[64,768]{1,0:T(8,128)(2,1)S(1)}, u32[]{:S(2)}, u32[]{:S(2)}) collective-permute-start(bf16[64,768]{1,0:T(8,128)(2,1)} %param.9), channel_id=1, source_target_pairs={{0,1},{1,2},{2,3},{3,0},{4,5},{5,6},{6,7},{7,4},{8,9},{9,10},{10,1... | collective-permute-start | bytes 294920 | tf_op jit(solution)/shard_map/ppermute | solution.py:195
  3.7 1.5 %collective-permute-start.1 = (bf16[64,768]{1,0:T(8,128)(2,1)}, bf16[64,768]{1,0:T(8,128)(2,1)S(1)}, u32[]{:S(2)}, u32[]{:S(2)}) collective-permute-start(bf16[64,768]{1,0:T(8,128)(2,1)} %param.9), channel_id=1, source_target_pairs={{0,2},{1,3},{2,0},{3,1},{4,6},{5,7},{6,4},{7,5},{8,10},{9,11},{10,... | collective-permute-start | bytes 294920 | tf_op jit(solution)/shard_map/ppermute | solution.py:195
  5.2 1.4 %collective-permute-start.2 = (bf16[64,768]{1,0:T(8,128)(2,1)}, bf16[64,768]{1,0:T(8,128)(2,1)S(1)}, u32[]{:S(2)}, u32[]{:S(2)}) collective-permute-start(bf16[64,768]{1,0:T(8,128)(2,1)} %param.9), channel_id=1, source_target_pairs={{0,3},{1,0},{2,1},{3,2},{4,7},{5,4},{6,5},{7,6},{8,11},{9,8},{10,9... | collective-permute-start | bytes 294920 | tf_op jit(solution)/shard_map/ppermute | solution.py:195
  8.1 1.2 %gather_fusion = s32[4,51]{1,0:T(4,128)S(1)} fusion(s32[4,51]{1,0:T(4,128)} %param.10, s32[1024]{0:T(1024)S(1)} %pad_clamp_fusion), kind=kCustom, calls=%fused_computation | custom fusion | bytes 1648 | tf_op jit(solution)/shard_map/gather | solution.py:280
  10.0 1.7 %convolution_reduce_fusion = bf16[768]{0:T(1024)(128)(2,1)S(1)} fusion(bf16[1024,1]{0,1:T(2,128)(2,1)S(1)} %reshape.270, bf16[1024,768]{1,0:T(8,128)(2,1)} %param.15), kind=kOutput, calls=%fused_computation.54 | convolution fusion | flops 1572864 | bytes 1576448 | tf_op jit(solution)/shard_map/jvp()/dot_general | solution.py:94
  11.7 1.2 %constant_dynamic-slice_fusion.keep_ref = s32[1,51]{1,0:T(1,128)} fusion(s32[4,51]{1,0:T(4,128)} %param.10, s32[]{:T(128)S(6)} %select_n.162), kind=kLoop, calls=%fused_computation.211 | loop fusion | bytes 412 | tf_op jit(solution)/shard_map/jit(dynamic_index_in_dim)/dynamic_slice | solution.py:239
  12.9 1.0 %select_select_fusion.3 = (bf16[64,768]{1,0:T(8,128)(2,1)S(1)}, bf16[64,768]{1,0:T(8,128)(2,1)S(1)}, bf16[64,768]{1,0:T(8,128)(2,1)S(1)}, bf16[64,768]{1,0:T(8,128)(2,1)S(1)}) fusion(bf16[64,768]{1,0:T(8,128)(2,1)S(1)} %collective-permute-done, bf16[64,768]{1,0:T(8,128)(2,1)S(1)} %collective-permute-done.1, bf16[64,768]{1,0:T(8,128)(2,1)S(1)} %collective-permute-done.2, ...), kind=kLoop, calls=%fused_computation.173 | loop fusion | flops 589824 | bytes 786444 | tf_op jit(solution)/shard_map/jit(_where)/select_n | solution.py:206
  13.9 2.2 %convert_reduce_fusion = (f32[256]{0:T(256)S(1)}, bf16[256,1024]{1,0:T(8,128)(2,1)S(1)}) fusion(bf16[768,1024]{1,0:T(8,128)(2,1)} %param.11, bf16[64,768]{1,0:T(8,128)(2,1)S(1)} %get-tuple-element.18, bf16[64,768]{1,0:T(8,128)(2,1)S(1)} %get-tuple-element.19, bf16[64,768]{1,0:T(8,128)(2,1)S(1)} %get-tuple-element.20, bf16[64,768]{1,0:T(8,128)(2,1)S(1)} %get-tuple-element.17), kind=kOutput, calls=%fused_computation.12 | convolution fusion | flops 405012224 | bytes 2491392 | tf_op jit(solution)/shard_map/dot_general | solution.py:241
  16.5 5.8 %convolution_convert_fusion = bf16[256,3072]{1,0:T(8,128)(2,1)} fusion(bf16[1024,3072]{1,0:T(8,128)(2,1)} %param.12, bf16[256,1024]{1,0:T(8,128)(2,1)S(1)} %get-tuple-element.24, f32[256]{0:T(256)S(1)} %add_rsqrt_fusion.3, f32[256]{0:T(256)S(1)} %broadcast_multiply_fusion.2), kind=kOutput, calls=%fused_computation.3 | convolution fusion | flops 1612447744 | bytes 8390656 | tf_op jit(solution)/shard_map/dot_general | solution.py:51
  22.3 2.6 %copy.62 = bf16[256,3072]{0,1:T(8,128)(2,1)} copy(bf16[256,3072]{1,0:T(8,128)(2,1)} %convolution_convert_fusion) | data formatting | bytes 3145728 | tf_op jit(solution)/shard_map/convert_element_type | solution.py:51
  24.9 1.9 %convolution_convert_fusion.1 = bf16[51,3072]{1,0:T(8,128)(2,1)S(1)} fusion(bf16[256,3072]{1,0:T(8,128)(2,1)} %convolution_convert_fusion, s32[51]{0:T(128)S(1)} %fusion.152), kind=kOutput, calls=%fused_computation.5 | convolution fusion | flops 80385792 | bytes 1886412 | tf_op jit(solution)/shard_map/dot_general | solution.py:252
  28.0 1.0 %fusion = (f32[16,256]{1,0:T(8,128)S(1)}, f32[16,256,256]{1,2,0:T(8,128)S(1)}) fusion(f32[256,16]{0,1:T(8,128)S(1)} %get-tuple-element.43, bf16[256,3,16,64]{0,3,2,1:T(8,128)(2,1)S(1)} %bitcast.163, f32[256,16]{0,1:T(8,128)S(1)} %get-tuple-element.44), kind=kOutput, calls=%fused_computation.4 | convolution fusion | flops 137883648 | bytes 5292032 | tf_op jit(solution)/shard_map/qhd,khd->hqk/dot_general | solution.py:34
  30.9 1.0 %multiply_convert_fusion.targets_ref = bf16[256,1024]{1,0:T(8,128)(2,1)} fusion(f32[256,1024]{1,0:T(8,128)S(1)} %get-tuple-element.32, f32[256]{0:T(256)S(1)} %add_rsqrt_fusion.2, f32[256]{0:T(256)S(1)} %broadcast_multiply_fusion.1), kind=kLoop, calls=%fused_computation.61 | loop fusion | flops 786432 | bytes 1574912 | tf_op jit(solution)/shard_map/convert_element_type | solution.py:258
  34.6 2.2 %convolution_convert_fusion.17 = bf16[51,768]{1,0:T(8,128)(2,1)S(1)} fusion(bf16[1024,768]{1,0:T(8,128)(2,1)} %param.15, f32[51,1024]{1,0:T(8,128)S(1)} %get-tuple-element.34, bf16[51,1024]{1,0:T(8,128)(2,1)S(1)} %reshape.248, bf16[1024,1024]{1,0:T(8,128)(2,1)S(1)} %copy-done), kind=kOutput, calls=%fused_computation.52 | convolution fusion | flops 187314432 | bytes 4061696 | tf_op jit(solution)/shard_map/jvp()/dot_general | solution.py:91
  37.4 1.3 %fusion.67 = f32[16,256,48]{1,2,0:T(8,128)S(1)} fusion(bf16[256,16,48]{0,2,1:T(8,128)(2,1)S(1)} %bitcast.169, bf16[3,16,48,48]{3,2,1,0:T(8,128)(2,1)} %param.16), kind=kOutput, calls=%fused_computation.131 | convolution fusion | flops 18874368 | bytes 1376256 | tf_op jit(solution)/shard_map/jvp(pgi,gio->pgo)/dot_general | solution.py:103
  38.8 1.2 %convolution_add_fusion.1 = f32[16,256,48]{1,2,0:T(8,128)S(1)} fusion(f32[16,256,48]{1,2,0:T(8,128)S(1)} %fusion.67, bf16[256,16,48]{0,2,1:T(8,128)(2,1)S(1)} %bitcast.170, bf16[3,16,48,48]{3,2,1,0:T(8,128)(2,1)} %param.16), kind=kOutput, calls=%fused_computation.15 | convolution fusion | flops 19070976 | bytes 2162688 | tf_op jit(solution)/shard_map/jvp(pgi,gio->pgo)/dot_general | solution.py:103
  40.0 1.4 %fusion.128 = (f32[256]{0:T(256)S(1)}, f32[16,256,48]{1,2,0:T(8,128)S(1)}) fusion(f32[16,256,48]{1,2,0:T(8,128)S(1)} %convolution_add_fusion.1, bf16[256,16,48]{0,2,1:T(8,128)(2,1)S(1)} %bitcast.171, bf16[3,16,48,48]{3,2,1,0:T(8,128)(2,1)} %param.16), kind=kOutput, calls=%fused_computation.225 | convolution fusion | flops 19267328 | bytes 2163712 | tf_op jit(solution)/shard_map/jvp(pgi,gio->pgo)/dot_general | solution.py:103
  42.2 1.4 %copy.61 = f32[256,768]{1,0:T(8,128)S(1)} copy(f32[256,768]{0,1:T(8,128)} %bitcast.165) | data formatting | bytes 1572864 | tf_op jit(solution)/shard_map/jvp()/reshape | solution.py:109
  43.6 3.0 %add_convert_fusion = (bf16[256,768]{1,0:T(8,128)(2,1)}, f32[256,768]{1,0:T(8,128)}) fusion(bf16[256,768]{1,0:T(8,128)(2,1)S(1)} %fusion.3, f32[256,768]{1,0:T(8,128)S(1)} %copy.61, f32[256]{0:T(256)S(1)} %fusion.111, f32[256]{0:T(256)S(1)} %broadcast_multiply_fusion), kind=kLoop, calls=%fused_computation.86 | loop fusion | flops 13565952 | bytes 2361344 | tf_op jit(solution)/shard_map/jvp()/convert_element_type | solution.py:110
  46.6 3.5 %jvp__.1 = (f32[1,1]{1,0:T(1,128)}, bf16[256,768]{1,0:T(8,128)(2,1)}) custom-call(bf16[256,768]{1,0:T(8,128)(2,1)} %get-tuple-element.12.hidden_ref, bf16[768,1024]{1,0:T(8,128)(2,1)} %dec_out_ref.1, bf16[256,1024]{1,0:T(8,128)(2,1)} %multiply_convert_fusion.targets_ref, s32[1,51]{1,0:T(1,128)} %constant_dynamic-slice_fusion.keep_ref), custom_call_target="tpu_custom_call" | custom-call | tf_op jit(solution)/shard_map/jvp()/pallas_call | solution.py:133
  50.2 2.0 %multiply_reduce_fusion.1 = f32[256]{0:T(256)S(1)} fusion(f32[256,768]{1,0:T(8,128)S(1)} %copy.61, f32[256]{0:T(256)S(1)} %broadcast_multiply_fusion, f32[256,768]{1,0:T(8,128)} %get-tuple-element.13, bf16[256,768]{1,0:T(8,128)(2,1)} %get-tuple-element.4, f32[256]{0:T(256)S(1)} %fusion.111), kind=kLoop, calls=%fused_computation.85 | loop fusion | flops 3538688 | bytes 1969152 | tf_op jit(solution)/shard_map/transpose(jvp())/reduce_sum | solution.py:24
  53.3 1.4 %fusion.7 = bf16[256,16,48]{0,2,1:T(8,128)(2,1)S(1)} fusion(bf16[16,48,256]{2,1,0:T(8,128)(2,1)S(1)} %bitcast.166, bf16[3,16,48,48]{3,2,1,0:T(8,128)(2,1)} %param.16), kind=kOutput, calls=%fused_computation.26 | convolution fusion | flops 18874368 | bytes 983040 | tf_op jit(solution)/shard_map/transpose(jvp(pgi,gio->pgo))/dot_general | solution.py:103
  54.6 1.2 %fusion.8 = bf16[256,16,48]{0,2,1:T(8,128)(2,1)S(1)} fusion(bf16[16,48,256]{2,1,0:T(8,128)(2,1)S(1)} %bitcast.167, bf16[3,16,48,48]{3,2,1,0:T(8,128)(2,1)} %param.16), kind=kOutput, calls=%fused_computation.27 | convolution fusion | flops 18874368 | bytes 983040 | tf_op jit(solution)/shard_map/transpose(jvp(pgi,gio->pgo))/dot_general | solution.py:103
  55.8 1.2 %fusion.9 = bf16[256,16,48]{0,2,1:T(8,128)(2,1)S(1)} fusion(bf16[16,48,256]{2,1,0:T(8,128)(2,1)S(1)} %bitcast.168, bf16[3,16,48,48]{3,2,1,0:T(8,128)(2,1)} %param.16), kind=kOutput, calls=%fused_computation.28 | convolution fusion | flops 18874368 | bytes 983040 | tf_op jit(solution)/shard_map/transpose(jvp(pgi,gio->pgo))/dot_general | solution.py:103
  57.5 2.2 %convolution_convert_fusion.12 = bf16[51,1024]{1,0:T(8,128)(2,1)S(1)} fusion(bf16[1024,768]{1,0:T(8,128)(2,1)} %param.15, bf16[256,768]{1,0:T(8,128)(2,1)S(1)} %copy-done.4, bf16[256,768]{1,0:T(8,128)(2,1)S(1)} %copy.68, pred[256]{0:T(512)(128)(4,1)} %copy-done.25, s32[51]{0:T(128)} %copy-done.23), kind=kOutput, calls=%fused_computation.46 | convolution fusion | flops 100964352 | bytes 2464204 | tf_op jit(solution)/shard_map/transpose(jvp())/dot_general | solution.py:91
  60.7 1.4 %fusion.16 = bf16[51,1,16,64]{3,0,2,1:T(8,128)(2,1)S(1)} fusion(bf16[51,16,64]{2,1,0:T(8,128)(2,1)S(1)} %reshape.255, f32[16,51,51]{1,2,0:T(8,128)} %copy-done.11, f32[16,51]{1,0:T(8,128)S(1)} %copy-done.22), kind=kOutput, calls=%fused_computation.42 | convolution fusion | flops 5462304 | bytes 378624 | tf_op jit(solution)/shard_map/transpose(jvp(hqk,khd->qhd))/dot_general | solution.py:39
  64.9 4.9 %convolution_convert_fusion.11 = bf16[51,1024]{1,0:T(8,128)(2,1)S(1)} fusion(bf16[51,3072]{1,0:T(8,128)(2,1)S(1)} %reshape.256, bf16[1024,3072]{1,0:T(8,128)(2,1)} %param.12), kind=kOutput, calls=%fused_computation.45 | convolution fusion | flops 320916480 | bytes 6709248 | tf_op jit(solution)/shard_map/transpose(jvp())/dot_general | solution.py:183
  71.0 1.5 %collective-permute-start.4 = (bf16[51,1024]{1,0:T(8,128)(2,1)S(1)}, bf16[51,1024]{1,0:T(8,128)(2,1)S(1)}, u32[]{:S(2)}, u32[]{:S(2)}) collective-permute-start(bf16[51,1024]{1,0:T(8,128)(2,1)S(1)} %fusion.99), channel_id=1, source_target_pairs={{0,2},{1,3},{2,0},{3,1},{4,6},{5,7},{6,4},{7,5},{8,10},{9,11},{10,... | collective-permute-start | bytes 313352 | tf_op jit(solution)/shard_map/ppermute | solution.py:195
  73.4 2.6 %collective-permute-done.3 = bf16[51,1024]{1,0:T(8,128)(2,1)S(1)} collective-permute-done((bf16[51,1024]{1,0:T(8,128)(2,1)S(1)}, bf16[51,1024]{1,0:T(8,128)(2,1)S(1)}, u32[]{:S(2)}, u32[]{:S(2)}) %collective-permute-start.3) | collective-permute-done | bytes 104480 | tf_op jit(solution)/shard_map/ppermute | solution.py:195
  75.9 1.0 %collective-permute-done.4 = bf16[51,1024]{1,0:T(8,128)(2,1)S(1)} collective-permute-done((bf16[51,1024]{1,0:T(8,128)(2,1)S(1)}, bf16[51,1024]{1,0:T(8,128)(2,1)S(1)}, u32[]{:S(2)}, u32[]{:S(2)}) %collective-permute-start.4) | collective-permute-done | bytes 104480 | tf_op jit(solution)/shard_map/ppermute | solution.py:195
  77.0 1.3 %collective-permute-done.5 = bf16[51,1024]{1,0:T(8,128)(2,1)S(1)} collective-permute-done((bf16[51,1024]{1,0:T(8,128)(2,1)S(1)}, bf16[51,1024]{1,0:T(8,128)(2,1)S(1)}, u32[]{:S(2)}, u32[]{:S(2)}) %collective-permute-start.5) | collective-permute-done | bytes 104480 | tf_op jit(solution)/shard_map/ppermute | solution.py:195
  78.2 1.4 %fusion.19 = f32[192,1024]{1,0:T(8,128)} fusion(bf16[51,1024]{1,0:T(8,128)(2,1)S(1)} %collective-permute-done.5, bf16[51,1024]{1,0:T(8,128)(2,1)S(1)} %collective-permute-done.4, bf16[51,1024]{1,0:T(8,128)(2,1)S(1)} %collective-permute-done.3, bf16[51,1024]{1,0:T(8,128)(2,1)S(1)} %fusion.99, bf16[256,768]{1,0:T(8,128)(2,1)S(1)} %pad_maximum_fusion, ...), kind=kOutput, calls=%fused_computation.53 | convolution fusion | flops 102032640 | bytes 1377284 | tf_op jit(solution)/shard_map/vc,vd->cd/dot_general | solution.py:286
  (119 shorter events, 16.1 us)
Async XLA Ops:
  0.6 29.2 %copy-start = (bf16[1024,1024]{1,0:T(8,128)(2,1)S(1)}, bf16[1024,1024]{1,0:T(8,128)(2,1)}, u32[]{:S(2)}) copy-start(bf16[1024,1024]{1,0:T(8,128)(2,1)} %param.13) | copy-start | bytes 6291460
  0.6 12.3 %collective-permute-start = (bf16[64,768]{1,0:T(8,128)(2,1)}, bf16[64,768]{1,0:T(8,128)(2,1)S(1)}, u32[]{:S(2)}, u32[]{:S(2)}) collective-permute-start(bf16[64,768]{1,0:T(8,128)(2,1)} %param.9), channel_id=1, source_target_pairs={{0,1},{1,2},{2,3},{3,0},{4,5},{5,6},{6,7},{7,4},{8,9},{9,10},{10,1... | collective-permute-start | bytes 294920 | tf_op jit(solution)/shard_map/ppermute | solution.py:195
  3.7 9.3 %collective-permute-start.1 = (bf16[64,768]{1,0:T(8,128)(2,1)}, bf16[64,768]{1,0:T(8,128)(2,1)S(1)}, u32[]{:S(2)}, u32[]{:S(2)}) collective-permute-start(bf16[64,768]{1,0:T(8,128)(2,1)} %param.9), channel_id=1, source_target_pairs={{0,2},{1,3},{2,0},{3,1},{4,6},{5,7},{6,4},{7,5},{8,10},{9,11},{10,... | collective-permute-start | bytes 294920 | tf_op jit(solution)/shard_map/ppermute | solution.py:195
  5.2 7.8 %collective-permute-start.2 = (bf16[64,768]{1,0:T(8,128)(2,1)}, bf16[64,768]{1,0:T(8,128)(2,1)S(1)}, u32[]{:S(2)}, u32[]{:S(2)}) collective-permute-start(bf16[64,768]{1,0:T(8,128)(2,1)} %param.9), channel_id=1, source_target_pairs={{0,3},{1,0},{2,1},{3,2},{4,7},{5,4},{6,5},{7,6},{8,11},{9,8},{10,9... | collective-permute-start | bytes 294920 | tf_op jit(solution)/shard_map/ppermute | solution.py:195
  7.3 29.5 %copy-start.23 = (s32[51]{0:T(128)}, s32[51]{0:T(128)S(1)}, u32[]{:S(2)}) copy-start(s32[51]{0:T(128)S(1)} %fusion.152) | copy-start | bytes 616
  7.4 29.4 %copy-start.25 = (pred[256]{0:T(512)(128)(4,1)}, pred[256]{0:T(512)(128)(4,1)S(1)}, u32[]{:S(2)}) copy-start(pred[256]{0:T(512)(128)(4,1)S(1)} %broadcast_compare_fusion) | copy-start | bytes 772
  13.9 2.5 %copy-start.13 = (bf16[64,768]{1,0:T(8,128)(2,1)}, bf16[64,768]{1,0:T(8,128)(2,1)S(1)}, u32[]{:S(2)}) copy-start(bf16[64,768]{1,0:T(8,128)(2,1)S(1)} %get-tuple-element.17) | copy-start | bytes 294916
  13.9 2.5 %copy-start.15 = (bf16[64,768]{1,0:T(8,128)(2,1)}, bf16[64,768]{1,0:T(8,128)(2,1)S(1)}, u32[]{:S(2)}) copy-start(bf16[64,768]{1,0:T(8,128)(2,1)S(1)} %get-tuple-element.18) | copy-start | bytes 294916
  13.9 2.5 %copy-start.17 = (bf16[64,768]{1,0:T(8,128)(2,1)}, bf16[64,768]{1,0:T(8,128)(2,1)S(1)}, u32[]{:S(2)}) copy-start(bf16[64,768]{1,0:T(8,128)(2,1)S(1)} %get-tuple-element.19) | copy-start | bytes 294916
  13.9 2.5 %copy-start.19 = (bf16[64,768]{1,0:T(8,128)(2,1)}, bf16[64,768]{1,0:T(8,128)(2,1)S(1)}, u32[]{:S(2)}) copy-start(bf16[64,768]{1,0:T(8,128)(2,1)S(1)} %get-tuple-element.20) | copy-start | bytes 294916
  24.9 2.8 %copy-start.1 = (bf16[256,3072]{0,1:T(8,128)(2,1)S(1)}, bf16[256,3072]{0,1:T(8,128)(2,1)}, u32[]{:S(2)}) copy-start(bf16[256,3072]{0,1:T(8,128)(2,1)} %copy.62) | copy-start | bytes 4718596
  32.4 1.2 %copy-start.7 = (bf16[51,1,16,64]{3,2,1,0:T(8,128)(2,1)}, bf16[51,1,16,64]{3,2,1,0:T(8,128)(2,1)S(1)}, u32[]{:S(2)}) copy-start(bf16[51,1,16,64]{3,2,1,0:T(8,128)(2,1)S(1)} %get-tuple-element.16) | copy-start | bytes 313348
  32.4 1.2 %copy-start.9 = (bf16[51,1,16,64]{3,2,1,0:T(8,128)(2,1)}, bf16[51,1,16,64]{3,2,1,0:T(8,128)(2,1)S(1)}, u32[]{:S(2)}) copy-start(bf16[51,1,16,64]{3,2,1,0:T(8,128)(2,1)S(1)} %get-tuple-element.15) | copy-start | bytes 313348
  33.6 0.8 copy-start.11
  33.7 1.0 %copy-start.21 = (f32[16,51]{1,0:T(8,128)}, f32[16,51]{1,0:T(8,128)S(1)}, u32[]{:S(2)}) copy-start(f32[16,51]{1,0:T(8,128)S(1)} %get-tuple-element.25) | copy-start | bytes 9796
  41.4 0.9 %copy-start.2 = (f32[16,256,48]{1,2,0:T(8,128)}, f32[16,256,48]{1,2,0:T(8,128)S(1)}, u32[]{:S(2)}) copy-start(f32[16,256,48]{1,2,0:T(8,128)S(1)} %get-tuple-element.28) | copy-start | bytes 2359300
  50.2 2.0 %copy-start.3 = (f32[256,768]{1,0:T(8,128)S(1)}, f32[256,768]{1,0:T(8,128)}, u32[]{:S(2)}) copy-start(f32[256,768]{1,0:T(8,128)} %get-tuple-element.13) | copy-start | bytes 2359300
  50.2 2.0 %copy-start.4 = (bf16[256,768]{1,0:T(8,128)(2,1)S(1)}, bf16[256,768]{1,0:T(8,128)(2,1)}, u32[]{:S(2)}) copy-start(bf16[256,768]{1,0:T(8,128)(2,1)} %get-tuple-element.4) | copy-start | bytes 1179652
  53.1 3.9 %copy-start.22 = (f32[16,51]{1,0:T(8,128)S(1)}, f32[16,51]{1,0:T(8,128)}, u32[]{:S(2)}) copy-start(f32[16,51]{1,0:T(8,128)} %copy-done.21) | copy-start | bytes 9796
  59.7 2.4 %copy-start.10 = (bf16[51,1,16,64]{3,2,1,0:T(8,128)(2,1)S(1)}, bf16[51,1,16,64]{3,2,1,0:T(8,128)(2,1)}, u32[]{:S(2)}) copy-start(bf16[51,1,16,64]{3,2,1,0:T(8,128)(2,1)} %copy-done.9) | copy-start | bytes 313348
  60.5 1.9 %copy-start.6 = (bf16[51,1,16,64]{3,2,1,0:T(8,128)(2,1)S(1)}, bf16[51,1,16,64]{3,2,1,0:T(8,128)(2,1)}, u32[]{:S(2)}) copy-start(bf16[51,1,16,64]{3,2,1,0:T(8,128)(2,1)} %copy-done.5) | copy-start | bytes 313348
  60.5 1.9 %copy-start.8 = (bf16[51,1,16,64]{3,2,1,0:T(8,128)(2,1)S(1)}, bf16[51,1,16,64]{3,2,1,0:T(8,128)(2,1)}, u32[]{:S(2)}) copy-start(bf16[51,1,16,64]{3,2,1,0:T(8,128)(2,1)} %copy-done.7) | copy-start | bytes 313348
  60.7 1.4 %copy-start.12 = (f32[16,51,51]{1,2,0:T(8,128)S(1)}, f32[16,51,51]{1,2,0:T(8,128)}, u32[]{:S(2)}) copy-start(f32[16,51,51]{1,2,0:T(8,128)} %copy-done.11) | copy-start | bytes 499396
  64.8 5.0 %copy-start.26 = (f32[51]{0:T(128)S(1)}, f32[51]{0:T(128)}, u32[]{:S(2)}) copy-start(f32[51]{0:T(128)} %get-tuple-element.33) | copy-start | bytes 616
  64.8 8.5 %copy-start.14 = (bf16[64,768]{1,0:T(8,128)(2,1)S(1)}, bf16[64,768]{1,0:T(8,128)(2,1)}, u32[]{:S(2)}) copy-start(bf16[64,768]{1,0:T(8,128)(2,1)} %copy-done.13) | copy-start | bytes 294916
  64.8 8.5 %copy-start.16 = (bf16[64,768]{1,0:T(8,128)(2,1)S(1)}, bf16[64,768]{1,0:T(8,128)(2,1)}, u32[]{:S(2)}) copy-start(bf16[64,768]{1,0:T(8,128)(2,1)} %copy-done.15) | copy-start | bytes 294916
  64.8 8.5 %copy-start.18 = (bf16[64,768]{1,0:T(8,128)(2,1)S(1)}, bf16[64,768]{1,0:T(8,128)(2,1)}, u32[]{:S(2)}) copy-start(bf16[64,768]{1,0:T(8,128)(2,1)} %copy-done.17) | copy-start | bytes 294916
  64.9 8.5 %copy-start.20 = (bf16[64,768]{1,0:T(8,128)(2,1)S(1)}, bf16[64,768]{1,0:T(8,128)(2,1)}, u32[]{:S(2)}) copy-start(bf16[64,768]{1,0:T(8,128)(2,1)} %copy-done.19) | copy-start | bytes 294916
  64.9 13.4 %copy-start.24 = (s32[204]{0:T(256)S(1)}, s32[204]{0:T(256)}, u32[]{:S(2)}) copy-start(s32[204]{0:T(256)} %eq.86) | copy-start | bytes 2452
  70.4 5.5 %collective-permute-start.3 = (bf16[51,1024]{1,0:T(8,128)(2,1)S(1)}, bf16[51,1024]{1,0:T(8,128)(2,1)S(1)}, u32[]{:S(2)}, u32[]{:S(2)}) collective-permute-start(bf16[51,1024]{1,0:T(8,128)(2,1)S(1)} %fusion.99), channel_id=1, source_target_pairs={{0,3},{1,0},{2,1},{3,2},{4,7},{5,4},{6,5},{7,6},{8,11},{9,8},{10,9... | collective-permute-start | bytes 313352 | tf_op jit(solution)/shard_map/ppermute | solution.py:195
  71.0 6.0 %collective-permute-start.4 = (bf16[51,1024]{1,0:T(8,128)(2,1)S(1)}, bf16[51,1024]{1,0:T(8,128)(2,1)S(1)}, u32[]{:S(2)}, u32[]{:S(2)}) collective-permute-start(bf16[51,1024]{1,0:T(8,128)(2,1)S(1)} %fusion.99), channel_id=1, source_target_pairs={{0,2},{1,3},{2,0},{3,1},{4,6},{5,7},{6,4},{7,5},{8,10},{9,11},{10,... | collective-permute-start | bytes 313352 | tf_op jit(solution)/shard_map/ppermute | solution.py:195
  72.5 5.7 %collective-permute-start.5 = (bf16[51,1024]{1,0:T(8,128)(2,1)S(1)}, bf16[51,1024]{1,0:T(8,128)(2,1)S(1)}, u32[]{:S(2)}, u32[]{:S(2)}) collective-permute-start(bf16[51,1024]{1,0:T(8,128)(2,1)S(1)} %fusion.99), channel_id=1, source_target_pairs={{0,1},{1,2},{2,3},{3,0},{4,5},{5,6},{6,7},{7,4},{8,9},{9,10},{10,1... | collective-permute-start | bytes 313352 | tf_op jit(solution)/shard_map/ppermute | solution.py:195
  (1 other events, 0.7 us)

commit v22 on v18

--- a/solution.py
+++ b/solution.py
@@ -86,15 +86,15 @@
 def decoder_output(visible_out, positions, total_rows, mask_embed, dec_in, conv_w, dec_out):
     slot_ids = jnp.arange(total_rows, dtype=jnp.int32)
     picks = (slot_ids[:, None] == positions[None, :]).astype(jnp.bfloat16)
-    seen = jnp.max(picks, axis=1, keepdims=True)
-    lowered_visible = jnp.dot(visible_out, dec_in, preferred_element_type=jnp.float32).astype(
-        jnp.bfloat16
-    )
-    lowered_mask = jnp.dot(
-        mask_embed[None, :], dec_in, preferred_element_type=jnp.float32
-    ).astype(jnp.bfloat16)
-    placed = jnp.dot(picks, lowered_visible, preferred_element_type=jnp.float32)
-    lowered = jnp.where(seen > 0, placed, lowered_mask.astype(jnp.float32)).astype(jnp.bfloat16)
+    unseen = 1.0 - jnp.max(picks, axis=1, keepdims=True)
+    picks = jnp.concatenate([picks, unseen], axis=1)
+    distinct_rows = jnp.concatenate([visible_out, mask_embed[None, :]], axis=0)
+    lowered_rows = jnp.dot(distinct_rows, dec_in, preferred_element_type=jnp.float32).astype(
+        jnp.bfloat16
+    )
+    lowered = jnp.dot(picks, lowered_rows, preferred_element_type=jnp.float32).astype(
+        jnp.bfloat16
+    )
     grouped = lowered.reshape(total_rows, GROUPS, DD // GROUPS)
     padded = jnp.pad(grouped, ((1, 1), (0, 0), (0, 0)))
     convolved = jnp.zeros((total_rows, GROUPS, DD // GROUPS), jnp.float32)

time: 78.9 us -> 82.5 us (1.046)
  other arithmetic: 11.5 us -> 14.5 us
    dot_general x1, matrix products: 3.1 us -> 5.83 us  [project_rows(): jnp.dot(normed, w_qkv, preferred_element_type=jnp.float32)]
    dot_general x4 -> x2, matrix products: 6.64 us -> 4.12 us  [the longest x1 2.08 us: decoder_output(): jnp.dot(distinct_rows, dec_in, preferred_element_type=jnp.float32)]
    unnamed x57 -> x68, local copies, waits for them, and re-layouts: 2.21 us -> 0.86 us
    dot_general x2 -> x3, matrix products: 1.58 us -> 2.06 us  [attention_from(): jnp.dot(context.reshape(row_count, D), w_out, preferred_element_type=jnp....]
  transfers between devices with their start and end apart: 6 -> 6, of which waited for: 3 -> 2; matrix products, arithmetic and copies ran while one was open for 8% -> 5% of each run, Pallas kernels for 0% -> 0%
where the time goes in v22:
time: 82.5 us; the launch traced here: 81.8 us
  matrix products  36.3 us (44%)
  other arithmetic  14.5 us (18%)
  local copies, waits for them, and re-layouts  10.9 us (13%)
  starting transfers between devices  8.47 us (10%)
  waiting for transfers between devices  5.02 us (6%)
  Pallas kernels  3.53 us (4%)
  between operations  3.18 us (4%)
    ppermute x6, starting transfers between devices, ring_gather(): parts.append(lax.ppermute(values, 'mask', pairs))  8.47 us
    dot_general x6, matrix products, decoder_output(): jnp.einsum('pgi,gio->pgo', padded[offset:offset + total_rows], conv_w[off...  7.62 us
    dot_general x1, matrix products, project_rows(): jnp.dot(normed, w_qkv, preferred_element_type=jnp.float32)  5.83 us
    ppermute x6, waiting for transfers between devices, ring_gather(): parts.append(lax.ppermute(values, 'mask', pairs))  5.02 us
    dot_general x1, matrix products, copy_terms(): branch = attention_from(reuse_rows(visible_in, w_qkv, projected), w_out)  4.89 us
    convert_element_type x1, other arithmetic, decoder_output(): return (lowered.astype(jnp.float32) + activated).astype(jnp.bfloat16)  3.65 us
    pallas_call x1, Pallas kernels, masked_squares(): pl.pallas_call(functools.partial(loss_kernel, scale=scale), out_shape=(ja...  3.53 us
    dot_general x4, matrix products, mix_heads(): jnp.einsum('hqk,khd->qhd', weights, values, preferred_element_type=jnp.fl...  2.81 us
  transfers between devices with their start and end apart: 6, of which 2 were waited for; matrix products, arithmetic and copies ran while one was open for 5% of the time, Pallas kernels for 0%

profile of v22, /device:TPU:0, one launch (start us, length us, event | category | flops | bytes accessed | tf_op | source)
XLA Modules:
  0.0 81.8 jit_solution(6684539591794851393)
XLA Ops:
  0.6 3.0 %collective-permute-start = (bf16[64,768]{1,0:T(8,128)(2,1)}, bf16[64,768]{1,0:T(8,128)(2,1)S(1)}, u32[]{:S(2)}, u32[]{:S(2)}) collective-permute-start(bf16[64,768]{1,0:T(8,128)(2,1)} %param.9), channel_id=1, source_target_pairs={{0,1},{1,2},{2,3},{3,0},{4,5},{5,6},{6,7},{7,4},{8,9},{9,10},{10,1... | collective-permute-start | bytes 294920 | tf_op jit(solution)/shard_map/ppermute | solution.py:192
  3.7 1.5 %collective-permute-start.1 = (bf16[64,768]{1,0:T(8,128)(2,1)}, bf16[64,768]{1,0:T(8,128)(2,1)S(1)}, u32[]{:S(2)}, u32[]{:S(2)}) collective-permute-start(bf16[64,768]{1,0:T(8,128)(2,1)} %param.9), channel_id=1, source_target_pairs={{0,2},{1,3},{2,0},{3,1},{4,6},{5,7},{6,4},{7,5},{8,10},{9,11},{10,... | collective-permute-start | bytes 294920 | tf_op jit(solution)/shard_map/ppermute | solution.py:192
  5.2 1.4 %collective-permute-start.2 = (bf16[64,768]{1,0:T(8,128)(2,1)}, bf16[64,768]{1,0:T(8,128)(2,1)S(1)}, u32[]{:S(2)}, u32[]{:S(2)}) collective-permute-start(bf16[64,768]{1,0:T(8,128)(2,1)} %param.9), channel_id=1, source_target_pairs={{0,3},{1,0},{2,1},{3,2},{4,7},{5,4},{6,5},{7,6},{8,11},{9,8},{10,9... | collective-permute-start | bytes 294920 | tf_op jit(solution)/shard_map/ppermute | solution.py:192
  9.1 1.2 %gather_fusion = s32[4,51]{1,0:T(4,128)S(1)} fusion(s32[4,51]{1,0:T(4,128)} %param.10, s32[1024]{0:T(1024)S(1)} %pad_clamp_fusion), kind=kCustom, calls=%fused_computation | custom fusion | bytes 1648 | tf_op jit(solution)/shard_map/gather | solution.py:277
  11.0 1.0 %select_select_fusion.3 = (bf16[64,768]{1,0:T(8,128)(2,1)S(1)}, bf16[64,768]{1,0:T(8,128)(2,1)S(1)}, bf16[64,768]{1,0:T(8,128)(2,1)S(1)}, bf16[64,768]{1,0:T(8,128)(2,1)S(1)}) fusion(bf16[64,768]{1,0:T(8,128)(2,1)S(1)} %collective-permute-done, bf16[64,768]{1,0:T(8,128)(2,1)S(1)} %collective-permute-done.1, bf16[64,768]{1,0:T(8,128)(2,1)S(1)} %collective-permute-done.2, ...), kind=kLoop, calls=%fused_computation.171 | loop fusion | flops 589824 | bytes 786444 | tf_op jit(solution)/shard_map/jit(_where)/select_n | solution.py:203
  12.0 2.2 %convert_reduce_fusion = (f32[256]{0:T(256)S(1)}, bf16[256,1024]{1,0:T(8,128)(2,1)S(1)}) fusion(bf16[768,1024]{1,0:T(8,128)(2,1)} %param.11, bf16[64,768]{1,0:T(8,128)(2,1)S(1)} %get-tuple-element.18, bf16[64,768]{1,0:T(8,128)(2,1)S(1)} %get-tuple-element.19, bf16[64,768]{1,0:T(8,128)(2,1)S(1)} %get-tuple-element.20, bf16[64,768]{1,0:T(8,128)(2,1)S(1)} %get-tuple-element.17), kind=kOutput, calls=%fused_computation.12 | convolution fusion | flops 405012224 | bytes 2491392 | tf_op jit(solution)/shard_map/dot_general | solution.py:238
  14.6 5.8 %convolution_convert_fusion = bf16[256,3072]{1,0:T(8,128)(2,1)} fusion(bf16[1024,3072]{1,0:T(8,128)(2,1)} %param.12, bf16[256,1024]{1,0:T(8,128)(2,1)S(1)} %get-tuple-element.26, f32[256]{0:T(256)S(1)} %add_rsqrt_fusion.3, f32[256]{0:T(256)S(1)} %broadcast_multiply_fusion.2), kind=kOutput, calls=%fused_computation.3 | convolution fusion | flops 1612447744 | bytes 8390656 | tf_op jit(solution)/shard_map/dot_general | solution.py:50
  20.4 2.6 %copy.64 = bf16[256,3072]{0,1:T(8,128)(2,1)} copy(bf16[256,3072]{1,0:T(8,128)(2,1)} %convolution_convert_fusion) | data formatting | bytes 3145728 | tf_op jit(solution)/shard_map/convert_element_type | solution.py:50
  23.0 1.9 %convolution_convert_fusion.1 = bf16[51,3072]{1,0:T(8,128)(2,1)S(1)} fusion(bf16[256,3072]{1,0:T(8,128)(2,1)} %convolution_convert_fusion, s32[51]{0:T(128)S(1)} %dynamic-slice_bitcast_fusion), kind=kOutput, calls=%fused_computation.5 | convolution fusion | flops 80385792 | bytes 1886412 | tf_op jit(solution)/shard_map/dot_general | solution.py:249
  24.9 0.9 %fusion.124 = (f32[51]{0:T(128)}, f32[51,1024]{1,0:T(8,128)S(1)}) fusion(bf16[256,1024]{1,0:T(8,128)(2,1)S(1)} %get-tuple-element.26, s32[51]{0:T(128)S(1)} %dynamic-slice_bitcast_fusion), kind=kOutput, calls=%fused_computation.223 | convolution fusion | flops 26908364 | bytes 733592 | tf_op jit(solution)/shard_map/dot_general | solution.py:243
  26.1 1.0 %fusion = (f32[16,256]{1,0:T(8,128)S(1)}, f32[16,256,256]{1,2,0:T(8,128)S(1)}) fusion(f32[256,16]{0,1:T(8,128)S(1)} %get-tuple-element.43, bf16[256,3,16,64]{0,3,2,1:T(8,128)(2,1)S(1)} %bitcast.160, f32[256,16]{0,1:T(8,128)S(1)} %get-tuple-element.44), kind=kOutput, calls=%fused_computation.4 | convolution fusion | flops 137883648 | bytes 5292032 | tf_op jit(solution)/shard_map/qhd,khd->hqk/dot_general | solution.py:33
  29.0 1.0 %multiply_convert_fusion.targets_ref = bf16[256,1024]{1,0:T(8,128)(2,1)} fusion(f32[256,1024]{1,0:T(8,128)S(1)} %get-tuple-element.34, f32[256]{0:T(256)S(1)} %add_rsqrt_fusion.2, f32[256]{0:T(256)S(1)} %broadcast_multiply_fusion.1), kind=kLoop, calls=%fused_computation.59 | loop fusion | flops 786432 | bytes 1574912 | tf_op jit(solution)/shard_map/convert_element_type | solution.py:255
  33.2 2.0 %convolution_convert_fusion.6 = bf16[256,768]{1,0:T(8,128)(2,1)S(1)} fusion(bf16[1024,768]{1,0:T(8,128)(2,1)} %param.15, bf16[1,1024]{1,0:T(2,128)(2,1)S(1)} %broadcast_in_dim.24, bf16[51,1024]{1,0:T(8,128)(2,1)S(1)} %fusion.16, bf16[256,1]{0,1:T(2,128)(2,1)S(1)} %sub.88, bf16[256,51]{0,1:T(8,128)(2,1)S(1)} %fusion.100), kind=kOutput, calls=%fused_computation.20 | convolution fusion | flops 102738944 | bytes 2099200 | tf_op jit(solution)/shard_map/jvp()/dot_general | solution.py:95
  35.5 1.3 %fusion.63 = f32[16,256,48]{1,2,0:T(8,128)S(1)} fusion(bf16[256,16,48]{0,2,1:T(8,128)(2,1)S(1)} %bitcast.166, bf16[3,16,48,48]{3,2,1,0:T(8,128)(2,1)} %param.16), kind=kOutput, calls=%fused_computation.127 | convolution fusion | flops 18874368 | bytes 1376256 | tf_op jit(solution)/shard_map/jvp(pgi,gio->pgo)/dot_general | solution.py:102
  36.8 1.2 %convolution_add_fusion.1 = f32[16,256,48]{1,2,0:T(8,128)S(1)} fusion(f32[16,256,48]{1,2,0:T(8,128)S(1)} %fusion.63, bf16[256,16,48]{0,2,1:T(8,128)(2,1)S(1)} %bitcast.167, bf16[3,16,48,48]{3,2,1,0:T(8,128)(2,1)} %param.16), kind=kOutput, calls=%fused_computation.15 | convolution fusion | flops 19070976 | bytes 2162688 | tf_op jit(solution)/shard_map/jvp(pgi,gio->pgo)/dot_general | solution.py:102
  38.0 1.4 %fusion.126 = (f32[256]{0:T(256)S(1)}, f32[16,256,48]{1,2,0:T(8,128)S(1)}) fusion(f32[16,256,48]{1,2,0:T(8,128)S(1)} %convolution_add_fusion.1, bf16[256,16,48]{0,2,1:T(8,128)(2,1)S(1)} %bitcast.168, bf16[3,16,48,48]{3,2,1,0:T(8,128)(2,1)} %param.16), kind=kOutput, calls=%fused_computation.225 | convolution fusion | flops 19267328 | bytes 2163712 | tf_op jit(solution)/shard_map/jvp(pgi,gio->pgo)/dot_general | solution.py:102
  40.3 1.4 %copy.63 = f32[256,768]{1,0:T(8,128)S(1)} copy(f32[256,768]{0,1:T(8,128)} %bitcast.162) | data formatting | bytes 1572864 | tf_op jit(solution)/shard_map/jvp()/reshape | solution.py:108
  41.7 3.6 %add_convert_fusion = (bf16[256,768]{1,0:T(8,128)(2,1)}, f32[256,768]{1,0:T(8,128)}) fusion(bf16[256,768]{1,0:T(8,128)(2,1)S(1)} %convolution_convert_fusion.6, f32[256,768]{1,0:T(8,128)S(1)} %copy.63, f32[256]{0:T(256)} %fusion.106, f32[256]{0:T(256)S(1)} %broadcast_multiply_fusion), kind=kLoop, calls=%fused_computation.82 | loop fusion | flops 13565952 | bytes 2361344 | tf_op jit(solution)/shard_map/jvp()/convert_element_type | solution.py:109
  45.3 3.5 %jvp__.1 = (f32[1,1]{1,0:T(1,128)}, bf16[256,768]{1,0:T(8,128)(2,1)}) custom-call(bf16[256,768]{1,0:T(8,128)(2,1)} %get-tuple-element.12.hidden_ref, bf16[768,1024]{1,0:T(8,128)(2,1)} %dec_out_ref.1, bf16[256,1024]{1,0:T(8,128)(2,1)} %multiply_convert_fusion.targets_ref, f32[256,1]{1,0:T(8,128)} %copy.66.keep_ref), custom_call_target="tpu_custom_call" | custom-call | tf_op jit(solution)/shard_map/jvp()/pallas_call | solution.py:128
  48.9 2.0 %multiply_reduce_fusion.1 = f32[256]{0:T(256)S(1)} fusion(f32[256,768]{1,0:T(8,128)S(1)} %copy.63, f32[256]{0:T(256)S(1)} %broadcast_multiply_fusion, f32[256,768]{1,0:T(8,128)} %get-tuple-element.13, bf16[256,768]{1,0:T(8,128)(2,1)} %get-tuple-element.4, f32[256]{0:T(256)} %fusion.106), kind=kLoop, calls=%fused_computation.81 | loop fusion | flops 3538688 | bytes 1969152 | tf_op jit(solution)/shard_map/transpose(jvp())/reduce_sum | solution.py:23
  51.6 1.4 %fusion.121 = (f32[256]{0:T(256)S(1)}, f32[256,768]{1,0:T(8,128)S(1)}) fusion(f32[256]{0:T(256)S(1)} %multiply_multiply_fusion.8, f32[256,768]{1,0:T(8,128)S(1)} %copy-done.3, bf16[256,768]{1,0:T(8,128)(2,1)S(1)} %copy-done.4, f32[256]{0:T(256)} %fusion.106, f32[256,768]{1,0:T(8,128)S(1)} %copy.63, f32[256]{0:T(256)S(1)} %broadcast_multiply_fusion), kind=kLoop, calls=%fused_computation.221 | loop fusion | flops 4128512 | bytes 2756608 | tf_op jit(solution)/shard_map/transpose(jvp())/reduce_sum | solution.py:21
  53.3 1.4 %fusion.6 = bf16[256,16,48]{0,2,1:T(8,128)(2,1)S(1)} fusion(bf16[16,48,256]{2,1,0:T(8,128)(2,1)S(1)} %bitcast.163, bf16[3,16,48,48]{3,2,1,0:T(8,128)(2,1)} %param.16), kind=kOutput, calls=%fused_computation.25 | convolution fusion | flops 18874368 | bytes 983040 | tf_op jit(solution)/shard_map/transpose(jvp(pgi,gio->pgo))/dot_general | solution.py:102
  54.7 1.2 %fusion.7 = bf16[256,16,48]{0,2,1:T(8,128)(2,1)S(1)} fusion(bf16[16,48,256]{2,1,0:T(8,128)(2,1)S(1)} %bitcast.164, bf16[3,16,48,48]{3,2,1,0:T(8,128)(2,1)} %param.16), kind=kOutput, calls=%fused_computation.26 | convolution fusion | flops 18874368 | bytes 983040 | tf_op jit(solution)/shard_map/transpose(jvp(pgi,gio->pgo))/dot_general | solution.py:102
  55.9 1.2 %fusion.8 = bf16[256,16,48]{0,2,1:T(8,128)(2,1)S(1)} fusion(bf16[16,48,256]{2,1,0:T(8,128)(2,1)S(1)} %bitcast.165, bf16[3,16,48,48]{3,2,1,0:T(8,128)(2,1)} %param.16), kind=kOutput, calls=%fused_computation.27 | convolution fusion | flops 18874368 | bytes 983040 | tf_op jit(solution)/shard_map/transpose(jvp(pgi,gio->pgo))/dot_general | solution.py:102
  58.2 2.1 %fusion.19 = bf16[52,1024]{1,0:T(8,128)(2,1)S(1)} fusion(bf16[1024,768]{1,0:T(8,128)(2,1)} %param.15, bf16[256,768]{1,0:T(8,128)(2,1)S(1)} %copy-done.4, bf16[256,768]{1,0:T(8,128)(2,1)S(1)} %copy.71, bf16[256,1]{0,1:T(2,128)(2,1)S(1)} %copy-done.31, bf16[256,51]{0,1:T(8,128)(2,1)S(1)} %fusion.100), kind=kOutput, calls=%fused_computation.52 | convolution fusion | flops 102525952 | bytes 2492416 | tf_op jit(solution)/shard_map/transpose(jvp())/dot_general | solution.py:92
  61.3 1.3 %fusion.15 = bf16[51,1,16,64]{3,0,2,1:T(8,128)(2,1)S(1)} fusion(bf16[51,16,64]{2,1,0:T(8,128)(2,1)S(1)} %reshape.264, f32[16,51,51]{1,2,0:T(8,128)} %copy-done.11, f32[16,51]{1,0:T(8,128)S(1)} %copy-done.29), kind=kOutput, calls=%fused_computation.41 | convolution fusion | flops 5462304 | bytes 378624 | tf_op jit(solution)/shard_map/transpose(jvp(hqk,khd->qhd))/dot_general | solution.py:38
  65.5 4.9 %convolution_convert_fusion.12 = bf16[51,1024]{1,0:T(8,128)(2,1)S(1)} fusion(bf16[51,3072]{1,0:T(8,128)(2,1)S(1)} %reshape.265, bf16[1024,3072]{1,0:T(8,128)(2,1)} %param.12), kind=kOutput, calls=%fused_computation.44 | convolution fusion | flops 320916480 | bytes 6709248 | tf_op jit(solution)/shard_map/transpose(jvp())/dot_general | solution.py:178
  71.1 1.4 %collective-permute-start.3 = (bf16[51,1024]{1,0:T(8,128)(2,1)S(1)}, bf16[51,1024]{1,0:T(8,128)(2,1)S(1)}, u32[]{:S(2)}, u32[]{:S(2)}) collective-permute-start(bf16[51,1024]{1,0:T(8,128)(2,1)S(1)} %fusion.91), channel_id=1, source_target_pairs={{0,3},{1,0},{2,1},{3,2},{4,7},{5,4},{6,5},{7,6},{8,11},{9,8},{10,9... | collective-permute-start | bytes 313352 | tf_op jit(solution)/shard_map/ppermute | solution.py:192
  72.4 1.0 %collective-permute-start.4 = (bf16[51,1024]{1,0:T(8,128)(2,1)S(1)}, bf16[51,1024]{1,0:T(8,128)(2,1)S(1)}, u32[]{:S(2)}, u32[]{:S(2)}) collective-permute-start(bf16[51,1024]{1,0:T(8,128)(2,1)S(1)} %fusion.91), channel_id=1, source_target_pairs={{0,2},{1,3},{2,0},{3,1},{4,6},{5,7},{6,4},{7,5},{8,10},{9,11},{10,... | collective-permute-start | bytes 313352 | tf_op jit(solution)/shard_map/ppermute | solution.py:192
  74.3 2.3 %collective-permute-done.3 = bf16[51,1024]{1,0:T(8,128)(2,1)S(1)} collective-permute-done((bf16[51,1024]{1,0:T(8,128)(2,1)S(1)}, bf16[51,1024]{1,0:T(8,128)(2,1)S(1)}, u32[]{:S(2)}, u32[]{:S(2)}) %collective-permute-start.3) | collective-permute-done | bytes 104480 | tf_op jit(solution)/shard_map/ppermute | solution.py:192
  76.6 2.7 %collective-permute-done.4 = bf16[51,1024]{1,0:T(8,128)(2,1)S(1)} collective-permute-done((bf16[51,1024]{1,0:T(8,128)(2,1)S(1)}, bf16[51,1024]{1,0:T(8,128)(2,1)S(1)}, u32[]{:S(2)}, u32[]{:S(2)}) %collective-permute-start.4) | collective-permute-done | bytes 104480 | tf_op jit(solution)/shard_map/ppermute | solution.py:192
  79.3 1.4 %fusion.18 = f32[192,1024]{1,0:T(8,128)} fusion(bf16[51,1024]{1,0:T(8,128)(2,1)S(1)} %collective-permute-done.5, bf16[51,1024]{1,0:T(8,128)(2,1)S(1)} %collective-permute-done.4, bf16[51,1024]{1,0:T(8,128)(2,1)S(1)} %collective-permute-done.3, bf16[51,1024]{1,0:T(8,128)(2,1)S(1)} %fusion.91, bf16[256,768]{1,0:T(8,128)(2,1)S(1)} %pad_maximum_fusion, ...), kind=kOutput, calls=%fused_computation.51 | convolution fusion | flops 102032640 | bytes 1377284 | tf_op jit(solution)/shard_map/vc,vd->cd/dot_general | solution.py:283
  (136 shorter events, 16.4 us)
Async XLA Ops:
  0.6 27.3 %copy-start = (bf16[1024,1024]{1,0:T(8,128)(2,1)S(1)}, bf16[1024,1024]{1,0:T(8,128)(2,1)}, u32[]{:S(2)}) copy-start(bf16[1024,1024]{1,0:T(8,128)(2,1)} %param.13) | copy-start | bytes 6291460
  0.6 10.4 %collective-permute-start = (bf16[64,768]{1,0:T(8,128)(2,1)}, bf16[64,768]{1,0:T(8,128)(2,1)S(1)}, u32[]{:S(2)}, u32[]{:S(2)}) collective-permute-start(bf16[64,768]{1,0:T(8,128)(2,1)} %param.9), channel_id=1, source_target_pairs={{0,1},{1,2},{2,3},{3,0},{4,5},{5,6},{6,7},{7,4},{8,9},{9,10},{10,1... | collective-permute-start | bytes 294920 | tf_op jit(solution)/shard_map/ppermute | solution.py:192
  3.7 7.4 %collective-permute-start.1 = (bf16[64,768]{1,0:T(8,128)(2,1)}, bf16[64,768]{1,0:T(8,128)(2,1)S(1)}, u32[]{:S(2)}, u32[]{:S(2)}) collective-permute-start(bf16[64,768]{1,0:T(8,128)(2,1)} %param.9), channel_id=1, source_target_pairs={{0,2},{1,3},{2,0},{3,1},{4,6},{5,7},{6,4},{7,5},{8,10},{9,11},{10,... | collective-permute-start | bytes 294920 | tf_op jit(solution)/shard_map/ppermute | solution.py:192
  5.2 5.9 %collective-permute-start.2 = (bf16[64,768]{1,0:T(8,128)(2,1)}, bf16[64,768]{1,0:T(8,128)(2,1)S(1)}, u32[]{:S(2)}, u32[]{:S(2)}) collective-permute-start(bf16[64,768]{1,0:T(8,128)(2,1)} %param.9), channel_id=1, source_target_pairs={{0,3},{1,0},{2,1},{3,2},{4,7},{5,4},{6,5},{7,6},{8,11},{9,8},{10,9... | collective-permute-start | bytes 294920 | tf_op jit(solution)/shard_map/ppermute | solution.py:192
  7.6 25.6 %copy-start.30 = (bf16[256,1]{0,1:T(2,128)(2,1)}, bf16[256,1]{0,1:T(2,128)(2,1)S(1)}, u32[]{:S(2)}) copy-start(bf16[256,1]{0,1:T(2,128)(2,1)S(1)} %sub.88) | copy-start | bytes 1540
  12.0 2.5 %copy-start.13 = (bf16[64,768]{1,0:T(8,128)(2,1)}, bf16[64,768]{1,0:T(8,128)(2,1)S(1)}, u32[]{:S(2)}) copy-start(bf16[64,768]{1,0:T(8,128)(2,1)S(1)} %get-tuple-element.17) | copy-start | bytes 294916
  12.0 2.5 %copy-start.15 = (bf16[64,768]{1,0:T(8,128)(2,1)}, bf16[64,768]{1,0:T(8,128)(2,1)S(1)}, u32[]{:S(2)}) copy-start(bf16[64,768]{1,0:T(8,128)(2,1)S(1)} %get-tuple-element.18) | copy-start | bytes 294916
  12.0 2.5 %copy-start.17 = (bf16[64,768]{1,0:T(8,128)(2,1)}, bf16[64,768]{1,0:T(8,128)(2,1)S(1)}, u32[]{:S(2)}) copy-start(bf16[64,768]{1,0:T(8,128)(2,1)S(1)} %get-tuple-element.19) | copy-start | bytes 294916
  12.0 2.5 %copy-start.19 = (bf16[64,768]{1,0:T(8,128)(2,1)}, bf16[64,768]{1,0:T(8,128)(2,1)S(1)}, u32[]{:S(2)}) copy-start(bf16[64,768]{1,0:T(8,128)(2,1)S(1)} %get-tuple-element.20) | copy-start | bytes 294916
  23.0 2.8 %copy-start.1 = (bf16[256,3072]{0,1:T(8,128)(2,1)S(1)}, bf16[256,3072]{0,1:T(8,128)(2,1)}, u32[]{:S(2)}) copy-start(bf16[256,3072]{0,1:T(8,128)(2,1)} %copy.64) | copy-start | bytes 4718596
  30.5 1.3 %copy-start.9 = (bf16[51,1,16,64]{3,2,1,0:T(8,128)(2,1)}, bf16[51,1,16,64]{3,2,1,0:T(8,128)(2,1)S(1)}, u32[]{:S(2)}) copy-start(bf16[51,1,16,64]{3,2,1,0:T(8,128)(2,1)S(1)} %get-tuple-element.14) | copy-start | bytes 313348
  31.8 1.5 %copy-start.27 = (f32[16,51]{1,0:T(8,128)}, f32[16,51]{1,0:T(8,128)S(1)}, u32[]{:S(2)}) copy-start(f32[16,51]{1,0:T(8,128)S(1)} %get-tuple-element.27) | copy-start | bytes 9796
  48.9 2.7 %copy-start.3 = (f32[256,768]{1,0:T(8,128)S(1)}, f32[256,768]{1,0:T(8,128)}, u32[]{:S(2)}) copy-start(f32[256,768]{1,0:T(8,128)} %get-tuple-element.13) | copy-start | bytes 2359300
  48.9 2.7 %copy-start.4 = (bf16[256,768]{1,0:T(8,128)(2,1)S(1)}, bf16[256,768]{1,0:T(8,128)(2,1)}, u32[]{:S(2)}) copy-start(bf16[256,768]{1,0:T(8,128)(2,1)} %get-tuple-element.4) | copy-start | bytes 1179652
  53.3 3.7 %copy-start.28 = (f32[16,51]{1,0:T(8,128)S(1)}, f32[16,51]{1,0:T(8,128)}, u32[]{:S(2)}) copy-start(f32[16,51]{1,0:T(8,128)} %copy-done.27) | copy-start | bytes 9796
  54.7 3.5 %copy-start.31 = (bf16[256,1]{0,1:T(2,128)(2,1)S(1)}, bf16[256,1]{0,1:T(2,128)(2,1)}, u32[]{:S(2)}) copy-start(bf16[256,1]{0,1:T(2,128)(2,1)} %copy-done.30) | copy-start | bytes 1540
  58.2 3.1 %copy-start.29 = (f32[16,51]{1,0:T(8,128)S(1)}, f32[16,51]{1,0:T(8,128)}, u32[]{:S(2)}) copy-start(f32[16,51]{1,0:T(8,128)} %copy-done.27) | copy-start | bytes 9796
  60.3 2.4 %copy-start.10 = (bf16[51,1,16,64]{3,2,1,0:T(8,128)(2,1)S(1)}, bf16[51,1,16,64]{3,2,1,0:T(8,128)(2,1)}, u32[]{:S(2)}) copy-start(bf16[51,1,16,64]{3,2,1,0:T(8,128)(2,1)} %copy-done.9) | copy-start | bytes 313348
  60.3 2.4 %copy-start.25 = (f32[16,51]{1,0:T(8,128)S(1)}, f32[16,51]{1,0:T(8,128)}, u32[]{:S(2)}) copy-start(f32[16,51]{1,0:T(8,128)} %multiply_divide_fusion) | copy-start | bytes 9796
  61.1 1.9 %copy-start.6 = (bf16[51,1,16,64]{3,2,1,0:T(8,128)(2,1)S(1)}, bf16[51,1,16,64]{3,2,1,0:T(8,128)(2,1)}, u32[]{:S(2)}) copy-start(bf16[51,1,16,64]{3,2,1,0:T(8,128)(2,1)} %copy-done.5) | copy-start | bytes 313348
  61.1 1.9 %copy-start.8 = (bf16[51,1,16,64]{3,2,1,0:T(8,128)(2,1)S(1)}, bf16[51,1,16,64]{3,2,1,0:T(8,128)(2,1)}, u32[]{:S(2)}) copy-start(bf16[51,1,16,64]{3,2,1,0:T(8,128)(2,1)} %copy-done.7) | copy-start | bytes 313348
  61.1 1.9 %copy-start.22 = (f32[51,16]{0,1:T(8,128)S(1)}, f32[51,16]{0,1:T(8,128)}, u32[]{:S(2)}) copy-start(f32[51,16]{0,1:T(8,128)} %copy-done.21) | copy-start | bytes 9796
  61.3 1.4 %copy-start.12 = (f32[16,51,51]{1,2,0:T(8,128)S(1)}, f32[16,51,51]{1,2,0:T(8,128)}, u32[]{:S(2)}) copy-start(f32[16,51,51]{1,2,0:T(8,128)} %copy-done.11) | copy-start | bytes 499396
  65.5 5.0 %copy-start.33 = (f32[51]{0:T(128)S(1)}, f32[51]{0:T(128)}, u32[]{:S(2)}) copy-start(f32[51]{0:T(128)} %get-tuple-element.23) | copy-start | bytes 616
  65.5 8.7 %copy-start.14 = (bf16[64,768]{1,0:T(8,128)(2,1)S(1)}, bf16[64,768]{1,0:T(8,128)(2,1)}, u32[]{:S(2)}) copy-start(bf16[64,768]{1,0:T(8,128)(2,1)} %copy-done.13) | copy-start | bytes 294916
  65.5 8.7 %copy-start.16 = (bf16[64,768]{1,0:T(8,128)(2,1)S(1)}, bf16[64,768]{1,0:T(8,128)(2,1)}, u32[]{:S(2)}) copy-start(bf16[64,768]{1,0:T(8,128)(2,1)} %copy-done.15) | copy-start | bytes 294916
  65.5 8.7 %copy-start.18 = (bf16[64,768]{1,0:T(8,128)(2,1)S(1)}, bf16[64,768]{1,0:T(8,128)(2,1)}, u32[]{:S(2)}) copy-start(bf16[64,768]{1,0:T(8,128)(2,1)} %copy-done.17) | copy-start | bytes 294916
  65.5 8.7 %copy-start.20 = (bf16[64,768]{1,0:T(8,128)(2,1)S(1)}, bf16[64,768]{1,0:T(8,128)(2,1)}, u32[]{:S(2)}) copy-start(bf16[64,768]{1,0:T(8,128)(2,1)} %copy-done.19) | copy-start | bytes 294916
  65.5 13.8 %copy-start.32 = (s32[204]{0:T(256)S(1)}, s32[204]{0:T(256)}, u32[]{:S(2)}) copy-start(s32[204]{0:T(256)} %eq.93) | copy-start | bytes 2452
  71.1 5.5 %collective-permute-start.3 = (bf16[51,1024]{1,0:T(8,128)(2,1)S(1)}, bf16[51,1024]{1,0:T(8,128)(2,1)S(1)}, u32[]{:S(2)}, u32[]{:S(2)}) collective-permute-start(bf16[51,1024]{1,0:T(8,128)(2,1)S(1)} %fusion.91), channel_id=1, source_target_pairs={{0,3},{1,0},{2,1},{3,2},{4,7},{5,4},{6,5},{7,6},{8,11},{9,8},{10,9... | collective-permute-start | bytes 313352 | tf_op jit(solution)/shard_map/ppermute | solution.py:192
  72.4 6.9 %collective-permute-start.4 = (bf16[51,1024]{1,0:T(8,128)(2,1)S(1)}, bf16[51,1024]{1,0:T(8,128)(2,1)S(1)}, u32[]{:S(2)}, u32[]{:S(2)}) collective-permute-start(bf16[51,1024]{1,0:T(8,128)(2,1)S(1)} %fusion.91), channel_id=1, source_target_pairs={{0,2},{1,3},{2,0},{3,1},{4,6},{5,7},{6,4},{7,5},{8,10},{9,11},{10,... | collective-permute-start | bytes 313352 | tf_op jit(solution)/shard_map/ppermute | solution.py:192
  73.4 5.9 %collective-permute-start.5 = (bf16[51,1024]{1,0:T(8,128)(2,1)S(1)}, bf16[51,1024]{1,0:T(8,128)(2,1)S(1)}, u32[]{:S(2)}, u32[]{:S(2)}) collective-permute-start(bf16[51,1024]{1,0:T(8,128)(2,1)S(1)} %fusion.91), channel_id=1, source_target_pairs={{0,1},{1,2},{2,3},{3,0},{4,5},{5,6},{6,7},{7,4},{8,9},{9,10},{10,1... | collective-permute-start | bytes 313352 | tf_op jit(solution)/shard_map/ppermute | solution.py:192
  (8 other events, 6.5 us)

commit v23 on v18

--- a/solution.py
+++ b/solution.py
@@ -273,8 +273,10 @@
     squares, pullback = jax.vjp(objective, visible_in)
     (grad_in,) = pullback(jnp.ones_like(squares) * factor)
     copy_loss = jnp.reshape(squares / ((total_rows - visible_count) * D), (1,))
-    slot_copy = (own_index + jnp.arange(group_size, dtype=jnp.int32)) % group_size
-    flat_index = visible_index[slot_copy].reshape(copies * visible_count)
+    doubled_index = jnp.concatenate([visible_index, visible_index], axis=0)
+    flat_index = lax.dynamic_slice_in_dim(doubled_index, own_index, copies, 0).reshape(
+        copies * visible_count
+    )
     own_cols = lax.dynamic_slice_in_dim(clip_pixels, own_index * col_width, col_width, 1)
     all_picks = (flat_index[:, None] == clip_ids[None, :]).astype(jnp.bfloat16)
     gathered = jnp.dot(all_picks, own_cols, preferred_element_type=jnp.float32).astype(

time: 78.9 us -> 78.4 us (level)
  local copies, waits for them, and re-layouts: 11.5 us -> 10.3 us
    gather x1 -> x0, local copies, waits for them, and re-layouts: 1.24 us -> none  [on_device(): flat_index = visible_index[slot_copy].reshape(copies * visible_count)]
  transfers between devices with their start and end apart: 6 -> 6, of which waited for: 3 -> 3; matrix products, arithmetic and copies ran while one was open for 8% -> 7% of each run, Pallas kernels for 0% -> 0%
where the time goes in v23:
time: 78.4 us; the launch traced here: 77.8 us
  matrix products  35.6 us (45%)
  other arithmetic  12.2 us (16%)
  local copies, waits for them, and re-layouts  10.3 us (13%)
  starting transfers between devices  8.16 us (10%)
  waiting for transfers between devices  4.86 us (6%)
  Pallas kernels  3.54 us (5%)
  between operations  3.16 us (4%)
    ppermute x6, starting transfers between devices, ring_gather(): parts.append(lax.ppermute(values, 'mask', pairs))  8.16 us
    dot_general x6, matrix products, decoder_output(): jnp.einsum('pgi,gio->pgo', padded[offset:offset + total_rows], conv_w[off...  7.62 us
    dot_general x1, matrix products, copy_terms(): branch = attention_from(reuse_rows(visible_in, w_qkv, projected), w_out)  4.89 us
    ppermute x6, waiting for transfers between devices, ring_gather(): parts.append(lax.ppermute(values, 'mask', pairs))  4.86 us
    dot_general x2, matrix products, decoder_output(): jnp.dot(visible_out, dec_in, preferred_element_type=jnp.float32)  4.38 us
    pallas_call x1, Pallas kernels, masked_squares(): pl.pallas_call(functools.partial(loss_kernel, scale=scale), out_shape=(ja...  3.54 us
    dot_general x1, matrix products, project_rows(): jnp.dot(normed, w_qkv, preferred_element_type=jnp.float32)  3.1 us
    convert_element_type x1, other arithmetic, decoder_output(): return (lowered.astype(jnp.float32) + activated).astype(jnp.bfloat16)  2.97 us
  transfers between devices with their start and end apart: 6, of which 3 were waited for; matrix products, arithmetic and copies ran while one was open for 7% of the time, Pallas kernels for 0%

profile of v23, /device:TPU:0, one launch (start us, length us, event | category | flops | bytes accessed | tf_op | source)
XLA Modules:
  0.0 77.8 jit_solution(13324772178353362272)
XLA Ops:
  0.6 3.0 %collective-permute-start = (bf16[64,768]{1,0:T(8,128)(2,1)}, bf16[64,768]{1,0:T(8,128)(2,1)S(1)}, u32[]{:S(2)}, u32[]{:S(2)}) collective-permute-start(bf16[64,768]{1,0:T(8,128)(2,1)} %param.9), channel_id=1, source_target_pairs={{0,1},{1,2},{2,3},{3,0},{4,5},{5,6},{6,7},{7,4},{8,9},{9,10},{10,1... | collective-permute-start | bytes 294920 | tf_op jit(solution)/shard_map/ppermute | solution.py:192
  3.7 1.5 %collective-permute-start.1 = (bf16[64,768]{1,0:T(8,128)(2,1)}, bf16[64,768]{1,0:T(8,128)(2,1)S(1)}, u32[]{:S(2)}, u32[]{:S(2)}) collective-permute-start(bf16[64,768]{1,0:T(8,128)(2,1)} %param.9), channel_id=1, source_target_pairs={{0,2},{1,3},{2,0},{3,1},{4,6},{5,7},{6,4},{7,5},{8,10},{9,11},{10,... | collective-permute-start | bytes 294920 | tf_op jit(solution)/shard_map/ppermute | solution.py:192
  5.2 1.4 %collective-permute-start.2 = (bf16[64,768]{1,0:T(8,128)(2,1)}, bf16[64,768]{1,0:T(8,128)(2,1)S(1)}, u32[]{:S(2)}, u32[]{:S(2)}) collective-permute-start(bf16[64,768]{1,0:T(8,128)(2,1)} %param.9), channel_id=1, source_target_pairs={{0,3},{1,0},{2,1},{3,2},{4,7},{5,4},{6,5},{7,6},{8,11},{9,8},{10,9... | collective-permute-start | bytes 294920 | tf_op jit(solution)/shard_map/ppermute | solution.py:192
  10.4 1.9 %convolution_reduce_fusion = bf16[768]{0:T(1024)(128)(2,1)S(1)} fusion(bf16[1024,1]{0,1:T(2,128)(2,1)S(1)} %reshape.222, bf16[1024,768]{1,0:T(8,128)(2,1)} %param.15), kind=kOutput, calls=%fused_computation.53 | convolution fusion | flops 1572864 | bytes 1576448 | tf_op jit(solution)/shard_map/jvp()/dot_general | solution.py:93
  12.4 1.3 %select_select_fusion.3 = (bf16[64,768]{1,0:T(8,128)(2,1)S(1)}, bf16[64,768]{1,0:T(8,128)(2,1)S(1)}, bf16[64,768]{1,0:T(8,128)(2,1)S(1)}, bf16[64,768]{1,0:T(8,128)(2,1)S(1)}) fusion(bf16[64,768]{1,0:T(8,128)(2,1)S(1)} %collective-permute-done, bf16[64,768]{1,0:T(8,128)(2,1)S(1)} %collective-permute-done.1, bf16[64,768]{1,0:T(8,128)(2,1)S(1)} %collective-permute-done.2, ...), kind=kLoop, calls=%fused_computation.172 | loop fusion | flops 589824 | bytes 786444 | tf_op jit(solution)/shard_map/jit(_where)/select_n | solution.py:203
  13.7 2.2 %convert_reduce_fusion = (f32[256]{0:T(256)S(1)}, bf16[256,1024]{1,0:T(8,128)(2,1)S(1)}) fusion(bf16[768,1024]{1,0:T(8,128)(2,1)} %param.11, bf16[64,768]{1,0:T(8,128)(2,1)S(1)} %get-tuple-element.18, bf16[64,768]{1,0:T(8,128)(2,1)S(1)} %get-tuple-element.19, bf16[64,768]{1,0:T(8,128)(2,1)S(1)} %get-tuple-element.20, bf16[64,768]{1,0:T(8,128)(2,1)S(1)} %get-tuple-element.17), kind=kOutput, calls=%fused_computation.11 | convolution fusion | flops 405012224 | bytes 2491392 | tf_op jit(solution)/shard_map/dot_general | solution.py:238
  16.3 3.1 %convolution_convert_fusion = bf16[256,3072]{1,0:T(8,128)(2,1)} fusion(bf16[1024,3072]{1,0:T(8,128)(2,1)S(1)} %copy-done.4, bf16[256,1024]{1,0:T(8,128)(2,1)S(1)} %get-tuple-element.24, f32[256]{0:T(256)S(1)} %add_rsqrt_fusion.3, f32[256]{0:T(256)S(1)} %broadcast_multiply_fusion.2), kind=kOutput, calls=%fused_computation.2 | convolution fusion | flops 1612447744 | bytes 8390656 | tf_op jit(solution)/shard_map/dot_general | solution.py:50
  19.4 2.6 %copy.63 = bf16[256,3072]{0,1:T(8,128)(2,1)} copy(bf16[256,3072]{1,0:T(8,128)(2,1)} %convolution_convert_fusion) | data formatting | bytes 3145728 | tf_op jit(solution)/shard_map/convert_element_type | solution.py:50
  21.9 1.9 %convolution_convert_fusion.1 = bf16[51,3072]{1,0:T(8,128)(2,1)S(1)} fusion(bf16[256,3072]{1,0:T(8,128)(2,1)} %convolution_convert_fusion, s32[51]{0:T(128)S(1)} %fusion.114), kind=kOutput, calls=%fused_computation.4 | convolution fusion | flops 80385792 | bytes 1886412 | tf_op jit(solution)/shard_map/dot_general | solution.py:249
  23.9 0.9 %fusion.129 = (f32[51]{0:T(128)}, f32[51,1024]{1,0:T(8,128)S(1)}) fusion(bf16[256,1024]{1,0:T(8,128)(2,1)S(1)} %get-tuple-element.24, s32[51]{0:T(128)S(1)} %fusion.114), kind=kOutput, calls=%fused_computation.224 | convolution fusion | flops 26908364 | bytes 733592 | tf_op jit(solution)/shard_map/dot_general | solution.py:243
  25.0 1.0 %fusion = (f32[16,256]{1,0:T(8,128)S(1)}, f32[16,256,256]{1,2,0:T(8,128)S(1)}) fusion(f32[256,16]{0,1:T(8,128)S(1)} %get-tuple-element.43, bf16[256,3,16,64]{0,3,2,1:T(8,128)(2,1)S(1)} %bitcast.162, f32[256,16]{0,1:T(8,128)S(1)} %get-tuple-element.44), kind=kOutput, calls=%fused_computation.3 | convolution fusion | flops 137883648 | bytes 5292032 | tf_op jit(solution)/shard_map/qhd,khd->hqk/dot_general | solution.py:33
  26.0 0.8 %fusion.2 = bf16[16,64,256]{2,1,0:T(8,128)(2,1)S(1)} fusion(f32[16,256,256]{1,2,0:T(8,128)S(1)} %get-tuple-element.30, f32[16,256]{1,0:T(8,128)S(1)} %get-tuple-element.29, bf16[256,3,16,64]{0,3,2,1:T(8,128)(2,1)S(1)} %bitcast.163), kind=kOutput, calls=%fused_computation.12 | convolution fusion | flops 137625600 | bytes 5259264 | tf_op jit(solution)/shard_map/hqk,khd->qhd/dot_general | solution.py:38
  28.0 1.0 %multiply_convert_fusion.targets_ref = bf16[256,1024]{1,0:T(8,128)(2,1)} fusion(f32[256,1024]{1,0:T(8,128)S(1)} %get-tuple-element.32, f32[256]{0:T(256)S(1)} %add_rsqrt_fusion.2, f32[256]{0:T(256)S(1)} %broadcast_multiply_fusion.1), kind=kLoop, calls=%fused_computation.60 | loop fusion | flops 786432 | bytes 1574912 | tf_op jit(solution)/shard_map/convert_element_type | solution.py:255
  31.7 2.2 %convolution_convert_fusion.17 = bf16[51,768]{1,0:T(8,128)(2,1)S(1)} fusion(bf16[1024,768]{1,0:T(8,128)(2,1)} %param.15, f32[51,1024]{1,0:T(8,128)S(1)} %get-tuple-element.34, bf16[51,1024]{1,0:T(8,128)(2,1)S(1)} %reshape.208, bf16[1024,1024]{1,0:T(8,128)(2,1)S(1)} %copy-done), kind=kOutput, calls=%fused_computation.51 | convolution fusion | flops 187314432 | bytes 4061696 | tf_op jit(solution)/shard_map/jvp()/dot_general | solution.py:90
  34.5 1.3 %fusion.67 = f32[16,256,48]{1,2,0:T(8,128)S(1)} fusion(bf16[256,16,48]{0,2,1:T(8,128)(2,1)S(1)} %bitcast.168, bf16[3,16,48,48]{3,2,1,0:T(8,128)(2,1)} %param.16), kind=kOutput, calls=%fused_computation.130 | convolution fusion | flops 18874368 | bytes 1376256 | tf_op jit(solution)/shard_map/jvp(pgi,gio->pgo)/dot_general | solution.py:102
  35.8 1.2 %convolution_add_fusion.1 = f32[16,256,48]{1,2,0:T(8,128)S(1)} fusion(f32[16,256,48]{1,2,0:T(8,128)S(1)} %fusion.67, bf16[256,16,48]{0,2,1:T(8,128)(2,1)S(1)} %bitcast.169, bf16[3,16,48,48]{3,2,1,0:T(8,128)(2,1)} %param.16), kind=kOutput, calls=%fused_computation.14 | convolution fusion | flops 19070976 | bytes 2162688 | tf_op jit(solution)/shard_map/jvp(pgi,gio->pgo)/dot_general | solution.py:102
  37.1 1.4 %fusion.127 = (f32[256]{0:T(256)S(1)}, f32[16,256,48]{1,2,0:T(8,128)S(1)}) fusion(f32[16,256,48]{1,2,0:T(8,128)S(1)} %convolution_add_fusion.1, bf16[256,16,48]{0,2,1:T(8,128)(2,1)S(1)} %bitcast.170, bf16[3,16,48,48]{3,2,1,0:T(8,128)(2,1)} %param.16), kind=kOutput, calls=%fused_computation.222 | convolution fusion | flops 19267328 | bytes 2163712 | tf_op jit(solution)/shard_map/jvp(pgi,gio->pgo)/dot_general | solution.py:102
  39.3 1.4 %copy.62 = f32[256,768]{1,0:T(8,128)S(1)} copy(f32[256,768]{0,1:T(8,128)} %bitcast.164) | data formatting | bytes 1572864 | tf_op jit(solution)/shard_map/jvp()/reshape | solution.py:108
  40.7 3.0 %add_convert_fusion = (bf16[256,768]{1,0:T(8,128)(2,1)}, f32[256,768]{1,0:T(8,128)}) fusion(bf16[256,768]{1,0:T(8,128)(2,1)S(1)} %fusion.3, f32[256,768]{1,0:T(8,128)S(1)} %copy.62, f32[256]{0:T(256)S(1)} %fusion.113, f32[256]{0:T(256)S(1)} %broadcast_multiply_fusion), kind=kLoop, calls=%fused_computation.85 | loop fusion | flops 13565952 | bytes 2361344 | tf_op jit(solution)/shard_map/jvp()/convert_element_type | solution.py:109
  43.7 3.5 %jvp__.1 = (f32[1,1]{1,0:T(1,128)}, bf16[256,768]{1,0:T(8,128)(2,1)}) custom-call(bf16[256,768]{1,0:T(8,128)(2,1)} %get-tuple-element.12.hidden_ref, bf16[768,1024]{1,0:T(8,128)(2,1)} %dec_out_ref.1, bf16[256,1024]{1,0:T(8,128)(2,1)} %multiply_convert_fusion.targets_ref, f32[256,1]{1,0:T(8,128)} %copy.65.keep_ref), custom_call_target="tpu_custom_call" | custom-call | tf_op jit(solution)/shard_map/jvp()/pallas_call | solution.py:128
  47.2 2.0 %multiply_reduce_fusion.1 = f32[256]{0:T(256)S(1)} fusion(f32[256,768]{1,0:T(8,128)S(1)} %copy.62, f32[256]{0:T(256)S(1)} %broadcast_multiply_fusion, f32[256,768]{1,0:T(8,128)} %get-tuple-element.13, bf16[256,768]{1,0:T(8,128)(2,1)} %get-tuple-element.4, f32[256]{0:T(256)S(1)} %fusion.113), kind=kLoop, calls=%fused_computation.84 | loop fusion | flops 3538688 | bytes 1969152 | tf_op jit(solution)/shard_map/transpose(jvp())/reduce_sum | solution.py:23
  50.3 1.4 %fusion.7 = bf16[256,16,48]{0,2,1:T(8,128)(2,1)S(1)} fusion(bf16[16,48,256]{2,1,0:T(8,128)(2,1)S(1)} %bitcast.165, bf16[3,16,48,48]{3,2,1,0:T(8,128)(2,1)} %param.16), kind=kOutput, calls=%fused_computation.25 | convolution fusion | flops 18874368 | bytes 983040 | tf_op jit(solution)/shard_map/transpose(jvp(pgi,gio->pgo))/dot_general | solution.py:102
  51.7 1.2 %fusion.8 = bf16[256,16,48]{0,2,1:T(8,128)(2,1)S(1)} fusion(bf16[16,48,256]{2,1,0:T(8,128)(2,1)S(1)} %bitcast.166, bf16[3,16,48,48]{3,2,1,0:T(8,128)(2,1)} %param.16), kind=kOutput, calls=%fused_computation.26 | convolution fusion | flops 18874368 | bytes 983040 | tf_op jit(solution)/shard_map/transpose(jvp(pgi,gio->pgo))/dot_general | solution.py:102
  52.9 1.2 %fusion.9 = bf16[256,16,48]{0,2,1:T(8,128)(2,1)S(1)} fusion(bf16[16,48,256]{2,1,0:T(8,128)(2,1)S(1)} %bitcast.167, bf16[3,16,48,48]{3,2,1,0:T(8,128)(2,1)} %param.16), kind=kOutput, calls=%fused_computation.27 | convolution fusion | flops 18874368 | bytes 983040 | tf_op jit(solution)/shard_map/transpose(jvp(pgi,gio->pgo))/dot_general | solution.py:102
  54.6 2.2 %convolution_convert_fusion.12 = bf16[51,1024]{1,0:T(8,128)(2,1)S(1)} fusion(bf16[1024,768]{1,0:T(8,128)(2,1)} %param.15, bf16[256,768]{1,0:T(8,128)(2,1)S(1)} %copy-done.5, bf16[256,768]{1,0:T(8,128)(2,1)S(1)} %copy.70, pred[256]{0:T(512)(128)(4,1)} %copy-done.26, s32[51]{0:T(128)} %copy-done.24), kind=kOutput, calls=%fused_computation.45 | convolution fusion | flops 100964352 | bytes 2464204 | tf_op jit(solution)/shard_map/transpose(jvp())/dot_general | solution.py:90
  57.7 1.4 %fusion.16 = bf16[51,1,16,64]{3,0,2,1:T(8,128)(2,1)S(1)} fusion(bf16[51,16,64]{2,1,0:T(8,128)(2,1)S(1)} %reshape.215, f32[16,51,51]{1,2,0:T(8,128)} %copy-done.12, f32[16,51]{1,0:T(8,128)S(1)} %copy-done.23), kind=kOutput, calls=%fused_computation.41 | convolution fusion | flops 5462304 | bytes 378624 | tf_op jit(solution)/shard_map/transpose(jvp(hqk,khd->qhd))/dot_general | solution.py:38
  61.9 4.9 %convolution_convert_fusion.11 = bf16[51,1024]{1,0:T(8,128)(2,1)S(1)} fusion(bf16[51,3072]{1,0:T(8,128)(2,1)S(1)} %reshape.216, bf16[1024,3072]{1,0:T(8,128)(2,1)} %param.12), kind=kOutput, calls=%fused_computation.44 | convolution fusion | flops 320916480 | bytes 6709248 | tf_op jit(solution)/shard_map/transpose(jvp())/dot_general | solution.py:178
  68.1 1.5 %collective-permute-start.4 = (bf16[51,1024]{1,0:T(8,128)(2,1)S(1)}, bf16[51,1024]{1,0:T(8,128)(2,1)S(1)}, u32[]{:S(2)}, u32[]{:S(2)}) collective-permute-start(bf16[51,1024]{1,0:T(8,128)(2,1)S(1)} %fusion.99), channel_id=1, source_target_pairs={{0,2},{1,3},{2,0},{3,1},{4,6},{5,7},{6,4},{7,5},{8,10},{9,11},{10,... | collective-permute-start | bytes 313352 | tf_op jit(solution)/shard_map/ppermute | solution.py:192
  70.4 2.6 %collective-permute-done.3 = bf16[51,1024]{1,0:T(8,128)(2,1)S(1)} collective-permute-done((bf16[51,1024]{1,0:T(8,128)(2,1)S(1)}, bf16[51,1024]{1,0:T(8,128)(2,1)S(1)}, u32[]{:S(2)}, u32[]{:S(2)}) %collective-permute-start.3) | collective-permute-done | bytes 104480 | tf_op jit(solution)/shard_map/ppermute | solution.py:192
  73.0 1.0 %collective-permute-done.4 = bf16[51,1024]{1,0:T(8,128)(2,1)S(1)} collective-permute-done((bf16[51,1024]{1,0:T(8,128)(2,1)S(1)}, bf16[51,1024]{1,0:T(8,128)(2,1)S(1)}, u32[]{:S(2)}, u32[]{:S(2)}) %collective-permute-start.4) | collective-permute-done | bytes 104480 | tf_op jit(solution)/shard_map/ppermute | solution.py:192
  74.0 1.2 %collective-permute-done.5 = bf16[51,1024]{1,0:T(8,128)(2,1)S(1)} collective-permute-done((bf16[51,1024]{1,0:T(8,128)(2,1)S(1)}, bf16[51,1024]{1,0:T(8,128)(2,1)S(1)}, u32[]{:S(2)}, u32[]{:S(2)}) %collective-permute-start.5) | collective-permute-done | bytes 104480 | tf_op jit(solution)/shard_map/ppermute | solution.py:192
  75.3 1.4 %fusion.19 = f32[192,1024]{1,0:T(8,128)} fusion(bf16[51,1024]{1,0:T(8,128)(2,1)S(1)} %collective-permute-done.5, bf16[51,1024]{1,0:T(8,128)(2,1)S(1)} %collective-permute-done.4, bf16[51,1024]{1,0:T(8,128)(2,1)S(1)} %collective-permute-done.3, bf16[51,1024]{1,0:T(8,128)(2,1)S(1)} %fusion.99, bf16[256,768]{1,0:T(8,128)(2,1)S(1)} %pad_maximum_fusion, ...), kind=kOutput, calls=%fused_computation.52 | convolution fusion | flops 102032640 | bytes 1377284 | tf_op jit(solution)/shard_map/vc,vd->cd/dot_general | solution.py:285
  (122 shorter events, 16.1 us)
Async XLA Ops:
  0.6 26.2 %copy-start = (bf16[1024,1024]{1,0:T(8,128)(2,1)S(1)}, bf16[1024,1024]{1,0:T(8,128)(2,1)}, u32[]{:S(2)}) copy-start(bf16[1024,1024]{1,0:T(8,128)(2,1)} %param.13) | copy-start | bytes 6291460
  0.6 11.7 %collective-permute-start = (bf16[64,768]{1,0:T(8,128)(2,1)}, bf16[64,768]{1,0:T(8,128)(2,1)S(1)}, u32[]{:S(2)}, u32[]{:S(2)}) collective-permute-start(bf16[64,768]{1,0:T(8,128)(2,1)} %param.9), channel_id=1, source_target_pairs={{0,1},{1,2},{2,3},{3,0},{4,5},{5,6},{6,7},{7,4},{8,9},{9,10},{10,1... | collective-permute-start | bytes 294920 | tf_op jit(solution)/shard_map/ppermute | solution.py:192
  3.7 8.7 %collective-permute-start.1 = (bf16[64,768]{1,0:T(8,128)(2,1)}, bf16[64,768]{1,0:T(8,128)(2,1)S(1)}, u32[]{:S(2)}, u32[]{:S(2)}) collective-permute-start(bf16[64,768]{1,0:T(8,128)(2,1)} %param.9), channel_id=1, source_target_pairs={{0,2},{1,3},{2,0},{3,1},{4,6},{5,7},{6,4},{7,5},{8,10},{9,11},{10,... | collective-permute-start | bytes 294920 | tf_op jit(solution)/shard_map/ppermute | solution.py:192
  5.2 7.2 %collective-permute-start.2 = (bf16[64,768]{1,0:T(8,128)(2,1)}, bf16[64,768]{1,0:T(8,128)(2,1)S(1)}, u32[]{:S(2)}, u32[]{:S(2)}) collective-permute-start(bf16[64,768]{1,0:T(8,128)(2,1)} %param.9), channel_id=1, source_target_pairs={{0,3},{1,0},{2,1},{3,2},{4,7},{5,4},{6,5},{7,6},{8,11},{9,8},{10,9... | collective-permute-start | bytes 294920 | tf_op jit(solution)/shard_map/ppermute | solution.py:192
  7.3 26.6 %copy-start.24 = (s32[51]{0:T(128)}, s32[51]{0:T(128)S(1)}, u32[]{:S(2)}) copy-start(s32[51]{0:T(128)S(1)} %fusion.114) | copy-start | bytes 616
  8.3 25.7 %copy-start.26 = (pred[256]{0:T(512)(128)(4,1)}, pred[256]{0:T(512)(128)(4,1)S(1)}, u32[]{:S(2)}) copy-start(pred[256]{0:T(512)(128)(4,1)S(1)} %broadcast_compare_fusion) | copy-start | bytes 772
  10.4 5.8 %copy-start.4 = (bf16[1024,3072]{1,0:T(8,128)(2,1)S(1)}, bf16[1024,3072]{1,0:T(8,128)(2,1)}, u32[]{:S(2)}) copy-start(bf16[1024,3072]{1,0:T(8,128)(2,1)} %param.12) | copy-start | bytes 18874372
  13.7 2.5 %copy-start.14 = (bf16[64,768]{1,0:T(8,128)(2,1)}, bf16[64,768]{1,0:T(8,128)(2,1)S(1)}, u32[]{:S(2)}) copy-start(bf16[64,768]{1,0:T(8,128)(2,1)S(1)} %get-tuple-element.17) | copy-start | bytes 294916
  13.7 2.5 %copy-start.16 = (bf16[64,768]{1,0:T(8,128)(2,1)}, bf16[64,768]{1,0:T(8,128)(2,1)S(1)}, u32[]{:S(2)}) copy-start(bf16[64,768]{1,0:T(8,128)(2,1)S(1)} %get-tuple-element.18) | copy-start | bytes 294916
  13.7 2.5 %copy-start.18 = (bf16[64,768]{1,0:T(8,128)(2,1)}, bf16[64,768]{1,0:T(8,128)(2,1)S(1)}, u32[]{:S(2)}) copy-start(bf16[64,768]{1,0:T(8,128)(2,1)S(1)} %get-tuple-element.19) | copy-start | bytes 294916
  13.7 2.5 %copy-start.20 = (bf16[64,768]{1,0:T(8,128)(2,1)}, bf16[64,768]{1,0:T(8,128)(2,1)S(1)}, u32[]{:S(2)}) copy-start(bf16[64,768]{1,0:T(8,128)(2,1)S(1)} %get-tuple-element.20) | copy-start | bytes 294916
  21.9 2.8 %copy-start.1 = (bf16[256,3072]{0,1:T(8,128)(2,1)S(1)}, bf16[256,3072]{0,1:T(8,128)(2,1)}, u32[]{:S(2)}) copy-start(bf16[256,3072]{0,1:T(8,128)(2,1)} %copy.63) | copy-start | bytes 4718596
  29.5 1.2 %copy-start.8 = (bf16[51,1,16,64]{3,2,1,0:T(8,128)(2,1)}, bf16[51,1,16,64]{3,2,1,0:T(8,128)(2,1)S(1)}, u32[]{:S(2)}) copy-start(bf16[51,1,16,64]{3,2,1,0:T(8,128)(2,1)S(1)} %get-tuple-element.16) | copy-start | bytes 313348
  29.5 1.2 %copy-start.10 = (bf16[51,1,16,64]{3,2,1,0:T(8,128)(2,1)}, bf16[51,1,16,64]{3,2,1,0:T(8,128)(2,1)S(1)}, u32[]{:S(2)}) copy-start(bf16[51,1,16,64]{3,2,1,0:T(8,128)(2,1)S(1)} %get-tuple-element.15) | copy-start | bytes 313348
  30.7 1.0 %copy-start.22 = (f32[16,51]{1,0:T(8,128)}, f32[16,51]{1,0:T(8,128)S(1)}, u32[]{:S(2)}) copy-start(f32[16,51]{1,0:T(8,128)S(1)} %get-tuple-element.25) | copy-start | bytes 9796
  38.4 0.9 %copy-start.2 = (f32[16,256,48]{1,2,0:T(8,128)}, f32[16,256,48]{1,2,0:T(8,128)S(1)}, u32[]{:S(2)}) copy-start(f32[16,256,48]{1,2,0:T(8,128)S(1)} %get-tuple-element.28) | copy-start | bytes 2359300
  47.2 2.0 %copy-start.3 = (f32[256,768]{1,0:T(8,128)S(1)}, f32[256,768]{1,0:T(8,128)}, u32[]{:S(2)}) copy-start(f32[256,768]{1,0:T(8,128)} %get-tuple-element.13) | copy-start | bytes 2359300
  47.2 2.0 %copy-start.5 = (bf16[256,768]{1,0:T(8,128)(2,1)S(1)}, bf16[256,768]{1,0:T(8,128)(2,1)}, u32[]{:S(2)}) copy-start(bf16[256,768]{1,0:T(8,128)(2,1)} %get-tuple-element.4) | copy-start | bytes 1179652
  50.1 3.9 %copy-start.23 = (f32[16,51]{1,0:T(8,128)S(1)}, f32[16,51]{1,0:T(8,128)}, u32[]{:S(2)}) copy-start(f32[16,51]{1,0:T(8,128)} %copy-done.22) | copy-start | bytes 9796
  56.8 2.4 %copy-start.11 = (bf16[51,1,16,64]{3,2,1,0:T(8,128)(2,1)S(1)}, bf16[51,1,16,64]{3,2,1,0:T(8,128)(2,1)}, u32[]{:S(2)}) copy-start(bf16[51,1,16,64]{3,2,1,0:T(8,128)(2,1)} %copy-done.10) | copy-start | bytes 313348
  57.5 1.9 %copy-start.7 = (bf16[51,1,16,64]{3,2,1,0:T(8,128)(2,1)S(1)}, bf16[51,1,16,64]{3,2,1,0:T(8,128)(2,1)}, u32[]{:S(2)}) copy-start(bf16[51,1,16,64]{3,2,1,0:T(8,128)(2,1)} %copy-done.6) | copy-start | bytes 313348
  57.5 1.9 %copy-start.9 = (bf16[51,1,16,64]{3,2,1,0:T(8,128)(2,1)S(1)}, bf16[51,1,16,64]{3,2,1,0:T(8,128)(2,1)}, u32[]{:S(2)}) copy-start(bf16[51,1,16,64]{3,2,1,0:T(8,128)(2,1)} %copy-done.8) | copy-start | bytes 313348
  57.7 1.4 %copy-start.13 = (f32[16,51,51]{1,2,0:T(8,128)S(1)}, f32[16,51,51]{1,2,0:T(8,128)}, u32[]{:S(2)}) copy-start(f32[16,51,51]{1,2,0:T(8,128)} %copy-done.12) | copy-start | bytes 499396
  61.9 5.0 %copy-start.27 = (f32[51]{0:T(128)S(1)}, f32[51]{0:T(128)}, u32[]{:S(2)}) copy-start(f32[51]{0:T(128)} %get-tuple-element.33) | copy-start | bytes 616
  61.9 8.5 %copy-start.15 = (bf16[64,768]{1,0:T(8,128)(2,1)S(1)}, bf16[64,768]{1,0:T(8,128)(2,1)}, u32[]{:S(2)}) copy-start(bf16[64,768]{1,0:T(8,128)(2,1)} %copy-done.14) | copy-start | bytes 294916
  61.9 8.5 %copy-start.17 = (bf16[64,768]{1,0:T(8,128)(2,1)S(1)}, bf16[64,768]{1,0:T(8,128)(2,1)}, u32[]{:S(2)}) copy-start(bf16[64,768]{1,0:T(8,128)(2,1)} %copy-done.16) | copy-start | bytes 294916
  61.9 8.5 %copy-start.19 = (bf16[64,768]{1,0:T(8,128)(2,1)S(1)}, bf16[64,768]{1,0:T(8,128)(2,1)}, u32[]{:S(2)}) copy-start(bf16[64,768]{1,0:T(8,128)(2,1)} %copy-done.18) | copy-start | bytes 294916
  61.9 8.5 %copy-start.21 = (bf16[64,768]{1,0:T(8,128)(2,1)S(1)}, bf16[64,768]{1,0:T(8,128)(2,1)}, u32[]{:S(2)}) copy-start(bf16[64,768]{1,0:T(8,128)(2,1)} %copy-done.20) | copy-start | bytes 294916
  61.9 13.4 %copy-start.25 = (s32[204]{0:T(256)S(1)}, s32[204]{0:T(256)}, u32[]{:S(2)}) copy-start(s32[204]{0:T(256)} %eq.91) | copy-start | bytes 2452
  67.5 5.5 %collective-permute-start.3 = (bf16[51,1024]{1,0:T(8,128)(2,1)S(1)}, bf16[51,1024]{1,0:T(8,128)(2,1)S(1)}, u32[]{:S(2)}, u32[]{:S(2)}) collective-permute-start(bf16[51,1024]{1,0:T(8,128)(2,1)S(1)} %fusion.99), channel_id=1, source_target_pairs={{0,3},{1,0},{2,1},{3,2},{4,7},{5,4},{6,5},{7,6},{8,11},{9,8},{10,9... | collective-permute-start | bytes 313352 | tf_op jit(solution)/shard_map/ppermute | solution.py:192
  68.1 6.0 %collective-permute-start.4 = (bf16[51,1024]{1,0:T(8,128)(2,1)S(1)}, bf16[51,1024]{1,0:T(8,128)(2,1)S(1)}, u32[]{:S(2)}, u32[]{:S(2)}) collective-permute-start(bf16[51,1024]{1,0:T(8,128)(2,1)S(1)} %fusion.99), channel_id=1, source_target_pairs={{0,2},{1,3},{2,0},{3,1},{4,6},{5,7},{6,4},{7,5},{8,10},{9,11},{10,... | collective-permute-start | bytes 313352 | tf_op jit(solution)/shard_map/ppermute | solution.py:192
  69.6 5.7 %collective-permute-start.5 = (bf16[51,1024]{1,0:T(8,128)(2,1)S(1)}, bf16[51,1024]{1,0:T(8,128)(2,1)S(1)}, u32[]{:S(2)}, u32[]{:S(2)}) collective-permute-start(bf16[51,1024]{1,0:T(8,128)(2,1)S(1)} %fusion.99), channel_id=1, source_target_pairs={{0,1},{1,2},{2,3},{3,0},{4,5},{5,6},{6,7},{7,4},{8,9},{9,10},{10,1... | collective-permute-start | bytes 313352 | tf_op jit(solution)/shard_map/ppermute | solution.py:192
  (2 other events, 1.5 us)

commit v24 on v23

--- a/solution.py
+++ b/solution.py
@@ -279,12 +279,11 @@
     )
     own_cols = lax.dynamic_slice_in_dim(clip_pixels, own_index * col_width, col_width, 1)
     all_picks = (flat_index[:, None] == clip_ids[None, :]).astype(jnp.bfloat16)
-    gathered = jnp.dot(all_picks, own_cols, preferred_element_type=jnp.float32).astype(
-        jnp.bfloat16
-    )
-    embed_grad = jnp.einsum(
-        "vc,vd->cd",
-        gathered,
+    gathered_t = jnp.einsum(
+        "sc,vs->cv", own_cols, all_picks, preferred_element_type=jnp.float32
+    ).astype(jnp.bfloat16)
+    embed_grad = jnp.dot(
+        gathered_t,
         jnp.concatenate(ring_gather(grad_in, group_size), axis=0),
         preferred_element_type=jnp.float32,
     )

time: 78.4 us -> 78.4 us (level)
  no operation moved by 1% of the time
where the time goes in v24:
time: 78.4 us; the launch traced here: 77.8 us
  matrix products  35.6 us (45%)
  other arithmetic  12.2 us (16%)
  local copies, waits for them, and re-layouts  10.3 us (13%)
  starting transfers between devices  8.16 us (10%)
  waiting for transfers between devices  4.86 us (6%)
  Pallas kernels  3.54 us (5%)
  between operations  3.16 us (4%)
    ppermute x6, starting transfers between devices, ring_gather(): parts.append(lax.ppermute(values, 'mask', pairs))  8.16 us
    dot_general x6, matrix products, decoder_output(): jnp.einsum('pgi,gio->pgo', padded[offset:offset + total_rows], conv_w[off...  7.62 us
    dot_general x1, matrix products, copy_terms(): branch = attention_from(reuse_rows(visible_in, w_qkv, projected), w_out)  4.89 us
    ppermute x6, waiting for transfers between devices, ring_gather(): parts.append(lax.ppermute(values, 'mask', pairs))  4.86 us
    dot_general x2, matrix products, decoder_output(): jnp.dot(visible_out, dec_in, preferred_element_type=jnp.float32)  4.38 us
    pallas_call x1, Pallas kernels, masked_squares(): pl.pallas_call(functools.partial(loss_kernel, scale=scale), out_shape=(ja...  3.54 us
    dot_general x1, matrix products, project_rows(): jnp.dot(normed, w_qkv, preferred_element_type=jnp.float32)  3.1 us
    convert_element_type x1, other arithmetic, decoder_output(): return (lowered.astype(jnp.float32) + activated).astype(jnp.bfloat16)  2.97 us
  transfers between devices with their start and end apart: 6, of which 3 were waited for; matrix products, arithmetic and copies ran while one was open for 7% of the time, Pallas kernels for 0%

profile of v24, /device:TPU:0, one launch (start us, length us, event | category | flops | bytes accessed | tf_op | source)
XLA Modules:
  0.0 77.8 jit_solution(7154679823105243763)
XLA Ops:
  0.6 3.0 %collective-permute-start = (bf16[64,768]{1,0:T(8,128)(2,1)}, bf16[64,768]{1,0:T(8,128)(2,1)S(1)}, u32[]{:S(2)}, u32[]{:S(2)}) collective-permute-start(bf16[64,768]{1,0:T(8,128)(2,1)} %param.9), channel_id=1, source_target_pairs={{0,1},{1,2},{2,3},{3,0},{4,5},{5,6},{6,7},{7,4},{8,9},{9,10},{10,1... | collective-permute-start | bytes 294920 | tf_op jit(solution)/shard_map/ppermute | solution.py:192
  3.7 1.5 %collective-permute-start.1 = (bf16[64,768]{1,0:T(8,128)(2,1)}, bf16[64,768]{1,0:T(8,128)(2,1)S(1)}, u32[]{:S(2)}, u32[]{:S(2)}) collective-permute-start(bf16[64,768]{1,0:T(8,128)(2,1)} %param.9), channel_id=1, source_target_pairs={{0,2},{1,3},{2,0},{3,1},{4,6},{5,7},{6,4},{7,5},{8,10},{9,11},{10,... | collective-permute-start | bytes 294920 | tf_op jit(solution)/shard_map/ppermute | solution.py:192
  5.2 1.4 %collective-permute-start.2 = (bf16[64,768]{1,0:T(8,128)(2,1)}, bf16[64,768]{1,0:T(8,128)(2,1)S(1)}, u32[]{:S(2)}, u32[]{:S(2)}) collective-permute-start(bf16[64,768]{1,0:T(8,128)(2,1)} %param.9), channel_id=1, source_target_pairs={{0,3},{1,0},{2,1},{3,2},{4,7},{5,4},{6,5},{7,6},{8,11},{9,8},{10,9... | collective-permute-start | bytes 294920 | tf_op jit(solution)/shard_map/ppermute | solution.py:192
  10.4 1.9 %convolution_reduce_fusion = bf16[768]{0:T(1024)(128)(2,1)S(1)} fusion(bf16[1024,1]{0,1:T(2,128)(2,1)S(1)} %reshape.222, bf16[1024,768]{1,0:T(8,128)(2,1)} %param.15), kind=kOutput, calls=%fused_computation.53 | convolution fusion | flops 1572864 | bytes 1576448 | tf_op jit(solution)/shard_map/jvp()/dot_general | solution.py:93
  12.4 1.3 %select_select_fusion.3 = (bf16[64,768]{1,0:T(8,128)(2,1)S(1)}, bf16[64,768]{1,0:T(8,128)(2,1)S(1)}, bf16[64,768]{1,0:T(8,128)(2,1)S(1)}, bf16[64,768]{1,0:T(8,128)(2,1)S(1)}) fusion(bf16[64,768]{1,0:T(8,128)(2,1)S(1)} %collective-permute-done, bf16[64,768]{1,0:T(8,128)(2,1)S(1)} %collective-permute-done.1, bf16[64,768]{1,0:T(8,128)(2,1)S(1)} %collective-permute-done.2, ...), kind=kLoop, calls=%fused_computation.172 | loop fusion | flops 589824 | bytes 786444 | tf_op jit(solution)/shard_map/jit(_where)/select_n | solution.py:203
  13.7 2.2 %convert_reduce_fusion = (f32[256]{0:T(256)S(1)}, bf16[256,1024]{1,0:T(8,128)(2,1)S(1)}) fusion(bf16[768,1024]{1,0:T(8,128)(2,1)} %param.11, bf16[64,768]{1,0:T(8,128)(2,1)S(1)} %get-tuple-element.18, bf16[64,768]{1,0:T(8,128)(2,1)S(1)} %get-tuple-element.19, bf16[64,768]{1,0:T(8,128)(2,1)S(1)} %get-tuple-element.20, bf16[64,768]{1,0:T(8,128)(2,1)S(1)} %get-tuple-element.17), kind=kOutput, calls=%fused_computation.11 | convolution fusion | flops 405012224 | bytes 2491392 | tf_op jit(solution)/shard_map/dot_general | solution.py:238
  16.3 3.1 %convolution_convert_fusion = bf16[256,3072]{1,0:T(8,128)(2,1)} fusion(bf16[1024,3072]{1,0:T(8,128)(2,1)S(1)} %copy-done.4, bf16[256,1024]{1,0:T(8,128)(2,1)S(1)} %get-tuple-element.24, f32[256]{0:T(256)S(1)} %add_rsqrt_fusion.3, f32[256]{0:T(256)S(1)} %broadcast_multiply_fusion.2), kind=kOutput, calls=%fused_computation.2 | convolution fusion | flops 1612447744 | bytes 8390656 | tf_op jit(solution)/shard_map/dot_general | solution.py:50
  19.4 2.6 %copy.63 = bf16[256,3072]{0,1:T(8,128)(2,1)} copy(bf16[256,3072]{1,0:T(8,128)(2,1)} %convolution_convert_fusion) | data formatting | bytes 3145728 | tf_op jit(solution)/shard_map/convert_element_type | solution.py:50
  21.9 1.9 %convolution_convert_fusion.1 = bf16[51,3072]{1,0:T(8,128)(2,1)S(1)} fusion(bf16[256,3072]{1,0:T(8,128)(2,1)} %convolution_convert_fusion, s32[51]{0:T(128)S(1)} %fusion.114), kind=kOutput, calls=%fused_computation.4 | convolution fusion | flops 80385792 | bytes 1886412 | tf_op jit(solution)/shard_map/dot_general | solution.py:249
  23.9 0.9 %fusion.129 = (f32[51]{0:T(128)}, f32[51,1024]{1,0:T(8,128)S(1)}) fusion(bf16[256,1024]{1,0:T(8,128)(2,1)S(1)} %get-tuple-element.24, s32[51]{0:T(128)S(1)} %fusion.114), kind=kOutput, calls=%fused_computation.224 | convolution fusion | flops 26908364 | bytes 733592 | tf_op jit(solution)/shard_map/dot_general | solution.py:243
  25.0 1.0 %fusion = (f32[16,256]{1,0:T(8,128)S(1)}, f32[16,256,256]{1,2,0:T(8,128)S(1)}) fusion(f32[256,16]{0,1:T(8,128)S(1)} %get-tuple-element.43, bf16[256,3,16,64]{0,3,2,1:T(8,128)(2,1)S(1)} %bitcast.162, f32[256,16]{0,1:T(8,128)S(1)} %get-tuple-element.44), kind=kOutput, calls=%fused_computation.3 | convolution fusion | flops 137883648 | bytes 5292032 | tf_op jit(solution)/shard_map/qhd,khd->hqk/dot_general | solution.py:33
  26.0 0.8 %fusion.2 = bf16[16,64,256]{2,1,0:T(8,128)(2,1)S(1)} fusion(f32[16,256,256]{1,2,0:T(8,128)S(1)} %get-tuple-element.30, f32[16,256]{1,0:T(8,128)S(1)} %get-tuple-element.29, bf16[256,3,16,64]{0,3,2,1:T(8,128)(2,1)S(1)} %bitcast.163), kind=kOutput, calls=%fused_computation.12 | convolution fusion | flops 137625600 | bytes 5259264 | tf_op jit(solution)/shard_map/hqk,khd->qhd/dot_general | solution.py:38
  28.0 1.0 %multiply_convert_fusion.targets_ref = bf16[256,1024]{1,0:T(8,128)(2,1)} fusion(f32[256,1024]{1,0:T(8,128)S(1)} %get-tuple-element.32, f32[256]{0:T(256)S(1)} %add_rsqrt_fusion.2, f32[256]{0:T(256)S(1)} %broadcast_multiply_fusion.1), kind=kLoop, calls=%fused_computation.60 | loop fusion | flops 786432 | bytes 1574912 | tf_op jit(solution)/shard_map/convert_element_type | solution.py:255
  31.7 2.2 %convolution_convert_fusion.17 = bf16[51,768]{1,0:T(8,128)(2,1)S(1)} fusion(bf16[1024,768]{1,0:T(8,128)(2,1)} %param.15, f32[51,1024]{1,0:T(8,128)S(1)} %get-tuple-element.34, bf16[51,1024]{1,0:T(8,128)(2,1)S(1)} %reshape.208, bf16[1024,1024]{1,0:T(8,128)(2,1)S(1)} %copy-done), kind=kOutput, calls=%fused_computation.51 | convolution fusion | flops 187314432 | bytes 4061696 | tf_op jit(solution)/shard_map/jvp()/dot_general | solution.py:90
  34.5 1.3 %fusion.67 = f32[16,256,48]{1,2,0:T(8,128)S(1)} fusion(bf16[256,16,48]{0,2,1:T(8,128)(2,1)S(1)} %bitcast.168, bf16[3,16,48,48]{3,2,1,0:T(8,128)(2,1)} %param.16), kind=kOutput, calls=%fused_computation.130 | convolution fusion | flops 18874368 | bytes 1376256 | tf_op jit(solution)/shard_map/jvp(pgi,gio->pgo)/dot_general | solution.py:102
  35.8 1.2 %convolution_add_fusion.1 = f32[16,256,48]{1,2,0:T(8,128)S(1)} fusion(f32[16,256,48]{1,2,0:T(8,128)S(1)} %fusion.67, bf16[256,16,48]{0,2,1:T(8,128)(2,1)S(1)} %bitcast.169, bf16[3,16,48,48]{3,2,1,0:T(8,128)(2,1)} %param.16), kind=kOutput, calls=%fused_computation.14 | convolution fusion | flops 19070976 | bytes 2162688 | tf_op jit(solution)/shard_map/jvp(pgi,gio->pgo)/dot_general | solution.py:102
  37.1 1.4 %fusion.127 = (f32[256]{0:T(256)S(1)}, f32[16,256,48]{1,2,0:T(8,128)S(1)}) fusion(f32[16,256,48]{1,2,0:T(8,128)S(1)} %convolution_add_fusion.1, bf16[256,16,48]{0,2,1:T(8,128)(2,1)S(1)} %bitcast.170, bf16[3,16,48,48]{3,2,1,0:T(8,128)(2,1)} %param.16), kind=kOutput, calls=%fused_computation.222 | convolution fusion | flops 19267328 | bytes 2163712 | tf_op jit(solution)/shard_map/jvp(pgi,gio->pgo)/dot_general | solution.py:102
  39.3 1.4 %copy.62 = f32[256,768]{1,0:T(8,128)S(1)} copy(f32[256,768]{0,1:T(8,128)} %bitcast.164) | data formatting | bytes 1572864 | tf_op jit(solution)/shard_map/jvp()/reshape | solution.py:108
  40.7 3.0 %add_convert_fusion = (bf16[256,768]{1,0:T(8,128)(2,1)}, f32[256,768]{1,0:T(8,128)}) fusion(bf16[256,768]{1,0:T(8,128)(2,1)S(1)} %fusion.3, f32[256,768]{1,0:T(8,128)S(1)} %copy.62, f32[256]{0:T(256)S(1)} %fusion.113, f32[256]{0:T(256)S(1)} %broadcast_multiply_fusion), kind=kLoop, calls=%fused_computation.85 | loop fusion | flops 13565952 | bytes 2361344 | tf_op jit(solution)/shard_map/jvp()/convert_element_type | solution.py:109
  43.7 3.5 %jvp__.1 = (f32[1,1]{1,0:T(1,128)}, bf16[256,768]{1,0:T(8,128)(2,1)}) custom-call(bf16[256,768]{1,0:T(8,128)(2,1)} %get-tuple-element.12.hidden_ref, bf16[768,1024]{1,0:T(8,128)(2,1)} %dec_out_ref.1, bf16[256,1024]{1,0:T(8,128)(2,1)} %multiply_convert_fusion.targets_ref, f32[256,1]{1,0:T(8,128)} %copy.65.keep_ref), custom_call_target="tpu_custom_call" | custom-call | tf_op jit(solution)/shard_map/jvp()/pallas_call | solution.py:128
  47.2 2.0 %multiply_reduce_fusion.1 = f32[256]{0:T(256)S(1)} fusion(f32[256,768]{1,0:T(8,128)S(1)} %copy.62, f32[256]{0:T(256)S(1)} %broadcast_multiply_fusion, f32[256,768]{1,0:T(8,128)} %get-tuple-element.13, bf16[256,768]{1,0:T(8,128)(2,1)} %get-tuple-element.4, f32[256]{0:T(256)S(1)} %fusion.113), kind=kLoop, calls=%fused_computation.84 | loop fusion | flops 3538688 | bytes 1969152 | tf_op jit(solution)/shard_map/transpose(jvp())/reduce_sum | solution.py:23
  50.3 1.4 %fusion.7 = bf16[256,16,48]{0,2,1:T(8,128)(2,1)S(1)} fusion(bf16[16,48,256]{2,1,0:T(8,128)(2,1)S(1)} %bitcast.165, bf16[3,16,48,48]{3,2,1,0:T(8,128)(2,1)} %param.16), kind=kOutput, calls=%fused_computation.25 | convolution fusion | flops 18874368 | bytes 983040 | tf_op jit(solution)/shard_map/transpose(jvp(pgi,gio->pgo))/dot_general | solution.py:102
  51.7 1.2 %fusion.8 = bf16[256,16,48]{0,2,1:T(8,128)(2,1)S(1)} fusion(bf16[16,48,256]{2,1,0:T(8,128)(2,1)S(1)} %bitcast.166, bf16[3,16,48,48]{3,2,1,0:T(8,128)(2,1)} %param.16), kind=kOutput, calls=%fused_computation.26 | convolution fusion | flops 18874368 | bytes 983040 | tf_op jit(solution)/shard_map/transpose(jvp(pgi,gio->pgo))/dot_general | solution.py:102
  52.9 1.2 %fusion.9 = bf16[256,16,48]{0,2,1:T(8,128)(2,1)S(1)} fusion(bf16[16,48,256]{2,1,0:T(8,128)(2,1)S(1)} %bitcast.167, bf16[3,16,48,48]{3,2,1,0:T(8,128)(2,1)} %param.16), kind=kOutput, calls=%fused_computation.27 | convolution fusion | flops 18874368 | bytes 983040 | tf_op jit(solution)/shard_map/transpose(jvp(pgi,gio->pgo))/dot_general | solution.py:102
  54.6 2.2 %convolution_convert_fusion.12 = bf16[51,1024]{1,0:T(8,128)(2,1)S(1)} fusion(bf16[1024,768]{1,0:T(8,128)(2,1)} %param.15, bf16[256,768]{1,0:T(8,128)(2,1)S(1)} %copy-done.5, bf16[256,768]{1,0:T(8,128)(2,1)S(1)} %copy.70, pred[256]{0:T(512)(128)(4,1)} %copy-done.26, s32[51]{0:T(128)} %copy-done.24), kind=kOutput, calls=%fused_computation.45 | convolution fusion | flops 100964352 | bytes 2464204 | tf_op jit(solution)/shard_map/transpose(jvp())/dot_general | solution.py:90
  57.7 1.4 %fusion.16 = bf16[51,1,16,64]{3,0,2,1:T(8,128)(2,1)S(1)} fusion(bf16[51,16,64]{2,1,0:T(8,128)(2,1)S(1)} %reshape.215, f32[16,51,51]{1,2,0:T(8,128)} %copy-done.12, f32[16,51]{1,0:T(8,128)S(1)} %copy-done.23), kind=kOutput, calls=%fused_computation.41 | convolution fusion | flops 5462304 | bytes 378624 | tf_op jit(solution)/shard_map/transpose(jvp(hqk,khd->qhd))/dot_general | solution.py:38
  61.9 4.9 %convolution_convert_fusion.11 = bf16[51,1024]{1,0:T(8,128)(2,1)S(1)} fusion(bf16[51,3072]{1,0:T(8,128)(2,1)S(1)} %reshape.216, bf16[1024,3072]{1,0:T(8,128)(2,1)} %param.12), kind=kOutput, calls=%fused_computation.44 | convolution fusion | flops 320916480 | bytes 6709248 | tf_op jit(solution)/shard_map/transpose(jvp())/dot_general | solution.py:178
  68.1 1.5 %collective-permute-start.4 = (bf16[51,1024]{1,0:T(8,128)(2,1)S(1)}, bf16[51,1024]{1,0:T(8,128)(2,1)S(1)}, u32[]{:S(2)}, u32[]{:S(2)}) collective-permute-start(bf16[51,1024]{1,0:T(8,128)(2,1)S(1)} %fusion.99), channel_id=1, source_target_pairs={{0,2},{1,3},{2,0},{3,1},{4,6},{5,7},{6,4},{7,5},{8,10},{9,11},{10,... | collective-permute-start | bytes 313352 | tf_op jit(solution)/shard_map/ppermute | solution.py:192
  70.4 2.6 %collective-permute-done.3 = bf16[51,1024]{1,0:T(8,128)(2,1)S(1)} collective-permute-done((bf16[51,1024]{1,0:T(8,128)(2,1)S(1)}, bf16[51,1024]{1,0:T(8,128)(2,1)S(1)}, u32[]{:S(2)}, u32[]{:S(2)}) %collective-permute-start.3) | collective-permute-done | bytes 104480 | tf_op jit(solution)/shard_map/ppermute | solution.py:192
  73.0 1.0 %collective-permute-done.4 = bf16[51,1024]{1,0:T(8,128)(2,1)S(1)} collective-permute-done((bf16[51,1024]{1,0:T(8,128)(2,1)S(1)}, bf16[51,1024]{1,0:T(8,128)(2,1)S(1)}, u32[]{:S(2)}, u32[]{:S(2)}) %collective-permute-start.4) | collective-permute-done | bytes 104480 | tf_op jit(solution)/shard_map/ppermute | solution.py:192
  74.0 1.2 %collective-permute-done.5 = bf16[51,1024]{1,0:T(8,128)(2,1)S(1)} collective-permute-done((bf16[51,1024]{1,0:T(8,128)(2,1)S(1)}, bf16[51,1024]{1,0:T(8,128)(2,1)S(1)}, u32[]{:S(2)}, u32[]{:S(2)}) %collective-permute-start.5) | collective-permute-done | bytes 104480 | tf_op jit(solution)/shard_map/ppermute | solution.py:192
  75.3 1.4 %fusion.19 = f32[192,1024]{1,0:T(8,128)} fusion(bf16[51,1024]{1,0:T(8,128)(2,1)S(1)} %collective-permute-done.5, bf16[51,1024]{1,0:T(8,128)(2,1)S(1)} %collective-permute-done.4, bf16[51,1024]{1,0:T(8,128)(2,1)S(1)} %collective-permute-done.3, bf16[51,1024]{1,0:T(8,128)(2,1)S(1)} %fusion.99, bf16[256,768]{1,0:T(8,128)(2,1)S(1)} %pad_maximum_fusion, ...), kind=kOutput, calls=%fused_computation.52 | convolution fusion | flops 102032640 | bytes 1377284 | tf_op jit(solution)/shard_map/dot_general | solution.py:285
  (122 shorter events, 16.1 us)
Async XLA Ops:
  0.6 26.2 %copy-start = (bf16[1024,1024]{1,0:T(8,128)(2,1)S(1)}, bf16[1024,1024]{1,0:T(8,128)(2,1)}, u32[]{:S(2)}) copy-start(bf16[1024,1024]{1,0:T(8,128)(2,1)} %param.13) | copy-start | bytes 6291460
  0.6 11.7 %collective-permute-start = (bf16[64,768]{1,0:T(8,128)(2,1)}, bf16[64,768]{1,0:T(8,128)(2,1)S(1)}, u32[]{:S(2)}, u32[]{:S(2)}) collective-permute-start(bf16[64,768]{1,0:T(8,128)(2,1)} %param.9), channel_id=1, source_target_pairs={{0,1},{1,2},{2,3},{3,0},{4,5},{5,6},{6,7},{7,4},{8,9},{9,10},{10,1... | collective-permute-start | bytes 294920 | tf_op jit(solution)/shard_map/ppermute | solution.py:192
  3.7 8.7 %collective-permute-start.1 = (bf16[64,768]{1,0:T(8,128)(2,1)}, bf16[64,768]{1,0:T(8,128)(2,1)S(1)}, u32[]{:S(2)}, u32[]{:S(2)}) collective-permute-start(bf16[64,768]{1,0:T(8,128)(2,1)} %param.9), channel_id=1, source_target_pairs={{0,2},{1,3},{2,0},{3,1},{4,6},{5,7},{6,4},{7,5},{8,10},{9,11},{10,... | collective-permute-start | bytes 294920 | tf_op jit(solution)/shard_map/ppermute | solution.py:192
  5.2 7.2 %collective-permute-start.2 = (bf16[64,768]{1,0:T(8,128)(2,1)}, bf16[64,768]{1,0:T(8,128)(2,1)S(1)}, u32[]{:S(2)}, u32[]{:S(2)}) collective-permute-start(bf16[64,768]{1,0:T(8,128)(2,1)} %param.9), channel_id=1, source_target_pairs={{0,3},{1,0},{2,1},{3,2},{4,7},{5,4},{6,5},{7,6},{8,11},{9,8},{10,9... | collective-permute-start | bytes 294920 | tf_op jit(solution)/shard_map/ppermute | solution.py:192
  7.3 26.6 %copy-start.24 = (s32[51]{0:T(128)}, s32[51]{0:T(128)S(1)}, u32[]{:S(2)}) copy-start(s32[51]{0:T(128)S(1)} %fusion.114) | copy-start | bytes 616
  8.3 25.7 %copy-start.26 = (pred[256]{0:T(512)(128)(4,1)}, pred[256]{0:T(512)(128)(4,1)S(1)}, u32[]{:S(2)}) copy-start(pred[256]{0:T(512)(128)(4,1)S(1)} %broadcast_compare_fusion) | copy-start | bytes 772
  10.4 5.8 %copy-start.4 = (bf16[1024,3072]{1,0:T(8,128)(2,1)S(1)}, bf16[1024,3072]{1,0:T(8,128)(2,1)}, u32[]{:S(2)}) copy-start(bf16[1024,3072]{1,0:T(8,128)(2,1)} %param.12) | copy-start | bytes 18874372
  13.7 2.5 %copy-start.14 = (bf16[64,768]{1,0:T(8,128)(2,1)}, bf16[64,768]{1,0:T(8,128)(2,1)S(1)}, u32[]{:S(2)}) copy-start(bf16[64,768]{1,0:T(8,128)(2,1)S(1)} %get-tuple-element.17) | copy-start | bytes 294916
  13.7 2.5 %copy-start.16 = (bf16[64,768]{1,0:T(8,128)(2,1)}, bf16[64,768]{1,0:T(8,128)(2,1)S(1)}, u32[]{:S(2)}) copy-start(bf16[64,768]{1,0:T(8,128)(2,1)S(1)} %get-tuple-element.18) | copy-start | bytes 294916
  13.7 2.5 %copy-start.18 = (bf16[64,768]{1,0:T(8,128)(2,1)}, bf16[64,768]{1,0:T(8,128)(2,1)S(1)}, u32[]{:S(2)}) copy-start(bf16[64,768]{1,0:T(8,128)(2,1)S(1)} %get-tuple-element.19) | copy-start | bytes 294916
  13.7 2.5 %copy-start.20 = (bf16[64,768]{1,0:T(8,128)(2,1)}, bf16[64,768]{1,0:T(8,128)(2,1)S(1)}, u32[]{:S(2)}) copy-start(bf16[64,768]{1,0:T(8,128)(2,1)S(1)} %get-tuple-element.20) | copy-start | bytes 294916
  21.9 2.8 %copy-start.1 = (bf16[256,3072]{0,1:T(8,128)(2,1)S(1)}, bf16[256,3072]{0,1:T(8,128)(2,1)}, u32[]{:S(2)}) copy-start(bf16[256,3072]{0,1:T(8,128)(2,1)} %copy.63) | copy-start | bytes 4718596
  29.5 1.2 %copy-start.8 = (bf16[51,1,16,64]{3,2,1,0:T(8,128)(2,1)}, bf16[51,1,16,64]{3,2,1,0:T(8,128)(2,1)S(1)}, u32[]{:S(2)}) copy-start(bf16[51,1,16,64]{3,2,1,0:T(8,128)(2,1)S(1)} %get-tuple-element.16) | copy-start | bytes 313348
  29.5 1.2 %copy-start.10 = (bf16[51,1,16,64]{3,2,1,0:T(8,128)(2,1)}, bf16[51,1,16,64]{3,2,1,0:T(8,128)(2,1)S(1)}, u32[]{:S(2)}) copy-start(bf16[51,1,16,64]{3,2,1,0:T(8,128)(2,1)S(1)} %get-tuple-element.15) | copy-start | bytes 313348
  30.7 1.0 %copy-start.22 = (f32[16,51]{1,0:T(8,128)}, f32[16,51]{1,0:T(8,128)S(1)}, u32[]{:S(2)}) copy-start(f32[16,51]{1,0:T(8,128)S(1)} %get-tuple-element.25) | copy-start | bytes 9796
  38.4 0.9 %copy-start.2 = (f32[16,256,48]{1,2,0:T(8,128)}, f32[16,256,48]{1,2,0:T(8,128)S(1)}, u32[]{:S(2)}) copy-start(f32[16,256,48]{1,2,0:T(8,128)S(1)} %get-tuple-element.28) | copy-start | bytes 2359300
  47.2 2.0 %copy-start.3 = (f32[256,768]{1,0:T(8,128)S(1)}, f32[256,768]{1,0:T(8,128)}, u32[]{:S(2)}) copy-start(f32[256,768]{1,0:T(8,128)} %get-tuple-element.13) | copy-start | bytes 2359300
  47.2 2.0 %copy-start.5 = (bf16[256,768]{1,0:T(8,128)(2,1)S(1)}, bf16[256,768]{1,0:T(8,128)(2,1)}, u32[]{:S(2)}) copy-start(bf16[256,768]{1,0:T(8,128)(2,1)} %get-tuple-element.4) | copy-start | bytes 1179652
  50.1 3.9 %copy-start.23 = (f32[16,51]{1,0:T(8,128)S(1)}, f32[16,51]{1,0:T(8,128)}, u32[]{:S(2)}) copy-start(f32[16,51]{1,0:T(8,128)} %copy-done.22) | copy-start | bytes 9796
  56.8 2.4 %copy-start.11 = (bf16[51,1,16,64]{3,2,1,0:T(8,128)(2,1)S(1)}, bf16[51,1,16,64]{3,2,1,0:T(8,128)(2,1)}, u32[]{:S(2)}) copy-start(bf16[51,1,16,64]{3,2,1,0:T(8,128)(2,1)} %copy-done.10) | copy-start | bytes 313348
  57.5 1.9 %copy-start.7 = (bf16[51,1,16,64]{3,2,1,0:T(8,128)(2,1)S(1)}, bf16[51,1,16,64]{3,2,1,0:T(8,128)(2,1)}, u32[]{:S(2)}) copy-start(bf16[51,1,16,64]{3,2,1,0:T(8,128)(2,1)} %copy-done.6) | copy-start | bytes 313348
  57.5 1.9 %copy-start.9 = (bf16[51,1,16,64]{3,2,1,0:T(8,128)(2,1)S(1)}, bf16[51,1,16,64]{3,2,1,0:T(8,128)(2,1)}, u32[]{:S(2)}) copy-start(bf16[51,1,16,64]{3,2,1,0:T(8,128)(2,1)} %copy-done.8) | copy-start | bytes 313348
  57.7 1.4 %copy-start.13 = (f32[16,51,51]{1,2,0:T(8,128)S(1)}, f32[16,51,51]{1,2,0:T(8,128)}, u32[]{:S(2)}) copy-start(f32[16,51,51]{1,2,0:T(8,128)} %copy-done.12) | copy-start | bytes 499396
  61.9 5.0 %copy-start.27 = (f32[51]{0:T(128)S(1)}, f32[51]{0:T(128)}, u32[]{:S(2)}) copy-start(f32[51]{0:T(128)} %get-tuple-element.33) | copy-start | bytes 616
  61.9 8.5 %copy-start.15 = (bf16[64,768]{1,0:T(8,128)(2,1)S(1)}, bf16[64,768]{1,0:T(8,128)(2,1)}, u32[]{:S(2)}) copy-start(bf16[64,768]{1,0:T(8,128)(2,1)} %copy-done.14) | copy-start | bytes 294916
  61.9 8.5 %copy-start.17 = (bf16[64,768]{1,0:T(8,128)(2,1)S(1)}, bf16[64,768]{1,0:T(8,128)(2,1)}, u32[]{:S(2)}) copy-start(bf16[64,768]{1,0:T(8,128)(2,1)} %copy-done.16) | copy-start | bytes 294916
  61.9 8.5 %copy-start.19 = (bf16[64,768]{1,0:T(8,128)(2,1)S(1)}, bf16[64,768]{1,0:T(8,128)(2,1)}, u32[]{:S(2)}) copy-start(bf16[64,768]{1,0:T(8,128)(2,1)} %copy-done.18) | copy-start | bytes 294916
  61.9 8.5 %copy-start.21 = (bf16[64,768]{1,0:T(8,128)(2,1)S(1)}, bf16[64,768]{1,0:T(8,128)(2,1)}, u32[]{:S(2)}) copy-start(bf16[64,768]{1,0:T(8,128)(2,1)} %copy-done.20) | copy-start | bytes 294916
  61.9 13.4 %copy-start.25 = (s32[204]{0:T(256)S(1)}, s32[204]{0:T(256)}, u32[]{:S(2)}) copy-start(s32[204]{0:T(256)} %eq.103) | copy-start | bytes 2452
  67.5 5.5 %collective-permute-start.3 = (bf16[51,1024]{1,0:T(8,128)(2,1)S(1)}, bf16[51,1024]{1,0:T(8,128)(2,1)S(1)}, u32[]{:S(2)}, u32[]{:S(2)}) collective-permute-start(bf16[51,1024]{1,0:T(8,128)(2,1)S(1)} %fusion.99), channel_id=1, source_target_pairs={{0,3},{1,0},{2,1},{3,2},{4,7},{5,4},{6,5},{7,6},{8,11},{9,8},{10,9... | collective-permute-start | bytes 313352 | tf_op jit(solution)/shard_map/ppermute | solution.py:192
  68.1 6.0 %collective-permute-start.4 = (bf16[51,1024]{1,0:T(8,128)(2,1)S(1)}, bf16[51,1024]{1,0:T(8,128)(2,1)S(1)}, u32[]{:S(2)}, u32[]{:S(2)}) collective-permute-start(bf16[51,1024]{1,0:T(8,128)(2,1)S(1)} %fusion.99), channel_id=1, source_target_pairs={{0,2},{1,3},{2,0},{3,1},{4,6},{5,7},{6,4},{7,5},{8,10},{9,11},{10,... | collective-permute-start | bytes 313352 | tf_op jit(solution)/shard_map/ppermute | solution.py:192
  69.6 5.7 %collective-permute-start.5 = (bf16[51,1024]{1,0:T(8,128)(2,1)S(1)}, bf16[51,1024]{1,0:T(8,128)(2,1)S(1)}, u32[]{:S(2)}, u32[]{:S(2)}) collective-permute-start(bf16[51,1024]{1,0:T(8,128)(2,1)S(1)} %fusion.99), channel_id=1, source_target_pairs={{0,1},{1,2},{2,3},{3,0},{4,5},{5,6},{6,7},{7,4},{8,9},{9,10},{10,1... | collective-permute-start | bytes 313352 | tf_op jit(solution)/shard_map/ppermute | solution.py:192
  (2 other events, 1.5 us)

commit v25 on v18

--- a/solution.py
+++ b/solution.py
@@ -233,7 +233,9 @@
     visible_count = visible_index.shape[1]
     total_rows = tok_rows * group_size
     col_width = patches.shape[1] // group_size
-    positions = lax.dynamic_index_in_dim(visible_index, own_index, 0, keepdims=False)
+    doubled_index = jnp.concatenate([visible_index, visible_index], axis=0)
+    slot_index = lax.dynamic_slice_in_dim(doubled_index, own_index, copies, 0)
+    positions = slot_index[0]
     clip_pixels = in_mask_order(ring_gather(patches, group_size), own_index)
     embedded = jnp.dot(clip_pixels, embed_w, preferred_element_type=jnp.float32).astype(
         jnp.bfloat16
@@ -273,8 +275,7 @@
     squares, pullback = jax.vjp(objective, visible_in)
     (grad_in,) = pullback(jnp.ones_like(squares) * factor)
     copy_loss = jnp.reshape(squares / ((total_rows - visible_count) * D), (1,))
-    slot_copy = (own_index + jnp.arange(group_size, dtype=jnp.int32)) % group_size
-    flat_index = visible_index[slot_copy].reshape(copies * visible_count)
+    flat_index = slot_index.reshape(copies * visible_count)
     own_cols = lax.dynamic_slice_in_dim(clip_pixels, own_index * col_width, col_width, 1)
     all_picks = (flat_index[:, None] == clip_ids[None, :]).astype(jnp.bfloat16)
     gathered = jnp.dot(all_picks, own_cols, preferred_element_type=jnp.float32).astype(

time: 78.9 us -> 77.7 us (0.985)
  local copies, waits for them, and re-layouts: 11.5 us -> 9.62 us
    gather x1 -> x0, local copies, waits for them, and re-layouts: 1.24 us -> none  [on_device(): flat_index = visible_index[slot_copy].reshape(copies * visible_count)]
  transfers between devices with their start and end apart: 6 -> 6, of which waited for: 3 -> 3; matrix products, arithmetic and copies ran while one was open for 8% -> 7% of each run, Pallas kernels for 0% -> 0%
where the time goes in v25:
time: 77.7 us; the launch traced here: 77.2 us
  matrix products  35.6 us (46%)
  other arithmetic  12.2 us (16%)
  local copies, waits for them, and re-layouts  9.62 us (12%)
  starting transfers between devices  8.15 us (10%)
  waiting for transfers between devices  4.86 us (6%)
  Pallas kernels  3.54 us (5%)
  between operations  3.17 us (4%)
    ppermute x6, starting transfers between devices, ring_gather(): parts.append(lax.ppermute(values, 'mask', pairs))  8.15 us
    dot_general x6, matrix products, decoder_output(): jnp.einsum('pgi,gio->pgo', padded[offset:offset + total_rows], conv_w[off...  7.62 us
    dot_general x1, matrix products, copy_terms(): branch = attention_from(reuse_rows(visible_in, w_qkv, projected), w_out)  4.89 us
    ppermute x6, waiting for transfers between devices, ring_gather(): parts.append(lax.ppermute(values, 'mask', pairs))  4.86 us
    dot_general x2, matrix products, decoder_output(): jnp.dot(visible_out, dec_in, preferred_element_type=jnp.float32)  4.38 us
    pallas_call x1, Pallas kernels, masked_squares(): pl.pallas_call(functools.partial(loss_kernel, scale=scale), out_shape=(ja...  3.54 us
    dot_general x1, matrix products, project_rows(): jnp.dot(normed, w_qkv, preferred_element_type=jnp.float32)  3.1 us
    convert_element_type x1, other arithmetic, decoder_output(): return (lowered.astype(jnp.float32) + activated).astype(jnp.bfloat16)  2.97 us
  transfers between devices with their start and end apart: 6, of which 3 were waited for; matrix products, arithmetic and copies ran while one was open for 7% of the time, Pallas kernels for 0%

profile of v25, /device:TPU:0, one launch (start us, length us, event | category | flops | bytes accessed | tf_op | source)
XLA Modules:
  0.0 77.2 jit_solution(220229210581903971)
XLA Ops:
  0.6 3.0 %collective-permute-start = (bf16[64,768]{1,0:T(8,128)(2,1)}, bf16[64,768]{1,0:T(8,128)(2,1)S(1)}, u32[]{:S(2)}, u32[]{:S(2)}) collective-permute-start(bf16[64,768]{1,0:T(8,128)(2,1)} %param.9), channel_id=1, source_target_pairs={{0,1},{1,2},{2,3},{3,0},{4,5},{5,6},{6,7},{7,4},{8,9},{9,10},{10,1... | collective-permute-start | bytes 294920 | tf_op jit(solution)/shard_map/ppermute | solution.py:192
  3.7 1.5 %collective-permute-start.1 = (bf16[64,768]{1,0:T(8,128)(2,1)}, bf16[64,768]{1,0:T(8,128)(2,1)S(1)}, u32[]{:S(2)}, u32[]{:S(2)}) collective-permute-start(bf16[64,768]{1,0:T(8,128)(2,1)} %param.9), channel_id=1, source_target_pairs={{0,2},{1,3},{2,0},{3,1},{4,6},{5,7},{6,4},{7,5},{8,10},{9,11},{10,... | collective-permute-start | bytes 294920 | tf_op jit(solution)/shard_map/ppermute | solution.py:192
  5.2 1.4 %collective-permute-start.2 = (bf16[64,768]{1,0:T(8,128)(2,1)}, bf16[64,768]{1,0:T(8,128)(2,1)S(1)}, u32[]{:S(2)}, u32[]{:S(2)}) collective-permute-start(bf16[64,768]{1,0:T(8,128)(2,1)} %param.9), channel_id=1, source_target_pairs={{0,3},{1,0},{2,1},{3,2},{4,7},{5,4},{6,5},{7,6},{8,11},{9,8},{10,9... | collective-permute-start | bytes 294920 | tf_op jit(solution)/shard_map/ppermute | solution.py:192
  9.8 1.9 %convolution_reduce_fusion = bf16[768]{0:T(1024)(128)(2,1)S(1)} fusion(bf16[1024,1]{0,1:T(2,128)(2,1)S(1)} %reshape.221, bf16[1024,768]{1,0:T(8,128)(2,1)} %param.15), kind=kOutput, calls=%fused_computation.53 | convolution fusion | flops 1572864 | bytes 1576448 | tf_op jit(solution)/shard_map/jvp()/dot_general | solution.py:93
  11.7 1.3 %select_select_fusion.3 = (bf16[64,768]{1,0:T(8,128)(2,1)S(1)}, bf16[64,768]{1,0:T(8,128)(2,1)S(1)}, bf16[64,768]{1,0:T(8,128)(2,1)S(1)}, bf16[64,768]{1,0:T(8,128)(2,1)S(1)}) fusion(bf16[64,768]{1,0:T(8,128)(2,1)S(1)} %collective-permute-done, bf16[64,768]{1,0:T(8,128)(2,1)S(1)} %collective-permute-done.1, bf16[64,768]{1,0:T(8,128)(2,1)S(1)} %collective-permute-done.2, ...), kind=kLoop, calls=%fused_computation.172 | loop fusion | flops 589824 | bytes 786444 | tf_op jit(solution)/shard_map/jit(_where)/select_n | solution.py:203
  13.0 2.2 %convert_reduce_fusion = (f32[256]{0:T(256)S(1)}, bf16[256,1024]{1,0:T(8,128)(2,1)S(1)}) fusion(bf16[768,1024]{1,0:T(8,128)(2,1)} %param.11, bf16[64,768]{1,0:T(8,128)(2,1)S(1)} %get-tuple-element.18, bf16[64,768]{1,0:T(8,128)(2,1)S(1)} %get-tuple-element.19, bf16[64,768]{1,0:T(8,128)(2,1)S(1)} %get-tuple-element.20, bf16[64,768]{1,0:T(8,128)(2,1)S(1)} %get-tuple-element.17), kind=kOutput, calls=%fused_computation.11 | convolution fusion | flops 405012224 | bytes 2491392 | tf_op jit(solution)/shard_map/dot_general | solution.py:240
  15.6 3.1 %convolution_convert_fusion = bf16[256,3072]{1,0:T(8,128)(2,1)} fusion(bf16[1024,3072]{1,0:T(8,128)(2,1)S(1)} %copy-done.4, bf16[256,1024]{1,0:T(8,128)(2,1)S(1)} %get-tuple-element.24, f32[256]{0:T(256)S(1)} %add_rsqrt_fusion.3, f32[256]{0:T(256)S(1)} %broadcast_multiply_fusion.2), kind=kOutput, calls=%fused_computation.2 | convolution fusion | flops 1612447744 | bytes 8390656 | tf_op jit(solution)/shard_map/dot_general | solution.py:50
  18.7 2.6 %copy.63 = bf16[256,3072]{0,1:T(8,128)(2,1)} copy(bf16[256,3072]{1,0:T(8,128)(2,1)} %convolution_convert_fusion) | data formatting | bytes 3145728 | tf_op jit(solution)/shard_map/convert_element_type | solution.py:50
  21.3 1.9 %convolution_convert_fusion.1 = bf16[51,3072]{1,0:T(8,128)(2,1)S(1)} fusion(bf16[256,3072]{1,0:T(8,128)(2,1)} %convolution_convert_fusion, s32[51]{0:T(128)S(1)} %slice_bitcast_fusion.6), kind=kOutput, calls=%fused_computation.4 | convolution fusion | flops 80385792 | bytes 1886412 | tf_op jit(solution)/shard_map/dot_general | solution.py:251
  23.2 0.9 %fusion.128 = (f32[51]{0:T(128)}, f32[51,1024]{1,0:T(8,128)S(1)}) fusion(bf16[256,1024]{1,0:T(8,128)(2,1)S(1)} %get-tuple-element.24, s32[51]{0:T(128)S(1)} %slice_bitcast_fusion.6), kind=kOutput, calls=%fused_computation.223 | convolution fusion | flops 26908364 | bytes 733592 | tf_op jit(solution)/shard_map/dot_general | solution.py:245
  24.4 1.0 %fusion = (f32[16,256]{1,0:T(8,128)S(1)}, f32[16,256,256]{1,2,0:T(8,128)S(1)}) fusion(f32[256,16]{0,1:T(8,128)S(1)} %get-tuple-element.43, bf16[256,3,16,64]{0,3,2,1:T(8,128)(2,1)S(1)} %bitcast.162, f32[256,16]{0,1:T(8,128)S(1)} %get-tuple-element.44), kind=kOutput, calls=%fused_computation.3 | convolution fusion | flops 137883648 | bytes 5292032 | tf_op jit(solution)/shard_map/qhd,khd->hqk/dot_general | solution.py:33
  25.3 0.8 %fusion.2 = bf16[16,64,256]{2,1,0:T(8,128)(2,1)S(1)} fusion(f32[16,256,256]{1,2,0:T(8,128)S(1)} %get-tuple-element.30, f32[16,256]{1,0:T(8,128)S(1)} %get-tuple-element.29, bf16[256,3,16,64]{0,3,2,1:T(8,128)(2,1)S(1)} %bitcast.163), kind=kOutput, calls=%fused_computation.12 | convolution fusion | flops 137625600 | bytes 5259264 | tf_op jit(solution)/shard_map/hqk,khd->qhd/dot_general | solution.py:38
  27.3 1.0 %multiply_convert_fusion.targets_ref = bf16[256,1024]{1,0:T(8,128)(2,1)} fusion(f32[256,1024]{1,0:T(8,128)S(1)} %get-tuple-element.32, f32[256]{0:T(256)S(1)} %add_rsqrt_fusion.2, f32[256]{0:T(256)S(1)} %broadcast_multiply_fusion.1), kind=kLoop, calls=%fused_computation.60 | loop fusion | flops 786432 | bytes 1574912 | tf_op jit(solution)/shard_map/convert_element_type | solution.py:257
  31.0 2.2 %convolution_convert_fusion.17 = bf16[51,768]{1,0:T(8,128)(2,1)S(1)} fusion(bf16[1024,768]{1,0:T(8,128)(2,1)} %param.15, f32[51,1024]{1,0:T(8,128)S(1)} %get-tuple-element.34, bf16[51,1024]{1,0:T(8,128)(2,1)S(1)} %reshape.207, bf16[1024,1024]{1,0:T(8,128)(2,1)S(1)} %copy-done), kind=kOutput, calls=%fused_computation.51 | convolution fusion | flops 187314432 | bytes 4061696 | tf_op jit(solution)/shard_map/jvp()/dot_general | solution.py:90
  33.8 1.3 %fusion.67 = f32[16,256,48]{1,2,0:T(8,128)S(1)} fusion(bf16[256,16,48]{0,2,1:T(8,128)(2,1)S(1)} %bitcast.168, bf16[3,16,48,48]{3,2,1,0:T(8,128)(2,1)} %param.16), kind=kOutput, calls=%fused_computation.130 | convolution fusion | flops 18874368 | bytes 1376256 | tf_op jit(solution)/shard_map/jvp(pgi,gio->pgo)/dot_general | solution.py:102
  35.1 1.2 %convolution_add_fusion.1 = f32[16,256,48]{1,2,0:T(8,128)S(1)} fusion(f32[16,256,48]{1,2,0:T(8,128)S(1)} %fusion.67, bf16[256,16,48]{0,2,1:T(8,128)(2,1)S(1)} %bitcast.169, bf16[3,16,48,48]{3,2,1,0:T(8,128)(2,1)} %param.16), kind=kOutput, calls=%fused_computation.14 | convolution fusion | flops 19070976 | bytes 2162688 | tf_op jit(solution)/shard_map/jvp(pgi,gio->pgo)/dot_general | solution.py:102
  36.4 1.4 %fusion.126 = (f32[256]{0:T(256)S(1)}, f32[16,256,48]{1,2,0:T(8,128)S(1)}) fusion(f32[16,256,48]{1,2,0:T(8,128)S(1)} %convolution_add_fusion.1, bf16[256,16,48]{0,2,1:T(8,128)(2,1)S(1)} %bitcast.170, bf16[3,16,48,48]{3,2,1,0:T(8,128)(2,1)} %param.16), kind=kOutput, calls=%fused_computation.221 | convolution fusion | flops 19267328 | bytes 2163712 | tf_op jit(solution)/shard_map/jvp(pgi,gio->pgo)/dot_general | solution.py:102
  38.6 1.4 %copy.62 = f32[256,768]{1,0:T(8,128)S(1)} copy(f32[256,768]{0,1:T(8,128)} %bitcast.164) | data formatting | bytes 1572864 | tf_op jit(solution)/shard_map/jvp()/reshape | solution.py:108
  40.0 3.0 %add_convert_fusion = (bf16[256,768]{1,0:T(8,128)(2,1)}, f32[256,768]{1,0:T(8,128)}) fusion(bf16[256,768]{1,0:T(8,128)(2,1)S(1)} %fusion.3, f32[256,768]{1,0:T(8,128)S(1)} %copy.62, f32[256]{0:T(256)S(1)} %fusion.111, f32[256]{0:T(256)S(1)} %broadcast_multiply_fusion), kind=kLoop, calls=%fused_computation.85 | loop fusion | flops 13565952 | bytes 2361344 | tf_op jit(solution)/shard_map/jvp()/convert_element_type | solution.py:109
  43.0 3.5 %jvp__.1 = (f32[1,1]{1,0:T(1,128)}, bf16[256,768]{1,0:T(8,128)(2,1)}) custom-call(bf16[256,768]{1,0:T(8,128)(2,1)} %get-tuple-element.12.hidden_ref, bf16[768,1024]{1,0:T(8,128)(2,1)} %dec_out_ref.1, bf16[256,1024]{1,0:T(8,128)(2,1)} %multiply_convert_fusion.targets_ref, f32[256,1]{1,0:T(8,128)} %copy.65.keep_ref), custom_call_target="tpu_custom_call" | custom-call | tf_op jit(solution)/shard_map/jvp()/pallas_call | solution.py:128
  46.5 2.0 %multiply_reduce_fusion.1 = f32[256]{0:T(256)S(1)} fusion(f32[256,768]{1,0:T(8,128)S(1)} %copy.62, f32[256]{0:T(256)S(1)} %broadcast_multiply_fusion, f32[256,768]{1,0:T(8,128)} %get-tuple-element.13, bf16[256,768]{1,0:T(8,128)(2,1)} %get-tuple-element.4, f32[256]{0:T(256)S(1)} %fusion.111), kind=kLoop, calls=%fused_computation.84 | loop fusion | flops 3538688 | bytes 1969152 | tf_op jit(solution)/shard_map/transpose(jvp())/reduce_sum | solution.py:23
  49.6 1.4 %fusion.7 = bf16[256,16,48]{0,2,1:T(8,128)(2,1)S(1)} fusion(bf16[16,48,256]{2,1,0:T(8,128)(2,1)S(1)} %bitcast.165, bf16[3,16,48,48]{3,2,1,0:T(8,128)(2,1)} %param.16), kind=kOutput, calls=%fused_computation.25 | convolution fusion | flops 18874368 | bytes 983040 | tf_op jit(solution)/shard_map/transpose(jvp(pgi,gio->pgo))/dot_general | solution.py:102
  51.0 1.2 %fusion.8 = bf16[256,16,48]{0,2,1:T(8,128)(2,1)S(1)} fusion(bf16[16,48,256]{2,1,0:T(8,128)(2,1)S(1)} %bitcast.166, bf16[3,16,48,48]{3,2,1,0:T(8,128)(2,1)} %param.16), kind=kOutput, calls=%fused_computation.26 | convolution fusion | flops 18874368 | bytes 983040 | tf_op jit(solution)/shard_map/transpose(jvp(pgi,gio->pgo))/dot_general | solution.py:102
  52.2 1.2 %fusion.9 = bf16[256,16,48]{0,2,1:T(8,128)(2,1)S(1)} fusion(bf16[16,48,256]{2,1,0:T(8,128)(2,1)S(1)} %bitcast.167, bf16[3,16,48,48]{3,2,1,0:T(8,128)(2,1)} %param.16), kind=kOutput, calls=%fused_computation.27 | convolution fusion | flops 18874368 | bytes 983040 | tf_op jit(solution)/shard_map/transpose(jvp(pgi,gio->pgo))/dot_general | solution.py:102
  53.9 2.2 %convolution_convert_fusion.12 = bf16[51,1024]{1,0:T(8,128)(2,1)S(1)} fusion(bf16[1024,768]{1,0:T(8,128)(2,1)} %param.15, bf16[256,768]{1,0:T(8,128)(2,1)S(1)} %copy-done.5, bf16[256,768]{1,0:T(8,128)(2,1)S(1)} %copy.70, pred[256]{0:T(512)(128)(4,1)} %copy-done.26, s32[51]{0:T(128)} %copy-done.24), kind=kOutput, calls=%fused_computation.45 | convolution fusion | flops 100964352 | bytes 2464204 | tf_op jit(solution)/shard_map/transpose(jvp())/dot_general | solution.py:90
  57.1 1.4 %fusion.16 = bf16[51,1,16,64]{3,0,2,1:T(8,128)(2,1)S(1)} fusion(bf16[51,16,64]{2,1,0:T(8,128)(2,1)S(1)} %reshape.214, f32[16,51,51]{1,2,0:T(8,128)} %copy-done.12, f32[16,51]{1,0:T(8,128)S(1)} %copy-done.23), kind=kOutput, calls=%fused_computation.41 | convolution fusion | flops 5462304 | bytes 378624 | tf_op jit(solution)/shard_map/transpose(jvp(hqk,khd->qhd))/dot_general | solution.py:38
  61.3 4.9 %convolution_convert_fusion.11 = bf16[51,1024]{1,0:T(8,128)(2,1)S(1)} fusion(bf16[51,3072]{1,0:T(8,128)(2,1)S(1)} %reshape.215, bf16[1024,3072]{1,0:T(8,128)(2,1)} %param.12), kind=kOutput, calls=%fused_computation.44 | convolution fusion | flops 320916480 | bytes 6709248 | tf_op jit(solution)/shard_map/transpose(jvp())/dot_general | solution.py:178
  67.4 1.5 %collective-permute-start.4 = (bf16[51,1024]{1,0:T(8,128)(2,1)S(1)}, bf16[51,1024]{1,0:T(8,128)(2,1)S(1)}, u32[]{:S(2)}, u32[]{:S(2)}) collective-permute-start(bf16[51,1024]{1,0:T(8,128)(2,1)S(1)} %fusion.99), channel_id=1, source_target_pairs={{0,2},{1,3},{2,0},{3,1},{4,6},{5,7},{6,4},{7,5},{8,10},{9,11},{10,... | collective-permute-start | bytes 313352 | tf_op jit(solution)/shard_map/ppermute | solution.py:192
  69.7 2.6 %collective-permute-done.3 = bf16[51,1024]{1,0:T(8,128)(2,1)S(1)} collective-permute-done((bf16[51,1024]{1,0:T(8,128)(2,1)S(1)}, bf16[51,1024]{1,0:T(8,128)(2,1)S(1)}, u32[]{:S(2)}, u32[]{:S(2)}) %collective-permute-start.3) | collective-permute-done | bytes 104480 | tf_op jit(solution)/shard_map/ppermute | solution.py:192
  72.3 1.0 %collective-permute-done.4 = bf16[51,1024]{1,0:T(8,128)(2,1)S(1)} collective-permute-done((bf16[51,1024]{1,0:T(8,128)(2,1)S(1)}, bf16[51,1024]{1,0:T(8,128)(2,1)S(1)}, u32[]{:S(2)}, u32[]{:S(2)}) %collective-permute-start.4) | collective-permute-done | bytes 104480 | tf_op jit(solution)/shard_map/ppermute | solution.py:192
  73.3 1.2 %collective-permute-done.5 = bf16[51,1024]{1,0:T(8,128)(2,1)S(1)} collective-permute-done((bf16[51,1024]{1,0:T(8,128)(2,1)S(1)}, bf16[51,1024]{1,0:T(8,128)(2,1)S(1)}, u32[]{:S(2)}, u32[]{:S(2)}) %collective-permute-start.5) | collective-permute-done | bytes 104480 | tf_op jit(solution)/shard_map/ppermute | solution.py:192
  74.6 1.4 %fusion.19 = f32[192,1024]{1,0:T(8,128)} fusion(bf16[51,1024]{1,0:T(8,128)(2,1)S(1)} %collective-permute-done.5, bf16[51,1024]{1,0:T(8,128)(2,1)S(1)} %collective-permute-done.4, bf16[51,1024]{1,0:T(8,128)(2,1)S(1)} %collective-permute-done.3, bf16[51,1024]{1,0:T(8,128)(2,1)S(1)} %fusion.99, bf16[256,768]{1,0:T(8,128)(2,1)S(1)} %pad_maximum_fusion, ...), kind=kOutput, calls=%fused_computation.52 | convolution fusion | flops 102032640 | bytes 1377284 | tf_op jit(solution)/shard_map/vc,vd->cd/dot_general | solution.py:284
  (122 shorter events, 15.4 us)
Async XLA Ops:
  0.6 25.6 %copy-start = (bf16[1024,1024]{1,0:T(8,128)(2,1)S(1)}, bf16[1024,1024]{1,0:T(8,128)(2,1)}, u32[]{:S(2)}) copy-start(bf16[1024,1024]{1,0:T(8,128)(2,1)} %param.13) | copy-start | bytes 6291460
  0.6 11.0 %collective-permute-start = (bf16[64,768]{1,0:T(8,128)(2,1)}, bf16[64,768]{1,0:T(8,128)(2,1)S(1)}, u32[]{:S(2)}, u32[]{:S(2)}) collective-permute-start(bf16[64,768]{1,0:T(8,128)(2,1)} %param.9), channel_id=1, source_target_pairs={{0,1},{1,2},{2,3},{3,0},{4,5},{5,6},{6,7},{7,4},{8,9},{9,10},{10,1... | collective-permute-start | bytes 294920 | tf_op jit(solution)/shard_map/ppermute | solution.py:192
  3.7 8.0 %collective-permute-start.1 = (bf16[64,768]{1,0:T(8,128)(2,1)}, bf16[64,768]{1,0:T(8,128)(2,1)S(1)}, u32[]{:S(2)}, u32[]{:S(2)}) collective-permute-start(bf16[64,768]{1,0:T(8,128)(2,1)} %param.9), channel_id=1, source_target_pairs={{0,2},{1,3},{2,0},{3,1},{4,6},{5,7},{6,4},{7,5},{8,10},{9,11},{10,... | collective-permute-start | bytes 294920 | tf_op jit(solution)/shard_map/ppermute | solution.py:192
  5.2 6.5 %collective-permute-start.2 = (bf16[64,768]{1,0:T(8,128)(2,1)}, bf16[64,768]{1,0:T(8,128)(2,1)S(1)}, u32[]{:S(2)}, u32[]{:S(2)}) collective-permute-start(bf16[64,768]{1,0:T(8,128)(2,1)} %param.9), channel_id=1, source_target_pairs={{0,3},{1,0},{2,1},{3,2},{4,7},{5,4},{6,5},{7,6},{8,11},{9,8},{10,9... | collective-permute-start | bytes 294920 | tf_op jit(solution)/shard_map/ppermute | solution.py:192
  7.4 25.8 %copy-start.24 = (s32[51]{0:T(128)}, s32[51]{0:T(128)S(1)}, u32[]{:S(2)}) copy-start(s32[51]{0:T(128)S(1)} %slice_bitcast_fusion.6) | copy-start | bytes 616
  8.3 25.0 %copy-start.26 = (pred[256]{0:T(512)(128)(4,1)}, pred[256]{0:T(512)(128)(4,1)S(1)}, u32[]{:S(2)}) copy-start(pred[256]{0:T(512)(128)(4,1)S(1)} %broadcast_compare_fusion) | copy-start | bytes 772
  9.8 5.8 %copy-start.4 = (bf16[1024,3072]{1,0:T(8,128)(2,1)S(1)}, bf16[1024,3072]{1,0:T(8,128)(2,1)}, u32[]{:S(2)}) copy-start(bf16[1024,3072]{1,0:T(8,128)(2,1)} %param.12) | copy-start | bytes 18874372
  13.0 2.5 %copy-start.14 = (bf16[64,768]{1,0:T(8,128)(2,1)}, bf16[64,768]{1,0:T(8,128)(2,1)S(1)}, u32[]{:S(2)}) copy-start(bf16[64,768]{1,0:T(8,128)(2,1)S(1)} %get-tuple-element.17) | copy-start | bytes 294916
  13.0 2.5 %copy-start.16 = (bf16[64,768]{1,0:T(8,128)(2,1)}, bf16[64,768]{1,0:T(8,128)(2,1)S(1)}, u32[]{:S(2)}) copy-start(bf16[64,768]{1,0:T(8,128)(2,1)S(1)} %get-tuple-element.18) | copy-start | bytes 294916
  13.0 2.5 %copy-start.18 = (bf16[64,768]{1,0:T(8,128)(2,1)}, bf16[64,768]{1,0:T(8,128)(2,1)S(1)}, u32[]{:S(2)}) copy-start(bf16[64,768]{1,0:T(8,128)(2,1)S(1)} %get-tuple-element.19) | copy-start | bytes 294916
  13.0 2.5 %copy-start.20 = (bf16[64,768]{1,0:T(8,128)(2,1)}, bf16[64,768]{1,0:T(8,128)(2,1)S(1)}, u32[]{:S(2)}) copy-start(bf16[64,768]{1,0:T(8,128)(2,1)S(1)} %get-tuple-element.20) | copy-start | bytes 294916
  21.3 2.8 %copy-start.1 = (bf16[256,3072]{0,1:T(8,128)(2,1)S(1)}, bf16[256,3072]{0,1:T(8,128)(2,1)}, u32[]{:S(2)}) copy-start(bf16[256,3072]{0,1:T(8,128)(2,1)} %copy.63) | copy-start | bytes 4718596
  28.8 1.2 %copy-start.8 = (bf16[51,1,16,64]{3,2,1,0:T(8,128)(2,1)}, bf16[51,1,16,64]{3,2,1,0:T(8,128)(2,1)S(1)}, u32[]{:S(2)}) copy-start(bf16[51,1,16,64]{3,2,1,0:T(8,128)(2,1)S(1)} %get-tuple-element.16) | copy-start | bytes 313348
  28.8 1.2 %copy-start.10 = (bf16[51,1,16,64]{3,2,1,0:T(8,128)(2,1)}, bf16[51,1,16,64]{3,2,1,0:T(8,128)(2,1)S(1)}, u32[]{:S(2)}) copy-start(bf16[51,1,16,64]{3,2,1,0:T(8,128)(2,1)S(1)} %get-tuple-element.15) | copy-start | bytes 313348
  30.0 1.0 %copy-start.22 = (f32[16,51]{1,0:T(8,128)}, f32[16,51]{1,0:T(8,128)S(1)}, u32[]{:S(2)}) copy-start(f32[16,51]{1,0:T(8,128)S(1)} %get-tuple-element.25) | copy-start | bytes 9796
  37.7 0.9 %copy-start.2 = (f32[16,256,48]{1,2,0:T(8,128)}, f32[16,256,48]{1,2,0:T(8,128)S(1)}, u32[]{:S(2)}) copy-start(f32[16,256,48]{1,2,0:T(8,128)S(1)} %get-tuple-element.28) | copy-start | bytes 2359300
  46.5 2.0 %copy-start.3 = (f32[256,768]{1,0:T(8,128)S(1)}, f32[256,768]{1,0:T(8,128)}, u32[]{:S(2)}) copy-start(f32[256,768]{1,0:T(8,128)} %get-tuple-element.13) | copy-start | bytes 2359300
  46.5 2.0 %copy-start.5 = (bf16[256,768]{1,0:T(8,128)(2,1)S(1)}, bf16[256,768]{1,0:T(8,128)(2,1)}, u32[]{:S(2)}) copy-start(bf16[256,768]{1,0:T(8,128)(2,1)} %get-tuple-element.4) | copy-start | bytes 1179652
  49.5 3.9 %copy-start.23 = (f32[16,51]{1,0:T(8,128)S(1)}, f32[16,51]{1,0:T(8,128)}, u32[]{:S(2)}) copy-start(f32[16,51]{1,0:T(8,128)} %copy-done.22) | copy-start | bytes 9796
  56.1 2.4 %copy-start.11 = (bf16[51,1,16,64]{3,2,1,0:T(8,128)(2,1)S(1)}, bf16[51,1,16,64]{3,2,1,0:T(8,128)(2,1)}, u32[]{:S(2)}) copy-start(bf16[51,1,16,64]{3,2,1,0:T(8,128)(2,1)} %copy-done.10) | copy-start | bytes 313348
  56.9 1.9 %copy-start.7 = (bf16[51,1,16,64]{3,2,1,0:T(8,128)(2,1)S(1)}, bf16[51,1,16,64]{3,2,1,0:T(8,128)(2,1)}, u32[]{:S(2)}) copy-start(bf16[51,1,16,64]{3,2,1,0:T(8,128)(2,1)} %copy-done.6) | copy-start | bytes 313348
  56.9 1.9 %copy-start.9 = (bf16[51,1,16,64]{3,2,1,0:T(8,128)(2,1)S(1)}, bf16[51,1,16,64]{3,2,1,0:T(8,128)(2,1)}, u32[]{:S(2)}) copy-start(bf16[51,1,16,64]{3,2,1,0:T(8,128)(2,1)} %copy-done.8) | copy-start | bytes 313348
  57.1 1.4 %copy-start.13 = (f32[16,51,51]{1,2,0:T(8,128)S(1)}, f32[16,51,51]{1,2,0:T(8,128)}, u32[]{:S(2)}) copy-start(f32[16,51,51]{1,2,0:T(8,128)} %copy-done.12) | copy-start | bytes 499396
  61.2 5.0 %copy-start.27 = (f32[51]{0:T(128)S(1)}, f32[51]{0:T(128)}, u32[]{:S(2)}) copy-start(f32[51]{0:T(128)} %get-tuple-element.33) | copy-start | bytes 616
  61.2 8.5 %copy-start.15 = (bf16[64,768]{1,0:T(8,128)(2,1)S(1)}, bf16[64,768]{1,0:T(8,128)(2,1)}, u32[]{:S(2)}) copy-start(bf16[64,768]{1,0:T(8,128)(2,1)} %copy-done.14) | copy-start | bytes 294916
  61.2 8.5 %copy-start.17 = (bf16[64,768]{1,0:T(8,128)(2,1)S(1)}, bf16[64,768]{1,0:T(8,128)(2,1)}, u32[]{:S(2)}) copy-start(bf16[64,768]{1,0:T(8,128)(2,1)} %copy-done.16) | copy-start | bytes 294916
  61.2 8.5 %copy-start.19 = (bf16[64,768]{1,0:T(8,128)(2,1)S(1)}, bf16[64,768]{1,0:T(8,128)(2,1)}, u32[]{:S(2)}) copy-start(bf16[64,768]{1,0:T(8,128)(2,1)} %copy-done.18) | copy-start | bytes 294916
  61.2 8.5 %copy-start.21 = (bf16[64,768]{1,0:T(8,128)(2,1)S(1)}, bf16[64,768]{1,0:T(8,128)(2,1)}, u32[]{:S(2)}) copy-start(bf16[64,768]{1,0:T(8,128)(2,1)} %copy-done.20) | copy-start | bytes 294916
  61.3 13.3 %copy-start.25 = (s32[204]{0:T(256)S(1)}, s32[204]{0:T(256)}, u32[]{:S(2)}) copy-start(s32[204]{0:T(256)} %eq.91) | copy-start | bytes 2452
  66.8 5.5 %collective-permute-start.3 = (bf16[51,1024]{1,0:T(8,128)(2,1)S(1)}, bf16[51,1024]{1,0:T(8,128)(2,1)S(1)}, u32[]{:S(2)}, u32[]{:S(2)}) collective-permute-start(bf16[51,1024]{1,0:T(8,128)(2,1)S(1)} %fusion.99), channel_id=1, source_target_pairs={{0,3},{1,0},{2,1},{3,2},{4,7},{5,4},{6,5},{7,6},{8,11},{9,8},{10,9... | collective-permute-start | bytes 313352 | tf_op jit(solution)/shard_map/ppermute | solution.py:192
  67.4 6.0 %collective-permute-start.4 = (bf16[51,1024]{1,0:T(8,128)(2,1)S(1)}, bf16[51,1024]{1,0:T(8,128)(2,1)S(1)}, u32[]{:S(2)}, u32[]{:S(2)}) collective-permute-start(bf16[51,1024]{1,0:T(8,128)(2,1)S(1)} %fusion.99), channel_id=1, source_target_pairs={{0,2},{1,3},{2,0},{3,1},{4,6},{5,7},{6,4},{7,5},{8,10},{9,11},{10,... | collective-permute-start | bytes 313352 | tf_op jit(solution)/shard_map/ppermute | solution.py:192
  68.9 5.7 %collective-permute-start.5 = (bf16[51,1024]{1,0:T(8,128)(2,1)S(1)}, bf16[51,1024]{1,0:T(8,128)(2,1)S(1)}, u32[]{:S(2)}, u32[]{:S(2)}) collective-permute-start(bf16[51,1024]{1,0:T(8,128)(2,1)S(1)} %fusion.99), channel_id=1, source_target_pairs={{0,1},{1,2},{2,3},{3,0},{4,5},{5,6},{6,7},{7,4},{8,9},{9,10},{10,1... | collective-permute-start | bytes 313352 | tf_op jit(solution)/shard_map/ppermute | solution.py:192
  (2 other events, 1.5 us)

commit v26 on v25

--- a/solution.py
+++ b/solution.py
@@ -106,7 +106,7 @@
             preferred_element_type=jnp.float32,
         )
     activated = jax.nn.gelu(row_norm(convolved.reshape(total_rows, DD)), approximate=False)
-    return (lowered.astype(jnp.float32) + activated).astype(jnp.bfloat16)
+    return (lowered.astype(jnp.float32) + activated).astype(jnp.bfloat16), seen
 
 
 def loss_kernel(hidden_ref, dec_out_ref, targets_ref, keep_ref, squares_ref, d_hidden_ref, *, scale):
@@ -177,12 +177,11 @@
     else:
         branch = attention_from(reuse_rows(visible_in, w_qkv, projected), w_out)
     visible_out = (visible_in.astype(jnp.float32) + branch).astype(jnp.bfloat16)
-    hidden = decoder_output(
+    hidden, seen = decoder_output(
         visible_out, positions, total_rows, mask_embed, dec_in, conv_w, dec_out
     )
     slot_ids = jnp.arange(total_rows, dtype=jnp.int32)
-    seen = jnp.max((slot_ids[:, None] == positions[None, :]).astype(jnp.float32), axis=1)
-    return squares_of(hidden, dec_out, targets, (1.0 - seen)[:, None], scale)
+    return squares_of(hidden, dec_out, targets, 1.0 - seen.astype(jnp.float32), scale)
 
 
 def ring_gather(values, group_size):

time: 77.7 us -> 77.6 us (level)
  transfers between devices with their start and end apart: 6 -> 6, of which waited for: 3 -> 3; matrix products, arithmetic and copies ran while one was open for 7% -> 6% of each run, Pallas kernels for 0% -> 0%
where the time goes in v26:
time: 77.6 us; the launch traced here: 77.1 us
  matrix products  35.6 us (46%)
  other arithmetic  12.2 us (16%)
  local copies, waits for them, and re-layouts  9.62 us (12%)
  starting transfers between devices  8.16 us (11%)
  waiting for transfers between devices  4.85 us (6%)
  Pallas kernels  3.54 us (5%)
  between operations  3.18 us (4%)
    ppermute x6, starting transfers between devices, ring_gather(): parts.append(lax.ppermute(values, 'mask', pairs))  8.16 us
    dot_general x6, matrix products, decoder_output(): jnp.einsum('pgi,gio->pgo', padded[offset:offset + total_rows], conv_w[off...  7.62 us
    dot_general x1, matrix products, copy_terms(): branch = attention_from(reuse_rows(visible_in, w_qkv, projected), w_out)  4.89 us
    ppermute x6, waiting for transfers between devices, ring_gather(): parts.append(lax.ppermute(values, 'mask', pairs))  4.85 us
    dot_general x2, matrix products, decoder_output(): jnp.dot(visible_out, dec_in, preferred_element_type=jnp.float32)  4.38 us
    pallas_call x1, Pallas kernels, masked_squares(): pl.pallas_call(functools.partial(loss_kernel, scale=scale), out_shape=(ja...  3.54 us
    dot_general x1, matrix products, project_rows(): jnp.dot(normed, w_qkv, preferred_element_type=jnp.float32)  3.1 us
    convert_element_type x1, other arithmetic, decoder_output(): (lowered.astype(jnp.float32) + activated).astype(jnp.bfloat16)  2.97 us
  transfers between devices with their start and end apart: 6, of which 3 were waited for; matrix products, arithmetic and copies ran while one was open for 6% of the time, Pallas kernels for 0%

profile of v26, /device:TPU:0, one launch (start us, length us, event | category | flops | bytes accessed | tf_op | source)
XLA Modules:
  0.0 77.1 jit_solution(18241503164332074177)
XLA Ops:
  0.6 3.0 %collective-permute-start = (bf16[64,768]{1,0:T(8,128)(2,1)}, bf16[64,768]{1,0:T(8,128)(2,1)S(1)}, u32[]{:S(2)}, u32[]{:S(2)}) collective-permute-start(bf16[64,768]{1,0:T(8,128)(2,1)} %param.9), channel_id=1, source_target_pairs={{0,1},{1,2},{2,3},{3,0},{4,5},{5,6},{6,7},{7,4},{8,9},{9,10},{10,1... | collective-permute-start | bytes 294920 | tf_op jit(solution)/shard_map/ppermute | solution.py:191
  3.7 1.5 %collective-permute-start.1 = (bf16[64,768]{1,0:T(8,128)(2,1)}, bf16[64,768]{1,0:T(8,128)(2,1)S(1)}, u32[]{:S(2)}, u32[]{:S(2)}) collective-permute-start(bf16[64,768]{1,0:T(8,128)(2,1)} %param.9), channel_id=1, source_target_pairs={{0,2},{1,3},{2,0},{3,1},{4,6},{5,7},{6,4},{7,5},{8,10},{9,11},{10,... | collective-permute-start | bytes 294920 | tf_op jit(solution)/shard_map/ppermute | solution.py:191
  5.2 1.4 %collective-permute-start.2 = (bf16[64,768]{1,0:T(8,128)(2,1)}, bf16[64,768]{1,0:T(8,128)(2,1)S(1)}, u32[]{:S(2)}, u32[]{:S(2)}) collective-permute-start(bf16[64,768]{1,0:T(8,128)(2,1)} %param.9), channel_id=1, source_target_pairs={{0,3},{1,0},{2,1},{3,2},{4,7},{5,4},{6,5},{7,6},{8,11},{9,8},{10,9... | collective-permute-start | bytes 294920 | tf_op jit(solution)/shard_map/ppermute | solution.py:191
  9.7 1.9 %convolution_reduce_fusion = bf16[768]{0:T(1024)(128)(2,1)S(1)} fusion(bf16[1024,1]{0,1:T(2,128)(2,1)S(1)} %reshape.227, bf16[1024,768]{1,0:T(8,128)(2,1)} %param.15), kind=kOutput, calls=%fused_computation.53 | convolution fusion | flops 1572864 | bytes 1576448 | tf_op jit(solution)/shard_map/jvp()/dot_general | solution.py:93
  11.6 1.3 %select_select_fusion.3 = (bf16[64,768]{1,0:T(8,128)(2,1)S(1)}, bf16[64,768]{1,0:T(8,128)(2,1)S(1)}, bf16[64,768]{1,0:T(8,128)(2,1)S(1)}, bf16[64,768]{1,0:T(8,128)(2,1)S(1)}) fusion(bf16[64,768]{1,0:T(8,128)(2,1)S(1)} %collective-permute-done, bf16[64,768]{1,0:T(8,128)(2,1)S(1)} %collective-permute-done.1, bf16[64,768]{1,0:T(8,128)(2,1)S(1)} %collective-permute-done.2, ...), kind=kLoop, calls=%fused_computation.172 | loop fusion | flops 589824 | bytes 786444 | tf_op jit(solution)/shard_map/jit(_where)/select_n | solution.py:202
  13.0 2.2 %convert_reduce_fusion = (f32[256]{0:T(256)S(1)}, bf16[256,1024]{1,0:T(8,128)(2,1)S(1)}) fusion(bf16[768,1024]{1,0:T(8,128)(2,1)} %param.11, bf16[64,768]{1,0:T(8,128)(2,1)S(1)} %get-tuple-element.18, bf16[64,768]{1,0:T(8,128)(2,1)S(1)} %get-tuple-element.19, bf16[64,768]{1,0:T(8,128)(2,1)S(1)} %get-tuple-element.20, bf16[64,768]{1,0:T(8,128)(2,1)S(1)} %get-tuple-element.17), kind=kOutput, calls=%fused_computation.11 | convolution fusion | flops 405012224 | bytes 2491392 | tf_op jit(solution)/shard_map/dot_general | solution.py:239
  15.5 3.1 %convolution_convert_fusion = bf16[256,3072]{1,0:T(8,128)(2,1)} fusion(bf16[1024,3072]{1,0:T(8,128)(2,1)S(1)} %copy-done.4, bf16[256,1024]{1,0:T(8,128)(2,1)S(1)} %get-tuple-element.24, f32[256]{0:T(256)S(1)} %add_rsqrt_fusion.3, f32[256]{0:T(256)S(1)} %broadcast_multiply_fusion.2), kind=kOutput, calls=%fused_computation.2 | convolution fusion | flops 1612447744 | bytes 8390656 | tf_op jit(solution)/shard_map/dot_general | solution.py:50
  18.6 2.6 %copy.63 = bf16[256,3072]{0,1:T(8,128)(2,1)} copy(bf16[256,3072]{1,0:T(8,128)(2,1)} %convolution_convert_fusion) | data formatting | bytes 3145728 | tf_op jit(solution)/shard_map/convert_element_type | solution.py:50
  21.2 1.9 %convolution_convert_fusion.1 = bf16[51,3072]{1,0:T(8,128)(2,1)S(1)} fusion(bf16[256,3072]{1,0:T(8,128)(2,1)} %convolution_convert_fusion, s32[51]{0:T(128)S(1)} %slice_bitcast_fusion.6), kind=kOutput, calls=%fused_computation.4 | convolution fusion | flops 80385792 | bytes 1886412 | tf_op jit(solution)/shard_map/dot_general | solution.py:250
  23.1 0.9 %fusion.128 = (f32[51]{0:T(128)}, f32[51,1024]{1,0:T(8,128)S(1)}) fusion(bf16[256,1024]{1,0:T(8,128)(2,1)S(1)} %get-tuple-element.24, s32[51]{0:T(128)S(1)} %slice_bitcast_fusion.6), kind=kOutput, calls=%fused_computation.222 | convolution fusion | flops 26908364 | bytes 733592 | tf_op jit(solution)/shard_map/dot_general | solution.py:244
  24.3 1.0 %fusion = (f32[16,256]{1,0:T(8,128)S(1)}, f32[16,256,256]{1,2,0:T(8,128)S(1)}) fusion(f32[256,16]{0,1:T(8,128)S(1)} %get-tuple-element.43, bf16[256,3,16,64]{0,3,2,1:T(8,128)(2,1)S(1)} %bitcast.162, f32[256,16]{0,1:T(8,128)S(1)} %get-tuple-element.44), kind=kOutput, calls=%fused_computation.3 | convolution fusion | flops 137883648 | bytes 5292032 | tf_op jit(solution)/shard_map/qhd,khd->hqk/dot_general | solution.py:33
  25.3 0.8 %fusion.2 = bf16[16,64,256]{2,1,0:T(8,128)(2,1)S(1)} fusion(f32[16,256,256]{1,2,0:T(8,128)S(1)} %get-tuple-element.30, f32[16,256]{1,0:T(8,128)S(1)} %get-tuple-element.29, bf16[256,3,16,64]{0,3,2,1:T(8,128)(2,1)S(1)} %bitcast.163), kind=kOutput, calls=%fused_computation.12 | convolution fusion | flops 137625600 | bytes 5259264 | tf_op jit(solution)/shard_map/hqk,khd->qhd/dot_general | solution.py:38
  27.2 1.0 %multiply_convert_fusion.targets_ref = bf16[256,1024]{1,0:T(8,128)(2,1)} fusion(f32[256,1024]{1,0:T(8,128)S(1)} %get-tuple-element.32, f32[256]{0:T(256)S(1)} %add_rsqrt_fusion.2, f32[256]{0:T(256)S(1)} %broadcast_multiply_fusion.1), kind=kLoop, calls=%fused_computation.60 | loop fusion | flops 786432 | bytes 1574912 | tf_op jit(solution)/shard_map/convert_element_type | solution.py:256
  30.9 2.2 %convolution_convert_fusion.17 = bf16[51,768]{1,0:T(8,128)(2,1)S(1)} fusion(bf16[1024,768]{1,0:T(8,128)(2,1)} %param.15, f32[51,1024]{1,0:T(8,128)S(1)} %get-tuple-element.34, bf16[51,1024]{1,0:T(8,128)(2,1)S(1)} %reshape.213, bf16[1024,1024]{1,0:T(8,128)(2,1)S(1)} %copy-done), kind=kOutput, calls=%fused_computation.51 | convolution fusion | flops 187314432 | bytes 4061696 | tf_op jit(solution)/shard_map/jvp()/dot_general | solution.py:90
  33.7 1.3 %fusion.67 = f32[16,256,48]{1,2,0:T(8,128)S(1)} fusion(bf16[256,16,48]{0,2,1:T(8,128)(2,1)S(1)} %bitcast.168, bf16[3,16,48,48]{3,2,1,0:T(8,128)(2,1)} %param.16), kind=kOutput, calls=%fused_computation.130 | convolution fusion | flops 18874368 | bytes 1376256 | tf_op jit(solution)/shard_map/jvp(pgi,gio->pgo)/dot_general | solution.py:102
  35.1 1.2 %convolution_add_fusion.1 = f32[16,256,48]{1,2,0:T(8,128)S(1)} fusion(f32[16,256,48]{1,2,0:T(8,128)S(1)} %fusion.67, bf16[256,16,48]{0,2,1:T(8,128)(2,1)S(1)} %bitcast.169, bf16[3,16,48,48]{3,2,1,0:T(8,128)(2,1)} %param.16), kind=kOutput, calls=%fused_computation.14 | convolution fusion | flops 19070976 | bytes 2162688 | tf_op jit(solution)/shard_map/jvp(pgi,gio->pgo)/dot_general | solution.py:102
  36.3 1.4 %fusion.126 = (f32[256]{0:T(256)S(1)}, f32[16,256,48]{1,2,0:T(8,128)S(1)}) fusion(f32[16,256,48]{1,2,0:T(8,128)S(1)} %convolution_add_fusion.1, bf16[256,16,48]{0,2,1:T(8,128)(2,1)S(1)} %bitcast.170, bf16[3,16,48,48]{3,2,1,0:T(8,128)(2,1)} %param.16), kind=kOutput, calls=%fused_computation.220 | convolution fusion | flops 19267328 | bytes 2163712 | tf_op jit(solution)/shard_map/jvp(pgi,gio->pgo)/dot_general | solution.py:102
  38.5 1.4 %copy.62 = f32[256,768]{1,0:T(8,128)S(1)} copy(f32[256,768]{0,1:T(8,128)} %bitcast.164) | data formatting | bytes 1572864 | tf_op jit(solution)/shard_map/jvp()/reshape | solution.py:108
  39.9 3.0 %add_convert_fusion = (bf16[256,768]{1,0:T(8,128)(2,1)}, f32[256,768]{1,0:T(8,128)}) fusion(bf16[256,768]{1,0:T(8,128)(2,1)S(1)} %fusion.3, f32[256,768]{1,0:T(8,128)S(1)} %copy.62, f32[256]{0:T(256)S(1)} %fusion.111, f32[256]{0:T(256)S(1)} %broadcast_multiply_fusion), kind=kLoop, calls=%fused_computation.85 | loop fusion | flops 13565952 | bytes 2361344 | tf_op jit(solution)/shard_map/jvp()/convert_element_type | solution.py:109
  42.9 3.5 %jvp__.1 = (f32[1,1]{1,0:T(1,128)}, bf16[256,768]{1,0:T(8,128)(2,1)}) custom-call(bf16[256,768]{1,0:T(8,128)(2,1)} %get-tuple-element.12.hidden_ref, bf16[768,1024]{1,0:T(8,128)(2,1)} %dec_out_ref.1, bf16[256,1024]{1,0:T(8,128)(2,1)} %multiply_convert_fusion.targets_ref, f32[256,1]{1,0:T(8,128)} %copy.65.keep_ref), custom_call_target="tpu_custom_call" | custom-call | tf_op jit(solution)/shard_map/jvp()/pallas_call | solution.py:128
  46.5 2.0 %multiply_reduce_fusion.1 = f32[256]{0:T(256)S(1)} fusion(f32[256,768]{1,0:T(8,128)S(1)} %copy.62, f32[256]{0:T(256)S(1)} %broadcast_multiply_fusion, f32[256,768]{1,0:T(8,128)} %get-tuple-element.13, bf16[256,768]{1,0:T(8,128)(2,1)} %get-tuple-element.4, f32[256]{0:T(256)S(1)} %fusion.111), kind=kLoop, calls=%fused_computation.84 | loop fusion | flops 3538688 | bytes 1969152 | tf_op jit(solution)/shard_map/transpose(jvp())/reduce_sum | solution.py:23
  49.6 1.4 %fusion.7 = bf16[256,16,48]{0,2,1:T(8,128)(2,1)S(1)} fusion(bf16[16,48,256]{2,1,0:T(8,128)(2,1)S(1)} %bitcast.165, bf16[3,16,48,48]{3,2,1,0:T(8,128)(2,1)} %param.16), kind=kOutput, calls=%fused_computation.25 | convolution fusion | flops 18874368 | bytes 983040 | tf_op jit(solution)/shard_map/transpose(jvp(pgi,gio->pgo))/dot_general | solution.py:102
  50.9 1.2 %fusion.8 = bf16[256,16,48]{0,2,1:T(8,128)(2,1)S(1)} fusion(bf16[16,48,256]{2,1,0:T(8,128)(2,1)S(1)} %bitcast.166, bf16[3,16,48,48]{3,2,1,0:T(8,128)(2,1)} %param.16), kind=kOutput, calls=%fused_computation.26 | convolution fusion | flops 18874368 | bytes 983040 | tf_op jit(solution)/shard_map/transpose(jvp(pgi,gio->pgo))/dot_general | solution.py:102
  52.1 1.2 %fusion.9 = bf16[256,16,48]{0,2,1:T(8,128)(2,1)S(1)} fusion(bf16[16,48,256]{2,1,0:T(8,128)(2,1)S(1)} %bitcast.167, bf16[3,16,48,48]{3,2,1,0:T(8,128)(2,1)} %param.16), kind=kOutput, calls=%fused_computation.27 | convolution fusion | flops 18874368 | bytes 983040 | tf_op jit(solution)/shard_map/transpose(jvp(pgi,gio->pgo))/dot_general | solution.py:102
  53.8 2.2 %convolution_convert_fusion.12 = bf16[51,1024]{1,0:T(8,128)(2,1)S(1)} fusion(bf16[1024,768]{1,0:T(8,128)(2,1)} %param.15, bf16[256,768]{1,0:T(8,128)(2,1)S(1)} %copy-done.5, bf16[256,768]{1,0:T(8,128)(2,1)S(1)} %copy.70, pred[256]{0:T(512)(128)(4,1)} %copy-done.26, s32[51]{0:T(128)} %copy-done.24), kind=kOutput, calls=%fused_computation.45 | convolution fusion | flops 100964352 | bytes 2464204 | tf_op jit(solution)/shard_map/transpose(jvp())/dot_general | solution.py:90
  57.0 1.4 %fusion.16 = bf16[51,1,16,64]{3,0,2,1:T(8,128)(2,1)S(1)} fusion(bf16[51,16,64]{2,1,0:T(8,128)(2,1)S(1)} %reshape.220, f32[16,51,51]{1,2,0:T(8,128)} %copy-done.12, f32[16,51]{1,0:T(8,128)S(1)} %copy-done.23), kind=kOutput, calls=%fused_computation.41 | convolution fusion | flops 5462304 | bytes 378624 | tf_op jit(solution)/shard_map/transpose(jvp(hqk,khd->qhd))/dot_general | solution.py:38
  61.2 4.9 %convolution_convert_fusion.11 = bf16[51,1024]{1,0:T(8,128)(2,1)S(1)} fusion(bf16[51,3072]{1,0:T(8,128)(2,1)S(1)} %reshape.221, bf16[1024,3072]{1,0:T(8,128)(2,1)} %param.12), kind=kOutput, calls=%fused_computation.44 | convolution fusion | flops 320916480 | bytes 6709248 | tf_op jit(solution)/shard_map/transpose(jvp())/dot_general | solution.py:178
  67.3 1.5 %collective-permute-start.4 = (bf16[51,1024]{1,0:T(8,128)(2,1)S(1)}, bf16[51,1024]{1,0:T(8,128)(2,1)S(1)}, u32[]{:S(2)}, u32[]{:S(2)}) collective-permute-start(bf16[51,1024]{1,0:T(8,128)(2,1)S(1)} %fusion.99), channel_id=1, source_target_pairs={{0,2},{1,3},{2,0},{3,1},{4,6},{5,7},{6,4},{7,5},{8,10},{9,11},{10,... | collective-permute-start | bytes 313352 | tf_op jit(solution)/shard_map/ppermute | solution.py:191
  69.7 2.6 %collective-permute-done.3 = bf16[51,1024]{1,0:T(8,128)(2,1)S(1)} collective-permute-done((bf16[51,1024]{1,0:T(8,128)(2,1)S(1)}, bf16[51,1024]{1,0:T(8,128)(2,1)S(1)}, u32[]{:S(2)}, u32[]{:S(2)}) %collective-permute-start.3) | collective-permute-done | bytes 104480 | tf_op jit(solution)/shard_map/ppermute | solution.py:191
  72.2 1.0 %collective-permute-done.4 = bf16[51,1024]{1,0:T(8,128)(2,1)S(1)} collective-permute-done((bf16[51,1024]{1,0:T(8,128)(2,1)S(1)}, bf16[51,1024]{1,0:T(8,128)(2,1)S(1)}, u32[]{:S(2)}, u32[]{:S(2)}) %collective-permute-start.4) | collective-permute-done | bytes 104480 | tf_op jit(solution)/shard_map/ppermute | solution.py:191
  73.3 1.2 %collective-permute-done.5 = bf16[51,1024]{1,0:T(8,128)(2,1)S(1)} collective-permute-done((bf16[51,1024]{1,0:T(8,128)(2,1)S(1)}, bf16[51,1024]{1,0:T(8,128)(2,1)S(1)}, u32[]{:S(2)}, u32[]{:S(2)}) %collective-permute-start.5) | collective-permute-done | bytes 104480 | tf_op jit(solution)/shard_map/ppermute | solution.py:191
  74.5 1.4 %fusion.19 = f32[192,1024]{1,0:T(8,128)} fusion(bf16[51,1024]{1,0:T(8,128)(2,1)S(1)} %collective-permute-done.5, bf16[51,1024]{1,0:T(8,128)(2,1)S(1)} %collective-permute-done.4, bf16[51,1024]{1,0:T(8,128)(2,1)S(1)} %collective-permute-done.3, bf16[51,1024]{1,0:T(8,128)(2,1)S(1)} %fusion.99, bf16[256,768]{1,0:T(8,128)(2,1)S(1)} %pad_maximum_fusion, ...), kind=kOutput, calls=%fused_computation.52 | convolution fusion | flops 102032640 | bytes 1377284 | tf_op jit(solution)/shard_map/vc,vd->cd/dot_general | solution.py:283
  (121 shorter events, 15.3 us)
Async XLA Ops:
  0.6 25.5 %copy-start = (bf16[1024,1024]{1,0:T(8,128)(2,1)S(1)}, bf16[1024,1024]{1,0:T(8,128)(2,1)}, u32[]{:S(2)}) copy-start(bf16[1024,1024]{1,0:T(8,128)(2,1)} %param.13) | copy-start | bytes 6291460
  0.6 10.9 %collective-permute-start = (bf16[64,768]{1,0:T(8,128)(2,1)}, bf16[64,768]{1,0:T(8,128)(2,1)S(1)}, u32[]{:S(2)}, u32[]{:S(2)}) collective-permute-start(bf16[64,768]{1,0:T(8,128)(2,1)} %param.9), channel_id=1, source_target_pairs={{0,1},{1,2},{2,3},{3,0},{4,5},{5,6},{6,7},{7,4},{8,9},{9,10},{10,1... | collective-permute-start | bytes 294920 | tf_op jit(solution)/shard_map/ppermute | solution.py:191
  3.7 7.9 %collective-permute-start.1 = (bf16[64,768]{1,0:T(8,128)(2,1)}, bf16[64,768]{1,0:T(8,128)(2,1)S(1)}, u32[]{:S(2)}, u32[]{:S(2)}) collective-permute-start(bf16[64,768]{1,0:T(8,128)(2,1)} %param.9), channel_id=1, source_target_pairs={{0,2},{1,3},{2,0},{3,1},{4,6},{5,7},{6,4},{7,5},{8,10},{9,11},{10,... | collective-permute-start | bytes 294920 | tf_op jit(solution)/shard_map/ppermute | solution.py:191
  5.2 6.4 %collective-permute-start.2 = (bf16[64,768]{1,0:T(8,128)(2,1)}, bf16[64,768]{1,0:T(8,128)(2,1)S(1)}, u32[]{:S(2)}, u32[]{:S(2)}) collective-permute-start(bf16[64,768]{1,0:T(8,128)(2,1)} %param.9), channel_id=1, source_target_pairs={{0,3},{1,0},{2,1},{3,2},{4,7},{5,4},{6,5},{7,6},{8,11},{9,8},{10,9... | collective-permute-start | bytes 294920 | tf_op jit(solution)/shard_map/ppermute | solution.py:191
  7.4 25.8 %copy-start.24 = (s32[51]{0:T(128)}, s32[51]{0:T(128)S(1)}, u32[]{:S(2)}) copy-start(s32[51]{0:T(128)S(1)} %slice_bitcast_fusion.6) | copy-start | bytes 616
  7.5 25.6 %copy-start.26 = (pred[256]{0:T(512)(128)(4,1)}, pred[256]{0:T(512)(128)(4,1)S(1)}, u32[]{:S(2)}) copy-start(pred[256]{0:T(512)(128)(4,1)S(1)} %broadcast_compare_fusion) | copy-start | bytes 772
  9.7 5.8 %copy-start.4 = (bf16[1024,3072]{1,0:T(8,128)(2,1)S(1)}, bf16[1024,3072]{1,0:T(8,128)(2,1)}, u32[]{:S(2)}) copy-start(bf16[1024,3072]{1,0:T(8,128)(2,1)} %param.12) | copy-start | bytes 18874372
  12.9 2.5 %copy-start.14 = (bf16[64,768]{1,0:T(8,128)(2,1)}, bf16[64,768]{1,0:T(8,128)(2,1)S(1)}, u32[]{:S(2)}) copy-start(bf16[64,768]{1,0:T(8,128)(2,1)S(1)} %get-tuple-element.17) | copy-start | bytes 294916
  12.9 2.5 %copy-start.16 = (bf16[64,768]{1,0:T(8,128)(2,1)}, bf16[64,768]{1,0:T(8,128)(2,1)S(1)}, u32[]{:S(2)}) copy-start(bf16[64,768]{1,0:T(8,128)(2,1)S(1)} %get-tuple-element.18) | copy-start | bytes 294916
  12.9 2.5 %copy-start.18 = (bf16[64,768]{1,0:T(8,128)(2,1)}, bf16[64,768]{1,0:T(8,128)(2,1)S(1)}, u32[]{:S(2)}) copy-start(bf16[64,768]{1,0:T(8,128)(2,1)S(1)} %get-tuple-element.19) | copy-start | bytes 294916
  12.9 2.5 %copy-start.20 = (bf16[64,768]{1,0:T(8,128)(2,1)}, bf16[64,768]{1,0:T(8,128)(2,1)S(1)}, u32[]{:S(2)}) copy-start(bf16[64,768]{1,0:T(8,128)(2,1)S(1)} %get-tuple-element.20) | copy-start | bytes 294916
  21.2 2.8 %copy-start.1 = (bf16[256,3072]{0,1:T(8,128)(2,1)S(1)}, bf16[256,3072]{0,1:T(8,128)(2,1)}, u32[]{:S(2)}) copy-start(bf16[256,3072]{0,1:T(8,128)(2,1)} %copy.63) | copy-start | bytes 4718596
  28.7 1.2 %copy-start.8 = (bf16[51,1,16,64]{3,2,1,0:T(8,128)(2,1)}, bf16[51,1,16,64]{3,2,1,0:T(8,128)(2,1)S(1)}, u32[]{:S(2)}) copy-start(bf16[51,1,16,64]{3,2,1,0:T(8,128)(2,1)S(1)} %get-tuple-element.16) | copy-start | bytes 313348
  28.7 1.2 %copy-start.10 = (bf16[51,1,16,64]{3,2,1,0:T(8,128)(2,1)}, bf16[51,1,16,64]{3,2,1,0:T(8,128)(2,1)S(1)}, u32[]{:S(2)}) copy-start(bf16[51,1,16,64]{3,2,1,0:T(8,128)(2,1)S(1)} %get-tuple-element.15) | copy-start | bytes 313348
  30.0 1.0 %copy-start.22 = (f32[16,51]{1,0:T(8,128)}, f32[16,51]{1,0:T(8,128)S(1)}, u32[]{:S(2)}) copy-start(f32[16,51]{1,0:T(8,128)S(1)} %get-tuple-element.25) | copy-start | bytes 9796
  37.7 0.9 %copy-start.2 = (f32[16,256,48]{1,2,0:T(8,128)}, f32[16,256,48]{1,2,0:T(8,128)S(1)}, u32[]{:S(2)}) copy-start(f32[16,256,48]{1,2,0:T(8,128)S(1)} %get-tuple-element.28) | copy-start | bytes 2359300
  46.5 2.0 %copy-start.3 = (f32[256,768]{1,0:T(8,128)S(1)}, f32[256,768]{1,0:T(8,128)}, u32[]{:S(2)}) copy-start(f32[256,768]{1,0:T(8,128)} %get-tuple-element.13) | copy-start | bytes 2359300
  46.5 2.0 %copy-start.5 = (bf16[256,768]{1,0:T(8,128)(2,1)S(1)}, bf16[256,768]{1,0:T(8,128)(2,1)}, u32[]{:S(2)}) copy-start(bf16[256,768]{1,0:T(8,128)(2,1)} %get-tuple-element.4) | copy-start | bytes 1179652
  49.4 3.9 %copy-start.23 = (f32[16,51]{1,0:T(8,128)S(1)}, f32[16,51]{1,0:T(8,128)}, u32[]{:S(2)}) copy-start(f32[16,51]{1,0:T(8,128)} %copy-done.22) | copy-start | bytes 9796
  56.0 2.4 %copy-start.11 = (bf16[51,1,16,64]{3,2,1,0:T(8,128)(2,1)S(1)}, bf16[51,1,16,64]{3,2,1,0:T(8,128)(2,1)}, u32[]{:S(2)}) copy-start(bf16[51,1,16,64]{3,2,1,0:T(8,128)(2,1)} %copy-done.10) | copy-start | bytes 313348
  56.8 1.9 %copy-start.7 = (bf16[51,1,16,64]{3,2,1,0:T(8,128)(2,1)S(1)}, bf16[51,1,16,64]{3,2,1,0:T(8,128)(2,1)}, u32[]{:S(2)}) copy-start(bf16[51,1,16,64]{3,2,1,0:T(8,128)(2,1)} %copy-done.6) | copy-start | bytes 313348
  56.8 1.9 %copy-start.9 = (bf16[51,1,16,64]{3,2,1,0:T(8,128)(2,1)S(1)}, bf16[51,1,16,64]{3,2,1,0:T(8,128)(2,1)}, u32[]{:S(2)}) copy-start(bf16[51,1,16,64]{3,2,1,0:T(8,128)(2,1)} %copy-done.8) | copy-start | bytes 313348
  57.0 1.4 %copy-start.13 = (f32[16,51,51]{1,2,0:T(8,128)S(1)}, f32[16,51,51]{1,2,0:T(8,128)}, u32[]{:S(2)}) copy-start(f32[16,51,51]{1,2,0:T(8,128)} %copy-done.12) | copy-start | bytes 499396
  61.1 5.0 %copy-start.27 = (f32[51]{0:T(128)S(1)}, f32[51]{0:T(128)}, u32[]{:S(2)}) copy-start(f32[51]{0:T(128)} %get-tuple-element.33) | copy-start | bytes 616
  61.1 8.5 %copy-start.15 = (bf16[64,768]{1,0:T(8,128)(2,1)S(1)}, bf16[64,768]{1,0:T(8,128)(2,1)}, u32[]{:S(2)}) copy-start(bf16[64,768]{1,0:T(8,128)(2,1)} %copy-done.14) | copy-start | bytes 294916
  61.1 8.5 %copy-start.17 = (bf16[64,768]{1,0:T(8,128)(2,1)S(1)}, bf16[64,768]{1,0:T(8,128)(2,1)}, u32[]{:S(2)}) copy-start(bf16[64,768]{1,0:T(8,128)(2,1)} %copy-done.16) | copy-start | bytes 294916
  61.1 8.5 %copy-start.19 = (bf16[64,768]{1,0:T(8,128)(2,1)S(1)}, bf16[64,768]{1,0:T(8,128)(2,1)}, u32[]{:S(2)}) copy-start(bf16[64,768]{1,0:T(8,128)(2,1)} %copy-done.18) | copy-start | bytes 294916
  61.2 8.5 %copy-start.21 = (bf16[64,768]{1,0:T(8,128)(2,1)S(1)}, bf16[64,768]{1,0:T(8,128)(2,1)}, u32[]{:S(2)}) copy-start(bf16[64,768]{1,0:T(8,128)(2,1)} %copy-done.20) | copy-start | bytes 294916
  61.2 13.3 %copy-start.25 = (s32[204]{0:T(256)S(1)}, s32[204]{0:T(256)}, u32[]{:S(2)}) copy-start(s32[204]{0:T(256)} %eq.84) | copy-start | bytes 2452
  66.7 5.5 %collective-permute-start.3 = (bf16[51,1024]{1,0:T(8,128)(2,1)S(1)}, bf16[51,1024]{1,0:T(8,128)(2,1)S(1)}, u32[]{:S(2)}, u32[]{:S(2)}) collective-permute-start(bf16[51,1024]{1,0:T(8,128)(2,1)S(1)} %fusion.99), channel_id=1, source_target_pairs={{0,3},{1,0},{2,1},{3,2},{4,7},{5,4},{6,5},{7,6},{8,11},{9,8},{10,9... | collective-permute-start | bytes 313352 | tf_op jit(solution)/shard_map/ppermute | solution.py:191
  67.3 6.0 %collective-permute-start.4 = (bf16[51,1024]{1,0:T(8,128)(2,1)S(1)}, bf16[51,1024]{1,0:T(8,128)(2,1)S(1)}, u32[]{:S(2)}, u32[]{:S(2)}) collective-permute-start(bf16[51,1024]{1,0:T(8,128)(2,1)S(1)} %fusion.99), channel_id=1, source_target_pairs={{0,2},{1,3},{2,0},{3,1},{4,6},{5,7},{6,4},{7,5},{8,10},{9,11},{10,... | collective-permute-start | bytes 313352 | tf_op jit(solution)/shard_map/ppermute | solution.py:191
  68.8 5.7 %collective-permute-start.5 = (bf16[51,1024]{1,0:T(8,128)(2,1)S(1)}, bf16[51,1024]{1,0:T(8,128)(2,1)S(1)}, u32[]{:S(2)}, u32[]{:S(2)}) collective-permute-start(bf16[51,1024]{1,0:T(8,128)(2,1)S(1)} %fusion.99), channel_id=1, source_target_pairs={{0,1},{1,2},{2,3},{3,0},{4,5},{5,6},{6,7},{7,4},{8,9},{9,10},{10,1... | collective-permute-start | bytes 313352 | tf_op jit(solution)/shard_map/ppermute | solution.py:191
  (2 other events, 1.5 us)

commit v27 on v26

--- a/solution.py
+++ b/solution.py
@@ -277,12 +277,11 @@
     flat_index = slot_index.reshape(copies * visible_count)
     own_cols = lax.dynamic_slice_in_dim(clip_pixels, own_index * col_width, col_width, 1)
     all_picks = (flat_index[:, None] == clip_ids[None, :]).astype(jnp.bfloat16)
-    gathered = jnp.dot(all_picks, own_cols, preferred_element_type=jnp.float32).astype(
-        jnp.bfloat16
-    )
-    embed_grad = jnp.einsum(
-        "vc,vd->cd",
-        gathered,
+    gathered_t = jnp.einsum(
+        "sc,vs->cv", own_cols, all_picks, preferred_element_type=jnp.float32
+    ).astype(jnp.bfloat16)
+    embed_grad = jnp.dot(
+        gathered_t,
         jnp.concatenate(ring_gather(grad_in, group_size), axis=0),
         preferred_element_type=jnp.float32,
     )

time: 77.6 us -> 77.6 us (level)
  no operation moved by 1% of the time
where the time goes in v27:
time: 77.6 us; the launch traced here: 77.1 us
  matrix products  35.6 us (46%)
  other arithmetic  12.2 us (16%)
  local copies, waits for them, and re-layouts  9.62 us (12%)
  starting transfers between devices  8.16 us (11%)
  waiting for transfers between devices  4.85 us (6%)
  Pallas kernels  3.54 us (5%)
  between operations  3.18 us (4%)
    ppermute x6, starting transfers between devices, ring_gather(): parts.append(lax.ppermute(values, 'mask', pairs))  8.16 us
    dot_general x6, matrix products, decoder_output(): jnp.einsum('pgi,gio->pgo', padded[offset:offset + total_rows], conv_w[off...  7.62 us
    dot_general x1, matrix products, copy_terms(): branch = attention_from(reuse_rows(visible_in, w_qkv, projected), w_out)  4.89 us
    ppermute x6, waiting for transfers between devices, ring_gather(): parts.append(lax.ppermute(values, 'mask', pairs))  4.85 us
    dot_general x2, matrix products, decoder_output(): jnp.dot(visible_out, dec_in, preferred_element_type=jnp.float32)  4.38 us
    pallas_call x1, Pallas kernels, masked_squares(): pl.pallas_call(functools.partial(loss_kernel, scale=scale), out_shape=(ja...  3.54 us
    dot_general x1, matrix products, project_rows(): jnp.dot(normed, w_qkv, preferred_element_type=jnp.float32)  3.1 us
    convert_element_type x1, other arithmetic, decoder_output(): (lowered.astype(jnp.float32) + activated).astype(jnp.bfloat16)  2.97 us
  transfers between devices with their start and end apart: 6, of which 3 were waited for; matrix products, arithmetic and copies ran while one was open for 6% of the time, Pallas kernels for 0%

profile of v27, /device:TPU:0, one launch (start us, length us, event | category | flops | bytes accessed | tf_op | source)
XLA Modules:
  0.0 77.1 jit_solution(6963004980644233679)
XLA Ops:
  0.6 3.0 %collective-permute-start = (bf16[64,768]{1,0:T(8,128)(2,1)}, bf16[64,768]{1,0:T(8,128)(2,1)S(1)}, u32[]{:S(2)}, u32[]{:S(2)}) collective-permute-start(bf16[64,768]{1,0:T(8,128)(2,1)} %param.9), channel_id=1, source_target_pairs={{0,1},{1,2},{2,3},{3,0},{4,5},{5,6},{6,7},{7,4},{8,9},{9,10},{10,1... | collective-permute-start | bytes 294920 | tf_op jit(solution)/shard_map/ppermute | solution.py:191
  3.7 1.5 %collective-permute-start.1 = (bf16[64,768]{1,0:T(8,128)(2,1)}, bf16[64,768]{1,0:T(8,128)(2,1)S(1)}, u32[]{:S(2)}, u32[]{:S(2)}) collective-permute-start(bf16[64,768]{1,0:T(8,128)(2,1)} %param.9), channel_id=1, source_target_pairs={{0,2},{1,3},{2,0},{3,1},{4,6},{5,7},{6,4},{7,5},{8,10},{9,11},{10,... | collective-permute-start | bytes 294920 | tf_op jit(solution)/shard_map/ppermute | solution.py:191
  5.2 1.4 %collective-permute-start.2 = (bf16[64,768]{1,0:T(8,128)(2,1)}, bf16[64,768]{1,0:T(8,128)(2,1)S(1)}, u32[]{:S(2)}, u32[]{:S(2)}) collective-permute-start(bf16[64,768]{1,0:T(8,128)(2,1)} %param.9), channel_id=1, source_target_pairs={{0,3},{1,0},{2,1},{3,2},{4,7},{5,4},{6,5},{7,6},{8,11},{9,8},{10,9... | collective-permute-start | bytes 294920 | tf_op jit(solution)/shard_map/ppermute | solution.py:191
  9.7 1.9 %convolution_reduce_fusion = bf16[768]{0:T(1024)(128)(2,1)S(1)} fusion(bf16[1024,1]{0,1:T(2,128)(2,1)S(1)} %reshape.227, bf16[1024,768]{1,0:T(8,128)(2,1)} %param.15), kind=kOutput, calls=%fused_computation.53 | convolution fusion | flops 1572864 | bytes 1576448 | tf_op jit(solution)/shard_map/jvp()/dot_general | solution.py:93
  11.6 1.3 %select_select_fusion.3 = (bf16[64,768]{1,0:T(8,128)(2,1)S(1)}, bf16[64,768]{1,0:T(8,128)(2,1)S(1)}, bf16[64,768]{1,0:T(8,128)(2,1)S(1)}, bf16[64,768]{1,0:T(8,128)(2,1)S(1)}) fusion(bf16[64,768]{1,0:T(8,128)(2,1)S(1)} %collective-permute-done, bf16[64,768]{1,0:T(8,128)(2,1)S(1)} %collective-permute-done.1, bf16[64,768]{1,0:T(8,128)(2,1)S(1)} %collective-permute-done.2, ...), kind=kLoop, calls=%fused_computation.172 | loop fusion | flops 589824 | bytes 786444 | tf_op jit(solution)/shard_map/jit(_where)/select_n | solution.py:202
  13.0 2.2 %convert_reduce_fusion = (f32[256]{0:T(256)S(1)}, bf16[256,1024]{1,0:T(8,128)(2,1)S(1)}) fusion(bf16[768,1024]{1,0:T(8,128)(2,1)} %param.11, bf16[64,768]{1,0:T(8,128)(2,1)S(1)} %get-tuple-element.18, bf16[64,768]{1,0:T(8,128)(2,1)S(1)} %get-tuple-element.19, bf16[64,768]{1,0:T(8,128)(2,1)S(1)} %get-tuple-element.20, bf16[64,768]{1,0:T(8,128)(2,1)S(1)} %get-tuple-element.17), kind=kOutput, calls=%fused_computation.11 | convolution fusion | flops 405012224 | bytes 2491392 | tf_op jit(solution)/shard_map/dot_general | solution.py:239
  15.5 3.1 %convolution_convert_fusion = bf16[256,3072]{1,0:T(8,128)(2,1)} fusion(bf16[1024,3072]{1,0:T(8,128)(2,1)S(1)} %copy-done.4, bf16[256,1024]{1,0:T(8,128)(2,1)S(1)} %get-tuple-element.24, f32[256]{0:T(256)S(1)} %add_rsqrt_fusion.3, f32[256]{0:T(256)S(1)} %broadcast_multiply_fusion.2), kind=kOutput, calls=%fused_computation.2 | convolution fusion | flops 1612447744 | bytes 8390656 | tf_op jit(solution)/shard_map/dot_general | solution.py:50
  18.6 2.6 %copy.63 = bf16[256,3072]{0,1:T(8,128)(2,1)} copy(bf16[256,3072]{1,0:T(8,128)(2,1)} %convolution_convert_fusion) | data formatting | bytes 3145728 | tf_op jit(solution)/shard_map/convert_element_type | solution.py:50
  21.2 1.9 %convolution_convert_fusion.1 = bf16[51,3072]{1,0:T(8,128)(2,1)S(1)} fusion(bf16[256,3072]{1,0:T(8,128)(2,1)} %convolution_convert_fusion, s32[51]{0:T(128)S(1)} %slice_bitcast_fusion.6), kind=kOutput, calls=%fused_computation.4 | convolution fusion | flops 80385792 | bytes 1886412 | tf_op jit(solution)/shard_map/dot_general | solution.py:250
  23.1 0.9 %fusion.128 = (f32[51]{0:T(128)}, f32[51,1024]{1,0:T(8,128)S(1)}) fusion(bf16[256,1024]{1,0:T(8,128)(2,1)S(1)} %get-tuple-element.24, s32[51]{0:T(128)S(1)} %slice_bitcast_fusion.6), kind=kOutput, calls=%fused_computation.222 | convolution fusion | flops 26908364 | bytes 733592 | tf_op jit(solution)/shard_map/dot_general | solution.py:244
  24.3 1.0 %fusion = (f32[16,256]{1,0:T(8,128)S(1)}, f32[16,256,256]{1,2,0:T(8,128)S(1)}) fusion(f32[256,16]{0,1:T(8,128)S(1)} %get-tuple-element.43, bf16[256,3,16,64]{0,3,2,1:T(8,128)(2,1)S(1)} %bitcast.162, f32[256,16]{0,1:T(8,128)S(1)} %get-tuple-element.44), kind=kOutput, calls=%fused_computation.3 | convolution fusion | flops 137883648 | bytes 5292032 | tf_op jit(solution)/shard_map/qhd,khd->hqk/dot_general | solution.py:33
  25.3 0.8 %fusion.2 = bf16[16,64,256]{2,1,0:T(8,128)(2,1)S(1)} fusion(f32[16,256,256]{1,2,0:T(8,128)S(1)} %get-tuple-element.30, f32[16,256]{1,0:T(8,128)S(1)} %get-tuple-element.29, bf16[256,3,16,64]{0,3,2,1:T(8,128)(2,1)S(1)} %bitcast.163), kind=kOutput, calls=%fused_computation.12 | convolution fusion | flops 137625600 | bytes 5259264 | tf_op jit(solution)/shard_map/hqk,khd->qhd/dot_general | solution.py:38
  27.2 1.0 %multiply_convert_fusion.targets_ref = bf16[256,1024]{1,0:T(8,128)(2,1)} fusion(f32[256,1024]{1,0:T(8,128)S(1)} %get-tuple-element.32, f32[256]{0:T(256)S(1)} %add_rsqrt_fusion.2, f32[256]{0:T(256)S(1)} %broadcast_multiply_fusion.1), kind=kLoop, calls=%fused_computation.60 | loop fusion | flops 786432 | bytes 1574912 | tf_op jit(solution)/shard_map/convert_element_type | solution.py:256
  30.9 2.2 %convolution_convert_fusion.17 = bf16[51,768]{1,0:T(8,128)(2,1)S(1)} fusion(bf16[1024,768]{1,0:T(8,128)(2,1)} %param.15, f32[51,1024]{1,0:T(8,128)S(1)} %get-tuple-element.34, bf16[51,1024]{1,0:T(8,128)(2,1)S(1)} %reshape.213, bf16[1024,1024]{1,0:T(8,128)(2,1)S(1)} %copy-done), kind=kOutput, calls=%fused_computation.51 | convolution fusion | flops 187314432 | bytes 4061696 | tf_op jit(solution)/shard_map/jvp()/dot_general | solution.py:90
  33.7 1.3 %fusion.67 = f32[16,256,48]{1,2,0:T(8,128)S(1)} fusion(bf16[256,16,48]{0,2,1:T(8,128)(2,1)S(1)} %bitcast.168, bf16[3,16,48,48]{3,2,1,0:T(8,128)(2,1)} %param.16), kind=kOutput, calls=%fused_computation.130 | convolution fusion | flops 18874368 | bytes 1376256 | tf_op jit(solution)/shard_map/jvp(pgi,gio->pgo)/dot_general | solution.py:102
  35.1 1.2 %convolution_add_fusion.1 = f32[16,256,48]{1,2,0:T(8,128)S(1)} fusion(f32[16,256,48]{1,2,0:T(8,128)S(1)} %fusion.67, bf16[256,16,48]{0,2,1:T(8,128)(2,1)S(1)} %bitcast.169, bf16[3,16,48,48]{3,2,1,0:T(8,128)(2,1)} %param.16), kind=kOutput, calls=%fused_computation.14 | convolution fusion | flops 19070976 | bytes 2162688 | tf_op jit(solution)/shard_map/jvp(pgi,gio->pgo)/dot_general | solution.py:102
  36.3 1.4 %fusion.126 = (f32[256]{0:T(256)S(1)}, f32[16,256,48]{1,2,0:T(8,128)S(1)}) fusion(f32[16,256,48]{1,2,0:T(8,128)S(1)} %convolution_add_fusion.1, bf16[256,16,48]{0,2,1:T(8,128)(2,1)S(1)} %bitcast.170, bf16[3,16,48,48]{3,2,1,0:T(8,128)(2,1)} %param.16), kind=kOutput, calls=%fused_computation.220 | convolution fusion | flops 19267328 | bytes 2163712 | tf_op jit(solution)/shard_map/jvp(pgi,gio->pgo)/dot_general | solution.py:102
  38.5 1.4 %copy.62 = f32[256,768]{1,0:T(8,128)S(1)} copy(f32[256,768]{0,1:T(8,128)} %bitcast.164) | data formatting | bytes 1572864 | tf_op jit(solution)/shard_map/jvp()/reshape | solution.py:108
  39.9 3.0 %add_convert_fusion = (bf16[256,768]{1,0:T(8,128)(2,1)}, f32[256,768]{1,0:T(8,128)}) fusion(bf16[256,768]{1,0:T(8,128)(2,1)S(1)} %fusion.3, f32[256,768]{1,0:T(8,128)S(1)} %copy.62, f32[256]{0:T(256)S(1)} %fusion.111, f32[256]{0:T(256)S(1)} %broadcast_multiply_fusion), kind=kLoop, calls=%fused_computation.85 | loop fusion | flops 13565952 | bytes 2361344 | tf_op jit(solution)/shard_map/jvp()/convert_element_type | solution.py:109
  42.9 3.5 %jvp__.1 = (f32[1,1]{1,0:T(1,128)}, bf16[256,768]{1,0:T(8,128)(2,1)}) custom-call(bf16[256,768]{1,0:T(8,128)(2,1)} %get-tuple-element.12.hidden_ref, bf16[768,1024]{1,0:T(8,128)(2,1)} %dec_out_ref.1, bf16[256,1024]{1,0:T(8,128)(2,1)} %multiply_convert_fusion.targets_ref, f32[256,1]{1,0:T(8,128)} %copy.65.keep_ref), custom_call_target="tpu_custom_call" | custom-call | tf_op jit(solution)/shard_map/jvp()/pallas_call | solution.py:128
  46.5 2.0 %multiply_reduce_fusion.1 = f32[256]{0:T(256)S(1)} fusion(f32[256,768]{1,0:T(8,128)S(1)} %copy.62, f32[256]{0:T(256)S(1)} %broadcast_multiply_fusion, f32[256,768]{1,0:T(8,128)} %get-tuple-element.13, bf16[256,768]{1,0:T(8,128)(2,1)} %get-tuple-element.4, f32[256]{0:T(256)S(1)} %fusion.111), kind=kLoop, calls=%fused_computation.84 | loop fusion | flops 3538688 | bytes 1969152 | tf_op jit(solution)/shard_map/transpose(jvp())/reduce_sum | solution.py:23
  49.6 1.4 %fusion.7 = bf16[256,16,48]{0,2,1:T(8,128)(2,1)S(1)} fusion(bf16[16,48,256]{2,1,0:T(8,128)(2,1)S(1)} %bitcast.165, bf16[3,16,48,48]{3,2,1,0:T(8,128)(2,1)} %param.16), kind=kOutput, calls=%fused_computation.25 | convolution fusion | flops 18874368 | bytes 983040 | tf_op jit(solution)/shard_map/transpose(jvp(pgi,gio->pgo))/dot_general | solution.py:102
  50.9 1.2 %fusion.8 = bf16[256,16,48]{0,2,1:T(8,128)(2,1)S(1)} fusion(bf16[16,48,256]{2,1,0:T(8,128)(2,1)S(1)} %bitcast.166, bf16[3,16,48,48]{3,2,1,0:T(8,128)(2,1)} %param.16), kind=kOutput, calls=%fused_computation.26 | convolution fusion | flops 18874368 | bytes 983040 | tf_op jit(solution)/shard_map/transpose(jvp(pgi,gio->pgo))/dot_general | solution.py:102
  52.1 1.2 %fusion.9 = bf16[256,16,48]{0,2,1:T(8,128)(2,1)S(1)} fusion(bf16[16,48,256]{2,1,0:T(8,128)(2,1)S(1)} %bitcast.167, bf16[3,16,48,48]{3,2,1,0:T(8,128)(2,1)} %param.16), kind=kOutput, calls=%fused_computation.27 | convolution fusion | flops 18874368 | bytes 983040 | tf_op jit(solution)/shard_map/transpose(jvp(pgi,gio->pgo))/dot_general | solution.py:102
  53.8 2.2 %convolution_convert_fusion.12 = bf16[51,1024]{1,0:T(8,128)(2,1)S(1)} fusion(bf16[1024,768]{1,0:T(8,128)(2,1)} %param.15, bf16[256,768]{1,0:T(8,128)(2,1)S(1)} %copy-done.5, bf16[256,768]{1,0:T(8,128)(2,1)S(1)} %copy.70, pred[256]{0:T(512)(128)(4,1)} %copy-done.26, s32[51]{0:T(128)} %copy-done.24), kind=kOutput, calls=%fused_computation.45 | convolution fusion | flops 100964352 | bytes 2464204 | tf_op jit(solution)/shard_map/transpose(jvp())/dot_general | solution.py:90
  57.0 1.4 %fusion.16 = bf16[51,1,16,64]{3,0,2,1:T(8,128)(2,1)S(1)} fusion(bf16[51,16,64]{2,1,0:T(8,128)(2,1)S(1)} %reshape.220, f32[16,51,51]{1,2,0:T(8,128)} %copy-done.12, f32[16,51]{1,0:T(8,128)S(1)} %copy-done.23), kind=kOutput, calls=%fused_computation.41 | convolution fusion | flops 5462304 | bytes 378624 | tf_op jit(solution)/shard_map/transpose(jvp(hqk,khd->qhd))/dot_general | solution.py:38
  61.2 4.9 %convolution_convert_fusion.11 = bf16[51,1024]{1,0:T(8,128)(2,1)S(1)} fusion(bf16[51,3072]{1,0:T(8,128)(2,1)S(1)} %reshape.221, bf16[1024,3072]{1,0:T(8,128)(2,1)} %param.12), kind=kOutput, calls=%fused_computation.44 | convolution fusion | flops 320916480 | bytes 6709248 | tf_op jit(solution)/shard_map/transpose(jvp())/dot_general | solution.py:178
  67.3 1.5 %collective-permute-start.4 = (bf16[51,1024]{1,0:T(8,128)(2,1)S(1)}, bf16[51,1024]{1,0:T(8,128)(2,1)S(1)}, u32[]{:S(2)}, u32[]{:S(2)}) collective-permute-start(bf16[51,1024]{1,0:T(8,128)(2,1)S(1)} %fusion.99), channel_id=1, source_target_pairs={{0,2},{1,3},{2,0},{3,1},{4,6},{5,7},{6,4},{7,5},{8,10},{9,11},{10,... | collective-permute-start | bytes 313352 | tf_op jit(solution)/shard_map/ppermute | solution.py:191
  69.7 2.6 %collective-permute-done.3 = bf16[51,1024]{1,0:T(8,128)(2,1)S(1)} collective-permute-done((bf16[51,1024]{1,0:T(8,128)(2,1)S(1)}, bf16[51,1024]{1,0:T(8,128)(2,1)S(1)}, u32[]{:S(2)}, u32[]{:S(2)}) %collective-permute-start.3) | collective-permute-done | bytes 104480 | tf_op jit(solution)/shard_map/ppermute | solution.py:191
  72.2 1.0 %collective-permute-done.4 = bf16[51,1024]{1,0:T(8,128)(2,1)S(1)} collective-permute-done((bf16[51,1024]{1,0:T(8,128)(2,1)S(1)}, bf16[51,1024]{1,0:T(8,128)(2,1)S(1)}, u32[]{:S(2)}, u32[]{:S(2)}) %collective-permute-start.4) | collective-permute-done | bytes 104480 | tf_op jit(solution)/shard_map/ppermute | solution.py:191
  73.3 1.2 %collective-permute-done.5 = bf16[51,1024]{1,0:T(8,128)(2,1)S(1)} collective-permute-done((bf16[51,1024]{1,0:T(8,128)(2,1)S(1)}, bf16[51,1024]{1,0:T(8,128)(2,1)S(1)}, u32[]{:S(2)}, u32[]{:S(2)}) %collective-permute-start.5) | collective-permute-done | bytes 104480 | tf_op jit(solution)/shard_map/ppermute | solution.py:191
  74.5 1.4 %fusion.19 = f32[192,1024]{1,0:T(8,128)} fusion(bf16[51,1024]{1,0:T(8,128)(2,1)S(1)} %collective-permute-done.5, bf16[51,1024]{1,0:T(8,128)(2,1)S(1)} %collective-permute-done.4, bf16[51,1024]{1,0:T(8,128)(2,1)S(1)} %collective-permute-done.3, bf16[51,1024]{1,0:T(8,128)(2,1)S(1)} %fusion.99, bf16[256,768]{1,0:T(8,128)(2,1)S(1)} %pad_maximum_fusion, ...), kind=kOutput, calls=%fused_computation.52 | convolution fusion | flops 102032640 | bytes 1377284 | tf_op jit(solution)/shard_map/dot_general | solution.py:283
  (121 shorter events, 15.3 us)
Async XLA Ops:
  0.6 25.5 %copy-start = (bf16[1024,1024]{1,0:T(8,128)(2,1)S(1)}, bf16[1024,1024]{1,0:T(8,128)(2,1)}, u32[]{:S(2)}) copy-start(bf16[1024,1024]{1,0:T(8,128)(2,1)} %param.13) | copy-start | bytes 6291460
  0.6 10.9 %collective-permute-start = (bf16[64,768]{1,0:T(8,128)(2,1)}, bf16[64,768]{1,0:T(8,128)(2,1)S(1)}, u32[]{:S(2)}, u32[]{:S(2)}) collective-permute-start(bf16[64,768]{1,0:T(8,128)(2,1)} %param.9), channel_id=1, source_target_pairs={{0,1},{1,2},{2,3},{3,0},{4,5},{5,6},{6,7},{7,4},{8,9},{9,10},{10,1... | collective-permute-start | bytes 294920 | tf_op jit(solution)/shard_map/ppermute | solution.py:191
  3.7 7.9 %collective-permute-start.1 = (bf16[64,768]{1,0:T(8,128)(2,1)}, bf16[64,768]{1,0:T(8,128)(2,1)S(1)}, u32[]{:S(2)}, u32[]{:S(2)}) collective-permute-start(bf16[64,768]{1,0:T(8,128)(2,1)} %param.9), channel_id=1, source_target_pairs={{0,2},{1,3},{2,0},{3,1},{4,6},{5,7},{6,4},{7,5},{8,10},{9,11},{10,... | collective-permute-start | bytes 294920 | tf_op jit(solution)/shard_map/ppermute | solution.py:191
  5.2 6.4 %collective-permute-start.2 = (bf16[64,768]{1,0:T(8,128)(2,1)}, bf16[64,768]{1,0:T(8,128)(2,1)S(1)}, u32[]{:S(2)}, u32[]{:S(2)}) collective-permute-start(bf16[64,768]{1,0:T(8,128)(2,1)} %param.9), channel_id=1, source_target_pairs={{0,3},{1,0},{2,1},{3,2},{4,7},{5,4},{6,5},{7,6},{8,11},{9,8},{10,9... | collective-permute-start | bytes 294920 | tf_op jit(solution)/shard_map/ppermute | solution.py:191
  7.4 25.8 %copy-start.24 = (s32[51]{0:T(128)}, s32[51]{0:T(128)S(1)}, u32[]{:S(2)}) copy-start(s32[51]{0:T(128)S(1)} %slice_bitcast_fusion.6) | copy-start | bytes 616
  7.5 25.6 %copy-start.26 = (pred[256]{0:T(512)(128)(4,1)}, pred[256]{0:T(512)(128)(4,1)S(1)}, u32[]{:S(2)}) copy-start(pred[256]{0:T(512)(128)(4,1)S(1)} %broadcast_compare_fusion) | copy-start | bytes 772
  9.7 5.8 %copy-start.4 = (bf16[1024,3072]{1,0:T(8,128)(2,1)S(1)}, bf16[1024,3072]{1,0:T(8,128)(2,1)}, u32[]{:S(2)}) copy-start(bf16[1024,3072]{1,0:T(8,128)(2,1)} %param.12) | copy-start | bytes 18874372
  12.9 2.5 %copy-start.14 = (bf16[64,768]{1,0:T(8,128)(2,1)}, bf16[64,768]{1,0:T(8,128)(2,1)S(1)}, u32[]{:S(2)}) copy-start(bf16[64,768]{1,0:T(8,128)(2,1)S(1)} %get-tuple-element.17) | copy-start | bytes 294916
  12.9 2.5 %copy-start.16 = (bf16[64,768]{1,0:T(8,128)(2,1)}, bf16[64,768]{1,0:T(8,128)(2,1)S(1)}, u32[]{:S(2)}) copy-start(bf16[64,768]{1,0:T(8,128)(2,1)S(1)} %get-tuple-element.18) | copy-start | bytes 294916
  12.9 2.5 %copy-start.18 = (bf16[64,768]{1,0:T(8,128)(2,1)}, bf16[64,768]{1,0:T(8,128)(2,1)S(1)}, u32[]{:S(2)}) copy-start(bf16[64,768]{1,0:T(8,128)(2,1)S(1)} %get-tuple-element.19) | copy-start | bytes 294916
  12.9 2.5 %copy-start.20 = (bf16[64,768]{1,0:T(8,128)(2,1)}, bf16[64,768]{1,0:T(8,128)(2,1)S(1)}, u32[]{:S(2)}) copy-start(bf16[64,768]{1,0:T(8,128)(2,1)S(1)} %get-tuple-element.20) | copy-start | bytes 294916
  21.2 2.8 %copy-start.1 = (bf16[256,3072]{0,1:T(8,128)(2,1)S(1)}, bf16[256,3072]{0,1:T(8,128)(2,1)}, u32[]{:S(2)}) copy-start(bf16[256,3072]{0,1:T(8,128)(2,1)} %copy.63) | copy-start | bytes 4718596
  28.7 1.2 %copy-start.8 = (bf16[51,1,16,64]{3,2,1,0:T(8,128)(2,1)}, bf16[51,1,16,64]{3,2,1,0:T(8,128)(2,1)S(1)}, u32[]{:S(2)}) copy-start(bf16[51,1,16,64]{3,2,1,0:T(8,128)(2,1)S(1)} %get-tuple-element.16) | copy-start | bytes 313348
  28.7 1.2 %copy-start.10 = (bf16[51,1,16,64]{3,2,1,0:T(8,128)(2,1)}, bf16[51,1,16,64]{3,2,1,0:T(8,128)(2,1)S(1)}, u32[]{:S(2)}) copy-start(bf16[51,1,16,64]{3,2,1,0:T(8,128)(2,1)S(1)} %get-tuple-element.15) | copy-start | bytes 313348
  30.0 1.0 %copy-start.22 = (f32[16,51]{1,0:T(8,128)}, f32[16,51]{1,0:T(8,128)S(1)}, u32[]{:S(2)}) copy-start(f32[16,51]{1,0:T(8,128)S(1)} %get-tuple-element.25) | copy-start | bytes 9796
  37.7 0.9 %copy-start.2 = (f32[16,256,48]{1,2,0:T(8,128)}, f32[16,256,48]{1,2,0:T(8,128)S(1)}, u32[]{:S(2)}) copy-start(f32[16,256,48]{1,2,0:T(8,128)S(1)} %get-tuple-element.28) | copy-start | bytes 2359300
  46.5 2.0 %copy-start.3 = (f32[256,768]{1,0:T(8,128)S(1)}, f32[256,768]{1,0:T(8,128)}, u32[]{:S(2)}) copy-start(f32[256,768]{1,0:T(8,128)} %get-tuple-element.13) | copy-start | bytes 2359300
  46.5 2.0 %copy-start.5 = (bf16[256,768]{1,0:T(8,128)(2,1)S(1)}, bf16[256,768]{1,0:T(8,128)(2,1)}, u32[]{:S(2)}) copy-start(bf16[256,768]{1,0:T(8,128)(2,1)} %get-tuple-element.4) | copy-start | bytes 1179652
  49.4 3.9 %copy-start.23 = (f32[16,51]{1,0:T(8,128)S(1)}, f32[16,51]{1,0:T(8,128)}, u32[]{:S(2)}) copy-start(f32[16,51]{1,0:T(8,128)} %copy-done.22) | copy-start | bytes 9796
  56.0 2.4 %copy-start.11 = (bf16[51,1,16,64]{3,2,1,0:T(8,128)(2,1)S(1)}, bf16[51,1,16,64]{3,2,1,0:T(8,128)(2,1)}, u32[]{:S(2)}) copy-start(bf16[51,1,16,64]{3,2,1,0:T(8,128)(2,1)} %copy-done.10) | copy-start | bytes 313348
  56.8 1.9 %copy-start.7 = (bf16[51,1,16,64]{3,2,1,0:T(8,128)(2,1)S(1)}, bf16[51,1,16,64]{3,2,1,0:T(8,128)(2,1)}, u32[]{:S(2)}) copy-start(bf16[51,1,16,64]{3,2,1,0:T(8,128)(2,1)} %copy-done.6) | copy-start | bytes 313348
  56.8 1.9 %copy-start.9 = (bf16[51,1,16,64]{3,2,1,0:T(8,128)(2,1)S(1)}, bf16[51,1,16,64]{3,2,1,0:T(8,128)(2,1)}, u32[]{:S(2)}) copy-start(bf16[51,1,16,64]{3,2,1,0:T(8,128)(2,1)} %copy-done.8) | copy-start | bytes 313348
  57.0 1.4 %copy-start.13 = (f32[16,51,51]{1,2,0:T(8,128)S(1)}, f32[16,51,51]{1,2,0:T(8,128)}, u32[]{:S(2)}) copy-start(f32[16,51,51]{1,2,0:T(8,128)} %copy-done.12) | copy-start | bytes 499396
  61.1 5.0 %copy-start.27 = (f32[51]{0:T(128)S(1)}, f32[51]{0:T(128)}, u32[]{:S(2)}) copy-start(f32[51]{0:T(128)} %get-tuple-element.33) | copy-start | bytes 616
  61.1 8.5 %copy-start.15 = (bf16[64,768]{1,0:T(8,128)(2,1)S(1)}, bf16[64,768]{1,0:T(8,128)(2,1)}, u32[]{:S(2)}) copy-start(bf16[64,768]{1,0:T(8,128)(2,1)} %copy-done.14) | copy-start | bytes 294916
  61.1 8.5 %copy-start.17 = (bf16[64,768]{1,0:T(8,128)(2,1)S(1)}, bf16[64,768]{1,0:T(8,128)(2,1)}, u32[]{:S(2)}) copy-start(bf16[64,768]{1,0:T(8,128)(2,1)} %copy-done.16) | copy-start | bytes 294916
  61.1 8.5 %copy-start.19 = (bf16[64,768]{1,0:T(8,128)(2,1)S(1)}, bf16[64,768]{1,0:T(8,128)(2,1)}, u32[]{:S(2)}) copy-start(bf16[64,768]{1,0:T(8,128)(2,1)} %copy-done.18) | copy-start | bytes 294916
  61.2 8.5 %copy-start.21 = (bf16[64,768]{1,0:T(8,128)(2,1)S(1)}, bf16[64,768]{1,0:T(8,128)(2,1)}, u32[]{:S(2)}) copy-start(bf16[64,768]{1,0:T(8,128)(2,1)} %copy-done.20) | copy-start | bytes 294916
  61.2 13.3 %copy-start.25 = (s32[204]{0:T(256)S(1)}, s32[204]{0:T(256)}, u32[]{:S(2)}) copy-start(s32[204]{0:T(256)} %eq.96) | copy-start | bytes 2452
  66.7 5.5 %collective-permute-start.3 = (bf16[51,1024]{1,0:T(8,128)(2,1)S(1)}, bf16[51,1024]{1,0:T(8,128)(2,1)S(1)}, u32[]{:S(2)}, u32[]{:S(2)}) collective-permute-start(bf16[51,1024]{1,0:T(8,128)(2,1)S(1)} %fusion.99), channel_id=1, source_target_pairs={{0,3},{1,0},{2,1},{3,2},{4,7},{5,4},{6,5},{7,6},{8,11},{9,8},{10,9... | collective-permute-start | bytes 313352 | tf_op jit(solution)/shard_map/ppermute | solution.py:191
  67.3 6.0 %collective-permute-start.4 = (bf16[51,1024]{1,0:T(8,128)(2,1)S(1)}, bf16[51,1024]{1,0:T(8,128)(2,1)S(1)}, u32[]{:S(2)}, u32[]{:S(2)}) collective-permute-start(bf16[51,1024]{1,0:T(8,128)(2,1)S(1)} %fusion.99), channel_id=1, source_target_pairs={{0,2},{1,3},{2,0},{3,1},{4,6},{5,7},{6,4},{7,5},{8,10},{9,11},{10,... | collective-permute-start | bytes 313352 | tf_op jit(solution)/shard_map/ppermute | solution.py:191
  68.8 5.7 %collective-permute-start.5 = (bf16[51,1024]{1,0:T(8,128)(2,1)S(1)}, bf16[51,1024]{1,0:T(8,128)(2,1)S(1)}, u32[]{:S(2)}, u32[]{:S(2)}) collective-permute-start(bf16[51,1024]{1,0:T(8,128)(2,1)S(1)} %fusion.99), channel_id=1, source_target_pairs={{0,1},{1,2},{2,3},{3,0},{4,5},{5,6},{6,7},{7,4},{8,9},{9,10},{10,1... | collective-permute-start | bytes 313352 | tf_op jit(solution)/shard_map/ppermute | solution.py:191
  (2 other events, 1.5 us)
